TPU v7x, 32 devices: a whole 2x2x4 slice. The times are simulated.
32 devices in a mesh: expert: 4 (over z), shard: 8 (over y, x, core).
Axes of the slice: x: 2, y: 2, z: 4, core: 2. Of those that a mesh axis runs over, the one named last changes fastest.
Arguments:
- tokens: bfloat16 [18912, 768], P(('expert', 'shard')), may hold values from -6 to 6
- image_counts: int32 [4, 8], P('expert', 'shard'), may hold values from 1 to 3, as said below
- routes: int32 [18912, 2], P(('expert', 'shard')), may hold values from 0 to 3, all different within a row; in each aligned block of 591 rows (0 to 590, 591 to 1181, ...) at most 376 rows name the same one
- w_qkv: bfloat16 [768, 2304], P('shard'), may hold values from -0.21875 to 0.21875
- w_out: bfloat16 [768, 768], P('shard'), may hold values from -1.5 to 1.5
- w_router: bfloat16 [768, 4], P('shard'), may hold values from -0.15625 to 0.15625
- gain_attn: bfloat16 [768], P('shard'), may hold values from 0.25 to 1.75
- gain_moe: bfloat16 [768], P('shard'), may hold values from 0.25 to 1.75
- w_in: bfloat16 [4, 768, 3072], P('expert', 'shard'), may hold values from -0.21875 to 0.21875
- w_back: bfloat16 [4, 3072, 768], P('expert', 'shard'), may hold values from -0.625 to 0.625
- cotangent: bfloat16 [18912, 768], P(('expert', 'shard')), may hold values from -6 to 6
Outputs:
- output: bfloat16 [18912, 768], P(('expert', 'shard'))
- grad_tokens: bfloat16 [18912, 768], P(('expert', 'shard'))
- grad_w_qkv: float32 [768, 2304], P('shard')
- grad_w_out: float32 [768, 768], P('shard')
- grad_w_router: float32 [768, 4], P('shard')
- grad_gain_attn: float32 [768], P('shard')
- grad_gain_moe: float32 [768], P('shard')
- grad_w_in: float32 [4, 768, 3072], P('expert', 'shard')
- grad_w_back: float32 [4, 3072, 768], P('expert', 'shard')
Inputs may be any that keep to these rules, and one draw needn't show every extreme that they name: `image_counts`: each device holds between 1 and 3 live images; some device holds 3 and some holds 1. `routes`: the two experts of a token differ; among the rows of one device at most 376 name any one expert.
All inputs are finite; a program needn't handle non-finite values.
Results may differ from a plain program's by a relative error of at most 0.024.
Values may be sent and summed in bfloat16 or wider, within the bound.
No kernel may reach another device: no remote copies, remote signals or barrier semaphores. Data moves between devices by JAX's collectives and lax.ppermute only.
A program may use at most 256 MiB of HBM per device.

v0:
```python
import jax
import jax.numpy as jnp
from jax import lax
from jax.sharding import PartitionSpec as P

H = 12
HD = 64
SEQ = 197


EPSILON = 1e-06
ROW_CONTRACT = (((0,), (0,)), ((), ()))
COL_CONTRACT = (((1,), (1,)), ((), ()))


def layer_norm(values, norm_gain):
    row_mean = jnp.mean(values, axis=-1, keepdims=True)
    centered = values - row_mean
    variance = jnp.mean(centered * centered, axis=-1, keepdims=True)
    return centered * lax.rsqrt(variance + EPSILON) * norm_gain


def normalize_rows(scores):
    row_top = jnp.max(scores, axis=-1, keepdims=True)
    exp_scores = jnp.exp(scores - row_top)
    return exp_scores / jnp.sum(exp_scores, axis=-1, keepdims=True)


def gelu_exact(values):
    return jax.nn.gelu(values, approximate=False)


def shards(
    tokens,
    image_counts,
    routes,
    w_qkv,
    w_out,
    w_router,
    gain_attn,
    gain_moe,
    w_in,
    w_back,
    cotangent,
):
    rows, width = tokens.shape
    experts = lax.axis_size("expert")
    capacity = 8 * (5 * rows // (16 * experts)) + 8
    overflow = experts * capacity
    images = rows // SEQ
    score_scale = HD ** (-0.5)
    row_ids = jnp.arange(rows, dtype=jnp.int32)
    live_int = (row_ids // SEQ < image_counts[0, 0]).astype(jnp.int32)
    live_rows = live_int.astype(jnp.float32)
    full_qkv, full_out, full_router, full_gain_attn, full_gain_moe = (
        lax.all_gather(w_qkv, "shard", axis=0, tiled=True),
        lax.all_gather(w_out, "shard", axis=0, tiled=True),
        lax.all_gather(w_router, "shard", axis=0, tiled=True),
        lax.all_gather(gain_attn, "shard", axis=0, tiled=True),
        lax.all_gather(gain_moe, "shard", axis=0, tiled=True),
    )
    gain_one = full_gain_attn.astype(jnp.float32)
    gain_two = full_gain_moe.astype(jnp.float32)
    gathered = (
        lax.all_gather(w_in, "shard", axis=1, tiled=True),
        lax.all_gather(w_back, "shard", axis=1, tiled=True),
    )
    expert_first = gathered[0][0]
    expert_second = gathered[1][0]
    token_f = tokens.astype(jnp.float32)
    attn_in = layer_norm(token_f, gain_one).astype(jnp.bfloat16)
    projected = jnp.dot(attn_in, full_qkv, preferred_element_type=jnp.float32).astype(jnp.bfloat16)
    split_heads = projected.reshape(images, SEQ, 3, H, HD)
    queries = split_heads[:, :, 0]
    keys_part = split_heads[:, :, 1]
    values_part = split_heads[:, :, 2]
    scores = (
        jnp.einsum("ishd,ithd->ihst", queries, keys_part, preferred_element_type=jnp.float32)
        * score_scale
    )
    row_top = jnp.max(scores, axis=-1, keepdims=True)
    log_total = row_top + jnp.log(jnp.sum(jnp.exp(scores - row_top), axis=-1, keepdims=True))
    attn_probs = jnp.exp(scores - log_total)
    mixed_rows = (
        jnp.einsum(
            "ihst,ithd->ishd",
            attn_probs.astype(jnp.bfloat16),
            values_part,
            preferred_element_type=jnp.float32,
        )
        .reshape(rows, width)
        .astype(jnp.bfloat16)
    )
    hidden_state = token_f + jnp.dot(mixed_rows, full_out, preferred_element_type=jnp.float32)
    moe_in = layer_norm(hidden_state, gain_two).astype(jnp.bfloat16)
    logits = jnp.dot(moe_in, full_router, preferred_element_type=jnp.float32)
    router_probs = normalize_rows(logits)
    expert_ids = jnp.arange(experts, dtype=jnp.int32)
    choose = (routes[:, :, None] == expert_ids).astype(jnp.float32)
    chosen = jnp.sum(choose * router_probs[:, None, :], axis=2)
    pick_table = (routes[:, :, None] == expert_ids).astype(jnp.int32) * live_int[:, None, None]
    flat_picks = pick_table.reshape(rows * 2, experts)
    before = jnp.cumsum(flat_picks, axis=0) - flat_picks
    slot_index = jnp.sum(before * flat_picks, axis=1).reshape(rows, 2)
    position = jnp.where(live_int[:, None] > 0, routes * capacity + slot_index, overflow)
    safe_index = jnp.minimum(position, overflow - 1)
    outgoing = jnp.zeros((overflow, width), jnp.bfloat16)
    outgoing = (
        outgoing.at[position[:, 0]]
        .set(moe_in, mode="drop")
        .at[position[:, 1]]
        .set(moe_in, mode="drop")
    )
    outgoing = outgoing.reshape(experts, capacity, width)
    arrived = lax.all_to_all(outgoing, "expert", split_axis=0, concat_axis=0, tiled=True)
    sources = arrived.shape[0]
    slot_count = arrived.shape[1]
    flat_rows = arrived.reshape(sources * slot_count, width)
    pre_act = jnp.dot(flat_rows, expert_first, preferred_element_type=jnp.float32)
    activated = gelu_exact(pre_act).astype(jnp.bfloat16)
    produced = jnp.dot(activated, expert_second, preferred_element_type=jnp.float32).astype(
        jnp.bfloat16
    )
    produced, pre_act, activated, arrived = (
        produced.reshape(sources, slot_count, width),
        pre_act.reshape(sources, slot_count, -1),
        activated.reshape(sources, slot_count, -1),
        arrived,
    )
    returned = lax.all_to_all(produced, "expert", split_axis=0, concat_axis=0, tiled=True)
    picked = returned.reshape(overflow, width)[safe_index].astype(jnp.float32)
    weighted = chosen * live_rows[:, None]
    moe_out = jnp.sum(weighted[:, :, None] * picked, axis=1)
    output = (live_rows[:, None] * (hidden_state + moe_out)).astype(jnp.bfloat16)
    grad_out = cotangent.astype(jnp.float32) * live_rows[:, None]
    grad_chosen = jnp.sum(grad_out[:, None, :] * picked, axis=2) * live_rows[:, None]
    grad_picked = (weighted[:, :, None] * grad_out[:, None, :]).astype(jnp.bfloat16)
    back_out = jnp.zeros((overflow, width), jnp.bfloat16)
    back_out = (
        back_out.at[position[:, 0]]
        .set(grad_picked[:, 0], mode="drop")
        .at[position[:, 1]]
        .set(grad_picked[:, 1], mode="drop")
    )
    arriving_grad = lax.all_to_all(
        back_out.reshape(experts, capacity, width),
        "expert",
        split_axis=0,
        concat_axis=0,
        tiled=True,
    )
    regathered = (
        lax.all_gather(w_in, "shard", axis=1, tiled=True),
        lax.all_gather(w_back, "shard", axis=1, tiled=True),
    )
    back_first = regathered[0][0]
    back_second = regathered[1][0]
    flat_grad = arriving_grad.reshape(overflow, width)
    flat_pre = pre_act.reshape(overflow, -1)
    flat_act = activated.reshape(overflow, -1)
    flat_arrived = arrived.reshape(overflow, width)
    grad_second = lax.dot_general(
        flat_act, flat_grad, ROW_CONTRACT, preferred_element_type=jnp.float32
    )
    hidden_grad = lax.dot_general(
        flat_grad, back_second, COL_CONTRACT, preferred_element_type=jnp.float32
    )
    gelu_value, gelu_back = jax.vjp(gelu_exact, flat_pre)
    pre_grad = gelu_back(hidden_grad)[0].astype(jnp.bfloat16)
    grad_first = lax.dot_general(
        flat_arrived, pre_grad, ROW_CONTRACT, preferred_element_type=jnp.float32
    )
    row_grad = lax.dot_general(
        pre_grad, back_first, COL_CONTRACT, preferred_element_type=jnp.float32
    ).astype(jnp.bfloat16)
    back_rows = lax.all_to_all(
        row_grad.reshape(experts, capacity, width),
        "expert",
        split_axis=0,
        concat_axis=0,
        tiled=True,
    )
    incoming = back_rows.reshape(overflow, width)[safe_index].astype(jnp.float32)
    expert_part = jnp.sum(incoming, axis=1) * live_rows[:, None]
    prob_sum = jnp.sum(choose * grad_chosen[:, :, None], axis=1)
    logit_grad = (
        router_probs * (prob_sum - jnp.sum(router_probs * prob_sum, axis=-1, keepdims=True))
    ).astype(jnp.bfloat16)
    grad_router = lax.dot_general(
        moe_in, logit_grad, ROW_CONTRACT, preferred_element_type=jnp.float32
    )
    moe_in_grad = expert_part + lax.dot_general(
        logit_grad, full_router, COL_CONTRACT, preferred_element_type=jnp.float32
    )
    norm_value, norm_back = jax.vjp(layer_norm, hidden_state, gain_two)
    state_part, grad_gain_two = norm_back(moe_in_grad)
    state_grad = grad_out + state_part
    branch_grad = state_grad.astype(jnp.bfloat16)
    grad_wout = lax.dot_general(
        mixed_rows, branch_grad, ROW_CONTRACT, preferred_element_type=jnp.float32
    )
    mixed_grad = lax.dot_general(
        branch_grad, full_out, COL_CONTRACT, preferred_element_type=jnp.float32
    )
    mixed_grad = mixed_grad.astype(jnp.bfloat16).reshape(images, SEQ, H, HD)
    again_scores = (
        jnp.einsum("ishd,ithd->ihst", queries, keys_part, preferred_element_type=jnp.float32)
        * score_scale
    )
    again_probs = jnp.exp(again_scores - log_total)
    grad_values = jnp.einsum(
        "ihst,ishd->ithd",
        again_probs.astype(jnp.bfloat16),
        mixed_grad,
        preferred_element_type=jnp.float32,
    )
    prob_grad = jnp.einsum(
        "ishd,ithd->ihst", mixed_grad, values_part, preferred_element_type=jnp.float32
    )
    score_grad = (
        again_probs * (prob_grad - jnp.sum(again_probs * prob_grad, axis=-1, keepdims=True))
    ).astype(jnp.bfloat16)
    grad_queries = (
        jnp.einsum("ihst,ithd->ishd", score_grad, keys_part, preferred_element_type=jnp.float32)
        * score_scale
    )
    grad_keys = (
        jnp.einsum("ihst,ishd->ithd", score_grad, queries, preferred_element_type=jnp.float32)
        * score_scale
    )
    projected_grad = (
        jnp.stack([grad_queries, grad_keys, grad_values], axis=2)
        .reshape(rows, 3 * width)
        .astype(jnp.bfloat16)
    )
    grad_qkv = lax.dot_general(
        attn_in, projected_grad, ROW_CONTRACT, preferred_element_type=jnp.float32
    )
    attn_in_grad = lax.dot_general(
        projected_grad, full_qkv, COL_CONTRACT, preferred_element_type=jnp.float32
    )
    first_value, first_back = jax.vjp(layer_norm, token_f, gain_one)
    token_part, grad_gain_one = first_back(attn_in_grad)
    grad_tokens = (state_grad + token_part).astype(jnp.bfloat16)
    grad_in_share, grad_back_share = (
        lax.psum_scatter(
            grad_first[None].astype(jnp.bfloat16), "shard", scatter_dimension=1, tiled=True
        ).astype(jnp.float32),
        lax.psum_scatter(
            grad_second[None].astype(jnp.bfloat16), "shard", scatter_dimension=1, tiled=True
        ).astype(jnp.float32),
    )
    shares = (
        lax.psum_scatter(
            grad_qkv.astype(jnp.bfloat16), "shard", scatter_dimension=0, tiled=True
        ).astype(jnp.float32),
        lax.psum_scatter(
            grad_wout.astype(jnp.bfloat16), "shard", scatter_dimension=0, tiled=True
        ).astype(jnp.float32),
        lax.psum_scatter(
            grad_router.astype(jnp.bfloat16), "shard", scatter_dimension=0, tiled=True
        ).astype(jnp.float32),
        lax.psum_scatter(
            grad_gain_one.astype(jnp.bfloat16), "shard", scatter_dimension=0, tiled=True
        ).astype(jnp.float32),
        lax.psum_scatter(
            grad_gain_two.astype(jnp.bfloat16), "shard", scatter_dimension=0, tiled=True
        ).astype(jnp.float32),
    )
    totals = (
        lax.psum(shares[0].astype(jnp.bfloat16), "expert").astype(jnp.float32),
        lax.psum(shares[1].astype(jnp.bfloat16), "expert").astype(jnp.float32),
        lax.psum(shares[2].astype(jnp.bfloat16), "expert").astype(jnp.float32),
        lax.psum(shares[3].astype(jnp.bfloat16), "expert").astype(jnp.float32),
        lax.psum(shares[4].astype(jnp.bfloat16), "expert").astype(jnp.float32),
    )
    return (
        output,
        grad_tokens,
        totals[0],
        totals[1],
        totals[2],
        totals[3],
        totals[4],
        grad_in_share,
        grad_back_share,
    )


def solution(mesh):
    return jax.shard_map(
        shards,
        mesh=mesh,
        in_specs=(
            P(("expert", "shard"), None),
            P("expert", "shard"),
            P(("expert", "shard"), None),
            P("shard", None),
            P("shard", None),
            P("shard", None),
            P("shard"),
            P("shard"),
            P("expert", "shard", None),
            P("expert", "shard", None),
            P(("expert", "shard"), None),
        ),
        out_specs=(
            P(("expert", "shard"), None),
            P(("expert", "shard"), None),
            P("shard", None),
            P("shard", None),
            P("shard", None),
            P("shard"),
            P("shard"),
            P("expert", "shard", None),
            P("expert", "shard", None),
        ),
        check_vma=False,
    )
```

profile of v0, /device:TPU:0, one launch (start us, length us, event | category | flops | bytes accessed | tf_op | source)
XLA Modules:
  0.0 761.1 jit_solution(17173408247433804776)
XLA Ops:
  9.4 1.3 fusion.75
  13.1 15.5 %all-reduce.6 = (bf16[768]{0:T(1024)(128)(2,1)S(1)}, bf16[768]{0:T(1024)(128)(2,1)S(1)}) all-reduce(bf16[768]{0:T(1024)(128)(2,1)S(1)} %dynamic-update-slice, bf16[768]{0:T(1024)(128)(2,1)S(1)} %dynamic-update-slice.1), channel_id=1, replica_groups=mesh['expert'=4,'shard'=8] {'shard'}, use_global_device_ids=true, to_apply=%add.1 | all-reduce | flops 1536 | bytes 6144
  34.2 12.4 %all-gather.6.cloned.1.call-done = bf16[768,2304]{1,0:T(8,128)(2,1)} async-done(((bf16[96,2304]{1,0:T(8,128)(2,1)}), bf16[768,2304]{1,0:T(8,128)(2,1)}) %all-gather.6.cloned.1.call-update) | async-done | bytes 3538960 | tf_op jit(solution)/shard_map/all_gather | solution.py:56
  46.6 6.0 convolution_convert_fusion.3
  52.6 9.3 %reshape.295 = bf16[3,197,3,12,64]{4,3,2,1,0:T(8,128)(2,1)} reshape(bf16[591,2304]{1,0:T(8,128)(2,1)} %convolution_convert_fusion.3) | data formatting | bytes 5446656 | tf_op jit(solution)/shard_map/reshape | solution.py:73
  61.8 6.7 fusion.74
  68.5 4.2 copy.146
  72.7 4.2 copy.147
  76.9 3.8 copy.145
  80.8 3.4 multiply_reduce_fusion.1
  84.2 1.6 exponential_reduce_fusion
  87.7 1.6 fusion.34
  90.3 2.1 convert_element_type.167
  92.4 2.6 fusion.76
  95.3 8.0 %scatter_custom_fusion = bf16[1504,768]{1,0:T(8,128)(2,1)} fusion(s32[591]{0:T(1024)S(1)} %get-tuple-element.16, bf16[]{:T(256)} %constant.53.clone.1, f32[591,768]{1,0:T(8,128)S(1)} %get-tuple-element.42, f32[768]{0:T(1024)S(1)} %convert_element_type.168, f32[591]{0:T(1024)S(1)} %fusion.63, f32[591]{0:T(1024)S(1)} %broadcast_multiply_fusion.2), kind=kCustom, calls=%fused_computation.92 | custom fusion | flops 1815552 | bytes 4141058 | tf_op jit(solution)/shard_map/scatter | solution.py:110
  103.4 9.9 %scatter_custom_fusion.1 = bf16[1504,768]{1,0:T(8,128)(2,1)} fusion(bf16[1504,768]{1,0:T(8,128)(2,1)} %scatter_custom_fusion, s32[591]{0:T(1024)S(1)} %get-tuple-element.15, f32[591,768]{1,0:T(8,128)S(1)} %get-tuple-element.42, f32[768]{0:T(1024)S(1)} %convert_element_type.168, f32[591]{0:T(1024)S(1)} %fusion.63, f32[591]{0:T(1024)S(1)} %broadcast_multiply_fusion.2), kind=kCustom, calls=%fused_computation.155 | custom fusion | flops 1815552 | bytes 4141056 | tf_op jit(solution)/shard_map/scatter | solution.py:112
  113.2 4.6 all-to-all-start
  118.5 52.6 %all-to-all-done = bf16[4,376,768]{2,1,0:T(8,128)(2,1)S(1)} async-done(((bf16[4,376,768]{2,1,0:T(8,128)(2,1)}), bf16[4,376,768]{2,1,0:T(8,128)(2,1)S(1)}, u32[]{:S(2)}, u32[]{:S(2)}) %all-to-all-start) | async-done | bytes 2310176 | tf_op jit(solution)/shard_map/all_to_all | solution.py:115
  171.0 47.9 %multiply_convert_fusion = (bf16[1504,3072]{1,0:T(8,128)(2,1)}, f32[1504,3072]{1,0:T(8,128)}, f32[1504,3072]{1,0:T(8,128)}) fusion(bf16[1504,768]{1,0:T(8,128)(2,1)S(1)} %bitcast.123, bf16[1,768,3072]{2,1,0:T(8,128)(2,1)} %all-gather.10.cloned.1.call-done), kind=kOutput, calls=%fused_computation.9 | convolution fusion | flops 7397081088 | bytes 53231616 | tf_op jit(solution)/shard_map/dot_general | solution.py:119
  218.9 12.3 %fusion.19 = bf16[1504,768]{1,0:T(8,128)(2,1)} fusion(bf16[1504,3072]{1,0:T(8,128)(2,1)} %get-tuple-element.30, bf16[1,3072,768]{2,1,0:T(8,128)(2,1)} %all-gather.12.cloned.1.call-done), kind=kOutput, calls=%fused_computation.47 | convolution fusion | flops 7097917440 | bytes 16269312 | tf_op jit(solution)/shard_map/dot_general | solution.py:121
  231.2 3.8 all-to-all-start.1
  235.1 9.3 %all-gather = bf16[8,96,4]{1,2,0:T(4,128)(2,1)S(1)} all-gather(bf16[1,96,4]{1,2,0:T(4,128)(2,1)S(1)} %bitcast.131), channel_id=1, replica_groups=mesh['expert'=4,'shard'=8] {'shard'}, dimensions={0}, use_global_device_ids=true | all-gather | bytes 6912 | tf_op jit(solution)/shard_map/all_gather | solution.py:58
  247.0 1.5 convert_multiply_fusion
  249.3 38.0 %all-to-all-done.1 = bf16[4,376,768]{2,1,0:T(8,128)(2,1)S(1)} async-done(((bf16[4,376,768]{2,1,0:T(8,128)(2,1)}), bf16[4,376,768]{2,1,0:T(8,128)(2,1)S(1)}, u32[]{:S(2)}, u32[]{:S(2)}) %all-to-all-start.1) | async-done | bytes 2310176 | tf_op jit(solution)/shard_map/all_to_all | solution.py:130
  287.3 4.8 gather_fusion
  292.1 5.2 reshape.277
  297.3 5.6 multiply_reduce_fusion.2
  302.9 6.9 scatter_custom_fusion.2
  309.9 7.5 scatter_custom_fusion.3
  317.4 55.0 %all_to_all.20 = bf16[4,376,768]{2,1,0:T(8,128)(2,1)S(1)} all-to-all(bf16[4,376,768]{2,1,0:T(8,128)(2,1)S(1)} %bitcast.122), channel_id=1, replica_groups=mesh['expert'=4,'shard'=8] {'expert'}, dimensions={0} | all-to-all | bytes 4620288 | tf_op jit(solution)/shard_map/all_to_all | solution.py:145
  372.4 23.0 %add_convert_fusion = bf16[1504,3072]{1,0:T(8,128)(2,1)} fusion(f32[1504,3072]{1,0:T(8,128)} %get-tuple-element.31, f32[1504,3072]{1,0:T(8,128)} %get-tuple-element.43, bf16[1504,768]{1,0:T(8,128)(2,1)S(1)} %bitcast.125, bf16[1,3072,768]{2,1,0:T(8,128)(2,1)} %all-gather.12.cloned.1.call-done), kind=kOutput, calls=%fused_computation.8 | convolution fusion | flops 7161446400 | bytes 53231616 | tf_op jit(solution)/shard_map/dot_general | solution.py:165
  395.4 12.4 %fusion.16 = bf16[1504,768]{1,0:T(8,128)(2,1)} fusion(bf16[1504,3072]{1,0:T(8,128)(2,1)} %add_convert_fusion, bf16[1,768,3072]{2,1,0:T(8,128)(2,1)} %all-gather.10.cloned.1.call-done), kind=kOutput, calls=%fused_computation.46 | convolution fusion | flops 7097917440 | bytes 16269312 | tf_op jit(solution)/shard_map/dot_general | solution.py:173
  407.7 3.6 all-to-all-start.3
  412.7 50.7 %all-to-all-done.3 = bf16[4,376,768]{2,1,0:T(8,128)(2,1)S(1)} async-done(((bf16[4,376,768]{2,1,0:T(8,128)(2,1)}), bf16[4,376,768]{2,1,0:T(8,128)(2,1)S(1)}, u32[]{:S(2)}, u32[]{:S(2)}) %all-to-all-start.3) | async-done | bytes 2310176 | tf_op jit(solution)/shard_map/all_to_all | solution.py:176
  463.4 4.8 gather_fusion.1
  468.3 5.0 reshape.278
  473.3 7.7 %reduce_sum.190 = f32[591,768]{1,0:T(8,128)} reduce(f32[591,2,768]{2,1,0:T(2,128)} %reshape.278, f32[]{:T(128)} %constant.48.clone.1), dimensions={1}, to_apply=%region_17.18 | reduce | flops 453888 | bytes 5446660 | tf_op jit(solution)/shard_map/reduce_sum | solution.py:184
  481.0 2.6 multiply_reduce_fusion.4
  483.7 1.8 fusion.72
  487.6 2.9 reshape.296
  490.6 4.7 copy.129
  495.3 6.1 multiply_reduce_fusion
  501.5 3.6 multiply_convert_fusion.1
  505.1 2.3 convolution_convert_fusion.6
  507.5 3.0 fusion.32
  512.3 4.8 fusion.35
  518.1 5.6 copy.134
  523.6 10.1 %convert_element_type.183 = bf16[591,2304]{0,1:T(8,128)(2,1)} reshape(bf16[3,197,3,12,64]{1,0,4,3,2:T(4,128)(2,1)} %copy.134) | data formatting | bytes 5446656 | tf_op jit(solution)/shard_map/convert_element_type | solution.py:234
  533.7 6.8 convolution_convert_fusion.1
  540.6 1.6 copy-done.21
  542.2 13.3 %fusion.15 = bf16[1,3072,768]{2,1,0:T(8,128)(2,1)} fusion(bf16[1504,3072]{1,0:T(8,128)(2,1)} %get-tuple-element.30, bf16[1504,768]{1,0:T(8,128)(2,1)S(1)} %bitcast.126), kind=kOutput, calls=%fused_computation.41 | convolution fusion | flops 7099121664 | bytes 16269312 | tf_op jit(solution)/shard_map/dot_general | solution.py:162
  555.7 1.8 copy-done.19
  557.4 13.2 %fusion.14 = bf16[1,768,3072]{2,1,0:T(8,128)(2,1)} fusion(bf16[1504,768]{1,0:T(8,128)(2,1)S(1)} %bitcast.124, bf16[1504,3072]{1,0:T(8,128)(2,1)} %add_convert_fusion), kind=kOutput, calls=%fused_computation.40 | convolution fusion | flops 7099121664 | bytes 16269312 | tf_op jit(solution)/shard_map/dot_general | solution.py:170
  572.3 5.7 fusion.31
  579.0 12.6 %all-reduce.5 = (bf16[768]{0:T(1024)(128)(2,1)S(1)}, bf16[768]{0:T(1024)(128)(2,1)S(1)}) all-reduce(bf16[768]{0:T(1024)(128)(2,1)S(1)} %get-tuple-element.13, bf16[768]{0:T(1024)(128)(2,1)S(1)} %get-tuple-element.9), channel_id=5, replica_groups=mesh['expert'=4,'shard'=8] {'shard'}, use_global_device_ids=true, to_apply=%region_33.34.clone | all-reduce | flops 1536 | bytes 6144
  591.8 9.4 %all-reduce.7 = (bf16[96,4]{0,1:T(4,128)(2,1)S(1)}, bf16[96]{0:T(256)(128)(2,1)S(1)}, bf16[96]{0:T(256)(128)(2,1)S(1)}) all-reduce(bf16[96,4]{0,1:T(4,128)(2,1)S(1)} %copy.140, bf16[96]{0:T(256)(128)(2,1)S(1)} %dynamic-slice.3, bf16[96]{0:T(256)(128)(2,1)S(1)} %dynamic-slice.5), channel_id=1, replica_groups=mesh['expert'=4,'shard'=8] {'expert'}, use_global_device_ids=true, to_apply=%region_31.32 | all-reduce | flops 576 | bytes 2304 | tf_op jit(solution)/shard_map/psum | solution.py:273
  602.8 3.1 add_convert_fusion.1
  605.9 45.2 %reduce-scatter.14.cloned.1.call-done = bf16[1,384,768]{2,1,0:T(8,128)(2,1)} async-done(((bf16[1,3072,768]{2,1,0:T(8,128)(2,1)}), bf16[1,384,768]{2,1,0:T(8,128)(2,1)}) %reduce-scatter.14.cloned.1.call-update) | async-done | bytes 589840 | tf_op jit(solution)/shard_map/reduce_scatter | solution.py:249
  651.1 2.2 convert_element_type.200
  653.3 55.1 %reduce-scatter.12.cloned.1.call-done = bf16[1,96,3072]{2,1,0:T(8,128)(2,1)} async-done(((bf16[1,768,3072]{2,1,0:T(8,128)(2,1)}), bf16[1,96,3072]{2,1,0:T(8,128)(2,1)}) %reduce-scatter.12.cloned.1.call-update) | async-done | bytes 589840 | tf_op jit(solution)/shard_map/reduce_scatter | solution.py:246
  708.4 2.2 convert_element_type.197
  710.6 39.9 %all-reduce.11.cloned.1.call-done = (bf16[96,2304]{1,0:T(8,128)(2,1)}, bf16[96,768]{1,0:T(8,128)(2,1)}) async-done(((bf16[96,2304]{1,0:T(8,128)(2,1)}, bf16[96,768]{1,0:T(8,128)(2,1)}), (bf16[96,2304]{1,0:T(8,128)(2,1)}, bf16[96,768]{1,0:T(8,128)(2,1)})) %all-reduce.11.cloned.1.call-update) | async-done | bytes 589840 | tf_op jit(solution)/shard_map/psum | solution.py:271
  750.5 2.0 convert_element_type.186
  752.4 1.6 convert_element_type.188
  (188 shorter events, 26.2 us)
Async XLA Ops:
  7.2 25.7 %copy-start.31 = (s32[591,2]{0,1:T(2,128)S(1)}, s32[591,2]{0,1:T(2,128)}, u32[]{:S(2)}) copy-start(s32[591,2]{0,1:T(2,128)} %param.13) | copy-start | bytes 14188
  7.2 26.3 %copy-start.5 = (bf16[591,768]{1,0:T(8,128)(2,1)S(1)}, bf16[591,768]{1,0:T(8,128)(2,1)}, u32[]{:S(2)}) copy-start(bf16[591,768]{1,0:T(8,128)(2,1)} %param.11) | copy-start | bytes 2723332
  7.2 39.4 %all-gather.6.cloned.1.call-start = ((), (), s32[]{:S(2)}) async-start(), calls=%async_computation.9 | async-start | bytes 3981312 | tf_op jit(solution)/shard_map/all_gather | solution.py:56
  7.9 84.4 %all-gather.8.cloned.1.call-start = ((), (), s32[]{:S(2)}) async-start(), calls=%async_computation.10 | async-start | bytes 1327104 | tf_op jit(solution)/shard_map/all_gather | solution.py:57
  8.7 109.8 %all-gather.10.cloned.1.call-start = ((), (), s32[]{:S(2)}) async-start(), calls=%async_computation.11 | async-start | bytes 5308416 | tf_op jit(solution)/shard_map/all_gather | solution.py:65
  28.6 23.9 %copy-start.39 = (f32[768]{0:T(1024)}, f32[768]{0:T(1024)S(1)}, u32[]{:S(2)}) copy-start(f32[768]{0:T(1024)S(1)} %convert_element_type.161) | copy-start | bytes 9220
  28.6 74.7 %copy-start.27 = (f32[768]{0:T(1024)}, f32[768]{0:T(1024)S(1)}, u32[]{:S(2)}) copy-start(f32[768]{0:T(1024)S(1)} %convert_element_type.168) | copy-start | bytes 9220
  33.5 61.8 %copy-start.44 = (s32[591]{0:T(1024)}, s32[591]{0:T(1024)S(1)}, u32[]{:S(2)}) copy-start(s32[591]{0:T(1024)S(1)} %get-tuple-element.16) | copy-start | bytes 7096
  33.5 69.8 %copy-start.43 = (s32[591]{0:T(1024)}, s32[591]{0:T(1024)S(1)}, u32[]{:S(2)}) copy-start(s32[591]{0:T(1024)S(1)} %get-tuple-element.15) | copy-start | bytes 7096
  33.8 18.8 %copy-start.33 = (f32[591]{0:T(1024)}, f32[591]{0:T(1024)S(1)}, u32[]{:S(2)}) copy-start(f32[591]{0:T(1024)S(1)} %broadcast_multiply_fusion.3) | copy-start | bytes 7096
  34.2 18.4 %copy-start.35 = (f32[591]{0:T(1024)}, f32[591]{0:T(1024)S(1)}, u32[]{:S(2)}) copy-start(f32[591]{0:T(1024)S(1)} %fusion.30) | copy-start | bytes 7096
  34.2 18.4 %copy-start.41 = (f32[591]{0:T(1024)}, f32[591]{0:T(1024)S(1)}, u32[]{:S(2)}) copy-start(f32[591]{0:T(1024)S(1)} %fusion.62) | copy-start | bytes 7096
  80.8 5.1 copy-start.7
  84.2 2.9 copy-start
  87.1 0.6 copy-start.22
  94.9 8.4 %copy-start.1 = (f32[591,768]{1,0:T(8,128)}, f32[591,768]{1,0:T(8,128)S(1)}, u32[]{:S(2)}) copy-start(f32[591,768]{1,0:T(8,128)S(1)} %get-tuple-element.42) | copy-start | bytes 5446660
  95.0 8.4 %copy-start.25 = (f32[591]{0:T(1024)}, f32[591]{0:T(1024)S(1)}, u32[]{:S(2)}) copy-start(f32[591]{0:T(1024)S(1)} %broadcast_multiply_fusion.2) | copy-start | bytes 7096
  95.3 17.9 %copy-start.37 = (f32[591]{0:T(1024)}, f32[591]{0:T(1024)S(1)}, u32[]{:S(2)}) copy-start(f32[591]{0:T(1024)S(1)} %multiply_reduce_fusion.6) | copy-start | bytes 7096
  95.3 17.9 %copy-start.29 = (f32[591]{0:T(1024)}, f32[591]{0:T(1024)S(1)}, u32[]{:S(2)}) copy-start(f32[591]{0:T(1024)S(1)} %fusion.63) | copy-start | bytes 7096
  113.2 57.8 %all-to-all-start = ((bf16[4,376,768]{2,1,0:T(8,128)(2,1)}), bf16[4,376,768]{2,1,0:T(8,128)(2,1)S(1)}, u32[]{:S(2)}, u32[]{:S(2)}) async-start(bf16[4,376,768]{2,1,0:T(8,128)(2,1)} %bitcast.121), calls=%async_computation | async-start | bytes 4620288 | tf_op jit(solution)/shard_map/all_to_all | solution.py:115
  117.9 101.1 %all-gather.12.cloned.1.call-start = ((), (), s32[]{:S(2)}) async-start(), calls=%async_computation.12 | async-start | bytes 5308416 | tf_op jit(solution)/shard_map/all_gather | solution.py:66
  171.0 47.9 %copy-start.18 = (bf16[4,376,768]{2,1,0:T(8,128)(2,1)}, bf16[4,376,768]{2,1,0:T(8,128)(2,1)S(1)}, u32[]{:S(2)}) copy-start(bf16[4,376,768]{2,1,0:T(8,128)(2,1)S(1)} %all-to-all-done) | copy-start | bytes 6930436
  231.2 3.8 copy-start.45
  231.2 15.7 %copy-start.15 = (bf16[591,768]{1,0:T(8,128)(2,1)S(1)}, bf16[591,768]{1,0:T(8,128)(2,1)}, u32[]{:S(2)}) copy-start(bf16[591,768]{1,0:T(8,128)(2,1)} %param.21) | copy-start | bytes 2723332
  231.2 56.1 %all-to-all-start.1 = ((bf16[4,376,768]{2,1,0:T(8,128)(2,1)}), bf16[4,376,768]{2,1,0:T(8,128)(2,1)S(1)}, u32[]{:S(2)}, u32[]{:S(2)}) async-start(bf16[4,376,768]{2,1,0:T(8,128)(2,1)} %bitcast.128), calls=%async_computation.1 | async-start | bytes 4620288 | tf_op jit(solution)/shard_map/all_to_all | solution.py:130
  235.0 13.5 %copy-start.26 = (f32[591]{0:T(1024)S(1)}, f32[591]{0:T(1024)}, u32[]{:S(2)}) copy-start(f32[591]{0:T(1024)} %copy-done.25) | copy-start | bytes 7096
  235.0 13.5 %copy-start.28 = (f32[768]{0:T(1024)S(1)}, f32[768]{0:T(1024)}, u32[]{:S(2)}) copy-start(f32[768]{0:T(1024)} %copy-done.27) | copy-start | bytes 9220
  235.0 13.5 %copy-start.30 = (f32[591]{0:T(1024)S(1)}, f32[591]{0:T(1024)}, u32[]{:S(2)}) copy-start(f32[591]{0:T(1024)} %copy-done.29) | copy-start | bytes 7096
  246.1 2.4 copy-start.2
  248.5 0.7 copy-start.32
  292.1 5.2 copy-start.13
  372.4 23.0 %copy-start.20 = (bf16[4,376,768]{2,1,0:T(8,128)(2,1)}, bf16[4,376,768]{2,1,0:T(8,128)(2,1)S(1)}, u32[]{:S(2)}) copy-start(bf16[4,376,768]{2,1,0:T(8,128)(2,1)S(1)} %all_to_all.20) | copy-start | bytes 6930436
  407.7 55.7 %all-to-all-start.3 = ((bf16[4,376,768]{2,1,0:T(8,128)(2,1)}), bf16[4,376,768]{2,1,0:T(8,128)(2,1)S(1)}, u32[]{:S(2)}, u32[]{:S(2)}) async-start(bf16[4,376,768]{2,1,0:T(8,128)(2,1)} %bitcast.127), calls=%async_computation.3 | async-start | bytes 4620288 | tf_op jit(solution)/shard_map/all_to_all | solution.py:176
  411.4 160.1 %reduce-scatter.16.cloned.1.call-start = ((), (), s32[]{:S(2)}) async-start(), calls=%async_computation.17 | async-start | bytes 221184
  412.6 190.2 %reduce-scatter.10.cloned.1.call-start = ((), (), s32[]{:S(2)}) async-start(), calls=%async_computation.14 | async-start | bytes 1327104 | tf_op jit(solution)/shard_map/reduce_scatter | solution.py:257
  473.3 7.7 %copy-start.3 = (f32[591,768]{1,0:T(8,128)S(1)}, f32[591,768]{1,0:T(8,128)}, u32[]{:S(2)}) copy-start(f32[591,768]{1,0:T(8,128)} %copy-done.1) | copy-start | bytes 5446660
  481.0 2.6 copy-start.38
  481.0 2.6 copy-start.14
  483.6 3.0 copy-start.16
  483.6 3.0 copy-start.46
  485.4 1.2 copy-start.11
  490.5 4.7 copy-start.23
  490.5 10.9 %slice-start = ((s8[7372800]{0:T(1024)(128)(4,1)}), s8[3178496]{0:T(1024)(128)(4,1)S(1)}, s32[]{:S(2)}) async-start(s8[7372800]{0:T(1024)(128)(4,1)} %bitcast.117), calls=%async_computation.19 | async-start | bytes 6356992
  495.3 6.1 slice-start.1
  501.4 3.6 copy-start.12
  501.4 3.6 copy-start.17
  501.4 3.6 copy-start.24
  505.1 2.4 copy-start.10
  507.4 3.1 copy-start.9
  507.4 95.4 %reduce-scatter.8.cloned.1.call-start = ((), (), s32[]{:S(2)}) async-start(), calls=%async_computation.13 | async-start | bytes 3981312 | tf_op jit(solution)/shard_map/reduce_scatter | solution.py:254
  507.5 3.5 copy-start.4
  511.0 1.3 copy-start.8
  523.6 10.1 %copy-start.6 = (bf16[591,768]{1,0:T(8,128)(2,1)S(1)}, bf16[591,768]{1,0:T(8,128)(2,1)}, u32[]{:S(2)}) copy-start(bf16[591,768]{1,0:T(8,128)(2,1)} %param.11) | copy-start | bytes 2723332
  523.6 10.1 %copy-start.34 = (f32[591]{0:T(1024)S(1)}, f32[591]{0:T(1024)}, u32[]{:S(2)}) copy-start(f32[591]{0:T(1024)} %copy-done.33) | copy-start | bytes 7096
  523.6 10.1 %copy-start.40 = (f32[768]{0:T(1024)S(1)}, f32[768]{0:T(1024)}, u32[]{:S(2)}) copy-start(f32[768]{0:T(1024)} %copy-done.39) | copy-start | bytes 9220
  523.6 10.1 %copy-start.42 = (f32[591]{0:T(1024)S(1)}, f32[591]{0:T(1024)}, u32[]{:S(2)}) copy-start(f32[591]{0:T(1024)} %copy-done.41) | copy-start | bytes 7096
  540.5 1.7 copy-start.21
  540.6 110.5 %reduce-scatter.14.cloned.1.call-start = ((), (), s32[]{:S(2)}) async-start(), calls=%async_computation.16 | async-start | bytes 5308416 | tf_op jit(solution)/shard_map/reduce_scatter | solution.py:249
  555.6 1.8 copy-start.19
  555.6 152.8 %reduce-scatter.12.cloned.1.call-start = ((), (), s32[]{:S(2)}) async-start(), calls=%async_computation.15 | async-start | bytes 5308416 | tf_op jit(solution)/shard_map/reduce_scatter | solution.py:246
  570.6 179.9 %all-reduce.11.cloned.1.call-start = ((), (), s32[]{:S(2)}) async-start(), calls=%async_computation.18 | async-start | bytes 1179648 | tf_op jit(solution)/shard_map/psum | solution.py:271
  572.3 5.7 copy-start.36
Sparse Core Ops, SparseCore 0:
  9.9 36.6 all-gather.5
  48.5 23.9 all-gather.7
  74.3 38.7 all-gather.9
  120.3 39.2 all-gather.11
  415.5 34.0 reduce-scatter.15
  507.5 34.7 reduce-scatter.9
  545.9 48.0 reduce-scatter.7
  597.4 53.7 reduce-scatter.13
  654.6 53.7 reduce-scatter.11
  710.7 39.7 all-reduce.10
where the time goes:
time: 769 us; the launch traced here: 761 us
  waiting for transfers between devices  297 us (39%)
  matrix products  170 us (22%)
  local copies, waits for them, and re-layouts  105 us (14%)
  blocking collectives  102 us (13%)
  other arithmetic  58.8 us (8%)
  between operations  17.1 us (2%)
  starting transfers between devices  12.6 us (2%)
    reduce_scatter x1, waiting for transfers between devices, shards(): lax.psum_scatter(grad_first[None].astype(jnp.bfloat16), 'shard', scatter_...  55.1 us
    all_to_all x1, blocking collectives, shards(): lax.all_to_all(back_out.reshape(experts, capacity, width), 'expert', spli...  55 us
    all_to_all x1, waiting for transfers between devices, shards(): lax.all_to_all(outgoing, 'expert', split_axis=0, concat_axis=0, tiled=True)  52.6 us
    all_to_all x1, waiting for transfers between devices, shards(): lax.all_to_all(row_grad.reshape(experts, capacity, width), 'expert', spli...  50.7 us
    dot_general x1, matrix products, shards(): jnp.dot(flat_rows, expert_first, preferred_element_type=jnp.float32)  47.9 us
    reduce_scatter x1, waiting for transfers between devices, shards(): lax.psum_scatter(grad_second[None].astype(jnp.bfloat16), 'shard', scatter...  45.2 us
    psum x1, waiting for transfers between devices, shards(): lax.psum(shares[0].astype(jnp.bfloat16), 'expert').astype(jnp.float32)  39.9 us
    all_to_all x1, waiting for transfers between devices, shards(): lax.all_to_all(produced, 'expert', split_axis=0, concat_axis=0, tiled=True)  38 us
  transfers between devices with their start and end apart: 13, of which 7 were waited for; matrix products, arithmetic and copies ran while one was open for 32% of the time, Pallas kernels for 0%

commit v1 on v0

v1 whole, which is shorter than its diff:
```python
import jax
import jax.numpy as jnp
from jax import lax
from jax.sharding import PartitionSpec as P

H = 12
HD = 64
SEQ = 197


EPSILON = 1e-06
ROW_CONTRACT = (((0,), (0,)), ((), ()))
COL_CONTRACT = (((1,), (1,)), ((), ()))


def layer_norm(values, norm_gain):
    row_mean = jnp.mean(values, axis=-1, keepdims=True)
    centered = values - row_mean
    variance = jnp.mean(centered * centered, axis=-1, keepdims=True)
    return centered * lax.rsqrt(variance + EPSILON) * norm_gain


def normalize_rows(scores):
    row_top = jnp.max(scores, axis=-1, keepdims=True)
    exp_scores = jnp.exp(scores - row_top)
    return exp_scores / jnp.sum(exp_scores, axis=-1, keepdims=True)


def gelu_exact(values):
    return jax.nn.gelu(values, approximate=False)


def shards(
    tokens,
    image_counts,
    routes,
    w_qkv,
    w_out,
    w_router,
    gain_attn,
    gain_moe,
    w_in,
    w_back,
    cotangent,
):
    rows, width = tokens.shape
    experts = lax.axis_size("expert")
    capacity = 8 * (5 * rows // (16 * experts)) + 8
    overflow = experts * capacity
    images = rows // SEQ
    qkv_cols = w_qkv.shape[1]
    n_route = w_router.shape[1]
    ff = w_in.shape[2]
    score_scale = HD ** (-0.5)
    row_ids = jnp.arange(rows, dtype=jnp.int32)
    live_int = (row_ids // SEQ < image_counts[0, 0]).astype(jnp.int32)
    live_rows = live_int.astype(jnp.float32)

    dense_local = jnp.concatenate(
        [w_qkv, w_out, w_router, gain_attn[:, None], gain_moe[:, None]], axis=1
    )
    dense_full = lax.all_gather(dense_local, "shard", axis=0, tiled=True)
    full_qkv = dense_full[:, :qkv_cols]
    full_out = dense_full[:, qkv_cols : qkv_cols + width]
    full_router = dense_full[:, qkv_cols + width : qkv_cols + width + n_route]
    gain_one = dense_full[:, -2].astype(jnp.float32)
    gain_two = dense_full[:, -1].astype(jnp.float32)

    back_rows = w_back.shape[1]
    expert_local = jnp.stack(
        [w_in[0], w_back[0].reshape(back_rows * width // ff, ff)], axis=0
    )
    expert_full = lax.all_gather(expert_local, "shard", axis=1, tiled=True)
    expert_first = expert_full[0]
    expert_second = expert_full[1].reshape(ff, width)

    token_f = tokens.astype(jnp.float32)
    attn_in = layer_norm(token_f, gain_one).astype(jnp.bfloat16)
    projected = jnp.dot(attn_in, full_qkv, preferred_element_type=jnp.float32).astype(jnp.bfloat16)
    split_heads = projected.reshape(images, SEQ, 3, H, HD)
    queries = split_heads[:, :, 0]
    keys_part = split_heads[:, :, 1]
    values_part = split_heads[:, :, 2]
    scores = (
        jnp.einsum("ishd,ithd->ihst", queries, keys_part, preferred_element_type=jnp.float32)
        * score_scale
    )
    row_top = jnp.max(scores, axis=-1, keepdims=True)
    log_total = row_top + jnp.log(jnp.sum(jnp.exp(scores - row_top), axis=-1, keepdims=True))
    attn_probs = jnp.exp(scores - log_total)
    probs_low = attn_probs.astype(jnp.bfloat16)
    mixed_rows = (
        jnp.einsum(
            "ihst,ithd->ishd",
            probs_low,
            values_part,
            preferred_element_type=jnp.float32,
        )
        .reshape(rows, width)
        .astype(jnp.bfloat16)
    )
    hidden_state = token_f + jnp.dot(mixed_rows, full_out, preferred_element_type=jnp.float32)
    moe_in = layer_norm(hidden_state, gain_two).astype(jnp.bfloat16)
    logits = jnp.dot(moe_in, full_router, preferred_element_type=jnp.float32)
    router_probs = normalize_rows(logits)
    expert_ids = jnp.arange(experts, dtype=jnp.int32)
    choose = (routes[:, :, None] == expert_ids).astype(jnp.float32)
    chosen = jnp.sum(choose * router_probs[:, None, :], axis=2)
    pick_table = (routes[:, :, None] == expert_ids).astype(jnp.int32) * live_int[:, None, None]
    flat_picks = pick_table.reshape(rows * 2, experts)
    before = jnp.cumsum(flat_picks, axis=0) - flat_picks
    slot_index = jnp.sum(before * flat_picks, axis=1).reshape(rows, 2)
    position = jnp.where(live_int[:, None] > 0, routes * capacity + slot_index, overflow)

    slot_ids = jnp.arange(overflow, dtype=jnp.int32)[:, None]
    take_first = (slot_ids == position[None, :, 0]).astype(jnp.bfloat16)
    take_second = (slot_ids == position[None, :, 1]).astype(jnp.bfloat16)

    grad_out = cotangent.astype(jnp.float32) * live_rows[:, None]
    weighted = chosen * live_rows[:, None]
    grad_picked = (weighted[:, :, None] * grad_out[:, None, :]).astype(jnp.bfloat16)

    sent_rows = jnp.dot(
        take_first + take_second, moe_in, preferred_element_type=jnp.float32
    ).astype(jnp.bfloat16)
    sent_grad = (
        jnp.dot(take_first, grad_picked[:, 0], preferred_element_type=jnp.float32)
        + jnp.dot(take_second, grad_picked[:, 1], preferred_element_type=jnp.float32)
    ).astype(jnp.bfloat16)
    outgoing = jnp.concatenate([sent_rows, sent_grad], axis=1).reshape(
        experts, capacity, 2 * width
    )
    arrived = lax.all_to_all(outgoing, "expert", split_axis=0, concat_axis=0, tiled=True)
    arrived = arrived.reshape(overflow, 2 * width)
    flat_arrived = arrived[:, :width]
    flat_grad = arrived[:, width:]

    pre_act = jnp.dot(flat_arrived, expert_first, preferred_element_type=jnp.float32)
    activated, gelu_back = jax.vjp(gelu_exact, pre_act)
    activated = activated.astype(jnp.bfloat16)
    produced = jnp.dot(activated, expert_second, preferred_element_type=jnp.float32).astype(
        jnp.bfloat16
    )
    hidden_grad = lax.dot_general(
        flat_grad, expert_second, COL_CONTRACT, preferred_element_type=jnp.float32
    )
    pre_grad = gelu_back(hidden_grad)[0].astype(jnp.bfloat16)
    row_grad = lax.dot_general(
        pre_grad, expert_first, COL_CONTRACT, preferred_element_type=jnp.float32
    ).astype(jnp.bfloat16)
    grad_second = lax.dot_general(
        activated, flat_grad, ROW_CONTRACT, preferred_element_type=jnp.float32
    )
    grad_first = lax.dot_general(
        flat_arrived, pre_grad, ROW_CONTRACT, preferred_element_type=jnp.float32
    )
    expert_grads = jnp.stack(
        [grad_first, grad_second.reshape(width, ff)], axis=0
    ).astype(jnp.bfloat16)
    expert_share = lax.psum_scatter(
        expert_grads, "shard", scatter_dimension=1, tiled=True
    ).astype(jnp.float32)
    grad_in_share = expert_share[0][None]
    grad_back_share = expert_share[1].reshape(back_rows, width)[None]

    returning = jnp.concatenate([produced, row_grad], axis=1).reshape(
        experts, capacity, 2 * width
    )
    returned = lax.all_to_all(returning, "expert", split_axis=0, concat_axis=0, tiled=True)
    returned = returned.reshape(overflow, 2 * width)
    picked_first = lax.dot_general(
        take_first, returned, ROW_CONTRACT, preferred_element_type=jnp.float32
    )
    picked_second = lax.dot_general(
        take_second, returned, ROW_CONTRACT, preferred_element_type=jnp.float32
    )
    moe_out = (
        weighted[:, 0:1] * picked_first[:, :width] + weighted[:, 1:2] * picked_second[:, :width]
    )
    output = (live_rows[:, None] * (hidden_state + moe_out)).astype(jnp.bfloat16)
    grad_chosen = jnp.stack(
        [
            jnp.sum(grad_out * picked_first[:, :width], axis=1),
            jnp.sum(grad_out * picked_second[:, :width], axis=1),
        ],
        axis=1,
    ) * live_rows[:, None]
    expert_part = (picked_first[:, width:] + picked_second[:, width:]) * live_rows[:, None]
    prob_sum = jnp.sum(choose * grad_chosen[:, :, None], axis=1)
    logit_grad = (
        router_probs * (prob_sum - jnp.sum(router_probs * prob_sum, axis=-1, keepdims=True))
    ).astype(jnp.bfloat16)
    grad_router = lax.dot_general(
        moe_in, logit_grad, ROW_CONTRACT, preferred_element_type=jnp.float32
    )
    moe_in_grad = expert_part + lax.dot_general(
        logit_grad, full_router, COL_CONTRACT, preferred_element_type=jnp.float32
    )
    norm_value, norm_back = jax.vjp(layer_norm, hidden_state, gain_two)
    state_part, grad_gain_two = norm_back(moe_in_grad)
    state_grad = grad_out + state_part
    branch_grad = state_grad.astype(jnp.bfloat16)
    grad_wout = lax.dot_general(
        mixed_rows, branch_grad, ROW_CONTRACT, preferred_element_type=jnp.float32
    )
    mixed_grad = lax.dot_general(
        branch_grad, full_out, COL_CONTRACT, preferred_element_type=jnp.float32
    )
    mixed_grad = mixed_grad.astype(jnp.bfloat16).reshape(images, SEQ, H, HD)
    grad_values = jnp.einsum(
        "ihst,ishd->ithd",
        probs_low,
        mixed_grad,
        preferred_element_type=jnp.float32,
    )
    prob_grad = jnp.einsum(
        "ishd,ithd->ihst", mixed_grad, values_part, preferred_element_type=jnp.float32
    )
    score_grad = (
        attn_probs * (prob_grad - jnp.sum(attn_probs * prob_grad, axis=-1, keepdims=True))
    ).astype(jnp.bfloat16)
    grad_queries = (
        jnp.einsum("ihst,ithd->ishd", score_grad, keys_part, preferred_element_type=jnp.float32)
        * score_scale
    )
    grad_keys = (
        jnp.einsum("ihst,ishd->ithd", score_grad, queries, preferred_element_type=jnp.float32)
        * score_scale
    )
    projected_grad = (
        jnp.stack([grad_queries, grad_keys, grad_values], axis=2)
        .reshape(rows, 3 * width)
        .astype(jnp.bfloat16)
    )
    grad_qkv = lax.dot_general(
        attn_in, projected_grad, ROW_CONTRACT, preferred_element_type=jnp.float32
    )
    attn_in_grad = lax.dot_general(
        projected_grad, full_qkv, COL_CONTRACT, preferred_element_type=jnp.float32
    )
    first_value, first_back = jax.vjp(layer_norm, token_f, gain_one)
    token_part, grad_gain_one = first_back(attn_in_grad)
    grad_tokens = (state_grad + token_part).astype(jnp.bfloat16)

    dense_grads = jnp.concatenate(
        [grad_qkv, grad_wout, grad_router, grad_gain_one[:, None], grad_gain_two[:, None]],
        axis=1,
    ).astype(jnp.bfloat16)
    dense_share = lax.psum_scatter(dense_grads, "shard", scatter_dimension=0, tiled=True)
    dense_total = lax.psum(dense_share, "expert").astype(jnp.float32)
    return (
        output,
        grad_tokens,
        dense_total[:, :qkv_cols],
        dense_total[:, qkv_cols : qkv_cols + width],
        dense_total[:, qkv_cols + width : qkv_cols + width + n_route],
        dense_total[:, -2],
        dense_total[:, -1],
        grad_in_share,
        grad_back_share,
    )


def solution(mesh):
    return jax.shard_map(
        shards,
        mesh=mesh,
        in_specs=(
            P(("expert", "shard"), None),
            P("expert", "shard"),
            P(("expert", "shard"), None),
            P("shard", None),
            P("shard", None),
            P("shard", None),
            P("shard"),
            P("shard"),
            P("expert", "shard", None),
            P("expert", "shard", None),
            P(("expert", "shard"), None),
        ),
        out_specs=(
            P(("expert", "shard"), None),
            P(("expert", "shard"), None),
            P("shard", None),
            P("shard", None),
            P("shard", None),
            P("shard"),
            P("shard"),
            P("expert", "shard", None),
            P("expert", "shard", None),
        ),
        check_vma=False,
    )
```

time: 769 us -> 711 us (0.925)
  blocking collectives: 102 us -> 0 us
  waiting for transfers between devices: 297 us -> 349 us
  other arithmetic: 58.8 us -> 35.9 us
  matrix products: 170 us -> 178 us
    all_to_all x1 -> x0, blocking collectives: 55 us -> none  [shards(): lax.all_to_all(back_out.reshape(experts, capacity, width), 'expert', spli...]
    all_to_all x1, waiting for transfers between devices: 52.6 us -> 89.7 us  [shards(): lax.all_to_all(outgoing, 'expert', split_axis=0, concat_axis=0, tiled=True)]
    unnamed x2 -> x0, blocking collectives: 28.1 us -> none
    all_gather x4 -> x2, waiting for transfers between devices: 12.4 us -> 32.8 us  [the longest x1 32.8 us: shards(): dense_full = lax.all_gather(dense_local, 'shard', axis=0, tiled=True)]
    another operation x0 -> x7, local copies, waits for them, and re-layouts: none -> 20 us  [the longest x1 8.48 us: shards(): jnp.stack([grad_first, grad_second.reshape(width, ff)], axis=0)]
    scatter x2 -> x0, other arithmetic: 17.9 us -> none  [shards(): outgoing = outgoing.at[position[:, 0]].set(moe_in, mode='drop').at[positi...]
    scatter x2 -> x0, local copies, waits for them, and re-layouts: 14.5 us -> none  [shards(): back_out = back_out.at[position[:, 0]].set(grad_picked[:, 0], mode='drop'...]
    reduce_scatter x4 -> x2, waiting for transfers between devices: 100 us -> 86 us  [the longest x1 80 us: shards(): lax.psum_scatter(expert_grads, 'shard', scatter_dimension=1, tiled=True)]
  transfers between devices with their start and end apart: 13 -> 7, of which waited for: 7 -> 6; matrix products, arithmetic and copies ran while one was open for 32% -> 19% of each run, Pallas kernels for 0% -> 0%
where the time goes in v1:
time: 711 us; the launch traced here: 696 us
  waiting for transfers between devices  349 us (49%)
  matrix products  178 us (25%)
  local copies, waits for them, and re-layouts  107 us (15%)
  other arithmetic  35.9 us (5%)
  between operations  15.7 us (2%)
  starting transfers between devices  10.4 us (1%)
    all_to_all x1, waiting for transfers between devices, shards(): lax.all_to_all(returning, 'expert', split_axis=0, concat_axis=0, tiled=True)  102 us
    all_to_all x1, waiting for transfers between devices, shards(): lax.all_to_all(outgoing, 'expert', split_axis=0, concat_axis=0, tiled=True)  89.7 us
    reduce_scatter x1, waiting for transfers between devices, shards(): lax.psum_scatter(expert_grads, 'shard', scatter_dimension=1, tiled=True)  80 us
    dot_general x1, matrix products, shards(): jnp.dot(flat_arrived, expert_first, preferred_element_type=jnp.float32)  48.2 us
    psum x1, waiting for transfers between devices, shards(): dense_total = lax.psum(dense_share, 'expert').astype(jnp.float32)  38.2 us
    all_gather x1, waiting for transfers between devices, shards(): dense_full = lax.all_gather(dense_local, 'shard', axis=0, tiled=True)  32.8 us
    dot_general x1, matrix products, shards(): lax.dot_general(flat_grad, expert_second, COL_CONTRACT, preferred_element...  22.7 us
    unnamed x125, local copies, waits for them, and re-layouts  19.5 us
  transfers between devices with their start and end apart: 7, of which 6 were waited for; matrix products, arithmetic and copies ran while one was open for 19% of the time, Pallas kernels for 0%

profile of v1, /device:TPU:0, one launch (start us, length us, event | category | flops | bytes accessed | tf_op | source)
XLA Modules:
  0.0 696.5 jit_solution(6221771275941900297)
XLA Ops:
  9.6 1.9 concatenate.17
  11.6 1.5 stack_reshape_squeeze.3
  13.2 2.3 pad_maximum_fusion.4
  19.8 1.5 convert_multiply_fusion
  21.3 32.8 %all-gather.3.cloned.1.call-done = bf16[768,3078]{1,0:T(8,128)(2,1)} async-done(((bf16[96,3078]{1,0:T(8,128)(2,1)}), bf16[768,3078]{1,0:T(8,128)(2,1)}) %all-gather.3.cloned.1.call-update) | async-done | bytes 4727824 | tf_op jit(solution)/shard_map/all_gather | solution.py:62
  55.4 6.0 convolution_convert_fusion.3
  61.4 9.3 %reshape.238 = bf16[3,197,3,12,64]{4,3,2,1,0:T(8,128)(2,1)} reshape(bf16[591,2304]{1,0:T(8,128)(2,1)} %convolution_convert_fusion.3) | data formatting | bytes 5446656 | tf_op jit(solution)/shard_map/reshape | solution.py:80
  70.7 6.6 fusion.84
  77.3 4.2 copy.148
  81.5 4.2 copy.149
  85.7 3.7 copy.147
  89.5 3.3 multiply_reduce_fusion.1
  92.8 1.5 exponential_reduce_fusion
  94.3 1.4 copy-done
  95.7 1.6 fusion.47
  98.3 2.3 convert_element_type.137
  100.6 2.6 fusion.86
  104.7 1.5 fusion.87
  107.2 2.0 fusion.11
  109.3 2.3 convolution_convert_fusion.5
  111.6 2.1 add_convert_fusion.1
  113.7 2.5 pad_maximum_fusion.1
  116.1 5.2 all-to-all-start
  121.4 4.9 slice.147
  126.2 8.5 %reshape_squeeze.3 = bf16[3072,768]{1,0:T(8,128)(2,1)} reshape(bf16[1,768,3072]{2,1,0:T(8,128)(2,1)} %slice.147) | data formatting | bytes 9437184 | tf_op jit(solution)/shard_map/reshape;squeeze | solution.py:75
  134.7 89.7 %all-to-all-done = bf16[4,376,1536]{2,1,0:T(8,128)(2,1)} async-done(((bf16[4,376,1536]{2,1,0:T(8,128)(2,1)}), bf16[4,376,1536]{2,1,0:T(8,128)(2,1)}, u32[]{:S(2)}, u32[]{:S(2)}) %all-to-all-start) | async-done | bytes 4620320 | tf_op jit(solution)/shard_map/all_to_all | solution.py:133
  224.4 48.2 %multiply_convert_fusion = (bf16[1504,3072]{1,0:T(8,128)(2,1)S(1)}, f32[1504,3072]{1,0:T(8,128)}, f32[1504,3072]{1,0:T(8,128)}) fusion(bf16[2,768,3072]{2,1,0:T(8,128)(2,1)} %all-gather.5.cloned.1.call-done, bf16[1504,1536]{1,0:T(8,128)(2,1)} %bitcast.11), kind=kOutput, calls=%fused_computation.3 | convolution fusion | flops 7397081088 | bytes 53231616 | tf_op jit(solution)/shard_map/dot_general | solution.py:138
  272.5 7.6 %convolution_convert_fusion.4 = bf16[1504,768]{1,0:T(8,128)(2,1)S(1)} fusion(bf16[1504,3072]{1,0:T(8,128)(2,1)S(1)} %get-tuple-element.70, bf16[3072,768]{1,0:T(8,128)(2,1)S(1)} %copy-done.18), kind=kOutput, calls=%fused_computation.46 | convolution fusion | flops 7097917440 | bytes 16269312 | tf_op jit(solution)/shard_map/dot_general | solution.py:141
  280.1 22.7 %add_convert_fusion = bf16[1504,3072]{1,0:T(8,128)(2,1)} fusion(f32[1504,3072]{1,0:T(8,128)} %get-tuple-element.71, f32[1504,3072]{1,0:T(8,128)} %get-tuple-element.84, bf16[3072,768]{1,0:T(8,128)(2,1)S(1)} %copy-done.18, bf16[1504,1536]{1,0:T(8,128)(2,1)} %bitcast.11), kind=kOutput, calls=%fused_computation.2 | convolution fusion | flops 7161446400 | bytes 53231616 | tf_op jit(solution)/shard_map/dot_general | solution.py:144
  302.9 11.3 %fusion.16 = bf16[1504,768]{1,0:T(8,128)(2,1)S(1)} fusion(bf16[1504,3072]{1,0:T(8,128)(2,1)} %add_convert_fusion, bf16[2,768,3072]{2,1,0:T(8,128)(2,1)} %all-gather.5.cloned.1.call-done), kind=kOutput, calls=%fused_computation.45 | convolution fusion | flops 7097917440 | bytes 16269312 | tf_op jit(solution)/shard_map/dot_general | solution.py:148
  314.2 2.5 pad_maximum_fusion.2
  316.7 5.1 all-to-all-start.1
  321.9 102.1 %all-to-all-done.1 = bf16[4,376,1536]{2,1,0:T(8,128)(2,1)} async-done(((bf16[4,376,1536]{2,1,0:T(8,128)(2,1)}), bf16[4,376,1536]{2,1,0:T(8,128)(2,1)}, u32[]{:S(2)}, u32[]{:S(2)}) %all-to-all-start.1) | async-done | bytes 4620320 | tf_op jit(solution)/shard_map/all_to_all | solution.py:169
  424.0 5.6 fusion.10
  429.6 5.6 fusion.13
  435.3 1.8 multiply_reduce_fusion.5
  437.5 2.0 multiply_reduce_fusion.2
  440.7 2.1 convolution_convert_fusion.8
  442.8 2.2 convolution_convert_fusion.9
  445.0 2.9 reshape.239
  447.9 4.7 copy.127
  452.7 6.1 multiply_reduce_fusion
  458.8 2.3 multiply_convert_fusion.1
  461.2 1.9 fusion.45
  463.0 2.3 fusion.46
  465.4 2.5 fusion.48
  468.0 2.4 pad_maximum_fusion.3
  470.4 5.6 copy.132
  476.0 9.9 %convert_element_type.156 = bf16[591,2304]{0,1:T(8,128)(2,1)} reshape(bf16[3,197,3,12,64]{1,0,4,3,2:T(4,128)(2,1)} %copy.132) | data formatting | bytes 5446656 | tf_op jit(solution)/shard_map/convert_element_type | solution.py:233
  486.0 7.0 convolution_convert_fusion.1
  492.9 4.7 fusion.42
  499.6 8.2 %concatenate.20 = bf16[768,3078]{1,0:T(8,128)(2,1)} concatenate(bf16[768,2304]{1,0:T(8,128)(2,1)} %convolution_convert_fusion.1, bf16[768,768]{1,0:T(8,128)(2,1)S(1)} %copy-done.22, bf16[768,4]{1,0:T(8,128)(2,1)S(1)} %copy.134, bf16[768,1]{1,0:T(8,128)(2,1)S(1)} %broadcast_in_dim.40, bf16[768,1]{1,0:T(8,128)(2,1)S(1)} %broadcast_in_dim.41), dimensions={1} | concatenate | bytes 9455616 | tf_op jit(solution)/shard_map/concatenate | solution.py:245
  507.8 12.5 %convolution_convert_fusion = bf16[3072,768]{1,0:T(8,128)(2,1)} fusion(bf16[1504,3072]{1,0:T(8,128)(2,1)} %copy-done.56, bf16[1504,1536]{1,0:T(8,128)(2,1)} %bitcast.11), kind=kOutput, calls=%fused_computation.23 | convolution fusion | flops 7099121664 | bytes 16269312 | tf_op jit(solution)/shard_map/dot_general | solution.py:151
  520.3 8.5 %stack_reshape.4 = bf16[1,768,3072]{2,1,0:T(8,128)(2,1)} reshape(bf16[3072,768]{1,0:T(8,128)(2,1)} %convolution_convert_fusion) | data formatting | bytes 9437184 | tf_op jit(solution)/shard_map/stack;reshape | solution.py:157
  528.7 12.5 %fusion.7 = bf16[1,768,3072]{2,1,0:T(8,128)(2,1)} fusion(bf16[1504,3072]{1,0:T(8,128)(2,1)} %add_convert_fusion, bf16[1504,1536]{1,0:T(8,128)(2,1)} %bitcast.11), kind=kOutput, calls=%fused_computation.32 | convolution fusion | flops 7099121664 | bytes 16269312 | tf_op jit(solution)/shard_map/dot_general | solution.py:154
  541.3 8.4 %pad_maximum_fusion = bf16[2,768,3072]{2,1,0:T(8,128)(2,1)} fusion(bf16[1,768,3072]{2,1,0:T(8,128)(2,1)} %stack_reshape.4, bf16[1,768,3072]{2,1,0:T(8,128)(2,1)} %fusion.7), kind=kLoop, calls=%fused_computation.17 | loop fusion | flops 4718592 | bytes 18874368 | tf_op jit(solution)/shard_map/stack | solution.py:157
  549.7 1.6 copy-done.4
  551.8 3.1 add_convert_fusion.2
  554.8 5.9 reduce-scatter.3.cloned.1.call-done
  560.8 80.0 %reduce-scatter.5.cloned.1.call-done = bf16[2,96,3072]{2,1,0:T(8,128)(2,1)} async-done(((bf16[2,768,3072]{2,1,0:T(8,128)(2,1)}), bf16[2,96,3072]{2,1,0:T(8,128)(2,1)}) %reduce-scatter.5.cloned.1.call-update) | async-done | bytes 1179664 | tf_op jit(solution)/shard_map/reduce_scatter | solution.py:160
  640.9 2.5 fusion.85
  644.7 38.2 %all-reduce.3.cloned.1.call-done = bf16[96,3078]{1,0:T(8,128)(2,1)} async-done(((bf16[96,3078]{1,0:T(8,128)(2,1)}), bf16[96,3078]{1,0:T(8,128)(2,1)}) %all-reduce.3.cloned.1.call-update) | async-done | bytes 590992 | tf_op jit(solution)/shard_map/psum | solution.py:250
  686.1 2.0 slice.154
  688.1 1.6 slice.155
  (189 shorter events, 19.7 us)
Async XLA Ops:
  7.2 9.3 %copy-start.32 = (s32[591,2]{0,1:T(2,128)S(1)}, s32[591,2]{0,1:T(2,128)}, u32[]{:S(2)}) copy-start(s32[591,2]{0,1:T(2,128)} %param.13) | copy-start | bytes 14188
  7.2 46.9 %all-gather.3.cloned.1.call-start = ((), (), s32[]{:S(2)}) async-start(), calls=%async_computation.4 | async-start | bytes 5529600 | tf_op jit(solution)/shard_map/all_gather | solution.py:62
  11.5 7.5 %copy-start.8 = (bf16[591,768]{1,0:T(8,128)(2,1)S(1)}, bf16[591,768]{1,0:T(8,128)(2,1)}, u32[]{:S(2)}) copy-start(bf16[591,768]{1,0:T(8,128)(2,1)} %param.11) | copy-start | bytes 2723332
  11.6 109.8 %all-gather.5.cloned.1.call-start = ((), (), s32[]{:S(2)}) async-start(), calls=%async_computation.5 | async-start | bytes 10616832 | tf_op jit(solution)/shard_map/all_gather | solution.py:73
  13.1 6.6 copy-start.5
  19.0 87.4 %copy-start.24 = (f32[591]{0:T(1024)}, f32[591]{0:T(1024)S(1)}, u32[]{:S(2)}) copy-start(f32[591]{0:T(1024)S(1)} %fusion.76) | copy-start | bytes 7096
  19.1 90.2 %copy-start.54 = (s32[591]{0:T(1024)}, s32[591]{0:T(1024)S(1)}, u32[]{:S(2)}) copy-start(s32[591]{0:T(1024)S(1)} %get-tuple-element.67) | copy-start | bytes 7096
  19.1 92.5 %copy-start.52 = (s32[591]{0:T(1024)}, s32[591]{0:T(1024)S(1)}, u32[]{:S(2)}) copy-start(s32[591]{0:T(1024)S(1)} %get-tuple-element.66) | copy-start | bytes 7096
  19.3 42.1 %copy-start.40 = (f32[591]{0:T(1024)}, f32[591]{0:T(1024)S(1)}, u32[]{:S(2)}) copy-start(f32[591]{0:T(1024)S(1)} %broadcast_multiply_fusion.2) | copy-start | bytes 7096
  19.7 41.6 %copy-start.44 = (f32[591]{0:T(1024)}, f32[591]{0:T(1024)S(1)}, u32[]{:S(2)}) copy-start(f32[591]{0:T(1024)S(1)} %fusion.41) | copy-start | bytes 7096
  19.8 41.6 %copy-start.50 = (f32[591]{0:T(1024)}, f32[591]{0:T(1024)S(1)}, u32[]{:S(2)}) copy-start(f32[591]{0:T(1024)S(1)} %fusion.74) | copy-start | bytes 7096
  55.4 6.0 copy-start.48
  55.4 48.8 %copy-start.34 = (f32[768]{0:T(1024)}, f32[768]{0:T(1024)S(1)}, u32[]{:S(2)}) copy-start(f32[768]{0:T(1024)S(1)} %get-tuple-element.54) | copy-start | bytes 9220
  89.5 4.8 copy-start.10
  92.8 3.0 copy-start
  95.7 1.6 copy-start.20
  103.2 1.2 copy-start.1
  103.2 3.7 copy-start.17
  103.2 3.2 copy-start.28
  104.2 3.0 copy-start.36
  104.7 4.5 copy-start.14
  106.3 0.6 copy-start.26
  106.3 0.6 copy-start.30
  106.9 2.3 copy-start.42
  116.1 108.2 %all-to-all-start = ((bf16[4,376,1536]{2,1,0:T(8,128)(2,1)}), bf16[4,376,1536]{2,1,0:T(8,128)(2,1)}, u32[]{:S(2)}, u32[]{:S(2)}) async-start(bf16[4,376,1536]{2,1,0:T(8,128)(2,1)} %bitcast.98), calls=%async_computation | async-start | bytes 9240576 | tf_op jit(solution)/shard_map/all_to_all | solution.py:133
  224.4 48.2 %copy-start.18 = (bf16[3072,768]{1,0:T(8,128)(2,1)S(1)}, bf16[3072,768]{1,0:T(8,128)(2,1)}, u32[]{:S(2)}) copy-start(bf16[3072,768]{1,0:T(8,128)(2,1)} %reshape_squeeze.3) | copy-start | bytes 14155780
  272.5 7.6 %copy-start.56 = (bf16[1504,3072]{1,0:T(8,128)(2,1)}, bf16[1504,3072]{1,0:T(8,128)(2,1)S(1)}, u32[]{:S(2)}) copy-start(bf16[1504,3072]{1,0:T(8,128)(2,1)S(1)} %get-tuple-element.70) | copy-start | bytes 27721732
  316.7 5.1 copy-start.43
  316.7 107.2 %copy-start.55 = (s32[591]{0:T(1024)S(1)}, s32[591]{0:T(1024)}, u32[]{:S(2)}) copy-start(s32[591]{0:T(1024)} %copy-done.54) | copy-start | bytes 7096
  316.7 107.2 %all-to-all-start.1 = ((bf16[4,376,1536]{2,1,0:T(8,128)(2,1)}), bf16[4,376,1536]{2,1,0:T(8,128)(2,1)}, u32[]{:S(2)}, u32[]{:S(2)}) async-start(bf16[4,376,1536]{2,1,0:T(8,128)(2,1)} %bitcast.99), calls=%async_computation.1 | async-start | bytes 9240576 | tf_op jit(solution)/shard_map/all_to_all | solution.py:169
  321.8 239.0 %reduce-scatter.3.cloned.1.call-start = ((), (), s32[]{:S(2)}) async-start(), calls=%async_computation.6 | async-start | bytes 5529600 | tf_op jit(solution)/shard_map/reduce_scatter | solution.py:249
  424.0 5.6 copy-start.53
  429.6 5.7 copy-start.2
  429.6 5.7 copy-start.6
  429.6 5.7 copy-start.25
  435.2 1.9 copy-start.33
  435.2 1.9 copy-start.27
  435.2 1.9 copy-start.31
  435.3 1.9 copy-start.39
  435.3 1.9 copy-start.15
  435.3 2.1 copy-start.29
  435.3 2.2 copy-start.35
  435.3 2.2 copy-start.37
  437.5 2.0 copy-start.47
  439.5 1.2 copy-start.23
  440.2 2.6 copy-start.3
  445.0 7.7 %copy-start.21 = (f32[3,12,197]{2,1,0:T(8,128)S(1)}, f32[3,12,197]{2,1,0:T(8,128)}, u32[]{:S(2)}) copy-start(f32[3,12,197]{2,1,0:T(8,128)} %copy-done.20) | copy-start | bytes 85108
  447.9 10.8 %slice-start = ((s8[7372800]{0:T(1024)(128)(4,1)}), s8[3178496]{0:T(1024)(128)(4,1)S(1)}, s32[]{:S(2)}) async-start(s8[7372800]{0:T(1024)(128)(4,1)} %bitcast.96), calls=%async_computation.9 | async-start | bytes 6356992
  452.7 6.1 slice-start.1
  458.8 2.4 copy-start.13
  461.2 1.9 copy-start.12
  463.0 2.3 copy-start.11
  476.0 9.9 %copy-start.9 = (bf16[591,768]{1,0:T(8,128)(2,1)S(1)}, bf16[591,768]{1,0:T(8,128)(2,1)}, u32[]{:S(2)}) copy-start(bf16[591,768]{1,0:T(8,128)(2,1)} %param.11) | copy-start | bytes 2723332
  476.0 9.9 %copy-start.41 = (f32[591]{0:T(1024)S(1)}, f32[591]{0:T(1024)}, u32[]{:S(2)}) copy-start(f32[591]{0:T(1024)} %copy-done.40) | copy-start | bytes 7096
  476.0 9.9 %copy-start.49 = (f32[768]{0:T(1024)S(1)}, f32[768]{0:T(1024)}, u32[]{:S(2)}) copy-start(f32[768]{0:T(1024)} %copy-done.48) | copy-start | bytes 9220
  476.0 9.9 %copy-start.51 = (f32[591]{0:T(1024)S(1)}, f32[591]{0:T(1024)}, u32[]{:S(2)}) copy-start(f32[591]{0:T(1024)} %copy-done.50) | copy-start | bytes 7096
  485.9 7.0 %copy-start.19 = (bf16[591,2304]{0,1:T(8,128)(2,1)S(1)}, bf16[591,2304]{0,1:T(8,128)(2,1)}, u32[]{:S(2)}) copy-start(bf16[591,2304]{0,1:T(8,128)(2,1)} %convert_element_type.156) | copy-start | bytes 8169988
  492.9 4.7 copy-start.45
  497.6 1.3 copy-start.16
  497.6 1.9 copy-start.22
  507.7 133.1 %reduce-scatter.5.cloned.1.call-start = ((), (), s32[]{:S(2)}) async-start(), calls=%async_computation.8 | async-start | bytes 10616832 | tf_op jit(solution)/shard_map/reduce_scatter | solution.py:160
  549.6 1.7 copy-start.4
  549.6 2.1 copy-start.7
  549.7 133.2 %all-reduce.3.cloned.1.call-start = ((), (), s32[]{:S(2)}) async-start(), calls=%async_computation.7 | async-start | bytes 1228800 | tf_op jit(solution)/shard_map/psum | solution.py:250
  (2 other events, 1.2 us)
Sparse Core Ops, SparseCore 0:
  11.7 42.3 all-gather.2
  56.5 58.6 all-gather.4
  507.9 52.8 reduce-scatter.2
  564.1 76.6 reduce-scatter.4
  643.1 39.7 all-reduce.2

commit v2 on v1

--- a/solution.py
+++ b/solution.py
@@ -112,7 +112,19 @@
     slot_index = jnp.sum(before * flat_picks, axis=1).reshape(rows, 2)
     position = jnp.where(live_int[:, None] > 0, routes * capacity + slot_index, overflow)
 
-    slot_ids = jnp.arange(overflow, dtype=jnp.int32)[:, None]
+    half_cap = 8 * ((capacity + 15) // 16)
+    chunk_sizes = [half_cap, capacity - half_cap] if capacity > half_cap else [capacity]
+    chunk_starts = [sum(chunk_sizes[:k]) for k in range(len(chunk_sizes))]
+    slot_ids = jnp.concatenate(
+        [
+            (
+                jnp.arange(experts, dtype=jnp.int32)[:, None] * capacity
+                + start
+                + jnp.arange(size, dtype=jnp.int32)[None, :]
+            ).reshape(-1)
+            for start, size in zip(chunk_starts, chunk_sizes)
+        ]
+    )[:, None]
     take_first = (slot_ids == position[None, :, 0]).astype(jnp.bfloat16)
     take_second = (slot_ids == position[None, :, 1]).astype(jnp.bfloat16)
 
@@ -127,33 +139,51 @@
         jnp.dot(take_first, grad_picked[:, 0], preferred_element_type=jnp.float32)
         + jnp.dot(take_second, grad_picked[:, 1], preferred_element_type=jnp.float32)
     ).astype(jnp.bfloat16)
-    outgoing = jnp.concatenate([sent_rows, sent_grad], axis=1).reshape(
-        experts, capacity, 2 * width
-    )
-    arrived = lax.all_to_all(outgoing, "expert", split_axis=0, concat_axis=0, tiled=True)
-    arrived = arrived.reshape(overflow, 2 * width)
-    flat_arrived = arrived[:, :width]
-    flat_grad = arrived[:, width:]
-
-    pre_act = jnp.dot(flat_arrived, expert_first, preferred_element_type=jnp.float32)
-    activated, gelu_back = jax.vjp(gelu_exact, pre_act)
-    activated = activated.astype(jnp.bfloat16)
-    produced = jnp.dot(activated, expert_second, preferred_element_type=jnp.float32).astype(
-        jnp.bfloat16
-    )
-    hidden_grad = lax.dot_general(
-        flat_grad, expert_second, COL_CONTRACT, preferred_element_type=jnp.float32
-    )
-    pre_grad = gelu_back(hidden_grad)[0].astype(jnp.bfloat16)
-    row_grad = lax.dot_general(
-        pre_grad, expert_first, COL_CONTRACT, preferred_element_type=jnp.float32
-    ).astype(jnp.bfloat16)
-    grad_second = lax.dot_general(
-        activated, flat_grad, ROW_CONTRACT, preferred_element_type=jnp.float32
-    )
-    grad_first = lax.dot_general(
-        flat_arrived, pre_grad, ROW_CONTRACT, preferred_element_type=jnp.float32
-    )
+    outgoing = jnp.concatenate([sent_rows, sent_grad], axis=1)
+
+    grad_first = None
+    grad_second = None
+    returned_parts = []
+    for start, size in zip(chunk_starts, chunk_sizes):
+        arrived = lax.all_to_all(
+            outgoing[experts * start : experts * (start + size)].reshape(
+                experts, size, 2 * width
+            ),
+            "expert",
+            split_axis=0,
+            concat_axis=0,
+            tiled=True,
+        ).reshape(experts * size, 2 * width)
+        flat_arrived = arrived[:, :width]
+        flat_grad = arrived[:, width:]
+        pre_act = jnp.dot(flat_arrived, expert_first, preferred_element_type=jnp.float32)
+        activated, gelu_back = jax.vjp(gelu_exact, pre_act)
+        activated = activated.astype(jnp.bfloat16)
+        produced = jnp.dot(
+            activated, expert_second, preferred_element_type=jnp.float32
+        ).astype(jnp.bfloat16)
+        hidden_grad = lax.dot_general(
+            flat_grad, expert_second, COL_CONTRACT, preferred_element_type=jnp.float32
+        )
+        pre_grad = gelu_back(hidden_grad)[0].astype(jnp.bfloat16)
+        row_grad = lax.dot_general(
+            pre_grad, expert_first, COL_CONTRACT, preferred_element_type=jnp.float32
+        ).astype(jnp.bfloat16)
+        part_second = lax.dot_general(
+            activated, flat_grad, ROW_CONTRACT, preferred_element_type=jnp.float32
+        )
+        part_first = lax.dot_general(
+            flat_arrived, pre_grad, ROW_CONTRACT, preferred_element_type=jnp.float32
+        )
+        grad_first = part_first if grad_first is None else grad_first + part_first
+        grad_second = part_second if grad_second is None else grad_second + part_second
+        returning = jnp.concatenate([produced, row_grad], axis=1).reshape(
+            experts, size, 2 * width
+        )
+        returned_parts.append(
+            lax.all_to_all(returning, "expert", split_axis=0, concat_axis=0, tiled=True)
+        )
+
     expert_grads = jnp.stack(
         [grad_first, grad_second.reshape(width, ff)], axis=0
     ).astype(jnp.bfloat16)
@@ -163,11 +193,9 @@
     grad_in_share = expert_share[0][None]
     grad_back_share = expert_share[1].reshape(back_rows, width)[None]
 
-    returning = jnp.concatenate([produced, row_grad], axis=1).reshape(
-        experts, capacity, 2 * width
-    )
-    returned = lax.all_to_all(returning, "expert", split_axis=0, concat_axis=0, tiled=True)
-    returned = returned.reshape(overflow, 2 * width)
+    returned = jnp.concatenate(
+        [part.reshape(-1, 2 * width) for part in returned_parts], axis=0
+    )
     picked_first = lax.dot_general(
         take_first, returned, ROW_CONTRACT, preferred_element_type=jnp.float32
     )

time: 711 us -> 624 us (0.88)
  waiting for transfers between devices: 349 us -> 235 us
  matrix products: 178 us -> 195 us
  starting transfers between devices: 10.4 us -> 19 us
    all_to_all x1 -> x2, waiting for transfers between devices: 102 us -> 52.4 us  [shards(): lax.all_to_all(returning, 'expert', split_axis=0, concat_axis=0, tiled=True)]
    all_to_all x1 -> x2, waiting for transfers between devices: 89.7 us -> 40.6 us  [shards(): lax.all_to_all(outgoing[experts * start:experts * (start + size)].reshape...]
    psum x1, waiting for transfers between devices: 38.2 us -> 8.51 us  [shards(): dense_total = lax.psum(dense_share, 'expert').astype(jnp.float32)]
    reduce_scatter x1, waiting for transfers between devices: 5.95 us -> 27.7 us  [shards(): lax.psum_scatter(dense_grads, 'shard', scatter_dimension=0, tiled=True)]
    dot_general x1 -> x2, matrix products: 12.5 us -> 20.7 us  [shards(): lax.dot_general(flat_arrived, pre_grad, ROW_CONTRACT, preferred_element_t...]
    reduce_scatter x1, waiting for transfers between devices: 80 us -> 72.8 us  [shards(): lax.psum_scatter(expert_grads, 'shard', scatter_dimension=1, tiled=True)]
    unnamed x125 -> x149, local copies, waits for them, and re-layouts: 19.5 us -> 23.7 us
    dot_general x1 -> x2, matrix products: 48.2 us -> 52.1 us  [shards(): jnp.dot(flat_arrived, expert_first, preferred_element_type=jnp.float32)]
  transfers between devices with their start and end apart: 7 -> 9, of which waited for: 6 -> 7; matrix products, arithmetic and copies ran while one was open for 19% -> 41% of each run, Pallas kernels for 0% -> 0%
where the time goes in v2:
time: 624 us; the launch traced here: 615 us
  waiting for transfers between devices  235 us (38%)
  matrix products  195 us (31%)
  local copies, waits for them, and re-layouts  114 us (18%)
  other arithmetic  35.9 us (6%)
  starting transfers between devices  19 us (3%)
  between operations  16.1 us (3%)
    reduce_scatter x1, waiting for transfers between devices, shards(): lax.psum_scatter(expert_grads, 'shard', scatter_dimension=1, tiled=True)  72.8 us
    all_to_all x2, waiting for transfers between devices, shards(): lax.all_to_all(returning, 'expert', split_axis=0, concat_axis=0, tiled=True)  52.4 us
    dot_general x2, matrix products, shards(): jnp.dot(flat_arrived, expert_first, preferred_element_type=jnp.float32)  52.1 us
    all_to_all x2, waiting for transfers between devices, shards(): lax.all_to_all(outgoing[experts * start:experts * (start + size)].reshape...  40.6 us
    all_gather x1, waiting for transfers between devices, shards(): dense_full = lax.all_gather(dense_local, 'shard', axis=0, tiled=True)  32.4 us
    reduce_scatter x1, waiting for transfers between devices, shards(): lax.psum_scatter(dense_grads, 'shard', scatter_dimension=0, tiled=True)  27.7 us
    unnamed x149, local copies, waits for them, and re-layouts  23.7 us
    dot_general x2, matrix products, shards(): lax.dot_general(flat_grad, expert_second, COL_CONTRACT, preferred_element...  22.8 us
  transfers between devices with their start and end apart: 9, of which 7 were waited for; matrix products, arithmetic and copies ran while one was open for 41% of the time, Pallas kernels for 0%

profile of v2, /device:TPU:0, one launch (start us, length us, event | category | flops | bytes accessed | tf_op | source)
XLA Modules:
  0.0 615.3 jit_solution(7871678161351734495)
XLA Ops:
  9.7 1.9 concatenate.26
  13.2 2.2 pad_maximum_fusion.8
  21.7 32.4 %all-gather.3.cloned.1.call-done = bf16[768,3078]{1,0:T(8,128)(2,1)} async-done(((bf16[96,3078]{1,0:T(8,128)(2,1)}), bf16[768,3078]{1,0:T(8,128)(2,1)}) %all-gather.3.cloned.1.call-update) | async-done | bytes 4727824 | tf_op jit(solution)/shard_map/all_gather | solution.py:62
  55.5 6.0 convolution_convert_fusion.1
  61.5 9.3 %reshape.271 = bf16[3,197,3,12,64]{4,3,2,1,0:T(8,128)(2,1)} reshape(bf16[591,2304]{1,0:T(8,128)(2,1)} %convolution_convert_fusion.1) | data formatting | bytes 5446656 | tf_op jit(solution)/shard_map/reshape | solution.py:80
  70.9 6.6 %fusion.117 = (bf16[3,197,1,12,64]{4,3,2,1,0:T(8,128)(2,1)}, bf16[3,197,1,12,64]{4,3,2,1,0:T(8,128)(2,1)}, bf16[3,197,1,12,64]{4,3,2,1,0:T(8,128)(2,1)}) fusion(bf16[3,197,3,12,64]{4,3,2,1,0:T(8,128)(2,1)} %reshape.271), kind=kLoop, calls=%fused_computation.219 | loop fusion | bytes 5446656 | tf_op jit(solution)/shard_map/slice | solution.py:81
  77.5 3.3 copy.152
  80.8 4.6 copy.154
  85.5 4.6 copy.153
  90.1 2.8 multiply_reduce_fusion.1
  97.1 2.1 convert_element_type.149
  99.2 2.7 fusion.119
  106.0 2.1 fusion.14
  108.1 2.2 convolution_convert_fusion.2
  110.3 2.5 add_convert_fusion.4
  115.8 4.6 all-to-all-start.2
  120.4 2.9 fusion.35
  123.3 4.8 slice.165
  128.1 8.5 %reshape_squeeze.3 = bf16[3072,768]{1,0:T(8,128)(2,1)} reshape(bf16[1,768,3072]{2,1,0:T(8,128)(2,1)} %slice.165) | data formatting | bytes 9437184 | tf_op jit(solution)/shard_map/reshape;squeeze | solution.py:75
  136.6 36.2 %all-to-all-done.2 = bf16[4,184,1536]{2,1,0:T(8,128)(2,1)} async-done(((bf16[4,184,1536]{2,1,0:T(8,128)(2,1)}), bf16[4,184,1536]{2,1,0:T(8,128)(2,1)}, u32[]{:S(2)}, u32[]{:S(2)}) %all-to-all-start.2) | async-done | bytes 2261024 | tf_op jit(solution)/shard_map/all_to_all | solution.py:148
  172.8 4.1 all-to-all-start
  176.9 25.8 %multiply_convert_fusion.1 = (bf16[736,3072]{1,0:T(8,128)(2,1)S(1)}, f32[736,3072]{1,0:T(8,128)}, f32[736,3072]{1,0:T(8,128)}) fusion(bf16[2,768,3072]{2,1,0:T(8,128)(2,1)} %all-gather.5.cloned.1.call-done, bf16[736,1536]{1,0:T(8,128)(2,1)} %bitcast.16), kind=kOutput, calls=%fused_computation.23 | convolution fusion | flops 3619848192 | bytes 28459008 | tf_op jit(solution)/shard_map/dot_general | solution.py:159
  202.7 3.7 convolution_convert_fusion.7
  206.4 11.8 %add_convert_fusion.3 = bf16[736,3072]{1,0:T(8,128)(2,1)} fusion(f32[736,3072]{1,0:T(8,128)} %get-tuple-element.73, f32[736,3072]{1,0:T(8,128)} %get-tuple-element.86, bf16[3072,768]{1,0:T(8,128)(2,1)S(1)} %copy-done.22, bf16[736,1536]{1,0:T(8,128)(2,1)} %bitcast.16), kind=kOutput, calls=%fused_computation.22 | convolution fusion | flops 3504537600 | bytes 28459008 | tf_op jit(solution)/shard_map/dot_general | solution.py:165
  218.2 6.1 fusion.58
  225.8 4.5 all-to-all-done
  230.3 4.7 all-to-all-start.3
  235.0 26.3 %multiply_convert_fusion = (bf16[768,3072]{1,0:T(8,128)(2,1)S(1)}, f32[768,3072]{1,0:T(8,128)}, f32[768,3072]{1,0:T(8,128)}) fusion(bf16[2,768,3072]{2,1,0:T(8,128)(2,1)} %all-gather.5.cloned.1.call-done, bf16[768,1536]{1,0:T(8,128)(2,1)S(1)} %bitcast.113), kind=kOutput, calls=%fused_computation.7 | convolution fusion | flops 3777232896 | bytes 29491200 | tf_op jit(solution)/shard_map/dot_general | solution.py:159
  261.2 8.1 %convolution_convert_fusion.4 = bf16[768,768]{0,1:T(8,128)(2,1)S(1)} fusion(bf16[768,3072]{1,0:T(8,128)(2,1)S(1)} %get-tuple-element.70, bf16[3072,768]{1,0:T(8,128)(2,1)} %reshape_squeeze.3), kind=kOutput, calls=%fused_computation.119 | convolution fusion | flops 3624468480 | bytes 10616832 | tf_op jit(solution)/shard_map/dot_general | solution.py:162
  269.4 11.0 %add_convert_fusion.2 = bf16[768,3072]{1,0:T(8,128)(2,1)S(1)} fusion(f32[768,3072]{1,0:T(8,128)} %get-tuple-element.71, f32[768,3072]{1,0:T(8,128)} %get-tuple-element.87, bf16[3072,768]{1,0:T(8,128)(2,1)} %reshape_squeeze.3, bf16[768,1536]{1,0:T(8,128)(2,1)S(1)} %bitcast.114), kind=kOutput, calls=%fused_computation.6 | convolution fusion | flops 3656908800 | bytes 29491200 | tf_op jit(solution)/shard_map/dot_general | solution.py:165
  280.4 8.0 %fusion.57 = bf16[768,768]{0,1:T(8,128)(2,1)S(1)} fusion(bf16[768,3072]{1,0:T(8,128)(2,1)S(1)} %add_convert_fusion.2, bf16[2,768,3072]{2,1,0:T(8,128)(2,1)} %all-gather.5.cloned.1.call-done), kind=kOutput, calls=%fused_computation.117 | convolution fusion | flops 3624468480 | bytes 10616832 | tf_op jit(solution)/shard_map/dot_general | solution.py:169
  288.6 2.5 copy.130
  291.1 5.1 all-to-all-start.1
  296.6 52.4 %all-to-all-done.1 = bf16[4,192,1536]{2,1,0:T(8,128)(2,1)S(1)} async-done(((bf16[4,192,1536]{2,1,0:T(8,128)(2,1)}), bf16[4,192,1536]{2,1,0:T(8,128)(2,1)S(1)}, u32[]{:S(2)}, u32[]{:S(2)}) %all-to-all-start.1) | async-done | bytes 2359328 | tf_op jit(solution)/shard_map/all_to_all | solution.py:184
  349.0 4.9 fusion.16
  354.0 5.1 fusion.12
  359.1 1.9 multiply_reduce_fusion.5
  361.3 2.1 multiply_reduce_fusion.2
  366.7 2.2 convolution_convert_fusion.8
  368.9 2.9 reshape.272
  371.9 4.5 copy.132
  376.4 5.1 fusion.62
  381.7 2.3 multiply_reduce_fusion
  384.0 2.3 multiply_convert_fusion.2
  389.2 2.1 convolution_convert_fusion.6
  392.3 5.6 copy.137
  397.9 9.9 %convert_element_type.172 = bf16[591,2304]{0,1:T(8,128)(2,1)} reshape(bf16[3,197,3,12,64]{1,0,4,3,2:T(4,128)(2,1)} %copy.137) | data formatting | bytes 5446656 | tf_op jit(solution)/shard_map/convert_element_type | solution.py:261
  407.9 7.0 %convolution_convert_fusion = bf16[768,2304]{1,0:T(8,128)(2,1)} fusion(bf16[591,2304]{0,1:T(8,128)(2,1)} %convert_element_type.172, bf16[591,768]{1,0:T(8,128)(2,1)S(1)} %copy-done.9, f32[768]{0:T(1024)S(1)} %copy-done.55, f32[591]{0:T(1024)S(1)} %copy-done.57, f32[591]{0:T(1024)S(1)} %copy-done.47), kind=kOutput, calls=%fused_computation.52 | convolution fusion | flops 2095554816 | bytes 7177848 | tf_op jit(solution)/shard_map/dot_general | solution.py:263
  414.9 4.7 fusion.54
  421.1 8.4 %concatenate.32 = bf16[768,3078]{1,0:T(8,128)(2,1)} concatenate(bf16[768,2304]{1,0:T(8,128)(2,1)} %convolution_convert_fusion, bf16[768,768]{1,0:T(8,128)(2,1)} %convolution_convert_fusion.6, bf16[768,4]{1,0:T(8,128)(2,1)S(1)} %copy.139, bf16[768,1]{1,0:T(8,128)(2,1)S(1)} %broadcast_in_dim.40, bf16[768,1]{1,0:T(8,128)(2,1)S(1)} %broadcast_in_dim.41), dimensions={1} | concatenate | bytes 9455616 | tf_op jit(solution)/shard_map/concatenate | solution.py:273
  429.6 1.6 copy-done.21
  431.2 6.0 fusion.72
  437.2 9.2 %fusion.78 = f32[768,3072]{1,0:T(8,128)} fusion(bf16[768,3072]{1,0:T(8,128)(2,1)} %copy-done.23, bf16[768,1536]{1,0:T(8,128)(2,1)S(1)} %bitcast.116), kind=kOutput, calls=%fused_computation.144 | convolution fusion | flops 3623878656 | bytes 15335424 | tf_op jit(solution)/shard_map/dot_general | solution.py:175
  446.4 8.7 %add_convert_fusion = bf16[3072,768]{1,0:T(8,128)(2,1)} fusion(f32[3072,768]{1,0:T(8,128)S(1)} %fusion.72, bf16[736,3072]{1,0:T(8,128)(2,1)} %copy-done.65, bf16[736,1536]{1,0:T(8,128)(2,1)} %bitcast.16), kind=kOutput, calls=%fused_computation.4 | convolution fusion | flops 3477602304 | bytes 19808256 | tf_op jit(solution)/shard_map/dot_general | solution.py:172
  455.0 27.7 %reduce-scatter.3.cloned.1.call-done = bf16[96,3078]{1,0:T(8,128)(2,1)} async-done(((bf16[768,3078]{1,0:T(8,128)(2,1)}), bf16[96,3078]{1,0:T(8,128)(2,1)}) %reduce-scatter.3.cloned.1.call-update) | async-done | bytes 590992 | tf_op jit(solution)/shard_map/reduce_scatter | solution.py:277
  482.8 11.5 %fusion.21 = bf16[1,768,3072]{2,1,0:T(8,128)(2,1)} fusion(f32[768,3072]{1,0:T(8,128)} %fusion.78, bf16[736,3072]{1,0:T(8,128)(2,1)} %add_convert_fusion.3, bf16[736,1536]{1,0:T(8,128)(2,1)} %bitcast.16), kind=kOutput, calls=%fused_computation.60 | convolution fusion | flops 3477602304 | bytes 19808256 | tf_op jit(solution)/shard_map/dot_general | solution.py:175
  494.3 8.7 %stack_reshape.4 = bf16[1,768,3072]{2,1,0:T(8,128)(2,1)} reshape(bf16[3072,768]{1,0:T(8,128)(2,1)} %add_convert_fusion) | data formatting | bytes 9437184 | tf_op jit(solution)/shard_map/stack;reshape | solution.py:187
  503.1 8.3 %pad_maximum_fusion = bf16[2,768,3072]{2,1,0:T(8,128)(2,1)} fusion(bf16[1,768,3072]{2,1,0:T(8,128)(2,1)} %stack_reshape.4, bf16[1,768,3072]{2,1,0:T(8,128)(2,1)} %fusion.21), kind=kLoop, calls=%fused_computation.3 | loop fusion | flops 4718592 | bytes 18874368 | tf_op jit(solution)/shard_map/stack | solution.py:187
  513.2 3.1 add_convert_fusion.5
  516.2 8.5 %all-reduce.3.cloned.1.call-done = bf16[96,3078]{1,0:T(8,128)(2,1)} async-done(((bf16[96,3078]{1,0:T(8,128)(2,1)}), bf16[96,3078]{1,0:T(8,128)(2,1)}) %all-reduce.3.cloned.1.call-update) | async-done | bytes 590992 | tf_op jit(solution)/shard_map/psum | solution.py:278
  526.1 2.0 slice.174
  528.1 1.6 slice.175
  531.6 72.8 %reduce-scatter.5.cloned.1.call-done = bf16[2,96,3072]{2,1,0:T(8,128)(2,1)} async-done(((bf16[2,768,3072]{2,1,0:T(8,128)(2,1)}), bf16[2,96,3072]{2,1,0:T(8,128)(2,1)}) %reduce-scatter.5.cloned.1.call-update) | async-done | bytes 1179664 | tf_op jit(solution)/shard_map/reduce_scatter | solution.py:190
  604.5 2.5 fusion.118
  (234 shorter events, 39.6 us)
Async XLA Ops:
  7.2 9.3 %copy-start.38 = (s32[591,2]{0,1:T(2,128)S(1)}, s32[591,2]{0,1:T(2,128)}, u32[]{:S(2)}) copy-start(s32[591,2]{0,1:T(2,128)} %param.13) | copy-start | bytes 14188
  7.2 46.9 %all-gather.3.cloned.1.call-start = ((), (), s32[]{:S(2)}) async-start(), calls=%async_computation.6 | async-start | bytes 5529600 | tf_op jit(solution)/shard_map/all_gather | solution.py:62
  8.0 11.4 %copy-start.8 = (bf16[591,768]{1,0:T(8,128)(2,1)S(1)}, bf16[591,768]{1,0:T(8,128)(2,1)}, u32[]{:S(2)}) copy-start(bf16[591,768]{1,0:T(8,128)(2,1)} %param.11) | copy-start | bytes 2723332
  11.6 8.5 %copy-start.5 = (bf16[591,768]{1,0:T(8,128)(2,1)S(1)}, bf16[591,768]{1,0:T(8,128)(2,1)}, u32[]{:S(2)}) copy-start(bf16[591,768]{1,0:T(8,128)(2,1)} %param.21) | copy-start | bytes 2723332
  11.6 111.7 %all-gather.5.cloned.1.call-start = ((), (), s32[]{:S(2)}) async-start(), calls=%async_computation.7 | async-start | bytes 10616832 | tf_op jit(solution)/shard_map/all_gather | solution.py:73
  19.3 85.8 %copy-start.30 = (f32[591]{0:T(1024)}, f32[591]{0:T(1024)S(1)}, u32[]{:S(2)}) copy-start(f32[591]{0:T(1024)S(1)} %fusion.106) | copy-start | bytes 7096
  19.4 90.9 %copy-start.58 = (s32[1504]{0:T(1024)}, s32[1504]{0:T(1024)S(1)}, u32[]{:S(2)}) copy-start(s32[1504]{0:T(1024)S(1)} %pad_add_fusion) | copy-start | bytes 18052
  19.4 88.7 %copy-start.60 = (s32[591]{0:T(1024)}, s32[591]{0:T(1024)S(1)}, u32[]{:S(2)}) copy-start(s32[591]{0:T(1024)S(1)} %get-tuple-element.67) | copy-start | bytes 7096
  19.4 90.9 %copy-start.62 = (s32[591]{0:T(1024)}, s32[591]{0:T(1024)S(1)}, u32[]{:S(2)}) copy-start(s32[591]{0:T(1024)S(1)} %get-tuple-element.66) | copy-start | bytes 7096
  19.7 41.8 %copy-start.46 = (f32[591]{0:T(1024)}, f32[591]{0:T(1024)S(1)}, u32[]{:S(2)}) copy-start(f32[591]{0:T(1024)S(1)} %broadcast_multiply_fusion.2) | copy-start | bytes 7096
  20.1 41.4 %copy-start.50 = (f32[591]{0:T(1024)}, f32[591]{0:T(1024)S(1)}, u32[]{:S(2)}) copy-start(f32[591]{0:T(1024)S(1)} %fusion.53) | copy-start | bytes 7096
  20.1 41.4 %copy-start.56 = (f32[591]{0:T(1024)}, f32[591]{0:T(1024)S(1)}, u32[]{:S(2)}) copy-start(f32[591]{0:T(1024)S(1)} %fusion.104) | copy-start | bytes 7096
  55.5 6.0 copy-start.54
  55.5 47.6 %copy-start.40 = (f32[768]{0:T(1024)}, f32[768]{0:T(1024)S(1)}, u32[]{:S(2)}) copy-start(f32[768]{0:T(1024)S(1)} %get-tuple-element.54) | copy-start | bytes 9220
  80.8 13.7 %copy-start.10 = (bf16[3,197,1,12,64]{1,4,3,0,2:T(8,128)(2,1)}, bf16[3,197,1,12,64]{1,4,3,0,2:T(8,128)(2,1)S(1)}, u32[]{:S(2)}) copy-start(bf16[3,197,1,12,64]{1,4,3,0,2:T(8,128)(2,1)S(1)} %copy.152) | copy-start | bytes 2723332
  92.9 3.1 copy-start
  99.2 6.5 %copy-start.19 = (f32[591,768]{1,0:T(8,128)S(1)}, f32[591,768]{1,0:T(8,128)}, u32[]{:S(2)}) copy-start(f32[591,768]{1,0:T(8,128)} %convert_multiply_fusion) | copy-start | bytes 5446660
  102.0 3.2 copy-start.34
  103.1 5.0 copy-start.42
  103.5 4.6 copy-start.16
  105.7 2.4 copy-start.48
  115.8 56.9 %all-to-all-start.2 = ((bf16[4,184,1536]{2,1,0:T(8,128)(2,1)}), bf16[4,184,1536]{2,1,0:T(8,128)(2,1)}, u32[]{:S(2)}, u32[]{:S(2)}) async-start(bf16[4,184,1536]{2,1,0:T(8,128)(2,1)} %bitcast.112), calls=%async_computation.2 | async-start | bytes 4521984 | tf_op jit(solution)/shard_map/all_to_all | solution.py:148
  172.8 57.5 %all-to-all-start = ((bf16[4,192,1536]{2,1,0:T(8,128)(2,1)}), bf16[4,192,1536]{2,1,0:T(8,128)(2,1)S(1)}, u32[]{:S(2)}, u32[]{:S(2)}) async-start(bf16[4,192,1536]{2,1,0:T(8,128)(2,1)} %bitcast.10), calls=%async_computation | async-start | bytes 4718592 | tf_op jit(solution)/shard_map/all_to_all | solution.py:148
  176.9 25.8 %copy-start.22 = (bf16[3072,768]{1,0:T(8,128)(2,1)S(1)}, bf16[3072,768]{1,0:T(8,128)(2,1)}, u32[]{:S(2)}) copy-start(bf16[3072,768]{1,0:T(8,128)(2,1)} %reshape_squeeze.3) | copy-start | bytes 14155780
  202.7 3.7 copy-start.65
  202.7 15.5 %slice-start.2 = ((s8[9437184]{0:T(1024)(128)(4,1)}), s8[4194304]{0:T(1024)(128)(4,1)S(1)}, s32[]{:S(2)}) async-start(s8[9437184]{0:T(1024)(128)(4,1)} %bitcast.117), calls=%async_computation.13 | async-start | bytes 8388608
  202.7 15.5 %slice-start.3 = ((s8[9437184]{0:T(1024)(128)(4,1)}), s8[4194304]{0:T(1024)(128)(4,1)S(1)}, s32[]{:S(2)}) async-start(s8[9437184]{0:T(1024)(128)(4,1)} %bitcast.117), calls=%async_computation.14 | async-start | bytes 8388608
  206.4 11.8 %slice-start.4 = ((s8[9437184]{0:T(1024)(128)(4,1)}), s8[1048576]{0:T(1024)(128)(4,1)S(1)}, s32[]{:S(2)}) async-start(s8[9437184]{0:T(1024)(128)(4,1)} %bitcast.117), calls=%async_computation.15 | async-start | bytes 2097152
  230.3 39.1 %copy-start.20 = (bf16[4,192,1536]{2,1,0:T(8,128)(2,1)}, bf16[4,192,1536]{2,1,0:T(8,128)(2,1)S(1)}, u32[]{:S(2)}) copy-start(bf16[4,192,1536]{2,1,0:T(8,128)(2,1)S(1)} %all-to-all-done) | copy-start | bytes 7077892
  230.3 60.8 %all-to-all-start.3 = ((bf16[4,184,1536]{2,1,0:T(8,128)(2,1)}), bf16[4,184,1536]{2,1,0:T(8,128)(2,1)}, u32[]{:S(2)}, u32[]{:S(2)}) async-start(bf16[4,184,1536]{2,1,0:T(8,128)(2,1)} %bitcast.17), calls=%async_computation.3 | async-start | bytes 4521984 | tf_op jit(solution)/shard_map/all_to_all | solution.py:184
  261.2 8.1 %copy-start.64 = (bf16[768,3072]{1,0:T(8,128)(2,1)}, bf16[768,3072]{1,0:T(8,128)(2,1)S(1)}, u32[]{:S(2)}) copy-start(bf16[768,3072]{1,0:T(8,128)(2,1)S(1)} %get-tuple-element.70) | copy-start | bytes 14155780
  280.4 8.0 %copy-start.23 = (bf16[768,3072]{1,0:T(8,128)(2,1)}, bf16[768,3072]{1,0:T(8,128)(2,1)S(1)}, u32[]{:S(2)}) copy-start(bf16[768,3072]{1,0:T(8,128)(2,1)S(1)} %add_convert_fusion.2) | copy-start | bytes 14155780
  288.6 8.0 %copy-start.49 = (f32[591,2]{0,1:T(2,128)S(1)}, f32[591,2]{0,1:T(2,128)}, u32[]{:S(2)}) copy-start(f32[591,2]{0,1:T(2,128)} %copy-done.48) | copy-start | bytes 14188
  288.6 60.4 %copy-start.59 = (s32[1504]{0:T(1024)S(1)}, s32[1504]{0:T(1024)}, u32[]{:S(2)}) copy-start(s32[1504]{0:T(1024)} %copy-done.58) | copy-start | bytes 18052
  288.6 60.4 %copy-start.63 = (s32[591]{0:T(1024)S(1)}, s32[591]{0:T(1024)}, u32[]{:S(2)}) copy-start(s32[591]{0:T(1024)} %copy-done.62) | copy-start | bytes 7096
  291.1 57.9 %all-to-all-start.1 = ((bf16[4,192,1536]{2,1,0:T(8,128)(2,1)}), bf16[4,192,1536]{2,1,0:T(8,128)(2,1)S(1)}, u32[]{:S(2)}, u32[]{:S(2)}) async-start(bf16[4,192,1536]{2,1,0:T(8,128)(2,1)} %bitcast.13), calls=%async_computation.1 | async-start | bytes 4718592 | tf_op jit(solution)/shard_map/all_to_all | solution.py:184
  296.2 186.6 %reduce-scatter.3.cloned.1.call-start = ((), (), s32[]{:S(2)}) async-start(), calls=%async_computation.8 | async-start | bytes 5529600 | tf_op jit(solution)/shard_map/reduce_scatter | solution.py:277
  349.0 4.9 copy-start.61
  353.9 5.2 copy-start.2
  353.9 5.2 copy-start.6
  353.9 5.2 copy-start.31
  359.1 2.1 copy-start.33
  359.1 2.1 copy-start.37
  359.1 2.1 copy-start.45
  359.1 2.1 copy-start.35
  359.1 2.1 copy-start.41
  359.1 2.1 copy-start.43
  361.1 2.3 copy-start.53
  368.9 7.4 %copy-start.26 = (f32[3,12,197]{2,1,0:T(8,128)S(1)}, f32[3,12,197]{2,1,0:T(8,128)}, u32[]{:S(2)}) copy-start(f32[3,12,197]{2,1,0:T(8,128)} %copy-done.25) | copy-start | bytes 85108
  371.9 9.6 %slice-start = ((s8[7372800]{0:T(1024)(128)(4,1)}), s8[3178496]{0:T(1024)(128)(4,1)S(1)}, s32[]{:S(2)}) async-start(s8[7372800]{0:T(1024)(128)(4,1)} %bitcast.110), calls=%async_computation.11 | async-start | bytes 6356992
  376.4 5.1 slice-start.1
  376.4 5.1 copy-start.11
  376.4 5.3 copy-start.12
  384.0 2.4 copy-start.14
  387.7 3.6 copy-start.17
  397.9 9.9 %copy-start.9 = (bf16[591,768]{1,0:T(8,128)(2,1)S(1)}, bf16[591,768]{1,0:T(8,128)(2,1)}, u32[]{:S(2)}) copy-start(bf16[591,768]{1,0:T(8,128)(2,1)} %param.11) | copy-start | bytes 2723332
  397.9 10.0 %copy-start.47 = (f32[591]{0:T(1024)S(1)}, f32[591]{0:T(1024)}, u32[]{:S(2)}) copy-start(f32[591]{0:T(1024)} %copy-done.46) | copy-start | bytes 7096
  397.9 10.0 %copy-start.55 = (f32[768]{0:T(1024)S(1)}, f32[768]{0:T(1024)}, u32[]{:S(2)}) copy-start(f32[768]{0:T(1024)} %copy-done.54) | copy-start | bytes 9220
  397.9 10.0 %copy-start.57 = (f32[591]{0:T(1024)S(1)}, f32[591]{0:T(1024)}, u32[]{:S(2)}) copy-start(f32[591]{0:T(1024)} %copy-done.56) | copy-start | bytes 7096
  407.9 7.0 %copy-start.24 = (bf16[591,2304]{0,1:T(8,128)(2,1)S(1)}, bf16[591,2304]{0,1:T(8,128)(2,1)}, u32[]{:S(2)}) copy-start(bf16[591,2304]{0,1:T(8,128)(2,1)} %convert_element_type.172) | copy-start | bytes 8169988
  414.9 4.7 copy-start.51
  419.6 10.0 %copy-start.18 = (f32[591,768]{1,0:T(8,128)}, f32[591,768]{1,0:T(8,128)S(1)}, u32[]{:S(2)}) copy-start(f32[591,768]{1,0:T(8,128)S(1)} %get-tuple-element.92) | copy-start | bytes 5446660
  429.6 95.2 %all-reduce.3.cloned.1.call-start = ((), (), s32[]{:S(2)}) async-start(), calls=%async_computation.9 | async-start | bytes 1228800 | tf_op jit(solution)/shard_map/psum | solution.py:278
  482.8 121.7 %reduce-scatter.5.cloned.1.call-start = ((), (), s32[]{:S(2)}) async-start(), calls=%async_computation.10 | async-start | bytes 10616832 | tf_op jit(solution)/shard_map/reduce_scatter | solution.py:190
  (16 other events, 20.1 us)
Sparse Core Ops, SparseCore 0:
  11.8 42.3 all-gather.2
  56.6 58.6 all-gather.4
  429.7 52.9 reduce-scatter.2
  484.9 39.7 all-reduce.2
  528.1 76.3 reduce-scatter.4

commit v3 on v2

--- a/solution.py
+++ b/solution.py
@@ -187,9 +187,8 @@
     expert_grads = jnp.stack(
         [grad_first, grad_second.reshape(width, ff)], axis=0
     ).astype(jnp.bfloat16)
-    expert_share = lax.psum_scatter(
-        expert_grads, "shard", scatter_dimension=1, tiled=True
-    ).astype(jnp.float32)
+    expert_share = lax.psum_scatter(expert_grads, "shard", scatter_dimension=1, tiled=True)
+    expert_share = expert_share.astype(jnp.float32)
     grad_in_share = expert_share[0][None]
     grad_back_share = expert_share[1].reshape(back_rows, width)[None]
 
@@ -224,7 +223,7 @@
     moe_in_grad = expert_part + lax.dot_general(
         logit_grad, full_router, COL_CONTRACT, preferred_element_type=jnp.float32
     )
-    norm_value, norm_back = jax.vjp(layer_norm, hidden_state, gain_two)
+    _, norm_back = jax.vjp(layer_norm, hidden_state, gain_two)
     state_part, grad_gain_two = norm_back(moe_in_grad)
     state_grad = grad_out + state_part
     branch_grad = state_grad.astype(jnp.bfloat16)
@@ -266,7 +265,7 @@
     attn_in_grad = lax.dot_general(
         projected_grad, full_qkv, COL_CONTRACT, preferred_element_type=jnp.float32
     )
-    first_value, first_back = jax.vjp(layer_norm, token_f, gain_one)
+    _, first_back = jax.vjp(layer_norm, token_f, gain_one)
     token_part, grad_gain_one = first_back(attn_in_grad)
     grad_tokens = (state_grad + token_part).astype(jnp.bfloat16)
 
@@ -290,6 +289,10 @@
 
 
 def solution(mesh):
+    return _mapped(mesh)
+
+
+def _mapped(mesh):
     return jax.shard_map(
         shards,
         mesh=mesh,

time: 624 us -> 624 us (level)
  no operation moved by 1% of the time
where the time goes in v3:
time: 624 us; the launch traced here: 615 us
  waiting for transfers between devices  235 us (38%)
  matrix products  195 us (31%)
  local copies, waits for them, and re-layouts  114 us (18%)
  other arithmetic  35.9 us (6%)
  starting transfers between devices  19 us (3%)
  between operations  16.1 us (3%)
    reduce_scatter x1, waiting for transfers between devices, shards(): lax.psum_scatter(expert_grads, 'shard', scatter_dimension=1, tiled=True)  72.8 us
    all_to_all x2, waiting for transfers between devices, shards(): lax.all_to_all(returning, 'expert', split_axis=0, concat_axis=0, tiled=True)  52.4 us
    dot_general x2, matrix products, shards(): jnp.dot(flat_arrived, expert_first, preferred_element_type=jnp.float32)  52.1 us
    all_to_all x2, waiting for transfers between devices, shards(): lax.all_to_all(outgoing[experts * start:experts * (start + size)].reshape...  40.6 us
    all_gather x1, waiting for transfers between devices, shards(): dense_full = lax.all_gather(dense_local, 'shard', axis=0, tiled=True)  32.4 us
    reduce_scatter x1, waiting for transfers between devices, shards(): lax.psum_scatter(dense_grads, 'shard', scatter_dimension=0, tiled=True)  27.7 us
    unnamed x149, local copies, waits for them, and re-layouts  23.7 us
    dot_general x2, matrix products, shards(): lax.dot_general(flat_grad, expert_second, COL_CONTRACT, preferred_element...  22.8 us
  transfers between devices with their start and end apart: 9, of which 7 were waited for; matrix products, arithmetic and copies ran while one was open for 41% of the time, Pallas kernels for 0%

profile of v3, /device:TPU:0, one launch (start us, length us, event | category | flops | bytes accessed | tf_op | source)
XLA Modules:
  0.0 615.3 jit_solution(7871678161351734495)
XLA Ops:
  9.7 1.9 concatenate.26
  13.2 2.2 pad_maximum_fusion.8
  21.7 32.4 %all-gather.3.cloned.1.call-done = bf16[768,3078]{1,0:T(8,128)(2,1)} async-done(((bf16[96,3078]{1,0:T(8,128)(2,1)}), bf16[768,3078]{1,0:T(8,128)(2,1)}) %all-gather.3.cloned.1.call-update) | async-done | bytes 4727824 | tf_op jit(solution)/shard_map/all_gather | solution.py:62
  55.5 6.0 convolution_convert_fusion.1
  61.5 9.3 %reshape.271 = bf16[3,197,3,12,64]{4,3,2,1,0:T(8,128)(2,1)} reshape(bf16[591,2304]{1,0:T(8,128)(2,1)} %convolution_convert_fusion.1) | data formatting | bytes 5446656 | tf_op jit(solution)/shard_map/reshape | solution.py:80
  70.9 6.6 %fusion.117 = (bf16[3,197,1,12,64]{4,3,2,1,0:T(8,128)(2,1)}, bf16[3,197,1,12,64]{4,3,2,1,0:T(8,128)(2,1)}, bf16[3,197,1,12,64]{4,3,2,1,0:T(8,128)(2,1)}) fusion(bf16[3,197,3,12,64]{4,3,2,1,0:T(8,128)(2,1)} %reshape.271), kind=kLoop, calls=%fused_computation.219 | loop fusion | bytes 5446656 | tf_op jit(solution)/shard_map/slice | solution.py:81
  77.5 3.3 copy.152
  80.8 4.6 copy.154
  85.5 4.6 copy.153
  90.1 2.8 multiply_reduce_fusion.1
  97.1 2.1 convert_element_type.149
  99.2 2.7 fusion.119
  106.0 2.1 fusion.14
  108.1 2.2 convolution_convert_fusion.2
  110.3 2.5 add_convert_fusion.4
  115.8 4.6 all-to-all-start.2
  120.4 2.9 fusion.35
  123.3 4.8 slice.165
  128.1 8.5 %reshape_squeeze.3 = bf16[3072,768]{1,0:T(8,128)(2,1)} reshape(bf16[1,768,3072]{2,1,0:T(8,128)(2,1)} %slice.165) | data formatting | bytes 9437184 | tf_op jit(solution)/shard_map/reshape;squeeze | solution.py:75
  136.6 36.2 %all-to-all-done.2 = bf16[4,184,1536]{2,1,0:T(8,128)(2,1)} async-done(((bf16[4,184,1536]{2,1,0:T(8,128)(2,1)}), bf16[4,184,1536]{2,1,0:T(8,128)(2,1)}, u32[]{:S(2)}, u32[]{:S(2)}) %all-to-all-start.2) | async-done | bytes 2261024 | tf_op jit(solution)/shard_map/all_to_all | solution.py:148
  172.8 4.1 all-to-all-start
  176.9 25.8 %multiply_convert_fusion.1 = (bf16[736,3072]{1,0:T(8,128)(2,1)S(1)}, f32[736,3072]{1,0:T(8,128)}, f32[736,3072]{1,0:T(8,128)}) fusion(bf16[2,768,3072]{2,1,0:T(8,128)(2,1)} %all-gather.5.cloned.1.call-done, bf16[736,1536]{1,0:T(8,128)(2,1)} %bitcast.16), kind=kOutput, calls=%fused_computation.23 | convolution fusion | flops 3619848192 | bytes 28459008 | tf_op jit(solution)/shard_map/dot_general | solution.py:159
  202.7 3.7 convolution_convert_fusion.7
  206.4 11.8 %add_convert_fusion.3 = bf16[736,3072]{1,0:T(8,128)(2,1)} fusion(f32[736,3072]{1,0:T(8,128)} %get-tuple-element.73, f32[736,3072]{1,0:T(8,128)} %get-tuple-element.86, bf16[3072,768]{1,0:T(8,128)(2,1)S(1)} %copy-done.22, bf16[736,1536]{1,0:T(8,128)(2,1)} %bitcast.16), kind=kOutput, calls=%fused_computation.22 | convolution fusion | flops 3504537600 | bytes 28459008 | tf_op jit(solution)/shard_map/dot_general | solution.py:165
  218.2 6.1 fusion.58
  225.8 4.5 all-to-all-done
  230.3 4.7 all-to-all-start.3
  235.0 26.3 %multiply_convert_fusion = (bf16[768,3072]{1,0:T(8,128)(2,1)S(1)}, f32[768,3072]{1,0:T(8,128)}, f32[768,3072]{1,0:T(8,128)}) fusion(bf16[2,768,3072]{2,1,0:T(8,128)(2,1)} %all-gather.5.cloned.1.call-done, bf16[768,1536]{1,0:T(8,128)(2,1)S(1)} %bitcast.113), kind=kOutput, calls=%fused_computation.7 | convolution fusion | flops 3777232896 | bytes 29491200 | tf_op jit(solution)/shard_map/dot_general | solution.py:159
  261.2 8.1 %convolution_convert_fusion.4 = bf16[768,768]{0,1:T(8,128)(2,1)S(1)} fusion(bf16[768,3072]{1,0:T(8,128)(2,1)S(1)} %get-tuple-element.70, bf16[3072,768]{1,0:T(8,128)(2,1)} %reshape_squeeze.3), kind=kOutput, calls=%fused_computation.119 | convolution fusion | flops 3624468480 | bytes 10616832 | tf_op jit(solution)/shard_map/dot_general | solution.py:162
  269.4 11.0 %add_convert_fusion.2 = bf16[768,3072]{1,0:T(8,128)(2,1)S(1)} fusion(f32[768,3072]{1,0:T(8,128)} %get-tuple-element.71, f32[768,3072]{1,0:T(8,128)} %get-tuple-element.87, bf16[3072,768]{1,0:T(8,128)(2,1)} %reshape_squeeze.3, bf16[768,1536]{1,0:T(8,128)(2,1)S(1)} %bitcast.114), kind=kOutput, calls=%fused_computation.6 | convolution fusion | flops 3656908800 | bytes 29491200 | tf_op jit(solution)/shard_map/dot_general | solution.py:165
  280.4 8.0 %fusion.57 = bf16[768,768]{0,1:T(8,128)(2,1)S(1)} fusion(bf16[768,3072]{1,0:T(8,128)(2,1)S(1)} %add_convert_fusion.2, bf16[2,768,3072]{2,1,0:T(8,128)(2,1)} %all-gather.5.cloned.1.call-done), kind=kOutput, calls=%fused_computation.117 | convolution fusion | flops 3624468480 | bytes 10616832 | tf_op jit(solution)/shard_map/dot_general | solution.py:169
  288.6 2.5 copy.130
  291.1 5.1 all-to-all-start.1
  296.6 52.4 %all-to-all-done.1 = bf16[4,192,1536]{2,1,0:T(8,128)(2,1)S(1)} async-done(((bf16[4,192,1536]{2,1,0:T(8,128)(2,1)}), bf16[4,192,1536]{2,1,0:T(8,128)(2,1)S(1)}, u32[]{:S(2)}, u32[]{:S(2)}) %all-to-all-start.1) | async-done | bytes 2359328 | tf_op jit(solution)/shard_map/all_to_all | solution.py:184
  349.0 4.9 fusion.16
  354.0 5.1 fusion.12
  359.1 1.9 multiply_reduce_fusion.5
  361.3 2.1 multiply_reduce_fusion.2
  366.7 2.2 convolution_convert_fusion.8
  368.9 2.9 reshape.272
  371.9 4.5 copy.132
  376.4 5.1 fusion.62
  381.7 2.3 multiply_reduce_fusion
  384.0 2.3 multiply_convert_fusion.2
  389.2 2.1 convolution_convert_fusion.6
  392.3 5.6 copy.137
  397.9 9.9 %convert_element_type.172 = bf16[591,2304]{0,1:T(8,128)(2,1)} reshape(bf16[3,197,3,12,64]{1,0,4,3,2:T(4,128)(2,1)} %copy.137) | data formatting | bytes 5446656 | tf_op jit(solution)/shard_map/convert_element_type | solution.py:260
  407.9 7.0 %convolution_convert_fusion = bf16[768,2304]{1,0:T(8,128)(2,1)} fusion(bf16[591,2304]{0,1:T(8,128)(2,1)} %convert_element_type.172, bf16[591,768]{1,0:T(8,128)(2,1)S(1)} %copy-done.9, f32[768]{0:T(1024)S(1)} %copy-done.55, f32[591]{0:T(1024)S(1)} %copy-done.57, f32[591]{0:T(1024)S(1)} %copy-done.47), kind=kOutput, calls=%fused_computation.52 | convolution fusion | flops 2095554816 | bytes 7177848 | tf_op jit(solution)/shard_map/dot_general | solution.py:262
  414.9 4.7 fusion.54
  421.1 8.4 %concatenate.32 = bf16[768,3078]{1,0:T(8,128)(2,1)} concatenate(bf16[768,2304]{1,0:T(8,128)(2,1)} %convolution_convert_fusion, bf16[768,768]{1,0:T(8,128)(2,1)} %convolution_convert_fusion.6, bf16[768,4]{1,0:T(8,128)(2,1)S(1)} %copy.139, bf16[768,1]{1,0:T(8,128)(2,1)S(1)} %broadcast_in_dim.40, bf16[768,1]{1,0:T(8,128)(2,1)S(1)} %broadcast_in_dim.41), dimensions={1} | concatenate | bytes 9455616 | tf_op jit(solution)/shard_map/concatenate | solution.py:272
  429.6 1.6 copy-done.21
  431.2 6.0 fusion.72
  437.2 9.2 %fusion.78 = f32[768,3072]{1,0:T(8,128)} fusion(bf16[768,3072]{1,0:T(8,128)(2,1)} %copy-done.23, bf16[768,1536]{1,0:T(8,128)(2,1)S(1)} %bitcast.116), kind=kOutput, calls=%fused_computation.144 | convolution fusion | flops 3623878656 | bytes 15335424 | tf_op jit(solution)/shard_map/dot_general | solution.py:175
  446.4 8.7 %add_convert_fusion = bf16[3072,768]{1,0:T(8,128)(2,1)} fusion(f32[3072,768]{1,0:T(8,128)S(1)} %fusion.72, bf16[736,3072]{1,0:T(8,128)(2,1)} %copy-done.65, bf16[736,1536]{1,0:T(8,128)(2,1)} %bitcast.16), kind=kOutput, calls=%fused_computation.4 | convolution fusion | flops 3477602304 | bytes 19808256 | tf_op jit(solution)/shard_map/dot_general | solution.py:172
  455.0 27.7 %reduce-scatter.3.cloned.1.call-done = bf16[96,3078]{1,0:T(8,128)(2,1)} async-done(((bf16[768,3078]{1,0:T(8,128)(2,1)}), bf16[96,3078]{1,0:T(8,128)(2,1)}) %reduce-scatter.3.cloned.1.call-update) | async-done | bytes 590992 | tf_op jit(solution)/shard_map/reduce_scatter | solution.py:276
  482.8 11.5 %fusion.21 = bf16[1,768,3072]{2,1,0:T(8,128)(2,1)} fusion(f32[768,3072]{1,0:T(8,128)} %fusion.78, bf16[736,3072]{1,0:T(8,128)(2,1)} %add_convert_fusion.3, bf16[736,1536]{1,0:T(8,128)(2,1)} %bitcast.16), kind=kOutput, calls=%fused_computation.60 | convolution fusion | flops 3477602304 | bytes 19808256 | tf_op jit(solution)/shard_map/dot_general | solution.py:175
  494.3 8.7 %stack_reshape.4 = bf16[1,768,3072]{2,1,0:T(8,128)(2,1)} reshape(bf16[3072,768]{1,0:T(8,128)(2,1)} %add_convert_fusion) | data formatting | bytes 9437184 | tf_op jit(solution)/shard_map/stack;reshape | solution.py:187
  503.1 8.3 %pad_maximum_fusion = bf16[2,768,3072]{2,1,0:T(8,128)(2,1)} fusion(bf16[1,768,3072]{2,1,0:T(8,128)(2,1)} %stack_reshape.4, bf16[1,768,3072]{2,1,0:T(8,128)(2,1)} %fusion.21), kind=kLoop, calls=%fused_computation.3 | loop fusion | flops 4718592 | bytes 18874368 | tf_op jit(solution)/shard_map/stack | solution.py:187
  513.2 3.1 add_convert_fusion.5
  516.2 8.5 %all-reduce.3.cloned.1.call-done = bf16[96,3078]{1,0:T(8,128)(2,1)} async-done(((bf16[96,3078]{1,0:T(8,128)(2,1)}), bf16[96,3078]{1,0:T(8,128)(2,1)}) %all-reduce.3.cloned.1.call-update) | async-done | bytes 590992 | tf_op jit(solution)/shard_map/psum | solution.py:277
  526.1 2.0 slice.174
  528.1 1.6 slice.175
  531.6 72.8 %reduce-scatter.5.cloned.1.call-done = bf16[2,96,3072]{2,1,0:T(8,128)(2,1)} async-done(((bf16[2,768,3072]{2,1,0:T(8,128)(2,1)}), bf16[2,96,3072]{2,1,0:T(8,128)(2,1)}) %reduce-scatter.5.cloned.1.call-update) | async-done | bytes 1179664 | tf_op jit(solution)/shard_map/reduce_scatter | solution.py:190
  604.5 2.5 fusion.118
  (234 shorter events, 39.6 us)
Async XLA Ops:
  7.2 9.3 %copy-start.38 = (s32[591,2]{0,1:T(2,128)S(1)}, s32[591,2]{0,1:T(2,128)}, u32[]{:S(2)}) copy-start(s32[591,2]{0,1:T(2,128)} %param.13) | copy-start | bytes 14188
  7.2 46.9 %all-gather.3.cloned.1.call-start = ((), (), s32[]{:S(2)}) async-start(), calls=%async_computation.6 | async-start | bytes 5529600 | tf_op jit(solution)/shard_map/all_gather | solution.py:62
  8.0 11.4 %copy-start.8 = (bf16[591,768]{1,0:T(8,128)(2,1)S(1)}, bf16[591,768]{1,0:T(8,128)(2,1)}, u32[]{:S(2)}) copy-start(bf16[591,768]{1,0:T(8,128)(2,1)} %param.11) | copy-start | bytes 2723332
  11.6 8.5 %copy-start.5 = (bf16[591,768]{1,0:T(8,128)(2,1)S(1)}, bf16[591,768]{1,0:T(8,128)(2,1)}, u32[]{:S(2)}) copy-start(bf16[591,768]{1,0:T(8,128)(2,1)} %param.21) | copy-start | bytes 2723332
  11.6 111.7 %all-gather.5.cloned.1.call-start = ((), (), s32[]{:S(2)}) async-start(), calls=%async_computation.7 | async-start | bytes 10616832 | tf_op jit(solution)/shard_map/all_gather | solution.py:73
  19.3 85.8 %copy-start.30 = (f32[591]{0:T(1024)}, f32[591]{0:T(1024)S(1)}, u32[]{:S(2)}) copy-start(f32[591]{0:T(1024)S(1)} %fusion.106) | copy-start | bytes 7096
  19.4 90.9 %copy-start.58 = (s32[1504]{0:T(1024)}, s32[1504]{0:T(1024)S(1)}, u32[]{:S(2)}) copy-start(s32[1504]{0:T(1024)S(1)} %pad_add_fusion) | copy-start | bytes 18052
  19.4 88.7 %copy-start.60 = (s32[591]{0:T(1024)}, s32[591]{0:T(1024)S(1)}, u32[]{:S(2)}) copy-start(s32[591]{0:T(1024)S(1)} %get-tuple-element.67) | copy-start | bytes 7096
  19.4 90.9 %copy-start.62 = (s32[591]{0:T(1024)}, s32[591]{0:T(1024)S(1)}, u32[]{:S(2)}) copy-start(s32[591]{0:T(1024)S(1)} %get-tuple-element.66) | copy-start | bytes 7096
  19.7 41.8 %copy-start.46 = (f32[591]{0:T(1024)}, f32[591]{0:T(1024)S(1)}, u32[]{:S(2)}) copy-start(f32[591]{0:T(1024)S(1)} %broadcast_multiply_fusion.2) | copy-start | bytes 7096
  20.1 41.4 %copy-start.50 = (f32[591]{0:T(1024)}, f32[591]{0:T(1024)S(1)}, u32[]{:S(2)}) copy-start(f32[591]{0:T(1024)S(1)} %fusion.53) | copy-start | bytes 7096
  20.1 41.4 %copy-start.56 = (f32[591]{0:T(1024)}, f32[591]{0:T(1024)S(1)}, u32[]{:S(2)}) copy-start(f32[591]{0:T(1024)S(1)} %fusion.104) | copy-start | bytes 7096
  55.5 6.0 copy-start.54
  55.5 47.6 %copy-start.40 = (f32[768]{0:T(1024)}, f32[768]{0:T(1024)S(1)}, u32[]{:S(2)}) copy-start(f32[768]{0:T(1024)S(1)} %get-tuple-element.54) | copy-start | bytes 9220
  80.8 13.7 %copy-start.10 = (bf16[3,197,1,12,64]{1,4,3,0,2:T(8,128)(2,1)}, bf16[3,197,1,12,64]{1,4,3,0,2:T(8,128)(2,1)S(1)}, u32[]{:S(2)}) copy-start(bf16[3,197,1,12,64]{1,4,3,0,2:T(8,128)(2,1)S(1)} %copy.152) | copy-start | bytes 2723332
  92.9 3.1 copy-start
  99.2 6.5 %copy-start.19 = (f32[591,768]{1,0:T(8,128)S(1)}, f32[591,768]{1,0:T(8,128)}, u32[]{:S(2)}) copy-start(f32[591,768]{1,0:T(8,128)} %convert_multiply_fusion) | copy-start | bytes 5446660
  102.0 3.2 copy-start.34
  103.1 5.0 copy-start.42
  103.5 4.6 copy-start.16
  105.7 2.4 copy-start.48
  115.8 56.9 %all-to-all-start.2 = ((bf16[4,184,1536]{2,1,0:T(8,128)(2,1)}), bf16[4,184,1536]{2,1,0:T(8,128)(2,1)}, u32[]{:S(2)}, u32[]{:S(2)}) async-start(bf16[4,184,1536]{2,1,0:T(8,128)(2,1)} %bitcast.112), calls=%async_computation.2 | async-start | bytes 4521984 | tf_op jit(solution)/shard_map/all_to_all | solution.py:148
  172.8 57.5 %all-to-all-start = ((bf16[4,192,1536]{2,1,0:T(8,128)(2,1)}), bf16[4,192,1536]{2,1,0:T(8,128)(2,1)S(1)}, u32[]{:S(2)}, u32[]{:S(2)}) async-start(bf16[4,192,1536]{2,1,0:T(8,128)(2,1)} %bitcast.10), calls=%async_computation | async-start | bytes 4718592 | tf_op jit(solution)/shard_map/all_to_all | solution.py:148
  176.9 25.8 %copy-start.22 = (bf16[3072,768]{1,0:T(8,128)(2,1)S(1)}, bf16[3072,768]{1,0:T(8,128)(2,1)}, u32[]{:S(2)}) copy-start(bf16[3072,768]{1,0:T(8,128)(2,1)} %reshape_squeeze.3) | copy-start | bytes 14155780
  202.7 3.7 copy-start.65
  202.7 15.5 %slice-start.2 = ((s8[9437184]{0:T(1024)(128)(4,1)}), s8[4194304]{0:T(1024)(128)(4,1)S(1)}, s32[]{:S(2)}) async-start(s8[9437184]{0:T(1024)(128)(4,1)} %bitcast.117), calls=%async_computation.13 | async-start | bytes 8388608
  202.7 15.5 %slice-start.3 = ((s8[9437184]{0:T(1024)(128)(4,1)}), s8[4194304]{0:T(1024)(128)(4,1)S(1)}, s32[]{:S(2)}) async-start(s8[9437184]{0:T(1024)(128)(4,1)} %bitcast.117), calls=%async_computation.14 | async-start | bytes 8388608
  206.4 11.8 %slice-start.4 = ((s8[9437184]{0:T(1024)(128)(4,1)}), s8[1048576]{0:T(1024)(128)(4,1)S(1)}, s32[]{:S(2)}) async-start(s8[9437184]{0:T(1024)(128)(4,1)} %bitcast.117), calls=%async_computation.15 | async-start | bytes 2097152
  230.3 39.1 %copy-start.20 = (bf16[4,192,1536]{2,1,0:T(8,128)(2,1)}, bf16[4,192,1536]{2,1,0:T(8,128)(2,1)S(1)}, u32[]{:S(2)}) copy-start(bf16[4,192,1536]{2,1,0:T(8,128)(2,1)S(1)} %all-to-all-done) | copy-start | bytes 7077892
  230.3 60.8 %all-to-all-start.3 = ((bf16[4,184,1536]{2,1,0:T(8,128)(2,1)}), bf16[4,184,1536]{2,1,0:T(8,128)(2,1)}, u32[]{:S(2)}, u32[]{:S(2)}) async-start(bf16[4,184,1536]{2,1,0:T(8,128)(2,1)} %bitcast.17), calls=%async_computation.3 | async-start | bytes 4521984 | tf_op jit(solution)/shard_map/all_to_all | solution.py:184
  261.2 8.1 %copy-start.64 = (bf16[768,3072]{1,0:T(8,128)(2,1)}, bf16[768,3072]{1,0:T(8,128)(2,1)S(1)}, u32[]{:S(2)}) copy-start(bf16[768,3072]{1,0:T(8,128)(2,1)S(1)} %get-tuple-element.70) | copy-start | bytes 14155780
  280.4 8.0 %copy-start.23 = (bf16[768,3072]{1,0:T(8,128)(2,1)}, bf16[768,3072]{1,0:T(8,128)(2,1)S(1)}, u32[]{:S(2)}) copy-start(bf16[768,3072]{1,0:T(8,128)(2,1)S(1)} %add_convert_fusion.2) | copy-start | bytes 14155780
  288.6 8.0 %copy-start.49 = (f32[591,2]{0,1:T(2,128)S(1)}, f32[591,2]{0,1:T(2,128)}, u32[]{:S(2)}) copy-start(f32[591,2]{0,1:T(2,128)} %copy-done.48) | copy-start | bytes 14188
  288.6 60.4 %copy-start.59 = (s32[1504]{0:T(1024)S(1)}, s32[1504]{0:T(1024)}, u32[]{:S(2)}) copy-start(s32[1504]{0:T(1024)} %copy-done.58) | copy-start | bytes 18052
  288.6 60.4 %copy-start.63 = (s32[591]{0:T(1024)S(1)}, s32[591]{0:T(1024)}, u32[]{:S(2)}) copy-start(s32[591]{0:T(1024)} %copy-done.62) | copy-start | bytes 7096
  291.1 57.9 %all-to-all-start.1 = ((bf16[4,192,1536]{2,1,0:T(8,128)(2,1)}), bf16[4,192,1536]{2,1,0:T(8,128)(2,1)S(1)}, u32[]{:S(2)}, u32[]{:S(2)}) async-start(bf16[4,192,1536]{2,1,0:T(8,128)(2,1)} %bitcast.13), calls=%async_computation.1 | async-start | bytes 4718592 | tf_op jit(solution)/shard_map/all_to_all | solution.py:184
  296.2 186.6 %reduce-scatter.3.cloned.1.call-start = ((), (), s32[]{:S(2)}) async-start(), calls=%async_computation.8 | async-start | bytes 5529600 | tf_op jit(solution)/shard_map/reduce_scatter | solution.py:276
  349.0 4.9 copy-start.61
  353.9 5.2 copy-start.2
  353.9 5.2 copy-start.6
  353.9 5.2 copy-start.31
  359.1 2.1 copy-start.33
  359.1 2.1 copy-start.37
  359.1 2.1 copy-start.45
  359.1 2.1 copy-start.35
  359.1 2.1 copy-start.41
  359.1 2.1 copy-start.43
  361.1 2.3 copy-start.53
  368.9 7.4 %copy-start.26 = (f32[3,12,197]{2,1,0:T(8,128)S(1)}, f32[3,12,197]{2,1,0:T(8,128)}, u32[]{:S(2)}) copy-start(f32[3,12,197]{2,1,0:T(8,128)} %copy-done.25) | copy-start | bytes 85108
  371.9 9.6 %slice-start = ((s8[7372800]{0:T(1024)(128)(4,1)}), s8[3178496]{0:T(1024)(128)(4,1)S(1)}, s32[]{:S(2)}) async-start(s8[7372800]{0:T(1024)(128)(4,1)} %bitcast.110), calls=%async_computation.11 | async-start | bytes 6356992
  376.4 5.1 slice-start.1
  376.4 5.1 copy-start.11
  376.4 5.3 copy-start.12
  384.0 2.4 copy-start.14
  387.7 3.6 copy-start.17
  397.9 9.9 %copy-start.9 = (bf16[591,768]{1,0:T(8,128)(2,1)S(1)}, bf16[591,768]{1,0:T(8,128)(2,1)}, u32[]{:S(2)}) copy-start(bf16[591,768]{1,0:T(8,128)(2,1)} %param.11) | copy-start | bytes 2723332
  397.9 10.0 %copy-start.47 = (f32[591]{0:T(1024)S(1)}, f32[591]{0:T(1024)}, u32[]{:S(2)}) copy-start(f32[591]{0:T(1024)} %copy-done.46) | copy-start | bytes 7096
  397.9 10.0 %copy-start.55 = (f32[768]{0:T(1024)S(1)}, f32[768]{0:T(1024)}, u32[]{:S(2)}) copy-start(f32[768]{0:T(1024)} %copy-done.54) | copy-start | bytes 9220
  397.9 10.0 %copy-start.57 = (f32[591]{0:T(1024)S(1)}, f32[591]{0:T(1024)}, u32[]{:S(2)}) copy-start(f32[591]{0:T(1024)} %copy-done.56) | copy-start | bytes 7096
  407.9 7.0 %copy-start.24 = (bf16[591,2304]{0,1:T(8,128)(2,1)S(1)}, bf16[591,2304]{0,1:T(8,128)(2,1)}, u32[]{:S(2)}) copy-start(bf16[591,2304]{0,1:T(8,128)(2,1)} %convert_element_type.172) | copy-start | bytes 8169988
  414.9 4.7 copy-start.51
  419.6 10.0 %copy-start.18 = (f32[591,768]{1,0:T(8,128)}, f32[591,768]{1,0:T(8,128)S(1)}, u32[]{:S(2)}) copy-start(f32[591,768]{1,0:T(8,128)S(1)} %get-tuple-element.92) | copy-start | bytes 5446660
  429.6 95.2 %all-reduce.3.cloned.1.call-start = ((), (), s32[]{:S(2)}) async-start(), calls=%async_computation.9 | async-start | bytes 1228800 | tf_op jit(solution)/shard_map/psum | solution.py:277
  482.8 121.7 %reduce-scatter.5.cloned.1.call-start = ((), (), s32[]{:S(2)}) async-start(), calls=%async_computation.10 | async-start | bytes 10616832 | tf_op jit(solution)/shard_map/reduce_scatter | solution.py:190
  (16 other events, 20.1 us)
Sparse Core Ops, SparseCore 0:
  11.8 42.3 all-gather.2
  56.6 58.6 all-gather.4
  429.7 52.9 reduce-scatter.2
  484.9 39.7 all-reduce.2
  528.1 76.3 reduce-scatter.4

commit v4 on v3

--- a/solution.py
+++ b/solution.py
@@ -112,8 +112,10 @@
     slot_index = jnp.sum(before * flat_picks, axis=1).reshape(rows, 2)
     position = jnp.where(live_int[:, None] > 0, routes * capacity + slot_index, overflow)
 
-    half_cap = 8 * ((capacity + 15) // 16)
-    chunk_sizes = [half_cap, capacity - half_cap] if capacity > half_cap else [capacity]
+    n_chunks = 4
+    part_cap = 8 * ((capacity + 8 * n_chunks - 1) // (8 * n_chunks))
+    chunk_sizes = [min(part_cap, capacity - k * part_cap) for k in range(n_chunks)]
+    chunk_sizes = [size for size in chunk_sizes if size > 0]
     chunk_starts = [sum(chunk_sizes[:k]) for k in range(len(chunk_sizes))]
     slot_ids = jnp.concatenate(
         [

time: 624 us -> 650 us (1.042)
  matrix products: 195 us -> 239 us
  waiting for transfers between devices: 235 us -> 199 us
  starting transfers between devices: 19 us -> 35.9 us
    reduce_scatter x1, waiting for transfers between devices: 27.7 us -> 9.14 us  [shards(): lax.psum_scatter(dense_grads, 'shard', scatter_dimension=0, tiled=True)]
    all_to_all x2 -> x4, waiting for transfers between devices: 40.6 us -> 25.6 us  [shards(): lax.all_to_all(outgoing[experts * start:experts * (start + size)].reshape...]
    dot_general x2 -> x4, matrix products: 14.6 us -> 28.8 us  [shards(): lax.dot_general(activated, flat_grad, ROW_CONTRACT, preferred_element_typ...]
    dot_general x2 -> x4, matrix products: 20.7 us -> 31 us  [shards(): lax.dot_general(flat_arrived, pre_grad, ROW_CONTRACT, preferred_element_t...]
    all_to_all x2 -> x4, starting transfers between devices: 9.73 us -> 18.5 us  [shards(): lax.all_to_all(returning, 'expert', split_axis=0, concat_axis=0, tiled=True)]
    all_to_all x2 -> x4, starting transfers between devices: 8.72 us -> 16.5 us  [shards(): lax.all_to_all(outgoing[experts * start:experts * (start + size)].reshape...]
    dot_general x2 -> x4, matrix products: 52.1 us -> 58.8 us  [shards(): jnp.dot(flat_arrived, expert_first, preferred_element_type=jnp.float32)]
    dot_general x2 -> x4, matrix products: 22.8 us -> 29 us  [shards(): lax.dot_general(flat_grad, expert_second, COL_CONTRACT, preferred_element...]
  transfers between devices with their start and end apart: 9 -> 13, of which waited for: 7 -> 10; matrix products, arithmetic and copies ran while one was open for 41% -> 46% of each run, Pallas kernels for 0% -> 0%
where the time goes in v4:
time: 650 us; the launch traced here: 641 us
  matrix products  239 us (37%)
  waiting for transfers between devices  199 us (31%)
  local copies, waits for them, and re-layouts  112 us (17%)
  other arithmetic  38.2 us (6%)
  starting transfers between devices  35.9 us (6%)
  between operations  16.4 us (3%)
    reduce_scatter x1, waiting for transfers between devices, shards(): lax.psum_scatter(expert_grads, 'shard', scatter_dimension=1, tiled=True)  72.8 us
    dot_general x4, matrix products, shards(): jnp.dot(flat_arrived, expert_first, preferred_element_type=jnp.float32)  58.8 us
    all_to_all x4, waiting for transfers between devices, shards(): lax.all_to_all(returning, 'expert', split_axis=0, concat_axis=0, tiled=True)  55.1 us
    all_gather x1, waiting for transfers between devices, shards(): dense_full = lax.all_gather(dense_local, 'shard', axis=0, tiled=True)  32.2 us
    dot_general x4, matrix products, shards(): lax.dot_general(flat_arrived, pre_grad, ROW_CONTRACT, preferred_element_t...  31 us
    dot_general x4, matrix products, shards(): lax.dot_general(flat_grad, expert_second, COL_CONTRACT, preferred_element...  29 us
    dot_general x4, matrix products, shards(): lax.dot_general(activated, flat_grad, ROW_CONTRACT, preferred_element_typ...  28.8 us
    all_to_all x4, waiting for transfers between devices, shards(): lax.all_to_all(outgoing[experts * start:experts * (start + size)].reshape...  25.6 us
  transfers between devices with their start and end apart: 13, of which 10 were waited for; matrix products, arithmetic and copies ran while one was open for 46% of the time, Pallas kernels for 0%

profile of v4, /device:TPU:0, one launch (start us, length us, event | category | flops | bytes accessed | tf_op | source)
XLA Modules:
  0.0 640.7 jit_solution(6204462486399999063)
XLA Ops:
  22.0 32.2 %all-gather.3.cloned.1.call-done = bf16[768,3078]{1,0:T(8,128)(2,1)} async-done(((bf16[96,3078]{1,0:T(8,128)(2,1)}), bf16[768,3078]{1,0:T(8,128)(2,1)}) %all-gather.3.cloned.1.call-update) | async-done | bytes 4727824 | tf_op jit(solution)/shard_map/all_gather | solution.py:62
  55.5 6.0 convolution_convert_fusion.1
  61.5 9.4 %reshape.317 = bf16[3,197,3,12,64]{4,3,2,1,0:T(8,128)(2,1)} reshape(bf16[591,2304]{1,0:T(8,128)(2,1)} %convolution_convert_fusion.1) | data formatting | bytes 5446656 | tf_op jit(solution)/shard_map/reshape | solution.py:80
  70.8 6.7 %fusion.149 = (bf16[3,197,1,12,64]{4,3,2,1,0:T(8,128)(2,1)}, bf16[3,197,1,12,64]{4,3,2,1,0:T(8,128)(2,1)}, bf16[3,197,1,12,64]{4,3,2,1,0:T(8,128)(2,1)}) fusion(bf16[3,197,3,12,64]{4,3,2,1,0:T(8,128)(2,1)} %reshape.317), kind=kLoop, calls=%fused_computation.283 | loop fusion | bytes 5446656 | tf_op jit(solution)/shard_map/slice | solution.py:81
  77.5 3.3 copy.147
  80.8 4.6 copy.149
  85.5 4.6 copy.148
  90.1 2.8 multiply_reduce_fusion.1
  110.2 2.8 add_convert_fusion.5
  115.4 4.6 all-to-all-start.6
  120.0 3.0 fusion.69
  123.0 4.9 slice.189
  127.9 8.5 %reshape_squeeze.3 = bf16[3072,768]{1,0:T(8,128)(2,1)} reshape(bf16[1,768,3072]{2,1,0:T(8,128)(2,1)} %slice.189) | data formatting | bytes 9437184 | tf_op jit(solution)/shard_map/reshape;squeeze | solution.py:75
  136.4 10.5 %all-to-all-done.6 = bf16[4,88,1536]{2,1,0:T(8,128)(2,1)S(1)} async-done(((bf16[4,88,1536]{2,1,0:T(8,128)(2,1)}), bf16[4,88,1536]{2,1,0:T(8,128)(2,1)S(1)}, u32[]{:S(2)}, u32[]{:S(2)}) %all-to-all-start.6) | async-done | bytes 1081376 | tf_op jit(solution)/shard_map/all_to_all | solution.py:150
  146.9 3.5 all-to-all-start.4
  150.4 13.9 %multiply_convert_fusion.4 = (bf16[352,3072]{1,0:T(8,128)(2,1)}, f32[352,3072]{1,0:T(8,128)}, f32[352,3072]{1,0:T(8,128)}) fusion(bf16[2,768,3072]{2,1,0:T(8,128)(2,1)} %all-gather.5.cloned.1.call-done, bf16[352,1536]{1,0:T(8,128)(2,1)S(1)} %bitcast.153), kind=kOutput, calls=%fused_computation.85 | convolution fusion | flops 1731231744 | bytes 16072704 | tf_op jit(solution)/shard_map/dot_general | solution.py:161
  164.3 14.2 %all-to-all-done.4 = bf16[4,96,1536]{2,1,0:T(8,128)(2,1)S(1)} async-done(((bf16[4,96,1536]{2,1,0:T(8,128)(2,1)}), bf16[4,96,1536]{2,1,0:T(8,128)(2,1)S(1)}, u32[]{:S(2)}, u32[]{:S(2)}) %all-to-all-start.4) | async-done | bytes 1179680 | tf_op jit(solution)/shard_map/all_to_all | solution.py:150
  178.5 4.0 all-to-all-start.2
  182.5 15.0 %multiply_convert_fusion.1 = (bf16[384,3072]{1,0:T(8,128)(2,1)}, f32[384,3072]{1,0:T(8,128)}, f32[384,3072]{1,0:T(8,128)}) fusion(bf16[2,768,3072]{2,1,0:T(8,128)(2,1)} %all-gather.5.cloned.1.call-done, bf16[384,1536]{1,0:T(8,128)(2,1)S(1)} %bitcast.136), kind=kOutput, calls=%fused_computation.35 | convolution fusion | flops 1888616448 | bytes 17104896 | tf_op jit(solution)/shard_map/dot_general | solution.py:161
  197.5 2.6 convolution_convert_fusion.14
  200.1 5.4 add_convert_fusion.6
  206.9 2.7 convolution_convert_fusion.13
  210.5 4.3 all-to-all-start
  214.9 15.0 %multiply_convert_fusion.2 = (bf16[384,3072]{1,0:T(8,128)(2,1)}, f32[384,3072]{1,0:T(8,128)}, f32[384,3072]{1,0:T(8,128)}) fusion(bf16[2,768,3072]{2,1,0:T(8,128)(2,1)} %all-gather.5.cloned.1.call-done, bf16[384,1536]{1,0:T(8,128)(2,1)S(1)} %bitcast.140), kind=kOutput, calls=%fused_computation.49 | convolution fusion | flops 1888616448 | bytes 17104896 | tf_op jit(solution)/shard_map/dot_general | solution.py:161
  231.0 5.9 convolution_convert_fusion.8
  237.0 7.3 %add_convert_fusion.2 = bf16[384,3072]{1,0:T(8,128)(2,1)} fusion(f32[384,3072]{1,0:T(8,128)S(1)} %bitcast.168, f32[384,3072]{1,0:T(8,128)S(1)} %bitcast.170, bf16[3072,768]{1,0:T(8,128)(2,1)} %reshape_squeeze.3, bf16[384,1536]{1,0:T(8,128)(2,1)S(1)} %bitcast.137), kind=kOutput, calls=%fused_computation.34 | convolution fusion | flops 1828454400 | bytes 17104896 | tf_op jit(solution)/shard_map/dot_general | solution.py:167
  244.3 5.3 all-to-all-start.7
  249.6 15.0 %multiply_convert_fusion.3 = (bf16[384,3072]{1,0:T(8,128)(2,1)}, f32[384,3072]{1,0:T(8,128)}, f32[384,3072]{1,0:T(8,128)}) fusion(bf16[2,768,3072]{2,1,0:T(8,128)(2,1)} %all-gather.5.cloned.1.call-done, bf16[384,1536]{1,0:T(8,128)(2,1)S(1)} %bitcast.144), kind=kOutput, calls=%fused_computation.63 | convolution fusion | flops 1888616448 | bytes 17104896 | tf_op jit(solution)/shard_map/dot_general | solution.py:161
  264.6 4.4 convolution_convert_fusion.7
  270.2 8.7 %add_convert_fusion.3 = bf16[384,3072]{1,0:T(8,128)(2,1)} fusion(f32[384,3072]{1,0:T(8,128)} %get-tuple-element.73, f32[384,3072]{1,0:T(8,128)} %get-tuple-element.95, bf16[3072,768]{1,0:T(8,128)(2,1)} %reshape_squeeze.3, bf16[384,1536]{1,0:T(8,128)(2,1)S(1)} %bitcast.141), kind=kOutput, calls=%fused_computation.48 | convolution fusion | flops 1828454400 | bytes 17104896 | tf_op jit(solution)/shard_map/dot_general | solution.py:167
  278.8 5.3 all-to-all-start.5
  284.2 5.2 convolution_convert_fusion.10
  289.4 4.5 convolution_convert_fusion.9
  297.0 13.5 %all-to-all-done.5 = bf16[4,96,1536]{2,1,0:T(8,128)(2,1)S(1)} async-done(((bf16[4,96,1536]{2,1,0:T(8,128)(2,1)}), bf16[4,96,1536]{2,1,0:T(8,128)(2,1)S(1)}, u32[]{:S(2)}, u32[]{:S(2)}) %all-to-all-start.5) | async-done | bytes 1179680 | tf_op jit(solution)/shard_map/all_to_all | solution.py:186
  310.6 4.3 all-to-all-start.3
  314.9 7.6 %add_convert_fusion.4 = bf16[384,3072]{1,0:T(8,128)(2,1)S(1)} fusion(f32[384,3072]{1,0:T(8,128)} %get-tuple-element.71, f32[384,3072]{1,0:T(8,128)} %get-tuple-element.96, bf16[3072,768]{1,0:T(8,128)(2,1)} %reshape_squeeze.3, bf16[384,1536]{1,0:T(8,128)(2,1)S(1)} %bitcast.145), kind=kOutput, calls=%fused_computation.62 | convolution fusion | flops 1828454400 | bytes 17104896 | tf_op jit(solution)/shard_map/dot_general | solution.py:167
  322.5 5.3 convolution_convert_fusion.11
  329.0 14.1 %all-to-all-done.3 = bf16[4,96,1536]{2,1,0:T(8,128)(2,1)} async-done(((bf16[4,96,1536]{2,1,0:T(8,128)(2,1)}), bf16[4,96,1536]{2,1,0:T(8,128)(2,1)}, u32[]{:S(2)}, u32[]{:S(2)}) %all-to-all-start.3) | async-done | bytes 1179680 | tf_op jit(solution)/shard_map/all_to_all | solution.py:186
  343.0 3.5 all-to-all-start.1
  347.1 27.5 %all-to-all-done.1 = bf16[4,96,1536]{2,1,0:T(8,128)(2,1)S(1)} async-done(((bf16[4,96,1536]{2,1,0:T(8,128)(2,1)}), bf16[4,96,1536]{2,1,0:T(8,128)(2,1)S(1)}, u32[]{:S(2)}, u32[]{:S(2)}) %all-to-all-start.1) | async-done | bytes 1179680 | tf_op jit(solution)/shard_map/all_to_all | solution.py:186
  374.6 4.7 fusion.4
  379.4 4.9 fusion
  393.8 2.9 reshape.318
  396.7 4.5 copy.127
  401.3 5.0 fusion.67
  417.2 5.6 copy.132
  422.8 9.9 %convert_element_type.204 = bf16[591,2304]{0,1:T(8,128)(2,1)} reshape(bf16[3,197,3,12,64]{1,0,4,3,2:T(4,128)(2,1)} %copy.132) | data formatting | bytes 5446656 | tf_op jit(solution)/shard_map/convert_element_type | solution.py:262
  432.8 7.2 %convolution_convert_fusion = bf16[768,2304]{1,0:T(8,128)(2,1)} fusion(bf16[591,2304]{0,1:T(8,128)(2,1)} %convert_element_type.204, bf16[591,768]{1,0:T(8,128)(2,1)S(1)} %copy-done.9, f32[768]{0:T(1024)S(1)} %copy-done.74, f32[591]{0:T(1024)S(1)} %copy-done.76, f32[591]{0:T(1024)S(1)} %copy-done.66), kind=kOutput, calls=%fused_computation.28 | convolution fusion | flops 2095554816 | bytes 7177848 | tf_op jit(solution)/shard_map/dot_general | solution.py:264
  439.9 4.7 fusion.61
  446.2 8.5 %concatenate.40 = bf16[768,3078]{1,0:T(8,128)(2,1)} concatenate(bf16[768,2304]{1,0:T(8,128)(2,1)} %convolution_convert_fusion, bf16[768,768]{1,0:T(8,128)(2,1)} %convolution_convert_fusion.5, bf16[768,4]{1,0:T(8,128)(2,1)S(1)} %copy.134, bf16[768,1]{1,0:T(8,128)(2,1)S(1)} %broadcast_in_dim.40, bf16[768,1]{1,0:T(8,128)(2,1)S(1)} %broadcast_in_dim.41), dimensions={1} | concatenate | bytes 9455616 | tf_op jit(solution)/shard_map/concatenate | solution.py:274
  454.8 4.6 fusion.86
  459.4 5.9 fusion.104
  465.3 5.1 fusion.95
  470.5 5.1 fusion.92
  475.6 5.1 fusion.110
  480.7 5.0 fusion.101
  485.7 13.2 %add_convert_fusion = bf16[3072,768]{1,0:T(8,128)(2,1)} fusion(f32[3072,768]{1,0:T(8,128)S(1)} %fusion.86, f32[3072,768]{1,0:T(8,128)} %fusion.104, f32[3072,768]{1,0:T(8,128)} %fusion.95, bf16[352,3072]{1,0:T(8,128)(2,1)} %get-tuple-element.76, bf16[352,1536]{1,0:T(8,128)(2,1)} %bitcast.155), kind=kOutput, calls=%fused_computation.1 | convolution fusion | flops 1670381568 | bytes 35733504 | tf_op jit(solution)/shard_map/dot_general | solution.py:174
  498.9 9.1 %reduce-scatter.3.cloned.1.call-done = bf16[96,3078]{1,0:T(8,128)(2,1)} async-done(((bf16[768,3078]{1,0:T(8,128)(2,1)}), bf16[96,3078]{1,0:T(8,128)(2,1)}) %reduce-scatter.3.cloned.1.call-update) | async-done | bytes 590992 | tf_op jit(solution)/shard_map/reduce_scatter | solution.py:278
  508.4 15.7 %fusion.27 = bf16[1,768,3072]{2,1,0:T(8,128)(2,1)} fusion(bf16[352,3072]{1,0:T(8,128)(2,1)} %copy-done.39, f32[768,3072]{1,0:T(8,128)} %fusion.92, f32[768,3072]{1,0:T(8,128)} %fusion.110, f32[768,3072]{1,0:T(8,128)} %fusion.101, bf16[352,1536]{1,0:T(8,128)(2,1)} %bitcast.156), kind=kOutput, calls=%fused_computation.82 | convolution fusion | flops 1670381568 | bytes 35733504 | tf_op jit(solution)/shard_map/dot_general | solution.py:177
  524.1 8.5 %stack_reshape.4 = bf16[1,768,3072]{2,1,0:T(8,128)(2,1)} reshape(bf16[3072,768]{1,0:T(8,128)(2,1)} %add_convert_fusion) | data formatting | bytes 9437184 | tf_op jit(solution)/shard_map/stack;reshape | solution.py:189
  532.6 8.3 %pad_maximum_fusion = bf16[2,768,3072]{2,1,0:T(8,128)(2,1)} fusion(bf16[1,768,3072]{2,1,0:T(8,128)(2,1)} %stack_reshape.4, bf16[1,768,3072]{2,1,0:T(8,128)(2,1)} %fusion.27), kind=kLoop, calls=%fused_computation | loop fusion | flops 4718592 | bytes 18874368 | tf_op jit(solution)/shard_map/stack | solution.py:189
  542.6 3.1 add_convert_fusion.7
  545.7 4.3 all-reduce.3.cloned.1.call-done
  556.9 72.8 %reduce-scatter.5.cloned.1.call-done = bf16[2,96,3072]{2,1,0:T(8,128)(2,1)} async-done(((bf16[2,768,3072]{2,1,0:T(8,128)(2,1)}), bf16[2,96,3072]{2,1,0:T(8,128)(2,1)}) %reduce-scatter.5.cloned.1.call-update) | async-done | bytes 1179664 | tf_op jit(solution)/shard_map/reduce_scatter | solution.py:192
  (312 shorter events, 78.5 us)
Async XLA Ops:
  7.2 9.3 %copy-start.57 = (s32[591,2]{0,1:T(2,128)S(1)}, s32[591,2]{0,1:T(2,128)}, u32[]{:S(2)}) copy-start(s32[591,2]{0,1:T(2,128)} %param.13) | copy-start | bytes 14188
  7.2 46.9 %all-gather.3.cloned.1.call-start = ((), (), s32[]{:S(2)}) async-start(), calls=%async_computation.10 | async-start | bytes 5529600 | tf_op jit(solution)/shard_map/all_gather | solution.py:62
  9.6 10.2 %copy-start.8 = (bf16[591,768]{1,0:T(8,128)(2,1)S(1)}, bf16[591,768]{1,0:T(8,128)(2,1)}, u32[]{:S(2)}) copy-start(bf16[591,768]{1,0:T(8,128)(2,1)} %param.11) | copy-start | bytes 2723332
  11.6 8.8 %copy-start.5 = (bf16[591,768]{1,0:T(8,128)(2,1)S(1)}, bf16[591,768]{1,0:T(8,128)(2,1)}, u32[]{:S(2)}) copy-start(bf16[591,768]{1,0:T(8,128)(2,1)} %param.21) | copy-start | bytes 2723332
  11.6 111.4 %all-gather.5.cloned.1.call-start = ((), (), s32[]{:S(2)}) async-start(), calls=%async_computation.11 | async-start | bytes 10616832 | tf_op jit(solution)/shard_map/all_gather | solution.py:73
  19.7 85.3 %copy-start.49 = (f32[591]{0:T(1024)}, f32[591]{0:T(1024)S(1)}, u32[]{:S(2)}) copy-start(f32[591]{0:T(1024)S(1)} %fusion.136) | copy-start | bytes 7096
  19.7 90.4 %copy-start.77 = (s32[1504]{0:T(1024)}, s32[1504]{0:T(1024)S(1)}, u32[]{:S(2)}) copy-start(s32[1504]{0:T(1024)S(1)} %pad_add_fusion) | copy-start | bytes 18052
  19.8 88.2 %copy-start.79 = (s32[591]{0:T(1024)}, s32[591]{0:T(1024)S(1)}, u32[]{:S(2)}) copy-start(s32[591]{0:T(1024)S(1)} %get-tuple-element.67) | copy-start | bytes 7096
  19.8 90.4 %copy-start.81 = (s32[591]{0:T(1024)}, s32[591]{0:T(1024)S(1)}, u32[]{:S(2)}) copy-start(s32[591]{0:T(1024)S(1)} %get-tuple-element.66) | copy-start | bytes 7096
  20.0 41.4 %copy-start.65 = (f32[591]{0:T(1024)}, f32[591]{0:T(1024)S(1)}, u32[]{:S(2)}) copy-start(f32[591]{0:T(1024)S(1)} %broadcast_multiply_fusion.2) | copy-start | bytes 7096
  20.4 41.0 %copy-start.69 = (f32[591]{0:T(1024)}, f32[591]{0:T(1024)S(1)}, u32[]{:S(2)}) copy-start(f32[591]{0:T(1024)S(1)} %fusion.60) | copy-start | bytes 7096
  20.5 41.0 %copy-start.75 = (f32[591]{0:T(1024)}, f32[591]{0:T(1024)S(1)}, u32[]{:S(2)}) copy-start(f32[591]{0:T(1024)S(1)} %fusion.134) | copy-start | bytes 7096
  55.5 6.0 copy-start.73
  55.5 47.5 %copy-start.59 = (f32[768]{0:T(1024)}, f32[768]{0:T(1024)S(1)}, u32[]{:S(2)}) copy-start(f32[768]{0:T(1024)S(1)} %get-tuple-element.54) | copy-start | bytes 9220
  80.8 13.7 %copy-start.10 = (bf16[3,197,1,12,64]{1,4,3,0,2:T(8,128)(2,1)}, bf16[3,197,1,12,64]{1,4,3,0,2:T(8,128)(2,1)S(1)}, u32[]{:S(2)}) copy-start(bf16[3,197,1,12,64]{1,4,3,0,2:T(8,128)(2,1)S(1)} %copy.147) | copy-start | bytes 2723332
  115.4 31.5 %all-to-all-start.6 = ((bf16[4,88,1536]{2,1,0:T(8,128)(2,1)}), bf16[4,88,1536]{2,1,0:T(8,128)(2,1)S(1)}, u32[]{:S(2)}, u32[]{:S(2)}) async-start(bf16[4,88,1536]{2,1,0:T(8,128)(2,1)} %bitcast.23), calls=%async_computation.6 | async-start | bytes 2162688 | tf_op jit(solution)/shard_map/all_to_all | solution.py:150
  146.9 53.3 %copy-start.27 = (bf16[4,88,1536]{2,1,0:T(8,128)(2,1)}, bf16[4,88,1536]{2,1,0:T(8,128)(2,1)S(1)}, u32[]{:S(2)}) copy-start(bf16[4,88,1536]{2,1,0:T(8,128)(2,1)S(1)} %all-to-all-done.6) | copy-start | bytes 3244036
  146.9 31.6 %all-to-all-start.4 = ((bf16[4,96,1536]{2,1,0:T(8,128)(2,1)}), bf16[4,96,1536]{2,1,0:T(8,128)(2,1)S(1)}, u32[]{:S(2)}, u32[]{:S(2)}) async-start(bf16[4,96,1536]{2,1,0:T(8,128)(2,1)} %bitcast.19), calls=%async_computation.4 | async-start | bytes 2359296 | tf_op jit(solution)/shard_map/all_to_all | solution.py:150
  178.5 58.5 %copy-start.20 = (bf16[4,96,1536]{2,1,0:T(8,128)(2,1)}, bf16[4,96,1536]{2,1,0:T(8,128)(2,1)S(1)}, u32[]{:S(2)}) copy-start(bf16[4,96,1536]{2,1,0:T(8,128)(2,1)S(1)} %all-to-all-done.4) | copy-start | bytes 3538948
  178.5 32.0 %all-to-all-start.2 = ((bf16[4,96,1536]{2,1,0:T(8,128)(2,1)}), bf16[4,96,1536]{2,1,0:T(8,128)(2,1)S(1)}, u32[]{:S(2)}, u32[]{:S(2)}) async-start(bf16[4,96,1536]{2,1,0:T(8,128)(2,1)} %bitcast.15), calls=%async_computation.2 | async-start | bytes 2359296 | tf_op jit(solution)/shard_map/all_to_all | solution.py:150
  182.5 15.0 %copy-start.26 = (bf16[3072,768]{1,0:T(8,128)(2,1)S(1)}, bf16[3072,768]{1,0:T(8,128)(2,1)}, u32[]{:S(2)}) copy-start(bf16[3072,768]{1,0:T(8,128)(2,1)} %reshape_squeeze.3) | copy-start | bytes 14155780
  182.5 15.0 %copy-start.40 = (bf16[352,3072]{1,0:T(8,128)(2,1)S(1)}, bf16[352,3072]{1,0:T(8,128)(2,1)}, u32[]{:S(2)}) copy-start(bf16[352,3072]{1,0:T(8,128)(2,1)} %get-tuple-element.76) | copy-start | bytes 6488068
  197.5 9.4 %slice-start.4 = ((s8[9437184]{0:T(1024)(128)(4,1)}), s8[4194304]{0:T(1024)(128)(4,1)S(1)}, s32[]{:S(2)}) async-start(s8[9437184]{0:T(1024)(128)(4,1)} %bitcast.157), calls=%async_computation.19 | async-start | bytes 8388608
  197.5 9.4 %slice-start.5 = ((s8[9437184]{0:T(1024)(128)(4,1)}), s8[4194304]{0:T(1024)(128)(4,1)S(1)}, s32[]{:S(2)}) async-start(s8[9437184]{0:T(1024)(128)(4,1)} %bitcast.157), calls=%async_computation.20 | async-start | bytes 8388608
  200.1 6.8 %slice-start.6 = ((s8[9437184]{0:T(1024)(128)(4,1)}), s8[1048576]{0:T(1024)(128)(4,1)S(1)}, s32[]{:S(2)}) async-start(s8[9437184]{0:T(1024)(128)(4,1)} %bitcast.157), calls=%async_computation.21 | async-start | bytes 2097152
  210.5 59.7 %copy-start.22 = (bf16[4,96,1536]{2,1,0:T(8,128)(2,1)}, bf16[4,96,1536]{2,1,0:T(8,128)(2,1)S(1)}, u32[]{:S(2)}) copy-start(bf16[4,96,1536]{2,1,0:T(8,128)(2,1)S(1)} %all-to-all-done.2) | copy-start | bytes 3538948
  210.5 33.8 %all-to-all-start = ((bf16[4,96,1536]{2,1,0:T(8,128)(2,1)}), bf16[4,96,1536]{2,1,0:T(8,128)(2,1)S(1)}, u32[]{:S(2)}, u32[]{:S(2)}) async-start(bf16[4,96,1536]{2,1,0:T(8,128)(2,1)} %bitcast.151), calls=%async_computation | async-start | bytes 2359296 | tf_op jit(solution)/shard_map/all_to_all | solution.py:150
  214.8 15.0 %copy-start.47 = (bf16[352,768]{1,0:T(8,128)(2,1)S(1)}, bf16[352,768]{1,0:T(8,128)(2,1)}, u32[]{:S(2)}) copy-start(bf16[352,768]{1,0:T(8,128)(2,1)} %convolution_convert_fusion.14) | copy-start | bytes 1622020
  214.9 15.0 %copy-start.48 = (bf16[352,768]{1,0:T(8,128)(2,1)S(1)}, bf16[352,768]{1,0:T(8,128)(2,1)}, u32[]{:S(2)}) copy-start(bf16[352,768]{1,0:T(8,128)(2,1)} %convolution_convert_fusion.13) | copy-start | bytes 1622020
  214.9 16.1 %copy-start.29 = (bf16[384,3072]{1,0:T(8,128)(2,1)S(1)}, bf16[384,3072]{1,0:T(8,128)(2,1)}, u32[]{:S(2)}) copy-start(bf16[384,3072]{1,0:T(8,128)(2,1)} %get-tuple-element.74) | copy-start | bytes 7077892
  229.8 7.1 %slice-start.7 = ((s8[4718592]{0:T(1024)(128)(4,1)}), s8[4194304]{0:T(1024)(128)(4,1)S(1)}, s32[]{:S(2)}) async-start(s8[4718592]{0:T(1024)(128)(4,1)} %bitcast.167), calls=%async_computation.22 | async-start | bytes 8388608
  229.9 7.1 %slice-start.9 = ((s8[4718592]{0:T(1024)(128)(4,1)}), s8[4194304]{0:T(1024)(128)(4,1)S(1)}, s32[]{:S(2)}) async-start(s8[4718592]{0:T(1024)(128)(4,1)} %bitcast.169), calls=%async_computation.24 | async-start | bytes 8388608
  231.0 6.0 slice-start.8
  231.0 6.0 slice-start.10
  244.3 70.6 %copy-start.24 = (bf16[4,96,1536]{2,1,0:T(8,128)(2,1)}, bf16[4,96,1536]{2,1,0:T(8,128)(2,1)S(1)}, u32[]{:S(2)}) copy-start(bf16[4,96,1536]{2,1,0:T(8,128)(2,1)S(1)} %all-to-all-done) | copy-start | bytes 3538948
  244.3 34.5 %all-to-all-start.7 = ((bf16[4,88,1536]{2,1,0:T(8,128)(2,1)}), bf16[4,88,1536]{2,1,0:T(8,128)(2,1)}, u32[]{:S(2)}, u32[]{:S(2)}) async-start(bf16[4,88,1536]{2,1,0:T(8,128)(2,1)} %bitcast.152), calls=%async_computation.7 | async-start | bytes 2162688 | tf_op jit(solution)/shard_map/all_to_all | solution.py:186
  249.6 15.0 %copy-start.33 = (bf16[384,3072]{1,0:T(8,128)(2,1)S(1)}, bf16[384,3072]{1,0:T(8,128)(2,1)}, u32[]{:S(2)}) copy-start(bf16[384,3072]{1,0:T(8,128)(2,1)} %add_convert_fusion.2) | copy-start | bytes 7077892
  270.2 24.9 %slice-start.2 = ((s8[4718592]{0:T(1024)(128)(4,1)}), s8[524288]{0:T(1024)(128)(4,1)S(1)}, s32[]{:S(2)}) async-start(s8[4718592]{0:T(1024)(128)(4,1)} %bitcast.148), calls=%async_computation.17 | async-start | bytes 1048576
  278.8 31.8 %all-to-all-start.5 = ((bf16[4,96,1536]{2,1,0:T(8,128)(2,1)}), bf16[4,96,1536]{2,1,0:T(8,128)(2,1)S(1)}, u32[]{:S(2)}, u32[]{:S(2)}) async-start(bf16[4,96,1536]{2,1,0:T(8,128)(2,1)} %bitcast.150), calls=%async_computation.5 | async-start | bytes 2359296 | tf_op jit(solution)/shard_map/all_to_all | solution.py:186
  284.2 5.2 copy-start.35
  284.2 10.9 %slice-start.3 = ((s8[4718592]{0:T(1024)(128)(4,1)}), s8[4194304]{0:T(1024)(128)(4,1)S(1)}, s32[]{:S(2)}) async-start(s8[4718592]{0:T(1024)(128)(4,1)} %bitcast.148), calls=%async_computation.18 | async-start | bytes 8388608
  289.4 5.6 copy-start.31
  310.6 32.4 %all-to-all-start.3 = ((bf16[4,96,1536]{2,1,0:T(8,128)(2,1)}), bf16[4,96,1536]{2,1,0:T(8,128)(2,1)}, u32[]{:S(2)}, u32[]{:S(2)}) async-start(bf16[4,96,1536]{2,1,0:T(8,128)(2,1)} %bitcast.17), calls=%async_computation.3 | async-start | bytes 2359296 | tf_op jit(solution)/shard_map/all_to_all | solution.py:186
  322.5 5.3 copy-start.37
  327.8 19.3 %copy-start.68 = (f32[591,2]{0,1:T(2,128)S(1)}, f32[591,2]{0,1:T(2,128)}, u32[]{:S(2)}) copy-start(f32[591,2]{0,1:T(2,128)} %copy-done.67) | copy-start | bytes 14188
  327.8 46.8 %copy-start.78 = (s32[1504]{0:T(1024)S(1)}, s32[1504]{0:T(1024)}, u32[]{:S(2)}) copy-start(s32[1504]{0:T(1024)} %copy-done.77) | copy-start | bytes 18052
  327.8 46.8 %copy-start.82 = (s32[591]{0:T(1024)S(1)}, s32[591]{0:T(1024)}, u32[]{:S(2)}) copy-start(s32[591]{0:T(1024)} %copy-done.81) | copy-start | bytes 7096
  343.0 31.6 %all-to-all-start.1 = ((bf16[4,96,1536]{2,1,0:T(8,128)(2,1)}), bf16[4,96,1536]{2,1,0:T(8,128)(2,1)S(1)}, u32[]{:S(2)}, u32[]{:S(2)}) async-start(bf16[4,96,1536]{2,1,0:T(8,128)(2,1)} %bitcast.13), calls=%async_computation.1 | async-start | bytes 2359296 | tf_op jit(solution)/shard_map/all_to_all | solution.py:186
  346.6 161.4 %reduce-scatter.3.cloned.1.call-start = ((), (), s32[]{:S(2)}) async-start(), calls=%async_computation.12 | async-start | bytes 5529600 | tf_op jit(solution)/shard_map/reduce_scatter | solution.py:278
  393.8 7.4 %copy-start.42 = (f32[3,12,197]{2,1,0:T(8,128)S(1)}, f32[3,12,197]{2,1,0:T(8,128)}, u32[]{:S(2)}) copy-start(f32[3,12,197]{2,1,0:T(8,128)} %copy-done.41) | copy-start | bytes 85108
  396.7 9.6 %slice-start = ((s8[7372800]{0:T(1024)(128)(4,1)}), s8[3178496]{0:T(1024)(128)(4,1)S(1)}, s32[]{:S(2)}) async-start(s8[7372800]{0:T(1024)(128)(4,1)} %bitcast.134), calls=%async_computation.15 | async-start | bytes 6356992
  401.2 5.3 copy-start.12
  422.8 9.9 %copy-start.9 = (bf16[591,768]{1,0:T(8,128)(2,1)S(1)}, bf16[591,768]{1,0:T(8,128)(2,1)}, u32[]{:S(2)}) copy-start(bf16[591,768]{1,0:T(8,128)(2,1)} %param.11) | copy-start | bytes 2723332
  422.8 9.9 %copy-start.66 = (f32[591]{0:T(1024)S(1)}, f32[591]{0:T(1024)}, u32[]{:S(2)}) copy-start(f32[591]{0:T(1024)} %copy-done.65) | copy-start | bytes 7096
  422.8 9.9 %copy-start.74 = (f32[768]{0:T(1024)S(1)}, f32[768]{0:T(1024)}, u32[]{:S(2)}) copy-start(f32[768]{0:T(1024)} %copy-done.73) | copy-start | bytes 9220
  422.8 9.9 %copy-start.76 = (f32[591]{0:T(1024)S(1)}, f32[591]{0:T(1024)}, u32[]{:S(2)}) copy-start(f32[591]{0:T(1024)} %copy-done.75) | copy-start | bytes 7096
  432.7 7.2 %copy-start.28 = (bf16[591,2304]{0,1:T(8,128)(2,1)S(1)}, bf16[591,2304]{0,1:T(8,128)(2,1)}, u32[]{:S(2)}) copy-start(bf16[591,2304]{0,1:T(8,128)(2,1)} %convert_element_type.204) | copy-start | bytes 8169988
  444.7 10.0 %copy-start.18 = (f32[591,768]{1,0:T(8,128)}, f32[591,768]{1,0:T(8,128)S(1)}, u32[]{:S(2)}) copy-start(f32[591,768]{1,0:T(8,128)S(1)} %get-tuple-element.101) | copy-start | bytes 5446660
  454.7 95.4 %all-reduce.3.cloned.1.call-start = ((), (), s32[]{:S(2)}) async-start(), calls=%async_computation.13 | async-start | bytes 1228800 | tf_op jit(solution)/shard_map/psum | solution.py:279
  459.4 5.9 copy-start.23
  459.4 5.9 copy-start.30
  465.3 5.1 copy-start.21
  465.3 5.1 copy-start.34
  508.0 121.7 %reduce-scatter.5.cloned.1.call-start = ((), (), s32[]{:S(2)}) async-start(), calls=%async_computation.14 | async-start | bytes 10616832 | tf_op jit(solution)/shard_map/reduce_scatter | solution.py:192
  (44 other events, 123.1 us)
Sparse Core Ops, SparseCore 0:
  11.8 42.3 all-gather.2
  56.6 58.6 all-gather.4
  454.8 53.1 reduce-scatter.2
  510.2 39.7 all-reduce.2
  553.4 76.3 reduce-scatter.4

commit v5 on v4

--- a/solution.py
+++ b/solution.py
@@ -1,4 +1,5 @@
 import jax
+import numpy as np
 import jax.numpy as jnp
 from jax import lax
 from jax.sharding import PartitionSpec as P
@@ -26,8 +27,11 @@
     return exp_scores / jnp.sum(exp_scores, axis=-1, keepdims=True)
 
 
-def gelu_exact(values):
-    return jax.nn.gelu(values, approximate=False)
+def gelu_parts(values):
+    sqrt_half = np.float32(np.sqrt(0.5))
+    tail = lax.erfc(-values * sqrt_half)
+    density = jnp.exp(-0.5 * values * values) * np.float32(1.0 / np.sqrt(2.0 * np.pi))
+    return 0.5 * values * tail, 0.5 * tail + values * density
 
 
 def shards(
@@ -112,7 +116,7 @@
     slot_index = jnp.sum(before * flat_picks, axis=1).reshape(rows, 2)
     position = jnp.where(live_int[:, None] > 0, routes * capacity + slot_index, overflow)
 
-    n_chunks = 4
+    n_chunks = 2
     part_cap = 8 * ((capacity + 8 * n_chunks - 1) // (8 * n_chunks))
     chunk_sizes = [min(part_cap, capacity - k * part_cap) for k in range(n_chunks)]
     chunk_sizes = [size for size in chunk_sizes if size > 0]
@@ -158,16 +162,16 @@
         ).reshape(experts * size, 2 * width)
         flat_arrived = arrived[:, :width]
         flat_grad = arrived[:, width:]
+        hidden_grad = lax.dot_general(
+            flat_grad, expert_second, COL_CONTRACT, preferred_element_type=jnp.float32
+        )
         pre_act = jnp.dot(flat_arrived, expert_first, preferred_element_type=jnp.float32)
-        activated, gelu_back = jax.vjp(gelu_exact, pre_act)
+        activated, slope = gelu_parts(pre_act)
         activated = activated.astype(jnp.bfloat16)
+        pre_grad = (hidden_grad * slope).astype(jnp.bfloat16)
         produced = jnp.dot(
             activated, expert_second, preferred_element_type=jnp.float32
         ).astype(jnp.bfloat16)
-        hidden_grad = lax.dot_general(
-            flat_grad, expert_second, COL_CONTRACT, preferred_element_type=jnp.float32
-        )
-        pre_grad = gelu_back(hidden_grad)[0].astype(jnp.bfloat16)
         row_grad = lax.dot_general(
             pre_grad, expert_first, COL_CONTRACT, preferred_element_type=jnp.float32
         ).astype(jnp.bfloat16)

time: 650 us -> 623 us (0.958)
  matrix products: 239 us -> 193 us
  waiting for transfers between devices: 199 us -> 236 us
  starting transfers between devices: 35.9 us -> 19 us
    reduce_scatter x1, waiting for transfers between devices: 9.14 us -> 27.7 us  [shards(): lax.psum_scatter(dense_grads, 'shard', scatter_dimension=0, tiled=True)]
    all_to_all x4 -> x2, waiting for transfers between devices: 25.6 us -> 41.7 us  [shards(): lax.all_to_all(outgoing[experts * start:experts * (start + size)].reshape...]
    dot_general x4 -> x2, matrix products: 28.8 us -> 14.6 us  [shards(): lax.dot_general(activated, flat_grad, ROW_CONTRACT, preferred_element_typ...]
    dot_general x4 -> x2, matrix products: 31 us -> 20.7 us  [shards(): lax.dot_general(flat_arrived, pre_grad, ROW_CONTRACT, preferred_element_t...]
    all_to_all x4 -> x2, starting transfers between devices: 18.5 us -> 9.73 us  [shards(): lax.all_to_all(returning, 'expert', split_axis=0, concat_axis=0, tiled=True)]
    dot_general x4 -> x2, matrix products: 29 us -> 20.8 us  [shards(): lax.dot_general(flat_grad, expert_second, COL_CONTRACT, preferred_element...]
    all_to_all x4 -> x2, starting transfers between devices: 16.5 us -> 8.72 us  [shards(): lax.all_to_all(outgoing[experts * start:experts * (start + size)].reshape...]
    dot_general x4 -> x2, matrix products: 58.8 us -> 52.1 us  [shards(): jnp.dot(flat_arrived, expert_first, preferred_element_type=jnp.float32)]
  transfers between devices with their start and end apart: 13 -> 9, of which waited for: 10 -> 7; matrix products, arithmetic and copies ran while one was open for 46% -> 41% of each run, Pallas kernels for 0% -> 0%
where the time goes in v5:
time: 623 us; the launch traced here: 614 us
  waiting for transfers between devices  236 us (38%)
  matrix products  193 us (31%)
  local copies, waits for them, and re-layouts  114 us (18%)
  other arithmetic  35.9 us (6%)
  starting transfers between devices  19 us (3%)
  between operations  16.1 us (3%)
    reduce_scatter x1, waiting for transfers between devices, shards(): lax.psum_scatter(expert_grads, 'shard', scatter_dimension=1, tiled=True)  72.8 us
    all_to_all x2, waiting for transfers between devices, shards(): lax.all_to_all(returning, 'expert', split_axis=0, concat_axis=0, tiled=True)  52.4 us
    dot_general x2, matrix products, shards(): jnp.dot(flat_arrived, expert_first, preferred_element_type=jnp.float32)  52.1 us
    all_to_all x2, waiting for transfers between devices, shards(): lax.all_to_all(outgoing[experts * start:experts * (start + size)].reshape...  41.7 us
    all_gather x1, waiting for transfers between devices, shards(): dense_full = lax.all_gather(dense_local, 'shard', axis=0, tiled=True)  32.4 us
    reduce_scatter x1, waiting for transfers between devices, shards(): lax.psum_scatter(dense_grads, 'shard', scatter_dimension=0, tiled=True)  27.7 us
    unnamed x149, local copies, waits for them, and re-layouts  23.7 us
    dot_general x2, matrix products, shards(): lax.dot_general(flat_grad, expert_second, COL_CONTRACT, preferred_element...  20.8 us
  transfers between devices with their start and end apart: 9, of which 7 were waited for; matrix products, arithmetic and copies ran while one was open for 41% of the time, Pallas kernels for 0%

profile of v5, /device:TPU:0, one launch (start us, length us, event | category | flops | bytes accessed | tf_op | source)
XLA Modules:
  0.0 614.3 jit_solution(8315201088563654754)
XLA Ops:
  9.7 1.9 concatenate.26
  13.2 2.2 pad_maximum_fusion.8
  21.7 32.4 %all-gather.3.cloned.1.call-done = bf16[768,3078]{1,0:T(8,128)(2,1)} async-done(((bf16[96,3078]{1,0:T(8,128)(2,1)}), bf16[768,3078]{1,0:T(8,128)(2,1)}) %all-gather.3.cloned.1.call-update) | async-done | bytes 4727824 | tf_op jit(solution)/shard_map/all_gather | solution.py:66
  55.5 6.0 convolution_convert_fusion.1
  61.5 9.3 %reshape.271 = bf16[3,197,3,12,64]{4,3,2,1,0:T(8,128)(2,1)} reshape(bf16[591,2304]{1,0:T(8,128)(2,1)} %convolution_convert_fusion.1) | data formatting | bytes 5446656 | tf_op jit(solution)/shard_map/reshape | solution.py:84
  70.9 6.6 %fusion.125 = (bf16[3,197,1,12,64]{4,3,2,1,0:T(8,128)(2,1)}, bf16[3,197,1,12,64]{4,3,2,1,0:T(8,128)(2,1)}, bf16[3,197,1,12,64]{4,3,2,1,0:T(8,128)(2,1)}) fusion(bf16[3,197,3,12,64]{4,3,2,1,0:T(8,128)(2,1)} %reshape.271), kind=kLoop, calls=%fused_computation.231 | loop fusion | bytes 5446656 | tf_op jit(solution)/shard_map/slice | solution.py:85
  77.5 3.3 copy.152
  80.8 4.6 copy.154
  85.5 4.6 copy.153
  90.1 2.8 multiply_reduce_fusion.1
  97.1 2.1 convert_element_type.149
  99.2 2.7 fusion.127
  106.0 2.1 fusion.28
  108.1 2.2 convolution_convert_fusion.2
  110.3 2.5 add_convert_fusion.2
  115.8 4.6 all-to-all-start.2
  120.4 2.9 fusion.49
  123.3 4.8 slice.165
  128.1 8.5 %reshape_squeeze.3 = bf16[3072,768]{1,0:T(8,128)(2,1)} reshape(bf16[1,768,3072]{2,1,0:T(8,128)(2,1)} %slice.165) | data formatting | bytes 9437184 | tf_op jit(solution)/shard_map/reshape;squeeze | solution.py:79
  136.6 36.2 %all-to-all-done.2 = bf16[4,184,1536]{2,1,0:T(8,128)(2,1)} async-done(((bf16[4,184,1536]{2,1,0:T(8,128)(2,1)}), bf16[4,184,1536]{2,1,0:T(8,128)(2,1)}, u32[]{:S(2)}, u32[]{:S(2)}) %all-to-all-start.2) | async-done | bytes 2261024 | tf_op jit(solution)/shard_map/all_to_all | solution.py:154
  172.8 4.1 all-to-all-start
  176.9 25.8 %multiply_convert_fusion.1 = (bf16[736,3072]{1,0:T(8,128)(2,1)S(1)}, f32[736,3072]{1,0:T(8,128)}, f32[736,3072]{1,0:T(8,128)}) fusion(bf16[2,768,3072]{2,1,0:T(8,128)(2,1)} %all-gather.5.cloned.1.call-done, bf16[736,1536]{1,0:T(8,128)(2,1)} %bitcast.16), kind=kOutput, calls=%fused_computation.36 | convolution fusion | flops 3619848192 | bytes 28459008 | tf_op jit(solution)/shard_map/dot_general | solution.py:168
  202.7 3.7 convolution_convert_fusion.7
  206.4 10.7 %fusion.19 = bf16[736,3072]{1,0:T(8,128)(2,1)} fusion(f32[736,3072]{1,0:T(8,128)} %get-tuple-element.86, f32[736,3072]{1,0:T(8,128)} %get-tuple-element.73, bf16[3072,768]{1,0:T(8,128)(2,1)S(1)} %copy-done.22, bf16[736,1536]{1,0:T(8,128)(2,1)} %bitcast.16), kind=kOutput, calls=%fused_computation.35 | convolution fusion | flops 3490971648 | bytes 28459008 | tf_op jit(solution)/shard_map/dot_general | solution.py:165
  217.2 6.1 fusion.72
  224.8 5.5 all-to-all-done
  230.3 4.7 all-to-all-start.3
  235.0 26.3 %multiply_convert_fusion = (bf16[768,3072]{1,0:T(8,128)(2,1)S(1)}, f32[768,3072]{1,0:T(8,128)}, f32[768,3072]{1,0:T(8,128)}) fusion(bf16[2,768,3072]{2,1,0:T(8,128)(2,1)} %all-gather.5.cloned.1.call-done, bf16[768,1536]{1,0:T(8,128)(2,1)S(1)} %bitcast.113), kind=kOutput, calls=%fused_computation.14 | convolution fusion | flops 3777232896 | bytes 29491200 | tf_op jit(solution)/shard_map/dot_general | solution.py:168
  261.2 8.1 %convolution_convert_fusion.4 = bf16[768,768]{0,1:T(8,128)(2,1)S(1)} fusion(bf16[768,3072]{1,0:T(8,128)(2,1)S(1)} %get-tuple-element.70, bf16[3072,768]{1,0:T(8,128)(2,1)} %reshape_squeeze.3), kind=kOutput, calls=%fused_computation.133 | convolution fusion | flops 3624468480 | bytes 10616832 | tf_op jit(solution)/shard_map/dot_general | solution.py:172
  269.4 10.1 %fusion.6 = bf16[768,3072]{1,0:T(8,128)(2,1)S(1)} fusion(f32[768,3072]{1,0:T(8,128)} %get-tuple-element.87, f32[768,3072]{1,0:T(8,128)} %get-tuple-element.71, bf16[3072,768]{1,0:T(8,128)(2,1)} %reshape_squeeze.3, bf16[768,1536]{1,0:T(8,128)(2,1)S(1)} %bitcast.114), kind=kOutput, calls=%fused_computation.10 | convolution fusion | flops 3642753024 | bytes 29491200 | tf_op jit(solution)/shard_map/dot_general | solution.py:165
  279.5 8.0 %fusion.71 = bf16[768,768]{0,1:T(8,128)(2,1)S(1)} fusion(bf16[768,3072]{1,0:T(8,128)(2,1)S(1)} %fusion.6, bf16[2,768,3072]{2,1,0:T(8,128)(2,1)} %all-gather.5.cloned.1.call-done), kind=kOutput, calls=%fused_computation.131 | convolution fusion | flops 3624468480 | bytes 10616832 | tf_op jit(solution)/shard_map/dot_general | solution.py:175
  287.7 2.5 copy.130
  290.1 5.1 all-to-all-start.1
  295.6 52.4 %all-to-all-done.1 = bf16[4,192,1536]{2,1,0:T(8,128)(2,1)S(1)} async-done(((bf16[4,192,1536]{2,1,0:T(8,128)(2,1)}), bf16[4,192,1536]{2,1,0:T(8,128)(2,1)S(1)}, u32[]{:S(2)}, u32[]{:S(2)}) %all-to-all-start.1) | async-done | bytes 2359328 | tf_op jit(solution)/shard_map/all_to_all | solution.py:190
  348.0 4.9 fusion.30
  353.0 5.1 fusion.26
  358.2 1.9 multiply_reduce_fusion.5
  360.3 2.1 multiply_reduce_fusion.2
  365.8 2.2 convolution_convert_fusion.8
  368.0 2.9 reshape.272
  370.9 4.5 copy.132
  375.4 5.1 fusion.76
  380.8 2.3 multiply_reduce_fusion
  383.1 2.3 multiply_convert_fusion.2
  388.2 2.1 convolution_convert_fusion.6
  391.4 5.6 copy.137
  397.0 9.9 %convert_element_type.172 = bf16[591,2304]{0,1:T(8,128)(2,1)} reshape(bf16[3,197,3,12,64]{1,0,4,3,2:T(4,128)(2,1)} %copy.137) | data formatting | bytes 5446656 | tf_op jit(solution)/shard_map/convert_element_type | solution.py:266
  406.9 7.0 %convolution_convert_fusion = bf16[768,2304]{1,0:T(8,128)(2,1)} fusion(bf16[591,2304]{0,1:T(8,128)(2,1)} %convert_element_type.172, bf16[591,768]{1,0:T(8,128)(2,1)S(1)} %copy-done.9, f32[768]{0:T(1024)S(1)} %copy-done.55, f32[591]{0:T(1024)S(1)} %copy-done.57, f32[591]{0:T(1024)S(1)} %copy-done.47), kind=kOutput, calls=%fused_computation.66 | convolution fusion | flops 2095554816 | bytes 7177848 | tf_op jit(solution)/shard_map/dot_general | solution.py:268
  413.9 4.7 fusion.68
  420.2 8.4 %concatenate.32 = bf16[768,3078]{1,0:T(8,128)(2,1)} concatenate(bf16[768,2304]{1,0:T(8,128)(2,1)} %convolution_convert_fusion, bf16[768,768]{1,0:T(8,128)(2,1)} %convolution_convert_fusion.6, bf16[768,4]{1,0:T(8,128)(2,1)S(1)} %copy.139, bf16[768,1]{1,0:T(8,128)(2,1)S(1)} %broadcast_in_dim.40, bf16[768,1]{1,0:T(8,128)(2,1)S(1)} %broadcast_in_dim.41), dimensions={1} | concatenate | bytes 9455616 | tf_op jit(solution)/shard_map/concatenate | solution.py:278
  428.7 1.6 copy-done.21
  430.3 6.0 fusion.86
  436.2 9.2 %fusion.89 = f32[768,3072]{1,0:T(8,128)} fusion(bf16[768,3072]{1,0:T(8,128)(2,1)} %copy-done.23, bf16[768,1536]{1,0:T(8,128)(2,1)S(1)} %bitcast.116), kind=kOutput, calls=%fused_computation.157 | convolution fusion | flops 3623878656 | bytes 15335424 | tf_op jit(solution)/shard_map/dot_general | solution.py:181
  445.4 8.7 %add_convert_fusion = bf16[3072,768]{1,0:T(8,128)(2,1)} fusion(f32[3072,768]{1,0:T(8,128)S(1)} %fusion.86, bf16[736,3072]{1,0:T(8,128)(2,1)} %copy-done.65, bf16[736,1536]{1,0:T(8,128)(2,1)} %bitcast.16), kind=kOutput, calls=%fused_computation.12 | convolution fusion | flops 3477602304 | bytes 19808256 | tf_op jit(solution)/shard_map/dot_general | solution.py:178
  454.1 27.7 %reduce-scatter.3.cloned.1.call-done = bf16[96,3078]{1,0:T(8,128)(2,1)} async-done(((bf16[768,3078]{1,0:T(8,128)(2,1)}), bf16[96,3078]{1,0:T(8,128)(2,1)}) %reduce-scatter.3.cloned.1.call-update) | async-done | bytes 590992 | tf_op jit(solution)/shard_map/reduce_scatter | solution.py:282
  481.9 11.5 %fusion.35 = bf16[1,768,3072]{2,1,0:T(8,128)(2,1)} fusion(f32[768,3072]{1,0:T(8,128)} %fusion.89, bf16[736,3072]{1,0:T(8,128)(2,1)} %fusion.19, bf16[736,1536]{1,0:T(8,128)(2,1)} %bitcast.16), kind=kOutput, calls=%fused_computation.74 | convolution fusion | flops 3477602304 | bytes 19808256 | tf_op jit(solution)/shard_map/dot_general | solution.py:181
  493.4 8.7 %stack_reshape.4 = bf16[1,768,3072]{2,1,0:T(8,128)(2,1)} reshape(bf16[3072,768]{1,0:T(8,128)(2,1)} %add_convert_fusion) | data formatting | bytes 9437184 | tf_op jit(solution)/shard_map/stack;reshape | solution.py:193
  502.1 8.3 %pad_maximum_fusion = bf16[2,768,3072]{2,1,0:T(8,128)(2,1)} fusion(bf16[1,768,3072]{2,1,0:T(8,128)(2,1)} %stack_reshape.4, bf16[1,768,3072]{2,1,0:T(8,128)(2,1)} %fusion.35), kind=kLoop, calls=%fused_computation.11 | loop fusion | flops 4718592 | bytes 18874368 | tf_op jit(solution)/shard_map/stack | solution.py:193
  512.2 3.1 add_convert_fusion.3
  515.3 8.5 %all-reduce.3.cloned.1.call-done = bf16[96,3078]{1,0:T(8,128)(2,1)} async-done(((bf16[96,3078]{1,0:T(8,128)(2,1)}), bf16[96,3078]{1,0:T(8,128)(2,1)}) %all-reduce.3.cloned.1.call-update) | async-done | bytes 590992 | tf_op jit(solution)/shard_map/psum | solution.py:283
  525.2 2.0 slice.174
  527.2 1.6 slice.175
  530.7 72.8 %reduce-scatter.5.cloned.1.call-done = bf16[2,96,3072]{2,1,0:T(8,128)(2,1)} async-done(((bf16[2,768,3072]{2,1,0:T(8,128)(2,1)}), bf16[2,96,3072]{2,1,0:T(8,128)(2,1)}) %reduce-scatter.5.cloned.1.call-update) | async-done | bytes 1179664 | tf_op jit(solution)/shard_map/reduce_scatter | solution.py:196
  603.5 2.5 fusion.126
  (234 shorter events, 39.6 us)
Async XLA Ops:
  7.2 9.3 %copy-start.38 = (s32[591,2]{0,1:T(2,128)S(1)}, s32[591,2]{0,1:T(2,128)}, u32[]{:S(2)}) copy-start(s32[591,2]{0,1:T(2,128)} %param.13) | copy-start | bytes 14188
  7.2 46.9 %all-gather.3.cloned.1.call-start = ((), (), s32[]{:S(2)}) async-start(), calls=%async_computation.6 | async-start | bytes 5529600 | tf_op jit(solution)/shard_map/all_gather | solution.py:66
  8.0 11.4 %copy-start.8 = (bf16[591,768]{1,0:T(8,128)(2,1)S(1)}, bf16[591,768]{1,0:T(8,128)(2,1)}, u32[]{:S(2)}) copy-start(bf16[591,768]{1,0:T(8,128)(2,1)} %param.11) | copy-start | bytes 2723332
  11.6 8.5 %copy-start.5 = (bf16[591,768]{1,0:T(8,128)(2,1)S(1)}, bf16[591,768]{1,0:T(8,128)(2,1)}, u32[]{:S(2)}) copy-start(bf16[591,768]{1,0:T(8,128)(2,1)} %param.21) | copy-start | bytes 2723332
  11.6 111.7 %all-gather.5.cloned.1.call-start = ((), (), s32[]{:S(2)}) async-start(), calls=%async_computation.7 | async-start | bytes 10616832 | tf_op jit(solution)/shard_map/all_gather | solution.py:77
  19.3 85.8 %copy-start.30 = (f32[591]{0:T(1024)}, f32[591]{0:T(1024)S(1)}, u32[]{:S(2)}) copy-start(f32[591]{0:T(1024)S(1)} %fusion.114) | copy-start | bytes 7096
  19.4 90.9 %copy-start.58 = (s32[1504]{0:T(1024)}, s32[1504]{0:T(1024)S(1)}, u32[]{:S(2)}) copy-start(s32[1504]{0:T(1024)S(1)} %pad_add_fusion) | copy-start | bytes 18052
  19.4 88.7 %copy-start.60 = (s32[591]{0:T(1024)}, s32[591]{0:T(1024)S(1)}, u32[]{:S(2)}) copy-start(s32[591]{0:T(1024)S(1)} %get-tuple-element.67) | copy-start | bytes 7096
  19.4 90.9 %copy-start.62 = (s32[591]{0:T(1024)}, s32[591]{0:T(1024)S(1)}, u32[]{:S(2)}) copy-start(s32[591]{0:T(1024)S(1)} %get-tuple-element.66) | copy-start | bytes 7096
  19.7 41.8 %copy-start.46 = (f32[591]{0:T(1024)}, f32[591]{0:T(1024)S(1)}, u32[]{:S(2)}) copy-start(f32[591]{0:T(1024)S(1)} %broadcast_multiply_fusion.2) | copy-start | bytes 7096
  20.1 41.4 %copy-start.50 = (f32[591]{0:T(1024)}, f32[591]{0:T(1024)S(1)}, u32[]{:S(2)}) copy-start(f32[591]{0:T(1024)S(1)} %fusion.67) | copy-start | bytes 7096
  20.1 41.4 %copy-start.56 = (f32[591]{0:T(1024)}, f32[591]{0:T(1024)S(1)}, u32[]{:S(2)}) copy-start(f32[591]{0:T(1024)S(1)} %fusion.112) | copy-start | bytes 7096
  55.5 6.0 copy-start.54
  55.5 47.6 %copy-start.40 = (f32[768]{0:T(1024)}, f32[768]{0:T(1024)S(1)}, u32[]{:S(2)}) copy-start(f32[768]{0:T(1024)S(1)} %get-tuple-element.54) | copy-start | bytes 9220
  80.8 13.7 %copy-start.10 = (bf16[3,197,1,12,64]{1,4,3,0,2:T(8,128)(2,1)}, bf16[3,197,1,12,64]{1,4,3,0,2:T(8,128)(2,1)S(1)}, u32[]{:S(2)}) copy-start(bf16[3,197,1,12,64]{1,4,3,0,2:T(8,128)(2,1)S(1)} %copy.152) | copy-start | bytes 2723332
  92.9 3.1 copy-start
  99.2 6.5 %copy-start.19 = (f32[591,768]{1,0:T(8,128)S(1)}, f32[591,768]{1,0:T(8,128)}, u32[]{:S(2)}) copy-start(f32[591,768]{1,0:T(8,128)} %convert_multiply_fusion) | copy-start | bytes 5446660
  102.0 3.2 copy-start.34
  103.1 5.0 copy-start.42
  103.5 4.6 copy-start.16
  105.7 2.4 copy-start.48
  115.8 56.9 %all-to-all-start.2 = ((bf16[4,184,1536]{2,1,0:T(8,128)(2,1)}), bf16[4,184,1536]{2,1,0:T(8,128)(2,1)}, u32[]{:S(2)}, u32[]{:S(2)}) async-start(bf16[4,184,1536]{2,1,0:T(8,128)(2,1)} %bitcast.112), calls=%async_computation.2 | async-start | bytes 4521984 | tf_op jit(solution)/shard_map/all_to_all | solution.py:154
  172.8 57.5 %all-to-all-start = ((bf16[4,192,1536]{2,1,0:T(8,128)(2,1)}), bf16[4,192,1536]{2,1,0:T(8,128)(2,1)S(1)}, u32[]{:S(2)}, u32[]{:S(2)}) async-start(bf16[4,192,1536]{2,1,0:T(8,128)(2,1)} %bitcast.10), calls=%async_computation | async-start | bytes 4718592 | tf_op jit(solution)/shard_map/all_to_all | solution.py:154
  176.9 25.8 %copy-start.22 = (bf16[3072,768]{1,0:T(8,128)(2,1)S(1)}, bf16[3072,768]{1,0:T(8,128)(2,1)}, u32[]{:S(2)}) copy-start(bf16[3072,768]{1,0:T(8,128)(2,1)} %reshape_squeeze.3) | copy-start | bytes 14155780
  202.7 3.7 copy-start.65
  202.7 14.5 %slice-start.2 = ((s8[9437184]{0:T(1024)(128)(4,1)}), s8[4194304]{0:T(1024)(128)(4,1)S(1)}, s32[]{:S(2)}) async-start(s8[9437184]{0:T(1024)(128)(4,1)} %bitcast.117), calls=%async_computation.13 | async-start | bytes 8388608
  202.7 14.5 %slice-start.3 = ((s8[9437184]{0:T(1024)(128)(4,1)}), s8[4194304]{0:T(1024)(128)(4,1)S(1)}, s32[]{:S(2)}) async-start(s8[9437184]{0:T(1024)(128)(4,1)} %bitcast.117), calls=%async_computation.14 | async-start | bytes 8388608
  206.4 10.8 %slice-start.4 = ((s8[9437184]{0:T(1024)(128)(4,1)}), s8[1048576]{0:T(1024)(128)(4,1)S(1)}, s32[]{:S(2)}) async-start(s8[9437184]{0:T(1024)(128)(4,1)} %bitcast.117), calls=%async_computation.15 | async-start | bytes 2097152
  230.3 39.1 %copy-start.20 = (bf16[4,192,1536]{2,1,0:T(8,128)(2,1)}, bf16[4,192,1536]{2,1,0:T(8,128)(2,1)S(1)}, u32[]{:S(2)}) copy-start(bf16[4,192,1536]{2,1,0:T(8,128)(2,1)S(1)} %all-to-all-done) | copy-start | bytes 7077892
  230.3 59.9 %all-to-all-start.3 = ((bf16[4,184,1536]{2,1,0:T(8,128)(2,1)}), bf16[4,184,1536]{2,1,0:T(8,128)(2,1)}, u32[]{:S(2)}, u32[]{:S(2)}) async-start(bf16[4,184,1536]{2,1,0:T(8,128)(2,1)} %bitcast.17), calls=%async_computation.3 | async-start | bytes 4521984 | tf_op jit(solution)/shard_map/all_to_all | solution.py:190
  261.2 8.1 %copy-start.64 = (bf16[768,3072]{1,0:T(8,128)(2,1)}, bf16[768,3072]{1,0:T(8,128)(2,1)S(1)}, u32[]{:S(2)}) copy-start(bf16[768,3072]{1,0:T(8,128)(2,1)S(1)} %get-tuple-element.70) | copy-start | bytes 14155780
  279.5 8.0 %copy-start.23 = (bf16[768,3072]{1,0:T(8,128)(2,1)}, bf16[768,3072]{1,0:T(8,128)(2,1)S(1)}, u32[]{:S(2)}) copy-start(bf16[768,3072]{1,0:T(8,128)(2,1)S(1)} %fusion.6) | copy-start | bytes 14155780
  287.6 8.0 %copy-start.49 = (f32[591,2]{0,1:T(2,128)S(1)}, f32[591,2]{0,1:T(2,128)}, u32[]{:S(2)}) copy-start(f32[591,2]{0,1:T(2,128)} %copy-done.48) | copy-start | bytes 14188
  287.6 60.4 %copy-start.59 = (s32[1504]{0:T(1024)S(1)}, s32[1504]{0:T(1024)}, u32[]{:S(2)}) copy-start(s32[1504]{0:T(1024)} %copy-done.58) | copy-start | bytes 18052
  287.6 60.4 %copy-start.63 = (s32[591]{0:T(1024)S(1)}, s32[591]{0:T(1024)}, u32[]{:S(2)}) copy-start(s32[591]{0:T(1024)} %copy-done.62) | copy-start | bytes 7096
  290.1 57.9 %all-to-all-start.1 = ((bf16[4,192,1536]{2,1,0:T(8,128)(2,1)}), bf16[4,192,1536]{2,1,0:T(8,128)(2,1)S(1)}, u32[]{:S(2)}, u32[]{:S(2)}) async-start(bf16[4,192,1536]{2,1,0:T(8,128)(2,1)} %bitcast.13), calls=%async_computation.1 | async-start | bytes 4718592 | tf_op jit(solution)/shard_map/all_to_all | solution.py:190
  295.2 186.6 %reduce-scatter.3.cloned.1.call-start = ((), (), s32[]{:S(2)}) async-start(), calls=%async_computation.8 | async-start | bytes 5529600 | tf_op jit(solution)/shard_map/reduce_scatter | solution.py:282
  348.0 4.9 copy-start.61
  353.0 5.2 copy-start.2
  353.0 5.2 copy-start.6
  353.0 5.2 copy-start.31
  358.1 2.1 copy-start.33
  358.1 2.1 copy-start.37
  358.1 2.1 copy-start.45
  358.1 2.1 copy-start.35
  358.1 2.1 copy-start.41
  358.2 2.1 copy-start.43
  360.1 2.3 copy-start.53
  368.0 7.4 %copy-start.26 = (f32[3,12,197]{2,1,0:T(8,128)S(1)}, f32[3,12,197]{2,1,0:T(8,128)}, u32[]{:S(2)}) copy-start(f32[3,12,197]{2,1,0:T(8,128)} %copy-done.25) | copy-start | bytes 85108
  370.9 9.6 %slice-start = ((s8[7372800]{0:T(1024)(128)(4,1)}), s8[3178496]{0:T(1024)(128)(4,1)S(1)}, s32[]{:S(2)}) async-start(s8[7372800]{0:T(1024)(128)(4,1)} %bitcast.110), calls=%async_computation.11 | async-start | bytes 6356992
  375.4 5.1 slice-start.1
  375.4 5.1 copy-start.11
  375.4 5.3 copy-start.12
  383.1 2.4 copy-start.14
  386.7 3.6 copy-start.17
  396.9 9.9 %copy-start.9 = (bf16[591,768]{1,0:T(8,128)(2,1)S(1)}, bf16[591,768]{1,0:T(8,128)(2,1)}, u32[]{:S(2)}) copy-start(bf16[591,768]{1,0:T(8,128)(2,1)} %param.11) | copy-start | bytes 2723332
  397.0 10.0 %copy-start.47 = (f32[591]{0:T(1024)S(1)}, f32[591]{0:T(1024)}, u32[]{:S(2)}) copy-start(f32[591]{0:T(1024)} %copy-done.46) | copy-start | bytes 7096
  397.0 10.0 %copy-start.55 = (f32[768]{0:T(1024)S(1)}, f32[768]{0:T(1024)}, u32[]{:S(2)}) copy-start(f32[768]{0:T(1024)} %copy-done.54) | copy-start | bytes 9220
  397.0 10.0 %copy-start.57 = (f32[591]{0:T(1024)S(1)}, f32[591]{0:T(1024)}, u32[]{:S(2)}) copy-start(f32[591]{0:T(1024)} %copy-done.56) | copy-start | bytes 7096
  406.9 7.0 %copy-start.24 = (bf16[591,2304]{0,1:T(8,128)(2,1)S(1)}, bf16[591,2304]{0,1:T(8,128)(2,1)}, u32[]{:S(2)}) copy-start(bf16[591,2304]{0,1:T(8,128)(2,1)} %convert_element_type.172) | copy-start | bytes 8169988
  413.9 4.7 copy-start.51
  418.6 10.0 %copy-start.18 = (f32[591,768]{1,0:T(8,128)}, f32[591,768]{1,0:T(8,128)S(1)}, u32[]{:S(2)}) copy-start(f32[591,768]{1,0:T(8,128)S(1)} %get-tuple-element.92) | copy-start | bytes 5446660
  428.6 95.2 %all-reduce.3.cloned.1.call-start = ((), (), s32[]{:S(2)}) async-start(), calls=%async_computation.9 | async-start | bytes 1228800 | tf_op jit(solution)/shard_map/psum | solution.py:283
  481.8 121.7 %reduce-scatter.5.cloned.1.call-start = ((), (), s32[]{:S(2)}) async-start(), calls=%async_computation.10 | async-start | bytes 10616832 | tf_op jit(solution)/shard_map/reduce_scatter | solution.py:196
  (16 other events, 20.1 us)
Sparse Core Ops, SparseCore 0:
  11.8 42.3 all-gather.2
  56.6 58.6 all-gather.4
  428.7 52.9 reduce-scatter.2
  484.0 39.7 all-reduce.2
  527.1 76.3 reduce-scatter.4

commit v6 on v5

--- a/solution.py
+++ b/solution.py
@@ -1,10 +1,13 @@
+import functools
+
 import jax
 import numpy as np
 import jax.numpy as jnp
 from jax import lax
+from jax.experimental import pallas as pl
+from jax.experimental.pallas import tpu as pltpu
 from jax.sharding import PartitionSpec as P
 
-H = 12
 HD = 64
 SEQ = 197
 
@@ -12,6 +15,102 @@
 EPSILON = 1e-06
 ROW_CONTRACT = (((0,), (0,)), ((), ()))
 COL_CONTRACT = (((1,), (1,)), ((), ()))
+
+
+def _image_of(idx, images):
+    count = jnp.zeros(idx.shape, jnp.int32)
+    for i in range(1, images + 1):
+        count = count + (idx >= i * SEQ).astype(jnp.int32)
+    return count
+
+
+def _same_image(size, images):
+    rows = lax.broadcasted_iota(jnp.int32, (size, size), 0)
+    cols = lax.broadcasted_iota(jnp.int32, (size, size), 1)
+    return _image_of(rows, images) == _image_of(cols, images)
+
+
+def _softmax_masked(qj, k, same):
+    s = lax.dot_general(qj, k, COL_CONTRACT, preferred_element_type=jnp.float32) * (HD ** -0.5)
+    s = jnp.where(same, s, -jnp.inf)
+    top = jnp.max(s, axis=1, keepdims=True)
+    e = jnp.exp(s - top)
+    return e / jnp.sum(e, axis=1, keepdims=True)
+
+
+def attn_fwd_kernel(q_ref, k_ref, v_ref, o_ref, *, images):
+    R = q_ref.shape[0]
+    q = q_ref[...]
+    k = k_ref[...]
+    v = v_ref[...]
+    same = _same_image(R, images)
+    lane = lax.broadcasted_iota(jnp.int32, (1, 2 * HD), 1)
+    out = jnp.zeros((R, 2 * HD), jnp.float32)
+    for j in range(2):
+        in_head = (lane >= HD) == (j == 1)
+        p = _softmax_masked(jnp.where(in_head, q, jnp.zeros_like(q)), k, same)
+        o = jnp.dot(p.astype(jnp.bfloat16), v, preferred_element_type=jnp.float32)
+        out = jnp.where(in_head, o, out)
+    o_ref[...] = out.astype(o_ref.dtype)
+
+
+def attn_bwd_kernel(q_ref, k_ref, v_ref, g_ref, dq_ref, dk_ref, dv_ref, *, images):
+    R = q_ref.shape[0]
+    q = q_ref[...]
+    k = k_ref[...]
+    v = v_ref[...]
+    g = g_ref[...]
+    same = _same_image(R, images)
+    lane = lax.broadcasted_iota(jnp.int32, (1, 2 * HD), 1)
+    dq = jnp.zeros((R, 2 * HD), jnp.float32)
+    dk = jnp.zeros((R, 2 * HD), jnp.float32)
+    dv = jnp.zeros((R, 2 * HD), jnp.float32)
+    for j in range(2):
+        in_head = (lane >= HD) == (j == 1)
+        p = _softmax_masked(jnp.where(in_head, q, jnp.zeros_like(q)), k, same)
+        gj = jnp.where(in_head, g, jnp.zeros_like(g))
+        dp = lax.dot_general(gj, v, COL_CONTRACT, preferred_element_type=jnp.float32)
+        ds = (p * (dp - jnp.sum(p * dp, axis=1, keepdims=True))).astype(jnp.bfloat16)
+        dq_j = jnp.dot(ds, k, preferred_element_type=jnp.float32) * (HD ** -0.5)
+        dk_j = lax.dot_general(ds, q, ROW_CONTRACT, preferred_element_type=jnp.float32) * (HD ** -0.5)
+        dv_j = lax.dot_general(p.astype(jnp.bfloat16), g, ROW_CONTRACT, preferred_element_type=jnp.float32)
+        dq = jnp.where(in_head, dq_j, dq)
+        dk = jnp.where(in_head, dk_j, dk)
+        dv = jnp.where(in_head, dv_j, dv)
+    dq_ref[...] = dq.astype(dq_ref.dtype)
+    dk_ref[...] = dk.astype(dk_ref.dtype)
+    dv_ref[...] = dv.astype(dv_ref.dtype)
+
+
+def attention_fwd(projected, images):
+    R = projected.shape[0]
+    W = projected.shape[1] // 3
+    pairs = W // (2 * HD)
+    blk = lambda off: pl.BlockSpec((R, 2 * HD), lambda h: (0, off + h))
+    return pl.pallas_call(
+        functools.partial(attn_fwd_kernel, images=images),
+        grid=(pairs,),
+        in_specs=[blk(0), blk(pairs), blk(2 * pairs)],
+        out_specs=blk(0),
+        out_shape=jax.ShapeDtypeStruct((R, W), jnp.bfloat16),
+        compiler_params=pltpu.CompilerParams(vmem_limit_bytes=48 * 1024 * 1024),
+    )(projected, projected, projected)
+
+
+def attention_bwd(projected, mixed_grad, images):
+    R = projected.shape[0]
+    W = projected.shape[1] // 3
+    pairs = W // (2 * HD)
+    blk = lambda off: pl.BlockSpec((R, 2 * HD), lambda h: (0, off + h))
+    out = jax.ShapeDtypeStruct((R, W), jnp.bfloat16)
+    return pl.pallas_call(
+        functools.partial(attn_bwd_kernel, images=images),
+        grid=(pairs,),
+        in_specs=[blk(0), blk(pairs), blk(2 * pairs), blk(0)],
+        out_specs=[blk(0), blk(0), blk(0)],
+        out_shape=[out, out, out],
+        compiler_params=pltpu.CompilerParams(vmem_limit_bytes=48 * 1024 * 1024),
+    )(projected, projected, projected, mixed_grad)
 
 
 def layer_norm(values, norm_gain):
@@ -55,7 +154,6 @@
     qkv_cols = w_qkv.shape[1]
     n_route = w_router.shape[1]
     ff = w_in.shape[2]
-    score_scale = HD ** (-0.5)
     row_ids = jnp.arange(rows, dtype=jnp.int32)
     live_int = (row_ids // SEQ < image_counts[0, 0]).astype(jnp.int32)
     live_rows = live_int.astype(jnp.float32)
@@ -81,28 +179,9 @@
     token_f = tokens.astype(jnp.float32)
     attn_in = layer_norm(token_f, gain_one).astype(jnp.bfloat16)
     projected = jnp.dot(attn_in, full_qkv, preferred_element_type=jnp.float32).astype(jnp.bfloat16)
-    split_heads = projected.reshape(images, SEQ, 3, H, HD)
-    queries = split_heads[:, :, 0]
-    keys_part = split_heads[:, :, 1]
-    values_part = split_heads[:, :, 2]
-    scores = (
-        jnp.einsum("ishd,ithd->ihst", queries, keys_part, preferred_element_type=jnp.float32)
-        * score_scale
-    )
-    row_top = jnp.max(scores, axis=-1, keepdims=True)
-    log_total = row_top + jnp.log(jnp.sum(jnp.exp(scores - row_top), axis=-1, keepdims=True))
-    attn_probs = jnp.exp(scores - log_total)
-    probs_low = attn_probs.astype(jnp.bfloat16)
-    mixed_rows = (
-        jnp.einsum(
-            "ihst,ithd->ishd",
-            probs_low,
-            values_part,
-            preferred_element_type=jnp.float32,
-        )
-        .reshape(rows, width)
-        .astype(jnp.bfloat16)
-    )
+    pad_rows = -(-rows // 128) * 128
+    projected_pad = jnp.pad(projected, ((0, pad_rows - rows), (0, 0)))
+    mixed_rows = attention_fwd(projected_pad, images)[:rows]
     hidden_state = token_f + jnp.dot(mixed_rows, full_out, preferred_element_type=jnp.float32)
     moe_in = layer_norm(hidden_state, gain_two).astype(jnp.bfloat16)
     logits = jnp.dot(moe_in, full_router, preferred_element_type=jnp.float32)
@@ -239,32 +318,9 @@
     mixed_grad = lax.dot_general(
         branch_grad, full_out, COL_CONTRACT, preferred_element_type=jnp.float32
     )
-    mixed_grad = mixed_grad.astype(jnp.bfloat16).reshape(images, SEQ, H, HD)
-    grad_values = jnp.einsum(
-        "ihst,ishd->ithd",
-        probs_low,
-        mixed_grad,
-        preferred_element_type=jnp.float32,
-    )
-    prob_grad = jnp.einsum(
-        "ishd,ithd->ihst", mixed_grad, values_part, preferred_element_type=jnp.float32
-    )
-    score_grad = (
-        attn_probs * (prob_grad - jnp.sum(attn_probs * prob_grad, axis=-1, keepdims=True))
-    ).astype(jnp.bfloat16)
-    grad_queries = (
-        jnp.einsum("ihst,ithd->ishd", score_grad, keys_part, preferred_element_type=jnp.float32)
-        * score_scale
-    )
-    grad_keys = (
-        jnp.einsum("ihst,ishd->ithd", score_grad, queries, preferred_element_type=jnp.float32)
-        * score_scale
-    )
-    projected_grad = (
-        jnp.stack([grad_queries, grad_keys, grad_values], axis=2)
-        .reshape(rows, 3 * width)
-        .astype(jnp.bfloat16)
-    )
+    mixed_grad = jnp.pad(mixed_grad.astype(jnp.bfloat16), ((0, pad_rows - rows), (0, 0)))
+    grad_q, grad_k, grad_v = attention_bwd(projected_pad, mixed_grad, images)
+    projected_grad = jnp.concatenate([grad_q, grad_k, grad_v], axis=1)[:rows]
     grad_qkv = lax.dot_general(
         attn_in, projected_grad, ROW_CONTRACT, preferred_element_type=jnp.float32
     )

time: 623 us -> 586 us (0.941)
  local copies, waits for them, and re-layouts: 114 us -> 53.6 us
  Pallas kernels: 0 us -> 35.3 us
  matrix products: 193 us -> 184 us
    pallas_call x0 -> x2, Pallas kernels: none -> 35.3 us  [the longest x1 21.8 us: attention_bwd(): pl.pallas_call(functools.partial(attn_bwd_kernel, images=images), grid=(p...]
    unnamed x149 -> x120, local copies, waits for them, and re-layouts: 23.7 us -> 4.69 us
    all_to_all x2, waiting for transfers between devices: 41.7 us -> 23.7 us  [shards(): lax.all_to_all(outgoing[experts * start:experts * (start + size)].reshape...]
    all_gather x1, waiting for transfers between devices: 0.01 us -> 17.9 us  [shards(): expert_full = lax.all_gather(expert_local, 'shard', axis=1, tiled=True)]
    reshape x4 -> x1, local copies, waits for them, and re-layouts: 16.8 us -> 0.02 us  [the longest x1 9.35 us: shards(): split_heads = projected.reshape(images, SEQ, 3, H, HD)]
    dot_general x6 -> x0, matrix products: 13.8 us -> none  [the longest x1 5.05 us: shards(): jnp.einsum('ihst,ishd->ithd', probs_low, mixed_grad, preferred_element_ty...]
    convert_element_type x3 -> x0, local copies, waits for them, and re-layouts: 13 us -> none  [the longest x1 9.94 us: shards(): projected_grad = jnp.stack([grad_queries, grad_keys, grad_values], axis=2...]
    dot_general x1, matrix products: 6.97 us -> 16 us  [shards(): lax.dot_general(attn_in, projected_grad, ROW_CONTRACT, preferred_element_...]
  transfers between devices with their start and end apart: 9 -> 9, of which waited for: 7 -> 8; matrix products, arithmetic and copies ran while one was open for 41% -> 36% of each run, Pallas kernels for 0% -> 2%
where the time goes in v6:
time: 586 us; the launch traced here: 579 us
  waiting for transfers between devices  239 us (41%)
  matrix products  184 us (31%)
  local copies, waits for them, and re-layouts  53.6 us (9%)
  Pallas kernels  35.3 us (6%)
  other arithmetic  32.7 us (6%)
  starting transfers between devices  19 us (3%)
  between operations  15.9 us (3%)
    reduce_scatter x1, waiting for transfers between devices, shards(): lax.psum_scatter(expert_grads, 'shard', scatter_dimension=1, tiled=True)  72.8 us
    all_to_all x2, waiting for transfers between devices, shards(): lax.all_to_all(returning, 'expert', split_axis=0, concat_axis=0, tiled=True)  52.4 us
    dot_general x2, matrix products, shards(): jnp.dot(flat_arrived, expert_first, preferred_element_type=jnp.float32)  52.1 us
    all_gather x1, waiting for transfers between devices, shards(): dense_full = lax.all_gather(dense_local, 'shard', axis=0, tiled=True)  32.5 us
    reduce_scatter x1, waiting for transfers between devices, shards(): lax.psum_scatter(dense_grads, 'shard', scatter_dimension=0, tiled=True)  29 us
    all_to_all x2, waiting for transfers between devices, shards(): lax.all_to_all(outgoing[experts * start:experts * (start + size)].reshape...  23.7 us
    pallas_call x1, Pallas kernels, attention_bwd(): pl.pallas_call(functools.partial(attn_bwd_kernel, images=images), grid=(p...  21.8 us
    dot_general x2, matrix products, shards(): lax.dot_general(flat_grad, expert_second, COL_CONTRACT, preferred_element...  20.8 us
  transfers between devices with their start and end apart: 9, of which 8 were waited for; matrix products, arithmetic and copies ran while one was open for 36% of the time, Pallas kernels for 2%

profile of v6, /device:TPU:0, one launch (start us, length us, event | category | flops | bytes accessed | tf_op | source)
XLA Modules:
  0.0 578.8 jit_solution(9739957591670667853)
XLA Ops:
  7.2 0.9 copy.71
  9.7 1.9 concatenate.29
  11.7 1.5 stack_reshape_squeeze.3
  13.2 2.2 pad_maximum_fusion.9
  16.9 1.2 reduce-window.6
  20.1 1.5 convert_multiply_fusion
  21.6 32.5 %all-gather.3.cloned.1.call-done = bf16[768,3078]{1,0:T(8,128)(2,1)} async-done(((bf16[96,3078]{1,0:T(8,128)(2,1)}), bf16[768,3078]{1,0:T(8,128)(2,1)}) %all-gather.3.cloned.1.call-update) | async-done | bytes 4727824 | tf_op jit(solution)/shard_map/all_gather | solution.py:164
  54.1 1.3 convert_reduce_fusion.1
  55.5 4.4 convolution_convert_fusion.1
  60.1 13.4 %shard_map.178 = bf16[640,768]{1,0:T(8,128)(2,1)S(1)} custom-call(bf16[640,2304]{1,0:T(8,128)(2,1)S(1)} %pad.11.q_ref.k_ref.v_ref, bf16[640,2304]{1,0:T(8,128)(2,1)S(1)} %pad.11.q_ref.k_ref.v_ref, bf16[640,2304]{1,0:T(8,128)(2,1)S(1)} %pad.11.q_ref.k_ref.v_ref), custom_call_target="tpu_custom_call" | custom-call | tf_op jit(solution)/shard_map/pallas_call | solution.py:90
  73.6 2.6 fusion.113
  77.8 1.5 fusion.114
  80.2 2.1 fusion.28
  82.3 2.2 convolution_convert_fusion.2
  84.5 2.5 add_convert_fusion.2
  87.1 1.4 copy-done.9
  88.4 1.6 pad_maximum_fusion.7
  90.0 4.6 all-to-all-start.2
  94.6 2.8 fusion.48
  97.4 17.9 %all-gather.5.cloned.1.call-done = bf16[2,768,3072]{2,1,0:T(8,128)(2,1)} async-done(((bf16[2,96,3072]{2,1,0:T(8,128)(2,1)}), bf16[2,768,3072]{2,1,0:T(8,128)(2,1)}) %all-gather.5.cloned.1.call-update) | async-done | bytes 9437200 | tf_op jit(solution)/shard_map/all_gather | solution.py:175
  115.3 4.9 slice.159
  120.2 8.5 %reshape_squeeze.3 = bf16[3072,768]{1,0:T(8,128)(2,1)} reshape(bf16[1,768,3072]{2,1,0:T(8,128)(2,1)} %slice.159) | data formatting | bytes 9437184 | tf_op jit(solution)/shard_map/reshape;squeeze | solution.py:177
  128.7 18.2 %all-to-all-done.2 = bf16[4,184,1536]{2,1,0:T(8,128)(2,1)} async-done(((bf16[4,184,1536]{2,1,0:T(8,128)(2,1)}), bf16[4,184,1536]{2,1,0:T(8,128)(2,1)}, u32[]{:S(2)}, u32[]{:S(2)}) %all-to-all-start.2) | async-done | bytes 2261024 | tf_op jit(solution)/shard_map/all_to_all | solution.py:233
  146.9 3.8 all-to-all-start
  150.8 25.8 %multiply_convert_fusion.1 = (bf16[736,3072]{1,0:T(8,128)(2,1)S(1)}, f32[736,3072]{1,0:T(8,128)}, f32[736,3072]{1,0:T(8,128)}) fusion(bf16[2,768,3072]{2,1,0:T(8,128)(2,1)} %all-gather.5.cloned.1.call-done, bf16[736,1536]{1,0:T(8,128)(2,1)} %bitcast.12), kind=kOutput, calls=%fused_computation.36 | convolution fusion | flops 3619848192 | bytes 28459008 | tf_op jit(solution)/shard_map/dot_general | solution.py:247
  176.6 3.7 convolution_convert_fusion.5
  180.3 10.7 %fusion.19 = bf16[736,3072]{1,0:T(8,128)(2,1)} fusion(f32[736,3072]{1,0:T(8,128)} %get-tuple-element.87, f32[736,3072]{1,0:T(8,128)} %get-tuple-element.79, bf16[3072,768]{1,0:T(8,128)(2,1)S(1)} %copy-done.15, bf16[736,1536]{1,0:T(8,128)(2,1)} %bitcast.12), kind=kOutput, calls=%fused_computation.35 | convolution fusion | flops 3490971648 | bytes 28459008 | tf_op jit(solution)/shard_map/dot_general | solution.py:244
  191.0 6.1 %fusion.71 = bf16[736,768]{1,0:T(8,128)(2,1)S(1)} fusion(bf16[736,3072]{1,0:T(8,128)(2,1)} %fusion.19, bf16[2,768,3072]{2,1,0:T(8,128)(2,1)S(1)} %bitcast.69), kind=kOutput, calls=%fused_computation.127 | convolution fusion | flops 3473448960 | bytes 10371072 | tf_op jit(solution)/shard_map/dot_general | solution.py:254
  197.2 1.6 pad_maximum_fusion.8
  198.8 5.4 all-to-all-done
  204.2 4.7 all-to-all-start.3
  208.9 26.3 %multiply_convert_fusion = (bf16[768,3072]{1,0:T(8,128)(2,1)S(1)}, f32[768,3072]{1,0:T(8,128)}, f32[768,3072]{1,0:T(8,128)}) fusion(bf16[2,768,3072]{2,1,0:T(8,128)(2,1)} %all-gather.5.cloned.1.call-done, bf16[768,1536]{1,0:T(8,128)(2,1)S(1)} %bitcast.64), kind=kOutput, calls=%fused_computation.14 | convolution fusion | flops 3777232896 | bytes 29491200 | tf_op jit(solution)/shard_map/dot_general | solution.py:247
  235.2 8.1 %convolution_convert_fusion.4 = bf16[768,768]{0,1:T(8,128)(2,1)S(1)} fusion(bf16[768,3072]{1,0:T(8,128)(2,1)S(1)} %get-tuple-element.76, bf16[3072,768]{1,0:T(8,128)(2,1)} %reshape_squeeze.3), kind=kOutput, calls=%fused_computation.126 | convolution fusion | flops 3624468480 | bytes 10616832 | tf_op jit(solution)/shard_map/dot_general | solution.py:251
  243.4 10.1 %fusion.6 = bf16[768,3072]{1,0:T(8,128)(2,1)S(1)} fusion(f32[768,3072]{1,0:T(8,128)} %get-tuple-element.88, f32[768,3072]{1,0:T(8,128)} %get-tuple-element.77, bf16[3072,768]{1,0:T(8,128)(2,1)} %reshape_squeeze.3, bf16[768,1536]{1,0:T(8,128)(2,1)S(1)} %bitcast.65), kind=kOutput, calls=%fused_computation.10 | convolution fusion | flops 3642753024 | bytes 29491200 | tf_op jit(solution)/shard_map/dot_general | solution.py:244
  253.5 8.0 %fusion.70 = bf16[768,768]{0,1:T(8,128)(2,1)S(1)} fusion(bf16[768,3072]{1,0:T(8,128)(2,1)S(1)} %fusion.6, bf16[2,768,3072]{2,1,0:T(8,128)(2,1)} %all-gather.5.cloned.1.call-done), kind=kOutput, calls=%fused_computation.124 | convolution fusion | flops 3624468480 | bytes 10616832 | tf_op jit(solution)/shard_map/dot_general | solution.py:254
  261.6 2.5 copy.76
  264.1 5.1 all-to-all-start.1
  269.6 52.4 %all-to-all-done.1 = bf16[4,192,1536]{2,1,0:T(8,128)(2,1)S(1)} async-done(((bf16[4,192,1536]{2,1,0:T(8,128)(2,1)}), bf16[4,192,1536]{2,1,0:T(8,128)(2,1)S(1)}, u32[]{:S(2)}, u32[]{:S(2)}) %all-to-all-start.1) | async-done | bytes 2359328 | tf_op jit(solution)/shard_map/all_to_all | solution.py:269
  322.0 5.1 fusion.30
  327.2 5.1 fusion.26
  332.3 1.9 multiply_reduce_fusion.3
  334.7 1.2 multiply_reduce_fusion
  337.0 2.1 convolution_convert_fusion.3
  339.2 0.9 convolution_convert_fusion.6
  340.2 21.8 %shard_map.179 = (bf16[640,768]{1,0:T(8,128)(2,1)S(1)}, bf16[640,768]{1,0:T(8,128)(2,1)S(1)}, bf16[640,768]{1,0:T(8,128)(2,1)S(1)}) custom-call(bf16[640,2304]{1,0:T(8,128)(2,1)} %copy-done, bf16[640,2304]{1,0:T(8,128)(2,1)} %copy-done, bf16[640,2304]{1,0:T(8,128)(2,1)} %copy-done, bf16[640,768]{1,0:T(8,128)(2,1)S(1)} %pad.13.g_ref), custom_call_target="tpu_custom_call" | custom-call | tf_op jit(solution)/shard_map/pallas_call | solution.py:106
  362.1 16.0 %convolution_convert_fusion = bf16[768,2304]{1,0:T(8,128)(2,1)} fusion(bf16[640,768]{1,0:T(8,128)(2,1)S(1)} %get-tuple-element.14, bf16[640,768]{1,0:T(8,128)(2,1)S(1)} %get-tuple-element.13, bf16[640,768]{1,0:T(8,128)(2,1)S(1)} %get-tuple-element.12, bf16[591,768]{1,0:T(8,128)(2,1)S(1)} %copy-done.8, f32[768]{0:T(1024)S(1)} %copy-done.42, ...), kind=kOutput, calls=%fused_computation.61 | convolution fusion | flops 2103724800 | bytes 7403640 | tf_op jit(solution)/shard_map/dot_general | solution.py:324
  378.1 3.5 fusion.67
  381.8 2.6 fusion.65
  384.8 8.4 %concatenate.36 = bf16[768,3078]{1,0:T(8,128)(2,1)} concatenate(bf16[768,2304]{1,0:T(8,128)(2,1)} %convolution_convert_fusion, bf16[768,768]{1,0:T(8,128)(2,1)} %convolution_convert_fusion.3, bf16[768,4]{1,0:T(8,128)(2,1)S(1)} %copy.78, bf16[768,1]{1,0:T(8,128)(2,1)S(1)} %broadcast_in_dim.40, bf16[768,1]{1,0:T(8,128)(2,1)S(1)} %broadcast_in_dim.41), dimensions={1} | concatenate | bytes 9455616 | tf_op jit(solution)/shard_map/concatenate | solution.py:334
  393.3 6.2 %fusion.73 = f32[3072,768]{1,0:T(8,128)S(1)} fusion(bf16[768,3072]{1,0:T(8,128)(2,1)} %copy-done.51, bf16[768,1536]{1,0:T(8,128)(2,1)} %bitcast.66), kind=kOutput, calls=%fused_computation.133 | convolution fusion | flops 3623878656 | bytes 15335424 | tf_op jit(solution)/shard_map/dot_general | solution.py:257
  399.6 9.2 %fusion.76 = f32[768,3072]{1,0:T(8,128)} fusion(bf16[768,3072]{1,0:T(8,128)(2,1)} %copy-done.16, bf16[768,1536]{1,0:T(8,128)(2,1)S(1)} %bitcast.67), kind=kOutput, calls=%fused_computation.136 | convolution fusion | flops 3623878656 | bytes 15335424 | tf_op jit(solution)/shard_map/dot_general | solution.py:260
  408.7 8.7 %add_convert_fusion = bf16[3072,768]{1,0:T(8,128)(2,1)} fusion(f32[3072,768]{1,0:T(8,128)S(1)} %fusion.73, bf16[736,3072]{1,0:T(8,128)(2,1)} %copy-done.52, bf16[736,1536]{1,0:T(8,128)(2,1)} %bitcast.12), kind=kOutput, calls=%fused_computation.12 | convolution fusion | flops 3477602304 | bytes 19808256 | tf_op jit(solution)/shard_map/dot_general | solution.py:257
  417.4 29.0 %reduce-scatter.3.cloned.1.call-done = bf16[96,3078]{1,0:T(8,128)(2,1)} async-done(((bf16[768,3078]{1,0:T(8,128)(2,1)}), bf16[96,3078]{1,0:T(8,128)(2,1)}) %reduce-scatter.3.cloned.1.call-update) | async-done | bytes 590992 | tf_op jit(solution)/shard_map/reduce_scatter | solution.py:338
  446.8 11.5 %fusion.34 = bf16[1,768,3072]{2,1,0:T(8,128)(2,1)} fusion(f32[768,3072]{1,0:T(8,128)} %fusion.76, bf16[736,3072]{1,0:T(8,128)(2,1)} %fusion.19, bf16[736,1536]{1,0:T(8,128)(2,1)} %bitcast.12), kind=kOutput, calls=%fused_computation.68 | convolution fusion | flops 3477602304 | bytes 19808256 | tf_op jit(solution)/shard_map/dot_general | solution.py:260
  458.3 8.5 %stack_reshape.4 = bf16[1,768,3072]{2,1,0:T(8,128)(2,1)} reshape(bf16[3072,768]{1,0:T(8,128)(2,1)} %add_convert_fusion) | data formatting | bytes 9437184 | tf_op jit(solution)/shard_map/stack;reshape | solution.py:272
  466.8 8.3 %pad_maximum_fusion = bf16[2,768,3072]{2,1,0:T(8,128)(2,1)} fusion(bf16[1,768,3072]{2,1,0:T(8,128)(2,1)} %stack_reshape.4, bf16[1,768,3072]{2,1,0:T(8,128)(2,1)} %fusion.34), kind=kLoop, calls=%fused_computation.11 | loop fusion | flops 4718592 | bytes 18874368 | tf_op jit(solution)/shard_map/stack | solution.py:272
  475.1 3.1 add_convert_fusion.3
  478.2 10.2 %all-reduce.5.cloned.1.call-done = bf16[96,3078]{1,0:T(8,128)(2,1)} async-done(((bf16[96,3078]{1,0:T(8,128)(2,1)}), bf16[96,3078]{1,0:T(8,128)(2,1)}) %all-reduce.5.cloned.1.call-update) | async-done | bytes 590992 | tf_op jit(solution)/shard_map/psum | solution.py:339
  489.8 2.0 slice.168
  491.8 1.6 slice.169
  493.5 1.2 convert_element_type.153
  495.3 72.8 %reduce-scatter.5.cloned.1.call-done = bf16[2,96,3072]{2,1,0:T(8,128)(2,1)} async-done(((bf16[2,768,3072]{2,1,0:T(8,128)(2,1)}), bf16[2,96,3072]{2,1,0:T(8,128)(2,1)}) %reduce-scatter.5.cloned.1.call-update) | async-done | bytes 1179664 | tf_op jit(solution)/shard_map/reduce_scatter | solution.py:275
  568.2 2.5 fusion.112
  570.7 1.3 broadcast_in_dim_reshape_squeeze.3
  (191 shorter events, 12.2 us)
Async XLA Ops:
  7.2 9.3 %copy-start.25 = (s32[591,2]{0,1:T(2,128)S(1)}, s32[591,2]{0,1:T(2,128)}, u32[]{:S(2)}) copy-start(s32[591,2]{0,1:T(2,128)} %param.13) | copy-start | bytes 14188
  7.2 12.2 %copy-start.7 = (bf16[591,768]{1,0:T(8,128)(2,1)S(1)}, bf16[591,768]{1,0:T(8,128)(2,1)}, u32[]{:S(2)}) copy-start(bf16[591,768]{1,0:T(8,128)(2,1)} %param.11) | copy-start | bytes 2723332
  7.2 46.9 %all-gather.3.cloned.1.call-start = ((), (), s32[]{:S(2)}) async-start(), calls=%async_computation.6 | async-start | bytes 5529600 | tf_op jit(solution)/shard_map/all_gather | solution.py:164
  11.6 8.5 %copy-start.5 = (bf16[591,768]{1,0:T(8,128)(2,1)S(1)}, bf16[591,768]{1,0:T(8,128)(2,1)}, u32[]{:S(2)}) copy-start(bf16[591,768]{1,0:T(8,128)(2,1)} %param.21) | copy-start | bytes 2723332
  11.6 103.7 %all-gather.5.cloned.1.call-start = ((), (), s32[]{:S(2)}) async-start(), calls=%async_computation.7 | async-start | bytes 10616832 | tf_op jit(solution)/shard_map/all_gather | solution.py:175
  19.3 60.1 %copy-start.17 = (f32[591]{0:T(1024)}, f32[591]{0:T(1024)S(1)}, u32[]{:S(2)}) copy-start(f32[591]{0:T(1024)S(1)} %fusion.101) | copy-start | bytes 7096
  19.4 65.2 %copy-start.45 = (s32[1504]{0:T(1024)}, s32[1504]{0:T(1024)S(1)}, u32[]{:S(2)}) copy-start(s32[1504]{0:T(1024)S(1)} %pad_add_fusion) | copy-start | bytes 18052
  19.4 62.9 %copy-start.47 = (s32[591]{0:T(1024)}, s32[591]{0:T(1024)S(1)}, u32[]{:S(2)}) copy-start(s32[591]{0:T(1024)S(1)} %get-tuple-element.73) | copy-start | bytes 7096
  19.4 65.1 %copy-start.49 = (s32[591]{0:T(1024)}, s32[591]{0:T(1024)S(1)}, u32[]{:S(2)}) copy-start(s32[591]{0:T(1024)S(1)} %get-tuple-element.72) | copy-start | bytes 7096
  19.7 40.2 %copy-start.33 = (f32[591]{0:T(1024)}, f32[591]{0:T(1024)S(1)}, u32[]{:S(2)}) copy-start(f32[591]{0:T(1024)S(1)} %broadcast_multiply_fusion.2) | copy-start | bytes 7096
  20.1 1.5 copy-start.37
  20.1 39.8 %copy-start.43 = (f32[591]{0:T(1024)}, f32[591]{0:T(1024)S(1)}, u32[]{:S(2)}) copy-start(f32[591]{0:T(1024)S(1)} %fusion.99) | copy-start | bytes 7096
  55.5 4.5 copy-start.41
  55.5 21.2 %copy-start.27 = (f32[768]{0:T(1024)}, f32[768]{0:T(1024)S(1)}, u32[]{:S(2)}) copy-start(f32[768]{0:T(1024)S(1)} %get-tuple-element.60) | copy-start | bytes 9220
  60.1 13.4 %copy-start = (bf16[640,2304]{1,0:T(8,128)(2,1)}, bf16[640,2304]{1,0:T(8,128)(2,1)S(1)}, u32[]{:S(2)}) copy-start(bf16[640,2304]{1,0:T(8,128)(2,1)S(1)} %pad.11.q_ref.k_ref.v_ref) | copy-start | bytes 8847364
  73.6 4.2 copy-start.1
  73.6 6.3 %copy-start.12 = (f32[591,768]{1,0:T(8,128)S(1)}, f32[591,768]{1,0:T(8,128)}, u32[]{:S(2)}) copy-start(f32[591,768]{1,0:T(8,128)} %convert_multiply_fusion) | copy-start | bytes 5446660
  76.2 3.1 copy-start.3
  76.2 1.2 copy-start.21
  76.6 2.7 copy-start.39
  76.6 5.7 copy-start.29
  77.8 4.6 copy-start.10
  79.4 2.9 copy-start.31
  79.9 2.4 copy-start.35
  87.0 1.4 copy-start.9
  90.0 57.0 %all-to-all-start.2 = ((bf16[4,184,1536]{2,1,0:T(8,128)(2,1)}), bf16[4,184,1536]{2,1,0:T(8,128)(2,1)}, u32[]{:S(2)}, u32[]{:S(2)}) async-start(bf16[4,184,1536]{2,1,0:T(8,128)(2,1)} %bitcast.63), calls=%async_computation.2 | async-start | bytes 4521984 | tf_op jit(solution)/shard_map/all_to_all | solution.py:233
  146.9 57.3 %all-to-all-start = ((bf16[4,192,1536]{2,1,0:T(8,128)(2,1)}), bf16[4,192,1536]{2,1,0:T(8,128)(2,1)S(1)}, u32[]{:S(2)}, u32[]{:S(2)}) async-start(bf16[4,192,1536]{2,1,0:T(8,128)(2,1)} %bitcast.6), calls=%async_computation | async-start | bytes 4718592 | tf_op jit(solution)/shard_map/all_to_all | solution.py:233
  150.8 25.8 %copy-start.15 = (bf16[3072,768]{1,0:T(8,128)(2,1)S(1)}, bf16[3072,768]{1,0:T(8,128)(2,1)}, u32[]{:S(2)}) copy-start(bf16[3072,768]{1,0:T(8,128)(2,1)} %reshape_squeeze.3) | copy-start | bytes 14155780
  176.6 3.7 copy-start.52
  176.6 14.4 %slice-start = ((s8[9437184]{0:T(1024)(128)(4,1)}), s8[4194304]{0:T(1024)(128)(4,1)S(1)}, s32[]{:S(2)}) async-start(s8[9437184]{0:T(1024)(128)(4,1)} %bitcast.68), calls=%async_computation.11 | async-start | bytes 8388608
  176.6 14.4 %slice-start.1 = ((s8[9437184]{0:T(1024)(128)(4,1)}), s8[4194304]{0:T(1024)(128)(4,1)S(1)}, s32[]{:S(2)}) async-start(s8[9437184]{0:T(1024)(128)(4,1)} %bitcast.68), calls=%async_computation.12 | async-start | bytes 8388608
  180.3 10.8 %slice-start.2 = ((s8[9437184]{0:T(1024)(128)(4,1)}), s8[1048576]{0:T(1024)(128)(4,1)S(1)}, s32[]{:S(2)}) async-start(s8[9437184]{0:T(1024)(128)(4,1)} %bitcast.68), calls=%async_computation.13 | async-start | bytes 2097152
  204.2 39.1 %copy-start.13 = (bf16[4,192,1536]{2,1,0:T(8,128)(2,1)}, bf16[4,192,1536]{2,1,0:T(8,128)(2,1)S(1)}, u32[]{:S(2)}) copy-start(bf16[4,192,1536]{2,1,0:T(8,128)(2,1)S(1)} %all-to-all-done) | copy-start | bytes 7077892
  204.2 59.9 %all-to-all-start.3 = ((bf16[4,184,1536]{2,1,0:T(8,128)(2,1)}), bf16[4,184,1536]{2,1,0:T(8,128)(2,1)}, u32[]{:S(2)}, u32[]{:S(2)}) async-start(bf16[4,184,1536]{2,1,0:T(8,128)(2,1)} %bitcast.13), calls=%async_computation.3 | async-start | bytes 4521984 | tf_op jit(solution)/shard_map/all_to_all | solution.py:269
  235.2 8.1 %copy-start.51 = (bf16[768,3072]{1,0:T(8,128)(2,1)}, bf16[768,3072]{1,0:T(8,128)(2,1)S(1)}, u32[]{:S(2)}) copy-start(bf16[768,3072]{1,0:T(8,128)(2,1)S(1)} %get-tuple-element.76) | copy-start | bytes 14155780
  253.5 8.0 %copy-start.16 = (bf16[768,3072]{1,0:T(8,128)(2,1)}, bf16[768,3072]{1,0:T(8,128)(2,1)S(1)}, u32[]{:S(2)}) copy-start(bf16[768,3072]{1,0:T(8,128)(2,1)S(1)} %fusion.6) | copy-start | bytes 14155780
  261.6 8.0 %copy-start.36 = (f32[591,2]{0,1:T(2,128)S(1)}, f32[591,2]{0,1:T(2,128)}, u32[]{:S(2)}) copy-start(f32[591,2]{0,1:T(2,128)} %copy-done.35) | copy-start | bytes 14188
  261.6 60.4 %copy-start.46 = (s32[1504]{0:T(1024)S(1)}, s32[1504]{0:T(1024)}, u32[]{:S(2)}) copy-start(s32[1504]{0:T(1024)} %copy-done.45) | copy-start | bytes 18052
  261.6 60.4 %copy-start.50 = (s32[591]{0:T(1024)S(1)}, s32[591]{0:T(1024)}, u32[]{:S(2)}) copy-start(s32[591]{0:T(1024)} %copy-done.49) | copy-start | bytes 7096
  264.1 57.9 %all-to-all-start.1 = ((bf16[4,192,1536]{2,1,0:T(8,128)(2,1)}), bf16[4,192,1536]{2,1,0:T(8,128)(2,1)S(1)}, u32[]{:S(2)}, u32[]{:S(2)}) async-start(bf16[4,192,1536]{2,1,0:T(8,128)(2,1)} %bitcast.9), calls=%async_computation.1 | async-start | bytes 4718592 | tf_op jit(solution)/shard_map/all_to_all | solution.py:269
  269.2 177.2 %reduce-scatter.3.cloned.1.call-start = ((), (), s32[]{:S(2)}) async-start(), calls=%async_computation.8 | async-start | bytes 5529600 | tf_op jit(solution)/shard_map/reduce_scatter | solution.py:338
  322.0 5.1 copy-start.48
  322.0 12.6 %slice-start.3 = ((s8[4915200]{0:T(1024)(128)(4,1)}), s8[4194304]{0:T(1024)(128)(4,1)S(1)}, s32[]{:S(2)}) async-start(s8[4915200]{0:T(1024)(128)(4,1)} %bitcast.72), calls=%async_computation.14 | async-start | bytes 8388608
  327.1 5.2 copy-start.4
  327.1 5.2 copy-start.6
  327.1 5.2 copy-start.18
  327.1 7.5 %slice-start.4 = ((s8[4915200]{0:T(1024)(128)(4,1)}), s8[720896]{0:T(1024)(128)(4,1)S(1)}, s32[]{:S(2)}) async-start(s8[4915200]{0:T(1024)(128)(4,1)} %bitcast.72), calls=%async_computation.15 | async-start | bytes 1441792
  332.2 2.0 copy-start.26
  332.2 2.1 copy-start.20
  332.2 2.1 copy-start.24
  332.3 2.1 copy-start.32
  332.3 2.1 copy-start.11
  332.3 2.4 copy-start.22
  332.3 2.4 copy-start.28
  332.3 2.4 copy-start.30
  334.2 1.6 copy-start.40
  340.2 21.9 %copy-start.8 = (bf16[591,768]{1,0:T(8,128)(2,1)S(1)}, bf16[591,768]{1,0:T(8,128)(2,1)}, u32[]{:S(2)}) copy-start(bf16[591,768]{1,0:T(8,128)(2,1)} %param.11) | copy-start | bytes 2723332
  340.2 21.9 %copy-start.34 = (f32[591]{0:T(1024)S(1)}, f32[591]{0:T(1024)}, u32[]{:S(2)}) copy-start(f32[591]{0:T(1024)} %copy-done.33) | copy-start | bytes 7096
  340.2 21.9 %copy-start.42 = (f32[768]{0:T(1024)S(1)}, f32[768]{0:T(1024)}, u32[]{:S(2)}) copy-start(f32[768]{0:T(1024)} %copy-done.41) | copy-start | bytes 9220
  340.2 21.9 %copy-start.44 = (f32[591]{0:T(1024)S(1)}, f32[591]{0:T(1024)}, u32[]{:S(2)}) copy-start(f32[591]{0:T(1024)} %copy-done.43) | copy-start | bytes 7096
  378.1 3.5 copy-start.38
  393.2 95.2 %all-reduce.5.cloned.1.call-start = ((), (), s32[]{:S(2)}) async-start(), calls=%async_computation.9 | async-start | bytes 1228800 | tf_op jit(solution)/shard_map/psum | solution.py:339
  393.3 6.3 %copy-start.14 = (bf16[4,192,1536]{2,1,0:T(8,128)(2,1)S(1)}, bf16[4,192,1536]{2,1,0:T(8,128)(2,1)}, u32[]{:S(2)}) copy-start(bf16[4,192,1536]{2,1,0:T(8,128)(2,1)} %copy-done.13) | copy-start | bytes 7077892
  446.5 121.7 %reduce-scatter.5.cloned.1.call-start = ((), (), s32[]{:S(2)}) async-start(), calls=%async_computation.10 | async-start | bytes 10616832 | tf_op jit(solution)/shard_map/reduce_scatter | solution.py:275
  (3 other events, 2.4 us)
Sparse Core Ops, SparseCore 0:
  11.8 42.3 all-gather.2
  56.6 58.6 all-gather.4
  393.4 53.0 reduce-scatter.2
  448.6 39.7 all-reduce.4
  491.8 76.3 reduce-scatter.4

commit v7 on v6

--- a/solution.py
+++ b/solution.py
@@ -113,6 +113,32 @@
     )(projected, projected, projected, mixed_grad)
 
 
+def _exchange(values, bits_left, bit, axis_name, size, index):
+    axis = bits_left.index(bit)
+    mine = (index >> bit) & 1
+    keep = lax.dynamic_index_in_dim(values, mine, axis, keepdims=False)
+    send = lax.dynamic_index_in_dim(values, 1 - mine, axis, keepdims=False)
+    pairs = [(i, i ^ (1 << bit)) for i in range(size)]
+    got = lax.ppermute(send.astype(jnp.bfloat16), axis_name, pairs)
+    return keep + got.astype(jnp.float32), [b for b in bits_left if b != bit]
+
+
+def shard_reduce_scatter(values, axis_name, split_col):
+    size = lax.axis_size(axis_name)
+    index = lax.axis_index(axis_name)
+    n_bits = size.bit_length() - 1
+    block = values.shape[0] // size
+    bits = list(range(n_bits - 1, -1, -1))
+    values = values.astype(jnp.float32).reshape([2] * n_bits + [block, values.shape[1]])
+    values, bits = _exchange(values, bits, 0, axis_name, size, index)
+    first, second = values[..., :split_col], values[..., split_col:]
+    first_bits, second_bits = list(bits), list(bits)
+    for up, down in zip(range(1, n_bits), range(n_bits - 1, 0, -1)):
+        first, first_bits = _exchange(first, first_bits, up, axis_name, size, index)
+        second, second_bits = _exchange(second, second_bits, down, axis_name, size, index)
+    return jnp.concatenate([first, second], axis=-1)
+
+
 def layer_norm(values, norm_gain):
     row_mean = jnp.mean(values, axis=-1, keepdims=True)
     centered = values - row_mean
@@ -177,7 +203,7 @@
     expert_second = expert_full[1].reshape(ff, width)
 
     token_f = tokens.astype(jnp.float32)
-    attn_in = layer_norm(token_f, gain_one).astype(jnp.bfloat16)
+    attn_in = lax.optimization_barrier(layer_norm(token_f, gain_one).astype(jnp.bfloat16))
     projected = jnp.dot(attn_in, full_qkv, preferred_element_type=jnp.float32).astype(jnp.bfloat16)
     pad_rows = -(-rows // 128) * 128
     projected_pad = jnp.pad(projected, ((0, pad_rows - rows), (0, 0)))
@@ -320,31 +346,33 @@
     )
     mixed_grad = jnp.pad(mixed_grad.astype(jnp.bfloat16), ((0, pad_rows - rows), (0, 0)))
     grad_q, grad_k, grad_v = attention_bwd(projected_pad, mixed_grad, images)
-    projected_grad = jnp.concatenate([grad_q, grad_k, grad_v], axis=1)[:rows]
+    projected_grad = jnp.concatenate([grad_q, grad_k, grad_v], axis=1)
+    attn_in_pad = jnp.pad(attn_in, ((0, pad_rows - rows), (0, 0)))
     grad_qkv = lax.dot_general(
-        attn_in, projected_grad, ROW_CONTRACT, preferred_element_type=jnp.float32
+        attn_in_pad, projected_grad, ROW_CONTRACT, preferred_element_type=jnp.float32
     )
     attn_in_grad = lax.dot_general(
-        projected_grad, full_qkv, COL_CONTRACT, preferred_element_type=jnp.float32
+        projected_grad[:rows], full_qkv, COL_CONTRACT, preferred_element_type=jnp.float32
     )
     _, first_back = jax.vjp(layer_norm, token_f, gain_one)
     token_part, grad_gain_one = first_back(attn_in_grad)
     grad_tokens = (state_grad + token_part).astype(jnp.bfloat16)
 
-    dense_grads = jnp.concatenate(
-        [grad_qkv, grad_wout, grad_router, grad_gain_one[:, None], grad_gain_two[:, None]],
-        axis=1,
-    ).astype(jnp.bfloat16)
-    dense_share = lax.psum_scatter(dense_grads, "shard", scatter_dimension=0, tiled=True)
-    dense_total = lax.psum(dense_share, "expert").astype(jnp.float32)
+    small = jnp.concatenate(
+        [grad_router, grad_gain_one[:, None], grad_gain_two[:, None]], axis=1
+    )
+    small = jnp.pad(small, ((0, 0), (0, 128 - small.shape[1])))
+    dense_grads = jnp.concatenate([grad_qkv, grad_wout, small], axis=1)
+    dense_share = shard_reduce_scatter(dense_grads, "shard", 128 * (dense_grads.shape[1] // 256))
+    dense_total = lax.psum(dense_share.astype(jnp.bfloat16), "expert").astype(jnp.float32)
     return (
         output,
         grad_tokens,
         dense_total[:, :qkv_cols],
         dense_total[:, qkv_cols : qkv_cols + width],
         dense_total[:, qkv_cols + width : qkv_cols + width + n_route],
-        dense_total[:, -2],
-        dense_total[:, -1],
+        dense_total[:, qkv_cols + width + n_route],
+        dense_total[:, qkv_cols + width + n_route + 1],
         grad_in_share,
         grad_back_share,
     )

time: 586 us -> 579 us (0.988)
  waiting for transfers between devices: 239 us -> 227 us
  matrix products: 184 us -> 177 us
  other arithmetic: 32.7 us -> 39.6 us
    reduce_scatter x1 -> x0, waiting for transfers between devices: 29 us -> none  [shards(): lax.psum_scatter(dense_grads, 'shard', scatter_dimension=0, tiled=True)]
    ppermute x0 -> x5, waiting for transfers between devices: none -> 21.6 us  [_exchange(): got = lax.ppermute(send.astype(jnp.bfloat16), axis_name, pairs)]
    dot_general x2, matrix products: 19.5 us -> 7.41 us  [the longest x1 4.97 us: shards(): lax.dot_general(attn_in_pad, projected_grad, ROW_CONTRACT, preferred_elem...]
    concatenate x1 -> x2, local copies, waits for them, and re-layouts: 8.43 us -> 0.25 us  [the longest x1 0.18 us: shards(): jnp.concatenate([grad_router, grad_gain_one[:, None], grad_gain_two[:, No...]
    dot_general x2, matrix products: 14.9 us -> 21.9 us  [shards(): lax.dot_general(activated, flat_grad, ROW_CONTRACT, preferred_element_typ...]
    unnamed x120 -> x140, local copies, waits for them, and re-layouts: 4.69 us -> 10.6 us
  transfers between devices with their start and end apart: 9 -> 13, of which waited for: 8 -> 11; matrix products, arithmetic and copies ran while one was open for 36% -> 38% of each run, Pallas kernels for 2% -> 2%
where the time goes in v7:
time: 579 us; the launch traced here: 572 us
  waiting for transfers between devices  227 us (39%)
  matrix products  177 us (31%)
  local copies, waits for them, and re-layouts  53.1 us (9%)
  other arithmetic  39.6 us (7%)
  Pallas kernels  35.2 us (6%)
  starting transfers between devices  24 us (4%)
  between operations  16 us (3%)
    reduce_scatter x1, waiting for transfers between devices, shards(): lax.psum_scatter(expert_grads, 'shard', scatter_dimension=1, tiled=True)  72.9 us
    all_to_all x2, waiting for transfers between devices, shards(): lax.all_to_all(returning, 'expert', split_axis=0, concat_axis=0, tiled=True)  52.4 us
    dot_general x2, matrix products, shards(): jnp.dot(flat_arrived, expert_first, preferred_element_type=jnp.float32)  52 us
    all_gather x1, waiting for transfers between devices, shards(): dense_full = lax.all_gather(dense_local, 'shard', axis=0, tiled=True)  32.5 us
    all_to_all x2, waiting for transfers between devices, shards(): lax.all_to_all(outgoing[experts * start:experts * (start + size)].reshape...  24.1 us
    dot_general x2, matrix products, shards(): lax.dot_general(activated, flat_grad, ROW_CONTRACT, preferred_element_typ...  21.9 us
    pallas_call x1, Pallas kernels, attention_bwd(): pl.pallas_call(functools.partial(attn_bwd_kernel, images=images), grid=(p...  21.8 us
    ppermute x5, waiting for transfers between devices, _exchange(): got = lax.ppermute(send.astype(jnp.bfloat16), axis_name, pairs)  21.6 us
  transfers between devices with their start and end apart: 13, of which 11 were waited for; matrix products, arithmetic and copies ran while one was open for 38% of the time, Pallas kernels for 2%

profile of v7, /device:TPU:0, one launch (start us, length us, event | category | flops | bytes accessed | tf_op | source)
XLA Modules:
  0.0 571.9 jit_solution(12017365516797256928)
XLA Ops:
  9.7 1.9 concatenate.35
  11.7 1.5 stack_reshape_squeeze.3
  13.2 2.2 pad_maximum_fusion.7
  20.1 1.5 convert_multiply_fusion
  21.6 32.5 %all-gather.3.cloned.1.call-done = bf16[768,3078]{1,0:T(8,128)(2,1)} async-done(((bf16[96,3078]{1,0:T(8,128)(2,1)}), bf16[768,3078]{1,0:T(8,128)(2,1)}) %all-gather.3.cloned.1.call-update) | async-done | bytes 4727824 | tf_op jit(solution)/shard_map/all_gather | solution.py:190
  55.8 4.6 convolution_convert_fusion
  60.7 13.4 %shard_map.178 = bf16[640,768]{1,0:T(8,128)(2,1)S(1)} custom-call(bf16[640,2304]{1,0:T(8,128)(2,1)S(1)} %pad.18.q_ref.k_ref.v_ref, bf16[640,2304]{1,0:T(8,128)(2,1)S(1)} %pad.18.q_ref.k_ref.v_ref, bf16[640,2304]{1,0:T(8,128)(2,1)S(1)} %pad.18.q_ref.k_ref.v_ref), custom_call_target="tpu_custom_call" | custom-call | tf_op jit(solution)/shard_map/pallas_call | solution.py:90
  74.2 2.6 fusion.121
  78.3 1.5 fusion.122
  80.7 2.1 fusion.28
  82.8 2.2 convolution_convert_fusion.1
  85.0 2.5 add_convert_fusion.2
  87.5 1.4 copy-done.10
  88.9 1.6 pad_maximum_fusion.5
  90.4 4.6 all-to-all-start.2
  95.0 3.0 fusion.50
  98.0 17.3 %all-gather.5.cloned.1.call-done = bf16[2,768,3072]{2,1,0:T(8,128)(2,1)} async-done(((bf16[2,96,3072]{2,1,0:T(8,128)(2,1)}), bf16[2,768,3072]{2,1,0:T(8,128)(2,1)}) %all-gather.5.cloned.1.call-update) | async-done | bytes 9437200 | tf_op jit(solution)/shard_map/all_gather | solution.py:201
  115.3 4.9 slice.167
  120.2 8.5 %reshape_squeeze.3 = bf16[3072,768]{1,0:T(8,128)(2,1)} reshape(bf16[1,768,3072]{2,1,0:T(8,128)(2,1)} %slice.167) | data formatting | bytes 9437184 | tf_op jit(solution)/shard_map/reshape;squeeze | solution.py:203
  128.7 18.7 %all-to-all-done.2 = bf16[4,184,1536]{2,1,0:T(8,128)(2,1)} async-done(((bf16[4,184,1536]{2,1,0:T(8,128)(2,1)}), bf16[4,184,1536]{2,1,0:T(8,128)(2,1)}, u32[]{:S(2)}, u32[]{:S(2)}) %all-to-all-start.2) | async-done | bytes 2261024 | tf_op jit(solution)/shard_map/all_to_all | solution.py:259
  147.4 3.8 all-to-all-start
  151.2 25.8 %multiply_convert_fusion.1 = (bf16[736,3072]{1,0:T(8,128)(2,1)S(1)}, f32[736,3072]{1,0:T(8,128)}, f32[736,3072]{1,0:T(8,128)}) fusion(bf16[2,768,3072]{2,1,0:T(8,128)(2,1)} %all-gather.5.cloned.1.call-done, bf16[736,1536]{1,0:T(8,128)(2,1)} %bitcast.12), kind=kOutput, calls=%fused_computation.38 | convolution fusion | flops 3619848192 | bytes 28459008 | tf_op jit(solution)/shard_map/dot_general | solution.py:273
  177.0 3.7 convolution_convert_fusion.3
  180.7 10.8 %fusion.19 = bf16[736,3072]{1,0:T(8,128)(2,1)} fusion(f32[736,3072]{1,0:T(8,128)} %get-tuple-element.105, f32[736,3072]{1,0:T(8,128)} %get-tuple-element.97, bf16[3072,768]{1,0:T(8,128)(2,1)S(1)} %copy-done.17, bf16[736,1536]{1,0:T(8,128)(2,1)} %bitcast.12), kind=kOutput, calls=%fused_computation.37 | convolution fusion | flops 3490971648 | bytes 28459008 | tf_op jit(solution)/shard_map/dot_general | solution.py:270
  191.5 6.1 %fusion.73 = bf16[736,768]{1,0:T(8,128)(2,1)S(1)} fusion(bf16[736,3072]{1,0:T(8,128)(2,1)} %fusion.19, bf16[2,768,3072]{2,1,0:T(8,128)(2,1)S(1)} %bitcast.106), kind=kOutput, calls=%fused_computation.129 | convolution fusion | flops 3473448960 | bytes 10371072 | tf_op jit(solution)/shard_map/dot_general | solution.py:280
  197.6 1.6 pad_maximum_fusion.6
  199.2 5.4 all-to-all-done
  204.6 4.7 all-to-all-start.3
  209.3 26.2 %multiply_convert_fusion = (bf16[768,3072]{1,0:T(8,128)(2,1)S(1)}, f32[768,3072]{1,0:T(8,128)}, f32[768,3072]{1,0:T(8,128)}) fusion(bf16[2,768,3072]{2,1,0:T(8,128)(2,1)} %all-gather.5.cloned.1.call-done, bf16[768,1536]{1,0:T(8,128)(2,1)S(1)} %bitcast.99), kind=kOutput, calls=%fused_computation.16 | convolution fusion | flops 3777232896 | bytes 29491200 | tf_op jit(solution)/shard_map/dot_general | solution.py:273
  235.5 8.1 %convolution_convert_fusion.2 = bf16[768,768]{0,1:T(8,128)(2,1)S(1)} fusion(bf16[768,3072]{1,0:T(8,128)(2,1)S(1)} %get-tuple-element.94, bf16[3072,768]{1,0:T(8,128)(2,1)} %reshape_squeeze.3), kind=kOutput, calls=%fused_computation.128 | convolution fusion | flops 3624468480 | bytes 10616832 | tf_op jit(solution)/shard_map/dot_general | solution.py:277
  243.7 10.1 %fusion.6 = bf16[768,3072]{1,0:T(8,128)(2,1)S(1)} fusion(f32[768,3072]{1,0:T(8,128)} %get-tuple-element.106, f32[768,3072]{1,0:T(8,128)} %get-tuple-element.95, bf16[3072,768]{1,0:T(8,128)(2,1)} %reshape_squeeze.3, bf16[768,1536]{1,0:T(8,128)(2,1)S(1)} %bitcast.100), kind=kOutput, calls=%fused_computation.12 | convolution fusion | flops 3642753024 | bytes 29491200 | tf_op jit(solution)/shard_map/dot_general | solution.py:270
  253.8 8.0 %fusion.72 = bf16[768,768]{0,1:T(8,128)(2,1)S(1)} fusion(bf16[768,3072]{1,0:T(8,128)(2,1)S(1)} %fusion.6, bf16[2,768,3072]{2,1,0:T(8,128)(2,1)} %all-gather.5.cloned.1.call-done), kind=kOutput, calls=%fused_computation.127 | convolution fusion | flops 3624468480 | bytes 10616832 | tf_op jit(solution)/shard_map/dot_general | solution.py:280
  262.0 2.5 copy.112
  264.4 5.1 all-to-all-start.1
  270.0 52.4 %all-to-all-done.1 = bf16[4,192,1536]{2,1,0:T(8,128)(2,1)S(1)} async-done(((bf16[4,192,1536]{2,1,0:T(8,128)(2,1)}), bf16[4,192,1536]{2,1,0:T(8,128)(2,1)S(1)}, u32[]{:S(2)}, u32[]{:S(2)}) %all-to-all-start.1) | async-done | bytes 2359328 | tf_op jit(solution)/shard_map/all_to_all | solution.py:295
  322.3 5.1 fusion.30
  327.5 5.1 fusion.26
  332.7 1.9 multiply_reduce_fusion.3
  337.4 2.5 fusion.89
  340.9 21.8 %shard_map.179 = (bf16[640,768]{1,0:T(8,128)(2,1)S(1)}, bf16[640,768]{1,0:T(8,128)(2,1)S(1)}, bf16[640,768]{1,0:T(8,128)(2,1)S(1)}) custom-call(bf16[640,2304]{1,0:T(8,128)(2,1)} %copy-done, bf16[640,2304]{1,0:T(8,128)(2,1)} %copy-done, bf16[640,2304]{1,0:T(8,128)(2,1)} %copy-done, bf16[640,768]{1,0:T(8,128)(2,1)S(1)} %pad.20.g_ref), custom_call_target="tpu_custom_call" | custom-call | tf_op jit(solution)/shard_map/pallas_call | solution.py:106
  363.9 5.0 fusion.87
  368.9 2.4 fusion.69
  373.8 4.7 select_maximum_fusion
  378.5 3.8 copy-done.5
  382.2 1.7 fusion.49
  383.9 10.4 %fusion.75 = f32[3072,768]{1,0:T(8,128)} fusion(bf16[768,3072]{1,0:T(8,128)(2,1)} %copy-done.55, bf16[768,1536]{1,0:T(8,128)(2,1)} %bitcast.101), kind=kOutput, calls=%fused_computation.138 | convolution fusion | flops 3623878656 | bytes 15335424 | tf_op jit(solution)/shard_map/dot_general | solution.py:283
  394.3 11.5 %add_convert_fusion = bf16[3072,768]{1,0:T(8,128)(2,1)} fusion(f32[3072,768]{1,0:T(8,128)} %fusion.75, bf16[736,3072]{1,0:T(8,128)(2,1)} %copy-done.56, bf16[736,1536]{1,0:T(8,128)(2,1)} %bitcast.12), kind=kOutput, calls=%fused_computation.14 | convolution fusion | flops 3477602304 | bytes 19808256 | tf_op jit(solution)/shard_map/dot_general | solution.py:283
  405.9 2.1 bitcast_add_fusion
  408.4 1.5 collective-permute-start.1
  409.9 6.4 %fusion.78 = f32[768,3072]{1,0:T(8,128)} fusion(bf16[768,3072]{1,0:T(8,128)(2,1)S(1)} %bitcast.104, bf16[768,1536]{1,0:T(8,128)(2,1)S(1)} %bitcast.102), kind=kOutput, calls=%fused_computation.141 | convolution fusion | flops 3623878656 | bytes 15335424 | tf_op jit(solution)/shard_map/dot_general | solution.py:286
  417.7 6.6 %collective-permute-done.1 = bf16[2,96,1536]{2,1,0:T(8,128)(2,1)S(1)} collective-permute-done((bf16[2,96,1536]{2,1,0:T(8,128)(2,1)S(1)}, bf16[2,96,1536]{2,1,0:T(8,128)(2,1)S(1)}, u32[]{:S(2)}, u32[]{:S(2)}) %collective-permute-start.1) | collective-permute-done | bytes 589856 | tf_op jit(solution)/shard_map/ppermute | solution.py:122
  425.7 8.2 %collective-permute-done.3 = bf16[2,96,1664]{2,1,0:T(8,128)(2,1)S(1)} collective-permute-done((bf16[2,96,1664]{2,1,0:T(8,128)(2,1)S(1)}, bf16[2,96,1664]{2,1,0:T(8,128)(2,1)S(1)}, u32[]{:S(2)}, u32[]{:S(2)}) %collective-permute-start.3) | collective-permute-done | bytes 639008 | tf_op jit(solution)/shard_map/ppermute | solution.py:122
  435.3 4.2 collective-permute-done.2
  439.6 2.6 collective-permute-done.4
  443.5 11.6 %fusion.34 = bf16[1,768,3072]{2,1,0:T(8,128)(2,1)} fusion(f32[768,3072]{1,0:T(8,128)} %fusion.78, bf16[736,3072]{1,0:T(8,128)(2,1)} %fusion.19, bf16[736,1536]{1,0:T(8,128)(2,1)} %bitcast.12), kind=kOutput, calls=%fused_computation.71 | convolution fusion | flops 3477602304 | bytes 19808256 | tf_op jit(solution)/shard_map/dot_general | solution.py:286
  455.1 8.5 %stack_reshape.4 = bf16[1,768,3072]{2,1,0:T(8,128)(2,1)} reshape(bf16[3072,768]{1,0:T(8,128)(2,1)} %add_convert_fusion) | data formatting | bytes 9437184 | tf_op jit(solution)/shard_map/stack;reshape | solution.py:298
  463.6 8.3 %pad_maximum_fusion = bf16[2,768,3072]{2,1,0:T(8,128)(2,1)} fusion(bf16[1,768,3072]{2,1,0:T(8,128)(2,1)} %stack_reshape.4, bf16[1,768,3072]{2,1,0:T(8,128)(2,1)} %fusion.34), kind=kLoop, calls=%fused_computation.13 | loop fusion | flops 4718592 | bytes 18874368 | tf_op jit(solution)/shard_map/stack | solution.py:298
  471.9 3.1 add_convert_fusion.3
  475.1 6.4 %all-reduce.7.cloned.1.call-done = bf16[96,3200]{1,0:T(8,128)(2,1)} async-done(((bf16[96,3200]{1,0:T(8,128)(2,1)}), bf16[96,3200]{1,0:T(8,128)(2,1)}) %all-reduce.7.cloned.1.call-update) | async-done | bytes 614416 | tf_op jit(solution)/shard_map/psum | solution.py:367
  482.9 2.0 slice.179
  484.9 1.6 slice.180
  488.4 72.9 %reduce-scatter.2.cloned.1.call-done = bf16[2,96,3072]{2,1,0:T(8,128)(2,1)} async-done(((bf16[2,768,3072]{2,1,0:T(8,128)(2,1)}), bf16[2,96,3072]{2,1,0:T(8,128)(2,1)}) %reduce-scatter.2.cloned.1.call-update) | async-done | bytes 1179664 | tf_op jit(solution)/shard_map/reduce_scatter | solution.py:301
  561.2 2.5 fusion.120
  563.7 1.3 broadcast_in_dim_reshape_squeeze.3
  (236 shorter events, 27.5 us)
Async XLA Ops:
  7.2 9.3 %copy-start.31 = (s32[591,2]{0,1:T(2,128)S(1)}, s32[591,2]{0,1:T(2,128)}, u32[]{:S(2)}) copy-start(s32[591,2]{0,1:T(2,128)} %param.13) | copy-start | bytes 14188
  7.2 12.2 %copy-start.6 = (bf16[591,768]{1,0:T(8,128)(2,1)S(1)}, bf16[591,768]{1,0:T(8,128)(2,1)}, u32[]{:S(2)}) copy-start(bf16[591,768]{1,0:T(8,128)(2,1)} %param.11) | copy-start | bytes 2723332
  7.2 46.9 %all-gather.3.cloned.1.call-start = ((), (), s32[]{:S(2)}) async-start(), calls=%async_computation.5 | async-start | bytes 5529600 | tf_op jit(solution)/shard_map/all_gather | solution.py:190
  11.6 8.5 %copy-start.8 = (bf16[591,768]{1,0:T(8,128)(2,1)S(1)}, bf16[591,768]{1,0:T(8,128)(2,1)}, u32[]{:S(2)}) copy-start(bf16[591,768]{1,0:T(8,128)(2,1)} %param.21) | copy-start | bytes 2723332
  11.6 103.7 %all-gather.5.cloned.1.call-start = ((), (), s32[]{:S(2)}) async-start(), calls=%async_computation.6 | async-start | bytes 10616832 | tf_op jit(solution)/shard_map/all_gather | solution.py:201
  19.3 60.6 %copy-start.21 = (f32[591]{0:T(1024)}, f32[591]{0:T(1024)S(1)}, u32[]{:S(2)}) copy-start(f32[591]{0:T(1024)S(1)} %fusion.112) | copy-start | bytes 7096
  19.4 65.6 %copy-start.49 = (s32[1504]{0:T(1024)}, s32[1504]{0:T(1024)S(1)}, u32[]{:S(2)}) copy-start(s32[1504]{0:T(1024)S(1)} %pad_add_fusion) | copy-start | bytes 18052
  19.4 63.4 %copy-start.51 = (s32[591]{0:T(1024)}, s32[591]{0:T(1024)S(1)}, u32[]{:S(2)}) copy-start(s32[591]{0:T(1024)S(1)} %get-tuple-element.91) | copy-start | bytes 7096
  19.4 65.6 %copy-start.53 = (s32[591]{0:T(1024)}, s32[591]{0:T(1024)S(1)}, u32[]{:S(2)}) copy-start(s32[591]{0:T(1024)S(1)} %get-tuple-element.90) | copy-start | bytes 7096
  19.7 40.8 %copy-start.29 = (f32[591]{0:T(1024)}, f32[591]{0:T(1024)S(1)}, u32[]{:S(2)}) copy-start(f32[591]{0:T(1024)S(1)} %broadcast_multiply_fusion.2) | copy-start | bytes 7096
  20.1 40.4 %copy-start.41 = (f32[591]{0:T(1024)}, f32[591]{0:T(1024)S(1)}, u32[]{:S(2)}) copy-start(f32[591]{0:T(1024)S(1)} %fusion.110) | copy-start | bytes 7096
  55.5 5.0 copy-start.39
  55.5 21.7 %copy-start.33 = (f32[768]{0:T(1024)}, f32[768]{0:T(1024)S(1)}, u32[]{:S(2)}) copy-start(f32[768]{0:T(1024)S(1)} %get-tuple-element.78) | copy-start | bytes 9220
  55.8 4.7 copy-start.19
  60.7 13.4 %copy-start = (bf16[640,2304]{1,0:T(8,128)(2,1)}, bf16[640,2304]{1,0:T(8,128)(2,1)S(1)}, u32[]{:S(2)}) copy-start(bf16[640,2304]{1,0:T(8,128)(2,1)S(1)} %pad.18.q_ref.k_ref.v_ref) | copy-start | bytes 8847364
  74.1 4.1 copy-start.1
  74.2 6.2 %copy-start.14 = (f32[591,768]{1,0:T(8,128)S(1)}, f32[591,768]{1,0:T(8,128)}, u32[]{:S(2)}) copy-start(f32[591,768]{1,0:T(8,128)} %convert_multiply_fusion) | copy-start | bytes 5446660
  76.8 3.0 copy-start.3
  77.2 2.6 copy-start.47
  77.2 5.6 copy-start.35
  78.2 4.6 copy-start.11
  79.9 2.9 copy-start.37
  80.4 2.4 copy-start.43
  90.4 56.9 %all-to-all-start.2 = ((bf16[4,184,1536]{2,1,0:T(8,128)(2,1)}), bf16[4,184,1536]{2,1,0:T(8,128)(2,1)}, u32[]{:S(2)}, u32[]{:S(2)}) async-start(bf16[4,184,1536]{2,1,0:T(8,128)(2,1)} %bitcast.98), calls=%async_computation.2 | async-start | bytes 4521984 | tf_op jit(solution)/shard_map/all_to_all | solution.py:259
  147.4 57.3 %all-to-all-start = ((bf16[4,192,1536]{2,1,0:T(8,128)(2,1)}), bf16[4,192,1536]{2,1,0:T(8,128)(2,1)S(1)}, u32[]{:S(2)}, u32[]{:S(2)}) async-start(bf16[4,192,1536]{2,1,0:T(8,128)(2,1)} %bitcast.6), calls=%async_computation | async-start | bytes 4718592 | tf_op jit(solution)/shard_map/all_to_all | solution.py:259
  151.2 25.8 %copy-start.17 = (bf16[3072,768]{1,0:T(8,128)(2,1)S(1)}, bf16[3072,768]{1,0:T(8,128)(2,1)}, u32[]{:S(2)}) copy-start(bf16[3072,768]{1,0:T(8,128)(2,1)} %reshape_squeeze.3) | copy-start | bytes 14155780
  177.0 3.7 copy-start.56
  177.0 14.5 %slice-start.5 = ((s8[9437184]{0:T(1024)(128)(4,1)}), s8[4194304]{0:T(1024)(128)(4,1)S(1)}, s32[]{:S(2)}) async-start(s8[9437184]{0:T(1024)(128)(4,1)} %bitcast.105), calls=%async_computation.14 | async-start | bytes 8388608
  177.0 14.5 %slice-start.6 = ((s8[9437184]{0:T(1024)(128)(4,1)}), s8[4194304]{0:T(1024)(128)(4,1)S(1)}, s32[]{:S(2)}) async-start(s8[9437184]{0:T(1024)(128)(4,1)} %bitcast.105), calls=%async_computation.15 | async-start | bytes 8388608
  180.7 10.8 %slice-start.7 = ((s8[9437184]{0:T(1024)(128)(4,1)}), s8[1048576]{0:T(1024)(128)(4,1)S(1)}, s32[]{:S(2)}) async-start(s8[9437184]{0:T(1024)(128)(4,1)} %bitcast.105), calls=%async_computation.16 | async-start | bytes 2097152
  204.6 39.0 %copy-start.15 = (bf16[4,192,1536]{2,1,0:T(8,128)(2,1)}, bf16[4,192,1536]{2,1,0:T(8,128)(2,1)S(1)}, u32[]{:S(2)}) copy-start(bf16[4,192,1536]{2,1,0:T(8,128)(2,1)S(1)} %all-to-all-done) | copy-start | bytes 7077892
  204.6 59.8 %all-to-all-start.3 = ((bf16[4,184,1536]{2,1,0:T(8,128)(2,1)}), bf16[4,184,1536]{2,1,0:T(8,128)(2,1)}, u32[]{:S(2)}, u32[]{:S(2)}) async-start(bf16[4,184,1536]{2,1,0:T(8,128)(2,1)} %bitcast.13), calls=%async_computation.3 | async-start | bytes 4521984 | tf_op jit(solution)/shard_map/all_to_all | solution.py:295
  235.5 8.1 %copy-start.55 = (bf16[768,3072]{1,0:T(8,128)(2,1)}, bf16[768,3072]{1,0:T(8,128)(2,1)S(1)}, u32[]{:S(2)}) copy-start(bf16[768,3072]{1,0:T(8,128)(2,1)S(1)} %get-tuple-element.94) | copy-start | bytes 14155780
  253.8 8.0 %copy-start.18 = (bf16[768,3072]{1,0:T(8,128)(2,1)}, bf16[768,3072]{1,0:T(8,128)(2,1)S(1)}, u32[]{:S(2)}) copy-start(bf16[768,3072]{1,0:T(8,128)(2,1)S(1)} %fusion.6) | copy-start | bytes 14155780
  261.9 8.0 %copy-start.44 = (f32[591,2]{0,1:T(2,128)S(1)}, f32[591,2]{0,1:T(2,128)}, u32[]{:S(2)}) copy-start(f32[591,2]{0,1:T(2,128)} %copy-done.43) | copy-start | bytes 14188
  262.0 60.4 %copy-start.50 = (s32[1504]{0:T(1024)S(1)}, s32[1504]{0:T(1024)}, u32[]{:S(2)}) copy-start(s32[1504]{0:T(1024)} %copy-done.49) | copy-start | bytes 18052
  262.0 60.4 %copy-start.54 = (s32[591]{0:T(1024)S(1)}, s32[591]{0:T(1024)}, u32[]{:S(2)}) copy-start(s32[591]{0:T(1024)} %copy-done.53) | copy-start | bytes 7096
  264.4 57.9 %all-to-all-start.1 = ((bf16[4,192,1536]{2,1,0:T(8,128)(2,1)}), bf16[4,192,1536]{2,1,0:T(8,128)(2,1)S(1)}, u32[]{:S(2)}, u32[]{:S(2)}) async-start(bf16[4,192,1536]{2,1,0:T(8,128)(2,1)} %bitcast.9), calls=%async_computation.1 | async-start | bytes 4718592 | tf_op jit(solution)/shard_map/all_to_all | solution.py:295
  269.5 212.0 %all-reduce.7.cloned.1.call-start = ((), (), s32[]{:S(2)}) async-start(), calls=%async_computation.7 | async-start | bytes 1228800 | tf_op jit(solution)/shard_map/psum | solution.py:367
  322.3 5.1 copy-start.52
  322.3 12.6 %slice-start.8 = ((s8[4915200]{0:T(1024)(128)(4,1)}), s8[4194304]{0:T(1024)(128)(4,1)S(1)}, s32[]{:S(2)}) async-start(s8[4915200]{0:T(1024)(128)(4,1)} %bitcast.109), calls=%async_computation.17 | async-start | bytes 8388608
  327.4 5.2 copy-start.4
  327.4 5.2 copy-start.9
  327.5 5.2 copy-start.22
  327.5 7.5 %slice-start.9 = ((s8[4915200]{0:T(1024)(128)(4,1)}), s8[720896]{0:T(1024)(128)(4,1)S(1)}, s32[]{:S(2)}) async-start(s8[4915200]{0:T(1024)(128)(4,1)} %bitcast.109), calls=%async_computation.18 | async-start | bytes 1441792
  332.6 2.4 copy-start.34
  332.6 2.4 copy-start.36
  363.9 5.0 copy-start.7
  363.9 5.0 copy-start.30
  363.9 5.0 copy-start.40
  368.9 2.5 copy-start.46
  368.9 3.7 copy-start.42
  378.4 3.8 copy-start.5
  383.9 22.0 %collective-permute-start = (bf16[2,2,96,3200]{3,2,1,0:T(8,128)(2,1)}, bf16[2,2,96,3200]{3,2,1,0:T(8,128)(2,1)}, u32[]{:S(2)}, u32[]{:S(2)}) collective-permute-start(bf16[2,2,96,3200]{3,2,1,0:T(8,128)(2,1)} %fusion.49), channel_id=1, source_target_pairs={{0,1},{1,0},{2,3},{3,2},{4,5},{5,4},{6,7},{7,6},{8,9},{9,8},{10,11... | collective-permute-start | bytes 7372808 | tf_op jit(solution)/shard_map/ppermute | solution.py:122
  383.9 22.0 %slice-start = ((s8[9830400]{0:T(1024)(128)(4,1)}), s8[4194304]{0:T(1024)(128)(4,1)S(1)}, s32[]{:S(2)}) async-start(s8[9830400]{0:T(1024)(128)(4,1)} %bitcast.95), calls=%async_computation.9 | async-start | bytes 8388608
  383.9 22.0 %slice-start.1 = ((s8[9830400]{0:T(1024)(128)(4,1)}), s8[4194304]{0:T(1024)(128)(4,1)S(1)}, s32[]{:S(2)}) async-start(s8[9830400]{0:T(1024)(128)(4,1)} %bitcast.95), calls=%async_computation.10 | async-start | bytes 8388608
  383.9 26.0 %slice-start.3 = ((s8[4718592]{0:T(1024)(128)(4,1)}), s8[4194304]{0:T(1024)(128)(4,1)S(1)}, s32[]{:S(2)}) async-start(s8[4718592]{0:T(1024)(128)(4,1)} %bitcast.103), calls=%async_computation.12 | async-start | bytes 8388608
  394.3 11.6 %slice-start.2 = ((s8[9830400]{0:T(1024)(128)(4,1)}), s8[1441792]{0:T(1024)(128)(4,1)S(1)}, s32[]{:S(2)}) async-start(s8[9830400]{0:T(1024)(128)(4,1)} %bitcast.95), calls=%async_computation.11 | async-start | bytes 2883584
  394.3 15.6 %slice-start.4 = ((s8[4718592]{0:T(1024)(128)(4,1)}), s8[524288]{0:T(1024)(128)(4,1)S(1)}, s32[]{:S(2)}) async-start(s8[4718592]{0:T(1024)(128)(4,1)} %bitcast.103), calls=%async_computation.13 | async-start | bytes 1048576
  408.4 15.8 %collective-permute-start.1 = (bf16[2,96,1536]{2,1,0:T(8,128)(2,1)S(1)}, bf16[2,96,1536]{2,1,0:T(8,128)(2,1)S(1)}, u32[]{:S(2)}, u32[]{:S(2)}) collective-permute-start(bf16[2,96,1536]{2,1,0:T(8,128)(2,1)S(1)} %fusion.94), channel_id=1, source_target_pairs={{0,2},{1,3},{2,0},{3,1},{4,6},{5,7},{6,4},{7,5},{8,10},{9,11},{10,... | collective-permute-start | bytes 1769480 | tf_op jit(solution)/shard_map/ppermute | solution.py:122
  416.6 17.3 %collective-permute-start.3 = (bf16[2,96,1664]{2,1,0:T(8,128)(2,1)S(1)}, bf16[2,96,1664]{2,1,0:T(8,128)(2,1)S(1)}, u32[]{:S(2)}, u32[]{:S(2)}) collective-permute-start(bf16[2,96,1664]{2,1,0:T(8,128)(2,1)S(1)} %fusion.92), channel_id=1, source_target_pairs={{0,4},{1,5},{2,6},{3,7},{4,0},{5,1},{6,2},{7,3},{8,12},{9,13},{10,... | collective-permute-start | bytes 1916936 | tf_op jit(solution)/shard_map/ppermute | solution.py:122
  424.4 15.1 %collective-permute-start.2 = (bf16[96,1536]{1,0:T(8,128)(2,1)S(1)}, bf16[96,1536]{1,0:T(8,128)(2,1)S(1)}, u32[]{:S(2)}, u32[]{:S(2)}) collective-permute-start(bf16[96,1536]{1,0:T(8,128)(2,1)S(1)} %fusion.97), channel_id=1, source_target_pairs={{0,4},{1,5},{2,6},{3,7},{4,0},{5,1},{6,2},{7,3},{8,12},{9,13},{10,... | collective-permute-start | bytes 884744 | tf_op jit(solution)/shard_map/ppermute | solution.py:122
  434.1 8.1 %collective-permute-start.4 = (bf16[96,1664]{1,0:T(8,128)(2,1)S(1)}, bf16[96,1664]{1,0:T(8,128)(2,1)S(1)}, u32[]{:S(2)}, u32[]{:S(2)}) collective-permute-start(bf16[96,1664]{1,0:T(8,128)(2,1)S(1)} %fusion.96), channel_id=1, source_target_pairs={{0,2},{1,3},{2,0},{3,1},{4,6},{5,7},{6,4},{7,5},{8,10},{9,11},{10,... | collective-permute-start | bytes 958472 | tf_op jit(solution)/shard_map/ppermute | solution.py:122
  443.2 118.0 %reduce-scatter.2.cloned.1.call-start = ((), (), s32[]{:S(2)}) async-start(), calls=%async_computation.8 | async-start | bytes 10616832 | tf_op jit(solution)/shard_map/reduce_scatter | solution.py:301
  (16 other events, 25.3 us)
Sparse Core Ops, SparseCore 0:
  11.8 42.3 all-gather.2
  56.6 58.6 all-gather.4
  443.3 38.1 all-reduce.6
  484.8 76.3 reduce-scatter.1

commit v8 on v7

--- a/solution.py
+++ b/solution.py
@@ -17,78 +17,69 @@
 COL_CONTRACT = (((1,), (1,)), ((), ()))
 
 
-def _image_of(idx, images):
-    count = jnp.zeros(idx.shape, jnp.int32)
-    for i in range(1, images + 1):
-        count = count + (idx >= i * SEQ).astype(jnp.int32)
-    return count
-
-
-def _same_image(size, images):
-    rows = lax.broadcasted_iota(jnp.int32, (size, size), 0)
-    cols = lax.broadcasted_iota(jnp.int32, (size, size), 1)
-    return _image_of(rows, images) == _image_of(cols, images)
-
-
-def _softmax_masked(qj, k, same):
+def _softmax_masked(qj, k, valid):
     s = lax.dot_general(qj, k, COL_CONTRACT, preferred_element_type=jnp.float32) * (HD ** -0.5)
-    s = jnp.where(same, s, -jnp.inf)
+    s = jnp.where(valid, s, -jnp.inf)
     top = jnp.max(s, axis=1, keepdims=True)
     e = jnp.exp(s - top)
     return e / jnp.sum(e, axis=1, keepdims=True)
 
 
-def attn_fwd_kernel(q_ref, k_ref, v_ref, o_ref, *, images):
-    R = q_ref.shape[0]
-    q = q_ref[...]
-    k = k_ref[...]
-    v = v_ref[...]
-    same = _same_image(R, images)
+def attn_fwd_kernel(q_ref, k_ref, v_ref, o_ref, *, images, slot):
+    valid = lax.broadcasted_iota(jnp.int32, (slot, slot), 1) < SEQ
     lane = lax.broadcasted_iota(jnp.int32, (1, 2 * HD), 1)
-    out = jnp.zeros((R, 2 * HD), jnp.float32)
-    for j in range(2):
-        in_head = (lane >= HD) == (j == 1)
-        p = _softmax_masked(jnp.where(in_head, q, jnp.zeros_like(q)), k, same)
-        o = jnp.dot(p.astype(jnp.bfloat16), v, preferred_element_type=jnp.float32)
-        out = jnp.where(in_head, o, out)
-    o_ref[...] = out.astype(o_ref.dtype)
-
-
-def attn_bwd_kernel(q_ref, k_ref, v_ref, g_ref, dq_ref, dk_ref, dv_ref, *, images):
-    R = q_ref.shape[0]
-    q = q_ref[...]
-    k = k_ref[...]
-    v = v_ref[...]
-    g = g_ref[...]
-    same = _same_image(R, images)
+    for i in range(images):
+        rows = pl.ds(i * slot, slot)
+        q = q_ref[rows, :]
+        k = k_ref[rows, :]
+        v = v_ref[rows, :]
+        out = jnp.zeros((slot, 2 * HD), jnp.float32)
+        for j in range(2):
+            in_head = (lane >= HD) == (j == 1)
+            p = _softmax_masked(jnp.where(in_head, q, jnp.zeros_like(q)), k, valid)
+            o = jnp.dot(p.astype(jnp.bfloat16), v, preferred_element_type=jnp.float32)
+            out = jnp.where(in_head, o, out)
+        o_ref[rows, :] = out.astype(o_ref.dtype)
+
+
+def attn_bwd_kernel(q_ref, k_ref, v_ref, g_ref, dq_ref, dk_ref, dv_ref, *, images, slot):
+    valid = lax.broadcasted_iota(jnp.int32, (slot, slot), 1) < SEQ
     lane = lax.broadcasted_iota(jnp.int32, (1, 2 * HD), 1)
-    dq = jnp.zeros((R, 2 * HD), jnp.float32)
-    dk = jnp.zeros((R, 2 * HD), jnp.float32)
-    dv = jnp.zeros((R, 2 * HD), jnp.float32)
-    for j in range(2):
-        in_head = (lane >= HD) == (j == 1)
-        p = _softmax_masked(jnp.where(in_head, q, jnp.zeros_like(q)), k, same)
-        gj = jnp.where(in_head, g, jnp.zeros_like(g))
-        dp = lax.dot_general(gj, v, COL_CONTRACT, preferred_element_type=jnp.float32)
-        ds = (p * (dp - jnp.sum(p * dp, axis=1, keepdims=True))).astype(jnp.bfloat16)
-        dq_j = jnp.dot(ds, k, preferred_element_type=jnp.float32) * (HD ** -0.5)
-        dk_j = lax.dot_general(ds, q, ROW_CONTRACT, preferred_element_type=jnp.float32) * (HD ** -0.5)
-        dv_j = lax.dot_general(p.astype(jnp.bfloat16), g, ROW_CONTRACT, preferred_element_type=jnp.float32)
-        dq = jnp.where(in_head, dq_j, dq)
-        dk = jnp.where(in_head, dk_j, dk)
-        dv = jnp.where(in_head, dv_j, dv)
-    dq_ref[...] = dq.astype(dq_ref.dtype)
-    dk_ref[...] = dk.astype(dk_ref.dtype)
-    dv_ref[...] = dv.astype(dv_ref.dtype)
-
-
-def attention_fwd(projected, images):
+    for i in range(images):
+        rows = pl.ds(i * slot, slot)
+        q = q_ref[rows, :]
+        k = k_ref[rows, :]
+        v = v_ref[rows, :]
+        g = g_ref[rows, :]
+        dq = jnp.zeros((slot, 2 * HD), jnp.float32)
+        dk = jnp.zeros((slot, 2 * HD), jnp.float32)
+        dv = jnp.zeros((slot, 2 * HD), jnp.float32)
+        for j in range(2):
+            in_head = (lane >= HD) == (j == 1)
+            p = _softmax_masked(jnp.where(in_head, q, jnp.zeros_like(q)), k, valid)
+            gj = jnp.where(in_head, g, jnp.zeros_like(g))
+            dp = lax.dot_general(gj, v, COL_CONTRACT, preferred_element_type=jnp.float32)
+            ds = (p * (dp - jnp.sum(p * dp, axis=1, keepdims=True))).astype(jnp.bfloat16)
+            dq_j = jnp.dot(ds, k, preferred_element_type=jnp.float32) * (HD ** -0.5)
+            dk_j = lax.dot_general(ds, q, ROW_CONTRACT, preferred_element_type=jnp.float32) * (HD ** -0.5)
+            dv_j = lax.dot_general(
+                p.astype(jnp.bfloat16), g, ROW_CONTRACT, preferred_element_type=jnp.float32
+            )
+            dq = jnp.where(in_head, dq_j, dq)
+            dk = jnp.where(in_head, dk_j, dk)
+            dv = jnp.where(in_head, dv_j, dv)
+        dq_ref[rows, :] = dq.astype(dq_ref.dtype)
+        dk_ref[rows, :] = dk.astype(dk_ref.dtype)
+        dv_ref[rows, :] = dv.astype(dv_ref.dtype)
+
+
+def attention_fwd(projected, images, slot):
     R = projected.shape[0]
     W = projected.shape[1] // 3
     pairs = W // (2 * HD)
     blk = lambda off: pl.BlockSpec((R, 2 * HD), lambda h: (0, off + h))
     return pl.pallas_call(
-        functools.partial(attn_fwd_kernel, images=images),
+        functools.partial(attn_fwd_kernel, images=images, slot=slot),
         grid=(pairs,),
         in_specs=[blk(0), blk(pairs), blk(2 * pairs)],
         out_specs=blk(0),
@@ -97,20 +88,31 @@
     )(projected, projected, projected)
 
 
-def attention_bwd(projected, mixed_grad, images):
+def attention_bwd(projected, mixed_grad, images, slot):
     R = projected.shape[0]
     W = projected.shape[1] // 3
     pairs = W // (2 * HD)
     blk = lambda off: pl.BlockSpec((R, 2 * HD), lambda h: (0, off + h))
     out = jax.ShapeDtypeStruct((R, W), jnp.bfloat16)
     return pl.pallas_call(
-        functools.partial(attn_bwd_kernel, images=images),
+        functools.partial(attn_bwd_kernel, images=images, slot=slot),
         grid=(pairs,),
         in_specs=[blk(0), blk(pairs), blk(2 * pairs), blk(0)],
         out_specs=[blk(0), blk(0), blk(0)],
         out_shape=[out, out, out],
         compiler_params=pltpu.CompilerParams(vmem_limit_bytes=48 * 1024 * 1024),
     )(projected, projected, projected, mixed_grad)
+
+
+def to_slots(values, images, slot):
+    cols = values.shape[1]
+    spaced = jnp.pad(values.reshape(images, SEQ, cols), ((0, 0), (0, slot - SEQ), (0, 0)))
+    return spaced.reshape(images * slot, cols)
+
+
+def from_slots(values, images, slot):
+    cols = values.shape[1]
+    return values.reshape(images, slot, cols)[:, :SEQ].reshape(images * SEQ, cols)
 
 
 def _exchange(values, bits_left, bit, axis_name, size, index):
@@ -205,9 +207,9 @@
     token_f = tokens.astype(jnp.float32)
     attn_in = lax.optimization_barrier(layer_norm(token_f, gain_one).astype(jnp.bfloat16))
     projected = jnp.dot(attn_in, full_qkv, preferred_element_type=jnp.float32).astype(jnp.bfloat16)
-    pad_rows = -(-rows // 128) * 128
-    projected_pad = jnp.pad(projected, ((0, pad_rows - rows), (0, 0)))
-    mixed_rows = attention_fwd(projected_pad, images)[:rows]
+    slot = -(-SEQ // 16) * 16
+    projected_pad = to_slots(projected, images, slot)
+    mixed_rows = from_slots(attention_fwd(projected_pad, images, slot), images, slot)
     hidden_state = token_f + jnp.dot(mixed_rows, full_out, preferred_element_type=jnp.float32)
     moe_in = layer_norm(hidden_state, gain_two).astype(jnp.bfloat16)
     logits = jnp.dot(moe_in, full_router, preferred_element_type=jnp.float32)
@@ -344,15 +346,18 @@
     mixed_grad = lax.dot_general(
         branch_grad, full_out, COL_CONTRACT, preferred_element_type=jnp.float32
     )
-    mixed_grad = jnp.pad(mixed_grad.astype(jnp.bfloat16), ((0, pad_rows - rows), (0, 0)))
-    grad_q, grad_k, grad_v = attention_bwd(projected_pad, mixed_grad, images)
+    mixed_grad = to_slots(mixed_grad.astype(jnp.bfloat16), images, slot)
+    grad_q, grad_k, grad_v = attention_bwd(projected_pad, mixed_grad, images, slot)
     projected_grad = jnp.concatenate([grad_q, grad_k, grad_v], axis=1)
-    attn_in_pad = jnp.pad(attn_in, ((0, pad_rows - rows), (0, 0)))
+    attn_in_pad = to_slots(attn_in, images, slot)
     grad_qkv = lax.dot_general(
         attn_in_pad, projected_grad, ROW_CONTRACT, preferred_element_type=jnp.float32
     )
     attn_in_grad = lax.dot_general(
-        projected_grad[:rows], full_qkv, COL_CONTRACT, preferred_element_type=jnp.float32
+        from_slots(projected_grad, images, slot),
+        full_qkv,
+        COL_CONTRACT,
+        preferred_element_type=jnp.float32,
     )
     _, first_back = jax.vjp(layer_norm, token_f, gain_one)
     token_part, grad_gain_one = first_back(attn_in_grad)

time: 579 us -> 596 us (1.029)
  local copies, waits for them, and re-layouts: 53.1 us -> 70.1 us
  matrix products: 177 us -> 185 us
    reshape x1 -> x6, local copies, waits for them, and re-layouts: 0.02 us -> 10.1 us  [the longest x3 5.92 us: to_slots(): values.reshape(images, SEQ, cols)]
  transfers between devices with their start and end apart: 13 -> 13, of which waited for: 11 -> 11; matrix products, arithmetic and copies ran while one was open for 38% -> 38% of each run, Pallas kernels for 2% -> 1%
where the time goes in v8:
time: 596 us; the launch traced here: 589 us
  waiting for transfers between devices  227 us (38%)
  matrix products  185 us (31%)
  local copies, waits for them, and re-layouts  70.1 us (12%)
  other arithmetic  35.8 us (6%)
  Pallas kernels  31 us (5%)
  starting transfers between devices  24.1 us (4%)
  between operations  15.9 us (3%)
    reduce_scatter x1, waiting for transfers between devices, shards(): lax.psum_scatter(expert_grads, 'shard', scatter_dimension=1, tiled=True)  72.9 us
    dot_general x2, matrix products, shards(): jnp.dot(flat_arrived, expert_first, preferred_element_type=jnp.float32)  52 us
    all_to_all x2, waiting for transfers between devices, shards(): lax.all_to_all(returning, 'expert', split_axis=0, concat_axis=0, tiled=True)  51.5 us
    all_gather x1, waiting for transfers between devices, shards(): dense_full = lax.all_gather(dense_local, 'shard', axis=0, tiled=True)  32.5 us
    all_to_all x2, waiting for transfers between devices, shards(): lax.all_to_all(outgoing[experts * start:experts * (start + size)].reshape...  28.5 us
    pallas_call x1, Pallas kernels, attention_bwd(): pl.pallas_call(functools.partial(attn_bwd_kernel, images=images, slot=slo...  22.5 us
    dot_general x2, matrix products, shards(): lax.dot_general(activated, flat_grad, ROW_CONTRACT, preferred_element_typ...  21.9 us
    ppermute x5, waiting for transfers between devices, _exchange(): got = lax.ppermute(send.astype(jnp.bfloat16), axis_name, pairs)  21.6 us
  transfers between devices with their start and end apart: 13, of which 11 were waited for; matrix products, arithmetic and copies ran while one was open for 38% of the time, Pallas kernels for 1%

profile of v8, /device:TPU:0, one launch (start us, length us, event | category | flops | bytes accessed | tf_op | source)
XLA Modules:
  0.0 588.9 jit_solution(1731720707939283655)
XLA Ops:
  9.7 1.9 concatenate.35
  13.2 2.2 pad_maximum_fusion.7
  21.6 32.5 %all-gather.3.cloned.1.call-done = bf16[768,3078]{1,0:T(8,128)(2,1)} async-done(((bf16[96,3078]{1,0:T(8,128)(2,1)}), bf16[768,3078]{1,0:T(8,128)(2,1)}) %all-gather.3.cloned.1.call-update) | async-done | bytes 4727824 | tf_op jit(solution)/shard_map/all_gather | solution.py:192
  56.8 5.8 convolution_convert_fusion
  62.6 4.3 reshape.274
  66.9 2.0 pad.18
  68.9 8.6 %shard_map.178 = bf16[624,768]{1,0:T(8,128)(2,1)S(1)} custom-call(bf16[624,2304]{1,0:T(8,128)(2,1)S(1)} %bitcast.103, bf16[624,2304]{1,0:T(8,128)(2,1)S(1)} %bitcast.104, bf16[624,2304]{1,0:T(8,128)(2,1)S(1)} %bitcast.105), custom_call_target="tpu_custom_call" | custom-call | tf_op jit(solution)/shard_map/pallas_call | solution.py:81
  77.8 2.6 fusion.114
  85.0 2.1 fusion.28
  87.1 2.2 convolution_convert_fusion.1
  89.3 2.5 add_convert_fusion.2
  93.2 1.5 pad_maximum_fusion.5
  94.7 4.6 all-to-all-start.2
  99.3 2.8 fusion.49
  102.1 13.2 %all-gather.5.cloned.1.call-done = bf16[2,768,3072]{2,1,0:T(8,128)(2,1)} async-done(((bf16[2,96,3072]{2,1,0:T(8,128)(2,1)}), bf16[2,768,3072]{2,1,0:T(8,128)(2,1)}) %all-gather.5.cloned.1.call-update) | async-done | bytes 9437200 | tf_op jit(solution)/shard_map/all_gather | solution.py:203
  115.3 4.9 slice.167
  120.2 8.5 %reshape_squeeze.3 = bf16[3072,768]{1,0:T(8,128)(2,1)} reshape(bf16[1,768,3072]{2,1,0:T(8,128)(2,1)} %slice.167) | data formatting | bytes 9437184 | tf_op jit(solution)/shard_map/reshape;squeeze | solution.py:205
  128.7 23.0 %all-to-all-done.2 = bf16[4,184,1536]{2,1,0:T(8,128)(2,1)} async-done(((bf16[4,184,1536]{2,1,0:T(8,128)(2,1)}), bf16[4,184,1536]{2,1,0:T(8,128)(2,1)}, u32[]{:S(2)}, u32[]{:S(2)}) %all-to-all-start.2) | async-done | bytes 2261024 | tf_op jit(solution)/shard_map/all_to_all | solution.py:261
  151.7 3.8 all-to-all-start
  155.5 25.8 %multiply_convert_fusion.1 = (bf16[736,3072]{1,0:T(8,128)(2,1)S(1)}, f32[736,3072]{1,0:T(8,128)}, f32[736,3072]{1,0:T(8,128)}) fusion(bf16[2,768,3072]{2,1,0:T(8,128)(2,1)} %all-gather.5.cloned.1.call-done, bf16[736,1536]{1,0:T(8,128)(2,1)} %bitcast.14), kind=kOutput, calls=%fused_computation.38 | convolution fusion | flops 3619848192 | bytes 28459008 | tf_op jit(solution)/shard_map/dot_general | solution.py:275
  181.3 3.7 convolution_convert_fusion.3
  185.0 10.8 %fusion.19 = bf16[736,3072]{1,0:T(8,128)(2,1)} fusion(f32[736,3072]{1,0:T(8,128)} %get-tuple-element.105, f32[736,3072]{1,0:T(8,128)} %get-tuple-element.97, bf16[3072,768]{1,0:T(8,128)(2,1)S(1)} %copy-done.16, bf16[736,1536]{1,0:T(8,128)(2,1)} %bitcast.14), kind=kOutput, calls=%fused_computation.37 | convolution fusion | flops 3490971648 | bytes 28459008 | tf_op jit(solution)/shard_map/dot_general | solution.py:272
  195.8 6.1 %fusion.72 = bf16[736,768]{1,0:T(8,128)(2,1)S(1)} fusion(bf16[736,3072]{1,0:T(8,128)(2,1)} %fusion.19, bf16[2,768,3072]{2,1,0:T(8,128)(2,1)S(1)} %bitcast.125), kind=kOutput, calls=%fused_computation.128 | convolution fusion | flops 3473448960 | bytes 10371072 | tf_op jit(solution)/shard_map/dot_general | solution.py:282
  201.9 1.6 pad_maximum_fusion.6
  203.5 5.5 all-to-all-done
  208.9 4.9 all-to-all-start.3
  213.8 26.2 %multiply_convert_fusion = (bf16[768,3072]{1,0:T(8,128)(2,1)S(1)}, f32[768,3072]{1,0:T(8,128)}, f32[768,3072]{1,0:T(8,128)}) fusion(bf16[2,768,3072]{2,1,0:T(8,128)(2,1)} %all-gather.5.cloned.1.call-done, bf16[768,1536]{1,0:T(8,128)(2,1)S(1)} %bitcast.117), kind=kOutput, calls=%fused_computation.16 | convolution fusion | flops 3777232896 | bytes 29491200 | tf_op jit(solution)/shard_map/dot_general | solution.py:275
  240.1 8.1 %convolution_convert_fusion.2 = bf16[768,768]{0,1:T(8,128)(2,1)S(1)} fusion(bf16[768,3072]{1,0:T(8,128)(2,1)S(1)} %get-tuple-element.94, bf16[3072,768]{1,0:T(8,128)(2,1)} %reshape_squeeze.3), kind=kOutput, calls=%fused_computation.127 | convolution fusion | flops 3624468480 | bytes 10616832 | tf_op jit(solution)/shard_map/dot_general | solution.py:279
  248.2 10.1 %fusion.6 = bf16[768,3072]{1,0:T(8,128)(2,1)S(1)} fusion(f32[768,3072]{1,0:T(8,128)} %get-tuple-element.106, f32[768,3072]{1,0:T(8,128)} %get-tuple-element.95, bf16[3072,768]{1,0:T(8,128)(2,1)} %reshape_squeeze.3, bf16[768,1536]{1,0:T(8,128)(2,1)S(1)} %bitcast.118), kind=kOutput, calls=%fused_computation.12 | convolution fusion | flops 3642753024 | bytes 29491200 | tf_op jit(solution)/shard_map/dot_general | solution.py:272
  258.3 8.0 %fusion.71 = bf16[768,768]{0,1:T(8,128)(2,1)S(1)} fusion(bf16[768,3072]{1,0:T(8,128)(2,1)S(1)} %fusion.6, bf16[2,768,3072]{2,1,0:T(8,128)(2,1)} %all-gather.5.cloned.1.call-done), kind=kOutput, calls=%fused_computation.126 | convolution fusion | flops 3624468480 | bytes 10616832 | tf_op jit(solution)/shard_map/dot_general | solution.py:282
  266.5 2.5 copy.112
  269.0 5.2 all-to-all-start.1
  275.7 51.5 %all-to-all-done.1 = bf16[4,192,1536]{2,1,0:T(8,128)(2,1)} async-done(((bf16[4,192,1536]{2,1,0:T(8,128)(2,1)}), bf16[4,192,1536]{2,1,0:T(8,128)(2,1)}, u32[]{:S(2)}, u32[]{:S(2)}) %all-to-all-start.1) | async-done | bytes 2359328 | tf_op jit(solution)/shard_map/all_to_all | solution.py:297
  327.2 5.6 fusion.30
  332.8 5.8 fusion.26
  338.7 1.9 multiply_reduce_fusion.3
  341.1 2.1 multiply_reduce_fusion
  344.4 2.6 fusion.117
  347.0 3.1 convolution_convert_fusion.4
  351.5 22.5 %shard_map.179 = (bf16[624,768]{1,0:T(8,128)(2,1)S(1)}, bf16[624,768]{1,0:T(8,128)(2,1)S(1)}, bf16[624,768]{1,0:T(8,128)(2,1)S(1)}) custom-call(bf16[624,2304]{1,0:T(8,128)(2,1)} %bitcast.106, bf16[624,2304]{1,0:T(8,128)(2,1)} %bitcast.107, bf16[624,2304]{1,0:T(8,128)(2,1)} %bitcast.108, bf16[624,768]{1,0:T(8,128)(2,1)S(1)} %bitcast.109), custom_call_target="tpu_custom_call" | custom-call | tf_op jit(solution)/shard_map/pallas_call | solution.py:97
  374.2 1.6 copy-done.6
  375.9 1.7 slice.176
  377.6 4.0 reshape.292
  381.6 5.2 fusion.68
  389.2 5.2 fusion.116
  395.6 3.8 copy-done.3
  399.3 1.7 fusion.48
  401.0 10.4 %fusion.74 = f32[3072,768]{1,0:T(8,128)} fusion(bf16[768,3072]{1,0:T(8,128)(2,1)} %copy-done.57, bf16[768,1536]{1,0:T(8,128)(2,1)} %bitcast.119), kind=kOutput, calls=%fused_computation.137 | convolution fusion | flops 3623878656 | bytes 15335424 | tf_op jit(solution)/shard_map/dot_general | solution.py:285
  411.4 11.6 %add_convert_fusion = bf16[3072,768]{1,0:T(8,128)(2,1)} fusion(f32[3072,768]{1,0:T(8,128)} %fusion.74, bf16[736,3072]{1,0:T(8,128)(2,1)} %copy-done.58, bf16[736,1536]{1,0:T(8,128)(2,1)} %bitcast.14), kind=kOutput, calls=%fused_computation.14 | convolution fusion | flops 3477602304 | bytes 19808256 | tf_op jit(solution)/shard_map/dot_general | solution.py:285
  423.0 2.1 bitcast_add_fusion
  427.0 6.4 %fusion.77 = f32[768,3072]{1,0:T(8,128)} fusion(bf16[768,3072]{1,0:T(8,128)(2,1)S(1)} %bitcast.122, bf16[768,1536]{1,0:T(8,128)(2,1)S(1)} %bitcast.120), kind=kOutput, calls=%fused_computation.140 | convolution fusion | flops 3623878656 | bytes 15335424 | tf_op jit(solution)/shard_map/dot_general | solution.py:288
  434.7 6.6 %collective-permute-done.1 = bf16[2,96,1536]{2,1,0:T(8,128)(2,1)S(1)} collective-permute-done((bf16[2,96,1536]{2,1,0:T(8,128)(2,1)S(1)}, bf16[2,96,1536]{2,1,0:T(8,128)(2,1)S(1)}, u32[]{:S(2)}, u32[]{:S(2)}) %collective-permute-start.1) | collective-permute-done | bytes 589856 | tf_op jit(solution)/shard_map/ppermute | solution.py:124
  442.8 8.1 %collective-permute-done.3 = bf16[2,96,1664]{2,1,0:T(8,128)(2,1)S(1)} collective-permute-done((bf16[2,96,1664]{2,1,0:T(8,128)(2,1)S(1)}, bf16[2,96,1664]{2,1,0:T(8,128)(2,1)S(1)}, u32[]{:S(2)}, u32[]{:S(2)}) %collective-permute-start.3) | collective-permute-done | bytes 639008 | tf_op jit(solution)/shard_map/ppermute | solution.py:124
  452.3 4.2 collective-permute-done.2
  456.6 2.7 collective-permute-done.4
  460.5 11.6 %fusion.34 = bf16[1,768,3072]{2,1,0:T(8,128)(2,1)} fusion(f32[768,3072]{1,0:T(8,128)} %fusion.77, bf16[736,3072]{1,0:T(8,128)(2,1)} %fusion.19, bf16[736,1536]{1,0:T(8,128)(2,1)} %bitcast.14), kind=kOutput, calls=%fused_computation.71 | convolution fusion | flops 3477602304 | bytes 19808256 | tf_op jit(solution)/shard_map/dot_general | solution.py:288
  472.1 8.5 %stack_reshape.4 = bf16[1,768,3072]{2,1,0:T(8,128)(2,1)} reshape(bf16[3072,768]{1,0:T(8,128)(2,1)} %add_convert_fusion) | data formatting | bytes 9437184 | tf_op jit(solution)/shard_map/stack;reshape | solution.py:300
  480.6 8.3 %pad_maximum_fusion = bf16[2,768,3072]{2,1,0:T(8,128)(2,1)} fusion(bf16[1,768,3072]{2,1,0:T(8,128)(2,1)} %stack_reshape.4, bf16[1,768,3072]{2,1,0:T(8,128)(2,1)} %fusion.34), kind=kLoop, calls=%fused_computation.13 | loop fusion | flops 4718592 | bytes 18874368 | tf_op jit(solution)/shard_map/stack | solution.py:300
  488.9 3.1 add_convert_fusion.3
  492.1 6.5 %all-reduce.7.cloned.1.call-done = bf16[96,3200]{1,0:T(8,128)(2,1)} async-done(((bf16[96,3200]{1,0:T(8,128)(2,1)}), bf16[96,3200]{1,0:T(8,128)(2,1)}) %all-reduce.7.cloned.1.call-update) | async-done | bytes 614416 | tf_op jit(solution)/shard_map/psum | solution.py:372
  499.9 2.0 slice.179
  501.9 1.6 slice.180
  505.4 72.9 %reduce-scatter.2.cloned.1.call-done = bf16[2,96,3072]{2,1,0:T(8,128)(2,1)} async-done(((bf16[2,768,3072]{2,1,0:T(8,128)(2,1)}), bf16[2,96,3072]{2,1,0:T(8,128)(2,1)}) %reduce-scatter.2.cloned.1.call-update) | async-done | bytes 1179664 | tf_op jit(solution)/shard_map/reduce_scatter | solution.py:303
  578.3 2.5 fusion.113
  (243 shorter events, 38.3 us)
Async XLA Ops:
  7.2 9.3 %copy-start.33 = (s32[591,2]{0,1:T(2,128)S(1)}, s32[591,2]{0,1:T(2,128)}, u32[]{:S(2)}) copy-start(s32[591,2]{0,1:T(2,128)} %param.13) | copy-start | bytes 14188
  7.2 46.9 %all-gather.3.cloned.1.call-start = ((), (), s32[]{:S(2)}) async-start(), calls=%async_computation.5 | async-start | bytes 5529600 | tf_op jit(solution)/shard_map/all_gather | solution.py:192
  8.0 11.4 %copy-start.4 = (bf16[591,768]{1,0:T(8,128)(2,1)S(1)}, bf16[591,768]{1,0:T(8,128)(2,1)}, u32[]{:S(2)}) copy-start(bf16[591,768]{1,0:T(8,128)(2,1)} %param.11) | copy-start | bytes 2723332
  11.6 8.5 %copy-start.7 = (bf16[591,768]{1,0:T(8,128)(2,1)S(1)}, bf16[591,768]{1,0:T(8,128)(2,1)}, u32[]{:S(2)}) copy-start(bf16[591,768]{1,0:T(8,128)(2,1)} %param.21) | copy-start | bytes 2723332
  11.7 103.7 %all-gather.5.cloned.1.call-start = ((), (), s32[]{:S(2)}) async-start(), calls=%async_computation.6 | async-start | bytes 10616832 | tf_op jit(solution)/shard_map/all_gather | solution.py:203
  19.3 64.8 %copy-start.23 = (f32[591]{0:T(1024)}, f32[591]{0:T(1024)S(1)}, u32[]{:S(2)}) copy-start(f32[591]{0:T(1024)S(1)} %fusion.106) | copy-start | bytes 7096
  19.4 69.9 %copy-start.51 = (s32[1504]{0:T(1024)}, s32[1504]{0:T(1024)S(1)}, u32[]{:S(2)}) copy-start(s32[1504]{0:T(1024)S(1)} %pad_add_fusion) | copy-start | bytes 18052
  19.4 67.6 %copy-start.53 = (s32[591]{0:T(1024)}, s32[591]{0:T(1024)S(1)}, u32[]{:S(2)}) copy-start(s32[591]{0:T(1024)S(1)} %get-tuple-element.91) | copy-start | bytes 7096
  19.4 69.8 %copy-start.55 = (s32[591]{0:T(1024)}, s32[591]{0:T(1024)S(1)}, u32[]{:S(2)}) copy-start(s32[591]{0:T(1024)S(1)} %get-tuple-element.90) | copy-start | bytes 7096
  19.7 42.9 %copy-start.31 = (f32[591]{0:T(1024)}, f32[591]{0:T(1024)S(1)}, u32[]{:S(2)}) copy-start(f32[591]{0:T(1024)S(1)} %broadcast_multiply_fusion.2) | copy-start | bytes 7096
  20.1 42.5 %copy-start.47 = (f32[591]{0:T(1024)}, f32[591]{0:T(1024)S(1)}, u32[]{:S(2)}) copy-start(f32[591]{0:T(1024)S(1)} %fusion.67) | copy-start | bytes 7096
  20.1 42.5 %copy-start.43 = (f32[591]{0:T(1024)}, f32[591]{0:T(1024)S(1)}, u32[]{:S(2)}) copy-start(f32[591]{0:T(1024)S(1)} %fusion.104) | copy-start | bytes 7096
  55.5 7.1 %copy-start.41 = (f32[768]{0:T(1024)}, f32[768]{0:T(1024)S(1)}, u32[]{:S(2)}) copy-start(f32[768]{0:T(1024)S(1)} %get-tuple-element.79) | copy-start | bytes 9220
  55.5 26.1 %copy-start.35 = (f32[768]{0:T(1024)}, f32[768]{0:T(1024)S(1)}, u32[]{:S(2)}) copy-start(f32[768]{0:T(1024)S(1)} %get-tuple-element.78) | copy-start | bytes 9220
  68.9 8.6 %copy-start = (bf16[3,208,2304]{2,1,0:T(8,128)(2,1)}, bf16[3,208,2304]{2,1,0:T(8,128)(2,1)S(1)}, u32[]{:S(2)}) copy-start(bf16[3,208,2304]{2,1,0:T(8,128)(2,1)S(1)} %pad.18) | copy-start | bytes 8626180
  77.8 4.7 copy-start.21
  77.8 6.9 %copy-start.13 = (f32[591,768]{1,0:T(8,128)S(1)}, f32[591,768]{1,0:T(8,128)}, u32[]{:S(2)}) copy-start(f32[591,768]{1,0:T(8,128)} %convert_multiply_fusion) | copy-start | bytes 5446660
  80.4 3.7 copy-start.27
  82.5 4.6 copy-start.10
  84.7 2.4 copy-start.45
  94.7 56.9 %all-to-all-start.2 = ((bf16[4,184,1536]{2,1,0:T(8,128)(2,1)}), bf16[4,184,1536]{2,1,0:T(8,128)(2,1)}, u32[]{:S(2)}, u32[]{:S(2)}) async-start(bf16[4,184,1536]{2,1,0:T(8,128)(2,1)} %bitcast.116), calls=%async_computation.2 | async-start | bytes 4521984 | tf_op jit(solution)/shard_map/all_to_all | solution.py:261
  151.7 57.3 %all-to-all-start = ((bf16[4,192,1536]{2,1,0:T(8,128)(2,1)}), bf16[4,192,1536]{2,1,0:T(8,128)(2,1)S(1)}, u32[]{:S(2)}, u32[]{:S(2)}) async-start(bf16[4,192,1536]{2,1,0:T(8,128)(2,1)} %bitcast.8), calls=%async_computation | async-start | bytes 4718592 | tf_op jit(solution)/shard_map/all_to_all | solution.py:261
  155.5 25.8 %copy-start.16 = (bf16[3072,768]{1,0:T(8,128)(2,1)S(1)}, bf16[3072,768]{1,0:T(8,128)(2,1)}, u32[]{:S(2)}) copy-start(bf16[3072,768]{1,0:T(8,128)(2,1)} %reshape_squeeze.3) | copy-start | bytes 14155780
  181.2 3.7 copy-start.58
  181.2 14.5 %slice-start.5 = ((s8[9437184]{0:T(1024)(128)(4,1)}), s8[4194304]{0:T(1024)(128)(4,1)S(1)}, s32[]{:S(2)}) async-start(s8[9437184]{0:T(1024)(128)(4,1)} %bitcast.124), calls=%async_computation.14 | async-start | bytes 8388608
  181.3 14.5 %slice-start.6 = ((s8[9437184]{0:T(1024)(128)(4,1)}), s8[4194304]{0:T(1024)(128)(4,1)S(1)}, s32[]{:S(2)}) async-start(s8[9437184]{0:T(1024)(128)(4,1)} %bitcast.124), calls=%async_computation.15 | async-start | bytes 8388608
  184.9 10.8 %slice-start.7 = ((s8[9437184]{0:T(1024)(128)(4,1)}), s8[1048576]{0:T(1024)(128)(4,1)S(1)}, s32[]{:S(2)}) async-start(s8[9437184]{0:T(1024)(128)(4,1)} %bitcast.124), calls=%async_computation.16 | async-start | bytes 2097152
  208.9 39.3 %copy-start.14 = (bf16[4,192,1536]{2,1,0:T(8,128)(2,1)}, bf16[4,192,1536]{2,1,0:T(8,128)(2,1)S(1)}, u32[]{:S(2)}) copy-start(bf16[4,192,1536]{2,1,0:T(8,128)(2,1)S(1)} %all-to-all-done) | copy-start | bytes 7077892
  208.9 60.1 %all-to-all-start.3 = ((bf16[4,184,1536]{2,1,0:T(8,128)(2,1)}), bf16[4,184,1536]{2,1,0:T(8,128)(2,1)}, u32[]{:S(2)}, u32[]{:S(2)}) async-start(bf16[4,184,1536]{2,1,0:T(8,128)(2,1)} %bitcast.15), calls=%async_computation.3 | async-start | bytes 4521984 | tf_op jit(solution)/shard_map/all_to_all | solution.py:297
  240.1 8.1 %copy-start.57 = (bf16[768,3072]{1,0:T(8,128)(2,1)}, bf16[768,3072]{1,0:T(8,128)(2,1)S(1)}, u32[]{:S(2)}) copy-start(bf16[768,3072]{1,0:T(8,128)(2,1)S(1)} %get-tuple-element.94) | copy-start | bytes 14155780
  258.3 8.0 %copy-start.17 = (bf16[768,3072]{1,0:T(8,128)(2,1)}, bf16[768,3072]{1,0:T(8,128)(2,1)S(1)}, u32[]{:S(2)}) copy-start(bf16[768,3072]{1,0:T(8,128)(2,1)S(1)} %fusion.6) | copy-start | bytes 14155780
  266.5 7.9 %copy-start.19 = (bf16[591,768]{1,0:T(8,128)(2,1)S(1)}, bf16[591,768]{1,0:T(8,128)(2,1)}, u32[]{:S(2)}) copy-start(bf16[591,768]{1,0:T(8,128)(2,1)} %copy-done.18) | copy-start | bytes 2723332
  269.0 6.6 %copy-start.46 = (f32[591,2]{0,1:T(2,128)S(1)}, f32[591,2]{0,1:T(2,128)}, u32[]{:S(2)}) copy-start(f32[591,2]{0,1:T(2,128)} %copy-done.45) | copy-start | bytes 14188
  269.0 58.1 %copy-start.52 = (s32[1504]{0:T(1024)S(1)}, s32[1504]{0:T(1024)}, u32[]{:S(2)}) copy-start(s32[1504]{0:T(1024)} %copy-done.51) | copy-start | bytes 18052
  269.0 58.2 %copy-start.56 = (s32[591]{0:T(1024)S(1)}, s32[591]{0:T(1024)}, u32[]{:S(2)}) copy-start(s32[591]{0:T(1024)} %copy-done.55) | copy-start | bytes 7096
  269.0 58.1 %all-to-all-start.1 = ((bf16[4,192,1536]{2,1,0:T(8,128)(2,1)}), bf16[4,192,1536]{2,1,0:T(8,128)(2,1)}, u32[]{:S(2)}, u32[]{:S(2)}) async-start(bf16[4,192,1536]{2,1,0:T(8,128)(2,1)} %bitcast.11), calls=%async_computation.1 | async-start | bytes 4718592 | tf_op jit(solution)/shard_map/all_to_all | solution.py:297
  274.2 224.3 %all-reduce.7.cloned.1.call-start = ((), (), s32[]{:S(2)}) async-start(), calls=%async_computation.7 | async-start | bytes 1228800 | tf_op jit(solution)/shard_map/psum | solution.py:372
  327.2 5.6 copy-start.54
  332.8 5.9 copy-start.2
  332.8 5.9 copy-start.8
  332.8 5.9 copy-start.24
  338.6 2.2 copy-start.11
  338.7 2.4 copy-start.28
  338.7 2.4 copy-start.36
  338.7 2.4 copy-start.38
  340.6 2.5 copy-start.50
  375.9 5.7 copy-start.5
  375.9 5.7 copy-start.32
  375.9 5.7 copy-start.42
  381.6 5.3 copy-start.48
  381.6 6.5 %copy-start.44 = (f32[591]{0:T(1024)S(1)}, f32[591]{0:T(1024)}, u32[]{:S(2)}) copy-start(f32[591]{0:T(1024)} %copy-done.43) | copy-start | bytes 7096
  389.2 5.2 copy-start.20
  395.5 3.8 copy-start.3
  401.0 22.0 %collective-permute-start = (bf16[2,2,96,3200]{3,2,1,0:T(8,128)(2,1)}, bf16[2,2,96,3200]{3,2,1,0:T(8,128)(2,1)}, u32[]{:S(2)}, u32[]{:S(2)}) collective-permute-start(bf16[2,2,96,3200]{3,2,1,0:T(8,128)(2,1)} %fusion.48), channel_id=1, source_target_pairs={{0,1},{1,0},{2,3},{3,2},{4,5},{5,4},{6,7},{7,6},{8,9},{9,8},{10,11... | collective-permute-start | bytes 7372808 | tf_op jit(solution)/shard_map/ppermute | solution.py:124
  401.0 22.0 %slice-start = ((s8[9830400]{0:T(1024)(128)(4,1)}), s8[4194304]{0:T(1024)(128)(4,1)S(1)}, s32[]{:S(2)}) async-start(s8[9830400]{0:T(1024)(128)(4,1)} %bitcast.112), calls=%async_computation.9 | async-start | bytes 8388608
  401.0 22.0 %slice-start.1 = ((s8[9830400]{0:T(1024)(128)(4,1)}), s8[4194304]{0:T(1024)(128)(4,1)S(1)}, s32[]{:S(2)}) async-start(s8[9830400]{0:T(1024)(128)(4,1)} %bitcast.112), calls=%async_computation.10 | async-start | bytes 8388608
  401.0 26.0 %slice-start.3 = ((s8[4718592]{0:T(1024)(128)(4,1)}), s8[4194304]{0:T(1024)(128)(4,1)S(1)}, s32[]{:S(2)}) async-start(s8[4718592]{0:T(1024)(128)(4,1)} %bitcast.121), calls=%async_computation.12 | async-start | bytes 8388608
  411.4 11.6 %slice-start.2 = ((s8[9830400]{0:T(1024)(128)(4,1)}), s8[1441792]{0:T(1024)(128)(4,1)S(1)}, s32[]{:S(2)}) async-start(s8[9830400]{0:T(1024)(128)(4,1)} %bitcast.112), calls=%async_computation.11 | async-start | bytes 2883584
  411.4 15.6 %slice-start.4 = ((s8[4718592]{0:T(1024)(128)(4,1)}), s8[524288]{0:T(1024)(128)(4,1)S(1)}, s32[]{:S(2)}) async-start(s8[4718592]{0:T(1024)(128)(4,1)} %bitcast.121), calls=%async_computation.13 | async-start | bytes 1048576
  425.5 15.8 %collective-permute-start.1 = (bf16[2,96,1536]{2,1,0:T(8,128)(2,1)S(1)}, bf16[2,96,1536]{2,1,0:T(8,128)(2,1)S(1)}, u32[]{:S(2)}, u32[]{:S(2)}) collective-permute-start(bf16[2,96,1536]{2,1,0:T(8,128)(2,1)S(1)} %fusion.88), channel_id=1, source_target_pairs={{0,2},{1,3},{2,0},{3,1},{4,6},{5,7},{6,4},{7,5},{8,10},{9,11},{10,... | collective-permute-start | bytes 1769480 | tf_op jit(solution)/shard_map/ppermute | solution.py:124
  433.6 17.3 %collective-permute-start.3 = (bf16[2,96,1664]{2,1,0:T(8,128)(2,1)S(1)}, bf16[2,96,1664]{2,1,0:T(8,128)(2,1)S(1)}, u32[]{:S(2)}, u32[]{:S(2)}) collective-permute-start(bf16[2,96,1664]{2,1,0:T(8,128)(2,1)S(1)} %fusion.86), channel_id=1, source_target_pairs={{0,4},{1,5},{2,6},{3,7},{4,0},{5,1},{6,2},{7,3},{8,12},{9,13},{10,... | collective-permute-start | bytes 1916936 | tf_op jit(solution)/shard_map/ppermute | solution.py:124
  441.5 15.1 %collective-permute-start.2 = (bf16[96,1536]{1,0:T(8,128)(2,1)S(1)}, bf16[96,1536]{1,0:T(8,128)(2,1)S(1)}, u32[]{:S(2)}, u32[]{:S(2)}) collective-permute-start(bf16[96,1536]{1,0:T(8,128)(2,1)S(1)} %fusion.91), channel_id=1, source_target_pairs={{0,4},{1,5},{2,6},{3,7},{4,0},{5,1},{6,2},{7,3},{8,12},{9,13},{10,... | collective-permute-start | bytes 884744 | tf_op jit(solution)/shard_map/ppermute | solution.py:124
  451.1 8.2 %collective-permute-start.4 = (bf16[96,1664]{1,0:T(8,128)(2,1)S(1)}, bf16[96,1664]{1,0:T(8,128)(2,1)S(1)}, u32[]{:S(2)}, u32[]{:S(2)}) collective-permute-start(bf16[96,1664]{1,0:T(8,128)(2,1)S(1)} %fusion.90), channel_id=1, source_target_pairs={{0,2},{1,3},{2,0},{3,1},{4,6},{5,7},{6,4},{7,5},{8,10},{9,11},{10,... | collective-permute-start | bytes 958472 | tf_op jit(solution)/shard_map/ppermute | solution.py:124
  460.2 118.0 %reduce-scatter.2.cloned.1.call-start = ((), (), s32[]{:S(2)}) async-start(), calls=%async_computation.8 | async-start | bytes 10616832 | tf_op jit(solution)/shard_map/reduce_scatter | solution.py:303
  (16 other events, 21.0 us)
Sparse Core Ops, SparseCore 0:
  11.8 42.3 all-gather.2
  56.6 58.6 all-gather.4
  460.4 38.1 all-reduce.6
  501.9 76.3 reduce-scatter.1

commit v9 on v7

--- a/solution.py
+++ b/solution.py
@@ -243,21 +243,21 @@
     weighted = chosen * live_rows[:, None]
     grad_picked = (weighted[:, :, None] * grad_out[:, None, :]).astype(jnp.bfloat16)
 
-    sent_rows = jnp.dot(
-        take_first + take_second, moe_in, preferred_element_type=jnp.float32
-    ).astype(jnp.bfloat16)
-    sent_grad = (
-        jnp.dot(take_first, grad_picked[:, 0], preferred_element_type=jnp.float32)
-        + jnp.dot(take_second, grad_picked[:, 1], preferred_element_type=jnp.float32)
-    ).astype(jnp.bfloat16)
-    outgoing = jnp.concatenate([sent_rows, sent_grad], axis=1)
+    def dispatch_rows(low, high):
+        first = take_first[low:high]
+        second = take_second[low:high]
+        sent_rows = jnp.dot(first + second, moe_in, preferred_element_type=jnp.float32)
+        sent_grad = jnp.dot(
+            first, grad_picked[:, 0], preferred_element_type=jnp.float32
+        ) + jnp.dot(second, grad_picked[:, 1], preferred_element_type=jnp.float32)
+        return jnp.concatenate([sent_rows, sent_grad], axis=1).astype(jnp.bfloat16)
 
     grad_first = None
     grad_second = None
     returned_parts = []
     for start, size in zip(chunk_starts, chunk_sizes):
         arrived = lax.all_to_all(
-            outgoing[experts * start : experts * (start + size)].reshape(
+            dispatch_rows(experts * start, experts * (start + size)).reshape(
                 experts, size, 2 * width
             ),
             "expert",
@@ -303,15 +303,19 @@
     grad_in_share = expert_share[0][None]
     grad_back_share = expert_share[1].reshape(back_rows, width)[None]
 
-    returned = jnp.concatenate(
-        [part.reshape(-1, 2 * width) for part in returned_parts], axis=0
-    )
-    picked_first = lax.dot_general(
-        take_first, returned, ROW_CONTRACT, preferred_element_type=jnp.float32
-    )
-    picked_second = lax.dot_general(
-        take_second, returned, ROW_CONTRACT, preferred_element_type=jnp.float32
-    )
+    picked_first = None
+    picked_second = None
+    for start, size, part in zip(chunk_starts, chunk_sizes, returned_parts):
+        low, high = experts * start, experts * (start + size)
+        part = part.reshape(-1, 2 * width)
+        part_first = lax.dot_general(
+            take_first[low:high], part, ROW_CONTRACT, preferred_element_type=jnp.float32
+        )
+        part_second = lax.dot_general(
+            take_second[low:high], part, ROW_CONTRACT, preferred_element_type=jnp.float32
+        )
+        picked_first = part_first if picked_first is None else picked_first + part_first
+        picked_second = part_second if picked_second is None else picked_second + part_second
     moe_out = (
         weighted[:, 0:1] * picked_first[:, :width] + weighted[:, 1:2] * picked_second[:, :width]
     )

time: 579 us -> 575 us (level)
  waiting for transfers between devices: 227 us -> 209 us
  matrix products: 177 us -> 187 us
    dot_general x5 -> x10, matrix products: 16.9 us -> 28.8 us  [the longest x2 9.52 us: shards(): lax.dot_general(take_first[low:high], part, ROW_CONTRACT, preferred_eleme...]
    all_to_all x2, waiting for transfers between devices: 52.4 us -> 41.9 us  [shards(): lax.all_to_all(returning, 'expert', split_axis=0, concat_axis=0, tiled=True)]
  transfers between devices with their start and end apart: 13 -> 13, of which waited for: 11 -> 11; matrix products, arithmetic and copies ran while one was open for 38% -> 41% of each run, Pallas kernels for 2% -> 2%
where the time goes in v9:
time: 575 us; the launch traced here: 567 us
  waiting for transfers between devices  209 us (36%)
  matrix products  187 us (33%)
  local copies, waits for them, and re-layouts  54.1 us (9%)
  other arithmetic  41.5 us (7%)
  Pallas kernels  35.2 us (6%)
  starting transfers between devices  24.1 us (4%)
  between operations  16.2 us (3%)
    reduce_scatter x1, waiting for transfers between devices, shards(): lax.psum_scatter(expert_grads, 'shard', scatter_dimension=1, tiled=True)  72.9 us
    dot_general x2, matrix products, shards(): jnp.dot(flat_arrived, expert_first, preferred_element_type=jnp.float32)  52 us
    all_to_all x2, waiting for transfers between devices, shards(): lax.all_to_all(returning, 'expert', split_axis=0, concat_axis=0, tiled=True)  41.9 us
    all_gather x1, waiting for transfers between devices, shards(): dense_full = lax.all_gather(dense_local, 'shard', axis=0, tiled=True)  29.1 us
    all_to_all x2, waiting for transfers between devices, shards(): lax.all_to_all(dispatch_rows(experts * start, experts * (start + size)).r...  23 us
    pallas_call x1, Pallas kernels, attention_bwd(): pl.pallas_call(functools.partial(attn_bwd_kernel, images=images), grid=(p...  21.8 us
    ppermute x5, waiting for transfers between devices, _exchange(): got = lax.ppermute(send.astype(jnp.bfloat16), axis_name, pairs)  21.6 us
    dot_general x2, matrix products, shards(): lax.dot_general(flat_grad, expert_second, COL_CONTRACT, preferred_element...  20.9 us
  transfers between devices with their start and end apart: 13, of which 11 were waited for; matrix products, arithmetic and copies ran while one was open for 41% of the time, Pallas kernels for 2%

profile of v9, /device:TPU:0, one launch (start us, length us, event | category | flops | bytes accessed | tf_op | source)
XLA Modules:
  0.0 566.7 jit_solution(15984261466600103317)
XLA Ops:
  9.6 1.9 concatenate.47
  11.6 1.5 stack_reshape_squeeze.3
  13.2 2.3 pad_maximum_fusion.5
  21.6 3.3 fusion.105
  25.0 29.1 %all-gather.3.cloned.1.call-done = bf16[768,3078]{1,0:T(8,128)(2,1)} async-done(((bf16[96,3078]{1,0:T(8,128)(2,1)}), bf16[768,3078]{1,0:T(8,128)(2,1)}) %all-gather.3.cloned.1.call-update) | async-done | bytes 4727824 | tf_op jit(solution)/shard_map/all_gather | solution.py:190
  55.8 4.6 convolution_convert_fusion
  60.6 13.4 %shard_map.178 = bf16[640,768]{1,0:T(8,128)(2,1)S(1)} custom-call(bf16[640,2304]{1,0:T(8,128)(2,1)S(1)} %pad.18.q_ref.k_ref.v_ref, bf16[640,2304]{1,0:T(8,128)(2,1)S(1)} %pad.18.q_ref.k_ref.v_ref, bf16[640,2304]{1,0:T(8,128)(2,1)S(1)} %pad.18.q_ref.k_ref.v_ref), custom_call_target="tpu_custom_call" | custom-call | tf_op jit(solution)/shard_map/pallas_call | solution.py:90
  74.1 2.6 fusion.111
  80.7 2.7 fusion.60
  83.4 2.3 convolution_convert_fusion.4
  85.7 2.4 add_convert_fusion.3
  88.1 1.5 pad_maximum_fusion.3
  89.6 4.6 all-to-all-start.2
  94.2 2.7 fusion.53
  99.9 1.6 pad_maximum_fusion.1
  101.5 13.7 %all-gather.5.cloned.1.call-done = bf16[2,768,3072]{2,1,0:T(8,128)(2,1)} async-done(((bf16[2,96,3072]{2,1,0:T(8,128)(2,1)}), bf16[2,768,3072]{2,1,0:T(8,128)(2,1)}) %all-gather.5.cloned.1.call-update) | async-done | bytes 9437200 | tf_op jit(solution)/shard_map/all_gather | solution.py:201
  115.3 4.9 slice.195
  120.1 8.5 %reshape_squeeze.3 = bf16[3072,768]{1,0:T(8,128)(2,1)} reshape(bf16[1,768,3072]{2,1,0:T(8,128)(2,1)} %slice.195) | data formatting | bytes 9437184 | tf_op jit(solution)/shard_map/reshape;squeeze | solution.py:203
  128.6 17.7 %all-to-all-done.2 = bf16[4,184,1536]{2,1,0:T(8,128)(2,1)S(1)} async-done(((bf16[4,184,1536]{2,1,0:T(8,128)(2,1)}), bf16[4,184,1536]{2,1,0:T(8,128)(2,1)S(1)}, u32[]{:S(2)}, u32[]{:S(2)}) %all-to-all-start.2) | async-done | bytes 2261024 | tf_op jit(solution)/shard_map/all_to_all | solution.py:259
  147.7 3.8 all-to-all-start
  151.6 25.8 %multiply_convert_fusion.1 = (bf16[736,3072]{1,0:T(8,128)(2,1)S(1)}, f32[736,3072]{1,0:T(8,128)}, f32[736,3072]{1,0:T(8,128)}) fusion(bf16[2,768,3072]{2,1,0:T(8,128)(2,1)} %all-gather.5.cloned.1.call-done, bf16[736,1536]{1,0:T(8,128)(2,1)} %bitcast.117), kind=kOutput, calls=%fused_computation.38 | convolution fusion | flops 3619848192 | bytes 28459008 | tf_op jit(solution)/shard_map/dot_general | solution.py:273
  177.4 3.7 convolution_convert_fusion.3
  181.1 10.8 %fusion.19 = bf16[736,3072]{1,0:T(8,128)(2,1)} fusion(f32[736,3072]{1,0:T(8,128)} %get-tuple-element.111, f32[736,3072]{1,0:T(8,128)} %get-tuple-element.97, bf16[3072,768]{1,0:T(8,128)(2,1)S(1)} %copy-done.16, bf16[736,1536]{1,0:T(8,128)(2,1)} %bitcast.118), kind=kOutput, calls=%fused_computation.37 | convolution fusion | flops 3490971648 | bytes 28459008 | tf_op jit(solution)/shard_map/dot_general | solution.py:270
  191.9 6.1 %fusion.49 = bf16[736,768]{1,0:T(8,128)(2,1)S(1)} fusion(bf16[736,3072]{1,0:T(8,128)(2,1)} %fusion.19, bf16[2,768,3072]{2,1,0:T(8,128)(2,1)S(1)} %bitcast.114), kind=kOutput, calls=%fused_computation.109 | convolution fusion | flops 3473448960 | bytes 10371072 | tf_op jit(solution)/shard_map/dot_general | solution.py:280
  198.0 1.6 pad_maximum_fusion.4
  199.6 5.3 all-to-all-done
  204.9 4.9 all-to-all-start.3
  209.8 26.2 %multiply_convert_fusion = (bf16[768,3072]{1,0:T(8,128)(2,1)S(1)}, f32[768,3072]{1,0:T(8,128)}, f32[768,3072]{1,0:T(8,128)}) fusion(bf16[2,768,3072]{2,1,0:T(8,128)(2,1)} %all-gather.5.cloned.1.call-done, bf16[768,1536]{1,0:T(8,128)(2,1)S(1)} %bitcast.107), kind=kOutput, calls=%fused_computation.16 | convolution fusion | flops 3777232896 | bytes 29491200 | tf_op jit(solution)/shard_map/dot_general | solution.py:273
  236.0 8.1 %convolution_convert_fusion.1 = bf16[768,768]{0,1:T(8,128)(2,1)S(1)} fusion(bf16[768,3072]{1,0:T(8,128)(2,1)S(1)} %get-tuple-element.94, bf16[3072,768]{1,0:T(8,128)(2,1)} %reshape_squeeze.3), kind=kOutput, calls=%fused_computation.107 | convolution fusion | flops 3624468480 | bytes 10616832 | tf_op jit(solution)/shard_map/dot_general | solution.py:277
  244.2 10.1 %fusion.6 = bf16[768,3072]{1,0:T(8,128)(2,1)S(1)} fusion(f32[768,3072]{1,0:T(8,128)} %get-tuple-element.112, f32[768,3072]{1,0:T(8,128)} %get-tuple-element.95, bf16[3072,768]{1,0:T(8,128)(2,1)} %reshape_squeeze.3, bf16[768,1536]{1,0:T(8,128)(2,1)S(1)} %bitcast.108), kind=kOutput, calls=%fused_computation.12 | convolution fusion | flops 3642753024 | bytes 29491200 | tf_op jit(solution)/shard_map/dot_general | solution.py:270
  254.3 8.0 %fusion.48 = bf16[768,768]{0,1:T(8,128)(2,1)S(1)} fusion(bf16[768,3072]{1,0:T(8,128)(2,1)S(1)} %fusion.6, bf16[2,768,3072]{2,1,0:T(8,128)(2,1)} %all-gather.5.cloned.1.call-done), kind=kOutput, calls=%fused_computation.106 | convolution fusion | flops 3624468480 | bytes 10616832 | tf_op jit(solution)/shard_map/dot_general | solution.py:280
  262.5 2.5 copy.111
  264.9 5.1 all-to-all-start.1
  270.2 5.5 fusion.58
  275.7 5.2 fusion.55
  280.9 41.9 %all-to-all-done.1 = bf16[4,192,1536]{2,1,0:T(8,128)(2,1)S(1)} async-done(((bf16[4,192,1536]{2,1,0:T(8,128)(2,1)}), bf16[4,192,1536]{2,1,0:T(8,128)(2,1)S(1)}, u32[]{:S(2)}, u32[]{:S(2)}) %all-to-all-start.1) | async-done | bytes 2359328 | tf_op jit(solution)/shard_map/all_to_all | solution.py:295
  322.8 4.0 convolution_add_fusion.1
  326.9 1.8 convolution_add_fusion
  328.9 1.8 multiply_reduce_fusion.3
  333.3 2.5 fusion.79
  336.8 21.8 %shard_map.179 = (bf16[640,768]{1,0:T(8,128)(2,1)S(1)}, bf16[640,768]{1,0:T(8,128)(2,1)S(1)}, bf16[640,768]{1,0:T(8,128)(2,1)S(1)}) custom-call(bf16[640,2304]{1,0:T(8,128)(2,1)} %copy-done, bf16[640,2304]{1,0:T(8,128)(2,1)} %copy-done, bf16[640,2304]{1,0:T(8,128)(2,1)} %copy-done, bf16[640,768]{1,0:T(8,128)(2,1)S(1)} %pad.20.g_ref), custom_call_target="tpu_custom_call" | custom-call | tf_op jit(solution)/shard_map/pallas_call | solution.py:106
  359.9 5.0 fusion.76
  364.9 2.4 fusion.45
  369.8 4.7 select_maximum_fusion
  374.5 3.8 copy-done.5
  378.3 1.7 fusion.39
  379.9 10.4 %fusion.63 = f32[3072,768]{1,0:T(8,128)} fusion(bf16[768,3072]{1,0:T(8,128)(2,1)} %copy-done.58, bf16[768,1536]{1,0:T(8,128)(2,1)} %bitcast.109), kind=kOutput, calls=%fused_computation.131 | convolution fusion | flops 3623878656 | bytes 15335424 | tf_op jit(solution)/shard_map/dot_general | solution.py:283
  390.3 10.1 %add_convert_fusion = bf16[3072,768]{1,0:T(8,128)(2,1)} fusion(f32[3072,768]{1,0:T(8,128)} %fusion.63, bf16[736,3072]{1,0:T(8,128)(2,1)} %copy-done.59, bf16[736,1536]{1,0:T(8,128)(2,1)S(1)} %bitcast.120), kind=kOutput, calls=%fused_computation.14 | convolution fusion | flops 3477602304 | bytes 19808256 | tf_op jit(solution)/shard_map/dot_general | solution.py:283
  400.5 2.1 bitcast_add_fusion
  403.0 1.5 collective-permute-start.1
  404.6 6.4 %fusion.66 = f32[768,3072]{1,0:T(8,128)} fusion(bf16[768,3072]{1,0:T(8,128)(2,1)S(1)} %bitcast.112, bf16[768,1536]{1,0:T(8,128)(2,1)S(1)} %bitcast.110), kind=kOutput, calls=%fused_computation.134 | convolution fusion | flops 3623878656 | bytes 15335424 | tf_op jit(solution)/shard_map/dot_general | solution.py:286
  412.2 6.6 %collective-permute-done.1 = bf16[2,96,1536]{2,1,0:T(8,128)(2,1)S(1)} collective-permute-done((bf16[2,96,1536]{2,1,0:T(8,128)(2,1)S(1)}, bf16[2,96,1536]{2,1,0:T(8,128)(2,1)S(1)}, u32[]{:S(2)}, u32[]{:S(2)}) %collective-permute-start.1) | collective-permute-done | bytes 589856 | tf_op jit(solution)/shard_map/ppermute | solution.py:122
  420.3 8.2 %collective-permute-done.3 = bf16[2,96,1664]{2,1,0:T(8,128)(2,1)S(1)} collective-permute-done((bf16[2,96,1664]{2,1,0:T(8,128)(2,1)S(1)}, bf16[2,96,1664]{2,1,0:T(8,128)(2,1)S(1)}, u32[]{:S(2)}, u32[]{:S(2)}) %collective-permute-start.3) | collective-permute-done | bytes 639008 | tf_op jit(solution)/shard_map/ppermute | solution.py:122
  429.9 4.2 collective-permute-done.2
  434.2 2.6 collective-permute-done.4
  438.1 11.6 %fusion.26 = bf16[1,768,3072]{2,1,0:T(8,128)(2,1)} fusion(f32[768,3072]{1,0:T(8,128)} %fusion.66, bf16[736,3072]{1,0:T(8,128)(2,1)} %fusion.19, bf16[736,1536]{1,0:T(8,128)(2,1)} %bitcast.119), kind=kOutput, calls=%fused_computation.57 | convolution fusion | flops 3477602304 | bytes 19808256 | tf_op jit(solution)/shard_map/dot_general | solution.py:286
  449.7 8.5 %stack_reshape.4 = bf16[1,768,3072]{2,1,0:T(8,128)(2,1)} reshape(bf16[3072,768]{1,0:T(8,128)(2,1)} %add_convert_fusion) | data formatting | bytes 9437184 | tf_op jit(solution)/shard_map/stack;reshape | solution.py:298
  458.2 8.3 %pad_maximum_fusion = bf16[2,768,3072]{2,1,0:T(8,128)(2,1)} fusion(bf16[1,768,3072]{2,1,0:T(8,128)(2,1)} %stack_reshape.4, bf16[1,768,3072]{2,1,0:T(8,128)(2,1)} %fusion.26), kind=kLoop, calls=%fused_computation.13 | loop fusion | flops 4718592 | bytes 18874368 | tf_op jit(solution)/shard_map/stack | solution.py:298
  466.5 3.1 add_convert_fusion.4
  469.7 6.4 %all-reduce.7.cloned.1.call-done = bf16[96,3200]{1,0:T(8,128)(2,1)} async-done(((bf16[96,3200]{1,0:T(8,128)(2,1)}), bf16[96,3200]{1,0:T(8,128)(2,1)}) %all-reduce.7.cloned.1.call-update) | async-done | bytes 614416 | tf_op jit(solution)/shard_map/psum | solution.py:371
  477.5 2.0 slice.211
  479.5 1.6 slice.212
  483.0 72.9 %reduce-scatter.2.cloned.1.call-done = bf16[2,96,3072]{2,1,0:T(8,128)(2,1)} async-done(((bf16[2,768,3072]{2,1,0:T(8,128)(2,1)}), bf16[2,96,3072]{2,1,0:T(8,128)(2,1)}) %reduce-scatter.2.cloned.1.call-update) | async-done | bytes 1179664 | tf_op jit(solution)/shard_map/reduce_scatter | solution.py:301
  555.8 2.5 fusion.110
  (248 shorter events, 36.1 us)
Async XLA Ops:
  7.2 46.9 %all-gather.3.cloned.1.call-start = ((), (), s32[]{:S(2)}) async-start(), calls=%async_computation.5 | async-start | bytes 5529600 | tf_op jit(solution)/shard_map/all_gather | solution.py:190
  8.8 7.7 %copy-start.39 = (s32[591,2]{0,1:T(2,128)S(1)}, s32[591,2]{0,1:T(2,128)}, u32[]{:S(2)}) copy-start(s32[591,2]{0,1:T(2,128)} %param.13) | copy-start | bytes 14188
  11.6 7.9 %copy-start.6 = (bf16[591,768]{1,0:T(8,128)(2,1)S(1)}, bf16[591,768]{1,0:T(8,128)(2,1)}, u32[]{:S(2)}) copy-start(bf16[591,768]{1,0:T(8,128)(2,1)} %param.11) | copy-start | bytes 2723332
  11.6 103.7 %all-gather.5.cloned.1.call-start = ((), (), s32[]{:S(2)}) async-start(), calls=%async_computation.6 | async-start | bytes 10616832 | tf_op jit(solution)/shard_map/all_gather | solution.py:201
  13.2 6.9 %copy-start.8 = (bf16[591,768]{1,0:T(8,128)(2,1)S(1)}, bf16[591,768]{1,0:T(8,128)(2,1)}, u32[]{:S(2)}) copy-start(bf16[591,768]{1,0:T(8,128)(2,1)} %param.21) | copy-start | bytes 2723332
  19.4 60.5 %copy-start.29 = (f32[591]{0:T(1024)}, f32[591]{0:T(1024)S(1)}, u32[]{:S(2)}) copy-start(f32[591]{0:T(1024)S(1)} %fusion.102) | copy-start | bytes 7096
  19.6 35.8 %copy-start.37 = (f32[591]{0:T(1024)}, f32[591]{0:T(1024)S(1)}, u32[]{:S(2)}) copy-start(f32[591]{0:T(1024)S(1)} %broadcast_multiply_fusion.2) | copy-start | bytes 7096
  20.1 35.3 %copy-start.49 = (f32[591]{0:T(1024)}, f32[591]{0:T(1024)S(1)}, u32[]{:S(2)}) copy-start(f32[591]{0:T(1024)S(1)} %fusion.100) | copy-start | bytes 7096
  25.0 58.5 %copy-start.22 = (bf16[1504,591]{1,0:T(8,128)(2,1)}, bf16[1504,591]{1,0:T(8,128)(2,1)S(1)}, u32[]{:S(2)}) copy-start(bf16[1504,591]{1,0:T(8,128)(2,1)S(1)} %get-tuple-element.101) | copy-start | bytes 5333188
  55.4 5.0 copy-start.47
  55.4 22.3 %copy-start.41 = (f32[768]{0:T(1024)}, f32[768]{0:T(1024)S(1)}, u32[]{:S(2)}) copy-start(f32[768]{0:T(1024)S(1)} %get-tuple-element.78) | copy-start | bytes 9220
  55.8 4.6 copy-start.18
  60.6 13.4 %copy-start = (bf16[640,2304]{1,0:T(8,128)(2,1)}, bf16[640,2304]{1,0:T(8,128)(2,1)S(1)}, u32[]{:S(2)}) copy-start(bf16[640,2304]{1,0:T(8,128)(2,1)S(1)} %pad.18.q_ref.k_ref.v_ref) | copy-start | bytes 8847364
  74.1 3.0 copy-start.1
  76.7 3.8 copy-start.13
  77.7 3.1 copy-start.43
  78.2 18.6 %copy-start.10 = (bf16[591,768]{1,0:T(8,128)(2,1)}, bf16[591,768]{1,0:T(8,128)(2,1)S(1)}, u32[]{:S(2)}) copy-start(bf16[591,768]{1,0:T(8,128)(2,1)S(1)} %multiply_convert_fusion.4) | copy-start | bytes 2723332
  80.4 3.0 copy-start.51
  80.7 5.0 copy-start.25
  89.6 56.7 %all-to-all-start.2 = ((bf16[4,184,1536]{2,1,0:T(8,128)(2,1)}), bf16[4,184,1536]{2,1,0:T(8,128)(2,1)S(1)}, u32[]{:S(2)}, u32[]{:S(2)}) async-start(bf16[4,184,1536]{2,1,0:T(8,128)(2,1)} %pad_maximum_fusion.3), calls=%async_computation.2 | async-start | bytes 4521984 | tf_op jit(solution)/shard_map/all_to_all | solution.py:259
  94.2 2.7 copy-start.23
  94.2 2.8 copy-start.24
  147.7 57.2 %all-to-all-start = ((bf16[4,192,1536]{2,1,0:T(8,128)(2,1)}), bf16[4,192,1536]{2,1,0:T(8,128)(2,1)S(1)}, u32[]{:S(2)}, u32[]{:S(2)}) async-start(bf16[4,192,1536]{2,1,0:T(8,128)(2,1)} %pad_maximum_fusion.1), calls=%async_computation | async-start | bytes 4718592 | tf_op jit(solution)/shard_map/all_to_all | solution.py:259
  151.6 25.8 %copy-start.16 = (bf16[3072,768]{1,0:T(8,128)(2,1)S(1)}, bf16[3072,768]{1,0:T(8,128)(2,1)}, u32[]{:S(2)}) copy-start(bf16[3072,768]{1,0:T(8,128)(2,1)} %reshape_squeeze.3) | copy-start | bytes 14155780
  177.4 3.7 copy-start.59
  177.4 14.5 %slice-start.5 = ((s8[9437184]{0:T(1024)(128)(4,1)}), s8[4194304]{0:T(1024)(128)(4,1)S(1)}, s32[]{:S(2)}) async-start(s8[9437184]{0:T(1024)(128)(4,1)} %bitcast.113), calls=%async_computation.14 | async-start | bytes 8388608
  177.4 14.5 %slice-start.6 = ((s8[9437184]{0:T(1024)(128)(4,1)}), s8[4194304]{0:T(1024)(128)(4,1)S(1)}, s32[]{:S(2)}) async-start(s8[9437184]{0:T(1024)(128)(4,1)} %bitcast.113), calls=%async_computation.15 | async-start | bytes 8388608
  181.1 10.8 %slice-start.7 = ((s8[9437184]{0:T(1024)(128)(4,1)}), s8[1048576]{0:T(1024)(128)(4,1)S(1)}, s32[]{:S(2)}) async-start(s8[9437184]{0:T(1024)(128)(4,1)} %bitcast.113), calls=%async_computation.16 | async-start | bytes 2097152
  204.9 39.3 %copy-start.14 = (bf16[4,192,1536]{2,1,0:T(8,128)(2,1)}, bf16[4,192,1536]{2,1,0:T(8,128)(2,1)S(1)}, u32[]{:S(2)}) copy-start(bf16[4,192,1536]{2,1,0:T(8,128)(2,1)S(1)} %all-to-all-done) | copy-start | bytes 7077892
  204.9 60.0 %all-to-all-start.3 = ((bf16[4,184,1536]{2,1,0:T(8,128)(2,1)}), bf16[4,184,1536]{2,1,0:T(8,128)(2,1)}, u32[]{:S(2)}, u32[]{:S(2)}) async-start(bf16[4,184,1536]{2,1,0:T(8,128)(2,1)} %bitcast.15), calls=%async_computation.3 | async-start | bytes 4521984 | tf_op jit(solution)/shard_map/all_to_all | solution.py:295
  236.0 8.1 %copy-start.58 = (bf16[768,3072]{1,0:T(8,128)(2,1)}, bf16[768,3072]{1,0:T(8,128)(2,1)S(1)}, u32[]{:S(2)}) copy-start(bf16[768,3072]{1,0:T(8,128)(2,1)S(1)} %get-tuple-element.94) | copy-start | bytes 14155780
  254.3 8.0 %copy-start.17 = (bf16[768,3072]{1,0:T(8,128)(2,1)}, bf16[768,3072]{1,0:T(8,128)(2,1)S(1)}, u32[]{:S(2)}) copy-start(bf16[768,3072]{1,0:T(8,128)(2,1)S(1)} %fusion.6) | copy-start | bytes 14155780
  262.4 7.7 %copy-start.52 = (f32[591,2]{0,1:T(2,128)S(1)}, f32[591,2]{0,1:T(2,128)}, u32[]{:S(2)}) copy-start(f32[591,2]{0,1:T(2,128)} %copy-done.51) | copy-start | bytes 14188
  264.9 57.9 %all-to-all-start.1 = ((bf16[4,192,1536]{2,1,0:T(8,128)(2,1)}), bf16[4,192,1536]{2,1,0:T(8,128)(2,1)S(1)}, u32[]{:S(2)}, u32[]{:S(2)}) async-start(bf16[4,192,1536]{2,1,0:T(8,128)(2,1)} %bitcast.10), calls=%async_computation.1 | async-start | bytes 4718592 | tf_op jit(solution)/shard_map/all_to_all | solution.py:295
  270.0 206.1 %all-reduce.7.cloned.1.call-start = ((), (), s32[]{:S(2)}) async-start(), calls=%async_computation.7 | async-start | bytes 1228800 | tf_op jit(solution)/shard_map/psum | solution.py:371
  270.2 5.5 copy-start.28
  322.8 4.0 copy-start.57
  322.8 8.2 %slice-start.8 = ((s8[4915200]{0:T(1024)(128)(4,1)}), s8[4194304]{0:T(1024)(128)(4,1)S(1)}, s32[]{:S(2)}) async-start(s8[4915200]{0:T(1024)(128)(4,1)} %bitcast.125), calls=%async_computation.17 | async-start | bytes 8388608
  326.9 4.1 slice-start.9
  328.8 1.9 copy-start.32
  328.8 1.9 copy-start.36
  328.8 1.9 copy-start.11
  328.8 2.2 copy-start.34
  328.8 2.2 copy-start.42
  328.8 2.2 copy-start.44
  359.9 5.0 copy-start.7
  359.9 5.0 copy-start.38
  359.9 5.0 copy-start.48
  364.9 2.5 copy-start.54
  364.9 3.7 copy-start.50
  374.5 3.8 copy-start.5
  379.9 20.5 %collective-permute-start = (bf16[2,2,96,3200]{3,2,1,0:T(8,128)(2,1)}, bf16[2,2,96,3200]{3,2,1,0:T(8,128)(2,1)}, u32[]{:S(2)}, u32[]{:S(2)}) collective-permute-start(bf16[2,2,96,3200]{3,2,1,0:T(8,128)(2,1)} %fusion.39), channel_id=1, source_target_pairs={{0,1},{1,0},{2,3},{3,2},{4,5},{5,4},{6,7},{7,6},{8,9},{9,8},{10,11... | collective-permute-start | bytes 7372808 | tf_op jit(solution)/shard_map/ppermute | solution.py:122
  379.9 10.4 %copy-start.21 = (bf16[4,184,1536]{2,1,0:T(8,128)(2,1)S(1)}, bf16[4,184,1536]{2,1,0:T(8,128)(2,1)}, u32[]{:S(2)}) copy-start(bf16[4,184,1536]{2,1,0:T(8,128)(2,1)} %copy-done.20) | copy-start | bytes 6782980
  379.9 20.5 %slice-start = ((s8[9830400]{0:T(1024)(128)(4,1)}), s8[4194304]{0:T(1024)(128)(4,1)S(1)}, s32[]{:S(2)}) async-start(s8[9830400]{0:T(1024)(128)(4,1)} %bitcast.104), calls=%async_computation.9 | async-start | bytes 8388608
  379.9 20.5 %slice-start.1 = ((s8[9830400]{0:T(1024)(128)(4,1)}), s8[4194304]{0:T(1024)(128)(4,1)S(1)}, s32[]{:S(2)}) async-start(s8[9830400]{0:T(1024)(128)(4,1)} %bitcast.104), calls=%async_computation.10 | async-start | bytes 8388608
  379.9 24.6 %slice-start.3 = ((s8[4718592]{0:T(1024)(128)(4,1)}), s8[4194304]{0:T(1024)(128)(4,1)S(1)}, s32[]{:S(2)}) async-start(s8[4718592]{0:T(1024)(128)(4,1)} %bitcast.111), calls=%async_computation.12 | async-start | bytes 8388608
  390.3 10.1 %slice-start.2 = ((s8[9830400]{0:T(1024)(128)(4,1)}), s8[1441792]{0:T(1024)(128)(4,1)S(1)}, s32[]{:S(2)}) async-start(s8[9830400]{0:T(1024)(128)(4,1)} %bitcast.104), calls=%async_computation.11 | async-start | bytes 2883584
  390.3 14.2 %slice-start.4 = ((s8[4718592]{0:T(1024)(128)(4,1)}), s8[524288]{0:T(1024)(128)(4,1)S(1)}, s32[]{:S(2)}) async-start(s8[4718592]{0:T(1024)(128)(4,1)} %bitcast.111), calls=%async_computation.13 | async-start | bytes 1048576
  402.6 1.9 copy-start.15
  403.0 15.8 %collective-permute-start.1 = (bf16[2,96,1536]{2,1,0:T(8,128)(2,1)S(1)}, bf16[2,96,1536]{2,1,0:T(8,128)(2,1)S(1)}, u32[]{:S(2)}, u32[]{:S(2)}) collective-permute-start(bf16[2,96,1536]{2,1,0:T(8,128)(2,1)S(1)} %fusion.84), channel_id=1, source_target_pairs={{0,2},{1,3},{2,0},{3,1},{4,6},{5,7},{6,4},{7,5},{8,10},{9,11},{10,... | collective-permute-start | bytes 1769480 | tf_op jit(solution)/shard_map/ppermute | solution.py:122
  411.2 17.3 %collective-permute-start.3 = (bf16[2,96,1664]{2,1,0:T(8,128)(2,1)S(1)}, bf16[2,96,1664]{2,1,0:T(8,128)(2,1)S(1)}, u32[]{:S(2)}, u32[]{:S(2)}) collective-permute-start(bf16[2,96,1664]{2,1,0:T(8,128)(2,1)S(1)} %fusion.82), channel_id=1, source_target_pairs={{0,4},{1,5},{2,6},{3,7},{4,0},{5,1},{6,2},{7,3},{8,12},{9,13},{10,... | collective-permute-start | bytes 1916936 | tf_op jit(solution)/shard_map/ppermute | solution.py:122
  419.0 15.1 %collective-permute-start.2 = (bf16[96,1536]{1,0:T(8,128)(2,1)S(1)}, bf16[96,1536]{1,0:T(8,128)(2,1)S(1)}, u32[]{:S(2)}, u32[]{:S(2)}) collective-permute-start(bf16[96,1536]{1,0:T(8,128)(2,1)S(1)} %fusion.87), channel_id=1, source_target_pairs={{0,4},{1,5},{2,6},{3,7},{4,0},{5,1},{6,2},{7,3},{8,12},{9,13},{10,... | collective-permute-start | bytes 884744 | tf_op jit(solution)/shard_map/ppermute | solution.py:122
  428.7 8.1 %collective-permute-start.4 = (bf16[96,1664]{1,0:T(8,128)(2,1)S(1)}, bf16[96,1664]{1,0:T(8,128)(2,1)S(1)}, u32[]{:S(2)}, u32[]{:S(2)}) collective-permute-start(bf16[96,1664]{1,0:T(8,128)(2,1)S(1)} %fusion.86), channel_id=1, source_target_pairs={{0,2},{1,3},{2,0},{3,1},{4,6},{5,7},{6,4},{7,5},{8,10},{9,11},{10,... | collective-permute-start | bytes 958472 | tf_op jit(solution)/shard_map/ppermute | solution.py:122
  437.8 118.1 %reduce-scatter.2.cloned.1.call-start = ((), (), s32[]{:S(2)}) async-start(), calls=%async_computation.8 | async-start | bytes 10616832 | tf_op jit(solution)/shard_map/reduce_scatter | solution.py:301
  (19 other events, 25.2 us)
Sparse Core Ops, SparseCore 0:
  11.7 42.3 all-gather.2
  56.5 58.6 all-gather.4
  437.9 38.1 all-reduce.6
  479.4 76.3 reduce-scatter.1

commit v10 on v9

--- a/solution.py
+++ b/solution.py
@@ -295,13 +295,14 @@
             lax.all_to_all(returning, "expert", split_axis=0, concat_axis=0, tiled=True)
         )
 
-    expert_grads = jnp.stack(
-        [grad_first, grad_second.reshape(width, ff)], axis=0
-    ).astype(jnp.bfloat16)
-    expert_share = lax.psum_scatter(expert_grads, "shard", scatter_dimension=1, tiled=True)
-    expert_share = expert_share.astype(jnp.float32)
-    grad_in_share = expert_share[0][None]
-    grad_back_share = expert_share[1].reshape(back_rows, width)[None]
+    in_share = lax.psum_scatter(
+        grad_first.astype(jnp.bfloat16), "shard", scatter_dimension=0, tiled=True
+    )
+    back_share = lax.psum_scatter(
+        grad_second.astype(jnp.bfloat16), "shard", scatter_dimension=0, tiled=True
+    )
+    grad_in_share = in_share.astype(jnp.float32)[None]
+    grad_back_share = back_share.astype(jnp.float32)[None]
 
     picked_first = None
     picked_second = None

time: 575 us -> 509 us (0.89)
  waiting for transfers between devices: 209 us -> 168 us
  local copies, waits for them, and re-layouts: 54.1 us -> 43 us
  other arithmetic: 41.5 us -> 33.6 us
  matrix products: 187 us -> 181 us
    reduce_scatter x1 -> x2, waiting for transfers between devices: 72.9 us -> 13.4 us  [the longest x1 13.4 us: shards(): lax.psum_scatter(grad_first.astype(jnp.bfloat16), 'shard', scatter_dimens...]
    psum x1, waiting for transfers between devices: 6.43 us -> 40.5 us  [shards(): lax.psum(dense_share.astype(jnp.bfloat16), 'expert').astype(jnp.float32)]
    all_to_all x2, waiting for transfers between devices: 41.9 us -> 18.8 us  [shards(): lax.all_to_all(returning, 'expert', split_axis=0, concat_axis=0, tiled=True)]
    another operation x3 -> x1, local copies, waits for them, and re-layouts: 9.81 us -> 0.01 us  [the longest x1 8.46 us: shards(): jnp.stack([grad_first, grad_second.reshape(width, ff)], axis=0)]
    ppermute x5, waiting for transfers between devices: 21.6 us -> 30.4 us  [_exchange(): got = lax.ppermute(send.astype(jnp.bfloat16), axis_name, pairs)]
    another operation x5 -> x4, other arithmetic: 9.79 us -> 1.47 us  [the longest x1 8.32 us: shards(): jnp.stack([grad_first, grad_second.reshape(width, ff)], axis=0)]
    dot_general x2, matrix products: 20.5 us -> 14.1 us  [shards(): lax.dot_general(activated, flat_grad, ROW_CONTRACT, preferred_element_typ...]
    unnamed x146 -> x158, local copies, waits for them, and re-layouts: 11.5 us -> 12.3 us
  transfers between devices with their start and end apart: 13 -> 14, of which waited for: 11 -> 11; matrix products, arithmetic and copies ran while one was open for 41% -> 47% of each run, Pallas kernels for 2% -> 7%
where the time goes in v10:
time: 509 us; the launch traced here: 501 us
  matrix products  181 us (36%)
  waiting for transfers between devices  168 us (33%)
  local copies, waits for them, and re-layouts  43 us (8%)
  Pallas kernels  35.2 us (7%)
  other arithmetic  33.6 us (7%)
  starting transfers between devices  23.5 us (5%)
  between operations  16.2 us (3%)
    dot_general x2, matrix products, shards(): jnp.dot(flat_arrived, expert_first, preferred_element_type=jnp.float32)  51.9 us
    psum x1, waiting for transfers between devices, shards(): lax.psum(dense_share.astype(jnp.bfloat16), 'expert').astype(jnp.float32)  40.5 us
    ppermute x5, waiting for transfers between devices, _exchange(): got = lax.ppermute(send.astype(jnp.bfloat16), axis_name, pairs)  30.4 us
    all_gather x1, waiting for transfers between devices, shards(): dense_full = lax.all_gather(dense_local, 'shard', axis=0, tiled=True)  29.2 us
    all_to_all x2, waiting for transfers between devices, shards(): lax.all_to_all(dispatch_rows(experts * start, experts * (start + size)).r...  23.1 us
    pallas_call x1, Pallas kernels, attention_bwd(): pl.pallas_call(functools.partial(attn_bwd_kernel, images=images), grid=(p...  21.8 us
    dot_general x2, matrix products, shards(): lax.dot_general(flat_grad, expert_second, COL_CONTRACT, preferred_element...  21.3 us
    all_to_all x2, waiting for transfers between devices, shards(): lax.all_to_all(returning, 'expert', split_axis=0, concat_axis=0, tiled=True)  18.8 us
  transfers between devices with their start and end apart: 14, of which 11 were waited for; matrix products, arithmetic and copies ran while one was open for 47% of the time, Pallas kernels for 7%

profile of v10, /device:TPU:0, one launch (start us, length us, event | category | flops | bytes accessed | tf_op | source)
XLA Modules:
  0.0 500.9 jit_solution(4664636728850734701)
XLA Ops:
  9.6 1.9 concatenate.47
  11.6 1.5 stack_reshape_squeeze.3
  13.2 2.3 pad_maximum_fusion.4
  20.1 1.5 convert_multiply_fusion
  21.6 3.3 fusion.104
  24.9 29.2 %all-gather.3.cloned.1.call-done = bf16[768,3078]{1,0:T(8,128)(2,1)} async-done(((bf16[96,3078]{1,0:T(8,128)(2,1)}), bf16[768,3078]{1,0:T(8,128)(2,1)}) %all-gather.3.cloned.1.call-update) | async-done | bytes 4727824 | tf_op jit(solution)/shard_map/all_gather | solution.py:190
  55.8 4.6 convolution_convert_fusion
  60.6 13.4 %shard_map.178 = bf16[640,768]{1,0:T(8,128)(2,1)S(1)} custom-call(bf16[640,2304]{1,0:T(8,128)(2,1)S(1)} %pad.18.q_ref.k_ref.v_ref, bf16[640,2304]{1,0:T(8,128)(2,1)S(1)} %pad.18.q_ref.k_ref.v_ref, bf16[640,2304]{1,0:T(8,128)(2,1)S(1)} %pad.18.q_ref.k_ref.v_ref), custom_call_target="tpu_custom_call" | custom-call | tf_op jit(solution)/shard_map/pallas_call | solution.py:90
  74.1 2.6 fusion.109
  78.2 1.5 fusion.110
  80.7 2.7 fusion.59
  83.4 2.3 convolution_convert_fusion.4
  85.7 2.4 add_convert_fusion.3
  88.1 1.6 pad_maximum_fusion.2
  89.6 4.6 all-to-all-start.2
  94.8 3.0 fusion.52
  100.8 1.6 pad_maximum_fusion
  102.4 12.8 %all-gather.5.cloned.1.call-done = bf16[2,768,3072]{2,1,0:T(8,128)(2,1)} async-done(((bf16[2,96,3072]{2,1,0:T(8,128)(2,1)}), bf16[2,768,3072]{2,1,0:T(8,128)(2,1)}) %all-gather.5.cloned.1.call-update) | async-done | bytes 9437200 | tf_op jit(solution)/shard_map/all_gather | solution.py:201
  115.3 4.9 slice.187
  120.1 8.5 %reshape_squeeze.3 = bf16[3072,768]{1,0:T(8,128)(2,1)} reshape(bf16[1,768,3072]{2,1,0:T(8,128)(2,1)} %slice.187) | data formatting | bytes 9437184 | tf_op jit(solution)/shard_map/reshape;squeeze | solution.py:203
  128.6 17.7 %all-to-all-done.2 = bf16[4,184,1536]{2,1,0:T(8,128)(2,1)S(1)} async-done(((bf16[4,184,1536]{2,1,0:T(8,128)(2,1)}), bf16[4,184,1536]{2,1,0:T(8,128)(2,1)S(1)}, u32[]{:S(2)}, u32[]{:S(2)}) %all-to-all-start.2) | async-done | bytes 2261024 | tf_op jit(solution)/shard_map/all_to_all | solution.py:259
  147.7 3.8 all-to-all-start
  151.6 25.7 %multiply_convert_fusion.1 = (bf16[736,3072]{1,0:T(8,128)(2,1)S(1)}, f32[736,3072]{1,0:T(8,128)}, f32[736,3072]{1,0:T(8,128)}) fusion(bf16[2,768,3072]{2,1,0:T(8,128)(2,1)} %all-gather.5.cloned.1.call-done, bf16[736,1536]{1,0:T(8,128)(2,1)} %bitcast.117), kind=kOutput, calls=%fused_computation.37 | convolution fusion | flops 3619848192 | bytes 28459008 | tf_op jit(solution)/shard_map/dot_general | solution.py:273
  177.3 3.7 convolution_convert_fusion.3
  181.0 10.8 %fusion.19 = bf16[736,3072]{1,0:T(8,128)(2,1)} fusion(f32[736,3072]{1,0:T(8,128)} %get-tuple-element.109, f32[736,3072]{1,0:T(8,128)} %get-tuple-element.97, bf16[3072,768]{1,0:T(8,128)(2,1)S(1)} %copy-done.21, bf16[736,1536]{1,0:T(8,128)(2,1)} %bitcast.118), kind=kOutput, calls=%fused_computation.36 | convolution fusion | flops 3490971648 | bytes 28459008 | tf_op jit(solution)/shard_map/dot_general | solution.py:270
  191.8 6.1 %fusion.48 = bf16[736,768]{1,0:T(8,128)(2,1)S(1)} fusion(bf16[736,3072]{1,0:T(8,128)(2,1)} %fusion.19, bf16[2,768,3072]{2,1,0:T(8,128)(2,1)S(1)} %bitcast.116), kind=kOutput, calls=%fused_computation.107 | convolution fusion | flops 3473448960 | bytes 10371072 | tf_op jit(solution)/shard_map/dot_general | solution.py:280
  197.9 1.6 pad_maximum_fusion.3
  199.6 5.3 %all-to-all-done = bf16[4,192,1536]{2,1,0:T(8,128)(2,1)S(1)} async-done(((bf16[4,192,1536]{2,1,0:T(8,128)(2,1)}), bf16[4,192,1536]{2,1,0:T(8,128)(2,1)S(1)}, u32[]{:S(2)}, u32[]{:S(2)}) %all-to-all-start) | async-done | bytes 2359328 | tf_op jit(solution)/shard_map/all_to_all | solution.py:259
  204.9 4.7 all-to-all-start.3
  209.6 26.2 %multiply_convert_fusion = (bf16[768,3072]{1,0:T(8,128)(2,1)S(1)}, f32[768,3072]{1,0:T(8,128)}, f32[768,3072]{1,0:T(8,128)}) fusion(bf16[2,768,3072]{2,1,0:T(8,128)(2,1)} %all-gather.5.cloned.1.call-done, bf16[768,1536]{1,0:T(8,128)(2,1)S(1)} %bitcast.111), kind=kOutput, calls=%fused_computation.15 | convolution fusion | flops 3777232896 | bytes 29491200 | tf_op jit(solution)/shard_map/dot_general | solution.py:273
  235.8 8.1 %convolution_convert_fusion.1 = bf16[768,768]{0,1:T(8,128)(2,1)S(1)} fusion(bf16[768,3072]{1,0:T(8,128)(2,1)S(1)} %get-tuple-element.94, bf16[3072,768]{1,0:T(8,128)(2,1)} %reshape_squeeze.3), kind=kOutput, calls=%fused_computation.105 | convolution fusion | flops 3624468480 | bytes 10616832 | tf_op jit(solution)/shard_map/dot_general | solution.py:277
  243.9 10.5 %fusion.6 = bf16[768,3072]{1,0:T(8,128)(2,1)S(1)} fusion(f32[768,3072]{1,0:T(8,128)} %get-tuple-element.110, f32[768,3072]{1,0:T(8,128)} %get-tuple-element.95, bf16[3072,768]{1,0:T(8,128)(2,1)} %reshape_squeeze.3, bf16[768,1536]{1,0:T(8,128)(2,1)S(1)} %bitcast.112), kind=kOutput, calls=%fused_computation.12 | convolution fusion | flops 3642753024 | bytes 29491200 | tf_op jit(solution)/shard_map/dot_general | solution.py:270
  254.4 8.0 %fusion.47 = bf16[768,768]{0,1:T(8,128)(2,1)S(1)} fusion(bf16[768,3072]{1,0:T(8,128)(2,1)S(1)} %fusion.6, bf16[2,768,3072]{2,1,0:T(8,128)(2,1)} %all-gather.5.cloned.1.call-done), kind=kOutput, calls=%fused_computation.104 | convolution fusion | flops 3624468480 | bytes 10616832 | tf_op jit(solution)/shard_map/dot_general | solution.py:280
  262.6 2.5 copy.111
  265.0 5.2 %all-to-all-start.1 = ((bf16[4,192,1536]{2,1,0:T(8,128)(2,1)}), bf16[4,192,1536]{2,1,0:T(8,128)(2,1)}, u32[]{:S(2)}, u32[]{:S(2)}) async-start(bf16[4,192,1536]{2,1,0:T(8,128)(2,1)} %bitcast.10), calls=%async_computation.1 | async-start | bytes 4718592 | tf_op jit(solution)/shard_map/all_to_all | solution.py:295
  270.2 5.9 %fusion.62 = f32[3072,768]{1,0:T(8,128)S(1)} fusion(bf16[768,3072]{1,0:T(8,128)(2,1)} %copy-done.66, bf16[768,1536]{1,0:T(8,128)(2,1)S(1)} %bitcast.113), kind=kOutput, calls=%fused_computation.129 | convolution fusion | flops 3623878656 | bytes 15335424 | tf_op jit(solution)/shard_map/dot_general | solution.py:283
  276.2 8.2 %add_convert_fusion = bf16[3072,768]{1,0:T(8,128)(2,1)} fusion(f32[3072,768]{1,0:T(8,128)S(1)} %fusion.62, bf16[736,3072]{1,0:T(8,128)(2,1)} %copy-done.67, bf16[736,1536]{1,0:T(8,128)(2,1)S(1)} %bitcast.119), kind=kOutput, calls=%fused_computation.13 | convolution fusion | flops 3477602304 | bytes 19808256 | tf_op jit(solution)/shard_map/dot_general | solution.py:283
  284.4 8.8 %fusion.65 = f32[768,3072]{1,0:T(8,128)} fusion(bf16[768,3072]{1,0:T(8,128)(2,1)} %copy-done.22, bf16[768,1536]{1,0:T(8,128)(2,1)S(1)} %bitcast.114), kind=kOutput, calls=%fused_computation.132 | convolution fusion | flops 3623878656 | bytes 15335424 | tf_op jit(solution)/shard_map/dot_general | solution.py:286
  293.3 5.8 %fusion.57 = f32[591,1536]{1,0:T(8,128)} fusion(bf16[736,1536]{1,0:T(8,128)(2,1)} %bitcast.16, pred[1504,591]{1,0:T(32,128)(4,1)S(1)} %copy-done.35), kind=kOutput, calls=%fused_computation.119 | convolution fusion | flops 1336246272 | bytes 6363136 | tf_op jit(solution)/shard_map/dot_general | solution.py:312
  299.1 5.3 %fusion.54 = f32[591,1536]{1,0:T(8,128)} fusion(bf16[736,1536]{1,0:T(8,128)(2,1)} %bitcast.16, pred[1504,591]{1,0:T(32,128)(4,1)S(1)} %copy-done.34), kind=kOutput, calls=%fused_computation.116 | convolution fusion | flops 1336246272 | bytes 6363136 | tf_op jit(solution)/shard_map/dot_general | solution.py:315
  304.4 18.8 %all-to-all-done.1 = bf16[4,192,1536]{2,1,0:T(8,128)(2,1)} async-done(((bf16[4,192,1536]{2,1,0:T(8,128)(2,1)}), bf16[4,192,1536]{2,1,0:T(8,128)(2,1)}, u32[]{:S(2)}, u32[]{:S(2)}) %all-to-all-start.1) | async-done | bytes 2359328 | tf_op jit(solution)/shard_map/all_to_all | solution.py:295
  323.2 4.7 convolution_add_fusion.1
  327.9 4.1 convolution_add_fusion
  332.2 1.8 multiply_reduce_fusion.3
  337.5 21.8 %shard_map.179 = (bf16[640,768]{1,0:T(8,128)(2,1)S(1)}, bf16[640,768]{1,0:T(8,128)(2,1)S(1)}, bf16[640,768]{1,0:T(8,128)(2,1)S(1)}) custom-call(bf16[640,2304]{1,0:T(8,128)(2,1)} %copy-done, bf16[640,2304]{1,0:T(8,128)(2,1)} %copy-done, bf16[640,2304]{1,0:T(8,128)(2,1)} %copy-done, bf16[640,768]{1,0:T(8,128)(2,1)S(1)} %pad.20.g_ref), custom_call_target="tpu_custom_call" | custom-call | tf_op jit(solution)/shard_map/pallas_call | solution.py:106
  360.5 2.4 fusion.44
  364.9 2.4 fusion.78
  367.3 3.0 fusion.75
  371.1 5.0 copy-done.5
  376.0 1.7 fusion.38
  377.7 8.1 %add_convert_fusion.1 = bf16[768,3072]{1,0:T(8,128)(2,1)} fusion(f32[768,3072]{1,0:T(8,128)S(1)} %bitcast.110, bf16[736,3072]{1,0:T(8,128)(2,1)} %fusion.19, bf16[736,1536]{1,0:T(8,128)(2,1)S(1)} %bitcast.120), kind=kOutput, calls=%fused_computation.14 | convolution fusion | flops 3477602304 | bytes 19808256 | tf_op jit(solution)/shard_map/dot_general | solution.py:286
  385.9 3.6 bitcast_add_fusion
  389.9 1.5 collective-permute-start.1
  391.7 1.8 add_convert_fusion.4
  394.9 10.8 %collective-permute-done.1 = bf16[2,96,1536]{2,1,0:T(8,128)(2,1)S(1)} collective-permute-done((bf16[2,96,1536]{2,1,0:T(8,128)(2,1)S(1)}, bf16[2,96,1536]{2,1,0:T(8,128)(2,1)S(1)}, u32[]{:S(2)}, u32[]{:S(2)}) %collective-permute-start.1) | collective-permute-done | bytes 589856 | tf_op jit(solution)/shard_map/ppermute | solution.py:122
  407.0 6.4 %collective-permute-done.3 = bf16[2,96,1664]{2,1,0:T(8,128)(2,1)S(1)} collective-permute-done((bf16[2,96,1664]{2,1,0:T(8,128)(2,1)S(1)}, bf16[2,96,1664]{2,1,0:T(8,128)(2,1)S(1)}, u32[]{:S(2)}, u32[]{:S(2)}) %collective-permute-start.3) | collective-permute-done | bytes 639008 | tf_op jit(solution)/shard_map/ppermute | solution.py:122
  414.9 10.8 %collective-permute-done.2 = bf16[96,1536]{1,0:T(8,128)(2,1)S(1)} collective-permute-done((bf16[96,1536]{1,0:T(8,128)(2,1)S(1)}, bf16[96,1536]{1,0:T(8,128)(2,1)S(1)}, u32[]{:S(2)}, u32[]{:S(2)}) %collective-permute-start.2) | collective-permute-done | bytes 294944 | tf_op jit(solution)/shard_map/ppermute | solution.py:122
  425.8 2.3 collective-permute-done.4
  429.1 2.2 bitcast_convert_fusion.1
  431.2 13.4 %reduce-scatter.3.cloned.1.call-done = bf16[96,3072]{1,0:T(8,128)(2,1)} async-done(((bf16[768,3072]{1,0:T(8,128)(2,1)}), bf16[96,3072]{1,0:T(8,128)(2,1)}) %reduce-scatter.3.cloned.1.call-update) | async-done | bytes 589840 | tf_op jit(solution)/shard_map/reduce_scatter | solution.py:298
  444.6 2.2 bitcast_convert_fusion.2
  446.8 40.5 %all-reduce.7.cloned.1.call-done = bf16[96,3200]{1,0:T(8,128)(2,1)} async-done(((bf16[96,3200]{1,0:T(8,128)(2,1)}), bf16[96,3200]{1,0:T(8,128)(2,1)}) %all-reduce.7.cloned.1.call-update) | async-done | bytes 614416 | tf_op jit(solution)/shard_map/psum | solution.py:372
  490.5 2.0 slice.203
  492.5 1.6 slice.204
  (260 shorter events, 32.1 us)
Async XLA Ops:
  7.2 46.9 %all-gather.3.cloned.1.call-start = ((), (), s32[]{:S(2)}) async-start(), calls=%async_computation.6 | async-start | bytes 5529600 | tf_op jit(solution)/shard_map/all_gather | solution.py:190
  8.8 7.7 %copy-start.47 = (s32[591,2]{0,1:T(2,128)S(1)}, s32[591,2]{0,1:T(2,128)}, u32[]{:S(2)}) copy-start(s32[591,2]{0,1:T(2,128)} %param.13) | copy-start | bytes 14188
  11.6 7.9 %copy-start.6 = (bf16[591,768]{1,0:T(8,128)(2,1)S(1)}, bf16[591,768]{1,0:T(8,128)(2,1)}, u32[]{:S(2)}) copy-start(bf16[591,768]{1,0:T(8,128)(2,1)} %param.11) | copy-start | bytes 2723332
  11.6 103.7 %all-gather.5.cloned.1.call-start = ((), (), s32[]{:S(2)}) async-start(), calls=%async_computation.7 | async-start | bytes 10616832 | tf_op jit(solution)/shard_map/all_gather | solution.py:201
  13.2 6.9 %copy-start.10 = (bf16[591,768]{1,0:T(8,128)(2,1)S(1)}, bf16[591,768]{1,0:T(8,128)(2,1)}, u32[]{:S(2)}) copy-start(bf16[591,768]{1,0:T(8,128)(2,1)} %param.21) | copy-start | bytes 2723332
  19.4 60.5 %copy-start.37 = (f32[591]{0:T(1024)}, f32[591]{0:T(1024)S(1)}, u32[]{:S(2)}) copy-start(f32[591]{0:T(1024)S(1)} %fusion.101) | copy-start | bytes 7096
  19.6 35.8 %copy-start.45 = (f32[591]{0:T(1024)}, f32[591]{0:T(1024)S(1)}, u32[]{:S(2)}) copy-start(f32[591]{0:T(1024)S(1)} %broadcast_multiply_fusion.2) | copy-start | bytes 7096
  20.1 35.3 %copy-start.57 = (f32[591]{0:T(1024)}, f32[591]{0:T(1024)S(1)}, u32[]{:S(2)}) copy-start(f32[591]{0:T(1024)S(1)} %fusion.99) | copy-start | bytes 7096
  24.9 58.5 %copy-start.28 = (bf16[1504,591]{1,0:T(8,128)(2,1)}, bf16[1504,591]{1,0:T(8,128)(2,1)S(1)}, u32[]{:S(2)}) copy-start(bf16[1504,591]{1,0:T(8,128)(2,1)S(1)} %get-tuple-element.99) | copy-start | bytes 5333188
  55.4 5.0 %copy-start.55 = (f32[768]{0:T(1024)}, f32[768]{0:T(1024)S(1)}, u32[]{:S(2)}) copy-start(f32[768]{0:T(1024)S(1)} %get-tuple-element.79) | copy-start | bytes 9220
  55.4 22.3 %copy-start.49 = (f32[768]{0:T(1024)}, f32[768]{0:T(1024)S(1)}, u32[]{:S(2)}) copy-start(f32[768]{0:T(1024)S(1)} %get-tuple-element.78) | copy-start | bytes 9220
  55.8 4.6 copy-start.23
  60.6 13.4 %copy-start = (bf16[640,2304]{1,0:T(8,128)(2,1)}, bf16[640,2304]{1,0:T(8,128)(2,1)S(1)}, u32[]{:S(2)}) copy-start(bf16[640,2304]{1,0:T(8,128)(2,1)S(1)} %pad.18.q_ref.k_ref.v_ref) | copy-start | bytes 8847364
  74.1 3.0 copy-start.1
  76.7 3.7 copy-start.16
  76.7 3.2 copy-start.41
  77.7 3.0 copy-start.51
  78.2 19.6 %copy-start.12 = (bf16[591,768]{1,0:T(8,128)(2,1)}, bf16[591,768]{1,0:T(8,128)(2,1)S(1)}, u32[]{:S(2)}) copy-start(bf16[591,768]{1,0:T(8,128)(2,1)S(1)} %multiply_convert_fusion.4) | copy-start | bytes 2723332
  80.7 5.0 copy-start.31
  89.6 56.7 %all-to-all-start.2 = ((bf16[4,184,1536]{2,1,0:T(8,128)(2,1)}), bf16[4,184,1536]{2,1,0:T(8,128)(2,1)S(1)}, u32[]{:S(2)}, u32[]{:S(2)}) async-start(bf16[4,184,1536]{2,1,0:T(8,128)(2,1)} %pad_maximum_fusion.2), calls=%async_computation.2 | async-start | bytes 4521984 | tf_op jit(solution)/shard_map/all_to_all | solution.py:259
  94.2 3.6 copy-start.29
  94.2 3.6 copy-start.30
  147.7 57.1 %all-to-all-start = ((bf16[4,192,1536]{2,1,0:T(8,128)(2,1)}), bf16[4,192,1536]{2,1,0:T(8,128)(2,1)S(1)}, u32[]{:S(2)}, u32[]{:S(2)}) async-start(bf16[4,192,1536]{2,1,0:T(8,128)(2,1)} %pad_maximum_fusion), calls=%async_computation | async-start | bytes 4718592 | tf_op jit(solution)/shard_map/all_to_all | solution.py:259
  151.6 25.8 %copy-start.21 = (bf16[3072,768]{1,0:T(8,128)(2,1)S(1)}, bf16[3072,768]{1,0:T(8,128)(2,1)}, u32[]{:S(2)}) copy-start(bf16[3072,768]{1,0:T(8,128)(2,1)} %reshape_squeeze.3) | copy-start | bytes 14155780
  177.3 3.7 copy-start.67
  177.3 14.5 %slice-start.3 = ((s8[9437184]{0:T(1024)(128)(4,1)}), s8[4194304]{0:T(1024)(128)(4,1)S(1)}, s32[]{:S(2)}) async-start(s8[9437184]{0:T(1024)(128)(4,1)} %bitcast.115), calls=%async_computation.14 | async-start | bytes 8388608
  177.3 14.5 %slice-start.4 = ((s8[9437184]{0:T(1024)(128)(4,1)}), s8[4194304]{0:T(1024)(128)(4,1)S(1)}, s32[]{:S(2)}) async-start(s8[9437184]{0:T(1024)(128)(4,1)} %bitcast.115), calls=%async_computation.15 | async-start | bytes 8388608
  181.0 10.8 %slice-start.5 = ((s8[9437184]{0:T(1024)(128)(4,1)}), s8[1048576]{0:T(1024)(128)(4,1)S(1)}, s32[]{:S(2)}) async-start(s8[9437184]{0:T(1024)(128)(4,1)} %bitcast.115), calls=%async_computation.16 | async-start | bytes 2097152
  204.9 39.0 %copy-start.17 = (bf16[4,192,1536]{2,1,0:T(8,128)(2,1)}, bf16[4,192,1536]{2,1,0:T(8,128)(2,1)S(1)}, u32[]{:S(2)}) copy-start(bf16[4,192,1536]{2,1,0:T(8,128)(2,1)S(1)} %all-to-all-done) | copy-start | bytes 7077892
  204.9 60.1 %all-to-all-start.3 = ((bf16[4,184,1536]{2,1,0:T(8,128)(2,1)}), bf16[4,184,1536]{2,1,0:T(8,128)(2,1)}, u32[]{:S(2)}, u32[]{:S(2)}) async-start(bf16[4,184,1536]{2,1,0:T(8,128)(2,1)} %bitcast.15), calls=%async_computation.3 | async-start | bytes 4521984 | tf_op jit(solution)/shard_map/all_to_all | solution.py:295
  235.8 8.1 %copy-start.66 = (bf16[768,3072]{1,0:T(8,128)(2,1)}, bf16[768,3072]{1,0:T(8,128)(2,1)S(1)}, u32[]{:S(2)}) copy-start(bf16[768,3072]{1,0:T(8,128)(2,1)S(1)} %get-tuple-element.94) | copy-start | bytes 14155780
  254.4 8.0 %copy-start.22 = (bf16[768,3072]{1,0:T(8,128)(2,1)}, bf16[768,3072]{1,0:T(8,128)(2,1)S(1)}, u32[]{:S(2)}) copy-start(bf16[768,3072]{1,0:T(8,128)(2,1)S(1)} %fusion.6) | copy-start | bytes 14155780
  265.0 5.2 %copy-start.18 = (bf16[4,192,1536]{2,1,0:T(8,128)(2,1)S(1)}, bf16[4,192,1536]{2,1,0:T(8,128)(2,1)}, u32[]{:S(2)}) copy-start(bf16[4,192,1536]{2,1,0:T(8,128)(2,1)} %copy-done.17) | copy-start | bytes 7077892
  265.0 58.1 %all-to-all-start.1 = ((bf16[4,192,1536]{2,1,0:T(8,128)(2,1)}), bf16[4,192,1536]{2,1,0:T(8,128)(2,1)}, u32[]{:S(2)}, u32[]{:S(2)}) async-start(bf16[4,192,1536]{2,1,0:T(8,128)(2,1)} %bitcast.10), calls=%async_computation.1 | async-start | bytes 4718592 | tf_op jit(solution)/shard_map/all_to_all | solution.py:295
  270.2 158.8 %reduce-scatter.5.cloned.1.call-start = ((), (), s32[]{:S(2)}) async-start(), calls=%async_computation.10 | async-start | bytes 5308416 | tf_op jit(solution)/shard_map/reduce_scatter | solution.py:301
  270.2 5.9 %copy-start.26 = (bf16[4,184,1536]{2,1,0:T(8,128)(2,1)S(1)}, bf16[4,184,1536]{2,1,0:T(8,128)(2,1)}, u32[]{:S(2)}) copy-start(bf16[4,184,1536]{2,1,0:T(8,128)(2,1)} %copy-done.25) | copy-start | bytes 6782980
  284.4 8.9 %copy-start.35 = (pred[1504,591]{1,0:T(32,128)(4,1)S(1)}, pred[1504,591]{1,0:T(32,128)(4,1)}, u32[]{:S(2)}) copy-start(pred[1504,591]{1,0:T(32,128)(4,1)} %get-tuple-element.100) | copy-start | bytes 2666596
  284.4 160.2 %reduce-scatter.3.cloned.1.call-start = ((), (), s32[]{:S(2)}) async-start(), calls=%async_computation.9 | async-start | bytes 5308416 | tf_op jit(solution)/shard_map/reduce_scatter | solution.py:298
  293.3 5.8 %copy-start.34 = (pred[1504,591]{1,0:T(32,128)(4,1)S(1)}, pred[1504,591]{1,0:T(32,128)(4,1)}, u32[]{:S(2)}) copy-start(pred[1504,591]{1,0:T(32,128)(4,1)} %get-tuple-element.103) | copy-start | bytes 2666596
  323.2 4.7 copy-start.65
  323.2 10.9 %slice-start.6 = ((s8[4915200]{0:T(1024)(128)(4,1)}), s8[4194304]{0:T(1024)(128)(4,1)S(1)}, s32[]{:S(2)}) async-start(s8[4915200]{0:T(1024)(128)(4,1)} %bitcast.125), calls=%async_computation.17 | async-start | bytes 8388608
  327.9 4.1 copy-start.4
  327.9 4.1 copy-start.11
  327.9 4.1 copy-start.38
  327.9 4.1 copy-start.63
  327.9 4.1 copy-start.64
  327.9 6.1 %slice-start.7 = ((s8[4915200]{0:T(1024)(128)(4,1)}), s8[720896]{0:T(1024)(128)(4,1)S(1)}, s32[]{:S(2)}) async-start(s8[4915200]{0:T(1024)(128)(4,1)} %bitcast.125), calls=%async_computation.18 | async-start | bytes 1441792
  360.5 2.5 copy-start.19
  360.5 2.5 copy-start.60
  360.5 2.5 copy-start.58
  360.5 3.5 copy-start.13
  364.9 2.5 copy-start.20
  364.9 2.5 copy-start.24
  367.3 10.4 %slice-start = ((s8[9437184]{0:T(1024)(128)(4,1)}), s8[4194304]{0:T(1024)(128)(4,1)S(1)}, s32[]{:S(2)}) async-start(s8[9437184]{0:T(1024)(128)(4,1)} %bitcast.109), calls=%async_computation.11 | async-start | bytes 8388608
  370.3 7.4 %slice-start.1 = ((s8[9437184]{0:T(1024)(128)(4,1)}), s8[4194304]{0:T(1024)(128)(4,1)S(1)}, s32[]{:S(2)}) async-start(s8[9437184]{0:T(1024)(128)(4,1)} %bitcast.109), calls=%async_computation.12 | async-start | bytes 8388608
  370.3 7.4 %slice-start.2 = ((s8[9437184]{0:T(1024)(128)(4,1)}), s8[1048576]{0:T(1024)(128)(4,1)S(1)}, s32[]{:S(2)}) async-start(s8[9437184]{0:T(1024)(128)(4,1)} %bitcast.109), calls=%async_computation.13 | async-start | bytes 2097152
  371.0 5.0 copy-start.5
  371.0 6.7 %copy-start.27 = (bf16[4,184,1536]{2,1,0:T(8,128)(2,1)S(1)}, bf16[4,184,1536]{2,1,0:T(8,128)(2,1)}, u32[]{:S(2)}) copy-start(bf16[4,184,1536]{2,1,0:T(8,128)(2,1)} %copy-done.25) | copy-start | bytes 6782980
  377.7 8.2 %collective-permute-start = (bf16[2,2,96,3200]{3,2,1,0:T(8,128)(2,1)}, bf16[2,2,96,3200]{3,2,1,0:T(8,128)(2,1)}, u32[]{:S(2)}, u32[]{:S(2)}) collective-permute-start(bf16[2,2,96,3200]{3,2,1,0:T(8,128)(2,1)} %fusion.38), channel_id=1, source_target_pairs={{0,1},{1,0},{2,3},{3,2},{4,5},{5,4},{6,7},{7,6},{8,9},{9,8},{10,11... | collective-permute-start | bytes 7372808 | tf_op jit(solution)/shard_map/ppermute | solution.py:122
  385.8 101.4 %all-reduce.7.cloned.1.call-start = ((), (), s32[]{:S(2)}) async-start(), calls=%async_computation.8 | async-start | bytes 1228800 | tf_op jit(solution)/shard_map/psum | solution.py:372
  389.9 15.8 %collective-permute-start.1 = (bf16[2,96,1536]{2,1,0:T(8,128)(2,1)S(1)}, bf16[2,96,1536]{2,1,0:T(8,128)(2,1)S(1)}, u32[]{:S(2)}, u32[]{:S(2)}) collective-permute-start(bf16[2,96,1536]{2,1,0:T(8,128)(2,1)S(1)} %fusion.83), channel_id=1, source_target_pairs={{0,2},{1,3},{2,0},{3,1},{4,6},{5,7},{6,4},{7,5},{8,10},{9,11},{10,... | collective-permute-start | bytes 1769480 | tf_op jit(solution)/shard_map/ppermute | solution.py:122
  393.7 19.7 %collective-permute-start.3 = (bf16[2,96,1664]{2,1,0:T(8,128)(2,1)S(1)}, bf16[2,96,1664]{2,1,0:T(8,128)(2,1)S(1)}, u32[]{:S(2)}, u32[]{:S(2)}) collective-permute-start(bf16[2,96,1664]{2,1,0:T(8,128)(2,1)S(1)} %fusion.81), channel_id=1, source_target_pairs={{0,4},{1,5},{2,6},{3,7},{4,0},{5,1},{6,2},{7,3},{8,12},{9,13},{10,... | collective-permute-start | bytes 1916936 | tf_op jit(solution)/shard_map/ppermute | solution.py:122
  405.9 19.8 %collective-permute-start.2 = (bf16[96,1536]{1,0:T(8,128)(2,1)S(1)}, bf16[96,1536]{1,0:T(8,128)(2,1)S(1)}, u32[]{:S(2)}, u32[]{:S(2)}) collective-permute-start(bf16[96,1536]{1,0:T(8,128)(2,1)S(1)} %fusion.86), channel_id=1, source_target_pairs={{0,4},{1,5},{2,6},{3,7},{4,0},{5,1},{6,2},{7,3},{8,12},{9,13},{10,... | collective-permute-start | bytes 884744 | tf_op jit(solution)/shard_map/ppermute | solution.py:122
  413.6 14.5 %collective-permute-start.4 = (bf16[96,1664]{1,0:T(8,128)(2,1)S(1)}, bf16[96,1664]{1,0:T(8,128)(2,1)S(1)}, u32[]{:S(2)}, u32[]{:S(2)}) collective-permute-start(bf16[96,1664]{1,0:T(8,128)(2,1)S(1)} %fusion.85), channel_id=1, source_target_pairs={{0,2},{1,3},{2,0},{3,1},{4,6},{5,7},{6,4},{7,5},{8,10},{9,11},{10,... | collective-permute-start | bytes 958472 | tf_op jit(solution)/shard_map/ppermute | solution.py:122
  (26 other events, 37.5 us)
Sparse Core Ops, SparseCore 0:
  11.7 42.3 all-gather.2
  56.5 58.6 all-gather.4
  284.5 54.2 reduce-scatter.4
  386.0 58.6 reduce-scatter.2
  447.4 39.8 all-reduce.6

commit v11 on v9

--- a/solution.py
+++ b/solution.py
@@ -38,46 +38,43 @@
     return e / jnp.sum(e, axis=1, keepdims=True)
 
 
+def _two_heads(values, lane):
+    zero = jnp.zeros_like(values)
+    return jnp.concatenate(
+        [jnp.where(lane < HD, values, zero), jnp.where(lane >= HD, values, zero)], axis=0
+    )
+
+
+def _pick_heads(stacked, lane, rows):
+    return jnp.where(lane < HD, stacked[:rows], stacked[rows:])
+
+
 def attn_fwd_kernel(q_ref, k_ref, v_ref, o_ref, *, images):
     R = q_ref.shape[0]
-    q = q_ref[...]
+    same = _same_image(R, images)
+    same = jnp.concatenate([same, same], axis=0)
+    lane = lax.broadcasted_iota(jnp.int32, (1, 2 * HD), 1)
+    p = _softmax_masked(_two_heads(q_ref[...], lane), k_ref[...], same)
+    o = jnp.dot(p.astype(jnp.bfloat16), v_ref[...], preferred_element_type=jnp.float32)
+    o_ref[...] = _pick_heads(o, lane, R).astype(o_ref.dtype)
+
+
+def attn_bwd_kernel(q_ref, k_ref, v_ref, g_ref, dq_ref, dk_ref, dv_ref, *, images):
+    R = q_ref.shape[0]
     k = k_ref[...]
     v = v_ref[...]
     same = _same_image(R, images)
+    same = jnp.concatenate([same, same], axis=0)
     lane = lax.broadcasted_iota(jnp.int32, (1, 2 * HD), 1)
-    out = jnp.zeros((R, 2 * HD), jnp.float32)
-    for j in range(2):
-        in_head = (lane >= HD) == (j == 1)
-        p = _softmax_masked(jnp.where(in_head, q, jnp.zeros_like(q)), k, same)
-        o = jnp.dot(p.astype(jnp.bfloat16), v, preferred_element_type=jnp.float32)
-        out = jnp.where(in_head, o, out)
-    o_ref[...] = out.astype(o_ref.dtype)
-
-
-def attn_bwd_kernel(q_ref, k_ref, v_ref, g_ref, dq_ref, dk_ref, dv_ref, *, images):
-    R = q_ref.shape[0]
-    q = q_ref[...]
-    k = k_ref[...]
-    v = v_ref[...]
-    g = g_ref[...]
-    same = _same_image(R, images)
-    lane = lax.broadcasted_iota(jnp.int32, (1, 2 * HD), 1)
-    dq = jnp.zeros((R, 2 * HD), jnp.float32)
-    dk = jnp.zeros((R, 2 * HD), jnp.float32)
-    dv = jnp.zeros((R, 2 * HD), jnp.float32)
-    for j in range(2):
-        in_head = (lane >= HD) == (j == 1)
-        p = _softmax_masked(jnp.where(in_head, q, jnp.zeros_like(q)), k, same)
-        gj = jnp.where(in_head, g, jnp.zeros_like(g))
-        dp = lax.dot_general(gj, v, COL_CONTRACT, preferred_element_type=jnp.float32)
-        ds = (p * (dp - jnp.sum(p * dp, axis=1, keepdims=True))).astype(jnp.bfloat16)
-        dq_j = jnp.dot(ds, k, preferred_element_type=jnp.float32) * (HD ** -0.5)
-        dk_j = lax.dot_general(ds, q, ROW_CONTRACT, preferred_element_type=jnp.float32) * (HD ** -0.5)
-        dv_j = lax.dot_general(p.astype(jnp.bfloat16), g, ROW_CONTRACT, preferred_element_type=jnp.float32)
-        dq = jnp.where(in_head, dq_j, dq)
-        dk = jnp.where(in_head, dk_j, dk)
-        dv = jnp.where(in_head, dv_j, dv)
-    dq_ref[...] = dq.astype(dq_ref.dtype)
+    q2 = _two_heads(q_ref[...], lane)
+    g2 = _two_heads(g_ref[...], lane)
+    p = _softmax_masked(q2, k, same)
+    dp = lax.dot_general(g2, v, COL_CONTRACT, preferred_element_type=jnp.float32)
+    ds = (p * (dp - jnp.sum(p * dp, axis=1, keepdims=True))).astype(jnp.bfloat16)
+    dq = jnp.dot(ds, k, preferred_element_type=jnp.float32) * (HD ** -0.5)
+    dk = lax.dot_general(ds, q2, ROW_CONTRACT, preferred_element_type=jnp.float32) * (HD ** -0.5)
+    dv = lax.dot_general(p.astype(jnp.bfloat16), g2, ROW_CONTRACT, preferred_element_type=jnp.float32)
+    dq_ref[...] = _pick_heads(dq, lane, R).astype(dq_ref.dtype)
     dk_ref[...] = dk.astype(dk_ref.dtype)
     dv_ref[...] = dv.astype(dv_ref.dtype)
 

time: 575 us -> 575 us (level)
  no operation moved by 1% of the time
where the time goes in v11:
time: 575 us; the launch traced here: 567 us
  waiting for transfers between devices  209 us (36%)
  matrix products  187 us (33%)
  local copies, waits for them, and re-layouts  54.1 us (9%)
  other arithmetic  41.5 us (7%)
  Pallas kernels  35.5 us (6%)
  starting transfers between devices  24.1 us (4%)
  between operations  16.2 us (3%)
    reduce_scatter x1, waiting for transfers between devices, shards(): lax.psum_scatter(expert_grads, 'shard', scatter_dimension=1, tiled=True)  72.9 us
    dot_general x2, matrix products, shards(): jnp.dot(flat_arrived, expert_first, preferred_element_type=jnp.float32)  52 us
    all_to_all x2, waiting for transfers between devices, shards(): lax.all_to_all(returning, 'expert', split_axis=0, concat_axis=0, tiled=True)  41.9 us
    all_gather x1, waiting for transfers between devices, shards(): dense_full = lax.all_gather(dense_local, 'shard', axis=0, tiled=True)  29.1 us
    all_to_all x2, waiting for transfers between devices, shards(): lax.all_to_all(dispatch_rows(experts * start, experts * (start + size)).r...  23 us
    pallas_call x1, Pallas kernels, attention_bwd(): pl.pallas_call(functools.partial(attn_bwd_kernel, images=images), grid=(p...  22.1 us
    ppermute x5, waiting for transfers between devices, _exchange(): got = lax.ppermute(send.astype(jnp.bfloat16), axis_name, pairs)  21.6 us
    dot_general x2, matrix products, shards(): lax.dot_general(flat_grad, expert_second, COL_CONTRACT, preferred_element...  20.9 us
  transfers between devices with their start and end apart: 13, of which 11 were waited for; matrix products, arithmetic and copies ran while one was open for 41% of the time, Pallas kernels for 2%

profile of v11, /device:TPU:0, one launch (start us, length us, event | category | flops | bytes accessed | tf_op | source)
XLA Modules:
  0.0 566.9 jit_solution(7531093707149227836)
XLA Ops:
  9.6 1.9 concatenate.47
  11.6 1.5 stack_reshape_squeeze.3
  13.2 2.3 pad_maximum_fusion.5
  21.6 3.3 fusion.105
  25.0 29.1 %all-gather.3.cloned.1.call-done = bf16[768,3078]{1,0:T(8,128)(2,1)} async-done(((bf16[96,3078]{1,0:T(8,128)(2,1)}), bf16[768,3078]{1,0:T(8,128)(2,1)}) %all-gather.3.cloned.1.call-update) | async-done | bytes 4727824 | tf_op jit(solution)/shard_map/all_gather | solution.py:187
  55.8 4.6 convolution_convert_fusion
  60.6 13.4 %shard_map.178 = bf16[640,768]{1,0:T(8,128)(2,1)S(1)} custom-call(bf16[640,2304]{1,0:T(8,128)(2,1)S(1)} %pad.18.q_ref.k_ref.v_ref, bf16[640,2304]{1,0:T(8,128)(2,1)S(1)} %pad.18.q_ref.k_ref.v_ref, bf16[640,2304]{1,0:T(8,128)(2,1)S(1)} %pad.18.q_ref.k_ref.v_ref), custom_call_target="tpu_custom_call" | custom-call | tf_op jit(solution)/shard_map/pallas_call | solution.py:87
  74.0 2.6 fusion.111
  80.7 2.7 fusion.60
  83.4 2.3 convolution_convert_fusion.4
  85.7 2.3 add_convert_fusion.3
  88.0 1.5 pad_maximum_fusion.3
  89.6 4.6 all-to-all-start.2
  94.2 2.7 fusion.53
  99.9 1.6 pad_maximum_fusion.1
  101.5 13.8 %all-gather.5.cloned.1.call-done = bf16[2,768,3072]{2,1,0:T(8,128)(2,1)} async-done(((bf16[2,96,3072]{2,1,0:T(8,128)(2,1)}), bf16[2,768,3072]{2,1,0:T(8,128)(2,1)}) %all-gather.5.cloned.1.call-update) | async-done | bytes 9437200 | tf_op jit(solution)/shard_map/all_gather | solution.py:198
  115.3 4.9 slice.195
  120.1 8.5 %reshape_squeeze.3 = bf16[3072,768]{1,0:T(8,128)(2,1)} reshape(bf16[1,768,3072]{2,1,0:T(8,128)(2,1)} %slice.195) | data formatting | bytes 9437184 | tf_op jit(solution)/shard_map/reshape;squeeze | solution.py:200
  128.6 17.7 %all-to-all-done.2 = bf16[4,184,1536]{2,1,0:T(8,128)(2,1)S(1)} async-done(((bf16[4,184,1536]{2,1,0:T(8,128)(2,1)}), bf16[4,184,1536]{2,1,0:T(8,128)(2,1)S(1)}, u32[]{:S(2)}, u32[]{:S(2)}) %all-to-all-start.2) | async-done | bytes 2261024 | tf_op jit(solution)/shard_map/all_to_all | solution.py:256
  147.7 3.8 all-to-all-start
  151.5 25.8 %multiply_convert_fusion.1 = (bf16[736,3072]{1,0:T(8,128)(2,1)S(1)}, f32[736,3072]{1,0:T(8,128)}, f32[736,3072]{1,0:T(8,128)}) fusion(bf16[2,768,3072]{2,1,0:T(8,128)(2,1)} %all-gather.5.cloned.1.call-done, bf16[736,1536]{1,0:T(8,128)(2,1)} %bitcast.117), kind=kOutput, calls=%fused_computation.38 | convolution fusion | flops 3619848192 | bytes 28459008 | tf_op jit(solution)/shard_map/dot_general | solution.py:270
  177.3 3.7 convolution_convert_fusion.3
  181.0 10.8 %fusion.19 = bf16[736,3072]{1,0:T(8,128)(2,1)} fusion(f32[736,3072]{1,0:T(8,128)} %get-tuple-element.111, f32[736,3072]{1,0:T(8,128)} %get-tuple-element.97, bf16[3072,768]{1,0:T(8,128)(2,1)S(1)} %copy-done.16, bf16[736,1536]{1,0:T(8,128)(2,1)} %bitcast.118), kind=kOutput, calls=%fused_computation.37 | convolution fusion | flops 3490971648 | bytes 28459008 | tf_op jit(solution)/shard_map/dot_general | solution.py:267
  191.9 6.1 %fusion.49 = bf16[736,768]{1,0:T(8,128)(2,1)S(1)} fusion(bf16[736,3072]{1,0:T(8,128)(2,1)} %fusion.19, bf16[2,768,3072]{2,1,0:T(8,128)(2,1)S(1)} %bitcast.114), kind=kOutput, calls=%fused_computation.109 | convolution fusion | flops 3473448960 | bytes 10371072 | tf_op jit(solution)/shard_map/dot_general | solution.py:277
  198.0 1.6 pad_maximum_fusion.4
  199.6 5.3 all-to-all-done
  204.9 4.9 all-to-all-start.3
  209.8 26.2 %multiply_convert_fusion = (bf16[768,3072]{1,0:T(8,128)(2,1)S(1)}, f32[768,3072]{1,0:T(8,128)}, f32[768,3072]{1,0:T(8,128)}) fusion(bf16[2,768,3072]{2,1,0:T(8,128)(2,1)} %all-gather.5.cloned.1.call-done, bf16[768,1536]{1,0:T(8,128)(2,1)S(1)} %bitcast.107), kind=kOutput, calls=%fused_computation.16 | convolution fusion | flops 3777232896 | bytes 29491200 | tf_op jit(solution)/shard_map/dot_general | solution.py:270
  236.0 8.1 %convolution_convert_fusion.1 = bf16[768,768]{0,1:T(8,128)(2,1)S(1)} fusion(bf16[768,3072]{1,0:T(8,128)(2,1)S(1)} %get-tuple-element.94, bf16[3072,768]{1,0:T(8,128)(2,1)} %reshape_squeeze.3), kind=kOutput, calls=%fused_computation.107 | convolution fusion | flops 3624468480 | bytes 10616832 | tf_op jit(solution)/shard_map/dot_general | solution.py:274
  244.2 10.1 %fusion.6 = bf16[768,3072]{1,0:T(8,128)(2,1)S(1)} fusion(f32[768,3072]{1,0:T(8,128)} %get-tuple-element.112, f32[768,3072]{1,0:T(8,128)} %get-tuple-element.95, bf16[3072,768]{1,0:T(8,128)(2,1)} %reshape_squeeze.3, bf16[768,1536]{1,0:T(8,128)(2,1)S(1)} %bitcast.108), kind=kOutput, calls=%fused_computation.12 | convolution fusion | flops 3642753024 | bytes 29491200 | tf_op jit(solution)/shard_map/dot_general | solution.py:267
  254.3 8.0 %fusion.48 = bf16[768,768]{0,1:T(8,128)(2,1)S(1)} fusion(bf16[768,3072]{1,0:T(8,128)(2,1)S(1)} %fusion.6, bf16[2,768,3072]{2,1,0:T(8,128)(2,1)} %all-gather.5.cloned.1.call-done), kind=kOutput, calls=%fused_computation.106 | convolution fusion | flops 3624468480 | bytes 10616832 | tf_op jit(solution)/shard_map/dot_general | solution.py:277
  262.4 2.5 copy.111
  264.9 5.1 all-to-all-start.1
  270.2 5.5 fusion.58
  275.7 5.2 fusion.55
  280.9 41.9 %all-to-all-done.1 = bf16[4,192,1536]{2,1,0:T(8,128)(2,1)S(1)} async-done(((bf16[4,192,1536]{2,1,0:T(8,128)(2,1)}), bf16[4,192,1536]{2,1,0:T(8,128)(2,1)S(1)}, u32[]{:S(2)}, u32[]{:S(2)}) %all-to-all-start.1) | async-done | bytes 2359328 | tf_op jit(solution)/shard_map/all_to_all | solution.py:292
  322.8 4.0 convolution_add_fusion.1
  326.9 1.8 convolution_add_fusion
  328.8 1.8 multiply_reduce_fusion.3
  333.3 2.5 fusion.79
  336.8 22.1 %shard_map.179 = (bf16[640,768]{1,0:T(8,128)(2,1)S(1)}, bf16[640,768]{1,0:T(8,128)(2,1)S(1)}, bf16[640,768]{1,0:T(8,128)(2,1)S(1)}) custom-call(bf16[640,2304]{1,0:T(8,128)(2,1)} %copy-done, bf16[640,2304]{1,0:T(8,128)(2,1)} %copy-done, bf16[640,2304]{1,0:T(8,128)(2,1)} %copy-done, bf16[640,768]{1,0:T(8,128)(2,1)S(1)} %pad.20.g_ref), custom_call_target="tpu_custom_call" | custom-call | tf_op jit(solution)/shard_map/pallas_call | solution.py:103
  360.1 5.0 fusion.76
  365.2 2.4 fusion.45
  370.0 4.7 select_maximum_fusion
  374.8 3.8 copy-done.5
  378.5 1.7 fusion.39
  380.2 10.4 %fusion.63 = f32[3072,768]{1,0:T(8,128)} fusion(bf16[768,3072]{1,0:T(8,128)(2,1)} %copy-done.58, bf16[768,1536]{1,0:T(8,128)(2,1)} %bitcast.109), kind=kOutput, calls=%fused_computation.131 | convolution fusion | flops 3623878656 | bytes 15335424 | tf_op jit(solution)/shard_map/dot_general | solution.py:280
  390.6 10.1 %add_convert_fusion = bf16[3072,768]{1,0:T(8,128)(2,1)} fusion(f32[3072,768]{1,0:T(8,128)} %fusion.63, bf16[736,3072]{1,0:T(8,128)(2,1)} %copy-done.59, bf16[736,1536]{1,0:T(8,128)(2,1)S(1)} %bitcast.120), kind=kOutput, calls=%fused_computation.14 | convolution fusion | flops 3477602304 | bytes 19808256 | tf_op jit(solution)/shard_map/dot_general | solution.py:280
  400.8 2.1 bitcast_add_fusion
  403.3 1.5 collective-permute-start.1
  404.8 6.4 %fusion.66 = f32[768,3072]{1,0:T(8,128)} fusion(bf16[768,3072]{1,0:T(8,128)(2,1)S(1)} %bitcast.112, bf16[768,1536]{1,0:T(8,128)(2,1)S(1)} %bitcast.110), kind=kOutput, calls=%fused_computation.134 | convolution fusion | flops 3623878656 | bytes 15335424 | tf_op jit(solution)/shard_map/dot_general | solution.py:283
  412.5 6.6 %collective-permute-done.1 = bf16[2,96,1536]{2,1,0:T(8,128)(2,1)S(1)} collective-permute-done((bf16[2,96,1536]{2,1,0:T(8,128)(2,1)S(1)}, bf16[2,96,1536]{2,1,0:T(8,128)(2,1)S(1)}, u32[]{:S(2)}, u32[]{:S(2)}) %collective-permute-start.1) | collective-permute-done | bytes 589856 | tf_op jit(solution)/shard_map/ppermute | solution.py:119
  420.6 8.2 %collective-permute-done.3 = bf16[2,96,1664]{2,1,0:T(8,128)(2,1)S(1)} collective-permute-done((bf16[2,96,1664]{2,1,0:T(8,128)(2,1)S(1)}, bf16[2,96,1664]{2,1,0:T(8,128)(2,1)S(1)}, u32[]{:S(2)}, u32[]{:S(2)}) %collective-permute-start.3) | collective-permute-done | bytes 639008 | tf_op jit(solution)/shard_map/ppermute | solution.py:119
  430.2 4.2 collective-permute-done.2
  434.4 2.6 collective-permute-done.4
  438.4 11.6 %fusion.26 = bf16[1,768,3072]{2,1,0:T(8,128)(2,1)} fusion(f32[768,3072]{1,0:T(8,128)} %fusion.66, bf16[736,3072]{1,0:T(8,128)(2,1)} %fusion.19, bf16[736,1536]{1,0:T(8,128)(2,1)} %bitcast.119), kind=kOutput, calls=%fused_computation.57 | convolution fusion | flops 3477602304 | bytes 19808256 | tf_op jit(solution)/shard_map/dot_general | solution.py:283
  450.0 8.5 %stack_reshape.4 = bf16[1,768,3072]{2,1,0:T(8,128)(2,1)} reshape(bf16[3072,768]{1,0:T(8,128)(2,1)} %add_convert_fusion) | data formatting | bytes 9437184 | tf_op jit(solution)/shard_map/stack;reshape | solution.py:295
  458.4 8.3 %pad_maximum_fusion = bf16[2,768,3072]{2,1,0:T(8,128)(2,1)} fusion(bf16[1,768,3072]{2,1,0:T(8,128)(2,1)} %stack_reshape.4, bf16[1,768,3072]{2,1,0:T(8,128)(2,1)} %fusion.26), kind=kLoop, calls=%fused_computation.13 | loop fusion | flops 4718592 | bytes 18874368 | tf_op jit(solution)/shard_map/stack | solution.py:295
  466.8 3.1 add_convert_fusion.4
  469.9 6.4 %all-reduce.7.cloned.1.call-done = bf16[96,3200]{1,0:T(8,128)(2,1)} async-done(((bf16[96,3200]{1,0:T(8,128)(2,1)}), bf16[96,3200]{1,0:T(8,128)(2,1)}) %all-reduce.7.cloned.1.call-update) | async-done | bytes 614416 | tf_op jit(solution)/shard_map/psum | solution.py:368
  477.7 2.0 slice.211
  479.7 1.6 slice.212
  483.2 72.9 %reduce-scatter.2.cloned.1.call-done = bf16[2,96,3072]{2,1,0:T(8,128)(2,1)} async-done(((bf16[2,768,3072]{2,1,0:T(8,128)(2,1)}), bf16[2,96,3072]{2,1,0:T(8,128)(2,1)}) %reduce-scatter.2.cloned.1.call-update) | async-done | bytes 1179664 | tf_op jit(solution)/shard_map/reduce_scatter | solution.py:298
  556.0 2.5 fusion.110
  (248 shorter events, 36.1 us)
Async XLA Ops:
  7.2 46.9 %all-gather.3.cloned.1.call-start = ((), (), s32[]{:S(2)}) async-start(), calls=%async_computation.5 | async-start | bytes 5529600 | tf_op jit(solution)/shard_map/all_gather | solution.py:187
  8.8 7.7 %copy-start.39 = (s32[591,2]{0,1:T(2,128)S(1)}, s32[591,2]{0,1:T(2,128)}, u32[]{:S(2)}) copy-start(s32[591,2]{0,1:T(2,128)} %param.13) | copy-start | bytes 14188
  11.6 7.9 %copy-start.6 = (bf16[591,768]{1,0:T(8,128)(2,1)S(1)}, bf16[591,768]{1,0:T(8,128)(2,1)}, u32[]{:S(2)}) copy-start(bf16[591,768]{1,0:T(8,128)(2,1)} %param.11) | copy-start | bytes 2723332
  11.6 103.7 %all-gather.5.cloned.1.call-start = ((), (), s32[]{:S(2)}) async-start(), calls=%async_computation.6 | async-start | bytes 10616832 | tf_op jit(solution)/shard_map/all_gather | solution.py:198
  13.2 6.9 %copy-start.8 = (bf16[591,768]{1,0:T(8,128)(2,1)S(1)}, bf16[591,768]{1,0:T(8,128)(2,1)}, u32[]{:S(2)}) copy-start(bf16[591,768]{1,0:T(8,128)(2,1)} %param.21) | copy-start | bytes 2723332
  19.4 60.5 %copy-start.29 = (f32[591]{0:T(1024)}, f32[591]{0:T(1024)S(1)}, u32[]{:S(2)}) copy-start(f32[591]{0:T(1024)S(1)} %fusion.102) | copy-start | bytes 7096
  19.6 35.8 %copy-start.37 = (f32[591]{0:T(1024)}, f32[591]{0:T(1024)S(1)}, u32[]{:S(2)}) copy-start(f32[591]{0:T(1024)S(1)} %broadcast_multiply_fusion.2) | copy-start | bytes 7096
  20.1 35.3 %copy-start.49 = (f32[591]{0:T(1024)}, f32[591]{0:T(1024)S(1)}, u32[]{:S(2)}) copy-start(f32[591]{0:T(1024)S(1)} %fusion.100) | copy-start | bytes 7096
  25.0 58.4 %copy-start.22 = (bf16[1504,591]{1,0:T(8,128)(2,1)}, bf16[1504,591]{1,0:T(8,128)(2,1)S(1)}, u32[]{:S(2)}) copy-start(bf16[1504,591]{1,0:T(8,128)(2,1)S(1)} %get-tuple-element.101) | copy-start | bytes 5333188
  55.4 5.0 copy-start.47
  55.4 22.2 %copy-start.41 = (f32[768]{0:T(1024)}, f32[768]{0:T(1024)S(1)}, u32[]{:S(2)}) copy-start(f32[768]{0:T(1024)S(1)} %get-tuple-element.78) | copy-start | bytes 9220
  55.8 4.6 copy-start.18
  60.6 13.4 %copy-start = (bf16[640,2304]{1,0:T(8,128)(2,1)}, bf16[640,2304]{1,0:T(8,128)(2,1)S(1)}, u32[]{:S(2)}) copy-start(bf16[640,2304]{1,0:T(8,128)(2,1)S(1)} %pad.18.q_ref.k_ref.v_ref) | copy-start | bytes 8847364
  74.0 3.0 copy-start.1
  76.6 3.8 copy-start.13
  77.6 3.1 copy-start.43
  78.2 18.6 %copy-start.10 = (bf16[591,768]{1,0:T(8,128)(2,1)}, bf16[591,768]{1,0:T(8,128)(2,1)S(1)}, u32[]{:S(2)}) copy-start(bf16[591,768]{1,0:T(8,128)(2,1)S(1)} %multiply_convert_fusion.4) | copy-start | bytes 2723332
  80.4 3.0 copy-start.51
  80.7 5.0 copy-start.25
  89.6 56.7 %all-to-all-start.2 = ((bf16[4,184,1536]{2,1,0:T(8,128)(2,1)}), bf16[4,184,1536]{2,1,0:T(8,128)(2,1)S(1)}, u32[]{:S(2)}, u32[]{:S(2)}) async-start(bf16[4,184,1536]{2,1,0:T(8,128)(2,1)} %pad_maximum_fusion.3), calls=%async_computation.2 | async-start | bytes 4521984 | tf_op jit(solution)/shard_map/all_to_all | solution.py:256
  94.2 2.7 copy-start.23
  94.2 2.8 copy-start.24
  147.7 57.2 %all-to-all-start = ((bf16[4,192,1536]{2,1,0:T(8,128)(2,1)}), bf16[4,192,1536]{2,1,0:T(8,128)(2,1)S(1)}, u32[]{:S(2)}, u32[]{:S(2)}) async-start(bf16[4,192,1536]{2,1,0:T(8,128)(2,1)} %pad_maximum_fusion.1), calls=%async_computation | async-start | bytes 4718592 | tf_op jit(solution)/shard_map/all_to_all | solution.py:256
  151.5 25.8 %copy-start.16 = (bf16[3072,768]{1,0:T(8,128)(2,1)S(1)}, bf16[3072,768]{1,0:T(8,128)(2,1)}, u32[]{:S(2)}) copy-start(bf16[3072,768]{1,0:T(8,128)(2,1)} %reshape_squeeze.3) | copy-start | bytes 14155780
  177.3 3.7 copy-start.59
  177.3 14.5 %slice-start.5 = ((s8[9437184]{0:T(1024)(128)(4,1)}), s8[4194304]{0:T(1024)(128)(4,1)S(1)}, s32[]{:S(2)}) async-start(s8[9437184]{0:T(1024)(128)(4,1)} %bitcast.113), calls=%async_computation.14 | async-start | bytes 8388608
  177.3 14.5 %slice-start.6 = ((s8[9437184]{0:T(1024)(128)(4,1)}), s8[4194304]{0:T(1024)(128)(4,1)S(1)}, s32[]{:S(2)}) async-start(s8[9437184]{0:T(1024)(128)(4,1)} %bitcast.113), calls=%async_computation.15 | async-start | bytes 8388608
  181.0 10.8 %slice-start.7 = ((s8[9437184]{0:T(1024)(128)(4,1)}), s8[1048576]{0:T(1024)(128)(4,1)S(1)}, s32[]{:S(2)}) async-start(s8[9437184]{0:T(1024)(128)(4,1)} %bitcast.113), calls=%async_computation.16 | async-start | bytes 2097152
  204.9 39.3 %copy-start.14 = (bf16[4,192,1536]{2,1,0:T(8,128)(2,1)}, bf16[4,192,1536]{2,1,0:T(8,128)(2,1)S(1)}, u32[]{:S(2)}) copy-start(bf16[4,192,1536]{2,1,0:T(8,128)(2,1)S(1)} %all-to-all-done) | copy-start | bytes 7077892
  204.9 60.0 %all-to-all-start.3 = ((bf16[4,184,1536]{2,1,0:T(8,128)(2,1)}), bf16[4,184,1536]{2,1,0:T(8,128)(2,1)}, u32[]{:S(2)}, u32[]{:S(2)}) async-start(bf16[4,184,1536]{2,1,0:T(8,128)(2,1)} %bitcast.15), calls=%async_computation.3 | async-start | bytes 4521984 | tf_op jit(solution)/shard_map/all_to_all | solution.py:292
  236.0 8.1 %copy-start.58 = (bf16[768,3072]{1,0:T(8,128)(2,1)}, bf16[768,3072]{1,0:T(8,128)(2,1)S(1)}, u32[]{:S(2)}) copy-start(bf16[768,3072]{1,0:T(8,128)(2,1)S(1)} %get-tuple-element.94) | copy-start | bytes 14155780
  254.3 8.0 %copy-start.17 = (bf16[768,3072]{1,0:T(8,128)(2,1)}, bf16[768,3072]{1,0:T(8,128)(2,1)S(1)}, u32[]{:S(2)}) copy-start(bf16[768,3072]{1,0:T(8,128)(2,1)S(1)} %fusion.6) | copy-start | bytes 14155780
  262.4 7.7 %copy-start.52 = (f32[591,2]{0,1:T(2,128)S(1)}, f32[591,2]{0,1:T(2,128)}, u32[]{:S(2)}) copy-start(f32[591,2]{0,1:T(2,128)} %copy-done.51) | copy-start | bytes 14188
  264.9 57.9 %all-to-all-start.1 = ((bf16[4,192,1536]{2,1,0:T(8,128)(2,1)}), bf16[4,192,1536]{2,1,0:T(8,128)(2,1)S(1)}, u32[]{:S(2)}, u32[]{:S(2)}) async-start(bf16[4,192,1536]{2,1,0:T(8,128)(2,1)} %bitcast.10), calls=%async_computation.1 | async-start | bytes 4718592 | tf_op jit(solution)/shard_map/all_to_all | solution.py:292
  270.0 206.4 %all-reduce.7.cloned.1.call-start = ((), (), s32[]{:S(2)}) async-start(), calls=%async_computation.7 | async-start | bytes 1228800 | tf_op jit(solution)/shard_map/psum | solution.py:368
  270.2 5.5 copy-start.28
  322.8 4.0 copy-start.57
  322.8 8.2 %slice-start.8 = ((s8[4915200]{0:T(1024)(128)(4,1)}), s8[4194304]{0:T(1024)(128)(4,1)S(1)}, s32[]{:S(2)}) async-start(s8[4915200]{0:T(1024)(128)(4,1)} %bitcast.125), calls=%async_computation.17 | async-start | bytes 8388608
  326.9 4.1 slice-start.9
  328.7 1.9 copy-start.32
  328.8 1.9 copy-start.36
  328.8 1.9 copy-start.11
  328.8 2.2 copy-start.34
  328.8 2.2 copy-start.42
  328.8 2.2 copy-start.44
  360.1 5.0 copy-start.7
  360.1 5.0 copy-start.38
  360.1 5.0 copy-start.48
  365.1 2.5 copy-start.54
  365.1 3.7 copy-start.50
  374.7 3.8 copy-start.5
  380.2 20.5 %collective-permute-start = (bf16[2,2,96,3200]{3,2,1,0:T(8,128)(2,1)}, bf16[2,2,96,3200]{3,2,1,0:T(8,128)(2,1)}, u32[]{:S(2)}, u32[]{:S(2)}) collective-permute-start(bf16[2,2,96,3200]{3,2,1,0:T(8,128)(2,1)} %fusion.39), channel_id=1, source_target_pairs={{0,1},{1,0},{2,3},{3,2},{4,5},{5,4},{6,7},{7,6},{8,9},{9,8},{10,11... | collective-permute-start | bytes 7372808 | tf_op jit(solution)/shard_map/ppermute | solution.py:119
  380.2 10.4 %copy-start.21 = (bf16[4,184,1536]{2,1,0:T(8,128)(2,1)S(1)}, bf16[4,184,1536]{2,1,0:T(8,128)(2,1)}, u32[]{:S(2)}) copy-start(bf16[4,184,1536]{2,1,0:T(8,128)(2,1)} %copy-done.20) | copy-start | bytes 6782980
  380.2 20.5 %slice-start = ((s8[9830400]{0:T(1024)(128)(4,1)}), s8[4194304]{0:T(1024)(128)(4,1)S(1)}, s32[]{:S(2)}) async-start(s8[9830400]{0:T(1024)(128)(4,1)} %bitcast.104), calls=%async_computation.9 | async-start | bytes 8388608
  380.2 20.5 %slice-start.1 = ((s8[9830400]{0:T(1024)(128)(4,1)}), s8[4194304]{0:T(1024)(128)(4,1)S(1)}, s32[]{:S(2)}) async-start(s8[9830400]{0:T(1024)(128)(4,1)} %bitcast.104), calls=%async_computation.10 | async-start | bytes 8388608
  380.2 24.6 %slice-start.3 = ((s8[4718592]{0:T(1024)(128)(4,1)}), s8[4194304]{0:T(1024)(128)(4,1)S(1)}, s32[]{:S(2)}) async-start(s8[4718592]{0:T(1024)(128)(4,1)} %bitcast.111), calls=%async_computation.12 | async-start | bytes 8388608
  390.6 10.1 %slice-start.2 = ((s8[9830400]{0:T(1024)(128)(4,1)}), s8[1441792]{0:T(1024)(128)(4,1)S(1)}, s32[]{:S(2)}) async-start(s8[9830400]{0:T(1024)(128)(4,1)} %bitcast.104), calls=%async_computation.11 | async-start | bytes 2883584
  390.6 14.2 %slice-start.4 = ((s8[4718592]{0:T(1024)(128)(4,1)}), s8[524288]{0:T(1024)(128)(4,1)S(1)}, s32[]{:S(2)}) async-start(s8[4718592]{0:T(1024)(128)(4,1)} %bitcast.111), calls=%async_computation.13 | async-start | bytes 1048576
  402.9 1.9 copy-start.15
  403.3 15.8 %collective-permute-start.1 = (bf16[2,96,1536]{2,1,0:T(8,128)(2,1)S(1)}, bf16[2,96,1536]{2,1,0:T(8,128)(2,1)S(1)}, u32[]{:S(2)}, u32[]{:S(2)}) collective-permute-start(bf16[2,96,1536]{2,1,0:T(8,128)(2,1)S(1)} %fusion.84), channel_id=1, source_target_pairs={{0,2},{1,3},{2,0},{3,1},{4,6},{5,7},{6,4},{7,5},{8,10},{9,11},{10,... | collective-permute-start | bytes 1769480 | tf_op jit(solution)/shard_map/ppermute | solution.py:119
  411.4 17.3 %collective-permute-start.3 = (bf16[2,96,1664]{2,1,0:T(8,128)(2,1)S(1)}, bf16[2,96,1664]{2,1,0:T(8,128)(2,1)S(1)}, u32[]{:S(2)}, u32[]{:S(2)}) collective-permute-start(bf16[2,96,1664]{2,1,0:T(8,128)(2,1)S(1)} %fusion.82), channel_id=1, source_target_pairs={{0,4},{1,5},{2,6},{3,7},{4,0},{5,1},{6,2},{7,3},{8,12},{9,13},{10,... | collective-permute-start | bytes 1916936 | tf_op jit(solution)/shard_map/ppermute | solution.py:119
  419.3 15.1 %collective-permute-start.2 = (bf16[96,1536]{1,0:T(8,128)(2,1)S(1)}, bf16[96,1536]{1,0:T(8,128)(2,1)S(1)}, u32[]{:S(2)}, u32[]{:S(2)}) collective-permute-start(bf16[96,1536]{1,0:T(8,128)(2,1)S(1)} %fusion.87), channel_id=1, source_target_pairs={{0,4},{1,5},{2,6},{3,7},{4,0},{5,1},{6,2},{7,3},{8,12},{9,13},{10,... | collective-permute-start | bytes 884744 | tf_op jit(solution)/shard_map/ppermute | solution.py:119
  428.9 8.1 %collective-permute-start.4 = (bf16[96,1664]{1,0:T(8,128)(2,1)S(1)}, bf16[96,1664]{1,0:T(8,128)(2,1)S(1)}, u32[]{:S(2)}, u32[]{:S(2)}) collective-permute-start(bf16[96,1664]{1,0:T(8,128)(2,1)S(1)} %fusion.86), channel_id=1, source_target_pairs={{0,2},{1,3},{2,0},{3,1},{4,6},{5,7},{6,4},{7,5},{8,10},{9,11},{10,... | collective-permute-start | bytes 958472 | tf_op jit(solution)/shard_map/ppermute | solution.py:119
  438.0 118.0 %reduce-scatter.2.cloned.1.call-start = ((), (), s32[]{:S(2)}) async-start(), calls=%async_computation.8 | async-start | bytes 10616832 | tf_op jit(solution)/shard_map/reduce_scatter | solution.py:298
  (19 other events, 25.2 us)
Sparse Core Ops, SparseCore 0:
  11.7 42.3 all-gather.2
  56.5 58.6 all-gather.4
  438.1 38.1 all-reduce.6
  479.7 76.3 reduce-scatter.1

commit v12 on v9

--- a/solution.py
+++ b/solution.py
@@ -139,6 +139,33 @@
     return jnp.concatenate([first, second], axis=-1)
 
 
+def _gather_back(values, bit, axis_name, size, index):
+    n_bits = size.bit_length() - 1
+    mine = (index >> bit) & 1
+    pairs = [(i, i ^ (1 << bit)) for i in range(size)]
+    got = lax.ppermute(values, axis_name, pairs)
+    low = jnp.where(mine == 0, values, got)
+    high = jnp.where(mine == 0, got, values)
+    return jnp.stack([low, high], axis=n_bits - 1 - bit)
+
+
+def expert_all_reduce(values, axis_name):
+    size = lax.axis_size(axis_name)
+    index = lax.axis_index(axis_name)
+    n_bits = size.bit_length() - 1
+    rows = values.shape[0]
+    if rows % size:
+        return lax.psum(values.astype(jnp.bfloat16), axis_name).astype(jnp.float32)
+    bits = list(range(n_bits - 1, -1, -1))
+    parts = values.astype(jnp.float32).reshape([2] * n_bits + [rows // size, values.shape[1]])
+    for bit in range(n_bits):
+        parts, bits = _exchange(parts, bits, bit, axis_name, size, index)
+    parts = parts.astype(jnp.bfloat16)
+    for bit in range(n_bits - 1, -1, -1):
+        parts = _gather_back(parts, bit, axis_name, size, index)
+    return parts.reshape(rows, values.shape[1]).astype(jnp.float32)
+
+
 def layer_norm(values, norm_gain):
     row_mean = jnp.mean(values, axis=-1, keepdims=True)
     centered = values - row_mean
@@ -367,8 +394,16 @@
     )
     small = jnp.pad(small, ((0, 0), (0, 128 - small.shape[1])))
     dense_grads = jnp.concatenate([grad_qkv, grad_wout, small], axis=1)
-    dense_share = shard_reduce_scatter(dense_grads, "shard", 128 * (dense_grads.shape[1] // 256))
-    dense_total = lax.psum(dense_share.astype(jnp.bfloat16), "expert").astype(jnp.float32)
+    chunk_cols = 128 * (dense_grads.shape[1] // 256)
+    dense_total = jnp.concatenate(
+        [
+            expert_all_reduce(
+                shard_reduce_scatter(part, "shard", 128 * (part.shape[1] // 256)), "expert"
+            )
+            for part in (dense_grads[:, :chunk_cols], dense_grads[:, chunk_cols:])
+        ],
+        axis=1,
+    )
     return (
         output,
         grad_tokens,

time: 575 us -> 475 us (0.83)
  waiting for transfers between devices: 209 us -> 108 us
  starting transfers between devices: 24.1 us -> 39 us
  other arithmetic: 41.5 us -> 33.9 us
    reduce_scatter x1, waiting for transfers between devices: 72.9 us -> 0.01 us  [shards(): lax.psum_scatter(expert_grads, 'shard', scatter_dimension=1, tiled=True)]
    all_to_all x2, waiting for transfers between devices: 41.9 us -> 0.05 us  [shards(): lax.all_to_all(returning, 'expert', split_axis=0, concat_axis=0, tiled=True)]
    ppermute x0 -> x4, waiting for transfers between devices: none -> 11.5 us  [_gather_back(): got = lax.ppermute(values, axis_name, pairs)]
    ppermute x5 -> x14, starting transfers between devices: 5.14 us -> 15.3 us  [_exchange(): got = lax.ppermute(send.astype(jnp.bfloat16), axis_name, pairs)]
    ppermute x5 -> x14, waiting for transfers between devices: 21.6 us -> 31 us  [_exchange(): got = lax.ppermute(send.astype(jnp.bfloat16), axis_name, pairs)]
    psum x1 -> x0, waiting for transfers between devices: 6.43 us -> none  [shards(): lax.psum(dense_share.astype(jnp.bfloat16), 'expert').astype(jnp.float32)]
  transfers between devices with their start and end apart: 13 -> 25, of which waited for: 11 -> 16; matrix products, arithmetic and copies ran while one was open for 41% -> 54% of each run, Pallas kernels for 2% -> 8%
where the time goes in v12:
time: 475 us; the launch traced here: 467 us
  matrix products  186 us (39%)
  waiting for transfers between devices  108 us (23%)
  local copies, waits for them, and re-layouts  48.6 us (10%)
  starting transfers between devices  39 us (8%)
  Pallas kernels  35.2 us (7%)
  other arithmetic  33.9 us (7%)
  between operations  16.4 us (3%)
    dot_general x2, matrix products, shards(): jnp.dot(flat_arrived, expert_first, preferred_element_type=jnp.float32)  52 us
    ppermute x14, waiting for transfers between devices, _exchange(): got = lax.ppermute(send.astype(jnp.bfloat16), axis_name, pairs)  31 us
    all_gather x1, waiting for transfers between devices, shards(): dense_full = lax.all_gather(dense_local, 'shard', axis=0, tiled=True)  29.1 us
    all_to_all x2, waiting for transfers between devices, shards(): lax.all_to_all(dispatch_rows(experts * start, experts * (start + size)).r...  23 us
    dot_general x2, matrix products, shards(): lax.dot_general(flat_grad, expert_second, COL_CONTRACT, preferred_element...  22.5 us
    pallas_call x1, Pallas kernels, attention_bwd(): pl.pallas_call(functools.partial(attn_bwd_kernel, images=images), grid=(p...  21.8 us
    dot_general x2, matrix products, shards(): lax.dot_general(activated, flat_grad, ROW_CONTRACT, preferred_element_typ...  20.4 us
    ppermute x14, starting transfers between devices, _exchange(): got = lax.ppermute(send.astype(jnp.bfloat16), axis_name, pairs)  15.3 us
  transfers between devices with their start and end apart: 25, of which 16 were waited for; matrix products, arithmetic and copies ran while one was open for 54% of the time, Pallas kernels for 8%

profile of v12, /device:TPU:0, one launch (start us, length us, event | category | flops | bytes accessed | tf_op | source)
XLA Modules:
  0.0 466.9 jit_solution(6492518723860786335)
XLA Ops:
  9.6 1.9 concatenate.52
  11.6 1.5 stack_reshape_squeeze.3
  13.2 2.3 pad_maximum_fusion.6
  21.6 3.3 fusion.115
  24.9 29.1 %all-gather.3.cloned.1.call-done = bf16[768,3078]{1,0:T(8,128)(2,1)} async-done(((bf16[96,3078]{1,0:T(8,128)(2,1)}), bf16[768,3078]{1,0:T(8,128)(2,1)}) %all-gather.3.cloned.1.call-update) | async-done | bytes 4727824 | tf_op jit(solution)/shard_map/all_gather | solution.py:217
  55.8 4.6 convolution_convert_fusion
  60.6 13.4 %shard_map.178 = bf16[640,768]{1,0:T(8,128)(2,1)S(1)} custom-call(bf16[640,2304]{1,0:T(8,128)(2,1)S(1)} %pad.18.q_ref.k_ref.v_ref, bf16[640,2304]{1,0:T(8,128)(2,1)S(1)} %pad.18.q_ref.k_ref.v_ref, bf16[640,2304]{1,0:T(8,128)(2,1)S(1)} %pad.18.q_ref.k_ref.v_ref), custom_call_target="tpu_custom_call" | custom-call | tf_op jit(solution)/shard_map/pallas_call | solution.py:90
  74.1 2.6 fusion.122
  78.2 1.5 fusion.123
  80.7 2.7 fusion.60
  83.4 2.3 convolution_convert_fusion.4
  85.7 2.4 add_convert_fusion.3
  88.1 1.6 pad_maximum_fusion.4
  89.6 4.6 all-to-all-start.2
  94.8 3.0 fusion.53
  100.8 1.6 pad_maximum_fusion.2
  102.4 12.9 %all-gather.5.cloned.1.call-done = bf16[2,768,3072]{2,1,0:T(8,128)(2,1)} async-done(((bf16[2,96,3072]{2,1,0:T(8,128)(2,1)}), bf16[2,768,3072]{2,1,0:T(8,128)(2,1)}) %all-gather.5.cloned.1.call-update) | async-done | bytes 9437200 | tf_op jit(solution)/shard_map/all_gather | solution.py:228
  115.3 4.9 %slice.211 = bf16[1,768,3072]{2,1,0:T(8,128)(2,1)} slice(bf16[2,768,3072]{2,1,0:T(8,128)(2,1)} %all-gather.5.cloned.1.call-done), slice={[1:2], [0:768], [0:3072]} | slice | bytes 9437184 | tf_op jit(solution)/shard_map/slice | solution.py:230
  120.1 8.5 %reshape_squeeze.3 = bf16[3072,768]{1,0:T(8,128)(2,1)} reshape(bf16[1,768,3072]{2,1,0:T(8,128)(2,1)} %slice.211) | data formatting | bytes 9437184 | tf_op jit(solution)/shard_map/reshape;squeeze | solution.py:230
  128.6 17.7 %all-to-all-done.2 = bf16[4,184,1536]{2,1,0:T(8,128)(2,1)S(1)} async-done(((bf16[4,184,1536]{2,1,0:T(8,128)(2,1)}), bf16[4,184,1536]{2,1,0:T(8,128)(2,1)S(1)}, u32[]{:S(2)}, u32[]{:S(2)}) %all-to-all-start.2) | async-done | bytes 2261024 | tf_op jit(solution)/shard_map/all_to_all | solution.py:286
  147.8 3.8 all-to-all-start
  151.6 25.8 %multiply_convert_fusion.1 = (bf16[736,3072]{1,0:T(8,128)(2,1)S(1)}, f32[736,3072]{1,0:T(8,128)}, f32[736,3072]{1,0:T(8,128)}) fusion(bf16[2,768,3072]{2,1,0:T(8,128)(2,1)} %all-gather.5.cloned.1.call-done, bf16[736,1536]{1,0:T(8,128)(2,1)} %bitcast.179), kind=kOutput, calls=%fused_computation.36 | convolution fusion | flops 3619848192 | bytes 28459008 | tf_op jit(solution)/shard_map/dot_general | solution.py:300
  177.4 3.7 convolution_convert_fusion.3
  181.1 10.8 %fusion.19 = bf16[736,3072]{1,0:T(8,128)(2,1)} fusion(f32[736,3072]{1,0:T(8,128)} %get-tuple-element.112, f32[736,3072]{1,0:T(8,128)} %get-tuple-element.88, bf16[3072,768]{1,0:T(8,128)(2,1)S(1)} %copy-done.18, bf16[736,1536]{1,0:T(8,128)(2,1)} %bitcast.180), kind=kOutput, calls=%fused_computation.35 | convolution fusion | flops 3490971648 | bytes 28459008 | tf_op jit(solution)/shard_map/dot_general | solution.py:297
  191.9 6.1 %fusion.49 = bf16[736,768]{1,0:T(8,128)(2,1)S(1)} fusion(bf16[736,3072]{1,0:T(8,128)(2,1)} %fusion.19, bf16[2,768,3072]{2,1,0:T(8,128)(2,1)S(1)} %bitcast.177), kind=kOutput, calls=%fused_computation.112 | convolution fusion | flops 3473448960 | bytes 10371072 | tf_op jit(solution)/shard_map/dot_general | solution.py:307
  198.0 1.6 pad_maximum_fusion.5
  199.6 5.3 %all-to-all-done = bf16[4,192,1536]{2,1,0:T(8,128)(2,1)S(1)} async-done(((bf16[4,192,1536]{2,1,0:T(8,128)(2,1)}), bf16[4,192,1536]{2,1,0:T(8,128)(2,1)S(1)}, u32[]{:S(2)}, u32[]{:S(2)}) %all-to-all-start) | async-done | bytes 2359328 | tf_op jit(solution)/shard_map/all_to_all | solution.py:286
  204.9 4.9 %all-to-all-start.3 = ((bf16[4,184,1536]{2,1,0:T(8,128)(2,1)}), bf16[4,184,1536]{2,1,0:T(8,128)(2,1)}, u32[]{:S(2)}, u32[]{:S(2)}) async-start(bf16[4,184,1536]{2,1,0:T(8,128)(2,1)} %bitcast.15), calls=%async_computation.3 | async-start | bytes 4521984 | tf_op jit(solution)/shard_map/all_to_all | solution.py:322
  209.8 26.2 %multiply_convert_fusion = (bf16[768,3072]{1,0:T(8,128)(2,1)S(1)}, f32[768,3072]{1,0:T(8,128)}, f32[768,3072]{1,0:T(8,128)}) fusion(bf16[2,768,3072]{2,1,0:T(8,128)(2,1)} %all-gather.5.cloned.1.call-done, bf16[768,1536]{1,0:T(8,128)(2,1)S(1)} %bitcast.168), kind=kOutput, calls=%fused_computation.14 | convolution fusion | flops 3777232896 | bytes 29491200 | tf_op jit(solution)/shard_map/dot_general | solution.py:300
  236.0 11.8 %fusion.6 = bf16[768,3072]{1,0:T(8,128)(2,1)S(1)} fusion(f32[768,3072]{1,0:T(8,128)} %get-tuple-element.113, f32[768,3072]{1,0:T(8,128)} %get-tuple-element.86, bf16[3072,768]{1,0:T(8,128)(2,1)} %reshape_squeeze.3, bf16[768,1536]{1,0:T(8,128)(2,1)S(1)} %bitcast.169), kind=kOutput, calls=%fused_computation.10 | convolution fusion | flops 3642753024 | bytes 29491200 | tf_op jit(solution)/shard_map/dot_general | solution.py:297
  247.8 8.1 %convolution_convert_fusion.1 = bf16[768,768]{0,1:T(8,128)(2,1)S(1)} fusion(bf16[768,3072]{1,0:T(8,128)(2,1)S(1)} %get-tuple-element.85, bf16[3072,768]{1,0:T(8,128)(2,1)} %reshape_squeeze.3), kind=kOutput, calls=%fused_computation.110 | convolution fusion | flops 3624468480 | bytes 10616832 | tf_op jit(solution)/shard_map/dot_general | solution.py:304
  256.0 6.3 %fusion.48 = bf16[768,768]{0,1:T(8,128)(2,1)S(1)} fusion(bf16[768,3072]{1,0:T(8,128)(2,1)S(1)} %fusion.6, bf16[2,768,3072]{2,1,0:T(8,128)(2,1)} %all-gather.5.cloned.1.call-done), kind=kOutput, calls=%fused_computation.109 | convolution fusion | flops 3624468480 | bytes 10616832 | tf_op jit(solution)/shard_map/dot_general | solution.py:307
  262.4 2.5 copy.113
  264.9 10.3 %fusion.65 = f32[3072,768]{1,0:T(8,128)} fusion(bf16[768,3072]{1,0:T(8,128)(2,1)} %copy-done.63, bf16[768,1536]{1,0:T(8,128)(2,1)} %bitcast.170), kind=kOutput, calls=%fused_computation.132 | convolution fusion | flops 3623878656 | bytes 15335424 | tf_op jit(solution)/shard_map/dot_general | solution.py:310
  275.2 5.2 %all-to-all-start.1 = ((bf16[4,192,1536]{2,1,0:T(8,128)(2,1)}), bf16[4,192,1536]{2,1,0:T(8,128)(2,1)}, u32[]{:S(2)}, u32[]{:S(2)}) async-start(bf16[4,192,1536]{2,1,0:T(8,128)(2,1)} %bitcast.10), calls=%async_computation.1 | async-start | bytes 4718592 | tf_op jit(solution)/shard_map/all_to_all | solution.py:322
  280.4 10.1 %add_convert_fusion = bf16[3072,768]{1,0:T(8,128)(2,1)} fusion(f32[3072,768]{1,0:T(8,128)} %fusion.65, bf16[736,3072]{1,0:T(8,128)(2,1)} %copy-done.64, bf16[736,1536]{1,0:T(8,128)(2,1)S(1)} %bitcast.181), kind=kOutput, calls=%fused_computation.12 | convolution fusion | flops 3477602304 | bytes 19808256 | tf_op jit(solution)/shard_map/dot_general | solution.py:310
  290.5 8.6 %stack_reshape.4 = bf16[1,768,3072]{2,1,0:T(8,128)(2,1)} reshape(bf16[3072,768]{1,0:T(8,128)(2,1)} %add_convert_fusion) | data formatting | bytes 9437184 | tf_op jit(solution)/shard_map/stack;reshape | solution.py:325
  299.1 5.9 %fusion.68 = f32[768,3072]{1,0:T(8,128)S(1)} fusion(bf16[768,3072]{1,0:T(8,128)(2,1)} %copy-done.19, bf16[768,1536]{1,0:T(8,128)(2,1)S(1)} %bitcast.171), kind=kOutput, calls=%fused_computation.135 | convolution fusion | flops 3623878656 | bytes 15335424 | tf_op jit(solution)/shard_map/dot_general | solution.py:313
  305.0 7.9 %fusion.27 = bf16[1,768,3072]{2,1,0:T(8,128)(2,1)} fusion(f32[768,3072]{1,0:T(8,128)S(1)} %fusion.68, bf16[736,3072]{1,0:T(8,128)(2,1)} %fusion.19, bf16[736,1536]{1,0:T(8,128)(2,1)S(1)} %bitcast.182), kind=kOutput, calls=%fused_computation.57 | convolution fusion | flops 3477602304 | bytes 19808256 | tf_op jit(solution)/shard_map/dot_general | solution.py:313
  312.9 8.3 %pad_maximum_fusion = bf16[2,768,3072]{2,1,0:T(8,128)(2,1)} fusion(bf16[1,768,3072]{2,1,0:T(8,128)(2,1)} %stack_reshape.4, bf16[1,768,3072]{2,1,0:T(8,128)(2,1)} %fusion.27), kind=kLoop, calls=%fused_computation.11 | loop fusion | flops 4718592 | bytes 18874368 | tf_op jit(solution)/shard_map/stack | solution.py:325
  322.4 5.5 %fusion.58 = f32[591,1536]{1,0:T(8,128)} fusion(bf16[736,1536]{1,0:T(8,128)(2,1)} %bitcast.16, pred[1504,591]{1,0:T(32,128)(4,1)S(1)} %copy-done.31), kind=kOutput, calls=%fused_computation.124 | convolution fusion | flops 1336246272 | bytes 6363136 | tf_op jit(solution)/shard_map/dot_general | solution.py:338
  327.9 5.4 %fusion.55 = f32[591,1536]{1,0:T(8,128)} fusion(bf16[736,1536]{1,0:T(8,128)(2,1)} %bitcast.16, pred[1504,591]{1,0:T(32,128)(4,1)S(1)} %copy-done.30), kind=kOutput, calls=%fused_computation.121 | convolution fusion | flops 1336246272 | bytes 6363136 | tf_op jit(solution)/shard_map/dot_general | solution.py:341
  333.3 6.1 %convolution_add_fusion.1 = f32[591,1536]{1,0:T(8,128)S(1)} fusion(f32[591,1536]{1,0:T(8,128)} %fusion.58, bf16[768,1536]{1,0:T(8,128)(2,1)} %bitcast.11, pred[1504,591]{1,0:T(32,128)(4,1)S(1)} %copy-done.31), kind=kOutput, calls=%fused_computation.60 | convolution fusion | flops 1395251712 | bytes 10113024 | tf_op jit(solution)/shard_map/dot_general | solution.py:338
  339.5 3.7 convolution_add_fusion
  343.3 1.9 multiply_reduce_fusion.3
  348.7 21.8 %shard_map.179 = (bf16[640,768]{1,0:T(8,128)(2,1)S(1)}, bf16[640,768]{1,0:T(8,128)(2,1)S(1)}, bf16[640,768]{1,0:T(8,128)(2,1)S(1)}) custom-call(bf16[640,2304]{1,0:T(8,128)(2,1)} %copy-done, bf16[640,2304]{1,0:T(8,128)(2,1)} %copy-done, bf16[640,2304]{1,0:T(8,128)(2,1)} %copy-done, bf16[640,768]{1,0:T(8,128)(2,1)S(1)} %pad.20.g_ref), custom_call_target="tpu_custom_call" | custom-call | tf_op jit(solution)/shard_map/pallas_call | solution.py:106
  371.8 2.4 fusion.45
  375.7 5.2 %fusion.78 = f32[768,2304]{1,0:T(8,128)S(1)} fusion(bf16[640,2304]{1,0:T(8,128)(2,1)} %copy-done.17, bf16[591,768]{1,0:T(8,128)(2,1)} %copy-done.20), kind=kOutput, calls=%fused_computation.146 | convolution fusion | flops 2264924160 | bytes 10934784 | tf_op jit(solution)/shard_map/dot_general | solution.py:382
  385.6 2.0 add_convert_fusion.4
  393.2 10.4 %collective-permute-done.3 = bf16[2,96,768]{2,1,0:T(8,128)(2,1)S(1)} collective-permute-done((bf16[2,96,768]{2,1,0:T(8,128)(2,1)S(1)}, bf16[2,96,768]{2,1,0:T(8,128)(2,1)S(1)}, u32[]{:S(2)}, u32[]{:S(2)}) %collective-permute-start.3) | collective-permute-done | bytes 294944 | tf_op jit(solution)/shard_map/ppermute | solution.py:122
  405.8 4.1 collective-permute-done.10
  410.0 1.6 collective-permute-start.11
  414.2 1.6 collective-permute-start.5
  417.0 2.5 collective-permute-done.5
  419.5 2.5 collective-permute-start.6
  422.1 2.8 collective-permute-done.6
  424.9 2.6 collective-permute-start.7
  427.4 2.3 collective-permute-start.14
  430.2 3.6 collective-permute-done.14
  434.0 2.4 collective-permute-start.8
  436.5 5.0 %collective-permute-done.15 = bf16[24,1664]{1,0:T(8,128)(2,1)S(1)} collective-permute-done((bf16[24,1664]{1,0:T(8,128)(2,1)S(1)}, bf16[24,1664]{1,0:T(8,128)(2,1)S(1)}, u32[]{:S(2)}, u32[]{:S(2)}) %collective-permute-start.15) | collective-permute-done | bytes 79904 | tf_op jit(solution)/shard_map/ppermute | solution.py:122
  441.6 5.9 %collective-permute-done.16 = bf16[24,1664]{1,0:T(8,128)(2,1)S(1)} collective-permute-done((bf16[24,1664]{1,0:T(8,128)(2,1)S(1)}, bf16[24,1664]{1,0:T(8,128)(2,1)S(1)}, u32[]{:S(2)}, u32[]{:S(2)}) %collective-permute-start.16) | collective-permute-done | bytes 79904 | tf_op jit(solution)/shard_map/ppermute | solution.py:146
  447.7 5.2 %collective-permute-done.17 = bf16[2,24,1664]{2,1,0:T(8,128)(2,1)S(1)} collective-permute-done((bf16[2,24,1664]{2,1,0:T(8,128)(2,1)S(1)}, bf16[2,24,1664]{2,1,0:T(8,128)(2,1)S(1)}, u32[]{:S(2)}, u32[]{:S(2)}) %collective-permute-start.17) | collective-permute-done | bytes 159776 | tf_op jit(solution)/shard_map/ppermute | solution.py:146
  456.1 2.5 fusion.121
  (299 shorter events, 46.2 us)
Async XLA Ops:
  7.2 46.9 %all-gather.3.cloned.1.call-start = ((), (), s32[]{:S(2)}) async-start(), calls=%async_computation.5 | async-start | bytes 5529600 | tf_op jit(solution)/shard_map/all_gather | solution.py:217
  8.8 7.7 %copy-start.44 = (s32[591,2]{0,1:T(2,128)S(1)}, s32[591,2]{0,1:T(2,128)}, u32[]{:S(2)}) copy-start(s32[591,2]{0,1:T(2,128)} %param.13) | copy-start | bytes 14188
  11.6 7.9 %copy-start.5 = (bf16[591,768]{1,0:T(8,128)(2,1)S(1)}, bf16[591,768]{1,0:T(8,128)(2,1)}, u32[]{:S(2)}) copy-start(bf16[591,768]{1,0:T(8,128)(2,1)} %param.11) | copy-start | bytes 2723332
  11.6 103.7 %all-gather.5.cloned.1.call-start = ((), (), s32[]{:S(2)}) async-start(), calls=%async_computation.6 | async-start | bytes 10616832 | tf_op jit(solution)/shard_map/all_gather | solution.py:228
  13.2 6.9 %copy-start.7 = (bf16[591,768]{1,0:T(8,128)(2,1)S(1)}, bf16[591,768]{1,0:T(8,128)(2,1)}, u32[]{:S(2)}) copy-start(bf16[591,768]{1,0:T(8,128)(2,1)} %param.21) | copy-start | bytes 2723332
  19.4 60.5 %copy-start.34 = (f32[591]{0:T(1024)}, f32[591]{0:T(1024)S(1)}, u32[]{:S(2)}) copy-start(f32[591]{0:T(1024)S(1)} %fusion.112) | copy-start | bytes 7096
  19.6 35.8 %copy-start.42 = (f32[591]{0:T(1024)}, f32[591]{0:T(1024)S(1)}, u32[]{:S(2)}) copy-start(f32[591]{0:T(1024)S(1)} %broadcast_multiply_fusion.2) | copy-start | bytes 7096
  20.1 35.3 %copy-start.54 = (f32[591]{0:T(1024)}, f32[591]{0:T(1024)S(1)}, u32[]{:S(2)}) copy-start(f32[591]{0:T(1024)S(1)} %fusion.110) | copy-start | bytes 7096
  24.9 58.5 %copy-start.24 = (bf16[1504,591]{1,0:T(8,128)(2,1)}, bf16[1504,591]{1,0:T(8,128)(2,1)S(1)}, u32[]{:S(2)}) copy-start(bf16[1504,591]{1,0:T(8,128)(2,1)S(1)} %get-tuple-element.102) | copy-start | bytes 5333188
  55.4 5.0 %copy-start.52 = (f32[768]{0:T(1024)}, f32[768]{0:T(1024)S(1)}, u32[]{:S(2)}) copy-start(f32[768]{0:T(1024)S(1)} %get-tuple-element.70) | copy-start | bytes 9220
  55.4 22.3 %copy-start.46 = (f32[768]{0:T(1024)}, f32[768]{0:T(1024)S(1)}, u32[]{:S(2)}) copy-start(f32[768]{0:T(1024)S(1)} %get-tuple-element.69) | copy-start | bytes 9220
  55.8 4.6 copy-start.20
  60.6 13.4 %copy-start = (bf16[640,2304]{1,0:T(8,128)(2,1)}, bf16[640,2304]{1,0:T(8,128)(2,1)S(1)}, u32[]{:S(2)}) copy-start(bf16[640,2304]{1,0:T(8,128)(2,1)S(1)} %pad.18.q_ref.k_ref.v_ref) | copy-start | bytes 8847364
  76.7 3.7 copy-start.14
  76.7 3.2 copy-start.38
  77.7 3.0 copy-start.48
  78.2 19.6 %copy-start.10 = (bf16[591,768]{1,0:T(8,128)(2,1)}, bf16[591,768]{1,0:T(8,128)(2,1)S(1)}, u32[]{:S(2)}) copy-start(bf16[591,768]{1,0:T(8,128)(2,1)S(1)} %multiply_convert_fusion.4) | copy-start | bytes 2723332
  80.7 5.0 %copy-start.27 = (bf16[591,2,768]{2,0,1:T(8,128)(2,1)}, bf16[591,2,768]{2,0,1:T(8,128)(2,1)S(1)}, u32[]{:S(2)}) copy-start(bf16[591,2,768]{2,0,1:T(8,128)(2,1)S(1)} %multiply_convert_fusion.2) | copy-start | bytes 5446660
  89.6 56.7 %all-to-all-start.2 = ((bf16[4,184,1536]{2,1,0:T(8,128)(2,1)}), bf16[4,184,1536]{2,1,0:T(8,128)(2,1)S(1)}, u32[]{:S(2)}, u32[]{:S(2)}) async-start(bf16[4,184,1536]{2,1,0:T(8,128)(2,1)} %pad_maximum_fusion.4), calls=%async_computation.2 | async-start | bytes 4521984 | tf_op jit(solution)/shard_map/all_to_all | solution.py:286
  94.2 3.6 copy-start.25
  94.2 3.6 copy-start.26
  147.8 57.2 %all-to-all-start = ((bf16[4,192,1536]{2,1,0:T(8,128)(2,1)}), bf16[4,192,1536]{2,1,0:T(8,128)(2,1)S(1)}, u32[]{:S(2)}, u32[]{:S(2)}) async-start(bf16[4,192,1536]{2,1,0:T(8,128)(2,1)} %pad_maximum_fusion.2), calls=%async_computation | async-start | bytes 4718592 | tf_op jit(solution)/shard_map/all_to_all | solution.py:286
  151.6 25.8 %copy-start.18 = (bf16[3072,768]{1,0:T(8,128)(2,1)S(1)}, bf16[3072,768]{1,0:T(8,128)(2,1)}, u32[]{:S(2)}) copy-start(bf16[3072,768]{1,0:T(8,128)(2,1)} %reshape_squeeze.3) | copy-start | bytes 14155780
  177.4 3.7 copy-start.64
  177.4 14.5 %slice-start = ((s8[9437184]{0:T(1024)(128)(4,1)}), s8[4194304]{0:T(1024)(128)(4,1)S(1)}, s32[]{:S(2)}) async-start(s8[9437184]{0:T(1024)(128)(4,1)} %bitcast.176), calls=%async_computation.8 | async-start | bytes 8388608
  177.4 14.5 %slice-start.1 = ((s8[9437184]{0:T(1024)(128)(4,1)}), s8[4194304]{0:T(1024)(128)(4,1)S(1)}, s32[]{:S(2)}) async-start(s8[9437184]{0:T(1024)(128)(4,1)} %bitcast.176), calls=%async_computation.9 | async-start | bytes 8388608
  181.1 10.8 %slice-start.2 = ((s8[9437184]{0:T(1024)(128)(4,1)}), s8[1048576]{0:T(1024)(128)(4,1)S(1)}, s32[]{:S(2)}) async-start(s8[9437184]{0:T(1024)(128)(4,1)} %bitcast.176), calls=%async_computation.10 | async-start | bytes 2097152
  204.9 31.1 %copy-start.15 = (bf16[4,192,1536]{2,1,0:T(8,128)(2,1)}, bf16[4,192,1536]{2,1,0:T(8,128)(2,1)S(1)}, u32[]{:S(2)}) copy-start(bf16[4,192,1536]{2,1,0:T(8,128)(2,1)S(1)} %all-to-all-done) | copy-start | bytes 7077892
  204.9 70.3 %all-to-all-start.3 = ((bf16[4,184,1536]{2,1,0:T(8,128)(2,1)}), bf16[4,184,1536]{2,1,0:T(8,128)(2,1)}, u32[]{:S(2)}, u32[]{:S(2)}) async-start(bf16[4,184,1536]{2,1,0:T(8,128)(2,1)} %bitcast.15), calls=%async_computation.3 | async-start | bytes 4521984 | tf_op jit(solution)/shard_map/all_to_all | solution.py:322
  236.0 11.8 %copy-start.63 = (bf16[768,3072]{1,0:T(8,128)(2,1)}, bf16[768,3072]{1,0:T(8,128)(2,1)S(1)}, u32[]{:S(2)}) copy-start(bf16[768,3072]{1,0:T(8,128)(2,1)S(1)} %get-tuple-element.85) | copy-start | bytes 14155780
  247.8 8.2 %copy-start.19 = (bf16[768,3072]{1,0:T(8,128)(2,1)}, bf16[768,3072]{1,0:T(8,128)(2,1)S(1)}, u32[]{:S(2)}) copy-start(bf16[768,3072]{1,0:T(8,128)(2,1)S(1)} %fusion.6) | copy-start | bytes 14155780
  275.2 5.2 %copy-start.22 = (bf16[4,184,1536]{2,1,0:T(8,128)(2,1)S(1)}, bf16[4,184,1536]{2,1,0:T(8,128)(2,1)}, u32[]{:S(2)}) copy-start(bf16[4,184,1536]{2,1,0:T(8,128)(2,1)} %copy-done.21) | copy-start | bytes 6782980
  275.2 58.1 %all-to-all-start.1 = ((bf16[4,192,1536]{2,1,0:T(8,128)(2,1)}), bf16[4,192,1536]{2,1,0:T(8,128)(2,1)}, u32[]{:S(2)}, u32[]{:S(2)}) async-start(bf16[4,192,1536]{2,1,0:T(8,128)(2,1)} %bitcast.10), calls=%async_computation.1 | async-start | bytes 4718592 | tf_op jit(solution)/shard_map/all_to_all | solution.py:322
  280.4 175.7 %reduce-scatter.2.cloned.1.call-start = ((), (), s32[]{:S(2)}) async-start(), calls=%async_computation.7 | async-start | bytes 10616832 | tf_op jit(solution)/shard_map/reduce_scatter | solution.py:328
  290.5 8.6 %copy-start.16 = (bf16[4,192,1536]{2,1,0:T(8,128)(2,1)S(1)}, bf16[4,192,1536]{2,1,0:T(8,128)(2,1)}, u32[]{:S(2)}) copy-start(bf16[4,192,1536]{2,1,0:T(8,128)(2,1)} %copy-done.15) | copy-start | bytes 7077892
  299.1 5.9 %copy-start.23 = (bf16[4,184,1536]{2,1,0:T(8,128)(2,1)S(1)}, bf16[4,184,1536]{2,1,0:T(8,128)(2,1)}, u32[]{:S(2)}) copy-start(bf16[4,184,1536]{2,1,0:T(8,128)(2,1)} %copy-done.21) | copy-start | bytes 6782980
  322.4 5.5 %copy-start.30 = (pred[1504,591]{1,0:T(32,128)(4,1)S(1)}, pred[1504,591]{1,0:T(32,128)(4,1)}, u32[]{:S(2)}) copy-start(pred[1504,591]{1,0:T(32,128)(4,1)} %get-tuple-element.106) | copy-start | bytes 2666596
  333.3 6.1 %copy-start.62 = (f32[591,1536]{1,0:T(8,128)S(1)}, f32[591,1536]{1,0:T(8,128)}, u32[]{:S(2)}) copy-start(f32[591,1536]{1,0:T(8,128)} %fusion.55) | copy-start | bytes 10893316
  333.3 12.1 %slice-start.3 = ((s8[4915200]{0:T(1024)(128)(4,1)}), s8[4194304]{0:T(1024)(128)(4,1)S(1)}, s32[]{:S(2)}) async-start(s8[4915200]{0:T(1024)(128)(4,1)} %bitcast.191), calls=%async_computation.11 | async-start | bytes 8388608
  339.4 3.8 copy-start.4
  339.4 3.8 copy-start.8
  339.4 3.8 copy-start.35
  339.5 3.8 copy-start.60
  339.5 3.8 copy-start.61
  339.5 5.9 %slice-start.4 = ((s8[4915200]{0:T(1024)(128)(4,1)}), s8[720896]{0:T(1024)(128)(4,1)S(1)}, s32[]{:S(2)}) async-start(s8[4915200]{0:T(1024)(128)(4,1)} %bitcast.191), calls=%async_computation.12 | async-start | bytes 1441792
  371.8 3.5 copy-start.11
  381.8 5.8 %collective-permute-start = (bf16[2,2,96,1536]{3,2,1,0:T(8,128)(2,1)S(1)}, bf16[2,2,96,1536]{3,2,1,0:T(8,128)(2,1)S(1)}, u32[]{:S(2)}, u32[]{:S(2)}) collective-permute-start(bf16[2,2,96,1536]{3,2,1,0:T(8,128)(2,1)S(1)} %fusion.63), channel_id=1, source_target_pairs={{0,1},{1,0},{2,3},{3,2},{4,5},{5,4},{6,7},{7,6},{8,9},{9,8},{10,11... | collective-permute-start | bytes 3538952 | tf_op jit(solution)/shard_map/ppermute | solution.py:122
  384.2 6.8 %collective-permute-start.9 = (bf16[2,2,96,1664]{3,2,1,0:T(8,128)(2,1)S(1)}, bf16[2,2,96,1664]{3,2,1,0:T(8,128)(2,1)S(1)}, u32[]{:S(2)}, u32[]{:S(2)}) collective-permute-start(bf16[2,2,96,1664]{3,2,1,0:T(8,128)(2,1)S(1)} %fusion.62), channel_id=1, source_target_pairs={{0,1},{1,0},{2,3},{3,2},{4,5},{5,4},{6,7},{7,6},{8,9},{9,8},{10,11... | collective-permute-start | bytes 3833864 | tf_op jit(solution)/shard_map/ppermute | solution.py:122
  388.3 15.2 %collective-permute-start.3 = (bf16[2,96,768]{2,1,0:T(8,128)(2,1)S(1)}, bf16[2,96,768]{2,1,0:T(8,128)(2,1)S(1)}, u32[]{:S(2)}, u32[]{:S(2)}) collective-permute-start(bf16[2,96,768]{2,1,0:T(8,128)(2,1)S(1)} %fusion.86), channel_id=1, source_target_pairs={{0,4},{1,5},{2,6},{3,7},{4,0},{5,1},{6,2},{7,3},{8,12},{9,13},{10,... | collective-permute-start | bytes 884744 | tf_op jit(solution)/shard_map/ppermute | solution.py:122
  389.8 15.4 %collective-permute-start.1 = (bf16[2,96,768]{2,1,0:T(8,128)(2,1)S(1)}, bf16[2,96,768]{2,1,0:T(8,128)(2,1)S(1)}, u32[]{:S(2)}, u32[]{:S(2)}) collective-permute-start(bf16[2,96,768]{2,1,0:T(8,128)(2,1)S(1)} %fusion.85), channel_id=1, source_target_pairs={{0,2},{1,3},{2,0},{3,1},{4,6},{5,7},{6,4},{7,5},{8,10},{9,11},{10,... | collective-permute-start | bytes 884744 | tf_op jit(solution)/shard_map/ppermute | solution.py:122
  391.5 20.1 %collective-permute-start.12 = (bf16[2,96,896]{2,1,0:T(8,128)(2,1)S(1)}, bf16[2,96,896]{2,1,0:T(8,128)(2,1)S(1)}, u32[]{:S(2)}, u32[]{:S(2)}) collective-permute-start(bf16[2,96,896]{2,1,0:T(8,128)(2,1)S(1)} %fusion.84), channel_id=1, source_target_pairs={{0,4},{1,5},{2,6},{3,7},{4,0},{5,1},{6,2},{7,3},{8,12},{9,13},{10,... | collective-permute-start | bytes 1032200 | tf_op jit(solution)/shard_map/ppermute | solution.py:122
  392.6 17.4 %collective-permute-start.10 = (bf16[2,96,768]{2,1,0:T(8,128)(2,1)S(1)}, bf16[2,96,768]{2,1,0:T(8,128)(2,1)S(1)}, u32[]{:S(2)}, u32[]{:S(2)}) collective-permute-start(bf16[2,96,768]{2,1,0:T(8,128)(2,1)S(1)} %fusion.87), channel_id=1, source_target_pairs={{0,2},{1,3},{2,0},{3,1},{4,6},{5,7},{6,4},{7,5},{8,10},{9,11},{10,... | collective-permute-start | bytes 884744 | tf_op jit(solution)/shard_map/ppermute | solution.py:122
  403.7 9.1 %collective-permute-start.4 = (bf16[96,768]{1,0:T(8,128)(2,1)S(1)}, bf16[96,768]{1,0:T(8,128)(2,1)S(1)}, u32[]{:S(2)}, u32[]{:S(2)}) collective-permute-start(bf16[96,768]{1,0:T(8,128)(2,1)S(1)} %fusion.95), channel_id=1, source_target_pairs={{0,2},{1,3},{2,0},{3,1},{4,6},{5,7},{6,4},{7,5},{8,10},{9,11},{10,... | collective-permute-start | bytes 442376 | tf_op jit(solution)/shard_map/ppermute | solution.py:122
  405.2 8.9 %collective-permute-start.2 = (bf16[96,768]{1,0:T(8,128)(2,1)S(1)}, bf16[96,768]{1,0:T(8,128)(2,1)S(1)}, u32[]{:S(2)}, u32[]{:S(2)}) collective-permute-start(bf16[96,768]{1,0:T(8,128)(2,1)S(1)} %fusion.94), channel_id=1, source_target_pairs={{0,4},{1,5},{2,6},{3,7},{4,0},{5,1},{6,2},{7,3},{8,12},{9,13},{10,... | collective-permute-start | bytes 442376 | tf_op jit(solution)/shard_map/ppermute | solution.py:122
  410.0 6.9 %collective-permute-start.11 = (bf16[96,768]{1,0:T(8,128)(2,1)S(1)}, bf16[96,768]{1,0:T(8,128)(2,1)S(1)}, u32[]{:S(2)}, u32[]{:S(2)}) collective-permute-start(bf16[96,768]{1,0:T(8,128)(2,1)S(1)} %fusion.97), channel_id=1, source_target_pairs={{0,4},{1,5},{2,6},{3,7},{4,0},{5,1},{6,2},{7,3},{8,12},{9,13},{10,... | collective-permute-start | bytes 442376 | tf_op jit(solution)/shard_map/ppermute | solution.py:122
  411.7 10.3 %collective-permute-start.13 = (bf16[96,896]{1,0:T(8,128)(2,1)S(1)}, bf16[96,896]{1,0:T(8,128)(2,1)S(1)}, u32[]{:S(2)}, u32[]{:S(2)}) collective-permute-start(bf16[96,896]{1,0:T(8,128)(2,1)S(1)} %fusion.91), channel_id=1, source_target_pairs={{0,2},{1,3},{2,0},{3,1},{4,6},{5,7},{6,4},{7,5},{8,10},{9,11},{10,... | collective-permute-start | bytes 516104 | tf_op jit(solution)/shard_map/ppermute | solution.py:122
  414.2 5.2 %collective-permute-start.5 = (bf16[2,24,1536]{2,1,0:T(8,128)(2,1)S(1)}, bf16[2,24,1536]{2,1,0:T(8,128)(2,1)S(1)}, u32[]{:S(2)}, u32[]{:S(2)}) collective-permute-start(bf16[2,24,1536]{2,1,0:T(8,128)(2,1)S(1)} %fusion.96), channel_id=1, source_target_pairs={{0,8},{8,0},{16,24},{24,16},{1,9},{9,1},{17,25},{25,17},{2,10},{10... | collective-permute-start | bytes 442376 | tf_op jit(solution)/shard_map/ppermute | solution.py:122
  419.5 5.3 %collective-permute-start.6 = (bf16[24,1536]{1,0:T(8,128)(2,1)S(1)}, bf16[24,1536]{1,0:T(8,128)(2,1)S(1)}, u32[]{:S(2)}, u32[]{:S(2)}) collective-permute-start(bf16[24,1536]{1,0:T(8,128)(2,1)S(1)} %fusion.100), channel_id=1, source_target_pairs={{0,16},{8,24},{16,0},{24,8},{1,17},{9,25},{17,1},{25,9},{2,18},{10... | collective-permute-start | bytes 221192 | tf_op jit(solution)/shard_map/ppermute | solution.py:122
  424.9 5.3 %collective-permute-start.7 = (bf16[24,1536]{1,0:T(8,128)(2,1)S(1)}, bf16[24,1536]{1,0:T(8,128)(2,1)S(1)}, u32[]{:S(2)}, u32[]{:S(2)}) collective-permute-start(bf16[24,1536]{1,0:T(8,128)(2,1)S(1)} %fusion.98), channel_id=1, source_target_pairs={{0,16},{8,24},{16,0},{24,8},{1,17},{9,25},{17,1},{25,9},{2,18},{10... | collective-permute-start | bytes 221192 | tf_op jit(solution)/shard_map/ppermute | solution.py:146
  427.4 6.4 %collective-permute-start.14 = (bf16[2,24,1664]{2,1,0:T(8,128)(2,1)S(1)}, bf16[2,24,1664]{2,1,0:T(8,128)(2,1)S(1)}, u32[]{:S(2)}, u32[]{:S(2)}) collective-permute-start(bf16[2,24,1664]{2,1,0:T(8,128)(2,1)S(1)} %fusion.92), channel_id=1, source_target_pairs={{0,8},{8,0},{16,24},{24,16},{1,9},{9,1},{17,25},{25,17},{2,10},{10... | collective-permute-start | bytes 479240 | tf_op jit(solution)/shard_map/ppermute | solution.py:122
  433.9 7.5 %collective-permute-start.15 = (bf16[24,1664]{1,0:T(8,128)(2,1)S(1)}, bf16[24,1664]{1,0:T(8,128)(2,1)S(1)}, u32[]{:S(2)}, u32[]{:S(2)}) collective-permute-start(bf16[24,1664]{1,0:T(8,128)(2,1)S(1)} %fusion.99), channel_id=1, source_target_pairs={{0,16},{8,24},{16,0},{24,8},{1,17},{9,25},{17,1},{25,9},{2,18},{10... | collective-permute-start | bytes 239624 | tf_op jit(solution)/shard_map/ppermute | solution.py:122
  434.0 7.5 %collective-permute-start.8 = (bf16[2,24,1536]{2,1,0:T(8,128)(2,1)S(1)}, bf16[2,24,1536]{2,1,0:T(8,128)(2,1)S(1)}, u32[]{:S(2)}, u32[]{:S(2)}) collective-permute-start(bf16[2,24,1536]{2,1,0:T(8,128)(2,1)S(1)} %pad_maximum_fusion.11), channel_id=1, source_target_pairs={{0,8},{8,0},{16,24},{24,16},{1,9},{9,1},{17,25},{25,17},{2,10},{10... | collective-permute-start | bytes 442376 | tf_op jit(solution)/shard_map/ppermute | solution.py:146
  441.5 6.0 %collective-permute-start.16 = (bf16[24,1664]{1,0:T(8,128)(2,1)S(1)}, bf16[24,1664]{1,0:T(8,128)(2,1)S(1)}, u32[]{:S(2)}, u32[]{:S(2)}) collective-permute-start(bf16[24,1664]{1,0:T(8,128)(2,1)S(1)} %fusion.93), channel_id=1, source_target_pairs={{0,16},{8,24},{16,0},{24,8},{1,17},{9,25},{17,1},{25,9},{2,18},{10... | collective-permute-start | bytes 239624 | tf_op jit(solution)/shard_map/ppermute | solution.py:146
  447.5 5.3 %collective-permute-start.17 = (bf16[2,24,1664]{2,1,0:T(8,128)(2,1)S(1)}, bf16[2,24,1664]{2,1,0:T(8,128)(2,1)S(1)}, u32[]{:S(2)}, u32[]{:S(2)}) collective-permute-start(bf16[2,24,1664]{2,1,0:T(8,128)(2,1)S(1)} %pad_maximum_fusion.10), channel_id=1, source_target_pairs={{0,8},{8,0},{16,24},{24,16},{1,9},{9,1},{17,25},{25,17},{2,10},{10... | collective-permute-start | bytes 479240 | tf_op jit(solution)/shard_map/ppermute | solution.py:146
  (31 other events, 48.3 us)
Sparse Core Ops, SparseCore 0:
  11.7 42.3 all-gather.2
  56.5 58.6 all-gather.4
  321.3 83.1 reduce-scatter.1

commit v13 on v11

--- a/solution.py
+++ b/solution.py
@@ -49,26 +49,25 @@
     return jnp.where(lane < HD, stacked[:rows], stacked[rows:])
 
 
-def attn_fwd_kernel(q_ref, k_ref, v_ref, o_ref, *, images):
+def attn_fwd_kernel(q_ref, k_ref, v_ref, o_ref, p_ref, *, images):
     R = q_ref.shape[0]
     same = _same_image(R, images)
     same = jnp.concatenate([same, same], axis=0)
     lane = lax.broadcasted_iota(jnp.int32, (1, 2 * HD), 1)
     p = _softmax_masked(_two_heads(q_ref[...], lane), k_ref[...], same)
+    p_ref[0] = p
     o = jnp.dot(p.astype(jnp.bfloat16), v_ref[...], preferred_element_type=jnp.float32)
     o_ref[...] = _pick_heads(o, lane, R).astype(o_ref.dtype)
 
 
-def attn_bwd_kernel(q_ref, k_ref, v_ref, g_ref, dq_ref, dk_ref, dv_ref, *, images):
+def attn_bwd_kernel(q_ref, k_ref, v_ref, g_ref, p_ref, dq_ref, dk_ref, dv_ref):
     R = q_ref.shape[0]
     k = k_ref[...]
     v = v_ref[...]
-    same = _same_image(R, images)
-    same = jnp.concatenate([same, same], axis=0)
     lane = lax.broadcasted_iota(jnp.int32, (1, 2 * HD), 1)
     q2 = _two_heads(q_ref[...], lane)
     g2 = _two_heads(g_ref[...], lane)
-    p = _softmax_masked(q2, k, same)
+    p = p_ref[0]
     dp = lax.dot_general(g2, v, COL_CONTRACT, preferred_element_type=jnp.float32)
     ds = (p * (dp - jnp.sum(p * dp, axis=1, keepdims=True))).astype(jnp.bfloat16)
     dq = jnp.dot(ds, k, preferred_element_type=jnp.float32) * (HD ** -0.5)
@@ -84,30 +83,40 @@
     W = projected.shape[1] // 3
     pairs = W // (2 * HD)
     blk = lambda off: pl.BlockSpec((R, 2 * HD), lambda h: (0, off + h))
+    probs = pl.BlockSpec((1, 2 * R, R), lambda h: (h, 0, 0))
     return pl.pallas_call(
         functools.partial(attn_fwd_kernel, images=images),
         grid=(pairs,),
         in_specs=[blk(0), blk(pairs), blk(2 * pairs)],
-        out_specs=blk(0),
-        out_shape=jax.ShapeDtypeStruct((R, W), jnp.bfloat16),
+        out_specs=[blk(0), probs],
+        out_shape=[
+            jax.ShapeDtypeStruct((R, W), jnp.bfloat16),
+            jax.ShapeDtypeStruct((pairs, 2 * R, R), jnp.float32),
+        ],
         compiler_params=pltpu.CompilerParams(vmem_limit_bytes=48 * 1024 * 1024),
     )(projected, projected, projected)
 
 
-def attention_bwd(projected, mixed_grad, images):
+def attention_bwd(projected, mixed_grad, probs):
     R = projected.shape[0]
     W = projected.shape[1] // 3
     pairs = W // (2 * HD)
     blk = lambda off: pl.BlockSpec((R, 2 * HD), lambda h: (0, off + h))
     out = jax.ShapeDtypeStruct((R, W), jnp.bfloat16)
     return pl.pallas_call(
-        functools.partial(attn_bwd_kernel, images=images),
+        attn_bwd_kernel,
         grid=(pairs,),
-        in_specs=[blk(0), blk(pairs), blk(2 * pairs), blk(0)],
+        in_specs=[
+            blk(0),
+            blk(pairs),
+            blk(2 * pairs),
+            blk(0),
+            pl.BlockSpec((1, 2 * R, R), lambda h: (h, 0, 0)),
+        ],
         out_specs=[blk(0), blk(0), blk(0)],
         out_shape=[out, out, out],
         compiler_params=pltpu.CompilerParams(vmem_limit_bytes=48 * 1024 * 1024),
-    )(projected, projected, projected, mixed_grad)
+    )(projected, projected, projected, mixed_grad, probs)
 
 
 def _exchange(values, bits_left, bit, axis_name, size, index):
@@ -134,6 +143,33 @@
         first, first_bits = _exchange(first, first_bits, up, axis_name, size, index)
         second, second_bits = _exchange(second, second_bits, down, axis_name, size, index)
     return jnp.concatenate([first, second], axis=-1)
+
+
+def _gather_back(values, bit, axis_name, size, index):
+    n_bits = size.bit_length() - 1
+    mine = (index >> bit) & 1
+    pairs = [(i, i ^ (1 << bit)) for i in range(size)]
+    got = lax.ppermute(values, axis_name, pairs)
+    low = jnp.where(mine == 0, values, got)
+    high = jnp.where(mine == 0, got, values)
+    return jnp.stack([low, high], axis=n_bits - 1 - bit)
+
+
+def expert_all_reduce(values, axis_name):
+    size = lax.axis_size(axis_name)
+    index = lax.axis_index(axis_name)
+    n_bits = size.bit_length() - 1
+    rows = values.shape[0]
+    if rows % size:
+        return lax.psum(values.astype(jnp.bfloat16), axis_name).astype(jnp.float32)
+    bits = list(range(n_bits - 1, -1, -1))
+    parts = values.astype(jnp.float32).reshape([2] * n_bits + [rows // size, values.shape[1]])
+    for bit in range(n_bits):
+        parts, bits = _exchange(parts, bits, bit, axis_name, size, index)
+    parts = parts.astype(jnp.bfloat16)
+    for bit in range(n_bits - 1, -1, -1):
+        parts = _gather_back(parts, bit, axis_name, size, index)
+    return parts.reshape(rows, values.shape[1]).astype(jnp.float32)
 
 
 def layer_norm(values, norm_gain):
@@ -204,7 +240,8 @@
     projected = jnp.dot(attn_in, full_qkv, preferred_element_type=jnp.float32).astype(jnp.bfloat16)
     pad_rows = -(-rows // 128) * 128
     projected_pad = jnp.pad(projected, ((0, pad_rows - rows), (0, 0)))
-    mixed_rows = attention_fwd(projected_pad, images)[:rows]
+    mixed_pad, attn_probs = attention_fwd(projected_pad, images)
+    mixed_rows = mixed_pad[:rows]
     hidden_state = token_f + jnp.dot(mixed_rows, full_out, preferred_element_type=jnp.float32)
     moe_in = layer_norm(hidden_state, gain_two).astype(jnp.bfloat16)
     logits = jnp.dot(moe_in, full_router, preferred_element_type=jnp.float32)
@@ -346,7 +383,7 @@
         branch_grad, full_out, COL_CONTRACT, preferred_element_type=jnp.float32
     )
     mixed_grad = jnp.pad(mixed_grad.astype(jnp.bfloat16), ((0, pad_rows - rows), (0, 0)))
-    grad_q, grad_k, grad_v = attention_bwd(projected_pad, mixed_grad, images)
+    grad_q, grad_k, grad_v = attention_bwd(projected_pad, mixed_grad, attn_probs)
     projected_grad = jnp.concatenate([grad_q, grad_k, grad_v], axis=1)
     attn_in_pad = jnp.pad(attn_in, ((0, pad_rows - rows), (0, 0)))
     grad_qkv = lax.dot_general(
@@ -364,8 +401,16 @@
     )
     small = jnp.pad(small, ((0, 0), (0, 128 - small.shape[1])))
     dense_grads = jnp.concatenate([grad_qkv, grad_wout, small], axis=1)
-    dense_share = shard_reduce_scatter(dense_grads, "shard", 128 * (dense_grads.shape[1] // 256))
-    dense_total = lax.psum(dense_share.astype(jnp.bfloat16), "expert").astype(jnp.float32)
+    chunk_cols = 128 * (dense_grads.shape[1] // 256)
+    dense_total = jnp.concatenate(
+        [
+            expert_all_reduce(
+                shard_reduce_scatter(part, "shard", 128 * (part.shape[1] // 256)), "expert"
+            )
+            for part in (dense_grads[:, :chunk_cols], dense_grads[:, chunk_cols:])
+        ],
+        axis=1,
+    )
     return (
         output,
         grad_tokens,

time: 575 us -> 475 us (0.83)
  waiting for transfers between devices: 209 us -> 108 us
  starting transfers between devices: 24.1 us -> 41.2 us
  other arithmetic: 41.5 us -> 33.8 us
  local copies, waits for them, and re-layouts: 54.1 us -> 48.3 us
    reduce_scatter x1, waiting for transfers between devices: 72.9 us -> 0.01 us  [shards(): lax.psum_scatter(expert_grads, 'shard', scatter_dimension=1, tiled=True)]
    all_to_all x2, waiting for transfers between devices: 41.9 us -> 0.14 us  [shards(): lax.all_to_all(returning, 'expert', split_axis=0, concat_axis=0, tiled=True)]
    ppermute x5 -> x14, starting transfers between devices: 5.14 us -> 16 us  [_exchange(): got = lax.ppermute(send.astype(jnp.bfloat16), axis_name, pairs)]
    ppermute x5 -> x14, waiting for transfers between devices: 21.6 us -> 32.4 us  [_exchange(): got = lax.ppermute(send.astype(jnp.bfloat16), axis_name, pairs)]
    ppermute x0 -> x4, waiting for transfers between devices: none -> 9.48 us  [_gather_back(): got = lax.ppermute(values, axis_name, pairs)]
    ppermute x0 -> x4, starting transfers between devices: none -> 6.74 us  [_gather_back(): got = lax.ppermute(values, axis_name, pairs)]
    psum x1 -> x0, waiting for transfers between devices: 6.39 us -> none  [shards(): lax.psum(dense_share.astype(jnp.bfloat16), 'expert').astype(jnp.float32)]
  transfers between devices with their start and end apart: 13 -> 25, of which waited for: 11 -> 18; matrix products, arithmetic and copies ran while one was open for 41% -> 54% of each run, Pallas kernels for 2% -> 7%
where the time goes in v13:
time: 475 us; the launch traced here: 467 us
  matrix products  186 us (39%)
  waiting for transfers between devices  108 us (23%)
  local copies, waits for them, and re-layouts  48.3 us (10%)
  starting transfers between devices  41.2 us (9%)
  Pallas kernels  34 us (7%)
  other arithmetic  33.8 us (7%)
  between operations  16.4 us (3%)
    dot_general x2, matrix products, shards(): jnp.dot(flat_arrived, expert_first, preferred_element_type=jnp.float32)  51.9 us
    ppermute x14, waiting for transfers between devices, _exchange(): got = lax.ppermute(send.astype(jnp.bfloat16), axis_name, pairs)  32.4 us
    all_gather x1, waiting for transfers between devices, shards(): dense_full = lax.all_gather(dense_local, 'shard', axis=0, tiled=True)  29 us
    all_to_all x2, waiting for transfers between devices, shards(): lax.all_to_all(dispatch_rows(experts * start, experts * (start + size)).r...  25.2 us
    dot_general x2, matrix products, shards(): lax.dot_general(flat_grad, expert_second, COL_CONTRACT, preferred_element...  22.5 us
    dot_general x2, matrix products, shards(): lax.dot_general(activated, flat_grad, ROW_CONTRACT, preferred_element_typ...  20.3 us
    pallas_call x1, Pallas kernels, attention_bwd(): pl.pallas_call(attn_bwd_kernel, grid=(pairs,), in_specs=[blk(0), blk(pair...  18.7 us
    ppermute x14, starting transfers between devices, _exchange(): got = lax.ppermute(send.astype(jnp.bfloat16), axis_name, pairs)  16 us
  transfers between devices with their start and end apart: 25, of which 18 were waited for; matrix products, arithmetic and copies ran while one was open for 54% of the time, Pallas kernels for 7%

profile of v13, /device:TPU:0, one launch (start us, length us, event | category | flops | bytes accessed | tf_op | source)
XLA Modules:
  0.0 466.8 jit_solution(2903639115515785834)
XLA Ops:
  9.6 1.9 concatenate.52
  13.2 2.3 pad_maximum_fusion.6
  20.1 1.6 convert_multiply_fusion
  21.7 3.4 fusion.115
  25.0 29.0 %all-gather.3.cloned.1.call-done = bf16[768,3078]{1,0:T(8,128)(2,1)} async-done(((bf16[96,3078]{1,0:T(8,128)(2,1)}), bf16[768,3078]{1,0:T(8,128)(2,1)}) %all-gather.3.cloned.1.call-update) | async-done | bytes 4727824 | tf_op jit(solution)/shard_map/all_gather | solution.py:223
  55.8 4.6 convolution_convert_fusion
  60.6 15.3 %shard_map.178 = (bf16[640,768]{1,0:T(8,128)(2,1)S(1)}, f32[6,1280,640]{2,1,0:T(8,128)}) custom-call(bf16[640,2304]{1,0:T(8,128)(2,1)S(1)} %pad.18.q_ref.k_ref.v_ref, bf16[640,2304]{1,0:T(8,128)(2,1)S(1)} %pad.18.q_ref.k_ref.v_ref, bf16[640,2304]{1,0:T(8,128)(2,1)S(1)} %pad.18.q_ref.k_ref.v_ref), custom_call_target="tpu_custom_call" | custom-call | tf_op jit(solution)/shard_map/pallas_call | solution.py:87
  76.0 2.6 fusion.122
  80.1 1.5 fusion.123
  82.6 2.7 fusion.60
  85.3 2.5 convolution_convert_fusion.4
  87.9 2.2 add_convert_fusion.3
  91.5 4.4 all-to-all-start.2
  96.6 2.8 fusion.53
  102.4 1.6 pad_maximum_fusion.2
  104.0 11.3 %all-gather.5.cloned.1.call-done = bf16[2,768,3072]{2,1,0:T(8,128)(2,1)} async-done(((bf16[2,96,3072]{2,1,0:T(8,128)(2,1)}), bf16[2,768,3072]{2,1,0:T(8,128)(2,1)}) %all-gather.5.cloned.1.call-update) | async-done | bytes 9437200 | tf_op jit(solution)/shard_map/all_gather | solution.py:234
  115.2 4.8 %slice.210 = bf16[1,768,3072]{2,1,0:T(8,128)(2,1)} slice(bf16[2,768,3072]{2,1,0:T(8,128)(2,1)} %all-gather.5.cloned.1.call-done), slice={[1:2], [0:768], [0:3072]} | slice | bytes 9437184 | tf_op jit(solution)/shard_map/slice | solution.py:236
  120.0 8.5 %reshape_squeeze.3 = bf16[3072,768]{1,0:T(8,128)(2,1)} reshape(bf16[1,768,3072]{2,1,0:T(8,128)(2,1)} %slice.210) | data formatting | bytes 9437184 | tf_op jit(solution)/shard_map/reshape;squeeze | solution.py:236
  128.5 19.7 %all-to-all-done.2 = bf16[4,184,1536]{2,1,0:T(8,128)(2,1)S(1)} async-done(((bf16[4,184,1536]{2,1,0:T(8,128)(2,1)}), bf16[4,184,1536]{2,1,0:T(8,128)(2,1)S(1)}, u32[]{:S(2)}, u32[]{:S(2)}) %all-to-all-start.2) | async-done | bytes 2261024 | tf_op jit(solution)/shard_map/all_to_all | solution.py:293
  149.6 3.8 all-to-all-start
  153.4 25.8 %multiply_convert_fusion.1 = (bf16[736,3072]{1,0:T(8,128)(2,1)S(1)}, f32[736,3072]{1,0:T(8,128)}, f32[736,3072]{1,0:T(8,128)}) fusion(bf16[2,768,3072]{2,1,0:T(8,128)(2,1)} %all-gather.5.cloned.1.call-done, bf16[736,1536]{1,0:T(8,128)(2,1)} %bitcast.179), kind=kOutput, calls=%fused_computation.36 | convolution fusion | flops 3619848192 | bytes 28459008 | tf_op jit(solution)/shard_map/dot_general | solution.py:307
  179.2 3.7 convolution_convert_fusion.3
  182.9 10.8 %fusion.19 = bf16[736,3072]{1,0:T(8,128)(2,1)} fusion(f32[736,3072]{1,0:T(8,128)} %get-tuple-element.116, f32[736,3072]{1,0:T(8,128)} %get-tuple-element.92, bf16[3072,768]{1,0:T(8,128)(2,1)S(1)} %copy-done.18, bf16[736,1536]{1,0:T(8,128)(2,1)} %bitcast.180), kind=kOutput, calls=%fused_computation.35 | convolution fusion | flops 3490971648 | bytes 28459008 | tf_op jit(solution)/shard_map/dot_general | solution.py:304
  193.7 6.1 %fusion.49 = bf16[736,768]{1,0:T(8,128)(2,1)S(1)} fusion(bf16[736,3072]{1,0:T(8,128)(2,1)} %fusion.19, bf16[2,768,3072]{2,1,0:T(8,128)(2,1)S(1)} %bitcast.177), kind=kOutput, calls=%fused_computation.112 | convolution fusion | flops 3473448960 | bytes 10371072 | tf_op jit(solution)/shard_map/dot_general | solution.py:314
  201.3 5.5 %all-to-all-done = bf16[4,192,1536]{2,1,0:T(8,128)(2,1)S(1)} async-done(((bf16[4,192,1536]{2,1,0:T(8,128)(2,1)}), bf16[4,192,1536]{2,1,0:T(8,128)(2,1)S(1)}, u32[]{:S(2)}, u32[]{:S(2)}) %all-to-all-start) | async-done | bytes 2359328 | tf_op jit(solution)/shard_map/all_to_all | solution.py:293
  206.8 4.9 %all-to-all-start.3 = ((bf16[4,184,1536]{2,1,0:T(8,128)(2,1)}), bf16[4,184,1536]{2,1,0:T(8,128)(2,1)}, u32[]{:S(2)}, u32[]{:S(2)}) async-start(bf16[4,184,1536]{2,1,0:T(8,128)(2,1)} %bitcast.15), calls=%async_computation.3 | async-start | bytes 4521984 | tf_op jit(solution)/shard_map/all_to_all | solution.py:329
  211.7 26.2 %multiply_convert_fusion = (bf16[768,3072]{1,0:T(8,128)(2,1)S(1)}, f32[768,3072]{1,0:T(8,128)}, f32[768,3072]{1,0:T(8,128)}) fusion(bf16[2,768,3072]{2,1,0:T(8,128)(2,1)} %all-gather.5.cloned.1.call-done, bf16[768,1536]{1,0:T(8,128)(2,1)S(1)} %bitcast.168), kind=kOutput, calls=%fused_computation.14 | convolution fusion | flops 3777232896 | bytes 29491200 | tf_op jit(solution)/shard_map/dot_general | solution.py:307
  237.9 11.8 %fusion.6 = bf16[768,3072]{1,0:T(8,128)(2,1)S(1)} fusion(f32[768,3072]{1,0:T(8,128)} %get-tuple-element.117, f32[768,3072]{1,0:T(8,128)} %get-tuple-element.90, bf16[3072,768]{1,0:T(8,128)(2,1)} %reshape_squeeze.3, bf16[768,1536]{1,0:T(8,128)(2,1)S(1)} %bitcast.169), kind=kOutput, calls=%fused_computation.10 | convolution fusion | flops 3642753024 | bytes 29491200 | tf_op jit(solution)/shard_map/dot_general | solution.py:304
  249.7 8.1 %convolution_convert_fusion.1 = bf16[768,768]{0,1:T(8,128)(2,1)S(1)} fusion(bf16[768,3072]{1,0:T(8,128)(2,1)S(1)} %get-tuple-element.89, bf16[3072,768]{1,0:T(8,128)(2,1)} %reshape_squeeze.3), kind=kOutput, calls=%fused_computation.110 | convolution fusion | flops 3624468480 | bytes 10616832 | tf_op jit(solution)/shard_map/dot_general | solution.py:311
  257.9 6.3 %fusion.48 = bf16[768,768]{0,1:T(8,128)(2,1)S(1)} fusion(bf16[768,3072]{1,0:T(8,128)(2,1)S(1)} %fusion.6, bf16[2,768,3072]{2,1,0:T(8,128)(2,1)} %all-gather.5.cloned.1.call-done), kind=kOutput, calls=%fused_computation.109 | convolution fusion | flops 3624468480 | bytes 10616832 | tf_op jit(solution)/shard_map/dot_general | solution.py:314
  264.3 2.4 copy.113
  266.7 10.2 %fusion.65 = f32[3072,768]{1,0:T(8,128)} fusion(bf16[768,3072]{1,0:T(8,128)(2,1)} %copy-done.63, bf16[768,1536]{1,0:T(8,128)(2,1)} %bitcast.170), kind=kOutput, calls=%fused_computation.132 | convolution fusion | flops 3623878656 | bytes 15335424 | tf_op jit(solution)/shard_map/dot_general | solution.py:317
  276.9 5.2 %all-to-all-start.1 = ((bf16[4,192,1536]{2,1,0:T(8,128)(2,1)}), bf16[4,192,1536]{2,1,0:T(8,128)(2,1)}, u32[]{:S(2)}, u32[]{:S(2)}) async-start(bf16[4,192,1536]{2,1,0:T(8,128)(2,1)} %bitcast.10), calls=%async_computation.1 | async-start | bytes 4718592 | tf_op jit(solution)/shard_map/all_to_all | solution.py:329
  282.1 10.1 %add_convert_fusion = bf16[3072,768]{1,0:T(8,128)(2,1)} fusion(f32[3072,768]{1,0:T(8,128)} %fusion.65, bf16[736,3072]{1,0:T(8,128)(2,1)} %copy-done.64, bf16[736,1536]{1,0:T(8,128)(2,1)S(1)} %bitcast.181), kind=kOutput, calls=%fused_computation.12 | convolution fusion | flops 3477602304 | bytes 19808256 | tf_op jit(solution)/shard_map/dot_general | solution.py:317
  292.2 8.6 %stack_reshape.4 = bf16[1,768,3072]{2,1,0:T(8,128)(2,1)} reshape(bf16[3072,768]{1,0:T(8,128)(2,1)} %add_convert_fusion) | data formatting | bytes 9437184 | tf_op jit(solution)/shard_map/stack;reshape | solution.py:332
  300.9 5.9 %fusion.68 = f32[768,3072]{1,0:T(8,128)S(1)} fusion(bf16[768,3072]{1,0:T(8,128)(2,1)} %copy-done.19, bf16[768,1536]{1,0:T(8,128)(2,1)S(1)} %bitcast.171), kind=kOutput, calls=%fused_computation.135 | convolution fusion | flops 3623878656 | bytes 15335424 | tf_op jit(solution)/shard_map/dot_general | solution.py:320
  306.8 7.8 %fusion.27 = bf16[1,768,3072]{2,1,0:T(8,128)(2,1)} fusion(f32[768,3072]{1,0:T(8,128)S(1)} %fusion.68, bf16[736,3072]{1,0:T(8,128)(2,1)} %fusion.19, bf16[736,1536]{1,0:T(8,128)(2,1)S(1)} %bitcast.182), kind=kOutput, calls=%fused_computation.57 | convolution fusion | flops 3477602304 | bytes 19808256 | tf_op jit(solution)/shard_map/dot_general | solution.py:320
  314.6 8.2 %pad_maximum_fusion = bf16[2,768,3072]{2,1,0:T(8,128)(2,1)} fusion(bf16[1,768,3072]{2,1,0:T(8,128)(2,1)} %stack_reshape.4, bf16[1,768,3072]{2,1,0:T(8,128)(2,1)} %fusion.27), kind=kLoop, calls=%fused_computation.11 | loop fusion | flops 4718592 | bytes 18874368 | tf_op jit(solution)/shard_map/stack | solution.py:332
  324.0 5.5 %fusion.58 = f32[591,1536]{1,0:T(8,128)} fusion(bf16[736,1536]{1,0:T(8,128)(2,1)} %bitcast.16, pred[1504,591]{1,0:T(32,128)(4,1)S(1)} %copy-done.31), kind=kOutput, calls=%fused_computation.124 | convolution fusion | flops 1336246272 | bytes 6363136 | tf_op jit(solution)/shard_map/dot_general | solution.py:345
  329.5 5.4 %fusion.55 = f32[591,1536]{1,0:T(8,128)} fusion(bf16[736,1536]{1,0:T(8,128)(2,1)} %bitcast.16, pred[1504,591]{1,0:T(32,128)(4,1)S(1)} %copy-done.30), kind=kOutput, calls=%fused_computation.121 | convolution fusion | flops 1336246272 | bytes 6363136 | tf_op jit(solution)/shard_map/dot_general | solution.py:348
  335.0 6.0 %convolution_add_fusion.1 = f32[591,1536]{1,0:T(8,128)S(1)} fusion(f32[591,1536]{1,0:T(8,128)} %fusion.58, bf16[768,1536]{1,0:T(8,128)(2,1)} %bitcast.11, pred[1504,591]{1,0:T(32,128)(4,1)S(1)} %copy-done.31), kind=kOutput, calls=%fused_computation.60 | convolution fusion | flops 1395251712 | bytes 10113024 | tf_op jit(solution)/shard_map/dot_general | solution.py:345
  341.2 3.7 convolution_add_fusion
  345.0 1.9 multiply_reduce_fusion.3
  350.4 18.7 %shard_map.179 = (bf16[640,768]{1,0:T(8,128)(2,1)S(1)}, bf16[640,768]{1,0:T(8,128)(2,1)S(1)}, bf16[640,768]{1,0:T(8,128)(2,1)S(1)}) custom-call(bf16[640,2304]{1,0:T(8,128)(2,1)} %copy-done, bf16[640,2304]{1,0:T(8,128)(2,1)} %copy-done, bf16[640,2304]{1,0:T(8,128)(2,1)} %copy-done, bf16[640,768]{1,0:T(8,128)(2,1)S(1)} %pad.20.g_ref, ...), custom_call_target="tpu_custom_call" | custom-call | tf_op jit(solution)/shard_map/pallas_call | solution.py:106
  370.3 2.4 fusion.45
  374.2 5.2 %fusion.78 = f32[768,2304]{1,0:T(8,128)S(1)} fusion(bf16[640,2304]{1,0:T(8,128)(2,1)} %copy-done.17, bf16[591,768]{1,0:T(8,128)(2,1)} %copy-done.20), kind=kOutput, calls=%fused_computation.146 | convolution fusion | flops 2264924160 | bytes 10934784 | tf_op jit(solution)/shard_map/dot_general | solution.py:389
  384.0 2.0 add_convert_fusion.4
  391.6 11.4 %collective-permute-done.3 = bf16[2,96,768]{2,1,0:T(8,128)(2,1)S(1)} collective-permute-done((bf16[2,96,768]{2,1,0:T(8,128)(2,1)S(1)}, bf16[2,96,768]{2,1,0:T(8,128)(2,1)S(1)}, u32[]{:S(2)}, u32[]{:S(2)}) %collective-permute-start.3) | collective-permute-done | bytes 294944 | tf_op jit(solution)/shard_map/ppermute | solution.py:128
  403.0 1.7 collective-permute-start.4
  406.0 5.6 %collective-permute-done.10 = bf16[2,96,768]{2,1,0:T(8,128)(2,1)S(1)} collective-permute-done((bf16[2,96,768]{2,1,0:T(8,128)(2,1)S(1)}, bf16[2,96,768]{2,1,0:T(8,128)(2,1)S(1)}, u32[]{:S(2)}, u32[]{:S(2)}) %collective-permute-start.10) | collective-permute-done | bytes 294944 | tf_op jit(solution)/shard_map/ppermute | solution.py:128
  411.7 1.6 collective-permute-start.11
  415.8 1.6 collective-permute-start.5
  418.6 2.6 collective-permute-done.5
  421.2 2.4 collective-permute-start.6
  423.8 2.8 collective-permute-done.6
  426.6 2.5 collective-permute-start.7
  429.1 2.2 collective-permute-start.14
  431.9 3.7 collective-permute-done.14
  435.8 2.5 collective-permute-start.8
  438.3 3.7 collective-permute-done.15
  442.5 4.9 %collective-permute-done.16 = bf16[24,1664]{1,0:T(8,128)(2,1)S(1)} collective-permute-done((bf16[24,1664]{1,0:T(8,128)(2,1)S(1)}, bf16[24,1664]{1,0:T(8,128)(2,1)S(1)}, u32[]{:S(2)}, u32[]{:S(2)}) %collective-permute-start.16) | collective-permute-done | bytes 79904 | tf_op jit(solution)/shard_map/ppermute | solution.py:152
  447.5 1.6 collective-permute-start.17
  449.1 3.7 collective-permute-done.17
  456.0 2.5 fusion.121
  (299 shorter events, 48.7 us)
Async XLA Ops:
  7.2 46.9 %all-gather.3.cloned.1.call-start = ((), (), s32[]{:S(2)}) async-start(), calls=%async_computation.5 | async-start | bytes 5529600 | tf_op jit(solution)/shard_map/all_gather | solution.py:223
  8.8 7.7 %copy-start.44 = (s32[591,2]{0,1:T(2,128)S(1)}, s32[591,2]{0,1:T(2,128)}, u32[]{:S(2)}) copy-start(s32[591,2]{0,1:T(2,128)} %param.13) | copy-start | bytes 14188
  11.6 7.9 %copy-start.5 = (bf16[591,768]{1,0:T(8,128)(2,1)S(1)}, bf16[591,768]{1,0:T(8,128)(2,1)}, u32[]{:S(2)}) copy-start(bf16[591,768]{1,0:T(8,128)(2,1)} %param.11) | copy-start | bytes 2723332
  11.6 103.7 %all-gather.5.cloned.1.call-start = ((), (), s32[]{:S(2)}) async-start(), calls=%async_computation.6 | async-start | bytes 10616832 | tf_op jit(solution)/shard_map/all_gather | solution.py:234
  13.2 6.9 %copy-start.7 = (bf16[591,768]{1,0:T(8,128)(2,1)S(1)}, bf16[591,768]{1,0:T(8,128)(2,1)}, u32[]{:S(2)}) copy-start(bf16[591,768]{1,0:T(8,128)(2,1)} %param.21) | copy-start | bytes 2723332
  19.4 62.4 %copy-start.34 = (f32[591]{0:T(1024)}, f32[591]{0:T(1024)S(1)}, u32[]{:S(2)}) copy-start(f32[591]{0:T(1024)S(1)} %fusion.112) | copy-start | bytes 7096
  19.6 35.8 %copy-start.42 = (f32[591]{0:T(1024)}, f32[591]{0:T(1024)S(1)}, u32[]{:S(2)}) copy-start(f32[591]{0:T(1024)S(1)} %broadcast_multiply_fusion.2) | copy-start | bytes 7096
  20.1 35.3 %copy-start.54 = (f32[591]{0:T(1024)}, f32[591]{0:T(1024)S(1)}, u32[]{:S(2)}) copy-start(f32[591]{0:T(1024)S(1)} %fusion.110) | copy-start | bytes 7096
  25.0 60.3 %copy-start.24 = (bf16[1504,591]{1,0:T(8,128)(2,1)}, bf16[1504,591]{1,0:T(8,128)(2,1)S(1)}, u32[]{:S(2)}) copy-start(bf16[1504,591]{1,0:T(8,128)(2,1)S(1)} %get-tuple-element.106) | copy-start | bytes 5333188
  55.4 5.0 %copy-start.52 = (f32[768]{0:T(1024)}, f32[768]{0:T(1024)S(1)}, u32[]{:S(2)}) copy-start(f32[768]{0:T(1024)S(1)} %get-tuple-element.74) | copy-start | bytes 9220
  55.4 24.2 %copy-start.46 = (f32[768]{0:T(1024)}, f32[768]{0:T(1024)S(1)}, u32[]{:S(2)}) copy-start(f32[768]{0:T(1024)S(1)} %get-tuple-element.73) | copy-start | bytes 9220
  55.8 4.6 copy-start.20
  60.6 15.3 %copy-start = (bf16[640,2304]{1,0:T(8,128)(2,1)}, bf16[640,2304]{1,0:T(8,128)(2,1)S(1)}, u32[]{:S(2)}) copy-start(bf16[640,2304]{1,0:T(8,128)(2,1)S(1)} %pad.18.q_ref.k_ref.v_ref) | copy-start | bytes 8847364
  78.6 3.7 copy-start.14
  78.6 3.2 copy-start.38
  79.5 3.0 copy-start.48
  80.1 19.3 %copy-start.10 = (bf16[591,768]{1,0:T(8,128)(2,1)}, bf16[591,768]{1,0:T(8,128)(2,1)S(1)}, u32[]{:S(2)}) copy-start(bf16[591,768]{1,0:T(8,128)(2,1)S(1)} %multiply_convert_fusion.4) | copy-start | bytes 2723332
  82.6 5.3 %copy-start.27 = (bf16[591,2,768]{2,0,1:T(8,128)(2,1)}, bf16[591,2,768]{2,0,1:T(8,128)(2,1)S(1)}, u32[]{:S(2)}) copy-start(bf16[591,2,768]{2,0,1:T(8,128)(2,1)S(1)} %multiply_convert_fusion.2) | copy-start | bytes 5446660
  91.5 56.7 %all-to-all-start.2 = ((bf16[4,184,1536]{2,1,0:T(8,128)(2,1)}), bf16[4,184,1536]{2,1,0:T(8,128)(2,1)S(1)}, u32[]{:S(2)}, u32[]{:S(2)}) async-start(bf16[4,184,1536]{2,1,0:T(8,128)(2,1)} %pad_maximum_fusion.4), calls=%async_computation.2 | async-start | bytes 4521984 | tf_op jit(solution)/shard_map/all_to_all | solution.py:293
  96.0 3.4 copy-start.25
  96.0 3.5 copy-start.26
  149.6 57.2 %all-to-all-start = ((bf16[4,192,1536]{2,1,0:T(8,128)(2,1)}), bf16[4,192,1536]{2,1,0:T(8,128)(2,1)S(1)}, u32[]{:S(2)}, u32[]{:S(2)}) async-start(bf16[4,192,1536]{2,1,0:T(8,128)(2,1)} %pad_maximum_fusion.2), calls=%async_computation | async-start | bytes 4718592 | tf_op jit(solution)/shard_map/all_to_all | solution.py:293
  153.4 25.8 %copy-start.18 = (bf16[3072,768]{1,0:T(8,128)(2,1)S(1)}, bf16[3072,768]{1,0:T(8,128)(2,1)}, u32[]{:S(2)}) copy-start(bf16[3072,768]{1,0:T(8,128)(2,1)} %reshape_squeeze.3) | copy-start | bytes 14155780
  179.2 3.7 copy-start.64
  179.2 14.5 %slice-start = ((s8[9437184]{0:T(1024)(128)(4,1)}), s8[4194304]{0:T(1024)(128)(4,1)S(1)}, s32[]{:S(2)}) async-start(s8[9437184]{0:T(1024)(128)(4,1)} %bitcast.176), calls=%async_computation.8 | async-start | bytes 8388608
  179.2 14.5 %slice-start.1 = ((s8[9437184]{0:T(1024)(128)(4,1)}), s8[4194304]{0:T(1024)(128)(4,1)S(1)}, s32[]{:S(2)}) async-start(s8[9437184]{0:T(1024)(128)(4,1)} %bitcast.176), calls=%async_computation.9 | async-start | bytes 8388608
  182.9 10.8 %slice-start.2 = ((s8[9437184]{0:T(1024)(128)(4,1)}), s8[1048576]{0:T(1024)(128)(4,1)S(1)}, s32[]{:S(2)}) async-start(s8[9437184]{0:T(1024)(128)(4,1)} %bitcast.176), calls=%async_computation.10 | async-start | bytes 2097152
  206.8 31.1 %copy-start.15 = (bf16[4,192,1536]{2,1,0:T(8,128)(2,1)}, bf16[4,192,1536]{2,1,0:T(8,128)(2,1)S(1)}, u32[]{:S(2)}) copy-start(bf16[4,192,1536]{2,1,0:T(8,128)(2,1)S(1)} %all-to-all-done) | copy-start | bytes 7077892
  206.8 70.1 %all-to-all-start.3 = ((bf16[4,184,1536]{2,1,0:T(8,128)(2,1)}), bf16[4,184,1536]{2,1,0:T(8,128)(2,1)}, u32[]{:S(2)}, u32[]{:S(2)}) async-start(bf16[4,184,1536]{2,1,0:T(8,128)(2,1)} %bitcast.15), calls=%async_computation.3 | async-start | bytes 4521984 | tf_op jit(solution)/shard_map/all_to_all | solution.py:329
  237.9 11.8 %copy-start.63 = (bf16[768,3072]{1,0:T(8,128)(2,1)}, bf16[768,3072]{1,0:T(8,128)(2,1)S(1)}, u32[]{:S(2)}) copy-start(bf16[768,3072]{1,0:T(8,128)(2,1)S(1)} %get-tuple-element.89) | copy-start | bytes 14155780
  249.7 8.2 %copy-start.19 = (bf16[768,3072]{1,0:T(8,128)(2,1)}, bf16[768,3072]{1,0:T(8,128)(2,1)S(1)}, u32[]{:S(2)}) copy-start(bf16[768,3072]{1,0:T(8,128)(2,1)S(1)} %fusion.6) | copy-start | bytes 14155780
  276.9 5.2 %copy-start.22 = (bf16[4,184,1536]{2,1,0:T(8,128)(2,1)S(1)}, bf16[4,184,1536]{2,1,0:T(8,128)(2,1)}, u32[]{:S(2)}) copy-start(bf16[4,184,1536]{2,1,0:T(8,128)(2,1)} %copy-done.21) | copy-start | bytes 6782980
  276.9 58.1 %all-to-all-start.1 = ((bf16[4,192,1536]{2,1,0:T(8,128)(2,1)}), bf16[4,192,1536]{2,1,0:T(8,128)(2,1)}, u32[]{:S(2)}, u32[]{:S(2)}) async-start(bf16[4,192,1536]{2,1,0:T(8,128)(2,1)} %bitcast.10), calls=%async_computation.1 | async-start | bytes 4718592 | tf_op jit(solution)/shard_map/all_to_all | solution.py:329
  282.1 173.9 %reduce-scatter.2.cloned.1.call-start = ((), (), s32[]{:S(2)}) async-start(), calls=%async_computation.7 | async-start | bytes 10616832 | tf_op jit(solution)/shard_map/reduce_scatter | solution.py:335
  292.2 8.6 %copy-start.16 = (bf16[4,192,1536]{2,1,0:T(8,128)(2,1)S(1)}, bf16[4,192,1536]{2,1,0:T(8,128)(2,1)}, u32[]{:S(2)}) copy-start(bf16[4,192,1536]{2,1,0:T(8,128)(2,1)} %copy-done.15) | copy-start | bytes 7077892
  300.9 5.9 %copy-start.23 = (bf16[4,184,1536]{2,1,0:T(8,128)(2,1)S(1)}, bf16[4,184,1536]{2,1,0:T(8,128)(2,1)}, u32[]{:S(2)}) copy-start(bf16[4,184,1536]{2,1,0:T(8,128)(2,1)} %copy-done.21) | copy-start | bytes 6782980
  324.0 5.5 %copy-start.30 = (pred[1504,591]{1,0:T(32,128)(4,1)S(1)}, pred[1504,591]{1,0:T(32,128)(4,1)}, u32[]{:S(2)}) copy-start(pred[1504,591]{1,0:T(32,128)(4,1)} %get-tuple-element.110) | copy-start | bytes 2666596
  335.0 6.1 %copy-start.62 = (f32[591,1536]{1,0:T(8,128)S(1)}, f32[591,1536]{1,0:T(8,128)}, u32[]{:S(2)}) copy-start(f32[591,1536]{1,0:T(8,128)} %fusion.55) | copy-start | bytes 10893316
  335.0 12.0 %slice-start.3 = ((s8[4915200]{0:T(1024)(128)(4,1)}), s8[4194304]{0:T(1024)(128)(4,1)S(1)}, s32[]{:S(2)}) async-start(s8[4915200]{0:T(1024)(128)(4,1)} %bitcast.191), calls=%async_computation.11 | async-start | bytes 8388608
  341.1 3.8 copy-start.4
  341.1 3.8 copy-start.8
  341.1 3.8 copy-start.35
  341.1 3.8 copy-start.60
  341.1 3.8 copy-start.61
  341.2 5.9 %slice-start.4 = ((s8[4915200]{0:T(1024)(128)(4,1)}), s8[720896]{0:T(1024)(128)(4,1)S(1)}, s32[]{:S(2)}) async-start(s8[4915200]{0:T(1024)(128)(4,1)} %bitcast.191), calls=%async_computation.12 | async-start | bytes 1441792
  370.3 3.5 copy-start.11
  380.3 5.7 %collective-permute-start = (bf16[2,2,96,1536]{3,2,1,0:T(8,128)(2,1)S(1)}, bf16[2,2,96,1536]{3,2,1,0:T(8,128)(2,1)S(1)}, u32[]{:S(2)}, u32[]{:S(2)}) collective-permute-start(bf16[2,2,96,1536]{3,2,1,0:T(8,128)(2,1)S(1)} %fusion.63), channel_id=1, source_target_pairs={{0,1},{1,0},{2,3},{3,2},{4,5},{5,4},{6,7},{7,6},{8,9},{9,8},{10,11... | collective-permute-start | bytes 3538952 | tf_op jit(solution)/shard_map/ppermute | solution.py:128
  382.6 7.0 %collective-permute-start.9 = (bf16[2,2,96,1664]{3,2,1,0:T(8,128)(2,1)S(1)}, bf16[2,2,96,1664]{3,2,1,0:T(8,128)(2,1)S(1)}, u32[]{:S(2)}, u32[]{:S(2)}) collective-permute-start(bf16[2,2,96,1664]{3,2,1,0:T(8,128)(2,1)S(1)} %fusion.62), channel_id=1, source_target_pairs={{0,1},{1,0},{2,3},{3,2},{4,5},{5,4},{6,7},{7,6},{8,9},{9,8},{10,11... | collective-permute-start | bytes 3833864 | tf_op jit(solution)/shard_map/ppermute | solution.py:128
  386.7 16.3 %collective-permute-start.3 = (bf16[2,96,768]{2,1,0:T(8,128)(2,1)S(1)}, bf16[2,96,768]{2,1,0:T(8,128)(2,1)S(1)}, u32[]{:S(2)}, u32[]{:S(2)}) collective-permute-start(bf16[2,96,768]{2,1,0:T(8,128)(2,1)S(1)} %fusion.86), channel_id=1, source_target_pairs={{0,4},{1,5},{2,6},{3,7},{4,0},{5,1},{6,2},{7,3},{8,12},{9,13},{10,... | collective-permute-start | bytes 884744 | tf_op jit(solution)/shard_map/ppermute | solution.py:128
  388.1 16.6 %collective-permute-start.1 = (bf16[2,96,768]{2,1,0:T(8,128)(2,1)S(1)}, bf16[2,96,768]{2,1,0:T(8,128)(2,1)S(1)}, u32[]{:S(2)}, u32[]{:S(2)}) collective-permute-start(bf16[2,96,768]{2,1,0:T(8,128)(2,1)S(1)} %fusion.85), channel_id=1, source_target_pairs={{0,2},{1,3},{2,0},{3,1},{4,6},{5,7},{6,4},{7,5},{8,10},{9,11},{10,... | collective-permute-start | bytes 884744 | tf_op jit(solution)/shard_map/ppermute | solution.py:128
  390.0 23.2 %collective-permute-start.12 = (bf16[2,96,896]{2,1,0:T(8,128)(2,1)S(1)}, bf16[2,96,896]{2,1,0:T(8,128)(2,1)S(1)}, u32[]{:S(2)}, u32[]{:S(2)}) collective-permute-start(bf16[2,96,896]{2,1,0:T(8,128)(2,1)S(1)} %fusion.84), channel_id=1, source_target_pairs={{0,4},{1,5},{2,6},{3,7},{4,0},{5,1},{6,2},{7,3},{8,12},{9,13},{10,... | collective-permute-start | bytes 1032200 | tf_op jit(solution)/shard_map/ppermute | solution.py:128
  391.1 20.5 %collective-permute-start.10 = (bf16[2,96,768]{2,1,0:T(8,128)(2,1)S(1)}, bf16[2,96,768]{2,1,0:T(8,128)(2,1)S(1)}, u32[]{:S(2)}, u32[]{:S(2)}) collective-permute-start(bf16[2,96,768]{2,1,0:T(8,128)(2,1)S(1)} %fusion.87), channel_id=1, source_target_pairs={{0,2},{1,3},{2,0},{3,1},{4,6},{5,7},{6,4},{7,5},{8,10},{9,11},{10,... | collective-permute-start | bytes 884744 | tf_op jit(solution)/shard_map/ppermute | solution.py:128
  403.0 11.3 %collective-permute-start.4 = (bf16[96,768]{1,0:T(8,128)(2,1)S(1)}, bf16[96,768]{1,0:T(8,128)(2,1)S(1)}, u32[]{:S(2)}, u32[]{:S(2)}) collective-permute-start(bf16[96,768]{1,0:T(8,128)(2,1)S(1)} %fusion.95), channel_id=1, source_target_pairs={{0,2},{1,3},{2,0},{3,1},{4,6},{5,7},{6,4},{7,5},{8,10},{9,11},{10,... | collective-permute-start | bytes 442376 | tf_op jit(solution)/shard_map/ppermute | solution.py:128
  404.8 10.9 %collective-permute-start.2 = (bf16[96,768]{1,0:T(8,128)(2,1)S(1)}, bf16[96,768]{1,0:T(8,128)(2,1)S(1)}, u32[]{:S(2)}, u32[]{:S(2)}) collective-permute-start(bf16[96,768]{1,0:T(8,128)(2,1)S(1)} %fusion.94), channel_id=1, source_target_pairs={{0,4},{1,5},{2,6},{3,7},{4,0},{5,1},{6,2},{7,3},{8,12},{9,13},{10,... | collective-permute-start | bytes 442376 | tf_op jit(solution)/shard_map/ppermute | solution.py:128
  411.7 6.9 %collective-permute-start.11 = (bf16[96,768]{1,0:T(8,128)(2,1)S(1)}, bf16[96,768]{1,0:T(8,128)(2,1)S(1)}, u32[]{:S(2)}, u32[]{:S(2)}) collective-permute-start(bf16[96,768]{1,0:T(8,128)(2,1)S(1)} %fusion.97), channel_id=1, source_target_pairs={{0,4},{1,5},{2,6},{3,7},{4,0},{5,1},{6,2},{7,3},{8,12},{9,13},{10,... | collective-permute-start | bytes 442376 | tf_op jit(solution)/shard_map/ppermute | solution.py:128
  413.3 10.4 %collective-permute-start.13 = (bf16[96,896]{1,0:T(8,128)(2,1)S(1)}, bf16[96,896]{1,0:T(8,128)(2,1)S(1)}, u32[]{:S(2)}, u32[]{:S(2)}) collective-permute-start(bf16[96,896]{1,0:T(8,128)(2,1)S(1)} %fusion.91), channel_id=1, source_target_pairs={{0,2},{1,3},{2,0},{3,1},{4,6},{5,7},{6,4},{7,5},{8,10},{9,11},{10,... | collective-permute-start | bytes 516104 | tf_op jit(solution)/shard_map/ppermute | solution.py:128
  415.8 5.3 %collective-permute-start.5 = (bf16[2,24,1536]{2,1,0:T(8,128)(2,1)S(1)}, bf16[2,24,1536]{2,1,0:T(8,128)(2,1)S(1)}, u32[]{:S(2)}, u32[]{:S(2)}) collective-permute-start(bf16[2,24,1536]{2,1,0:T(8,128)(2,1)S(1)} %fusion.96), channel_id=1, source_target_pairs={{0,8},{8,0},{16,24},{24,16},{1,9},{9,1},{17,25},{25,17},{2,10},{10... | collective-permute-start | bytes 442376 | tf_op jit(solution)/shard_map/ppermute | solution.py:128
  421.2 5.3 %collective-permute-start.6 = (bf16[24,1536]{1,0:T(8,128)(2,1)S(1)}, bf16[24,1536]{1,0:T(8,128)(2,1)S(1)}, u32[]{:S(2)}, u32[]{:S(2)}) collective-permute-start(bf16[24,1536]{1,0:T(8,128)(2,1)S(1)} %fusion.100), channel_id=1, source_target_pairs={{0,16},{8,24},{16,0},{24,8},{1,17},{9,25},{17,1},{25,9},{2,18},{10... | collective-permute-start | bytes 221192 | tf_op jit(solution)/shard_map/ppermute | solution.py:128
  426.6 5.3 %collective-permute-start.7 = (bf16[24,1536]{1,0:T(8,128)(2,1)S(1)}, bf16[24,1536]{1,0:T(8,128)(2,1)S(1)}, u32[]{:S(2)}, u32[]{:S(2)}) collective-permute-start(bf16[24,1536]{1,0:T(8,128)(2,1)S(1)} %fusion.98), channel_id=1, source_target_pairs={{0,16},{8,24},{16,0},{24,8},{1,17},{9,25},{17,1},{25,9},{2,18},{10... | collective-permute-start | bytes 221192 | tf_op jit(solution)/shard_map/ppermute | solution.py:152
  429.1 6.5 %collective-permute-start.14 = (bf16[2,24,1664]{2,1,0:T(8,128)(2,1)S(1)}, bf16[2,24,1664]{2,1,0:T(8,128)(2,1)S(1)}, u32[]{:S(2)}, u32[]{:S(2)}) collective-permute-start(bf16[2,24,1664]{2,1,0:T(8,128)(2,1)S(1)} %fusion.92), channel_id=1, source_target_pairs={{0,8},{8,0},{16,24},{24,16},{1,9},{9,1},{17,25},{25,17},{2,10},{10... | collective-permute-start | bytes 479240 | tf_op jit(solution)/shard_map/ppermute | solution.py:128
  435.7 6.3 %collective-permute-start.15 = (bf16[24,1664]{1,0:T(8,128)(2,1)S(1)}, bf16[24,1664]{1,0:T(8,128)(2,1)S(1)}, u32[]{:S(2)}, u32[]{:S(2)}) collective-permute-start(bf16[24,1664]{1,0:T(8,128)(2,1)S(1)} %fusion.99), channel_id=1, source_target_pairs={{0,16},{8,24},{16,0},{24,8},{1,17},{9,25},{17,1},{25,9},{2,18},{10... | collective-permute-start | bytes 239624 | tf_op jit(solution)/shard_map/ppermute | solution.py:128
  435.8 6.7 %collective-permute-start.8 = (bf16[2,24,1536]{2,1,0:T(8,128)(2,1)S(1)}, bf16[2,24,1536]{2,1,0:T(8,128)(2,1)S(1)}, u32[]{:S(2)}, u32[]{:S(2)}) collective-permute-start(bf16[2,24,1536]{2,1,0:T(8,128)(2,1)S(1)} %pad_maximum_fusion.11), channel_id=1, source_target_pairs={{0,8},{8,0},{16,24},{24,16},{1,9},{9,1},{17,25},{25,17},{2,10},{10... | collective-permute-start | bytes 442376 | tf_op jit(solution)/shard_map/ppermute | solution.py:152
  442.0 5.4 %collective-permute-start.16 = (bf16[24,1664]{1,0:T(8,128)(2,1)S(1)}, bf16[24,1664]{1,0:T(8,128)(2,1)S(1)}, u32[]{:S(2)}, u32[]{:S(2)}) collective-permute-start(bf16[24,1664]{1,0:T(8,128)(2,1)S(1)} %fusion.93), channel_id=1, source_target_pairs={{0,16},{8,24},{16,0},{24,8},{1,17},{9,25},{17,1},{25,9},{2,18},{10... | collective-permute-start | bytes 239624 | tf_op jit(solution)/shard_map/ppermute | solution.py:152
  447.5 5.3 %collective-permute-start.17 = (bf16[2,24,1664]{2,1,0:T(8,128)(2,1)S(1)}, bf16[2,24,1664]{2,1,0:T(8,128)(2,1)S(1)}, u32[]{:S(2)}, u32[]{:S(2)}) collective-permute-start(bf16[2,24,1664]{2,1,0:T(8,128)(2,1)S(1)} %pad_maximum_fusion.10), channel_id=1, source_target_pairs={{0,8},{8,0},{16,24},{24,16},{1,9},{9,1},{17,25},{25,17},{2,10},{10... | collective-permute-start | bytes 479240 | tf_op jit(solution)/shard_map/ppermute | solution.py:152
  (31 other events, 48.3 us)
Sparse Core Ops, SparseCore 0:
  11.7 42.3 all-gather.2
  56.5 58.6 all-gather.4
  322.9 86.2 reduce-scatter.1

commit v14 on v12

--- a/solution.py
+++ b/solution.py
@@ -394,15 +394,8 @@
     )
     small = jnp.pad(small, ((0, 0), (0, 128 - small.shape[1])))
     dense_grads = jnp.concatenate([grad_qkv, grad_wout, small], axis=1)
-    chunk_cols = 128 * (dense_grads.shape[1] // 256)
-    dense_total = jnp.concatenate(
-        [
-            expert_all_reduce(
-                shard_reduce_scatter(part, "shard", 128 * (part.shape[1] // 256)), "expert"
-            )
-            for part in (dense_grads[:, :chunk_cols], dense_grads[:, chunk_cols:])
-        ],
-        axis=1,
+    dense_total = expert_all_reduce(
+        shard_reduce_scatter(dense_grads, "shard", 128 * (dense_grads.shape[1] // 256)), "expert"
     )
     return (
         output,

time: 475 us -> 493 us (1.038)
  local copies, waits for them, and re-layouts: 48.6 us -> 60.6 us
  other arithmetic: 33.9 us -> 43.3 us
  starting transfers between devices: 39 us -> 33 us
    unnamed x146 -> x148, local copies, waits for them, and re-layouts: 9.56 us -> 17.3 us
    ppermute x14 -> x7, waiting for transfers between devices: 31 us -> 37.6 us  [_exchange(): got = lax.ppermute(send.astype(jnp.bfloat16), axis_name, pairs)]
    ppermute x14 -> x7, starting transfers between devices: 15.3 us -> 9.27 us  [_exchange(): got = lax.ppermute(send.astype(jnp.bfloat16), axis_name, pairs)]
    add x12 -> x6, other arithmetic: 1.02 us -> 6.22 us  [_exchange(): return (keep + got.astype(jnp.float32), [b for b in bits_left if b != bit])]
    ppermute x4 -> x2, waiting for transfers between devices: 11.5 us -> 7.01 us  [_gather_back(): got = lax.ppermute(values, axis_name, pairs)]
  transfers between devices with their start and end apart: 25 -> 16, of which waited for: 16 -> 13; matrix products, arithmetic and copies ran while one was open for 54% -> 55% of each run, Pallas kernels for 8% -> 7%
where the time goes in v14:
time: 493 us; the launch traced here: 485 us
  matrix products  187 us (38%)
  waiting for transfers between devices  110 us (22%)
  local copies, waits for them, and re-layouts  60.6 us (12%)
  other arithmetic  43.3 us (9%)
  Pallas kernels  35 us (7%)
  starting transfers between devices  33 us (7%)
  between operations  16.1 us (3%)
    dot_general x2, matrix products, shards(): jnp.dot(flat_arrived, expert_first, preferred_element_type=jnp.float32)  52 us
    ppermute x7, waiting for transfers between devices, _exchange(): got = lax.ppermute(send.astype(jnp.bfloat16), axis_name, pairs)  37.6 us
    all_gather x1, waiting for transfers between devices, shards(): dense_full = lax.all_gather(dense_local, 'shard', axis=0, tiled=True)  29.2 us
    all_to_all x2, waiting for transfers between devices, shards(): lax.all_to_all(dispatch_rows(experts * start, experts * (start + size)).r...  23 us
    dot_general x2, matrix products, shards(): lax.dot_general(flat_grad, expert_second, COL_CONTRACT, preferred_element...  22.6 us
    pallas_call x1, Pallas kernels, attention_bwd(): pl.pallas_call(functools.partial(attn_bwd_kernel, images=images), grid=(p...  21.6 us
    dot_general x2, matrix products, shards(): lax.dot_general(activated, flat_grad, ROW_CONTRACT, preferred_element_typ...  20.4 us
    unnamed x148, local copies, waits for them, and re-layouts  17.3 us
  transfers between devices with their start and end apart: 16, of which 13 were waited for; matrix products, arithmetic and copies ran while one was open for 55% of the time, Pallas kernels for 7%

profile of v14, /device:TPU:0, one launch (start us, length us, event | category | flops | bytes accessed | tf_op | source)
XLA Modules:
  0.0 485.1 jit_solution(197406068291598840)
XLA Ops:
  9.6 1.9 concatenate.46
  13.2 2.3 pad_maximum_fusion.6
  21.6 3.3 fusion.106
  24.9 29.2 %all-gather.3.cloned.1.call-done = bf16[768,3078]{1,0:T(8,128)(2,1)} async-done(((bf16[96,3078]{1,0:T(8,128)(2,1)}), bf16[768,3078]{1,0:T(8,128)(2,1)}) %all-gather.3.cloned.1.call-update) | async-done | bytes 4727824 | tf_op jit(solution)/shard_map/all_gather | solution.py:217
  55.8 4.6 convolution_convert_fusion
  60.7 13.4 %shard_map.178 = bf16[640,768]{1,0:T(8,128)(2,1)S(1)} custom-call(bf16[640,2304]{1,0:T(8,128)(2,1)S(1)} %pad.18.q_ref.k_ref.v_ref, bf16[640,2304]{1,0:T(8,128)(2,1)S(1)} %pad.18.q_ref.k_ref.v_ref, bf16[640,2304]{1,0:T(8,128)(2,1)S(1)} %pad.18.q_ref.k_ref.v_ref), custom_call_target="tpu_custom_call" | custom-call | tf_op jit(solution)/shard_map/pallas_call | solution.py:90
  74.1 2.6 fusion.112
  80.7 2.7 fusion.60
  83.4 2.3 convolution_convert_fusion.4
  85.7 2.4 add_convert_fusion.3
  89.6 4.6 all-to-all-start.2
  94.8 3.0 fusion.53
  102.4 12.8 %all-gather.5.cloned.1.call-done = bf16[2,768,3072]{2,1,0:T(8,128)(2,1)} async-done(((bf16[2,96,3072]{2,1,0:T(8,128)(2,1)}), bf16[2,768,3072]{2,1,0:T(8,128)(2,1)}) %all-gather.5.cloned.1.call-update) | async-done | bytes 9437200 | tf_op jit(solution)/shard_map/all_gather | solution.py:228
  115.3 4.9 %slice.195 = bf16[1,768,3072]{2,1,0:T(8,128)(2,1)} slice(bf16[2,768,3072]{2,1,0:T(8,128)(2,1)} %all-gather.5.cloned.1.call-done), slice={[1:2], [0:768], [0:3072]} | slice | bytes 9437184 | tf_op jit(solution)/shard_map/slice | solution.py:230
  120.2 8.5 %reshape_squeeze.3 = bf16[3072,768]{1,0:T(8,128)(2,1)} reshape(bf16[1,768,3072]{2,1,0:T(8,128)(2,1)} %slice.195) | data formatting | bytes 9437184 | tf_op jit(solution)/shard_map/reshape;squeeze | solution.py:230
  128.6 17.7 %all-to-all-done.2 = bf16[4,184,1536]{2,1,0:T(8,128)(2,1)S(1)} async-done(((bf16[4,184,1536]{2,1,0:T(8,128)(2,1)}), bf16[4,184,1536]{2,1,0:T(8,128)(2,1)S(1)}, u32[]{:S(2)}, u32[]{:S(2)}) %all-to-all-start.2) | async-done | bytes 2261024 | tf_op jit(solution)/shard_map/all_to_all | solution.py:286
  147.7 3.8 all-to-all-start
  151.5 25.8 %multiply_convert_fusion.1 = (bf16[736,3072]{1,0:T(8,128)(2,1)S(1)}, f32[736,3072]{1,0:T(8,128)}, f32[736,3072]{1,0:T(8,128)}) fusion(bf16[2,768,3072]{2,1,0:T(8,128)(2,1)} %all-gather.5.cloned.1.call-done, bf16[736,1536]{1,0:T(8,128)(2,1)} %bitcast.133), kind=kOutput, calls=%fused_computation.38 | convolution fusion | flops 3619848192 | bytes 28459008 | tf_op jit(solution)/shard_map/dot_general | solution.py:300
  177.3 3.7 convolution_convert_fusion.3
  181.0 10.8 %fusion.19 = bf16[736,3072]{1,0:T(8,128)(2,1)} fusion(f32[736,3072]{1,0:T(8,128)} %get-tuple-element.106, f32[736,3072]{1,0:T(8,128)} %get-tuple-element.88, bf16[3072,768]{1,0:T(8,128)(2,1)S(1)} %copy-done.19, bf16[736,1536]{1,0:T(8,128)(2,1)} %bitcast.134), kind=kOutput, calls=%fused_computation.37 | convolution fusion | flops 3490971648 | bytes 28459008 | tf_op jit(solution)/shard_map/dot_general | solution.py:297
  191.8 6.1 %fusion.49 = bf16[736,768]{1,0:T(8,128)(2,1)S(1)} fusion(bf16[736,3072]{1,0:T(8,128)(2,1)} %fusion.19, bf16[2,768,3072]{2,1,0:T(8,128)(2,1)S(1)} %bitcast.132), kind=kOutput, calls=%fused_computation.109 | convolution fusion | flops 3473448960 | bytes 10371072 | tf_op jit(solution)/shard_map/dot_general | solution.py:307
  199.5 5.3 %all-to-all-done = bf16[4,192,1536]{2,1,0:T(8,128)(2,1)S(1)} async-done(((bf16[4,192,1536]{2,1,0:T(8,128)(2,1)}), bf16[4,192,1536]{2,1,0:T(8,128)(2,1)S(1)}, u32[]{:S(2)}, u32[]{:S(2)}) %all-to-all-start) | async-done | bytes 2359328 | tf_op jit(solution)/shard_map/all_to_all | solution.py:286
  204.8 4.9 %all-to-all-start.3 = ((bf16[4,184,1536]{2,1,0:T(8,128)(2,1)}), bf16[4,184,1536]{2,1,0:T(8,128)(2,1)}, u32[]{:S(2)}, u32[]{:S(2)}) async-start(bf16[4,184,1536]{2,1,0:T(8,128)(2,1)} %bitcast.15), calls=%async_computation.3 | async-start | bytes 4521984 | tf_op jit(solution)/shard_map/all_to_all | solution.py:322
  209.7 26.2 %multiply_convert_fusion = (bf16[768,3072]{1,0:T(8,128)(2,1)S(1)}, f32[768,3072]{1,0:T(8,128)}, f32[768,3072]{1,0:T(8,128)}) fusion(bf16[2,768,3072]{2,1,0:T(8,128)(2,1)} %all-gather.5.cloned.1.call-done, bf16[768,1536]{1,0:T(8,128)(2,1)S(1)} %bitcast.125), kind=kOutput, calls=%fused_computation.16 | convolution fusion | flops 3777232896 | bytes 29491200 | tf_op jit(solution)/shard_map/dot_general | solution.py:300
  235.9 11.8 %fusion.6 = bf16[768,3072]{1,0:T(8,128)(2,1)S(1)} fusion(f32[768,3072]{1,0:T(8,128)} %get-tuple-element.107, f32[768,3072]{1,0:T(8,128)} %get-tuple-element.86, bf16[3072,768]{1,0:T(8,128)(2,1)} %reshape_squeeze.3, bf16[768,1536]{1,0:T(8,128)(2,1)S(1)} %bitcast.126), kind=kOutput, calls=%fused_computation.12 | convolution fusion | flops 3642753024 | bytes 29491200 | tf_op jit(solution)/shard_map/dot_general | solution.py:297
  247.7 8.1 %convolution_convert_fusion.1 = bf16[768,768]{0,1:T(8,128)(2,1)S(1)} fusion(bf16[768,3072]{1,0:T(8,128)(2,1)S(1)} %get-tuple-element.85, bf16[3072,768]{1,0:T(8,128)(2,1)} %reshape_squeeze.3), kind=kOutput, calls=%fused_computation.107 | convolution fusion | flops 3624468480 | bytes 10616832 | tf_op jit(solution)/shard_map/dot_general | solution.py:304
  255.9 6.3 %fusion.48 = bf16[768,768]{0,1:T(8,128)(2,1)S(1)} fusion(bf16[768,3072]{1,0:T(8,128)(2,1)S(1)} %fusion.6, bf16[2,768,3072]{2,1,0:T(8,128)(2,1)} %all-gather.5.cloned.1.call-done), kind=kOutput, calls=%fused_computation.106 | convolution fusion | flops 3624468480 | bytes 10616832 | tf_op jit(solution)/shard_map/dot_general | solution.py:307
  262.3 2.4 copy.100
  264.7 10.2 %fusion.63 = f32[3072,768]{1,0:T(8,128)} fusion(bf16[768,3072]{1,0:T(8,128)(2,1)} %copy-done.64, bf16[768,1536]{1,0:T(8,128)(2,1)} %bitcast.127), kind=kOutput, calls=%fused_computation.132 | convolution fusion | flops 3623878656 | bytes 15335424 | tf_op jit(solution)/shard_map/dot_general | solution.py:310
  275.0 5.2 %all-to-all-start.1 = ((bf16[4,192,1536]{2,1,0:T(8,128)(2,1)}), bf16[4,192,1536]{2,1,0:T(8,128)(2,1)}, u32[]{:S(2)}, u32[]{:S(2)}) async-start(bf16[4,192,1536]{2,1,0:T(8,128)(2,1)} %bitcast.10), calls=%async_computation.1 | async-start | bytes 4718592 | tf_op jit(solution)/shard_map/all_to_all | solution.py:322
  280.2 10.2 %add_convert_fusion = bf16[3072,768]{1,0:T(8,128)(2,1)} fusion(f32[3072,768]{1,0:T(8,128)} %fusion.63, bf16[736,3072]{1,0:T(8,128)(2,1)} %copy-done.65, bf16[736,1536]{1,0:T(8,128)(2,1)S(1)} %bitcast.135), kind=kOutput, calls=%fused_computation.14 | convolution fusion | flops 3477602304 | bytes 19808256 | tf_op jit(solution)/shard_map/dot_general | solution.py:310
  290.4 8.6 %stack_reshape.4 = bf16[1,768,3072]{2,1,0:T(8,128)(2,1)} reshape(bf16[3072,768]{1,0:T(8,128)(2,1)} %add_convert_fusion) | data formatting | bytes 9437184 | tf_op jit(solution)/shard_map/stack;reshape | solution.py:325
  299.0 5.9 %fusion.66 = f32[768,3072]{1,0:T(8,128)S(1)} fusion(bf16[768,3072]{1,0:T(8,128)(2,1)} %copy-done.20, bf16[768,1536]{1,0:T(8,128)(2,1)S(1)} %bitcast.128), kind=kOutput, calls=%fused_computation.135 | convolution fusion | flops 3623878656 | bytes 15335424 | tf_op jit(solution)/shard_map/dot_general | solution.py:313
  304.9 7.9 %fusion.26 = bf16[1,768,3072]{2,1,0:T(8,128)(2,1)} fusion(f32[768,3072]{1,0:T(8,128)S(1)} %fusion.66, bf16[736,3072]{1,0:T(8,128)(2,1)} %fusion.19, bf16[736,1536]{1,0:T(8,128)(2,1)S(1)} %bitcast.136), kind=kOutput, calls=%fused_computation.57 | convolution fusion | flops 3477602304 | bytes 19808256 | tf_op jit(solution)/shard_map/dot_general | solution.py:313
  312.8 8.3 %pad_maximum_fusion = bf16[2,768,3072]{2,1,0:T(8,128)(2,1)} fusion(bf16[1,768,3072]{2,1,0:T(8,128)(2,1)} %stack_reshape.4, bf16[1,768,3072]{2,1,0:T(8,128)(2,1)} %fusion.26), kind=kLoop, calls=%fused_computation.13 | loop fusion | flops 4718592 | bytes 18874368 | tf_op jit(solution)/shard_map/stack | solution.py:325
  322.3 5.5 %fusion.58 = f32[591,1536]{1,0:T(8,128)} fusion(bf16[736,1536]{1,0:T(8,128)(2,1)} %bitcast.16, pred[1504,591]{1,0:T(32,128)(4,1)S(1)} %copy-done.34), kind=kOutput, calls=%fused_computation.121 | convolution fusion | flops 1336246272 | bytes 6363136 | tf_op jit(solution)/shard_map/dot_general | solution.py:338
  327.8 5.4 %fusion.55 = f32[591,1536]{1,0:T(8,128)} fusion(bf16[736,1536]{1,0:T(8,128)(2,1)} %bitcast.16, pred[1504,591]{1,0:T(32,128)(4,1)S(1)} %copy-done.33), kind=kOutput, calls=%fused_computation.118 | convolution fusion | flops 1336246272 | bytes 6363136 | tf_op jit(solution)/shard_map/dot_general | solution.py:341
  333.2 6.0 %convolution_add_fusion.1 = f32[591,1536]{1,0:T(8,128)S(1)} fusion(f32[591,1536]{1,0:T(8,128)} %fusion.58, bf16[768,1536]{1,0:T(8,128)(2,1)} %bitcast.11, pred[1504,591]{1,0:T(32,128)(4,1)S(1)} %copy-done.34), kind=kOutput, calls=%fused_computation.60 | convolution fusion | flops 1395251712 | bytes 10113024 | tf_op jit(solution)/shard_map/dot_general | solution.py:338
  339.3 3.8 convolution_add_fusion
  343.2 1.8 multiply_reduce_fusion.3
  347.7 2.8 fusion.79
  351.5 21.6 %shard_map.179 = (bf16[640,768]{1,0:T(8,128)(2,1)S(1)}, bf16[640,768]{1,0:T(8,128)(2,1)S(1)}, bf16[640,768]{1,0:T(8,128)(2,1)S(1)}) custom-call(bf16[640,2304]{1,0:T(8,128)(2,1)} %copy-done, bf16[640,2304]{1,0:T(8,128)(2,1)} %copy-done, bf16[640,2304]{1,0:T(8,128)(2,1)} %copy-done, bf16[640,768]{1,0:T(8,128)(2,1)S(1)} %pad.20.g_ref), custom_call_target="tpu_custom_call" | custom-call | tf_op jit(solution)/shard_map/pallas_call | solution.py:106
  374.4 5.0 %fusion.76 = f32[768,2304]{1,0:T(8,128)} fusion(bf16[640,2304]{1,0:T(8,128)(2,1)S(1)} %constant_dynamic-update-slice_fusion, bf16[591,768]{1,0:T(8,128)(2,1)S(1)} %copy-done.23), kind=kOutput, calls=%fused_computation.146 | convolution fusion | flops 2264924160 | bytes 10934784 | tf_op jit(solution)/shard_map/dot_general | solution.py:382
  379.4 2.4 fusion.45
  384.3 4.5 select_maximum_fusion
  388.8 3.8 copy-done.5
  392.6 1.7 fusion.39
  394.3 5.0 %collective-permute-done = bf16[2,2,96,3200]{3,2,1,0:T(8,128)(2,1)} collective-permute-done((bf16[2,2,96,3200]{3,2,1,0:T(8,128)(2,1)}, bf16[2,2,96,3200]{3,2,1,0:T(8,128)(2,1)}, u32[]{:S(2)}, u32[]{:S(2)}) %collective-permute-start) | collective-permute-done | bytes 2457632 | tf_op jit(solution)/shard_map/ppermute | solution.py:122
  399.3 3.6 bitcast_add_fusion
  402.9 2.2 copy-done.8
  408.5 2.0 slice.210
  411.9 10.5 %collective-permute-done.1 = bf16[2,96,1536]{2,1,0:T(8,128)(2,1)} collective-permute-done((bf16[2,96,1536]{2,1,0:T(8,128)(2,1)S(1)}, bf16[2,96,1536]{2,1,0:T(8,128)(2,1)}, u32[]{:S(2)}, u32[]{:S(2)}) %collective-permute-start.1) | collective-permute-done | bytes 589856 | tf_op jit(solution)/shard_map/ppermute | solution.py:122
  425.2 2.8 collective-permute-done.3
  428.2 5.0 %collective-permute-done.2 = bf16[96,1536]{1,0:T(8,128)(2,1)S(1)} collective-permute-done((bf16[96,1536]{1,0:T(8,128)(2,1)S(1)}, bf16[96,1536]{1,0:T(8,128)(2,1)S(1)}, u32[]{:S(2)}, u32[]{:S(2)}) %collective-permute-start.2) | collective-permute-done | bytes 294944 | tf_op jit(solution)/shard_map/ppermute | solution.py:122
  433.3 2.3 collective-permute-done.4
  436.8 2.0 collective-permute-start.5
  438.7 5.1 %collective-permute-done.5 = bf16[2,24,3200]{2,1,0:T(8,128)(2,1)} collective-permute-done((bf16[2,24,3200]{2,1,0:T(8,128)(2,1)S(1)}, bf16[2,24,3200]{2,1,0:T(8,128)(2,1)}, u32[]{:S(2)}, u32[]{:S(2)}) %collective-permute-start.5) | collective-permute-done | bytes 307232 | tf_op jit(solution)/shard_map/ppermute | solution.py:122
  445.7 2.8 collective-permute-start.6
  448.5 7.1 %collective-permute-done.6 = bf16[24,3200]{1,0:T(8,128)(2,1)S(1)} collective-permute-done((bf16[24,3200]{1,0:T(8,128)(2,1)}, bf16[24,3200]{1,0:T(8,128)(2,1)S(1)}, u32[]{:S(2)}, u32[]{:S(2)}) %collective-permute-start.6) | collective-permute-done | bytes 153632 | tf_op jit(solution)/shard_map/ppermute | solution.py:122
  456.6 5.3 %collective-permute-done.7 = bf16[24,3200]{1,0:T(8,128)(2,1)S(1)} collective-permute-done((bf16[24,3200]{1,0:T(8,128)(2,1)S(1)}, bf16[24,3200]{1,0:T(8,128)(2,1)S(1)}, u32[]{:S(2)}, u32[]{:S(2)}) %collective-permute-start.7) | collective-permute-done | bytes 153632 | tf_op jit(solution)/shard_map/ppermute | solution.py:146
  461.9 4.2 collective-permute-start.8
  466.1 3.1 add_convert_fusion.4
  469.2 1.7 collective-permute-done.8
  474.3 2.5 fusion.111
  (261 shorter events, 50.3 us)
Async XLA Ops:
  7.2 46.9 %all-gather.3.cloned.1.call-start = ((), (), s32[]{:S(2)}) async-start(), calls=%async_computation.5 | async-start | bytes 5529600 | tf_op jit(solution)/shard_map/all_gather | solution.py:217
  8.8 7.7 %copy-start.45 = (s32[591,2]{0,1:T(2,128)S(1)}, s32[591,2]{0,1:T(2,128)}, u32[]{:S(2)}) copy-start(s32[591,2]{0,1:T(2,128)} %param.13) | copy-start | bytes 14188
  11.6 7.9 %copy-start.6 = (bf16[591,768]{1,0:T(8,128)(2,1)S(1)}, bf16[591,768]{1,0:T(8,128)(2,1)}, u32[]{:S(2)}) copy-start(bf16[591,768]{1,0:T(8,128)(2,1)} %param.11) | copy-start | bytes 2723332
  11.6 103.7 %all-gather.5.cloned.1.call-start = ((), (), s32[]{:S(2)}) async-start(), calls=%async_computation.6 | async-start | bytes 10616832 | tf_op jit(solution)/shard_map/all_gather | solution.py:228
  13.2 6.9 %copy-start.9 = (bf16[591,768]{1,0:T(8,128)(2,1)S(1)}, bf16[591,768]{1,0:T(8,128)(2,1)}, u32[]{:S(2)}) copy-start(bf16[591,768]{1,0:T(8,128)(2,1)} %param.21) | copy-start | bytes 2723332
  19.4 60.5 %copy-start.35 = (f32[591]{0:T(1024)}, f32[591]{0:T(1024)S(1)}, u32[]{:S(2)}) copy-start(f32[591]{0:T(1024)S(1)} %fusion.103) | copy-start | bytes 7096
  19.6 35.8 %copy-start.43 = (f32[591]{0:T(1024)}, f32[591]{0:T(1024)S(1)}, u32[]{:S(2)}) copy-start(f32[591]{0:T(1024)S(1)} %broadcast_multiply_fusion.2) | copy-start | bytes 7096
  20.1 35.4 %copy-start.55 = (f32[591]{0:T(1024)}, f32[591]{0:T(1024)S(1)}, u32[]{:S(2)}) copy-start(f32[591]{0:T(1024)S(1)} %fusion.101) | copy-start | bytes 7096
  24.9 58.5 %copy-start.27 = (bf16[1504,591]{1,0:T(8,128)(2,1)}, bf16[1504,591]{1,0:T(8,128)(2,1)S(1)}, u32[]{:S(2)}) copy-start(bf16[1504,591]{1,0:T(8,128)(2,1)S(1)} %get-tuple-element.96) | copy-start | bytes 5333188
  55.4 5.0 %copy-start.53 = (f32[768]{0:T(1024)}, f32[768]{0:T(1024)S(1)}, u32[]{:S(2)}) copy-start(f32[768]{0:T(1024)S(1)} %get-tuple-element.70) | copy-start | bytes 9220
  55.5 22.2 %copy-start.47 = (f32[768]{0:T(1024)}, f32[768]{0:T(1024)S(1)}, u32[]{:S(2)}) copy-start(f32[768]{0:T(1024)S(1)} %get-tuple-element.69) | copy-start | bytes 9220
  55.8 4.6 copy-start.22
  60.7 13.4 %copy-start = (bf16[640,2304]{1,0:T(8,128)(2,1)}, bf16[640,2304]{1,0:T(8,128)(2,1)S(1)}, u32[]{:S(2)}) copy-start(bf16[640,2304]{1,0:T(8,128)(2,1)S(1)} %pad.18.q_ref.k_ref.v_ref) | copy-start | bytes 8847364
  74.1 3.0 copy-start.1
  76.7 3.7 copy-start.14
  77.7 3.0 copy-start.49
  78.2 19.6 %copy-start.11 = (bf16[591,768]{1,0:T(8,128)(2,1)}, bf16[591,768]{1,0:T(8,128)(2,1)S(1)}, u32[]{:S(2)}) copy-start(bf16[591,768]{1,0:T(8,128)(2,1)S(1)} %multiply_convert_fusion.4) | copy-start | bytes 2723332
  80.7 5.0 %copy-start.30 = (bf16[591,2,768]{2,0,1:T(8,128)(2,1)}, bf16[591,2,768]{2,0,1:T(8,128)(2,1)S(1)}, u32[]{:S(2)}) copy-start(bf16[591,2,768]{2,0,1:T(8,128)(2,1)S(1)} %multiply_convert_fusion.2) | copy-start | bytes 5446660
  89.6 56.7 %all-to-all-start.2 = ((bf16[4,184,1536]{2,1,0:T(8,128)(2,1)}), bf16[4,184,1536]{2,1,0:T(8,128)(2,1)S(1)}, u32[]{:S(2)}, u32[]{:S(2)}) async-start(bf16[4,184,1536]{2,1,0:T(8,128)(2,1)} %pad_maximum_fusion.3), calls=%async_computation.2 | async-start | bytes 4521984 | tf_op jit(solution)/shard_map/all_to_all | solution.py:286
  94.2 3.6 copy-start.28
  94.2 3.6 copy-start.29
  147.7 57.2 %all-to-all-start = ((bf16[4,192,1536]{2,1,0:T(8,128)(2,1)}), bf16[4,192,1536]{2,1,0:T(8,128)(2,1)S(1)}, u32[]{:S(2)}, u32[]{:S(2)}) async-start(bf16[4,192,1536]{2,1,0:T(8,128)(2,1)} %pad_maximum_fusion.1), calls=%async_computation | async-start | bytes 4718592 | tf_op jit(solution)/shard_map/all_to_all | solution.py:286
  151.5 25.8 %copy-start.19 = (bf16[3072,768]{1,0:T(8,128)(2,1)S(1)}, bf16[3072,768]{1,0:T(8,128)(2,1)}, u32[]{:S(2)}) copy-start(bf16[3072,768]{1,0:T(8,128)(2,1)} %reshape_squeeze.3) | copy-start | bytes 14155780
  177.3 3.7 copy-start.65
  177.3 14.5 %slice-start = ((s8[9437184]{0:T(1024)(128)(4,1)}), s8[4194304]{0:T(1024)(128)(4,1)S(1)}, s32[]{:S(2)}) async-start(s8[9437184]{0:T(1024)(128)(4,1)} %bitcast.131), calls=%async_computation.8 | async-start | bytes 8388608
  177.3 14.5 %slice-start.1 = ((s8[9437184]{0:T(1024)(128)(4,1)}), s8[4194304]{0:T(1024)(128)(4,1)S(1)}, s32[]{:S(2)}) async-start(s8[9437184]{0:T(1024)(128)(4,1)} %bitcast.131), calls=%async_computation.9 | async-start | bytes 8388608
  181.0 10.8 %slice-start.2 = ((s8[9437184]{0:T(1024)(128)(4,1)}), s8[1048576]{0:T(1024)(128)(4,1)S(1)}, s32[]{:S(2)}) async-start(s8[9437184]{0:T(1024)(128)(4,1)} %bitcast.131), calls=%async_computation.10 | async-start | bytes 2097152
  204.8 31.1 %copy-start.17 = (bf16[4,192,1536]{2,1,0:T(8,128)(2,1)}, bf16[4,192,1536]{2,1,0:T(8,128)(2,1)S(1)}, u32[]{:S(2)}) copy-start(bf16[4,192,1536]{2,1,0:T(8,128)(2,1)S(1)} %all-to-all-done) | copy-start | bytes 7077892
  204.8 70.1 %all-to-all-start.3 = ((bf16[4,184,1536]{2,1,0:T(8,128)(2,1)}), bf16[4,184,1536]{2,1,0:T(8,128)(2,1)}, u32[]{:S(2)}, u32[]{:S(2)}) async-start(bf16[4,184,1536]{2,1,0:T(8,128)(2,1)} %bitcast.15), calls=%async_computation.3 | async-start | bytes 4521984 | tf_op jit(solution)/shard_map/all_to_all | solution.py:322
  235.9 11.8 %copy-start.64 = (bf16[768,3072]{1,0:T(8,128)(2,1)}, bf16[768,3072]{1,0:T(8,128)(2,1)S(1)}, u32[]{:S(2)}) copy-start(bf16[768,3072]{1,0:T(8,128)(2,1)S(1)} %get-tuple-element.85) | copy-start | bytes 14155780
  247.7 8.2 %copy-start.20 = (bf16[768,3072]{1,0:T(8,128)(2,1)}, bf16[768,3072]{1,0:T(8,128)(2,1)S(1)}, u32[]{:S(2)}) copy-start(bf16[768,3072]{1,0:T(8,128)(2,1)S(1)} %fusion.6) | copy-start | bytes 14155780
  275.0 5.2 %copy-start.25 = (bf16[4,184,1536]{2,1,0:T(8,128)(2,1)S(1)}, bf16[4,184,1536]{2,1,0:T(8,128)(2,1)}, u32[]{:S(2)}) copy-start(bf16[4,184,1536]{2,1,0:T(8,128)(2,1)} %copy-done.24) | copy-start | bytes 6782980
  275.0 58.2 %all-to-all-start.1 = ((bf16[4,192,1536]{2,1,0:T(8,128)(2,1)}), bf16[4,192,1536]{2,1,0:T(8,128)(2,1)}, u32[]{:S(2)}, u32[]{:S(2)}) async-start(bf16[4,192,1536]{2,1,0:T(8,128)(2,1)} %bitcast.10), calls=%async_computation.1 | async-start | bytes 4718592 | tf_op jit(solution)/shard_map/all_to_all | solution.py:322
  280.2 194.1 %reduce-scatter.2.cloned.1.call-start = ((), (), s32[]{:S(2)}) async-start(), calls=%async_computation.7 | async-start | bytes 10616832 | tf_op jit(solution)/shard_map/reduce_scatter | solution.py:328
  290.4 8.6 %copy-start.18 = (bf16[4,192,1536]{2,1,0:T(8,128)(2,1)S(1)}, bf16[4,192,1536]{2,1,0:T(8,128)(2,1)}, u32[]{:S(2)}) copy-start(bf16[4,192,1536]{2,1,0:T(8,128)(2,1)} %copy-done.17) | copy-start | bytes 7077892
  299.0 5.9 %copy-start.26 = (bf16[4,184,1536]{2,1,0:T(8,128)(2,1)S(1)}, bf16[4,184,1536]{2,1,0:T(8,128)(2,1)}, u32[]{:S(2)}) copy-start(bf16[4,184,1536]{2,1,0:T(8,128)(2,1)} %copy-done.24) | copy-start | bytes 6782980
  322.3 5.5 %copy-start.33 = (pred[1504,591]{1,0:T(32,128)(4,1)S(1)}, pred[1504,591]{1,0:T(32,128)(4,1)}, u32[]{:S(2)}) copy-start(pred[1504,591]{1,0:T(32,128)(4,1)} %get-tuple-element.100) | copy-start | bytes 2666596
  333.2 6.1 %copy-start.63 = (f32[591,1536]{1,0:T(8,128)S(1)}, f32[591,1536]{1,0:T(8,128)}, u32[]{:S(2)}) copy-start(f32[591,1536]{1,0:T(8,128)} %fusion.55) | copy-start | bytes 10893316
  333.2 12.2 %slice-start.3 = ((s8[4915200]{0:T(1024)(128)(4,1)}), s8[4194304]{0:T(1024)(128)(4,1)S(1)}, s32[]{:S(2)}) async-start(s8[4915200]{0:T(1024)(128)(4,1)} %bitcast.141), calls=%async_computation.11 | async-start | bytes 8388608
  339.2 3.9 copy-start.4
  339.2 3.9 copy-start.10
  339.3 3.9 copy-start.36
  339.3 3.9 copy-start.61
  339.3 3.9 copy-start.62
  339.3 6.1 %slice-start.4 = ((s8[4915200]{0:T(1024)(128)(4,1)}), s8[720896]{0:T(1024)(128)(4,1)S(1)}, s32[]{:S(2)}) async-start(s8[4915200]{0:T(1024)(128)(4,1)} %bitcast.141), calls=%async_computation.12 | async-start | bytes 1441792
  343.2 2.2 copy-start.48
  343.2 2.2 copy-start.50
  374.4 5.0 %copy-start.7 = (bf16[591,768]{1,0:T(8,128)(2,1)S(1)}, bf16[591,768]{1,0:T(8,128)(2,1)}, u32[]{:S(2)}) copy-start(bf16[591,768]{1,0:T(8,128)(2,1)} %param.11) | copy-start | bytes 2723332
  374.4 5.0 %copy-start.44 = (f32[591]{0:T(1024)S(1)}, f32[591]{0:T(1024)}, u32[]{:S(2)}) copy-start(f32[591]{0:T(1024)} %copy-done.43) | copy-start | bytes 7096
  374.4 5.0 %copy-start.54 = (f32[768]{0:T(1024)S(1)}, f32[768]{0:T(1024)}, u32[]{:S(2)}) copy-start(f32[768]{0:T(1024)} %copy-done.53) | copy-start | bytes 9220
  379.4 2.5 copy-start.58
  379.4 3.8 copy-start.56
  388.8 3.8 copy-start.5
  394.3 5.0 %collective-permute-start = (bf16[2,2,96,3200]{3,2,1,0:T(8,128)(2,1)}, bf16[2,2,96,3200]{3,2,1,0:T(8,128)(2,1)}, u32[]{:S(2)}, u32[]{:S(2)}) collective-permute-start(bf16[2,2,96,3200]{3,2,1,0:T(8,128)(2,1)} %fusion.39), channel_id=1, source_target_pairs={{0,1},{1,0},{2,3},{3,2},{4,5},{5,4},{6,7},{7,6},{8,9},{9,8},{10,11... | collective-permute-start | bytes 7372808 | tf_op jit(solution)/shard_map/ppermute | solution.py:122
  402.9 2.2 copy-start.8
  406.8 15.5 %collective-permute-start.1 = (bf16[2,96,1536]{2,1,0:T(8,128)(2,1)S(1)}, bf16[2,96,1536]{2,1,0:T(8,128)(2,1)}, u32[]{:S(2)}, u32[]{:S(2)}) collective-permute-start(bf16[2,96,1536]{2,1,0:T(8,128)(2,1)S(1)} %fusion.83), channel_id=1, source_target_pairs={{0,2},{1,3},{2,0},{3,1},{4,6},{5,7},{6,4},{7,5},{8,10},{9,11},{10,... | collective-permute-start | bytes 1769480 | tf_op jit(solution)/shard_map/ppermute | solution.py:122
  408.5 13.9 %copy-start.16 = (f32[2,2,96,1536]{3,2,1,0:T(8,128)S(1)}, f32[2,2,96,1536]{3,2,1,0:T(8,128)}, u32[]{:S(2)}) copy-start(f32[2,2,96,1536]{3,2,1,0:T(8,128)} %copy-done.15) | copy-start | bytes 7077892
  410.7 17.3 %collective-permute-start.3 = (bf16[2,96,1664]{2,1,0:T(8,128)(2,1)S(1)}, bf16[2,96,1664]{2,1,0:T(8,128)(2,1)S(1)}, u32[]{:S(2)}, u32[]{:S(2)}) collective-permute-start(bf16[2,96,1664]{2,1,0:T(8,128)(2,1)S(1)} %fusion.82), channel_id=1, source_target_pairs={{0,4},{1,5},{2,6},{3,7},{4,0},{5,1},{6,2},{7,3},{8,12},{9,13},{10,... | collective-permute-start | bytes 1916936 | tf_op jit(solution)/shard_map/ppermute | solution.py:122
  423.7 9.5 %collective-permute-start.2 = (bf16[96,1536]{1,0:T(8,128)(2,1)S(1)}, bf16[96,1536]{1,0:T(8,128)(2,1)S(1)}, u32[]{:S(2)}, u32[]{:S(2)}) collective-permute-start(bf16[96,1536]{1,0:T(8,128)(2,1)S(1)} %fusion.87), channel_id=1, source_target_pairs={{0,4},{1,5},{2,6},{3,7},{4,0},{5,1},{6,2},{7,3},{8,12},{9,13},{10,... | collective-permute-start | bytes 884744 | tf_op jit(solution)/shard_map/ppermute | solution.py:122
  428.1 7.4 %collective-permute-start.4 = (bf16[96,1664]{1,0:T(8,128)(2,1)S(1)}, bf16[96,1664]{1,0:T(8,128)(2,1)S(1)}, u32[]{:S(2)}, u32[]{:S(2)}) collective-permute-start(bf16[96,1664]{1,0:T(8,128)(2,1)S(1)} %fusion.84), channel_id=1, source_target_pairs={{0,2},{1,3},{2,0},{3,1},{4,6},{5,7},{6,4},{7,5},{8,10},{9,11},{10,... | collective-permute-start | bytes 958472 | tf_op jit(solution)/shard_map/ppermute | solution.py:122
  436.8 7.0 %collective-permute-start.5 = (bf16[2,24,3200]{2,1,0:T(8,128)(2,1)S(1)}, bf16[2,24,3200]{2,1,0:T(8,128)(2,1)}, u32[]{:S(2)}, u32[]{:S(2)}) collective-permute-start(bf16[2,24,3200]{2,1,0:T(8,128)(2,1)S(1)} %fusion.85), channel_id=1, source_target_pairs={{0,8},{8,0},{16,24},{24,16},{1,9},{9,1},{17,25},{25,17},{2,10},{10... | collective-permute-start | bytes 921608 | tf_op jit(solution)/shard_map/ppermute | solution.py:122
  445.7 9.8 %collective-permute-start.6 = (bf16[24,3200]{1,0:T(8,128)(2,1)}, bf16[24,3200]{1,0:T(8,128)(2,1)S(1)}, u32[]{:S(2)}, u32[]{:S(2)}) collective-permute-start(bf16[24,3200]{1,0:T(8,128)(2,1)} %fusion.91), channel_id=1, source_target_pairs={{0,16},{8,24},{16,0},{24,8},{1,17},{9,25},{17,1},{25,9},{2,18},{10... | collective-permute-start | bytes 460808 | tf_op jit(solution)/shard_map/ppermute | solution.py:122
  455.6 6.3 %collective-permute-start.7 = (bf16[24,3200]{1,0:T(8,128)(2,1)S(1)}, bf16[24,3200]{1,0:T(8,128)(2,1)S(1)}, u32[]{:S(2)}, u32[]{:S(2)}) collective-permute-start(bf16[24,3200]{1,0:T(8,128)(2,1)S(1)} %fusion.86), channel_id=1, source_target_pairs={{0,16},{8,24},{16,0},{24,8},{1,17},{9,25},{17,1},{25,9},{2,18},{10... | collective-permute-start | bytes 460808 | tf_op jit(solution)/shard_map/ppermute | solution.py:146
  461.9 9.0 %collective-permute-start.8 = (bf16[2,24,3200]{2,1,0:T(8,128)(2,1)S(1)}, bf16[2,24,3200]{2,1,0:T(8,128)(2,1)S(1)}, u32[]{:S(2)}, u32[]{:S(2)}) collective-permute-start(bf16[2,24,3200]{2,1,0:T(8,128)(2,1)S(1)} %pad_maximum_fusion.7), channel_id=1, source_target_pairs={{0,8},{8,0},{16,24},{24,16},{1,9},{9,1},{17,25},{25,17},{2,10},{10... | collective-permute-start | bytes 921608 | tf_op jit(solution)/shard_map/ppermute | solution.py:146
  (23 other events, 31.2 us)
Sparse Core Ops, SparseCore 0:
  11.7 42.3 all-gather.2
  56.5 58.6 all-gather.4
  321.2 77.1 reduce-scatter.1

commit v15 on v12

--- a/solution.py
+++ b/solution.py
@@ -394,13 +394,15 @@
     )
     small = jnp.pad(small, ((0, 0), (0, 128 - small.shape[1])))
     dense_grads = jnp.concatenate([grad_qkv, grad_wout, small], axis=1)
-    chunk_cols = 128 * (dense_grads.shape[1] // 256)
+    n_parts = 3
+    bounds = [128 * (dense_grads.shape[1] * k // (128 * n_parts)) for k in range(n_parts)]
+    bounds = bounds + [dense_grads.shape[1]]
     dense_total = jnp.concatenate(
         [
             expert_all_reduce(
                 shard_reduce_scatter(part, "shard", 128 * (part.shape[1] // 256)), "expert"
             )
-            for part in (dense_grads[:, :chunk_cols], dense_grads[:, chunk_cols:])
+            for part in (dense_grads[:, low:high] for low, high in zip(bounds[:-1], bounds[1:]))
         ],
         axis=1,
     )

time: 475 us -> 474 us (level)
  waiting for transfers between devices: 108 us -> 87.6 us
  starting transfers between devices: 39 us -> 53.8 us
    ppermute x14 -> x21, waiting for transfers between devices: 31 us -> 13.7 us  [_exchange(): got = lax.ppermute(send.astype(jnp.bfloat16), axis_name, pairs)]
    ppermute x14 -> x21, starting transfers between devices: 15.3 us -> 28 us  [_exchange(): got = lax.ppermute(send.astype(jnp.bfloat16), axis_name, pairs)]
    ppermute x4 -> x6, waiting for transfers between devices: 11.5 us -> 8.83 us  [_gather_back(): got = lax.ppermute(values, axis_name, pairs)]
    unnamed x146 -> x156, local copies, waits for them, and re-layouts: 9.56 us -> 9.56 us
  transfers between devices with their start and end apart: 25 -> 34, of which waited for: 16 -> 15; matrix products, arithmetic and copies ran while one was open for 54% -> 55% of each run, Pallas kernels for 8% -> 8%
where the time goes in v15:
time: 474 us; the launch traced here: 466 us
  matrix products  186 us (39%)
  waiting for transfers between devices  87.6 us (18%)
  starting transfers between devices  53.8 us (11%)
  local copies, waits for them, and re-layouts  52.8 us (11%)
  Pallas kernels  35.2 us (7%)
  other arithmetic  34.1 us (7%)
  between operations  16.6 us (4%)
    dot_general x2, matrix products, shards(): jnp.dot(flat_arrived, expert_first, preferred_element_type=jnp.float32)  51.9 us
    all_gather x1, waiting for transfers between devices, shards(): dense_full = lax.all_gather(dense_local, 'shard', axis=0, tiled=True)  29.1 us
    ppermute x21, starting transfers between devices, _exchange(): got = lax.ppermute(send.astype(jnp.bfloat16), axis_name, pairs)  28 us
    all_to_all x2, waiting for transfers between devices, shards(): lax.all_to_all(dispatch_rows(experts * start, experts * (start + size)).r...  23 us
    dot_general x2, matrix products, shards(): lax.dot_general(flat_grad, expert_second, COL_CONTRACT, preferred_element...  22.6 us
    pallas_call x1, Pallas kernels, attention_bwd(): pl.pallas_call(functools.partial(attn_bwd_kernel, images=images), grid=(p...  21.8 us
    dot_general x2, matrix products, shards(): lax.dot_general(activated, flat_grad, ROW_CONTRACT, preferred_element_typ...  20.4 us
    ppermute x21, waiting for transfers between devices, _exchange(): got = lax.ppermute(send.astype(jnp.bfloat16), axis_name, pairs)  13.7 us
  transfers between devices with their start and end apart: 34, of which 15 were waited for; matrix products, arithmetic and copies ran while one was open for 55% of the time, Pallas kernels for 8%

profile of v15, /device:TPU:0, one launch (start us, length us, event | category | flops | bytes accessed | tf_op | source)
XLA Modules:
  0.0 465.6 jit_solution(3813673979936009906)
XLA Ops:
  9.6 1.9 concatenate.55
  13.2 2.3 pad_maximum_fusion.6
  21.6 3.3 fusion.123
  24.9 29.1 %all-gather.3.cloned.1.call-done = bf16[768,3078]{1,0:T(8,128)(2,1)} async-done(((bf16[96,3078]{1,0:T(8,128)(2,1)}), bf16[768,3078]{1,0:T(8,128)(2,1)}) %all-gather.3.cloned.1.call-update) | async-done | bytes 4727824 | tf_op jit(solution)/shard_map/all_gather | solution.py:217
  55.8 4.6 convolution_convert_fusion
  60.6 13.4 %shard_map.178 = bf16[640,768]{1,0:T(8,128)(2,1)S(1)} custom-call(bf16[640,2304]{1,0:T(8,128)(2,1)S(1)} %pad.18.q_ref.k_ref.v_ref, bf16[640,2304]{1,0:T(8,128)(2,1)S(1)} %pad.18.q_ref.k_ref.v_ref, bf16[640,2304]{1,0:T(8,128)(2,1)S(1)} %pad.18.q_ref.k_ref.v_ref), custom_call_target="tpu_custom_call" | custom-call | tf_op jit(solution)/shard_map/pallas_call | solution.py:90
  74.1 2.6 fusion.132
  80.7 2.7 fusion.60
  83.4 2.3 convolution_convert_fusion.4
  85.7 2.4 add_convert_fusion.3
  89.6 4.6 all-to-all-start.2
  94.8 3.0 fusion.53
  102.4 12.9 %all-gather.5.cloned.1.call-done = bf16[2,768,3072]{2,1,0:T(8,128)(2,1)} async-done(((bf16[2,96,3072]{2,1,0:T(8,128)(2,1)}), bf16[2,768,3072]{2,1,0:T(8,128)(2,1)}) %all-gather.5.cloned.1.call-update) | async-done | bytes 9437200 | tf_op jit(solution)/shard_map/all_gather | solution.py:228
  115.3 4.9 %slice.223 = bf16[1,768,3072]{2,1,0:T(8,128)(2,1)} slice(bf16[2,768,3072]{2,1,0:T(8,128)(2,1)} %all-gather.5.cloned.1.call-done), slice={[1:2], [0:768], [0:3072]} | slice | bytes 9437184 | tf_op jit(solution)/shard_map/slice | solution.py:230
  120.1 8.5 %reshape_squeeze.3 = bf16[3072,768]{1,0:T(8,128)(2,1)} reshape(bf16[1,768,3072]{2,1,0:T(8,128)(2,1)} %slice.223) | data formatting | bytes 9437184 | tf_op jit(solution)/shard_map/reshape;squeeze | solution.py:230
  128.6 17.7 %all-to-all-done.2 = bf16[4,184,1536]{2,1,0:T(8,128)(2,1)S(1)} async-done(((bf16[4,184,1536]{2,1,0:T(8,128)(2,1)}), bf16[4,184,1536]{2,1,0:T(8,128)(2,1)S(1)}, u32[]{:S(2)}, u32[]{:S(2)}) %all-to-all-start.2) | async-done | bytes 2261024 | tf_op jit(solution)/shard_map/all_to_all | solution.py:286
  147.7 3.8 all-to-all-start
  151.5 25.7 %multiply_convert_fusion.1 = (bf16[736,3072]{1,0:T(8,128)(2,1)S(1)}, f32[736,3072]{1,0:T(8,128)}, f32[736,3072]{1,0:T(8,128)}) fusion(bf16[2,768,3072]{2,1,0:T(8,128)(2,1)} %all-gather.5.cloned.1.call-done, bf16[736,1536]{1,0:T(8,128)(2,1)} %bitcast.231), kind=kOutput, calls=%fused_computation.36 | convolution fusion | flops 3619848192 | bytes 28459008 | tf_op jit(solution)/shard_map/dot_general | solution.py:300
  177.2 3.7 convolution_convert_fusion.3
  180.9 10.8 %fusion.19 = bf16[736,3072]{1,0:T(8,128)(2,1)} fusion(f32[736,3072]{1,0:T(8,128)} %get-tuple-element.120, f32[736,3072]{1,0:T(8,128)} %get-tuple-element.88, bf16[3072,768]{1,0:T(8,128)(2,1)S(1)} %copy-done.20, bf16[736,1536]{1,0:T(8,128)(2,1)} %bitcast.232), kind=kOutput, calls=%fused_computation.35 | convolution fusion | flops 3490971648 | bytes 28459008 | tf_op jit(solution)/shard_map/dot_general | solution.py:297
  191.8 6.1 %fusion.49 = bf16[736,768]{1,0:T(8,128)(2,1)S(1)} fusion(bf16[736,3072]{1,0:T(8,128)(2,1)} %fusion.19, bf16[2,768,3072]{2,1,0:T(8,128)(2,1)S(1)} %bitcast.230), kind=kOutput, calls=%fused_computation.114 | convolution fusion | flops 3473448960 | bytes 10371072 | tf_op jit(solution)/shard_map/dot_general | solution.py:307
  199.5 5.3 %all-to-all-done = bf16[4,192,1536]{2,1,0:T(8,128)(2,1)S(1)} async-done(((bf16[4,192,1536]{2,1,0:T(8,128)(2,1)}), bf16[4,192,1536]{2,1,0:T(8,128)(2,1)S(1)}, u32[]{:S(2)}, u32[]{:S(2)}) %all-to-all-start) | async-done | bytes 2359328 | tf_op jit(solution)/shard_map/all_to_all | solution.py:286
  204.8 4.9 %all-to-all-start.3 = ((bf16[4,184,1536]{2,1,0:T(8,128)(2,1)}), bf16[4,184,1536]{2,1,0:T(8,128)(2,1)}, u32[]{:S(2)}, u32[]{:S(2)}) async-start(bf16[4,184,1536]{2,1,0:T(8,128)(2,1)} %bitcast.15), calls=%async_computation.3 | async-start | bytes 4521984 | tf_op jit(solution)/shard_map/all_to_all | solution.py:322
  209.7 26.2 %multiply_convert_fusion = (bf16[768,3072]{1,0:T(8,128)(2,1)S(1)}, f32[768,3072]{1,0:T(8,128)}, f32[768,3072]{1,0:T(8,128)}) fusion(bf16[2,768,3072]{2,1,0:T(8,128)(2,1)} %all-gather.5.cloned.1.call-done, bf16[768,1536]{1,0:T(8,128)(2,1)S(1)} %bitcast.221), kind=kOutput, calls=%fused_computation.14 | convolution fusion | flops 3777232896 | bytes 29491200 | tf_op jit(solution)/shard_map/dot_general | solution.py:300
  235.9 11.8 %fusion.6 = bf16[768,3072]{1,0:T(8,128)(2,1)S(1)} fusion(f32[768,3072]{1,0:T(8,128)} %get-tuple-element.121, f32[768,3072]{1,0:T(8,128)} %get-tuple-element.86, bf16[3072,768]{1,0:T(8,128)(2,1)} %reshape_squeeze.3, bf16[768,1536]{1,0:T(8,128)(2,1)S(1)} %bitcast.222), kind=kOutput, calls=%fused_computation.10 | convolution fusion | flops 3642753024 | bytes 29491200 | tf_op jit(solution)/shard_map/dot_general | solution.py:297
  247.7 8.1 %convolution_convert_fusion.1 = bf16[768,768]{0,1:T(8,128)(2,1)S(1)} fusion(bf16[768,3072]{1,0:T(8,128)(2,1)S(1)} %get-tuple-element.85, bf16[3072,768]{1,0:T(8,128)(2,1)} %reshape_squeeze.3), kind=kOutput, calls=%fused_computation.112 | convolution fusion | flops 3624468480 | bytes 10616832 | tf_op jit(solution)/shard_map/dot_general | solution.py:304
  255.8 6.3 %fusion.48 = bf16[768,768]{0,1:T(8,128)(2,1)S(1)} fusion(bf16[768,3072]{1,0:T(8,128)(2,1)S(1)} %fusion.6, bf16[2,768,3072]{2,1,0:T(8,128)(2,1)} %all-gather.5.cloned.1.call-done), kind=kOutput, calls=%fused_computation.111 | convolution fusion | flops 3624468480 | bytes 10616832 | tf_op jit(solution)/shard_map/dot_general | solution.py:307
  262.2 2.5 copy.130
  264.7 10.3 %fusion.63 = f32[3072,768]{1,0:T(8,128)} fusion(bf16[768,3072]{1,0:T(8,128)(2,1)} %copy-done.66, bf16[768,1536]{1,0:T(8,128)(2,1)} %bitcast.223), kind=kOutput, calls=%fused_computation.132 | convolution fusion | flops 3623878656 | bytes 15335424 | tf_op jit(solution)/shard_map/dot_general | solution.py:310
  275.0 5.2 %all-to-all-start.1 = ((bf16[4,192,1536]{2,1,0:T(8,128)(2,1)}), bf16[4,192,1536]{2,1,0:T(8,128)(2,1)}, u32[]{:S(2)}, u32[]{:S(2)}) async-start(bf16[4,192,1536]{2,1,0:T(8,128)(2,1)} %bitcast.10), calls=%async_computation.1 | async-start | bytes 4718592 | tf_op jit(solution)/shard_map/all_to_all | solution.py:322
  280.2 10.2 %add_convert_fusion = bf16[3072,768]{1,0:T(8,128)(2,1)} fusion(f32[3072,768]{1,0:T(8,128)} %fusion.63, bf16[736,3072]{1,0:T(8,128)(2,1)} %copy-done.67, bf16[736,1536]{1,0:T(8,128)(2,1)S(1)} %bitcast.233), kind=kOutput, calls=%fused_computation.12 | convolution fusion | flops 3477602304 | bytes 19808256 | tf_op jit(solution)/shard_map/dot_general | solution.py:310
  290.4 8.6 %stack_reshape.4 = bf16[1,768,3072]{2,1,0:T(8,128)(2,1)} reshape(bf16[3072,768]{1,0:T(8,128)(2,1)} %add_convert_fusion) | data formatting | bytes 9437184 | tf_op jit(solution)/shard_map/stack;reshape | solution.py:325
  299.0 5.9 %fusion.66 = f32[768,3072]{1,0:T(8,128)S(1)} fusion(bf16[768,3072]{1,0:T(8,128)(2,1)} %copy-done.21, bf16[768,1536]{1,0:T(8,128)(2,1)S(1)} %bitcast.224), kind=kOutput, calls=%fused_computation.135 | convolution fusion | flops 3623878656 | bytes 15335424 | tf_op jit(solution)/shard_map/dot_general | solution.py:313
  304.9 7.8 %fusion.26 = bf16[1,768,3072]{2,1,0:T(8,128)(2,1)} fusion(f32[768,3072]{1,0:T(8,128)S(1)} %fusion.66, bf16[736,3072]{1,0:T(8,128)(2,1)} %fusion.19, bf16[736,1536]{1,0:T(8,128)(2,1)S(1)} %bitcast.234), kind=kOutput, calls=%fused_computation.53 | convolution fusion | flops 3477602304 | bytes 19808256 | tf_op jit(solution)/shard_map/dot_general | solution.py:313
  312.8 8.3 %pad_maximum_fusion = bf16[2,768,3072]{2,1,0:T(8,128)(2,1)} fusion(bf16[1,768,3072]{2,1,0:T(8,128)(2,1)} %stack_reshape.4, bf16[1,768,3072]{2,1,0:T(8,128)(2,1)} %fusion.26), kind=kLoop, calls=%fused_computation.11 | loop fusion | flops 4718592 | bytes 18874368 | tf_op jit(solution)/shard_map/stack | solution.py:325
  322.3 5.5 %fusion.58 = f32[591,1536]{1,0:T(8,128)} fusion(bf16[736,1536]{1,0:T(8,128)(2,1)} %bitcast.16, pred[1504,591]{1,0:T(32,128)(4,1)S(1)} %copy-done.34), kind=kOutput, calls=%fused_computation.126 | convolution fusion | flops 1336246272 | bytes 6363136 | tf_op jit(solution)/shard_map/dot_general | solution.py:338
  327.8 5.4 %fusion.55 = f32[591,1536]{1,0:T(8,128)} fusion(bf16[736,1536]{1,0:T(8,128)(2,1)} %bitcast.16, pred[1504,591]{1,0:T(32,128)(4,1)S(1)} %copy-done.33), kind=kOutput, calls=%fused_computation.123 | convolution fusion | flops 1336246272 | bytes 6363136 | tf_op jit(solution)/shard_map/dot_general | solution.py:341
  333.2 6.0 %convolution_add_fusion.1 = f32[591,1536]{1,0:T(8,128)S(1)} fusion(f32[591,1536]{1,0:T(8,128)} %fusion.58, bf16[768,1536]{1,0:T(8,128)(2,1)} %bitcast.11, pred[1504,591]{1,0:T(32,128)(4,1)S(1)} %copy-done.34), kind=kOutput, calls=%fused_computation.60 | convolution fusion | flops 1395251712 | bytes 10113024 | tf_op jit(solution)/shard_map/dot_general | solution.py:338
  339.3 3.7 convolution_add_fusion
  343.1 1.8 multiply_reduce_fusion.3
  348.9 21.8 %shard_map.179 = (bf16[640,768]{1,0:T(8,128)(2,1)S(1)}, bf16[640,768]{1,0:T(8,128)(2,1)S(1)}, bf16[640,768]{1,0:T(8,128)(2,1)S(1)}) custom-call(bf16[640,2304]{1,0:T(8,128)(2,1)} %copy-done, bf16[640,2304]{1,0:T(8,128)(2,1)} %copy-done, bf16[640,2304]{1,0:T(8,128)(2,1)} %copy-done, bf16[640,768]{1,0:T(8,128)(2,1)S(1)} %pad.20.g_ref), custom_call_target="tpu_custom_call" | custom-call | tf_op jit(solution)/shard_map/pallas_call | solution.py:106
  371.9 4.9 %fusion.76 = f32[768,2304]{1,0:T(8,128)} fusion(bf16[640,2304]{1,0:T(8,128)(2,1)S(1)} %constant_dynamic-update-slice_fusion, bf16[591,768]{1,0:T(8,128)(2,1)S(1)} %copy-done.23), kind=kOutput, calls=%fused_computation.146 | convolution fusion | flops 2264924160 | bytes 10934784 | tf_op jit(solution)/shard_map/dot_general | solution.py:382
  376.9 2.4 fusion.45
  380.8 4.6 fusion.128
  389.5 2.0 add_convert_fusion.4
  392.1 1.8 collective-permute-start.12
  397.4 1.8 collective-permute-start.21
  399.2 1.9 collective-permute-done.12
  403.4 1.9 collective-permute-done.3
  406.0 1.6 collective-permute-start.4
  407.7 2.5 collective-permute-done.19
  413.4 1.7 collective-permute-start.14
  419.1 2.4 collective-permute-start.15
  421.6 1.7 collective-permute-start.6
  423.3 1.8 collective-permute-done.15
  426.7 1.7 collective-permute-start.7
  428.5 3.2 collective-permute-start.23
  431.9 2.0 collective-permute-start.8
  434.7 3.0 collective-permute-start.24
  438.1 3.0 collective-permute-done.24
  441.1 1.8 collective-permute-start.25
  442.9 3.8 collective-permute-done.25
  447.0 4.6 collective-permute-done.26
  454.8 2.5 fusion.131
  (349 shorter events, 58.3 us)
Async XLA Ops:
  7.2 46.9 %all-gather.3.cloned.1.call-start = ((), (), s32[]{:S(2)}) async-start(), calls=%async_computation.5 | async-start | bytes 5529600 | tf_op jit(solution)/shard_map/all_gather | solution.py:217
  8.8 7.7 %copy-start.47 = (s32[591,2]{0,1:T(2,128)S(1)}, s32[591,2]{0,1:T(2,128)}, u32[]{:S(2)}) copy-start(s32[591,2]{0,1:T(2,128)} %param.13) | copy-start | bytes 14188
  11.6 7.9 %copy-start.5 = (bf16[591,768]{1,0:T(8,128)(2,1)S(1)}, bf16[591,768]{1,0:T(8,128)(2,1)}, u32[]{:S(2)}) copy-start(bf16[591,768]{1,0:T(8,128)(2,1)} %param.11) | copy-start | bytes 2723332
  11.6 103.7 %all-gather.5.cloned.1.call-start = ((), (), s32[]{:S(2)}) async-start(), calls=%async_computation.6 | async-start | bytes 10616832 | tf_op jit(solution)/shard_map/all_gather | solution.py:228
  13.2 6.9 %copy-start.10 = (bf16[591,768]{1,0:T(8,128)(2,1)S(1)}, bf16[591,768]{1,0:T(8,128)(2,1)}, u32[]{:S(2)}) copy-start(bf16[591,768]{1,0:T(8,128)(2,1)} %param.21) | copy-start | bytes 2723332
  19.4 60.5 %copy-start.37 = (f32[591]{0:T(1024)}, f32[591]{0:T(1024)S(1)}, u32[]{:S(2)}) copy-start(f32[591]{0:T(1024)S(1)} %fusion.120) | copy-start | bytes 7096
  19.6 35.8 %copy-start.45 = (f32[591]{0:T(1024)}, f32[591]{0:T(1024)S(1)}, u32[]{:S(2)}) copy-start(f32[591]{0:T(1024)S(1)} %broadcast_multiply_fusion.2) | copy-start | bytes 7096
  20.1 35.3 %copy-start.57 = (f32[591]{0:T(1024)}, f32[591]{0:T(1024)S(1)}, u32[]{:S(2)}) copy-start(f32[591]{0:T(1024)S(1)} %fusion.118) | copy-start | bytes 7096
  24.9 58.4 %copy-start.27 = (bf16[1504,591]{1,0:T(8,128)(2,1)}, bf16[1504,591]{1,0:T(8,128)(2,1)S(1)}, u32[]{:S(2)}) copy-start(bf16[1504,591]{1,0:T(8,128)(2,1)S(1)} %get-tuple-element.110) | copy-start | bytes 5333188
  55.4 5.0 %copy-start.55 = (f32[768]{0:T(1024)}, f32[768]{0:T(1024)S(1)}, u32[]{:S(2)}) copy-start(f32[768]{0:T(1024)S(1)} %get-tuple-element.70) | copy-start | bytes 9220
  55.4 22.3 %copy-start.49 = (f32[768]{0:T(1024)}, f32[768]{0:T(1024)S(1)}, u32[]{:S(2)}) copy-start(f32[768]{0:T(1024)S(1)} %get-tuple-element.69) | copy-start | bytes 9220
  60.6 13.4 %copy-start = (bf16[640,2304]{1,0:T(8,128)(2,1)}, bf16[640,2304]{1,0:T(8,128)(2,1)S(1)}, u32[]{:S(2)}) copy-start(bf16[640,2304]{1,0:T(8,128)(2,1)S(1)} %pad.18.q_ref.k_ref.v_ref) | copy-start | bytes 8847364
  78.2 19.6 %copy-start.13 = (bf16[591,768]{1,0:T(8,128)(2,1)}, bf16[591,768]{1,0:T(8,128)(2,1)S(1)}, u32[]{:S(2)}) copy-start(bf16[591,768]{1,0:T(8,128)(2,1)S(1)} %multiply_convert_fusion.4) | copy-start | bytes 2723332
  80.7 5.0 %copy-start.30 = (bf16[591,2,768]{2,0,1:T(8,128)(2,1)}, bf16[591,2,768]{2,0,1:T(8,128)(2,1)S(1)}, u32[]{:S(2)}) copy-start(bf16[591,2,768]{2,0,1:T(8,128)(2,1)S(1)} %multiply_convert_fusion.2) | copy-start | bytes 5446660
  89.6 56.7 %all-to-all-start.2 = ((bf16[4,184,1536]{2,1,0:T(8,128)(2,1)}), bf16[4,184,1536]{2,1,0:T(8,128)(2,1)S(1)}, u32[]{:S(2)}, u32[]{:S(2)}) async-start(bf16[4,184,1536]{2,1,0:T(8,128)(2,1)} %pad_maximum_fusion.4), calls=%async_computation.2 | async-start | bytes 4521984 | tf_op jit(solution)/shard_map/all_to_all | solution.py:286
  147.7 57.2 %all-to-all-start = ((bf16[4,192,1536]{2,1,0:T(8,128)(2,1)}), bf16[4,192,1536]{2,1,0:T(8,128)(2,1)S(1)}, u32[]{:S(2)}, u32[]{:S(2)}) async-start(bf16[4,192,1536]{2,1,0:T(8,128)(2,1)} %pad_maximum_fusion.2), calls=%async_computation | async-start | bytes 4718592 | tf_op jit(solution)/shard_map/all_to_all | solution.py:286
  151.5 25.8 %copy-start.20 = (bf16[3072,768]{1,0:T(8,128)(2,1)S(1)}, bf16[3072,768]{1,0:T(8,128)(2,1)}, u32[]{:S(2)}) copy-start(bf16[3072,768]{1,0:T(8,128)(2,1)} %reshape_squeeze.3) | copy-start | bytes 14155780
  177.2 14.6 %slice-start.2 = ((s8[9437184]{0:T(1024)(128)(4,1)}), s8[4194304]{0:T(1024)(128)(4,1)S(1)}, s32[]{:S(2)}) async-start(s8[9437184]{0:T(1024)(128)(4,1)} %bitcast.229), calls=%async_computation.10 | async-start | bytes 8388608
  177.2 14.5 %slice-start.3 = ((s8[9437184]{0:T(1024)(128)(4,1)}), s8[4194304]{0:T(1024)(128)(4,1)S(1)}, s32[]{:S(2)}) async-start(s8[9437184]{0:T(1024)(128)(4,1)} %bitcast.229), calls=%async_computation.11 | async-start | bytes 8388608
  180.9 10.9 %slice-start.4 = ((s8[9437184]{0:T(1024)(128)(4,1)}), s8[1048576]{0:T(1024)(128)(4,1)S(1)}, s32[]{:S(2)}) async-start(s8[9437184]{0:T(1024)(128)(4,1)} %bitcast.229), calls=%async_computation.12 | async-start | bytes 2097152
  204.8 31.1 %copy-start.18 = (bf16[4,192,1536]{2,1,0:T(8,128)(2,1)}, bf16[4,192,1536]{2,1,0:T(8,128)(2,1)S(1)}, u32[]{:S(2)}) copy-start(bf16[4,192,1536]{2,1,0:T(8,128)(2,1)S(1)} %all-to-all-done) | copy-start | bytes 7077892
  204.8 70.2 %all-to-all-start.3 = ((bf16[4,184,1536]{2,1,0:T(8,128)(2,1)}), bf16[4,184,1536]{2,1,0:T(8,128)(2,1)}, u32[]{:S(2)}, u32[]{:S(2)}) async-start(bf16[4,184,1536]{2,1,0:T(8,128)(2,1)} %bitcast.15), calls=%async_computation.3 | async-start | bytes 4521984 | tf_op jit(solution)/shard_map/all_to_all | solution.py:322
  235.9 11.8 %copy-start.66 = (bf16[768,3072]{1,0:T(8,128)(2,1)}, bf16[768,3072]{1,0:T(8,128)(2,1)S(1)}, u32[]{:S(2)}) copy-start(bf16[768,3072]{1,0:T(8,128)(2,1)S(1)} %get-tuple-element.85) | copy-start | bytes 14155780
  247.6 8.2 %copy-start.21 = (bf16[768,3072]{1,0:T(8,128)(2,1)}, bf16[768,3072]{1,0:T(8,128)(2,1)S(1)}, u32[]{:S(2)}) copy-start(bf16[768,3072]{1,0:T(8,128)(2,1)S(1)} %fusion.6) | copy-start | bytes 14155780
  275.0 5.2 %copy-start.25 = (bf16[4,184,1536]{2,1,0:T(8,128)(2,1)S(1)}, bf16[4,184,1536]{2,1,0:T(8,128)(2,1)}, u32[]{:S(2)}) copy-start(bf16[4,184,1536]{2,1,0:T(8,128)(2,1)} %copy-done.24) | copy-start | bytes 6782980
  275.0 58.2 %all-to-all-start.1 = ((bf16[4,192,1536]{2,1,0:T(8,128)(2,1)}), bf16[4,192,1536]{2,1,0:T(8,128)(2,1)}, u32[]{:S(2)}, u32[]{:S(2)}) async-start(bf16[4,192,1536]{2,1,0:T(8,128)(2,1)} %bitcast.10), calls=%async_computation.1 | async-start | bytes 4718592 | tf_op jit(solution)/shard_map/all_to_all | solution.py:322
  280.2 174.6 %reduce-scatter.2.cloned.1.call-start = ((), (), s32[]{:S(2)}) async-start(), calls=%async_computation.7 | async-start | bytes 10616832 | tf_op jit(solution)/shard_map/reduce_scatter | solution.py:328
  290.4 8.6 %copy-start.19 = (bf16[4,192,1536]{2,1,0:T(8,128)(2,1)S(1)}, bf16[4,192,1536]{2,1,0:T(8,128)(2,1)}, u32[]{:S(2)}) copy-start(bf16[4,192,1536]{2,1,0:T(8,128)(2,1)} %copy-done.18) | copy-start | bytes 7077892
  299.0 5.9 %copy-start.26 = (bf16[4,184,1536]{2,1,0:T(8,128)(2,1)S(1)}, bf16[4,184,1536]{2,1,0:T(8,128)(2,1)}, u32[]{:S(2)}) copy-start(bf16[4,184,1536]{2,1,0:T(8,128)(2,1)} %copy-done.24) | copy-start | bytes 6782980
  322.3 5.5 %copy-start.33 = (pred[1504,591]{1,0:T(32,128)(4,1)S(1)}, pred[1504,591]{1,0:T(32,128)(4,1)}, u32[]{:S(2)}) copy-start(pred[1504,591]{1,0:T(32,128)(4,1)} %get-tuple-element.114) | copy-start | bytes 2666596
  333.2 6.0 %copy-start.65 = (f32[591,1536]{1,0:T(8,128)S(1)}, f32[591,1536]{1,0:T(8,128)}, u32[]{:S(2)}) copy-start(f32[591,1536]{1,0:T(8,128)} %fusion.55) | copy-start | bytes 10893316
  333.2 12.2 %slice-start.5 = ((s8[4915200]{0:T(1024)(128)(4,1)}), s8[4194304]{0:T(1024)(128)(4,1)S(1)}, s32[]{:S(2)}) async-start(s8[4915200]{0:T(1024)(128)(4,1)} %bitcast.247), calls=%async_computation.13 | async-start | bytes 8388608
  339.3 6.1 %slice-start.6 = ((s8[4915200]{0:T(1024)(128)(4,1)}), s8[720896]{0:T(1024)(128)(4,1)S(1)}, s32[]{:S(2)}) async-start(s8[4915200]{0:T(1024)(128)(4,1)} %bitcast.247), calls=%async_computation.14 | async-start | bytes 1441792
  371.9 4.9 %copy-start.46 = (f32[591]{0:T(1024)S(1)}, f32[591]{0:T(1024)}, u32[]{:S(2)}) copy-start(f32[591]{0:T(1024)} %copy-done.45) | copy-start | bytes 7096
  371.9 4.9 %copy-start.56 = (f32[768]{0:T(1024)S(1)}, f32[768]{0:T(1024)}, u32[]{:S(2)}) copy-start(f32[768]{0:T(1024)} %copy-done.55) | copy-start | bytes 9220
  380.6 6.2 %slice-start = ((s8[7077888]{0:T(1024)(128)(4,1)}), s8[2883584]{0:T(1024)(128)(4,1)S(1)}, s32[]{:S(2)}) async-start(s8[7077888]{0:T(1024)(128)(4,1)} %bitcast.213), calls=%async_computation.8 | async-start | bytes 5767168
  380.8 6.0 %slice-start.1 = ((s8[7077888]{0:T(1024)(128)(4,1)}), s8[4194304]{0:T(1024)(128)(4,1)S(1)}, s32[]{:S(2)}) async-start(s8[7077888]{0:T(1024)(128)(4,1)} %bitcast.213), calls=%async_computation.9 | async-start | bytes 8388608
  385.5 6.0 %collective-permute-start.9 = (bf16[2,2,96,1024]{3,2,1,0:T(8,128)(2,1)S(1)}, bf16[2,2,96,1024]{3,2,1,0:T(8,128)(2,1)S(1)}, u32[]{:S(2)}, u32[]{:S(2)}) collective-permute-start(bf16[2,2,96,1024]{3,2,1,0:T(8,128)(2,1)S(1)} %fusion.83), channel_id=1, source_target_pairs={{0,1},{1,0},{2,3},{3,2},{4,5},{5,4},{6,7},{7,6},{8,9},{9,8},{10,11... | collective-permute-start | bytes 2359304 | tf_op jit(solution)/shard_map/ppermute | solution.py:122
  387.2 9.8 %collective-permute-start.18 = (bf16[2,2,96,1152]{3,2,1,0:T(8,128)(2,1)S(1)}, bf16[2,2,96,1152]{3,2,1,0:T(8,128)(2,1)S(1)}, u32[]{:S(2)}, u32[]{:S(2)}) collective-permute-start(bf16[2,2,96,1152]{3,2,1,0:T(8,128)(2,1)S(1)} %fusion.79), channel_id=1, source_target_pairs={{0,1},{1,0},{2,3},{3,2},{4,5},{5,4},{6,7},{7,6},{8,9},{9,8},{10,11... | collective-permute-start | bytes 2654216 | tf_op jit(solution)/shard_map/ppermute | solution.py:122
  387.8 7.5 %collective-permute-start = (bf16[2,2,96,1024]{3,2,1,0:T(8,128)(2,1)S(1)}, bf16[2,2,96,1024]{3,2,1,0:T(8,128)(2,1)S(1)}, u32[]{:S(2)}, u32[]{:S(2)}) collective-permute-start(bf16[2,2,96,1024]{3,2,1,0:T(8,128)(2,1)S(1)} %fusion.84), channel_id=1, source_target_pairs={{0,1},{1,0},{2,3},{3,2},{4,5},{5,4},{6,7},{7,6},{8,9},{9,8},{10,11... | collective-permute-start | bytes 2359304 | tf_op jit(solution)/shard_map/ppermute | solution.py:122
  392.1 9.0 %collective-permute-start.12 = (bf16[2,96,512]{2,1,0:T(8,128)(2,1)S(1)}, bf16[2,96,512]{2,1,0:T(8,128)(2,1)S(1)}, u32[]{:S(2)}, u32[]{:S(2)}) collective-permute-start(bf16[2,96,512]{2,1,0:T(8,128)(2,1)S(1)} %fusion.89), channel_id=1, source_target_pairs={{0,4},{1,5},{2,6},{3,7},{4,0},{5,1},{6,2},{7,3},{8,12},{9,13},{10,... | collective-permute-start | bytes 589832 | tf_op jit(solution)/shard_map/ppermute | solution.py:122
  393.9 8.8 %collective-permute-start.10 = (bf16[2,96,512]{2,1,0:T(8,128)(2,1)S(1)}, bf16[2,96,512]{2,1,0:T(8,128)(2,1)S(1)}, u32[]{:S(2)}, u32[]{:S(2)}) collective-permute-start(bf16[2,96,512]{2,1,0:T(8,128)(2,1)S(1)} %fusion.88), channel_id=1, source_target_pairs={{0,2},{1,3},{2,0},{3,1},{4,6},{5,7},{6,4},{7,5},{8,10},{9,11},{10,... | collective-permute-start | bytes 589832 | tf_op jit(solution)/shard_map/ppermute | solution.py:122
  395.8 9.5 %collective-permute-start.3 = (bf16[2,96,512]{2,1,0:T(8,128)(2,1)S(1)}, bf16[2,96,512]{2,1,0:T(8,128)(2,1)S(1)}, u32[]{:S(2)}, u32[]{:S(2)}) collective-permute-start(bf16[2,96,512]{2,1,0:T(8,128)(2,1)S(1)} %fusion.87), channel_id=1, source_target_pairs={{0,4},{1,5},{2,6},{3,7},{4,0},{5,1},{6,2},{7,3},{8,12},{9,13},{10,... | collective-permute-start | bytes 589832 | tf_op jit(solution)/shard_map/ppermute | solution.py:122
  396.8 9.2 %collective-permute-start.1 = (bf16[2,96,512]{2,1,0:T(8,128)(2,1)S(1)}, bf16[2,96,512]{2,1,0:T(8,128)(2,1)S(1)}, u32[]{:S(2)}, u32[]{:S(2)}) collective-permute-start(bf16[2,96,512]{2,1,0:T(8,128)(2,1)S(1)} %fusion.86), channel_id=1, source_target_pairs={{0,2},{1,3},{2,0},{3,1},{4,6},{5,7},{6,4},{7,5},{8,10},{9,11},{10,... | collective-permute-start | bytes 589832 | tf_op jit(solution)/shard_map/ppermute | solution.py:122
  397.4 20.0 %collective-permute-start.21 = (bf16[2,96,640]{2,1,0:T(8,128)(2,1)S(1)}, bf16[2,96,640]{2,1,0:T(8,128)(2,1)S(1)}, u32[]{:S(2)}, u32[]{:S(2)}) collective-permute-start(bf16[2,96,640]{2,1,0:T(8,128)(2,1)S(1)} %fusion.85), channel_id=1, source_target_pairs={{0,4},{1,5},{2,6},{3,7},{4,0},{5,1},{6,2},{7,3},{8,12},{9,13},{10,... | collective-permute-start | bytes 737288 | tf_op jit(solution)/shard_map/ppermute | solution.py:122
  401.1 9.1 %collective-permute-start.19 = (bf16[2,96,512]{2,1,0:T(8,128)(2,1)S(1)}, bf16[2,96,512]{2,1,0:T(8,128)(2,1)S(1)}, u32[]{:S(2)}, u32[]{:S(2)}) collective-permute-start(bf16[2,96,512]{2,1,0:T(8,128)(2,1)S(1)} %fusion.90), channel_id=1, source_target_pairs={{0,2},{1,3},{2,0},{3,1},{4,6},{5,7},{6,4},{7,5},{8,10},{9,11},{10,... | collective-permute-start | bytes 589832 | tf_op jit(solution)/shard_map/ppermute | solution.py:122
  402.7 9.6 %collective-permute-start.13 = (bf16[96,512]{1,0:T(8,128)(2,1)S(1)}, bf16[96,512]{1,0:T(8,128)(2,1)S(1)}, u32[]{:S(2)}, u32[]{:S(2)}) collective-permute-start(bf16[96,512]{1,0:T(8,128)(2,1)S(1)} %fusion.101), channel_id=1, source_target_pairs={{0,2},{1,3},{2,0},{3,1},{4,6},{5,7},{6,4},{7,5},{8,10},{9,11},{10,... | collective-permute-start | bytes 294920 | tf_op jit(solution)/shard_map/ppermute | solution.py:122
  405.3 7.9 %collective-permute-start.11 = (bf16[96,512]{1,0:T(8,128)(2,1)S(1)}, bf16[96,512]{1,0:T(8,128)(2,1)S(1)}, u32[]{:S(2)}, u32[]{:S(2)}) collective-permute-start(bf16[96,512]{1,0:T(8,128)(2,1)S(1)} %fusion.100), channel_id=1, source_target_pairs={{0,4},{1,5},{2,6},{3,7},{4,0},{5,1},{6,2},{7,3},{8,12},{9,13},{10,... | collective-permute-start | bytes 294920 | tf_op jit(solution)/shard_map/ppermute | solution.py:122
  406.0 9.0 %collective-permute-start.4 = (bf16[96,512]{1,0:T(8,128)(2,1)S(1)}, bf16[96,512]{1,0:T(8,128)(2,1)S(1)}, u32[]{:S(2)}, u32[]{:S(2)}) collective-permute-start(bf16[96,512]{1,0:T(8,128)(2,1)S(1)} %fusion.98), channel_id=1, source_target_pairs={{0,2},{1,3},{2,0},{3,1},{4,6},{5,7},{6,4},{7,5},{8,10},{9,11},{10,... | collective-permute-start | bytes 294920 | tf_op jit(solution)/shard_map/ppermute | solution.py:122
  410.2 5.6 %collective-permute-start.2 = (bf16[96,512]{1,0:T(8,128)(2,1)S(1)}, bf16[96,512]{1,0:T(8,128)(2,1)S(1)}, u32[]{:S(2)}, u32[]{:S(2)}) collective-permute-start(bf16[96,512]{1,0:T(8,128)(2,1)S(1)} %fusion.97), channel_id=1, source_target_pairs={{0,4},{1,5},{2,6},{3,7},{4,0},{5,1},{6,2},{7,3},{8,12},{9,13},{10,... | collective-permute-start | bytes 294920 | tf_op jit(solution)/shard_map/ppermute | solution.py:122
  412.3 6.7 %collective-permute-start.20 = (bf16[96,512]{1,0:T(8,128)(2,1)S(1)}, bf16[96,512]{1,0:T(8,128)(2,1)S(1)}, u32[]{:S(2)}, u32[]{:S(2)}) collective-permute-start(bf16[96,512]{1,0:T(8,128)(2,1)S(1)} %fusion.102), channel_id=1, source_target_pairs={{0,4},{1,5},{2,6},{3,7},{4,0},{5,1},{6,2},{7,3},{8,12},{9,13},{10,... | collective-permute-start | bytes 294920 | tf_op jit(solution)/shard_map/ppermute | solution.py:122
  413.4 5.7 %collective-permute-start.14 = (bf16[2,24,1024]{2,1,0:T(8,128)(2,1)S(1)}, bf16[2,24,1024]{2,1,0:T(8,128)(2,1)S(1)}, u32[]{:S(2)}, u32[]{:S(2)}) collective-permute-start(bf16[2,24,1024]{2,1,0:T(8,128)(2,1)S(1)} %fusion.103), channel_id=1, source_target_pairs={{0,8},{8,0},{16,24},{24,16},{1,9},{9,1},{17,25},{25,17},{2,10},{10... | collective-permute-start | bytes 294920 | tf_op jit(solution)/shard_map/ppermute | solution.py:122
  415.9 5.6 %collective-permute-start.5 = (bf16[2,24,1024]{2,1,0:T(8,128)(2,1)S(1)}, bf16[2,24,1024]{2,1,0:T(8,128)(2,1)S(1)}, u32[]{:S(2)}, u32[]{:S(2)}) collective-permute-start(bf16[2,24,1024]{2,1,0:T(8,128)(2,1)S(1)} %fusion.99), channel_id=1, source_target_pairs={{0,8},{8,0},{16,24},{24,16},{1,9},{9,1},{17,25},{25,17},{2,10},{10... | collective-permute-start | bytes 294920 | tf_op jit(solution)/shard_map/ppermute | solution.py:122
  417.5 10.9 %collective-permute-start.22 = (bf16[96,640]{1,0:T(8,128)(2,1)S(1)}, bf16[96,640]{1,0:T(8,128)(2,1)S(1)}, u32[]{:S(2)}, u32[]{:S(2)}) collective-permute-start(bf16[96,640]{1,0:T(8,128)(2,1)S(1)} %fusion.94), channel_id=1, source_target_pairs={{0,2},{1,3},{2,0},{3,1},{4,6},{5,7},{6,4},{7,5},{8,10},{9,11},{10,... | collective-permute-start | bytes 368648 | tf_op jit(solution)/shard_map/ppermute | solution.py:122
  419.1 6.0 %collective-permute-start.15 = (bf16[24,1024]{1,0:T(8,128)(2,1)S(1)}, bf16[24,1024]{1,0:T(8,128)(2,1)S(1)}, u32[]{:S(2)}, u32[]{:S(2)}) collective-permute-start(bf16[24,1024]{1,0:T(8,128)(2,1)S(1)} %fusion.108), channel_id=1, source_target_pairs={{0,16},{8,24},{16,0},{24,8},{1,17},{9,25},{17,1},{25,9},{2,18},{10... | collective-permute-start | bytes 147464 | tf_op jit(solution)/shard_map/ppermute | solution.py:122
  421.6 5.1 %collective-permute-start.6 = (bf16[24,1024]{1,0:T(8,128)(2,1)S(1)}, bf16[24,1024]{1,0:T(8,128)(2,1)S(1)}, u32[]{:S(2)}, u32[]{:S(2)}) collective-permute-start(bf16[24,1024]{1,0:T(8,128)(2,1)S(1)} %fusion.107), channel_id=1, source_target_pairs={{0,16},{8,24},{16,0},{24,8},{1,17},{9,25},{17,1},{25,9},{2,18},{10... | collective-permute-start | bytes 147464 | tf_op jit(solution)/shard_map/ppermute | solution.py:122
  425.1 6.5 %collective-permute-start.16 = (bf16[24,1024]{1,0:T(8,128)(2,1)S(1)}, bf16[24,1024]{1,0:T(8,128)(2,1)S(1)}, u32[]{:S(2)}, u32[]{:S(2)}) collective-permute-start(bf16[24,1024]{1,0:T(8,128)(2,1)S(1)} %fusion.104), channel_id=1, source_target_pairs={{0,16},{8,24},{16,0},{24,8},{1,17},{9,25},{17,1},{25,9},{2,18},{10... | collective-permute-start | bytes 147464 | tf_op jit(solution)/shard_map/ppermute | solution.py:146
  426.7 5.2 %collective-permute-start.7 = (bf16[24,1024]{1,0:T(8,128)(2,1)S(1)}, bf16[24,1024]{1,0:T(8,128)(2,1)S(1)}, u32[]{:S(2)}, u32[]{:S(2)}) collective-permute-start(bf16[24,1024]{1,0:T(8,128)(2,1)S(1)} %fusion.105), channel_id=1, source_target_pairs={{0,16},{8,24},{16,0},{24,8},{1,17},{9,25},{17,1},{25,9},{2,18},{10... | collective-permute-start | bytes 147464 | tf_op jit(solution)/shard_map/ppermute | solution.py:146
  428.5 6.1 %collective-permute-start.23 = (bf16[2,24,1152]{2,1,0:T(8,128)(2,1)S(1)}, bf16[2,24,1152]{2,1,0:T(8,128)(2,1)S(1)}, u32[]{:S(2)}, u32[]{:S(2)}) collective-permute-start(bf16[2,24,1152]{2,1,0:T(8,128)(2,1)S(1)} %fusion.95), channel_id=1, source_target_pairs={{0,8},{8,0},{16,24},{24,16},{1,9},{9,1},{17,25},{25,17},{2,10},{10... | collective-permute-start | bytes 331784 | tf_op jit(solution)/shard_map/ppermute | solution.py:122
  431.7 6.0 %collective-permute-start.17 = (bf16[2,24,1024]{2,1,0:T(8,128)(2,1)S(1)}, bf16[2,24,1024]{2,1,0:T(8,128)(2,1)S(1)}, u32[]{:S(2)}, u32[]{:S(2)}) collective-permute-start(bf16[2,24,1024]{2,1,0:T(8,128)(2,1)S(1)} %pad_maximum_fusion.14), channel_id=1, source_target_pairs={{0,8},{8,0},{16,24},{24,16},{1,9},{9,1},{17,25},{25,17},{2,10},{10... | collective-permute-start | bytes 294920 | tf_op jit(solution)/shard_map/ppermute | solution.py:146
  431.9 6.2 %collective-permute-start.8 = (bf16[2,24,1024]{2,1,0:T(8,128)(2,1)S(1)}, bf16[2,24,1024]{2,1,0:T(8,128)(2,1)S(1)}, u32[]{:S(2)}, u32[]{:S(2)}) collective-permute-start(bf16[2,24,1024]{2,1,0:T(8,128)(2,1)S(1)} %pad_maximum_fusion.13), channel_id=1, source_target_pairs={{0,8},{8,0},{16,24},{24,16},{1,9},{9,1},{17,25},{25,17},{2,10},{10... | collective-permute-start | bytes 294920 | tf_op jit(solution)/shard_map/ppermute | solution.py:146
  434.7 6.4 %collective-permute-start.24 = (bf16[24,1152]{1,0:T(8,128)(2,1)S(1)}, bf16[24,1152]{1,0:T(8,128)(2,1)S(1)}, u32[]{:S(2)}, u32[]{:S(2)}) collective-permute-start(bf16[24,1152]{1,0:T(8,128)(2,1)S(1)} %fusion.106), channel_id=1, source_target_pairs={{0,16},{8,24},{16,0},{24,8},{1,17},{9,25},{17,1},{25,9},{2,18},{10... | collective-permute-start | bytes 165896 | tf_op jit(solution)/shard_map/ppermute | solution.py:122
  441.1 5.7 %collective-permute-start.25 = (bf16[24,1152]{1,0:T(8,128)(2,1)S(1)}, bf16[24,1152]{1,0:T(8,128)(2,1)S(1)}, u32[]{:S(2)}, u32[]{:S(2)}) collective-permute-start(bf16[24,1152]{1,0:T(8,128)(2,1)S(1)} %fusion.96), channel_id=1, source_target_pairs={{0,16},{8,24},{16,0},{24,8},{1,17},{9,25},{17,1},{25,9},{2,18},{10... | collective-permute-start | bytes 165896 | tf_op jit(solution)/shard_map/ppermute | solution.py:146
  446.8 4.8 %collective-permute-start.26 = (bf16[2,24,1152]{2,1,0:T(8,128)(2,1)S(1)}, bf16[2,24,1152]{2,1,0:T(8,128)(2,1)S(1)}, u32[]{:S(2)}, u32[]{:S(2)}) collective-permute-start(bf16[2,24,1152]{2,1,0:T(8,128)(2,1)S(1)} %pad_maximum_fusion.12), channel_id=1, source_target_pairs={{0,8},{8,0},{16,24},{24,16},{1,9},{9,1},{17,25},{25,17},{2,10},{10... | collective-permute-start | bytes 331784 | tf_op jit(solution)/shard_map/ppermute | solution.py:146
  (45 other events, 107.7 us)
Sparse Core Ops, SparseCore 0:
  11.7 42.3 all-gather.2
  56.5 58.6 all-gather.4
  321.2 78.7 reduce-scatter.1

commit v16 on v15

--- a/solution.py
+++ b/solution.py
@@ -282,18 +282,13 @@
     grad_first = None
     grad_second = None
     returned_parts = []
-    for start, size in zip(chunk_starts, chunk_sizes):
-        arrived = lax.all_to_all(
-            dispatch_rows(experts * start, experts * (start + size)).reshape(
-                experts, size, 2 * width
-            ),
-            "expert",
-            split_axis=0,
-            concat_axis=0,
-            tiled=True,
-        ).reshape(experts * size, 2 * width)
-        flat_arrived = arrived[:, :width]
-        flat_grad = arrived[:, width:]
+    expert_index = lax.axis_index("expert")
+    rotation = (expert_index + jnp.arange(experts, dtype=jnp.int32)) % experts
+    restore = (jnp.arange(experts, dtype=jnp.int32) - expert_index) % experts
+
+    def expert_block(rows_in):
+        flat_arrived = rows_in[:, :width]
+        flat_grad = rows_in[:, width:]
         hidden_grad = lax.dot_general(
             flat_grad, expert_second, COL_CONTRACT, preferred_element_type=jnp.float32
         )
@@ -313,11 +308,25 @@
         part_first = lax.dot_general(
             flat_arrived, pre_grad, ROW_CONTRACT, preferred_element_type=jnp.float32
         )
+        return jnp.concatenate([produced, row_grad], axis=1), part_first, part_second
+
+    for start, size in zip(chunk_starts, chunk_sizes):
+        sending = dispatch_rows(experts * start, experts * (start + size)).reshape(
+            experts, size, 2 * width
+        )
+        own = lax.dynamic_index_in_dim(sending, expert_index, 0, keepdims=False)
+        own_out, own_first, own_second = expert_block(own)
+        arrived = lax.all_to_all(sending, "expert", split_axis=0, concat_axis=0, tiled=True)
+        remote = jnp.take(arrived, rotation[1:], axis=0).reshape((experts - 1) * size, 2 * width)
+        remote_out, remote_first, remote_second = expert_block(remote)
+        part_first = own_first + remote_first
+        part_second = own_second + remote_second
         grad_first = part_first if grad_first is None else grad_first + part_first
         grad_second = part_second if grad_second is None else grad_second + part_second
-        returning = jnp.concatenate([produced, row_grad], axis=1).reshape(
-            experts, size, 2 * width
-        )
+        rotated = jnp.concatenate(
+            [own_out[None], remote_out.reshape(experts - 1, size, 2 * width)], axis=0
+        )
+        returning = jnp.take(rotated, restore, axis=0)
         returned_parts.append(
             lax.all_to_all(returning, "expert", split_axis=0, concat_axis=0, tiled=True)
         )

time: 474 us -> 578 us (1.22)
  the two profiles are of different devices: /device:TPU:0 before, /device:TPU:2 now
where the time goes in v16:
time: 578 us; the launch traced here: 567 us
  matrix products  209 us (36%)
  waiting for transfers between devices  138 us (24%)
  local copies, waits for them, and re-layouts  66.6 us (12%)
  starting transfers between devices  52.7 us (9%)
  other arithmetic  48.9 us (8%)
  Pallas kernels  34.9 us (6%)
  between operations  16.9 us (3%)
    all_to_all x2, waiting for transfers between devices, shards(): lax.all_to_all(sending, 'expert', split_axis=0, concat_axis=0, tiled=True)  84.1 us
    dot_general x4, matrix products, expert_block(): jnp.dot(flat_arrived, expert_first, preferred_element_type=jnp.float32)  56.7 us
    dot_general x4, matrix products, expert_block(): lax.dot_general(flat_arrived, pre_grad, ROW_CONTRACT, preferred_element_t...  32.4 us
    all_gather x1, waiting for transfers between devices, shards(): dense_full = lax.all_gather(dense_local, 'shard', axis=0, tiled=True)  29.7 us
    ppermute x21, starting transfers between devices, _exchange(): got = lax.ppermute(send.astype(jnp.bfloat16), axis_name, pairs)  25.3 us
    dot_general x4, matrix products, expert_block(): lax.dot_general(activated, flat_grad, ROW_CONTRACT, preferred_element_typ...  24.8 us
    pallas_call x1, Pallas kernels, attention_bwd(): pl.pallas_call(functools.partial(attn_bwd_kernel, images=images), grid=(p...  22 us
    dot_general x4, matrix products, expert_block(): lax.dot_general(flat_grad, expert_second, COL_CONTRACT, preferred_element...  17.7 us
  transfers between devices with their start and end apart: 34, of which 15 were waited for; matrix products, arithmetic and copies ran while one was open for 41% of the time, Pallas kernels for 6%

profile of v16, /device:TPU:2, one launch (start us, length us, event | category | flops | bytes accessed | tf_op | source)
XLA Modules:
  0.0 567.4 jit_solution(5103614798321151339)
XLA Ops:
  9.7 1.9 concatenate.67
  19.6 3.3 fusion.165
  22.9 29.7 %all-gather.3.cloned.1.call-done = bf16[768,3078]{1,0:T(8,128)(2,1)} async-done(((bf16[96,3078]{1,0:T(8,128)(2,1)}), bf16[768,3078]{1,0:T(8,128)(2,1)}) %all-gather.3.cloned.1.call-update) | async-done | bytes 4727824 | tf_op jit(solution)/shard_map/all_gather | solution.py:217
  54.5 4.6 convolution_convert_fusion
  59.3 12.9 %shard_map.178 = bf16[640,768]{1,0:T(8,128)(2,1)S(1)} custom-call(bf16[640,2304]{1,0:T(8,128)(2,1)S(1)} %pad.18.q_ref.k_ref.v_ref, bf16[640,2304]{1,0:T(8,128)(2,1)S(1)} %pad.18.q_ref.k_ref.v_ref, bf16[640,2304]{1,0:T(8,128)(2,1)S(1)} %pad.18.q_ref.k_ref.v_ref), custom_call_target="tpu_custom_call" | custom-call | tf_op jit(solution)/shard_map/pallas_call | solution.py:90
  72.2 2.6 fusion.176
  78.8 2.7 fusion.78
  81.5 2.3 convolution_convert_fusion.2
  83.8 2.6 add_convert_fusion.3
  88.9 5.1 all-to-all-start.2
  94.0 2.7 fusion.71
  102.3 43.8 %all-to-all-done.2 = bf16[4,184,1536]{2,1,0:T(8,128)(2,1)S(1)} async-done(((bf16[4,184,1536]{2,1,0:T(8,128)(2,1)}), bf16[4,184,1536]{2,1,0:T(8,128)(2,1)S(1)}, u32[]{:S(2)}, u32[]{:S(2)}) %all-to-all-start.2) | async-done | bytes 2261024 | tf_op jit(solution)/shard_map/all_to_all | solution.py:319
  147.5 3.6 all-to-all-start
  157.8 3.6 gather_fusion.2
  161.4 2.8 bitcast_select_fusion.1
  164.2 40.2 %all-to-all-done = bf16[4,192,1536]{2,1,0:T(8,128)(2,1)S(1)} async-done(((bf16[4,192,1536]{2,1,0:T(8,128)(2,1)}), bf16[4,192,1536]{2,1,0:T(8,128)(2,1)S(1)}, u32[]{:S(2)}, u32[]{:S(2)}) %all-to-all-start) | async-done | bytes 2359328 | tf_op jit(solution)/shard_map/all_to_all | solution.py:319
  206.4 2.9 bitcast_select_fusion
  209.4 4.9 slice.252
  214.2 8.6 %reshape_squeeze.3 = bf16[3072,768]{1,0:T(8,128)(2,1)} reshape(bf16[1,768,3072]{2,1,0:T(8,128)(2,1)} %slice.252) | data formatting | bytes 9437184 | tf_op jit(solution)/shard_map/reshape;squeeze | solution.py:230
  222.8 19.6 %multiply_convert_fusion.1 = (bf16[552,3072]{1,0:T(8,128)(2,1)S(1)}, f32[552,3072]{1,0:T(8,128)}, f32[552,3072]{1,0:T(8,128)}) fusion(bf16[2,768,3072]{2,1,0:T(8,128)(2,1)} %all-gather.5.cloned.1.call-done, bf16[552,1536]{1,0:T(8,128)(2,1)S(1)} %copy-done.31), kind=kOutput, calls=%fused_computation.40 | convolution fusion | flops 2714886144 | bytes 22523904 | tf_op jit(solution)/shard_map/dot_general | solution.py:295
  242.5 2.9 convolution_convert_fusion.7
  245.4 8.3 %multiply_convert_fusion.4 = (bf16[184,3072]{1,0:T(8,128)(2,1)S(1)}, f32[184,3072]{1,0:T(8,128)S(1)}, f32[184,3072]{1,0:T(8,128)}) fusion(bf16[2,768,3072]{2,1,0:T(8,128)(2,1)} %all-gather.5.cloned.1.call-done, bf16[184,1536]{1,0:T(8,128)(2,1)S(1)} %copy-done.38), kind=kOutput, calls=%fused_computation.121 | convolution fusion | flops 904962048 | bytes 10653696 | tf_op jit(solution)/shard_map/dot_general | solution.py:295
  254.7 6.8 %fusion.19 = bf16[552,3072]{1,0:T(8,128)(2,1)S(1)} fusion(f32[552,3072]{1,0:T(8,128)} %get-tuple-element.126, f32[552,3072]{1,0:T(8,128)} %get-tuple-element.92, bf16[3072,768]{1,0:T(8,128)(2,1)S(1)} %copy-done.5, bf16[552,1536]{1,0:T(8,128)(2,1)S(1)} %copy-done.31), kind=kOutput, calls=%fused_computation.39 | convolution fusion | flops 2618228736 | bytes 22523904 | tf_op jit(solution)/shard_map/dot_general | solution.py:292
  261.6 6.5 %convolution_convert_fusion.6 = bf16[552,768]{1,0:T(8,128)(2,1)S(1)} fusion(bf16[552,3072]{1,0:T(8,128)(2,1)S(1)} %fusion.19, bf16[2,768,3072]{2,1,0:T(8,128)(2,1)} %all-gather.5.cloned.1.call-done), kind=kOutput, calls=%fused_computation.186 | convolution fusion | flops 2605086720 | bytes 8957952 | tf_op jit(solution)/shard_map/dot_general | solution.py:302
  273.6 2.1 gather_fusion.3
  275.7 3.4 broadcast_select_fusion.1
  279.1 4.9 all-to-all-start.3
  284.0 20.4 %multiply_convert_fusion = (bf16[576,3072]{1,0:T(8,128)(2,1)S(1)}, f32[576,3072]{1,0:T(8,128)}, f32[576,3072]{1,0:T(8,128)}) fusion(bf16[2,768,3072]{2,1,0:T(8,128)(2,1)} %all-gather.5.cloned.1.call-done, bf16[576,1536]{1,0:T(8,128)(2,1)S(1)} %copy-done.29), kind=kOutput, calls=%fused_computation.18 | convolution fusion | flops 2832924672 | bytes 23298048 | tf_op jit(solution)/shard_map/dot_general | solution.py:295
  304.4 2.9 convolution_convert_fusion.5
  307.4 8.4 %multiply_convert_fusion.3 = (bf16[192,3072]{1,0:T(8,128)(2,1)S(1)}, f32[192,3072]{1,0:T(8,128)S(1)}, f32[192,3072]{1,0:T(8,128)}) fusion(bf16[2,768,3072]{2,1,0:T(8,128)(2,1)} %all-gather.5.cloned.1.call-done, bf16[192,1536]{1,0:T(8,128)(2,1)S(1)} %copy-done.33), kind=kOutput, calls=%fused_computation.98 | convolution fusion | flops 944308224 | bytes 10911744 | tf_op jit(solution)/shard_map/dot_general | solution.py:295
  316.9 7.2 %fusion.6 = bf16[576,3072]{1,0:T(8,128)(2,1)S(1)} fusion(f32[576,3072]{1,0:T(8,128)} %get-tuple-element.128, f32[576,3072]{1,0:T(8,128)} %get-tuple-element.88, bf16[3072,768]{1,0:T(8,128)(2,1)S(1)} %bitcast.244, bf16[576,1536]{1,0:T(8,128)(2,1)S(1)} %copy-done.29), kind=kOutput, calls=%fused_computation.17 | convolution fusion | flops 2732064768 | bytes 23298048 | tf_op jit(solution)/shard_map/dot_general | solution.py:292
  324.2 6.6 %convolution_convert_fusion.4 = bf16[576,768]{1,0:T(8,128)(2,1)S(1)} fusion(bf16[576,3072]{1,0:T(8,128)(2,1)S(1)} %fusion.6, bf16[2,768,3072]{2,1,0:T(8,128)(2,1)} %all-gather.5.cloned.1.call-done), kind=kOutput, calls=%fused_computation.184 | convolution fusion | flops 2718351360 | bytes 9142272 | tf_op jit(solution)/shard_map/dot_general | solution.py:302
  336.3 2.1 gather_fusion.1
  338.4 3.5 broadcast_select_fusion
  344.4 6.3 %fusion.103 = f32[3072,768]{1,0:T(8,128)} fusion(bf16[552,3072]{1,0:T(8,128)(2,1)S(1)} %copy-done.94, bf16[552,1536]{1,0:T(8,128)(2,1)S(1)} %copy-done.32), kind=kOutput, calls=%fused_computation.222 | convolution fusion | flops 2604662784 | bytes 13676544 | tf_op jit(solution)/shard_map/dot_general | solution.py:305
  350.7 6.5 %fusion.106 = f32[768,3072]{1,0:T(8,128)} fusion(bf16[552,3072]{1,0:T(8,128)(2,1)S(1)} %copy-done.41, bf16[552,1536]{1,0:T(8,128)(2,1)S(1)} %copy-done.32), kind=kOutput, calls=%fused_computation.225 | convolution fusion | flops 2604662784 | bytes 13676544 | tf_op jit(solution)/shard_map/dot_general | solution.py:308
  357.2 6.5 %fusion.97 = f32[3072,768]{1,0:T(8,128)} fusion(bf16[576,3072]{1,0:T(8,128)(2,1)S(1)} %copy-done.92, bf16[576,1536]{1,0:T(8,128)(2,1)S(1)} %copy-done.30), kind=kOutput, calls=%fused_computation.216 | convolution fusion | flops 2717908992 | bytes 13860864 | tf_op jit(solution)/shard_map/dot_general | solution.py:305
  363.7 10.5 %add_convert_fusion = bf16[3072,768]{1,0:T(8,128)(2,1)} fusion(f32[3072,768]{1,0:T(8,128)S(1)} %fusion.117, f32[3072,768]{1,0:T(8,128)} %fusion.103, f32[3072,768]{1,0:T(8,128)} %fusion.97, bf16[192,3072]{1,0:T(8,128)(2,1)} %copy-done.51, bf16[192,1536]{1,0:T(8,128)(2,1)S(1)} %copy-done.34), kind=kOutput, calls=%fused_computation.9 | convolution fusion | flops 915406848 | bytes 34504704 | tf_op jit(solution)/shard_map/dot_general | solution.py:305
  374.2 5.2 all-to-all-start.1
  379.4 6.0 %fusion.120 = f32[768,3072]{1,0:T(8,128)} fusion(bf16[184,3072]{1,0:T(8,128)(2,1)S(1)} %copy-done.26, bf16[184,1536]{1,0:T(8,128)(2,1)} %fusion.112), kind=kOutput, calls=%fused_computation.258 | convolution fusion | flops 868220928 | bytes 10850304 | tf_op jit(solution)/shard_map/dot_general | solution.py:308
  385.4 8.5 %stack_reshape.4 = bf16[1,768,3072]{2,1,0:T(8,128)(2,1)} reshape(bf16[3072,768]{1,0:T(8,128)(2,1)} %add_convert_fusion) | data formatting | bytes 9437184 | tf_op jit(solution)/shard_map/stack;reshape | solution.py:334
  393.8 9.9 %fusion.100 = f32[768,3072]{1,0:T(8,128)} fusion(bf16[576,3072]{1,0:T(8,128)(2,1)} %copy-done.37, bf16[576,1536]{1,0:T(8,128)(2,1)} %bitcast_select_fusion), kind=kOutput, calls=%fused_computation.219 | convolution fusion | flops 2717908992 | bytes 13860864 | tf_op jit(solution)/shard_map/dot_general | solution.py:308
  403.7 10.1 %fusion.26 = bf16[1,768,3072]{2,1,0:T(8,128)(2,1)} fusion(f32[768,3072]{1,0:T(8,128)S(1)} %copy-done.6, f32[768,3072]{1,0:T(8,128)} %fusion.106, f32[768,3072]{1,0:T(8,128)} %fusion.100, bf16[192,3072]{1,0:T(8,128)(2,1)S(1)} %fusion.27, bf16[192,1536]{1,0:T(8,128)(2,1)S(1)} %copy-done.34), kind=kOutput, calls=%fused_computation.57 | convolution fusion | flops 915406848 | bytes 34504704 | tf_op jit(solution)/shard_map/dot_general | solution.py:308
  413.8 8.4 %pad_maximum_fusion = bf16[2,768,3072]{2,1,0:T(8,128)(2,1)} fusion(bf16[1,768,3072]{2,1,0:T(8,128)(2,1)} %stack_reshape.4, bf16[1,768,3072]{2,1,0:T(8,128)(2,1)} %fusion.26), kind=kLoop, calls=%fused_computation.8 | loop fusion | flops 4718592 | bytes 18874368 | tf_op jit(solution)/shard_map/stack | solution.py:334
  423.4 5.4 fusion.76
  428.8 5.6 fusion.73
  434.3 6.1 %convolution_add_fusion.1 = f32[591,1536]{1,0:T(8,128)S(1)} fusion(f32[591,1536]{1,0:T(8,128)} %fusion.76, bf16[768,1536]{1,0:T(8,128)(2,1)} %bitcast.14, pred[1504,591]{1,0:T(32,128)(4,1)S(1)} %copy-done.54), kind=kOutput, calls=%fused_computation.72 | convolution fusion | flops 1395251712 | bytes 10113024 | tf_op jit(solution)/shard_map/dot_general | solution.py:347
  440.5 3.8 convolution_add_fusion
  450.1 22.0 %shard_map.179 = (bf16[640,768]{1,0:T(8,128)(2,1)S(1)}, bf16[640,768]{1,0:T(8,128)(2,1)S(1)}, bf16[640,768]{1,0:T(8,128)(2,1)S(1)}) custom-call(bf16[640,2304]{1,0:T(8,128)(2,1)} %copy-done, bf16[640,2304]{1,0:T(8,128)(2,1)} %copy-done, bf16[640,2304]{1,0:T(8,128)(2,1)} %copy-done, bf16[640,768]{1,0:T(8,128)(2,1)S(1)} %pad.20.g_ref), custom_call_target="tpu_custom_call" | custom-call | tf_op jit(solution)/shard_map/pallas_call | solution.py:106
  473.4 4.9 fusion.84
  478.4 2.4 fusion.65
  482.3 4.4 fusion.172
  491.1 1.9 add_convert_fusion.4
  499.9 2.5 collective-permute-done.12
  504.6 1.9 collective-permute-done.3
  507.7 3.1 collective-permute-done.19
  519.6 3.0 collective-permute-start.15
  524.7 3.0 collective-permute-start.16
  529.6 3.0 collective-permute-start.23
  534.0 2.9 collective-permute-start.8
  539.6 3.7 collective-permute-done.24
  544.0 4.7 collective-permute-done.25
  549.0 4.7 collective-permute-done.26
  556.8 2.5 fusion.175
  (450 shorter events, 94.5 us)
Async XLA Ops:
  7.2 45.4 %all-gather.3.cloned.1.call-start = ((), (), s32[]{:S(2)}) async-start(), calls=%async_computation.5 | async-start | bytes 5529600 | tf_op jit(solution)/shard_map/all_gather | solution.py:217
  11.6 197.7 %all-gather.5.cloned.1.call-start = ((), (), s32[]{:S(2)}) async-start(), calls=%async_computation.6 | async-start | bytes 10616832 | tf_op jit(solution)/shard_map/all_gather | solution.py:228
  17.3 60.7 %copy-start.59 = (f32[591]{0:T(1024)}, f32[591]{0:T(1024)S(1)}, u32[]{:S(2)}) copy-start(f32[591]{0:T(1024)S(1)} %fusion.158) | copy-start | bytes 7096
  17.6 36.5 %copy-start.67 = (f32[591]{0:T(1024)}, f32[591]{0:T(1024)S(1)}, u32[]{:S(2)}) copy-start(f32[591]{0:T(1024)S(1)} %broadcast_multiply_fusion.2) | copy-start | bytes 7096
  18.0 36.1 %copy-start.79 = (f32[591]{0:T(1024)}, f32[591]{0:T(1024)S(1)}, u32[]{:S(2)}) copy-start(f32[591]{0:T(1024)S(1)} %fusion.156) | copy-start | bytes 7096
  22.9 58.6 %copy-start.46 = (bf16[1504,591]{1,0:T(8,128)(2,1)}, bf16[1504,591]{1,0:T(8,128)(2,1)S(1)}, u32[]{:S(2)}) copy-start(bf16[1504,591]{1,0:T(8,128)(2,1)S(1)} %get-tuple-element.116) | copy-start | bytes 5333188
  54.1 21.9 %copy-start.71 = (f32[768]{0:T(1024)}, f32[768]{0:T(1024)S(1)}, u32[]{:S(2)}) copy-start(f32[768]{0:T(1024)S(1)} %get-tuple-element.69) | copy-start | bytes 9220
  59.3 12.9 %copy-start = (bf16[640,2304]{1,0:T(8,128)(2,1)}, bf16[640,2304]{1,0:T(8,128)(2,1)S(1)}, u32[]{:S(2)}) copy-start(bf16[640,2304]{1,0:T(8,128)(2,1)S(1)} %pad.18.q_ref.k_ref.v_ref) | copy-start | bytes 8847364
  76.3 20.4 %copy-start.15 = (bf16[591,768]{1,0:T(8,128)(2,1)}, bf16[591,768]{1,0:T(8,128)(2,1)S(1)}, u32[]{:S(2)}) copy-start(bf16[591,768]{1,0:T(8,128)(2,1)S(1)} %multiply_convert_fusion.6) | copy-start | bytes 2723332
  88.9 57.2 %all-to-all-start.2 = ((bf16[4,184,1536]{2,1,0:T(8,128)(2,1)}), bf16[4,184,1536]{2,1,0:T(8,128)(2,1)S(1)}, u32[]{:S(2)}, u32[]{:S(2)}) async-start(bf16[4,184,1536]{2,1,0:T(8,128)(2,1)} %pad_maximum_fusion.3), calls=%async_computation.2 | async-start | bytes 4521984 | tf_op jit(solution)/shard_map/all_to_all | solution.py:319
  147.5 57.0 %all-to-all-start = ((bf16[4,192,1536]{2,1,0:T(8,128)(2,1)}), bf16[4,192,1536]{2,1,0:T(8,128)(2,1)S(1)}, u32[]{:S(2)}, u32[]{:S(2)}) async-start(bf16[4,192,1536]{2,1,0:T(8,128)(2,1)} %pad_maximum_fusion.2), calls=%async_computation | async-start | bytes 4718592 | tf_op jit(solution)/shard_map/all_to_all | solution.py:319
  151.1 5.8 %copy-start.22 = (bf16[768,768]{1,0:T(8,128)(2,1)S(1)}, bf16[768,768]{1,0:T(8,128)(2,1)}, u32[]{:S(2)}) copy-start(bf16[768,768]{1,0:T(8,128)(2,1)} %copy-done.21) | copy-start | bytes 3538948
  164.2 42.2 %copy-start.88 = (pred[576]{0:T(1024)(128)(4,1)S(1)}, pred[576]{0:T(1024)(128)(4,1)}, u32[]{:S(2)}) copy-start(pred[576]{0:T(1024)(128)(4,1)} %broadcast_in_dim.134) | copy-start | bytes 1732
  214.2 8.6 %copy-start.31 = (bf16[552,1536]{1,0:T(8,128)(2,1)S(1)}, bf16[552,1536]{1,0:T(8,128)(2,1)}, u32[]{:S(2)}) copy-start(bf16[552,1536]{1,0:T(8,128)(2,1)} %bitcast_select_fusion.1) | copy-start | bytes 5087236
  222.8 19.6 %copy-start.5 = (bf16[3072,768]{1,0:T(8,128)(2,1)S(1)}, bf16[3072,768]{1,0:T(8,128)(2,1)}, u32[]{:S(2)}) copy-start(bf16[3072,768]{1,0:T(8,128)(2,1)} %reshape_squeeze.3) | copy-start | bytes 14155780
  261.5 6.5 %copy-start.40 = (bf16[552,3072]{1,0:T(8,128)(2,1)}, bf16[552,3072]{1,0:T(8,128)(2,1)S(1)}, u32[]{:S(2)}) copy-start(bf16[552,3072]{1,0:T(8,128)(2,1)S(1)} %fusion.19) | copy-start | bytes 10174468
  261.6 10.0 %slice-start.4 = ((s8[9437184]{0:T(1024)(128)(4,1)}), s8[4194304]{0:T(1024)(128)(4,1)S(1)}, s32[]{:S(2)}) async-start(s8[9437184]{0:T(1024)(128)(4,1)} %bitcast.265), calls=%async_computation.12 | async-start | bytes 8388608
  261.6 10.0 %slice-start.5 = ((s8[9437184]{0:T(1024)(128)(4,1)}), s8[4194304]{0:T(1024)(128)(4,1)S(1)}, s32[]{:S(2)}) async-start(s8[9437184]{0:T(1024)(128)(4,1)} %bitcast.265), calls=%async_computation.13 | async-start | bytes 8388608
  279.1 25.3 %slice-start.2 = ((s8[4718592]{0:T(1024)(128)(4,1)}), s8[524288]{0:T(1024)(128)(4,1)S(1)}, s32[]{:S(2)}) async-start(s8[4718592]{0:T(1024)(128)(4,1)} %bitcast.243), calls=%async_computation.10 | async-start | bytes 1048576
  279.1 95.1 %all-to-all-start.3 = ((bf16[4,184,1536]{2,1,0:T(8,128)(2,1)}), bf16[4,184,1536]{2,1,0:T(8,128)(2,1)}, u32[]{:S(2)}, u32[]{:S(2)}) async-start(bf16[4,184,1536]{2,1,0:T(8,128)(2,1)} %broadcast_select_fusion.1), calls=%async_computation.3 | async-start | bytes 4521984 | tf_op jit(solution)/shard_map/all_to_all | solution.py:331
  284.0 20.4 %slice-start.3 = ((s8[4718592]{0:T(1024)(128)(4,1)}), s8[4194304]{0:T(1024)(128)(4,1)S(1)}, s32[]{:S(2)}) async-start(s8[4718592]{0:T(1024)(128)(4,1)} %bitcast.243), calls=%async_computation.11 | async-start | bytes 8388608
  324.2 6.7 %copy-start.37 = (bf16[576,3072]{1,0:T(8,128)(2,1)}, bf16[576,3072]{1,0:T(8,128)(2,1)S(1)}, u32[]{:S(2)}) copy-start(bf16[576,3072]{1,0:T(8,128)(2,1)S(1)} %fusion.6) | copy-start | bytes 10616836
  324.2 10.1 %slice-start.7 = ((s8[9437184]{0:T(1024)(128)(4,1)}), s8[4194304]{0:T(1024)(128)(4,1)S(1)}, s32[]{:S(2)}) async-start(s8[9437184]{0:T(1024)(128)(4,1)} %bitcast.267), calls=%async_computation.15 | async-start | bytes 8388608
  324.2 10.1 %slice-start.8 = ((s8[9437184]{0:T(1024)(128)(4,1)}), s8[4194304]{0:T(1024)(128)(4,1)S(1)}, s32[]{:S(2)}) async-start(s8[9437184]{0:T(1024)(128)(4,1)} %bitcast.267), calls=%async_computation.16 | async-start | bytes 8388608
  344.4 6.3 %copy-start.41 = (bf16[552,3072]{1,0:T(8,128)(2,1)S(1)}, bf16[552,3072]{1,0:T(8,128)(2,1)}, u32[]{:S(2)}) copy-start(bf16[552,3072]{1,0:T(8,128)(2,1)} %copy-done.40) | copy-start | bytes 10174468
  350.7 6.5 %copy-start.30 = (bf16[576,1536]{1,0:T(8,128)(2,1)S(1)}, bf16[576,1536]{1,0:T(8,128)(2,1)}, u32[]{:S(2)}) copy-start(bf16[576,1536]{1,0:T(8,128)(2,1)} %bitcast_select_fusion) | copy-start | bytes 5308420
  350.7 6.5 %copy-start.92 = (bf16[576,3072]{1,0:T(8,128)(2,1)S(1)}, bf16[576,3072]{1,0:T(8,128)(2,1)}, u32[]{:S(2)}) copy-start(bf16[576,3072]{1,0:T(8,128)(2,1)} %copy-done.91) | copy-start | bytes 10616836
  357.2 6.5 %copy-start.34 = (bf16[192,1536]{1,0:T(8,128)(2,1)S(1)}, bf16[192,1536]{1,0:T(8,128)(2,1)}, u32[]{:S(2)}) copy-start(bf16[192,1536]{1,0:T(8,128)(2,1)} %fusion.110) | copy-start | bytes 1769476
  374.2 60.1 %all-to-all-start.1 = ((bf16[4,192,1536]{2,1,0:T(8,128)(2,1)}), bf16[4,192,1536]{2,1,0:T(8,128)(2,1)}, u32[]{:S(2)}, u32[]{:S(2)}) async-start(bf16[4,192,1536]{2,1,0:T(8,128)(2,1)} %broadcast_select_fusion), calls=%async_computation.1 | async-start | bytes 4718592 | tf_op jit(solution)/shard_map/all_to_all | solution.py:331
  379.4 177.4 %reduce-scatter.2.cloned.1.call-start = ((), (), s32[]{:S(2)}) async-start(), calls=%async_computation.7 | async-start | bytes 10616832 | tf_op jit(solution)/shard_map/reduce_scatter | solution.py:337
  393.8 9.9 %copy-start.6 = (f32[768,3072]{1,0:T(8,128)S(1)}, f32[768,3072]{1,0:T(8,128)}, u32[]{:S(2)}) copy-start(f32[768,3072]{1,0:T(8,128)} %fusion.120) | copy-start | bytes 28311556
  423.4 5.4 copy-start.53
  434.3 6.1 %copy-start.90 = (f32[591,1536]{1,0:T(8,128)S(1)}, f32[591,1536]{1,0:T(8,128)}, u32[]{:S(2)}) copy-start(f32[591,1536]{1,0:T(8,128)} %fusion.73) | copy-start | bytes 10893316
  434.3 12.2 %slice-start.10 = ((s8[4915200]{0:T(1024)(128)(4,1)}), s8[4194304]{0:T(1024)(128)(4,1)S(1)}, s32[]{:S(2)}) async-start(s8[4915200]{0:T(1024)(128)(4,1)} %bitcast.277), calls=%async_computation.18 | async-start | bytes 8388608
  440.5 6.1 %slice-start.11 = ((s8[4915200]{0:T(1024)(128)(4,1)}), s8[720896]{0:T(1024)(128)(4,1)S(1)}, s32[]{:S(2)}) async-start(s8[4915200]{0:T(1024)(128)(4,1)} %bitcast.277), calls=%async_computation.19 | async-start | bytes 1441792
  482.1 6.0 %slice-start = ((s8[7077888]{0:T(1024)(128)(4,1)}), s8[2883584]{0:T(1024)(128)(4,1)S(1)}, s32[]{:S(2)}) async-start(s8[7077888]{0:T(1024)(128)(4,1)} %bitcast.241), calls=%async_computation.8 | async-start | bytes 5767168
  482.3 6.0 %slice-start.1 = ((s8[7077888]{0:T(1024)(128)(4,1)}), s8[4194304]{0:T(1024)(128)(4,1)S(1)}, s32[]{:S(2)}) async-start(s8[7077888]{0:T(1024)(128)(4,1)} %bitcast.241), calls=%async_computation.9 | async-start | bytes 8388608
  486.8 6.2 %collective-permute-start.9 = (bf16[2,2,96,1024]{3,2,1,0:T(8,128)(2,1)S(1)}, bf16[2,2,96,1024]{3,2,1,0:T(8,128)(2,1)S(1)}, u32[]{:S(2)}, u32[]{:S(2)}) collective-permute-start(bf16[2,2,96,1024]{3,2,1,0:T(8,128)(2,1)S(1)} %fusion.95), channel_id=1, source_target_pairs={{0,1},{1,0},{2,3},{3,2},{4,5},{5,4},{6,7},{7,6},{8,9},{9,8},{10,11... | collective-permute-start | bytes 2359304 | tf_op jit(solution)/shard_map/ppermute | solution.py:122
  488.7 9.6 %collective-permute-start.18 = (bf16[2,2,96,1152]{3,2,1,0:T(8,128)(2,1)S(1)}, bf16[2,2,96,1152]{3,2,1,0:T(8,128)(2,1)S(1)}, u32[]{:S(2)}, u32[]{:S(2)}) collective-permute-start(bf16[2,2,96,1152]{3,2,1,0:T(8,128)(2,1)S(1)} %fusion.87), channel_id=1, source_target_pairs={{0,1},{1,0},{2,3},{3,2},{4,5},{5,4},{6,7},{7,6},{8,9},{9,8},{10,11... | collective-permute-start | bytes 2654216 | tf_op jit(solution)/shard_map/ppermute | solution.py:122
  489.2 6.2 %collective-permute-start = (bf16[2,2,96,1024]{3,2,1,0:T(8,128)(2,1)S(1)}, bf16[2,2,96,1024]{3,2,1,0:T(8,128)(2,1)S(1)}, u32[]{:S(2)}, u32[]{:S(2)}) collective-permute-start(bf16[2,2,96,1024]{3,2,1,0:T(8,128)(2,1)S(1)} %fusion.96), channel_id=1, source_target_pairs={{0,1},{1,0},{2,3},{3,2},{4,5},{5,4},{6,7},{7,6},{8,9},{9,8},{10,11... | collective-permute-start | bytes 2359304 | tf_op jit(solution)/shard_map/ppermute | solution.py:122
  493.5 8.8 %collective-permute-start.12 = (bf16[2,96,512]{2,1,0:T(8,128)(2,1)S(1)}, bf16[2,96,512]{2,1,0:T(8,128)(2,1)S(1)}, u32[]{:S(2)}, u32[]{:S(2)}) collective-permute-start(bf16[2,96,512]{2,1,0:T(8,128)(2,1)S(1)} %fusion.127), channel_id=1, source_target_pairs={{0,4},{1,5},{2,6},{3,7},{4,0},{5,1},{6,2},{7,3},{8,12},{9,13},{10,... | collective-permute-start | bytes 589832 | tf_op jit(solution)/shard_map/ppermute | solution.py:122
  494.6 8.3 %collective-permute-start.10 = (bf16[2,96,512]{2,1,0:T(8,128)(2,1)S(1)}, bf16[2,96,512]{2,1,0:T(8,128)(2,1)S(1)}, u32[]{:S(2)}, u32[]{:S(2)}) collective-permute-start(bf16[2,96,512]{2,1,0:T(8,128)(2,1)S(1)} %fusion.126), channel_id=1, source_target_pairs={{0,2},{1,3},{2,0},{3,1},{4,6},{5,7},{6,4},{7,5},{8,10},{9,11},{10,... | collective-permute-start | bytes 589832 | tf_op jit(solution)/shard_map/ppermute | solution.py:122
  495.8 10.7 %collective-permute-start.3 = (bf16[2,96,512]{2,1,0:T(8,128)(2,1)S(1)}, bf16[2,96,512]{2,1,0:T(8,128)(2,1)S(1)}, u32[]{:S(2)}, u32[]{:S(2)}) collective-permute-start(bf16[2,96,512]{2,1,0:T(8,128)(2,1)S(1)} %fusion.125), channel_id=1, source_target_pairs={{0,4},{1,5},{2,6},{3,7},{4,0},{5,1},{6,2},{7,3},{8,12},{9,13},{10,... | collective-permute-start | bytes 589832 | tf_op jit(solution)/shard_map/ppermute | solution.py:122
  496.5 10.7 %collective-permute-start.1 = (bf16[2,96,512]{2,1,0:T(8,128)(2,1)S(1)}, bf16[2,96,512]{2,1,0:T(8,128)(2,1)S(1)}, u32[]{:S(2)}, u32[]{:S(2)}) collective-permute-start(bf16[2,96,512]{2,1,0:T(8,128)(2,1)S(1)} %fusion.124), channel_id=1, source_target_pairs={{0,2},{1,3},{2,0},{3,1},{4,6},{5,7},{6,4},{7,5},{8,10},{9,11},{10,... | collective-permute-start | bytes 589832 | tf_op jit(solution)/shard_map/ppermute | solution.py:122
  498.7 19.5 %collective-permute-start.21 = (bf16[2,96,640]{2,1,0:T(8,128)(2,1)S(1)}, bf16[2,96,640]{2,1,0:T(8,128)(2,1)S(1)}, u32[]{:S(2)}, u32[]{:S(2)}) collective-permute-start(bf16[2,96,640]{2,1,0:T(8,128)(2,1)S(1)} %fusion.123), channel_id=1, source_target_pairs={{0,4},{1,5},{2,6},{3,7},{4,0},{5,1},{6,2},{7,3},{8,12},{9,13},{10,... | collective-permute-start | bytes 737288 | tf_op jit(solution)/shard_map/ppermute | solution.py:122
  502.3 8.4 %collective-permute-start.19 = (bf16[2,96,512]{2,1,0:T(8,128)(2,1)S(1)}, bf16[2,96,512]{2,1,0:T(8,128)(2,1)S(1)}, u32[]{:S(2)}, u32[]{:S(2)}) collective-permute-start(bf16[2,96,512]{2,1,0:T(8,128)(2,1)S(1)} %fusion.128), channel_id=1, source_target_pairs={{0,2},{1,3},{2,0},{3,1},{4,6},{5,7},{6,4},{7,5},{8,10},{9,11},{10,... | collective-permute-start | bytes 589832 | tf_op jit(solution)/shard_map/ppermute | solution.py:122
  503.0 9.9 %collective-permute-start.13 = (bf16[96,512]{1,0:T(8,128)(2,1)S(1)}, bf16[96,512]{1,0:T(8,128)(2,1)S(1)}, u32[]{:S(2)}, u32[]{:S(2)}) collective-permute-start(bf16[96,512]{1,0:T(8,128)(2,1)S(1)} %fusion.139), channel_id=1, source_target_pairs={{0,2},{1,3},{2,0},{3,1},{4,6},{5,7},{6,4},{7,5},{8,10},{9,11},{10,... | collective-permute-start | bytes 294920 | tf_op jit(solution)/shard_map/ppermute | solution.py:122
  506.6 7.5 %collective-permute-start.11 = (bf16[96,512]{1,0:T(8,128)(2,1)S(1)}, bf16[96,512]{1,0:T(8,128)(2,1)S(1)}, u32[]{:S(2)}, u32[]{:S(2)}) collective-permute-start(bf16[96,512]{1,0:T(8,128)(2,1)S(1)} %fusion.138), channel_id=1, source_target_pairs={{0,4},{1,5},{2,6},{3,7},{4,0},{5,1},{6,2},{7,3},{8,12},{9,13},{10,... | collective-permute-start | bytes 294920 | tf_op jit(solution)/shard_map/ppermute | solution.py:122
  507.2 8.7 %collective-permute-start.4 = (bf16[96,512]{1,0:T(8,128)(2,1)S(1)}, bf16[96,512]{1,0:T(8,128)(2,1)S(1)}, u32[]{:S(2)}, u32[]{:S(2)}) collective-permute-start(bf16[96,512]{1,0:T(8,128)(2,1)S(1)} %fusion.136), channel_id=1, source_target_pairs={{0,2},{1,3},{2,0},{3,1},{4,6},{5,7},{6,4},{7,5},{8,10},{9,11},{10,... | collective-permute-start | bytes 294920 | tf_op jit(solution)/shard_map/ppermute | solution.py:122
  510.8 5.7 collective-permute-start.2
  512.9 6.3 %collective-permute-start.20 = (bf16[96,512]{1,0:T(8,128)(2,1)S(1)}, bf16[96,512]{1,0:T(8,128)(2,1)S(1)}, u32[]{:S(2)}, u32[]{:S(2)}) collective-permute-start(bf16[96,512]{1,0:T(8,128)(2,1)S(1)} %fusion.140), channel_id=1, source_target_pairs={{0,4},{1,5},{2,6},{3,7},{4,0},{5,1},{6,2},{7,3},{8,12},{9,13},{10,... | collective-permute-start | bytes 294920 | tf_op jit(solution)/shard_map/ppermute | solution.py:122
  514.1 5.4 collective-permute-start.14
  516.5 6.1 %collective-permute-start.5 = (bf16[2,24,1024]{2,1,0:T(8,128)(2,1)S(1)}, bf16[2,24,1024]{2,1,0:T(8,128)(2,1)S(1)}, u32[]{:S(2)}, u32[]{:S(2)}) collective-permute-start(bf16[2,24,1024]{2,1,0:T(8,128)(2,1)S(1)} %fusion.137), channel_id=1, source_target_pairs={{0,8},{8,0},{16,24},{24,16},{1,9},{9,1},{17,25},{25,17},{2,10},{10... | collective-permute-start | bytes 294920 | tf_op jit(solution)/shard_map/ppermute | solution.py:122
  518.3 11.2 %collective-permute-start.22 = (bf16[96,640]{1,0:T(8,128)(2,1)S(1)}, bf16[96,640]{1,0:T(8,128)(2,1)S(1)}, u32[]{:S(2)}, u32[]{:S(2)}) collective-permute-start(bf16[96,640]{1,0:T(8,128)(2,1)S(1)} %fusion.132), channel_id=1, source_target_pairs={{0,2},{1,3},{2,0},{3,1},{4,6},{5,7},{6,4},{7,5},{8,10},{9,11},{10,... | collective-permute-start | bytes 368648 | tf_op jit(solution)/shard_map/ppermute | solution.py:122
  519.6 5.1 collective-permute-start.15
  522.7 6.1 %collective-permute-start.6 = (bf16[24,1024]{1,0:T(8,128)(2,1)S(1)}, bf16[24,1024]{1,0:T(8,128)(2,1)S(1)}, u32[]{:S(2)}, u32[]{:S(2)}) collective-permute-start(bf16[24,1024]{1,0:T(8,128)(2,1)S(1)} %fusion.145), channel_id=1, source_target_pairs={{0,16},{8,24},{16,0},{24,8},{1,17},{9,25},{17,1},{25,9},{2,18},{10... | collective-permute-start | bytes 147464 | tf_op jit(solution)/shard_map/ppermute | solution.py:122
  524.7 7.9 %collective-permute-start.16 = (bf16[24,1024]{1,0:T(8,128)(2,1)S(1)}, bf16[24,1024]{1,0:T(8,128)(2,1)S(1)}, u32[]{:S(2)}, u32[]{:S(2)}) collective-permute-start(bf16[24,1024]{1,0:T(8,128)(2,1)S(1)} %fusion.142), channel_id=1, source_target_pairs={{0,16},{8,24},{16,0},{24,8},{1,17},{9,25},{17,1},{25,9},{2,18},{10... | collective-permute-start | bytes 147464 | tf_op jit(solution)/shard_map/ppermute | solution.py:146
  528.8 5.2 collective-permute-start.7
  529.6 7.3 %collective-permute-start.23 = (bf16[2,24,1152]{2,1,0:T(8,128)(2,1)S(1)}, bf16[2,24,1152]{2,1,0:T(8,128)(2,1)S(1)}, u32[]{:S(2)}, u32[]{:S(2)}) collective-permute-start(bf16[2,24,1152]{2,1,0:T(8,128)(2,1)S(1)} %fusion.133), channel_id=1, source_target_pairs={{0,8},{8,0},{16,24},{24,16},{1,9},{9,1},{17,25},{25,17},{2,10},{10... | collective-permute-start | bytes 331784 | tf_op jit(solution)/shard_map/ppermute | solution.py:122
  532.7 6.1 %collective-permute-start.17 = (bf16[2,24,1024]{2,1,0:T(8,128)(2,1)S(1)}, bf16[2,24,1024]{2,1,0:T(8,128)(2,1)S(1)}, u32[]{:S(2)}, u32[]{:S(2)}) collective-permute-start(bf16[2,24,1024]{2,1,0:T(8,128)(2,1)S(1)} %pad_maximum_fusion.16), channel_id=1, source_target_pairs={{0,8},{8,0},{16,24},{24,16},{1,9},{9,1},{17,25},{25,17},{2,10},{10... | collective-permute-start | bytes 294920 | tf_op jit(solution)/shard_map/ppermute | solution.py:146
  534.0 5.5 collective-permute-start.8
  537.0 6.3 %collective-permute-start.24 = (bf16[24,1152]{1,0:T(8,128)(2,1)S(1)}, bf16[24,1152]{1,0:T(8,128)(2,1)S(1)}, u32[]{:S(2)}, u32[]{:S(2)}) collective-permute-start(bf16[24,1152]{1,0:T(8,128)(2,1)S(1)} %fusion.144), channel_id=1, source_target_pairs={{0,16},{8,24},{16,0},{24,8},{1,17},{9,25},{17,1},{25,9},{2,18},{10... | collective-permute-start | bytes 165896 | tf_op jit(solution)/shard_map/ppermute | solution.py:122
  543.3 5.4 collective-permute-start.25
  548.8 4.8 collective-permute-start.26
  (77 other events, 205.3 us)
Sparse Core Ops, SparseCore 0:
  11.8 40.8 all-gather.2
  55.1 58.6 all-gather.4
  422.3 78.7 reduce-scatter.1

commit v17 on v15

--- a/solution.py
+++ b/solution.py
@@ -124,6 +124,7 @@
 
 
 def shard_reduce_scatter(values, axis_name, split_col):
+    del split_col
     size = lax.axis_size(axis_name)
     index = lax.axis_index(axis_name)
     n_bits = size.bit_length() - 1
@@ -131,12 +132,30 @@
     bits = list(range(n_bits - 1, -1, -1))
     values = values.astype(jnp.float32).reshape([2] * n_bits + [block, values.shape[1]])
     values, bits = _exchange(values, bits, 0, axis_name, size, index)
-    first, second = values[..., :split_col], values[..., split_col:]
-    first_bits, second_bits = list(bits), list(bits)
-    for up, down in zip(range(1, n_bits), range(n_bits - 1, 0, -1)):
-        first, first_bits = _exchange(first, first_bits, up, axis_name, size, index)
-        second, second_bits = _exchange(second, second_bits, down, axis_name, size, index)
-    return jnp.concatenate([first, second], axis=-1)
+    if n_bits == 1:
+        return values
+    rest = list(range(1, n_bits))
+    half = (len(rest) + 1) // 2
+    orders = (rest, rest[half:] + rest[:half])
+    core = index & 1
+    lead = n_bits - 1
+    layouts = [[lead - b for b in reversed(order)] for order in orders]
+    tail = list(range(lead, values.ndim))
+    values = jnp.where(
+        core == 0,
+        jnp.transpose(values, layouts[0] + tail),
+        jnp.transpose(values, layouts[1] + tail),
+    )
+    for step in range(len(rest)):
+        axis = values.ndim - 3
+        bit_0, bit_1 = orders[0][step], orders[1][step]
+        mine = jnp.where(core == 0, (index >> bit_0) & 1, (index >> bit_1) & 1)
+        keep = lax.dynamic_index_in_dim(values, mine, axis, keepdims=False)
+        send = lax.dynamic_index_in_dim(values, 1 - mine, axis, keepdims=False)
+        pairs = [(i, i ^ (1 << (bit_0 if i % 2 == 0 else bit_1))) for i in range(size)]
+        got = lax.ppermute(send.astype(jnp.bfloat16), axis_name, pairs)
+        values = keep + got.astype(jnp.float32)
+    return values
 
 
 def _gather_back(values, bit, axis_name, size, index):

time: 474 us -> 476 us (level)
  waiting for transfers between devices: 87.6 us -> 103 us
  starting transfers between devices: 53.8 us -> 44.6 us
    ppermute x21 -> x9, starting transfers between devices: 28 us -> 10.8 us  [_exchange(): got = lax.ppermute(send.astype(jnp.bfloat16), axis_name, pairs)]
    ppermute x0 -> x6, waiting for transfers between devices: none -> 16 us  [shard_reduce_scatter(): got = lax.ppermute(send.astype(jnp.bfloat16), axis_name, pairs)]
    ppermute x0 -> x6, starting transfers between devices: none -> 9.43 us  [shard_reduce_scatter(): got = lax.ppermute(send.astype(jnp.bfloat16), axis_name, pairs)]
    ppermute x21 -> x9, waiting for transfers between devices: 13.7 us -> 8.83 us  [_exchange(): got = lax.ppermute(send.astype(jnp.bfloat16), axis_name, pairs)]
    unnamed x156 -> x148, local copies, waits for them, and re-layouts: 9.56 us -> 10.2 us
  transfers between devices with their start and end apart: 34 -> 28, of which waited for: 15 -> 16; matrix products, arithmetic and copies ran while one was open for 55% -> 54% of each run, Pallas kernels for 8% -> 8%
where the time goes in v17:
time: 476 us; the launch traced here: 468 us
  matrix products  186 us (39%)
  waiting for transfers between devices  103 us (22%)
  local copies, waits for them, and re-layouts  49.2 us (10%)
  starting transfers between devices  44.6 us (9%)
  Pallas kernels  35.2 us (7%)
  other arithmetic  33 us (7%)
  between operations  16.5 us (3%)
    dot_general x2, matrix products, shards(): jnp.dot(flat_arrived, expert_first, preferred_element_type=jnp.float32)  52 us
    all_gather x1, waiting for transfers between devices, shards(): dense_full = lax.all_gather(dense_local, 'shard', axis=0, tiled=True)  30.3 us
    all_to_all x2, waiting for transfers between devices, shards(): lax.all_to_all(dispatch_rows(experts * start, experts * (start + size)).r...  23 us
    dot_general x2, matrix products, shards(): lax.dot_general(flat_grad, expert_second, COL_CONTRACT, preferred_element...  22.6 us
    pallas_call x1, Pallas kernels, attention_bwd(): pl.pallas_call(functools.partial(attn_bwd_kernel, images=images), grid=(p...  21.8 us
    dot_general x2, matrix products, shards(): lax.dot_general(activated, flat_grad, ROW_CONTRACT, preferred_element_typ...  20.5 us
    ppermute x6, waiting for transfers between devices, shard_reduce_scatter(): got = lax.ppermute(send.astype(jnp.bfloat16), axis_name, pairs)  16 us
    dot_general x2, matrix products, shards(): lax.dot_general(flat_arrived, pre_grad, ROW_CONTRACT, preferred_element_t...  13.8 us
  transfers between devices with their start and end apart: 28, of which 16 were waited for; matrix products, arithmetic and copies ran while one was open for 54% of the time, Pallas kernels for 8%

profile of v17, /device:TPU:0, one launch (start us, length us, event | category | flops | bytes accessed | tf_op | source)
XLA Modules:
  0.0 467.7 jit_solution(4965876792681235366)
XLA Ops:
  9.6 2.0 concatenate.46
  20.5 3.3 fusion.117
  23.9 30.3 %all-gather.3.cloned.1.call-done = bf16[768,3078]{1,0:T(8,128)(2,1)} async-done(((bf16[96,3078]{1,0:T(8,128)(2,1)}), bf16[768,3078]{1,0:T(8,128)(2,1)}) %all-gather.3.cloned.1.call-update) | async-done | bytes 4727824 | tf_op jit(solution)/shard_map/all_gather | solution.py:236
  55.8 4.6 convolution_convert_fusion
  60.7 13.4 %shard_map.178 = bf16[640,768]{1,0:T(8,128)(2,1)S(1)} custom-call(bf16[640,2304]{1,0:T(8,128)(2,1)S(1)} %pad.18.q_ref.k_ref.v_ref, bf16[640,2304]{1,0:T(8,128)(2,1)S(1)} %pad.18.q_ref.k_ref.v_ref, bf16[640,2304]{1,0:T(8,128)(2,1)S(1)} %pad.18.q_ref.k_ref.v_ref), custom_call_target="tpu_custom_call" | custom-call | tf_op jit(solution)/shard_map/pallas_call | solution.py:90
  74.1 2.6 fusion.124
  80.7 2.7 fusion.60
  83.4 2.3 convolution_convert_fusion.4
  85.7 2.4 add_convert_fusion.3
  88.1 1.5 pad_maximum_fusion.4
  89.6 4.6 all-to-all-start.2
  94.9 3.0 fusion.53
  100.8 1.6 pad_maximum_fusion.2
  102.4 12.9 %all-gather.5.cloned.1.call-done = bf16[2,768,3072]{2,1,0:T(8,128)(2,1)} async-done(((bf16[2,96,3072]{2,1,0:T(8,128)(2,1)}), bf16[2,768,3072]{2,1,0:T(8,128)(2,1)}) %all-gather.5.cloned.1.call-update) | async-done | bytes 9437200 | tf_op jit(solution)/shard_map/all_gather | solution.py:247
  115.3 4.9 %slice.199 = bf16[1,768,3072]{2,1,0:T(8,128)(2,1)} slice(bf16[2,768,3072]{2,1,0:T(8,128)(2,1)} %all-gather.5.cloned.1.call-done), slice={[1:2], [0:768], [0:3072]} | slice | bytes 9437184 | tf_op jit(solution)/shard_map/slice | solution.py:249
  120.2 8.5 %reshape_squeeze.3 = bf16[3072,768]{1,0:T(8,128)(2,1)} reshape(bf16[1,768,3072]{2,1,0:T(8,128)(2,1)} %slice.199) | data formatting | bytes 9437184 | tf_op jit(solution)/shard_map/reshape;squeeze | solution.py:249
  128.7 17.7 %all-to-all-done.2 = bf16[4,184,1536]{2,1,0:T(8,128)(2,1)S(1)} async-done(((bf16[4,184,1536]{2,1,0:T(8,128)(2,1)}), bf16[4,184,1536]{2,1,0:T(8,128)(2,1)S(1)}, u32[]{:S(2)}, u32[]{:S(2)}) %all-to-all-start.2) | async-done | bytes 2261024 | tf_op jit(solution)/shard_map/all_to_all | solution.py:305
  147.7 3.8 all-to-all-start
  151.5 25.8 %multiply_convert_fusion.1 = (bf16[736,3072]{1,0:T(8,128)(2,1)S(1)}, f32[736,3072]{1,0:T(8,128)}, f32[736,3072]{1,0:T(8,128)}) fusion(bf16[2,768,3072]{2,1,0:T(8,128)(2,1)} %all-gather.5.cloned.1.call-done, bf16[736,1536]{1,0:T(8,128)(2,1)} %bitcast.211), kind=kOutput, calls=%fused_computation.36 | convolution fusion | flops 3619848192 | bytes 28459008 | tf_op jit(solution)/shard_map/dot_general | solution.py:319
  177.4 3.7 convolution_convert_fusion.3
  181.1 10.8 %fusion.19 = bf16[736,3072]{1,0:T(8,128)(2,1)} fusion(f32[736,3072]{1,0:T(8,128)} %get-tuple-element.116, f32[736,3072]{1,0:T(8,128)} %get-tuple-element.88, bf16[3072,768]{1,0:T(8,128)(2,1)S(1)} %copy-done.18, bf16[736,1536]{1,0:T(8,128)(2,1)} %bitcast.212), kind=kOutput, calls=%fused_computation.35 | convolution fusion | flops 3490971648 | bytes 28459008 | tf_op jit(solution)/shard_map/dot_general | solution.py:316
  191.9 6.1 %fusion.49 = bf16[736,768]{1,0:T(8,128)(2,1)S(1)} fusion(bf16[736,3072]{1,0:T(8,128)(2,1)} %fusion.19, bf16[2,768,3072]{2,1,0:T(8,128)(2,1)S(1)} %bitcast.210), kind=kOutput, calls=%fused_computation.117 | convolution fusion | flops 3473448960 | bytes 10371072 | tf_op jit(solution)/shard_map/dot_general | solution.py:326
  198.0 1.6 pad_maximum_fusion.5
  199.6 5.3 %all-to-all-done = bf16[4,192,1536]{2,1,0:T(8,128)(2,1)S(1)} async-done(((bf16[4,192,1536]{2,1,0:T(8,128)(2,1)}), bf16[4,192,1536]{2,1,0:T(8,128)(2,1)S(1)}, u32[]{:S(2)}, u32[]{:S(2)}) %all-to-all-start) | async-done | bytes 2359328 | tf_op jit(solution)/shard_map/all_to_all | solution.py:305
  204.9 4.9 %all-to-all-start.3 = ((bf16[4,184,1536]{2,1,0:T(8,128)(2,1)}), bf16[4,184,1536]{2,1,0:T(8,128)(2,1)}, u32[]{:S(2)}, u32[]{:S(2)}) async-start(bf16[4,184,1536]{2,1,0:T(8,128)(2,1)} %bitcast.15), calls=%async_computation.3 | async-start | bytes 4521984 | tf_op jit(solution)/shard_map/all_to_all | solution.py:341
  209.8 26.2 %multiply_convert_fusion = (bf16[768,3072]{1,0:T(8,128)(2,1)S(1)}, f32[768,3072]{1,0:T(8,128)}, f32[768,3072]{1,0:T(8,128)}) fusion(bf16[2,768,3072]{2,1,0:T(8,128)(2,1)} %all-gather.5.cloned.1.call-done, bf16[768,1536]{1,0:T(8,128)(2,1)S(1)} %bitcast.201), kind=kOutput, calls=%fused_computation.14 | convolution fusion | flops 3777232896 | bytes 29491200 | tf_op jit(solution)/shard_map/dot_general | solution.py:319
  236.0 11.8 %fusion.6 = bf16[768,3072]{1,0:T(8,128)(2,1)S(1)} fusion(f32[768,3072]{1,0:T(8,128)} %get-tuple-element.117, f32[768,3072]{1,0:T(8,128)} %get-tuple-element.86, bf16[3072,768]{1,0:T(8,128)(2,1)} %reshape_squeeze.3, bf16[768,1536]{1,0:T(8,128)(2,1)S(1)} %bitcast.202), kind=kOutput, calls=%fused_computation.10 | convolution fusion | flops 3642753024 | bytes 29491200 | tf_op jit(solution)/shard_map/dot_general | solution.py:316
  247.8 8.1 %convolution_convert_fusion.1 = bf16[768,768]{0,1:T(8,128)(2,1)S(1)} fusion(bf16[768,3072]{1,0:T(8,128)(2,1)S(1)} %get-tuple-element.85, bf16[3072,768]{1,0:T(8,128)(2,1)} %reshape_squeeze.3), kind=kOutput, calls=%fused_computation.115 | convolution fusion | flops 3624468480 | bytes 10616832 | tf_op jit(solution)/shard_map/dot_general | solution.py:323
  255.9 6.3 %fusion.48 = bf16[768,768]{0,1:T(8,128)(2,1)S(1)} fusion(bf16[768,3072]{1,0:T(8,128)(2,1)S(1)} %fusion.6, bf16[2,768,3072]{2,1,0:T(8,128)(2,1)} %all-gather.5.cloned.1.call-done), kind=kOutput, calls=%fused_computation.114 | convolution fusion | flops 3624468480 | bytes 10616832 | tf_op jit(solution)/shard_map/dot_general | solution.py:326
  262.4 2.5 copy.143
  264.9 10.3 %fusion.63 = f32[3072,768]{1,0:T(8,128)} fusion(bf16[768,3072]{1,0:T(8,128)(2,1)} %copy-done.64, bf16[768,1536]{1,0:T(8,128)(2,1)} %bitcast.203), kind=kOutput, calls=%fused_computation.135 | convolution fusion | flops 3623878656 | bytes 15335424 | tf_op jit(solution)/shard_map/dot_general | solution.py:329
  275.2 5.2 %all-to-all-start.1 = ((bf16[4,192,1536]{2,1,0:T(8,128)(2,1)}), bf16[4,192,1536]{2,1,0:T(8,128)(2,1)}, u32[]{:S(2)}, u32[]{:S(2)}) async-start(bf16[4,192,1536]{2,1,0:T(8,128)(2,1)} %bitcast.10), calls=%async_computation.1 | async-start | bytes 4718592 | tf_op jit(solution)/shard_map/all_to_all | solution.py:341
  280.4 10.1 %add_convert_fusion = bf16[3072,768]{1,0:T(8,128)(2,1)} fusion(f32[3072,768]{1,0:T(8,128)} %fusion.63, bf16[736,3072]{1,0:T(8,128)(2,1)} %copy-done.65, bf16[736,1536]{1,0:T(8,128)(2,1)S(1)} %bitcast.213), kind=kOutput, calls=%fused_computation.12 | convolution fusion | flops 3477602304 | bytes 19808256 | tf_op jit(solution)/shard_map/dot_general | solution.py:329
  290.5 8.6 %stack_reshape.4 = bf16[1,768,3072]{2,1,0:T(8,128)(2,1)} reshape(bf16[3072,768]{1,0:T(8,128)(2,1)} %add_convert_fusion) | data formatting | bytes 9437184 | tf_op jit(solution)/shard_map/stack;reshape | solution.py:344
  299.1 5.9 %fusion.66 = f32[768,3072]{1,0:T(8,128)S(1)} fusion(bf16[768,3072]{1,0:T(8,128)(2,1)} %copy-done.19, bf16[768,1536]{1,0:T(8,128)(2,1)S(1)} %bitcast.204), kind=kOutput, calls=%fused_computation.138 | convolution fusion | flops 3623878656 | bytes 15335424 | tf_op jit(solution)/shard_map/dot_general | solution.py:332
  305.1 7.9 %fusion.26 = bf16[1,768,3072]{2,1,0:T(8,128)(2,1)} fusion(f32[768,3072]{1,0:T(8,128)S(1)} %fusion.66, bf16[736,3072]{1,0:T(8,128)(2,1)} %fusion.19, bf16[736,1536]{1,0:T(8,128)(2,1)S(1)} %bitcast.214), kind=kOutput, calls=%fused_computation.53 | convolution fusion | flops 3477602304 | bytes 19808256 | tf_op jit(solution)/shard_map/dot_general | solution.py:332
  312.9 8.3 %pad_maximum_fusion = bf16[2,768,3072]{2,1,0:T(8,128)(2,1)} fusion(bf16[1,768,3072]{2,1,0:T(8,128)(2,1)} %stack_reshape.4, bf16[1,768,3072]{2,1,0:T(8,128)(2,1)} %fusion.26), kind=kLoop, calls=%fused_computation.11 | loop fusion | flops 4718592 | bytes 18874368 | tf_op jit(solution)/shard_map/stack | solution.py:344
  322.4 5.5 %fusion.58 = f32[591,1536]{1,0:T(8,128)} fusion(bf16[736,1536]{1,0:T(8,128)(2,1)} %bitcast.16, pred[1504,591]{1,0:T(32,128)(4,1)S(1)} %copy-done.31), kind=kOutput, calls=%fused_computation.129 | convolution fusion | flops 1336246272 | bytes 6363136 | tf_op jit(solution)/shard_map/dot_general | solution.py:357
  327.9 5.4 %fusion.55 = f32[591,1536]{1,0:T(8,128)} fusion(bf16[736,1536]{1,0:T(8,128)(2,1)} %bitcast.16, pred[1504,591]{1,0:T(32,128)(4,1)S(1)} %copy-done.30), kind=kOutput, calls=%fused_computation.126 | convolution fusion | flops 1336246272 | bytes 6363136 | tf_op jit(solution)/shard_map/dot_general | solution.py:360
  333.3 6.0 %convolution_add_fusion.1 = f32[591,1536]{1,0:T(8,128)S(1)} fusion(f32[591,1536]{1,0:T(8,128)} %fusion.58, bf16[768,1536]{1,0:T(8,128)(2,1)} %bitcast.11, pred[1504,591]{1,0:T(32,128)(4,1)S(1)} %copy-done.31), kind=kOutput, calls=%fused_computation.60 | convolution fusion | flops 1395251712 | bytes 10113024 | tf_op jit(solution)/shard_map/dot_general | solution.py:357
  339.4 3.8 convolution_add_fusion
  343.4 1.8 multiply_reduce_fusion.3
  348.9 21.8 %shard_map.179 = (bf16[640,768]{1,0:T(8,128)(2,1)S(1)}, bf16[640,768]{1,0:T(8,128)(2,1)S(1)}, bf16[640,768]{1,0:T(8,128)(2,1)S(1)}) custom-call(bf16[640,2304]{1,0:T(8,128)(2,1)} %copy-done, bf16[640,2304]{1,0:T(8,128)(2,1)} %copy-done, bf16[640,2304]{1,0:T(8,128)(2,1)} %copy-done, bf16[640,768]{1,0:T(8,128)(2,1)S(1)} %pad.20.g_ref), custom_call_target="tpu_custom_call" | custom-call | tf_op jit(solution)/shard_map/pallas_call | solution.py:106
  372.0 2.4 fusion.45
  376.8 5.1 %fusion.76 = f32[768,2304]{1,0:T(8,128)S(1)} fusion(bf16[640,2304]{1,0:T(8,128)(2,1)} %copy-done.17, bf16[591,768]{1,0:T(8,128)(2,1)} %copy-done.20), kind=kOutput, calls=%fused_computation.149 | convolution fusion | flops 2264924160 | bytes 10934784 | tf_op jit(solution)/shard_map/dot_general | solution.py:401
  386.7 2.0 add_convert_fusion.4
  389.4 1.8 collective-permute-start.8
  392.3 1.8 collective-permute-start.15
  394.2 7.0 %collective-permute-done.8 = bf16[2,96,1024]{2,1,0:T(8,128)(2,1)S(1)} collective-permute-done((bf16[2,96,1024]{2,1,0:T(8,128)(2,1)S(1)}, bf16[2,96,1024]{2,1,0:T(8,128)(2,1)S(1)}, u32[]{:S(2)}, u32[]{:S(2)}) %collective-permute-start.8) | collective-permute-done | bytes 393248 | tf_op jit(solution)/shard_map/ppermute | solution.py:156
  401.4 1.5 collective-permute-start.9
  402.9 3.8 collective-permute-done.1
  406.9 2.4 collective-permute-start.2
  409.2 5.1 %collective-permute-done.15 = bf16[2,96,1152]{2,1,0:T(8,128)(2,1)S(1)} collective-permute-done((bf16[2,96,1152]{2,1,0:T(8,128)(2,1)S(1)}, bf16[2,96,1152]{2,1,0:T(8,128)(2,1)S(1)}, u32[]{:S(2)}, u32[]{:S(2)}) %collective-permute-start.15) | collective-permute-done | bytes 442400 | tf_op jit(solution)/shard_map/ppermute | solution.py:156
  416.1 1.6 collective-permute-start.10
  418.4 3.4 collective-permute-done.10
  421.8 2.5 collective-permute-start.11
  425.9 2.2 collective-permute-done.11
  431.2 2.2 collective-permute-start.17
  435.4 2.0 collective-permute-start.6
  437.4 1.7 collective-permute-start.18
  440.7 2.5 collective-permute-done.18
  444.4 4.5 collective-permute-done.19
  449.0 4.7 collective-permute-done.20
  456.9 2.5 fusion.123
  (312 shorter events, 52.8 us)
Async XLA Ops:
  7.2 6.0 %copy-start.34 = (bf16[1,96,3072]{2,1,0:T(8,128)(2,1)S(1)}, bf16[1,96,3072]{2,1,0:T(8,128)(2,1)}, u32[]{:S(2)}) copy-start(bf16[1,96,3072]{2,1,0:T(8,128)(2,1)} %param.19) | copy-start | bytes 1769476
  7.2 46.9 %all-gather.3.cloned.1.call-start = ((), (), s32[]{:S(2)}) async-start(), calls=%async_computation.5 | async-start | bytes 5529600 | tf_op jit(solution)/shard_map/all_gather | solution.py:236
  9.6 5.8 %copy-start.45 = (s32[591,2]{0,1:T(2,128)S(1)}, s32[591,2]{0,1:T(2,128)}, u32[]{:S(2)}) copy-start(s32[591,2]{0,1:T(2,128)} %param.13) | copy-start | bytes 14188
  11.6 6.7 %copy-start.5 = (bf16[591,768]{1,0:T(8,128)(2,1)S(1)}, bf16[591,768]{1,0:T(8,128)(2,1)}, u32[]{:S(2)}) copy-start(bf16[591,768]{1,0:T(8,128)(2,1)} %param.11) | copy-start | bytes 2723332
  11.6 103.7 %all-gather.5.cloned.1.call-start = ((), (), s32[]{:S(2)}) async-start(), calls=%async_computation.6 | async-start | bytes 10616832 | tf_op jit(solution)/shard_map/all_gather | solution.py:247
  13.2 5.8 %copy-start.7 = (bf16[591,768]{1,0:T(8,128)(2,1)S(1)}, bf16[591,768]{1,0:T(8,128)(2,1)}, u32[]{:S(2)}) copy-start(bf16[591,768]{1,0:T(8,128)(2,1)} %param.21) | copy-start | bytes 2723332
  18.3 61.6 %copy-start.35 = (f32[591]{0:T(1024)}, f32[591]{0:T(1024)S(1)}, u32[]{:S(2)}) copy-start(f32[591]{0:T(1024)S(1)} %fusion.114) | copy-start | bytes 7096
  18.6 36.9 %copy-start.43 = (f32[591]{0:T(1024)}, f32[591]{0:T(1024)S(1)}, u32[]{:S(2)}) copy-start(f32[591]{0:T(1024)S(1)} %broadcast_multiply_fusion.2) | copy-start | bytes 7096
  19.0 4.9 %copy-start.57 = (f32[591]{0:T(1024)}, f32[591]{0:T(1024)S(1)}, u32[]{:S(2)}) copy-start(f32[591]{0:T(1024)S(1)} %fusion.44) | copy-start | bytes 7096
  19.0 36.5 %copy-start.55 = (f32[591]{0:T(1024)}, f32[591]{0:T(1024)S(1)}, u32[]{:S(2)}) copy-start(f32[591]{0:T(1024)S(1)} %fusion.112) | copy-start | bytes 7096
  23.9 59.6 %copy-start.24 = (bf16[1504,591]{1,0:T(8,128)(2,1)}, bf16[1504,591]{1,0:T(8,128)(2,1)S(1)}, u32[]{:S(2)}) copy-start(bf16[1504,591]{1,0:T(8,128)(2,1)S(1)} %get-tuple-element.106) | copy-start | bytes 5333188
  55.4 5.0 %copy-start.53 = (f32[768]{0:T(1024)}, f32[768]{0:T(1024)S(1)}, u32[]{:S(2)}) copy-start(f32[768]{0:T(1024)S(1)} %get-tuple-element.70) | copy-start | bytes 9220
  55.4 21.7 %copy-start.47 = (f32[768]{0:T(1024)}, f32[768]{0:T(1024)S(1)}, u32[]{:S(2)}) copy-start(f32[768]{0:T(1024)S(1)} %get-tuple-element.69) | copy-start | bytes 9220
  55.8 4.6 copy-start.20
  60.7 13.4 %copy-start = (bf16[640,2304]{1,0:T(8,128)(2,1)}, bf16[640,2304]{1,0:T(8,128)(2,1)S(1)}, u32[]{:S(2)}) copy-start(bf16[640,2304]{1,0:T(8,128)(2,1)S(1)} %pad.18.q_ref.k_ref.v_ref) | copy-start | bytes 8847364
  76.7 3.7 copy-start.14
  78.3 19.6 %copy-start.10 = (bf16[591,768]{1,0:T(8,128)(2,1)}, bf16[591,768]{1,0:T(8,128)(2,1)S(1)}, u32[]{:S(2)}) copy-start(bf16[591,768]{1,0:T(8,128)(2,1)S(1)} %multiply_convert_fusion.4) | copy-start | bytes 2723332
  80.7 5.0 %copy-start.27 = (bf16[591,2,768]{2,0,1:T(8,128)(2,1)}, bf16[591,2,768]{2,0,1:T(8,128)(2,1)S(1)}, u32[]{:S(2)}) copy-start(bf16[591,2,768]{2,0,1:T(8,128)(2,1)S(1)} %multiply_convert_fusion.2) | copy-start | bytes 5446660
  89.6 56.7 %all-to-all-start.2 = ((bf16[4,184,1536]{2,1,0:T(8,128)(2,1)}), bf16[4,184,1536]{2,1,0:T(8,128)(2,1)S(1)}, u32[]{:S(2)}, u32[]{:S(2)}) async-start(bf16[4,184,1536]{2,1,0:T(8,128)(2,1)} %pad_maximum_fusion.4), calls=%async_computation.2 | async-start | bytes 4521984 | tf_op jit(solution)/shard_map/all_to_all | solution.py:305
  147.7 57.2 %all-to-all-start = ((bf16[4,192,1536]{2,1,0:T(8,128)(2,1)}), bf16[4,192,1536]{2,1,0:T(8,128)(2,1)S(1)}, u32[]{:S(2)}, u32[]{:S(2)}) async-start(bf16[4,192,1536]{2,1,0:T(8,128)(2,1)} %pad_maximum_fusion.2), calls=%async_computation | async-start | bytes 4718592 | tf_op jit(solution)/shard_map/all_to_all | solution.py:305
  151.5 25.8 %copy-start.18 = (bf16[3072,768]{1,0:T(8,128)(2,1)S(1)}, bf16[3072,768]{1,0:T(8,128)(2,1)}, u32[]{:S(2)}) copy-start(bf16[3072,768]{1,0:T(8,128)(2,1)} %reshape_squeeze.3) | copy-start | bytes 14155780
  177.4 3.7 copy-start.65
  177.4 14.5 %slice-start = ((s8[9437184]{0:T(1024)(128)(4,1)}), s8[4194304]{0:T(1024)(128)(4,1)S(1)}, s32[]{:S(2)}) async-start(s8[9437184]{0:T(1024)(128)(4,1)} %bitcast.209), calls=%async_computation.8 | async-start | bytes 8388608
  177.4 14.5 %slice-start.1 = ((s8[9437184]{0:T(1024)(128)(4,1)}), s8[4194304]{0:T(1024)(128)(4,1)S(1)}, s32[]{:S(2)}) async-start(s8[9437184]{0:T(1024)(128)(4,1)} %bitcast.209), calls=%async_computation.9 | async-start | bytes 8388608
  181.1 10.8 %slice-start.2 = ((s8[9437184]{0:T(1024)(128)(4,1)}), s8[1048576]{0:T(1024)(128)(4,1)S(1)}, s32[]{:S(2)}) async-start(s8[9437184]{0:T(1024)(128)(4,1)} %bitcast.209), calls=%async_computation.10 | async-start | bytes 2097152
  204.9 31.1 %copy-start.15 = (bf16[4,192,1536]{2,1,0:T(8,128)(2,1)}, bf16[4,192,1536]{2,1,0:T(8,128)(2,1)S(1)}, u32[]{:S(2)}) copy-start(bf16[4,192,1536]{2,1,0:T(8,128)(2,1)S(1)} %all-to-all-done) | copy-start | bytes 7077892
  204.9 70.3 %all-to-all-start.3 = ((bf16[4,184,1536]{2,1,0:T(8,128)(2,1)}), bf16[4,184,1536]{2,1,0:T(8,128)(2,1)}, u32[]{:S(2)}, u32[]{:S(2)}) async-start(bf16[4,184,1536]{2,1,0:T(8,128)(2,1)} %bitcast.15), calls=%async_computation.3 | async-start | bytes 4521984 | tf_op jit(solution)/shard_map/all_to_all | solution.py:341
  236.0 11.8 %copy-start.64 = (bf16[768,3072]{1,0:T(8,128)(2,1)}, bf16[768,3072]{1,0:T(8,128)(2,1)S(1)}, u32[]{:S(2)}) copy-start(bf16[768,3072]{1,0:T(8,128)(2,1)S(1)} %get-tuple-element.85) | copy-start | bytes 14155780
  247.8 8.2 %copy-start.19 = (bf16[768,3072]{1,0:T(8,128)(2,1)}, bf16[768,3072]{1,0:T(8,128)(2,1)S(1)}, u32[]{:S(2)}) copy-start(bf16[768,3072]{1,0:T(8,128)(2,1)S(1)} %fusion.6) | copy-start | bytes 14155780
  275.2 5.2 %copy-start.22 = (bf16[4,184,1536]{2,1,0:T(8,128)(2,1)S(1)}, bf16[4,184,1536]{2,1,0:T(8,128)(2,1)}, u32[]{:S(2)}) copy-start(bf16[4,184,1536]{2,1,0:T(8,128)(2,1)} %copy-done.21) | copy-start | bytes 6782980
  275.2 58.1 %all-to-all-start.1 = ((bf16[4,192,1536]{2,1,0:T(8,128)(2,1)}), bf16[4,192,1536]{2,1,0:T(8,128)(2,1)}, u32[]{:S(2)}, u32[]{:S(2)}) async-start(bf16[4,192,1536]{2,1,0:T(8,128)(2,1)} %bitcast.10), calls=%async_computation.1 | async-start | bytes 4718592 | tf_op jit(solution)/shard_map/all_to_all | solution.py:341
  280.4 176.5 %reduce-scatter.2.cloned.1.call-start = ((), (), s32[]{:S(2)}) async-start(), calls=%async_computation.7 | async-start | bytes 10616832 | tf_op jit(solution)/shard_map/reduce_scatter | solution.py:347
  290.5 8.6 %copy-start.16 = (bf16[4,192,1536]{2,1,0:T(8,128)(2,1)S(1)}, bf16[4,192,1536]{2,1,0:T(8,128)(2,1)}, u32[]{:S(2)}) copy-start(bf16[4,192,1536]{2,1,0:T(8,128)(2,1)} %copy-done.15) | copy-start | bytes 7077892
  299.1 5.9 %copy-start.23 = (bf16[4,184,1536]{2,1,0:T(8,128)(2,1)S(1)}, bf16[4,184,1536]{2,1,0:T(8,128)(2,1)}, u32[]{:S(2)}) copy-start(bf16[4,184,1536]{2,1,0:T(8,128)(2,1)} %copy-done.21) | copy-start | bytes 6782980
  322.4 5.5 %copy-start.30 = (pred[1504,591]{1,0:T(32,128)(4,1)S(1)}, pred[1504,591]{1,0:T(32,128)(4,1)}, u32[]{:S(2)}) copy-start(pred[1504,591]{1,0:T(32,128)(4,1)} %get-tuple-element.110) | copy-start | bytes 2666596
  333.3 6.0 %copy-start.63 = (f32[591,1536]{1,0:T(8,128)S(1)}, f32[591,1536]{1,0:T(8,128)}, u32[]{:S(2)}) copy-start(f32[591,1536]{1,0:T(8,128)} %fusion.55) | copy-start | bytes 10893316
  333.3 12.3 %slice-start.3 = ((s8[4915200]{0:T(1024)(128)(4,1)}), s8[4194304]{0:T(1024)(128)(4,1)S(1)}, s32[]{:S(2)}) async-start(s8[4915200]{0:T(1024)(128)(4,1)} %bitcast.227), calls=%async_computation.11 | async-start | bytes 8388608
  339.4 3.9 copy-start.4
  339.4 3.9 copy-start.8
  339.4 3.9 copy-start.36
  339.4 3.9 copy-start.61
  339.4 3.9 copy-start.62
  339.4 6.2 %slice-start.4 = ((s8[4915200]{0:T(1024)(128)(4,1)}), s8[720896]{0:T(1024)(128)(4,1)S(1)}, s32[]{:S(2)}) async-start(s8[4915200]{0:T(1024)(128)(4,1)} %bitcast.227), calls=%async_computation.12 | async-start | bytes 1441792
  383.1 5.9 %collective-permute-start.7 = (bf16[2,2,96,1024]{3,2,1,0:T(8,128)(2,1)S(1)}, bf16[2,2,96,1024]{3,2,1,0:T(8,128)(2,1)S(1)}, u32[]{:S(2)}, u32[]{:S(2)}) collective-permute-start(bf16[2,2,96,1024]{3,2,1,0:T(8,128)(2,1)S(1)} %fusion.83), channel_id=1, source_target_pairs={{0,1},{1,0},{2,3},{3,2},{4,5},{5,4},{6,7},{7,6},{8,9},{9,8},{10,11... | collective-permute-start | bytes 2359304 | tf_op jit(solution)/shard_map/ppermute | solution.py:122
  383.3 7.9 %collective-permute-start = (bf16[2,2,96,1024]{3,2,1,0:T(8,128)(2,1)S(1)}, bf16[2,2,96,1024]{3,2,1,0:T(8,128)(2,1)S(1)}, u32[]{:S(2)}, u32[]{:S(2)}) collective-permute-start(bf16[2,2,96,1024]{3,2,1,0:T(8,128)(2,1)S(1)} %fusion.84), channel_id=1, source_target_pairs={{0,1},{1,0},{2,3},{3,2},{4,5},{5,4},{6,7},{7,6},{8,9},{9,8},{10,11... | collective-permute-start | bytes 2359304 | tf_op jit(solution)/shard_map/ppermute | solution.py:122
  388.9 3.1 collective-permute-start.14
  389.4 11.8 %collective-permute-start.8 = (bf16[2,96,1024]{2,1,0:T(8,128)(2,1)S(1)}, bf16[2,96,1024]{2,1,0:T(8,128)(2,1)S(1)}, u32[]{:S(2)}, u32[]{:S(2)}) collective-permute-start(bf16[2,96,1024]{2,1,0:T(8,128)(2,1)S(1)} %fusion.87), channel_id=1, source_target_pairs={{0,2},{1,5},{2,0},{3,7},{4,6},{5,1},{6,4},{7,3},{8,10},{9,13},{10,... | collective-permute-start | bytes 1179656 | tf_op jit(solution)/shard_map/ppermute | solution.py:156
  391.6 15.1 %collective-permute-start.1 = (bf16[2,96,1024]{2,1,0:T(8,128)(2,1)S(1)}, bf16[2,96,1024]{2,1,0:T(8,128)(2,1)S(1)}, u32[]{:S(2)}, u32[]{:S(2)}) collective-permute-start(bf16[2,96,1024]{2,1,0:T(8,128)(2,1)S(1)} %fusion.86), channel_id=1, source_target_pairs={{0,2},{1,5},{2,0},{3,7},{4,6},{5,1},{6,4},{7,3},{8,10},{9,13},{10,... | collective-permute-start | bytes 1179656 | tf_op jit(solution)/shard_map/ppermute | solution.py:156
  392.3 22.0 %collective-permute-start.15 = (bf16[2,96,1152]{2,1,0:T(8,128)(2,1)S(1)}, bf16[2,96,1152]{2,1,0:T(8,128)(2,1)S(1)}, u32[]{:S(2)}, u32[]{:S(2)}) collective-permute-start(bf16[2,96,1152]{2,1,0:T(8,128)(2,1)S(1)} %fusion.85), channel_id=1, source_target_pairs={{0,2},{1,5},{2,0},{3,7},{4,6},{5,1},{6,4},{7,3},{8,10},{9,13},{10,... | collective-permute-start | bytes 1327112 | tf_op jit(solution)/shard_map/ppermute | solution.py:156
  401.4 14.7 %collective-permute-start.9 = (bf16[96,1024]{1,0:T(8,128)(2,1)S(1)}, bf16[96,1024]{1,0:T(8,128)(2,1)S(1)}, u32[]{:S(2)}, u32[]{:S(2)}) collective-permute-start(bf16[96,1024]{1,0:T(8,128)(2,1)S(1)} %fusion.90), channel_id=1, source_target_pairs={{0,4},{1,3},{2,6},{3,1},{4,0},{5,7},{6,2},{7,5},{8,12},{9,11},{10,... | collective-permute-start | bytes 589832 | tf_op jit(solution)/shard_map/ppermute | solution.py:156
  406.9 10.8 %collective-permute-start.2 = (bf16[96,1024]{1,0:T(8,128)(2,1)S(1)}, bf16[96,1024]{1,0:T(8,128)(2,1)S(1)}, u32[]{:S(2)}, u32[]{:S(2)}) collective-permute-start(bf16[96,1024]{1,0:T(8,128)(2,1)S(1)} %fusion.89), channel_id=1, source_target_pairs={{0,4},{1,3},{2,6},{3,1},{4,0},{5,7},{6,2},{7,5},{8,12},{9,11},{10,... | collective-permute-start | bytes 589832 | tf_op jit(solution)/shard_map/ppermute | solution.py:156
  414.5 16.6 %collective-permute-start.16 = (bf16[96,1152]{1,0:T(8,128)(2,1)S(1)}, bf16[96,1152]{1,0:T(8,128)(2,1)S(1)}, u32[]{:S(2)}, u32[]{:S(2)}) collective-permute-start(bf16[96,1152]{1,0:T(8,128)(2,1)S(1)} %fusion.88), channel_id=1, source_target_pairs={{0,4},{1,3},{2,6},{3,1},{4,0},{5,7},{6,2},{7,5},{8,12},{9,11},{10,... | collective-permute-start | bytes 663560 | tf_op jit(solution)/shard_map/ppermute | solution.py:156
  416.1 5.6 %collective-permute-start.10 = (bf16[2,24,1024]{2,1,0:T(8,128)(2,1)S(1)}, bf16[2,24,1024]{2,1,0:T(8,128)(2,1)S(1)}, u32[]{:S(2)}, u32[]{:S(2)}) collective-permute-start(bf16[2,24,1024]{2,1,0:T(8,128)(2,1)S(1)} %fusion.97), channel_id=1, source_target_pairs={{0,8},{8,0},{16,24},{24,16},{1,9},{9,1},{17,25},{25,17},{2,10},{10... | collective-permute-start | bytes 294920 | tf_op jit(solution)/shard_map/ppermute | solution.py:122
  417.7 6.5 %collective-permute-start.3 = (bf16[2,24,1024]{2,1,0:T(8,128)(2,1)S(1)}, bf16[2,24,1024]{2,1,0:T(8,128)(2,1)S(1)}, u32[]{:S(2)}, u32[]{:S(2)}) collective-permute-start(bf16[2,24,1024]{2,1,0:T(8,128)(2,1)S(1)} %fusion.96), channel_id=1, source_target_pairs={{0,8},{8,0},{16,24},{24,16},{1,9},{9,1},{17,25},{25,17},{2,10},{10... | collective-permute-start | bytes 294920 | tf_op jit(solution)/shard_map/ppermute | solution.py:122
  421.8 6.2 %collective-permute-start.11 = (bf16[24,1024]{1,0:T(8,128)(2,1)S(1)}, bf16[24,1024]{1,0:T(8,128)(2,1)S(1)}, u32[]{:S(2)}, u32[]{:S(2)}) collective-permute-start(bf16[24,1024]{1,0:T(8,128)(2,1)S(1)} %fusion.102), channel_id=1, source_target_pairs={{0,16},{8,24},{16,0},{24,8},{1,17},{9,25},{17,1},{25,9},{2,18},{10... | collective-permute-start | bytes 147464 | tf_op jit(solution)/shard_map/ppermute | solution.py:122
  424.3 5.9 %collective-permute-start.4 = (bf16[24,1024]{1,0:T(8,128)(2,1)S(1)}, bf16[24,1024]{1,0:T(8,128)(2,1)S(1)}, u32[]{:S(2)}, u32[]{:S(2)}) collective-permute-start(bf16[24,1024]{1,0:T(8,128)(2,1)S(1)} %fusion.101), channel_id=1, source_target_pairs={{0,16},{8,24},{16,0},{24,8},{1,17},{9,25},{17,1},{25,9},{2,18},{10... | collective-permute-start | bytes 147464 | tf_op jit(solution)/shard_map/ppermute | solution.py:122
  428.1 5.6 %collective-permute-start.12 = (bf16[24,1024]{1,0:T(8,128)(2,1)S(1)}, bf16[24,1024]{1,0:T(8,128)(2,1)S(1)}, u32[]{:S(2)}, u32[]{:S(2)}) collective-permute-start(bf16[24,1024]{1,0:T(8,128)(2,1)S(1)} %fusion.98), channel_id=1, source_target_pairs={{0,16},{8,24},{16,0},{24,8},{1,17},{9,25},{17,1},{25,9},{2,18},{10... | collective-permute-start | bytes 147464 | tf_op jit(solution)/shard_map/ppermute | solution.py:165
  430.2 5.1 %collective-permute-start.5 = (bf16[24,1024]{1,0:T(8,128)(2,1)S(1)}, bf16[24,1024]{1,0:T(8,128)(2,1)S(1)}, u32[]{:S(2)}, u32[]{:S(2)}) collective-permute-start(bf16[24,1024]{1,0:T(8,128)(2,1)S(1)} %fusion.99), channel_id=1, source_target_pairs={{0,16},{8,24},{16,0},{24,8},{1,17},{9,25},{17,1},{25,9},{2,18},{10... | collective-permute-start | bytes 147464 | tf_op jit(solution)/shard_map/ppermute | solution.py:165
  431.2 6.2 %collective-permute-start.17 = (bf16[2,24,1152]{2,1,0:T(8,128)(2,1)S(1)}, bf16[2,24,1152]{2,1,0:T(8,128)(2,1)S(1)}, u32[]{:S(2)}, u32[]{:S(2)}) collective-permute-start(bf16[2,24,1152]{2,1,0:T(8,128)(2,1)S(1)} %fusion.94), channel_id=1, source_target_pairs={{0,8},{8,0},{16,24},{24,16},{1,9},{9,1},{17,25},{25,17},{2,10},{10... | collective-permute-start | bytes 331784 | tf_op jit(solution)/shard_map/ppermute | solution.py:122
  433.7 5.5 %collective-permute-start.13 = (bf16[2,24,1024]{2,1,0:T(8,128)(2,1)S(1)}, bf16[2,24,1024]{2,1,0:T(8,128)(2,1)S(1)}, u32[]{:S(2)}, u32[]{:S(2)}) collective-permute-start(bf16[2,24,1024]{2,1,0:T(8,128)(2,1)S(1)} %pad_maximum_fusion.11), channel_id=1, source_target_pairs={{0,8},{8,0},{16,24},{24,16},{1,9},{9,1},{17,25},{25,17},{2,10},{10... | collective-permute-start | bytes 294920 | tf_op jit(solution)/shard_map/ppermute | solution.py:165
  435.4 5.3 %collective-permute-start.6 = (bf16[2,24,1024]{2,1,0:T(8,128)(2,1)S(1)}, bf16[2,24,1024]{2,1,0:T(8,128)(2,1)S(1)}, u32[]{:S(2)}, u32[]{:S(2)}) collective-permute-start(bf16[2,24,1024]{2,1,0:T(8,128)(2,1)S(1)} %pad_maximum_fusion.10), channel_id=1, source_target_pairs={{0,8},{8,0},{16,24},{24,16},{1,9},{9,1},{17,25},{25,17},{2,10},{10... | collective-permute-start | bytes 294920 | tf_op jit(solution)/shard_map/ppermute | solution.py:165
  437.4 5.7 %collective-permute-start.18 = (bf16[24,1152]{1,0:T(8,128)(2,1)S(1)}, bf16[24,1152]{1,0:T(8,128)(2,1)S(1)}, u32[]{:S(2)}, u32[]{:S(2)}) collective-permute-start(bf16[24,1152]{1,0:T(8,128)(2,1)S(1)} %fusion.100), channel_id=1, source_target_pairs={{0,16},{8,24},{16,0},{24,8},{1,17},{9,25},{17,1},{25,9},{2,18},{10... | collective-permute-start | bytes 165896 | tf_op jit(solution)/shard_map/ppermute | solution.py:122
  443.1 5.7 %collective-permute-start.19 = (bf16[24,1152]{1,0:T(8,128)(2,1)S(1)}, bf16[24,1152]{1,0:T(8,128)(2,1)S(1)}, u32[]{:S(2)}, u32[]{:S(2)}) collective-permute-start(bf16[24,1152]{1,0:T(8,128)(2,1)S(1)} %fusion.95), channel_id=1, source_target_pairs={{0,16},{8,24},{16,0},{24,8},{1,17},{9,25},{17,1},{25,9},{2,18},{10... | collective-permute-start | bytes 165896 | tf_op jit(solution)/shard_map/ppermute | solution.py:165
  448.9 4.8 %collective-permute-start.20 = (bf16[2,24,1152]{2,1,0:T(8,128)(2,1)S(1)}, bf16[2,24,1152]{2,1,0:T(8,128)(2,1)S(1)}, u32[]{:S(2)}, u32[]{:S(2)}) collective-permute-start(bf16[2,24,1152]{2,1,0:T(8,128)(2,1)S(1)} %pad_maximum_fusion.9), channel_id=1, source_target_pairs={{0,8},{8,0},{16,24},{24,16},{1,9},{9,1},{17,25},{25,17},{2,10},{10... | collective-permute-start | bytes 331784 | tf_op jit(solution)/shard_map/ppermute | solution.py:165
  (35 other events, 70.2 us)
Sparse Core Ops, SparseCore 0:
  11.7 42.3 all-gather.2
  56.6 58.6 all-gather.4
  321.4 79.4 reduce-scatter.1

commit v18 on v8

--- a/solution.py
+++ b/solution.py
@@ -141,6 +141,33 @@
     return jnp.concatenate([first, second], axis=-1)
 
 
+def _gather_back(values, bit, axis_name, size, index):
+    n_bits = size.bit_length() - 1
+    mine = (index >> bit) & 1
+    pairs = [(i, i ^ (1 << bit)) for i in range(size)]
+    got = lax.ppermute(values, axis_name, pairs)
+    low = jnp.where(mine == 0, values, got)
+    high = jnp.where(mine == 0, got, values)
+    return jnp.stack([low, high], axis=n_bits - 1 - bit)
+
+
+def expert_all_reduce(values, axis_name):
+    size = lax.axis_size(axis_name)
+    index = lax.axis_index(axis_name)
+    n_bits = size.bit_length() - 1
+    rows = values.shape[0]
+    if rows % size:
+        return lax.psum(values.astype(jnp.bfloat16), axis_name).astype(jnp.float32)
+    bits = list(range(n_bits - 1, -1, -1))
+    parts = values.astype(jnp.float32).reshape([2] * n_bits + [rows // size, values.shape[1]])
+    for bit in range(n_bits):
+        parts, bits = _exchange(parts, bits, bit, axis_name, size, index)
+    parts = parts.astype(jnp.bfloat16)
+    for bit in range(n_bits - 1, -1, -1):
+        parts = _gather_back(parts, bit, axis_name, size, index)
+    return parts.reshape(rows, values.shape[1]).astype(jnp.float32)
+
+
 def layer_norm(values, norm_gain):
     row_mean = jnp.mean(values, axis=-1, keepdims=True)
     centered = values - row_mean
@@ -206,9 +233,11 @@
 
     token_f = tokens.astype(jnp.float32)
     attn_in = lax.optimization_barrier(layer_norm(token_f, gain_one).astype(jnp.bfloat16))
-    projected = jnp.dot(attn_in, full_qkv, preferred_element_type=jnp.float32).astype(jnp.bfloat16)
     slot = -(-SEQ // 16) * 16
-    projected_pad = to_slots(projected, images, slot)
+    attn_in_pad = to_slots(attn_in, images, slot)
+    projected_pad = jnp.dot(
+        attn_in_pad, full_qkv, preferred_element_type=jnp.float32
+    ).astype(jnp.bfloat16)
     mixed_rows = from_slots(attention_fwd(projected_pad, images, slot), images, slot)
     hidden_state = token_f + jnp.dot(mixed_rows, full_out, preferred_element_type=jnp.float32)
     moe_in = layer_norm(hidden_state, gain_two).astype(jnp.bfloat16)
@@ -245,21 +274,21 @@
     weighted = chosen * live_rows[:, None]
     grad_picked = (weighted[:, :, None] * grad_out[:, None, :]).astype(jnp.bfloat16)
 
-    sent_rows = jnp.dot(
-        take_first + take_second, moe_in, preferred_element_type=jnp.float32
-    ).astype(jnp.bfloat16)
-    sent_grad = (
-        jnp.dot(take_first, grad_picked[:, 0], preferred_element_type=jnp.float32)
-        + jnp.dot(take_second, grad_picked[:, 1], preferred_element_type=jnp.float32)
-    ).astype(jnp.bfloat16)
-    outgoing = jnp.concatenate([sent_rows, sent_grad], axis=1)
+    def dispatch_rows(low, high):
+        first = take_first[low:high]
+        second = take_second[low:high]
+        sent_rows = jnp.dot(first + second, moe_in, preferred_element_type=jnp.float32)
+        sent_grad = jnp.dot(
+            first, grad_picked[:, 0], preferred_element_type=jnp.float32
+        ) + jnp.dot(second, grad_picked[:, 1], preferred_element_type=jnp.float32)
+        return jnp.concatenate([sent_rows, sent_grad], axis=1).astype(jnp.bfloat16)
 
     grad_first = None
     grad_second = None
     returned_parts = []
     for start, size in zip(chunk_starts, chunk_sizes):
         arrived = lax.all_to_all(
-            outgoing[experts * start : experts * (start + size)].reshape(
+            dispatch_rows(experts * start, experts * (start + size)).reshape(
                 experts, size, 2 * width
             ),
             "expert",
@@ -305,15 +334,19 @@
     grad_in_share = expert_share[0][None]
     grad_back_share = expert_share[1].reshape(back_rows, width)[None]
 
-    returned = jnp.concatenate(
-        [part.reshape(-1, 2 * width) for part in returned_parts], axis=0
-    )
-    picked_first = lax.dot_general(
-        take_first, returned, ROW_CONTRACT, preferred_element_type=jnp.float32
-    )
-    picked_second = lax.dot_general(
-        take_second, returned, ROW_CONTRACT, preferred_element_type=jnp.float32
-    )
+    picked_first = None
+    picked_second = None
+    for start, size, part in zip(chunk_starts, chunk_sizes, returned_parts):
+        low, high = experts * start, experts * (start + size)
+        part = part.reshape(-1, 2 * width)
+        part_first = lax.dot_general(
+            take_first[low:high], part, ROW_CONTRACT, preferred_element_type=jnp.float32
+        )
+        part_second = lax.dot_general(
+            take_second[low:high], part, ROW_CONTRACT, preferred_element_type=jnp.float32
+        )
+        picked_first = part_first if picked_first is None else picked_first + part_first
+        picked_second = part_second if picked_second is None else picked_second + part_second
     moe_out = (
         weighted[:, 0:1] * picked_first[:, :width] + weighted[:, 1:2] * picked_second[:, :width]
     )
@@ -349,15 +382,15 @@
     mixed_grad = to_slots(mixed_grad.astype(jnp.bfloat16), images, slot)
     grad_q, grad_k, grad_v = attention_bwd(projected_pad, mixed_grad, images, slot)
     projected_grad = jnp.concatenate([grad_q, grad_k, grad_v], axis=1)
-    attn_in_pad = to_slots(attn_in, images, slot)
     grad_qkv = lax.dot_general(
         attn_in_pad, projected_grad, ROW_CONTRACT, preferred_element_type=jnp.float32
     )
-    attn_in_grad = lax.dot_general(
-        from_slots(projected_grad, images, slot),
-        full_qkv,
-        COL_CONTRACT,
-        preferred_element_type=jnp.float32,
+    attn_in_grad = from_slots(
+        lax.dot_general(
+            projected_grad, full_qkv, COL_CONTRACT, preferred_element_type=jnp.float32
+        ),
+        images,
+        slot,
     )
     _, first_back = jax.vjp(layer_norm, token_f, gain_one)
     token_part, grad_gain_one = first_back(attn_in_grad)
@@ -368,8 +401,18 @@
     )
     small = jnp.pad(small, ((0, 0), (0, 128 - small.shape[1])))
     dense_grads = jnp.concatenate([grad_qkv, grad_wout, small], axis=1)
-    dense_share = shard_reduce_scatter(dense_grads, "shard", 128 * (dense_grads.shape[1] // 256))
-    dense_total = lax.psum(dense_share.astype(jnp.bfloat16), "expert").astype(jnp.float32)
+    n_parts = 3
+    bounds = [128 * (dense_grads.shape[1] * k // (128 * n_parts)) for k in range(n_parts)]
+    bounds = bounds + [dense_grads.shape[1]]
+    dense_total = jnp.concatenate(
+        [
+            expert_all_reduce(
+                shard_reduce_scatter(part, "shard", 128 * (part.shape[1] // 256)), "expert"
+            )
+            for part in (dense_grads[:, low:high] for low, high in zip(bounds[:-1], bounds[1:]))
+        ],
+        axis=1,
+    )
     return (
         output,
         grad_tokens,

time: 596 us -> 477 us (0.80)
  waiting for transfers between devices: 227 us -> 85.1 us
  starting transfers between devices: 24.1 us -> 53.4 us
  local copies, waits for them, and re-layouts: 70.1 us -> 59.4 us
    reduce_scatter x1, waiting for transfers between devices: 72.9 us -> 0.01 us  [shards(): lax.psum_scatter(expert_grads, 'shard', scatter_dimension=1, tiled=True)]
    all_to_all x2, waiting for transfers between devices: 51.5 us -> 0.01 us  [shards(): lax.all_to_all(returning, 'expert', split_axis=0, concat_axis=0, tiled=True)]
    ppermute x5 -> x21, starting transfers between devices: 5.15 us -> 27.6 us  [_exchange(): got = lax.ppermute(send.astype(jnp.bfloat16), axis_name, pairs)]
    dot_general x7 -> x12, matrix products: 29.2 us -> 40.2 us  [the longest x2 11.5 us: shards(): lax.dot_general(take_first[low:high], part, ROW_CONTRACT, preferred_eleme...]
    ppermute x5 -> x21, waiting for transfers between devices: 21.6 us -> 11.1 us  [_exchange(): got = lax.ppermute(send.astype(jnp.bfloat16), axis_name, pairs)]
    ppermute x0 -> x6, waiting for transfers between devices: none -> 9.46 us  [_gather_back(): got = lax.ppermute(values, axis_name, pairs)]
    all_to_all x2, waiting for transfers between devices: 28.5 us -> 19.4 us  [shards(): lax.all_to_all(dispatch_rows(experts * start, experts * (start + size)).r...]
    ppermute x0 -> x6, starting transfers between devices: none -> 7.25 us  [_gather_back(): got = lax.ppermute(values, axis_name, pairs)]
  transfers between devices with their start and end apart: 13 -> 34, of which waited for: 11 -> 16; matrix products, arithmetic and copies ran while one was open for 38% -> 56% of each run, Pallas kernels for 1% -> 7%
where the time goes in v18:
time: 477 us; the launch traced here: 470 us
  matrix products  187 us (39%)
  waiting for transfers between devices  85.1 us (18%)
  local copies, waits for them, and re-layouts  59.4 us (12%)
  starting transfers between devices  53.4 us (11%)
  other arithmetic  36.7 us (8%)
  Pallas kernels  30.8 us (6%)
  between operations  16.7 us (4%)
    dot_general x2, matrix products, shards(): jnp.dot(flat_arrived, expert_first, preferred_element_type=jnp.float32)  52 us
    all_gather x1, waiting for transfers between devices, shards(): dense_full = lax.all_gather(dense_local, 'shard', axis=0, tiled=True)  28.5 us
    ppermute x21, starting transfers between devices, _exchange(): got = lax.ppermute(send.astype(jnp.bfloat16), axis_name, pairs)  27.6 us
    dot_general x2, matrix products, shards(): lax.dot_general(flat_grad, expert_second, COL_CONTRACT, preferred_element...  22.5 us
    pallas_call x1, Pallas kernels, attention_bwd(): pl.pallas_call(functools.partial(attn_bwd_kernel, images=images, slot=slo...  22.3 us
    dot_general x2, matrix products, shards(): lax.dot_general(activated, flat_grad, ROW_CONTRACT, preferred_element_typ...  20.4 us
    all_to_all x2, waiting for transfers between devices, shards(): lax.all_to_all(dispatch_rows(experts * start, experts * (start + size)).r...  19.4 us
    all_gather x1, waiting for transfers between devices, shards(): expert_full = lax.all_gather(expert_local, 'shard', axis=1, tiled=True)  16.6 us
  transfers between devices with their start and end apart: 34, of which 16 were waited for; matrix products, arithmetic and copies ran while one was open for 56% of the time, Pallas kernels for 7%

profile of v18, /device:TPU:0, one launch (start us, length us, event | category | flops | bytes accessed | tf_op | source)
XLA Modules:
  0.0 469.6 jit_solution(9661620733363758429)
XLA Ops:
  9.6 1.9 concatenate.55
  13.2 2.3 pad_maximum_fusion.6
  21.6 4.0 fusion.116
  25.6 28.5 %all-gather.3.cloned.1.call-done = bf16[768,3078]{1,0:T(8,128)(2,1)} async-done(((bf16[96,3078]{1,0:T(8,128)(2,1)}), bf16[768,3078]{1,0:T(8,128)(2,1)}) %all-gather.3.cloned.1.call-update) | async-done | bytes 4727824 | tf_op jit(solution)/shard_map/all_gather | solution.py:219
  57.6 4.4 convolution_convert_fusion.q_ref.k_ref.v_ref
  62.0 8.6 %shard_map.178 = bf16[624,768]{1,0:T(8,128)(2,1)S(1)} custom-call(bf16[624,2304]{1,0:T(8,128)(2,1)S(1)} %convolution_convert_fusion.q_ref.k_ref.v_ref, bf16[624,2304]{1,0:T(8,128)(2,1)S(1)} %convolution_convert_fusion.q_ref.k_ref.v_ref, bf16[624,2304]{1,0:T(8,128)(2,1)S(1)} %convolution_convert_fusion.q_ref.k_ref.v_ref), custom_call_target="tpu_custom_call" | custom-call | tf_op jit(solution)/shard_map/pallas_call | solution.py:81
  70.9 2.6 fusion.125
  77.0 2.7 fusion.59
  79.7 2.6 convolution_convert_fusion.4
  82.3 2.2 add_convert_fusion.3
  86.0 4.6 all-to-all-start.2
  91.2 2.9 fusion.52
  98.6 16.6 %all-gather.5.cloned.1.call-done = bf16[2,768,3072]{2,1,0:T(8,128)(2,1)} async-done(((bf16[2,96,3072]{2,1,0:T(8,128)(2,1)}), bf16[2,768,3072]{2,1,0:T(8,128)(2,1)}) %all-gather.5.cloned.1.call-update) | async-done | bytes 9437200 | tf_op jit(solution)/shard_map/all_gather | solution.py:230
  115.2 4.9 %slice.223 = bf16[1,768,3072]{2,1,0:T(8,128)(2,1)} slice(bf16[2,768,3072]{2,1,0:T(8,128)(2,1)} %all-gather.5.cloned.1.call-done), slice={[1:2], [0:768], [0:3072]} | slice | bytes 9437184 | tf_op jit(solution)/shard_map/slice | solution.py:232
  120.1 8.5 %reshape_squeeze.3 = bf16[3072,768]{1,0:T(8,128)(2,1)} reshape(bf16[1,768,3072]{2,1,0:T(8,128)(2,1)} %slice.223) | data formatting | bytes 9437184 | tf_op jit(solution)/shard_map/reshape;squeeze | solution.py:232
  128.6 14.1 %all-to-all-done.2 = bf16[4,184,1536]{2,1,0:T(8,128)(2,1)S(1)} async-done(((bf16[4,184,1536]{2,1,0:T(8,128)(2,1)}), bf16[4,184,1536]{2,1,0:T(8,128)(2,1)S(1)}, u32[]{:S(2)}, u32[]{:S(2)}) %all-to-all-start.2) | async-done | bytes 2261024 | tf_op jit(solution)/shard_map/all_to_all | solution.py:290
  144.0 3.8 all-to-all-start
  147.9 25.8 %multiply_convert_fusion.1 = (bf16[736,3072]{1,0:T(8,128)(2,1)S(1)}, f32[736,3072]{1,0:T(8,128)}, f32[736,3072]{1,0:T(8,128)}) fusion(bf16[2,768,3072]{2,1,0:T(8,128)(2,1)} %all-gather.5.cloned.1.call-done, bf16[736,1536]{1,0:T(8,128)(2,1)} %bitcast.243), kind=kOutput, calls=%fused_computation.36 | convolution fusion | flops 3619848192 | bytes 28459008 | tf_op jit(solution)/shard_map/dot_general | solution.py:304
  173.7 3.7 convolution_convert_fusion.3
  177.4 10.8 %fusion.19 = bf16[736,3072]{1,0:T(8,128)(2,1)} fusion(f32[736,3072]{1,0:T(8,128)} %get-tuple-element.120, f32[736,3072]{1,0:T(8,128)} %get-tuple-element.88, bf16[3072,768]{1,0:T(8,128)(2,1)S(1)} %copy-done.18, bf16[736,1536]{1,0:T(8,128)(2,1)} %bitcast.244), kind=kOutput, calls=%fused_computation.35 | convolution fusion | flops 3490971648 | bytes 28459008 | tf_op jit(solution)/shard_map/dot_general | solution.py:301
  188.2 6.1 %fusion.48 = bf16[736,768]{1,0:T(8,128)(2,1)S(1)} fusion(bf16[736,3072]{1,0:T(8,128)(2,1)} %fusion.19, bf16[2,768,3072]{2,1,0:T(8,128)(2,1)S(1)} %bitcast.242), kind=kOutput, calls=%fused_computation.113 | convolution fusion | flops 3473448960 | bytes 10371072 | tf_op jit(solution)/shard_map/dot_general | solution.py:311
  195.9 5.3 %all-to-all-done = bf16[4,192,1536]{2,1,0:T(8,128)(2,1)S(1)} async-done(((bf16[4,192,1536]{2,1,0:T(8,128)(2,1)}), bf16[4,192,1536]{2,1,0:T(8,128)(2,1)S(1)}, u32[]{:S(2)}, u32[]{:S(2)}) %all-to-all-start) | async-done | bytes 2359328 | tf_op jit(solution)/shard_map/all_to_all | solution.py:290
  201.2 4.9 %all-to-all-start.3 = ((bf16[4,184,1536]{2,1,0:T(8,128)(2,1)}), bf16[4,184,1536]{2,1,0:T(8,128)(2,1)}, u32[]{:S(2)}, u32[]{:S(2)}) async-start(bf16[4,184,1536]{2,1,0:T(8,128)(2,1)} %bitcast.17), calls=%async_computation.3 | async-start | bytes 4521984 | tf_op jit(solution)/shard_map/all_to_all | solution.py:326
  206.1 26.2 %multiply_convert_fusion = (bf16[768,3072]{1,0:T(8,128)(2,1)S(1)}, f32[768,3072]{1,0:T(8,128)}, f32[768,3072]{1,0:T(8,128)}) fusion(bf16[2,768,3072]{2,1,0:T(8,128)(2,1)} %all-gather.5.cloned.1.call-done, bf16[768,1536]{1,0:T(8,128)(2,1)S(1)} %bitcast.231), kind=kOutput, calls=%fused_computation.14 | convolution fusion | flops 3777232896 | bytes 29491200 | tf_op jit(solution)/shard_map/dot_general | solution.py:304
  232.3 11.8 %fusion.6 = bf16[768,3072]{1,0:T(8,128)(2,1)S(1)} fusion(f32[768,3072]{1,0:T(8,128)} %get-tuple-element.121, f32[768,3072]{1,0:T(8,128)} %get-tuple-element.86, bf16[3072,768]{1,0:T(8,128)(2,1)} %reshape_squeeze.3, bf16[768,1536]{1,0:T(8,128)(2,1)S(1)} %bitcast.232), kind=kOutput, calls=%fused_computation.10 | convolution fusion | flops 3642753024 | bytes 29491200 | tf_op jit(solution)/shard_map/dot_general | solution.py:301
  244.1 8.1 %convolution_convert_fusion.1 = bf16[768,768]{0,1:T(8,128)(2,1)S(1)} fusion(bf16[768,3072]{1,0:T(8,128)(2,1)S(1)} %get-tuple-element.85, bf16[3072,768]{1,0:T(8,128)(2,1)} %reshape_squeeze.3), kind=kOutput, calls=%fused_computation.111 | convolution fusion | flops 3624468480 | bytes 10616832 | tf_op jit(solution)/shard_map/dot_general | solution.py:308
  252.3 6.3 %fusion.47 = bf16[768,768]{0,1:T(8,128)(2,1)S(1)} fusion(bf16[768,3072]{1,0:T(8,128)(2,1)S(1)} %fusion.6, bf16[2,768,3072]{2,1,0:T(8,128)(2,1)} %all-gather.5.cloned.1.call-done), kind=kOutput, calls=%fused_computation.110 | convolution fusion | flops 3624468480 | bytes 10616832 | tf_op jit(solution)/shard_map/dot_general | solution.py:311
  258.7 2.5 copy.130
  261.2 10.3 %fusion.62 = f32[3072,768]{1,0:T(8,128)} fusion(bf16[768,3072]{1,0:T(8,128)(2,1)} %copy-done.65, bf16[768,1536]{1,0:T(8,128)(2,1)} %bitcast.233), kind=kOutput, calls=%fused_computation.131 | convolution fusion | flops 3623878656 | bytes 15335424 | tf_op jit(solution)/shard_map/dot_general | solution.py:314
  271.5 5.2 %all-to-all-start.1 = ((bf16[4,192,1536]{2,1,0:T(8,128)(2,1)}), bf16[4,192,1536]{2,1,0:T(8,128)(2,1)}, u32[]{:S(2)}, u32[]{:S(2)}) async-start(bf16[4,192,1536]{2,1,0:T(8,128)(2,1)} %bitcast.12), calls=%async_computation.1 | async-start | bytes 4718592 | tf_op jit(solution)/shard_map/all_to_all | solution.py:326
  276.7 10.1 %add_convert_fusion = bf16[3072,768]{1,0:T(8,128)(2,1)} fusion(f32[3072,768]{1,0:T(8,128)} %fusion.62, bf16[736,3072]{1,0:T(8,128)(2,1)} %copy-done.66, bf16[736,1536]{1,0:T(8,128)(2,1)S(1)} %bitcast.245), kind=kOutput, calls=%fused_computation.12 | convolution fusion | flops 3477602304 | bytes 19808256 | tf_op jit(solution)/shard_map/dot_general | solution.py:314
  286.8 8.6 %stack_reshape.4 = bf16[1,768,3072]{2,1,0:T(8,128)(2,1)} reshape(bf16[3072,768]{1,0:T(8,128)(2,1)} %add_convert_fusion) | data formatting | bytes 9437184 | tf_op jit(solution)/shard_map/stack;reshape | solution.py:329
  295.4 5.9 %fusion.65 = f32[768,3072]{1,0:T(8,128)S(1)} fusion(bf16[768,3072]{1,0:T(8,128)(2,1)} %copy-done.19, bf16[768,1536]{1,0:T(8,128)(2,1)S(1)} %bitcast.234), kind=kOutput, calls=%fused_computation.134 | convolution fusion | flops 3623878656 | bytes 15335424 | tf_op jit(solution)/shard_map/dot_general | solution.py:317
  301.4 7.8 %fusion.26 = bf16[1,768,3072]{2,1,0:T(8,128)(2,1)} fusion(f32[768,3072]{1,0:T(8,128)S(1)} %fusion.65, bf16[736,3072]{1,0:T(8,128)(2,1)} %fusion.19, bf16[736,1536]{1,0:T(8,128)(2,1)S(1)} %bitcast.246), kind=kOutput, calls=%fused_computation.53 | convolution fusion | flops 3477602304 | bytes 19808256 | tf_op jit(solution)/shard_map/dot_general | solution.py:317
  309.2 8.3 %pad_maximum_fusion = bf16[2,768,3072]{2,1,0:T(8,128)(2,1)} fusion(bf16[1,768,3072]{2,1,0:T(8,128)(2,1)} %stack_reshape.4, bf16[1,768,3072]{2,1,0:T(8,128)(2,1)} %fusion.26), kind=kLoop, calls=%fused_computation.11 | loop fusion | flops 4718592 | bytes 18874368 | tf_op jit(solution)/shard_map/stack | solution.py:329
  318.7 5.5 %fusion.57 = f32[591,1536]{1,0:T(8,128)} fusion(bf16[736,1536]{1,0:T(8,128)(2,1)} %bitcast.18, pred[1504,591]{1,0:T(32,128)(4,1)S(1)} %copy-done.31), kind=kOutput, calls=%fused_computation.125 | convolution fusion | flops 1336246272 | bytes 6363136 | tf_op jit(solution)/shard_map/dot_general | solution.py:342
  324.2 5.4 %fusion.54 = f32[591,1536]{1,0:T(8,128)} fusion(bf16[736,1536]{1,0:T(8,128)(2,1)} %bitcast.18, pred[1504,591]{1,0:T(32,128)(4,1)S(1)} %copy-done.30), kind=kOutput, calls=%fused_computation.122 | convolution fusion | flops 1336246272 | bytes 6363136 | tf_op jit(solution)/shard_map/dot_general | solution.py:345
  329.6 6.0 %convolution_add_fusion.1 = f32[591,1536]{1,0:T(8,128)S(1)} fusion(f32[591,1536]{1,0:T(8,128)} %fusion.57, bf16[768,1536]{1,0:T(8,128)(2,1)} %bitcast.13, pred[1504,591]{1,0:T(32,128)(4,1)S(1)} %copy-done.31), kind=kOutput, calls=%fused_computation.60 | convolution fusion | flops 1395251712 | bytes 10113024 | tf_op jit(solution)/shard_map/dot_general | solution.py:342
  335.7 3.8 convolution_add_fusion
  339.6 1.8 multiply_reduce_fusion.3
  341.8 2.0 multiply_reduce_fusion
  347.0 2.2 convolution_convert_fusion.5
  349.7 22.3 %shard_map.179 = (bf16[624,768]{1,0:T(8,128)(2,1)S(1)}, bf16[624,768]{1,0:T(8,128)(2,1)S(1)}, bf16[624,768]{1,0:T(8,128)(2,1)S(1)}) custom-call(bf16[624,2304]{1,0:T(8,128)(2,1)} %copy-done, bf16[624,2304]{1,0:T(8,128)(2,1)} %copy-done, bf16[624,2304]{1,0:T(8,128)(2,1)} %copy-done, bf16[624,768]{1,0:T(8,128)(2,1)S(1)} %bitcast.221), custom_call_target="tpu_custom_call" | custom-call | tf_op jit(solution)/shard_map/pallas_call | solution.py:97
  373.2 4.9 %fusion.127 = f32[768,2304]{1,0:T(8,128)} fusion(bf16[624,768]{1,0:T(8,128)(2,1)S(1)} %bitcast.240, bf16[624,2304]{1,0:T(8,128)(2,1)S(1)} %constant_dynamic-update-slice_fusion), kind=kOutput, calls=%fused_computation.302 | convolution fusion | flops 2208301056 | bytes 10911744 | tf_op jit(solution)/shard_map/dot_general | solution.py:385
  378.1 2.4 fusion.28
  382.0 1.7 reshape.328
  385.0 2.8 fusion.42
  388.1 3.9 fusion.121
  396.1 2.0 add_convert_fusion.4
  413.4 2.9 collective-permute-done.19
  419.2 2.1 collective-permute-start.14
  421.7 1.9 collective-permute-start.5
  424.7 2.4 collective-permute-start.15
  427.2 2.1 collective-permute-start.6
  429.4 1.8 collective-permute-done.15
  434.7 2.6 collective-permute-start.23
  437.5 2.8 collective-permute-done.7
  440.5 2.6 collective-permute-start.24
  443.1 1.9 collective-permute-done.8
  445.6 3.0 collective-permute-start.25
  448.7 2.1 collective-permute-done.25
  450.8 2.0 collective-permute-start.26
  452.9 2.7 collective-permute-done.26
  458.8 2.5 fusion.124
  (354 shorter events, 68.3 us)
Async XLA Ops:
  7.2 46.9 %all-gather.3.cloned.1.call-start = ((), (), s32[]{:S(2)}) async-start(), calls=%async_computation.5 | async-start | bytes 5529600 | tf_op jit(solution)/shard_map/all_gather | solution.py:219
  8.8 7.7 %copy-start.48 = (s32[591,2]{0,1:T(2,128)S(1)}, s32[591,2]{0,1:T(2,128)}, u32[]{:S(2)}) copy-start(s32[591,2]{0,1:T(2,128)} %param.13) | copy-start | bytes 14188
  11.6 7.9 %copy-start.3 = (bf16[591,768]{1,0:T(8,128)(2,1)S(1)}, bf16[591,768]{1,0:T(8,128)(2,1)}, u32[]{:S(2)}) copy-start(bf16[591,768]{1,0:T(8,128)(2,1)} %param.11) | copy-start | bytes 2723332
  11.6 103.7 %all-gather.5.cloned.1.call-start = ((), (), s32[]{:S(2)}) async-start(), calls=%async_computation.6 | async-start | bytes 10616832 | tf_op jit(solution)/shard_map/all_gather | solution.py:230
  13.2 6.9 %copy-start.10 = (bf16[591,768]{1,0:T(8,128)(2,1)S(1)}, bf16[591,768]{1,0:T(8,128)(2,1)}, u32[]{:S(2)}) copy-start(bf16[591,768]{1,0:T(8,128)(2,1)} %param.21) | copy-start | bytes 2723332
  19.4 57.3 %copy-start.36 = (f32[591]{0:T(1024)}, f32[591]{0:T(1024)S(1)}, u32[]{:S(2)}) copy-start(f32[591]{0:T(1024)S(1)} %fusion.114) | copy-start | bytes 7096
  19.6 35.8 %copy-start.40 = (f32[591]{0:T(1024)}, f32[591]{0:T(1024)S(1)}, u32[]{:S(2)}) copy-start(f32[591]{0:T(1024)S(1)} %broadcast_multiply_fusion.2) | copy-start | bytes 7096
  20.1 5.5 %copy-start.58 = (f32[591]{0:T(1024)}, f32[591]{0:T(1024)S(1)}, u32[]{:S(2)}) copy-start(f32[591]{0:T(1024)S(1)} %fusion.43) | copy-start | bytes 7096
  20.1 35.3 %copy-start.56 = (f32[591]{0:T(1024)}, f32[591]{0:T(1024)S(1)}, u32[]{:S(2)}) copy-start(f32[591]{0:T(1024)S(1)} %fusion.112) | copy-start | bytes 7096
  55.4 18.5 %copy-start.50 = (f32[768]{0:T(1024)}, f32[768]{0:T(1024)S(1)}, u32[]{:S(2)}) copy-start(f32[768]{0:T(1024)S(1)} %get-tuple-element.69) | copy-start | bytes 9220
  62.0 8.6 %copy-start = (bf16[624,2304]{1,0:T(8,128)(2,1)}, bf16[624,2304]{1,0:T(8,128)(2,1)S(1)}, u32[]{:S(2)}) copy-start(bf16[624,2304]{1,0:T(8,128)(2,1)S(1)} %convolution_convert_fusion.q_ref.k_ref.v_ref) | copy-start | bytes 8626180
  70.9 4.1 copy-start.34
  75.0 19.1 %copy-start.13 = (bf16[591,768]{1,0:T(8,128)(2,1)}, bf16[591,768]{1,0:T(8,128)(2,1)S(1)}, u32[]{:S(2)}) copy-start(bf16[591,768]{1,0:T(8,128)(2,1)S(1)} %multiply_convert_fusion.4) | copy-start | bytes 2723332
  77.0 5.3 %copy-start.27 = (bf16[591,2,768]{2,0,1:T(8,128)(2,1)}, bf16[591,2,768]{2,0,1:T(8,128)(2,1)S(1)}, u32[]{:S(2)}) copy-start(bf16[591,2,768]{2,0,1:T(8,128)(2,1)S(1)} %multiply_convert_fusion.2) | copy-start | bytes 5446660
  86.0 56.7 %all-to-all-start.2 = ((bf16[4,184,1536]{2,1,0:T(8,128)(2,1)}), bf16[4,184,1536]{2,1,0:T(8,128)(2,1)S(1)}, u32[]{:S(2)}, u32[]{:S(2)}) async-start(bf16[4,184,1536]{2,1,0:T(8,128)(2,1)} %pad_maximum_fusion.4), calls=%async_computation.2 | async-start | bytes 4521984 | tf_op jit(solution)/shard_map/all_to_all | solution.py:290
  144.0 57.2 %all-to-all-start = ((bf16[4,192,1536]{2,1,0:T(8,128)(2,1)}), bf16[4,192,1536]{2,1,0:T(8,128)(2,1)S(1)}, u32[]{:S(2)}, u32[]{:S(2)}) async-start(bf16[4,192,1536]{2,1,0:T(8,128)(2,1)} %pad_maximum_fusion.2), calls=%async_computation | async-start | bytes 4718592 | tf_op jit(solution)/shard_map/all_to_all | solution.py:290
  147.9 25.8 %copy-start.18 = (bf16[3072,768]{1,0:T(8,128)(2,1)S(1)}, bf16[3072,768]{1,0:T(8,128)(2,1)}, u32[]{:S(2)}) copy-start(bf16[3072,768]{1,0:T(8,128)(2,1)} %reshape_squeeze.3) | copy-start | bytes 14155780
  173.7 14.5 %slice-start.2 = ((s8[9437184]{0:T(1024)(128)(4,1)}), s8[4194304]{0:T(1024)(128)(4,1)S(1)}, s32[]{:S(2)}) async-start(s8[9437184]{0:T(1024)(128)(4,1)} %bitcast.241), calls=%async_computation.10 | async-start | bytes 8388608
  173.7 14.5 %slice-start.3 = ((s8[9437184]{0:T(1024)(128)(4,1)}), s8[4194304]{0:T(1024)(128)(4,1)S(1)}, s32[]{:S(2)}) async-start(s8[9437184]{0:T(1024)(128)(4,1)} %bitcast.241), calls=%async_computation.11 | async-start | bytes 8388608
  177.4 10.8 %slice-start.4 = ((s8[9437184]{0:T(1024)(128)(4,1)}), s8[1048576]{0:T(1024)(128)(4,1)S(1)}, s32[]{:S(2)}) async-start(s8[9437184]{0:T(1024)(128)(4,1)} %bitcast.241), calls=%async_computation.12 | async-start | bytes 2097152
  201.2 31.1 %copy-start.16 = (bf16[4,192,1536]{2,1,0:T(8,128)(2,1)}, bf16[4,192,1536]{2,1,0:T(8,128)(2,1)S(1)}, u32[]{:S(2)}) copy-start(bf16[4,192,1536]{2,1,0:T(8,128)(2,1)S(1)} %all-to-all-done) | copy-start | bytes 7077892
  201.2 70.3 %all-to-all-start.3 = ((bf16[4,184,1536]{2,1,0:T(8,128)(2,1)}), bf16[4,184,1536]{2,1,0:T(8,128)(2,1)}, u32[]{:S(2)}, u32[]{:S(2)}) async-start(bf16[4,184,1536]{2,1,0:T(8,128)(2,1)} %bitcast.17), calls=%async_computation.3 | async-start | bytes 4521984 | tf_op jit(solution)/shard_map/all_to_all | solution.py:326
  232.3 11.8 %copy-start.65 = (bf16[768,3072]{1,0:T(8,128)(2,1)}, bf16[768,3072]{1,0:T(8,128)(2,1)S(1)}, u32[]{:S(2)}) copy-start(bf16[768,3072]{1,0:T(8,128)(2,1)S(1)} %get-tuple-element.85) | copy-start | bytes 14155780
  244.1 8.2 %copy-start.19 = (bf16[768,3072]{1,0:T(8,128)(2,1)}, bf16[768,3072]{1,0:T(8,128)(2,1)S(1)}, u32[]{:S(2)}) copy-start(bf16[768,3072]{1,0:T(8,128)(2,1)S(1)} %fusion.6) | copy-start | bytes 14155780
  271.5 5.2 %copy-start.23 = (bf16[4,184,1536]{2,1,0:T(8,128)(2,1)S(1)}, bf16[4,184,1536]{2,1,0:T(8,128)(2,1)}, u32[]{:S(2)}) copy-start(bf16[4,184,1536]{2,1,0:T(8,128)(2,1)} %copy-done.22) | copy-start | bytes 6782980
  271.5 58.2 %all-to-all-start.1 = ((bf16[4,192,1536]{2,1,0:T(8,128)(2,1)}), bf16[4,192,1536]{2,1,0:T(8,128)(2,1)}, u32[]{:S(2)}, u32[]{:S(2)}) async-start(bf16[4,192,1536]{2,1,0:T(8,128)(2,1)} %bitcast.12), calls=%async_computation.1 | async-start | bytes 4718592 | tf_op jit(solution)/shard_map/all_to_all | solution.py:326
  276.7 182.1 %reduce-scatter.2.cloned.1.call-start = ((), (), s32[]{:S(2)}) async-start(), calls=%async_computation.7 | async-start | bytes 10616832 | tf_op jit(solution)/shard_map/reduce_scatter | solution.py:332
  286.8 8.7 %copy-start.17 = (bf16[4,192,1536]{2,1,0:T(8,128)(2,1)S(1)}, bf16[4,192,1536]{2,1,0:T(8,128)(2,1)}, u32[]{:S(2)}) copy-start(bf16[4,192,1536]{2,1,0:T(8,128)(2,1)} %copy-done.16) | copy-start | bytes 7077892
  295.4 5.9 %copy-start.24 = (bf16[4,184,1536]{2,1,0:T(8,128)(2,1)S(1)}, bf16[4,184,1536]{2,1,0:T(8,128)(2,1)}, u32[]{:S(2)}) copy-start(bf16[4,184,1536]{2,1,0:T(8,128)(2,1)} %copy-done.22) | copy-start | bytes 6782980
  318.7 5.5 %copy-start.30 = (pred[1504,591]{1,0:T(32,128)(4,1)S(1)}, pred[1504,591]{1,0:T(32,128)(4,1)}, u32[]{:S(2)}) copy-start(pred[1504,591]{1,0:T(32,128)(4,1)} %get-tuple-element.114) | copy-start | bytes 2666596
  329.6 6.0 %copy-start.64 = (f32[591,1536]{1,0:T(8,128)S(1)}, f32[591,1536]{1,0:T(8,128)}, u32[]{:S(2)}) copy-start(f32[591,1536]{1,0:T(8,128)} %fusion.54) | copy-start | bytes 10893316
  372.1 6.0 %slice-start.5 = ((s8[4915200]{0:T(1024)(128)(4,1)}), s8[4194304]{0:T(1024)(128)(4,1)S(1)}, s32[]{:S(2)}) async-start(s8[4915200]{0:T(1024)(128)(4,1)} %bitcast.260), calls=%async_computation.13 | async-start | bytes 8388608
  373.2 4.9 %slice-start.6 = ((s8[4915200]{0:T(1024)(128)(4,1)}), s8[720896]{0:T(1024)(128)(4,1)S(1)}, s32[]{:S(2)}) async-start(s8[4915200]{0:T(1024)(128)(4,1)} %bitcast.260), calls=%async_computation.14 | async-start | bytes 1441792
  385.0 8.3 %slice-start = ((s8[7077888]{0:T(1024)(128)(4,1)}), s8[2883584]{0:T(1024)(128)(4,1)S(1)}, s32[]{:S(2)}) async-start(s8[7077888]{0:T(1024)(128)(4,1)} %bitcast.223), calls=%async_computation.8 | async-start | bytes 5767168
  388.1 4.1 copy-start.33
  388.1 4.1 copy-start.35
  388.1 5.3 %slice-start.1 = ((s8[7077888]{0:T(1024)(128)(4,1)}), s8[4194304]{0:T(1024)(128)(4,1)S(1)}, s32[]{:S(2)}) async-start(s8[7077888]{0:T(1024)(128)(4,1)} %bitcast.223), calls=%async_computation.9 | async-start | bytes 8388608
  392.1 6.0 %collective-permute-start.9 = (bf16[2,2,96,1024]{3,2,1,0:T(8,128)(2,1)S(1)}, bf16[2,2,96,1024]{3,2,1,0:T(8,128)(2,1)S(1)}, u32[]{:S(2)}, u32[]{:S(2)}) collective-permute-start(bf16[2,2,96,1024]{3,2,1,0:T(8,128)(2,1)S(1)} %fusion.77), channel_id=1, source_target_pairs={{0,1},{1,0},{2,3},{3,2},{4,5},{5,4},{6,7},{7,6},{8,9},{9,8},{10,11... | collective-permute-start | bytes 2359304 | tf_op jit(solution)/shard_map/ppermute | solution.py:124
  393.7 9.6 %collective-permute-start.18 = (bf16[2,2,96,1152]{3,2,1,0:T(8,128)(2,1)S(1)}, bf16[2,2,96,1152]{3,2,1,0:T(8,128)(2,1)S(1)}, u32[]{:S(2)}, u32[]{:S(2)}) collective-permute-start(bf16[2,2,96,1152]{3,2,1,0:T(8,128)(2,1)S(1)} %fusion.76), channel_id=1, source_target_pairs={{0,1},{1,0},{2,3},{3,2},{4,5},{5,4},{6,7},{7,6},{8,9},{9,8},{10,11... | collective-permute-start | bytes 2654216 | tf_op jit(solution)/shard_map/ppermute | solution.py:124
  394.4 6.9 %collective-permute-start = (bf16[2,2,96,1024]{3,2,1,0:T(8,128)(2,1)S(1)}, bf16[2,2,96,1024]{3,2,1,0:T(8,128)(2,1)S(1)}, u32[]{:S(2)}, u32[]{:S(2)}) collective-permute-start(bf16[2,2,96,1024]{3,2,1,0:T(8,128)(2,1)S(1)} %fusion.78), channel_id=1, source_target_pairs={{0,1},{1,0},{2,3},{3,2},{4,5},{5,4},{6,7},{7,6},{8,9},{9,8},{10,11... | collective-permute-start | bytes 2359304 | tf_op jit(solution)/shard_map/ppermute | solution.py:124
  398.6 7.8 %collective-permute-start.12 = (bf16[2,96,512]{2,1,0:T(8,128)(2,1)S(1)}, bf16[2,96,512]{2,1,0:T(8,128)(2,1)S(1)}, u32[]{:S(2)}, u32[]{:S(2)}) collective-permute-start(bf16[2,96,512]{2,1,0:T(8,128)(2,1)S(1)} %fusion.83), channel_id=1, source_target_pairs={{0,4},{1,5},{2,6},{3,7},{4,0},{5,1},{6,2},{7,3},{8,12},{9,13},{10,... | collective-permute-start | bytes 589832 | tf_op jit(solution)/shard_map/ppermute | solution.py:124
  400.1 8.0 %collective-permute-start.10 = (bf16[2,96,512]{2,1,0:T(8,128)(2,1)S(1)}, bf16[2,96,512]{2,1,0:T(8,128)(2,1)S(1)}, u32[]{:S(2)}, u32[]{:S(2)}) collective-permute-start(bf16[2,96,512]{2,1,0:T(8,128)(2,1)S(1)} %fusion.82), channel_id=1, source_target_pairs={{0,2},{1,3},{2,0},{3,1},{4,6},{5,7},{6,4},{7,5},{8,10},{9,11},{10,... | collective-permute-start | bytes 589832 | tf_op jit(solution)/shard_map/ppermute | solution.py:124
  401.7 8.9 %collective-permute-start.3 = (bf16[2,96,512]{2,1,0:T(8,128)(2,1)S(1)}, bf16[2,96,512]{2,1,0:T(8,128)(2,1)S(1)}, u32[]{:S(2)}, u32[]{:S(2)}) collective-permute-start(bf16[2,96,512]{2,1,0:T(8,128)(2,1)S(1)} %fusion.81), channel_id=1, source_target_pairs={{0,4},{1,5},{2,6},{3,7},{4,0},{5,1},{6,2},{7,3},{8,12},{9,13},{10,... | collective-permute-start | bytes 589832 | tf_op jit(solution)/shard_map/ppermute | solution.py:124
  402.9 9.2 %collective-permute-start.1 = (bf16[2,96,512]{2,1,0:T(8,128)(2,1)S(1)}, bf16[2,96,512]{2,1,0:T(8,128)(2,1)S(1)}, u32[]{:S(2)}, u32[]{:S(2)}) collective-permute-start(bf16[2,96,512]{2,1,0:T(8,128)(2,1)S(1)} %fusion.80), channel_id=1, source_target_pairs={{0,2},{1,3},{2,0},{3,1},{4,6},{5,7},{6,4},{7,5},{8,10},{9,11},{10,... | collective-permute-start | bytes 589832 | tf_op jit(solution)/shard_map/ppermute | solution.py:124
  403.8 19.8 %collective-permute-start.21 = (bf16[2,96,640]{2,1,0:T(8,128)(2,1)S(1)}, bf16[2,96,640]{2,1,0:T(8,128)(2,1)S(1)}, u32[]{:S(2)}, u32[]{:S(2)}) collective-permute-start(bf16[2,96,640]{2,1,0:T(8,128)(2,1)S(1)} %fusion.79), channel_id=1, source_target_pairs={{0,4},{1,5},{2,6},{3,7},{4,0},{5,1},{6,2},{7,3},{8,12},{9,13},{10,... | collective-permute-start | bytes 737288 | tf_op jit(solution)/shard_map/ppermute | solution.py:124
  406.4 9.9 %collective-permute-start.19 = (bf16[2,96,512]{2,1,0:T(8,128)(2,1)S(1)}, bf16[2,96,512]{2,1,0:T(8,128)(2,1)S(1)}, u32[]{:S(2)}, u32[]{:S(2)}) collective-permute-start(bf16[2,96,512]{2,1,0:T(8,128)(2,1)S(1)} %fusion.84), channel_id=1, source_target_pairs={{0,2},{1,3},{2,0},{3,1},{4,6},{5,7},{6,4},{7,5},{8,10},{9,11},{10,... | collective-permute-start | bytes 589832 | tf_op jit(solution)/shard_map/ppermute | solution.py:124
  408.1 10.3 %collective-permute-start.13 = (bf16[96,512]{1,0:T(8,128)(2,1)S(1)}, bf16[96,512]{1,0:T(8,128)(2,1)S(1)}, u32[]{:S(2)}, u32[]{:S(2)}) collective-permute-start(bf16[96,512]{1,0:T(8,128)(2,1)S(1)} %fusion.95), channel_id=1, source_target_pairs={{0,2},{1,3},{2,0},{3,1},{4,6},{5,7},{6,4},{7,5},{8,10},{9,11},{10,... | collective-permute-start | bytes 294920 | tf_op jit(solution)/shard_map/ppermute | solution.py:124
  410.6 8.5 %collective-permute-start.11 = (bf16[96,512]{1,0:T(8,128)(2,1)S(1)}, bf16[96,512]{1,0:T(8,128)(2,1)S(1)}, u32[]{:S(2)}, u32[]{:S(2)}) collective-permute-start(bf16[96,512]{1,0:T(8,128)(2,1)S(1)} %fusion.94), channel_id=1, source_target_pairs={{0,4},{1,5},{2,6},{3,7},{4,0},{5,1},{6,2},{7,3},{8,12},{9,13},{10,... | collective-permute-start | bytes 294920 | tf_op jit(solution)/shard_map/ppermute | solution.py:124
  412.1 9.2 %collective-permute-start.4 = (bf16[96,512]{1,0:T(8,128)(2,1)S(1)}, bf16[96,512]{1,0:T(8,128)(2,1)S(1)}, u32[]{:S(2)}, u32[]{:S(2)}) collective-permute-start(bf16[96,512]{1,0:T(8,128)(2,1)S(1)} %fusion.92), channel_id=1, source_target_pairs={{0,2},{1,3},{2,0},{3,1},{4,6},{5,7},{6,4},{7,5},{8,10},{9,11},{10,... | collective-permute-start | bytes 294920 | tf_op jit(solution)/shard_map/ppermute | solution.py:124
  416.3 5.3 %collective-permute-start.2 = (bf16[96,512]{1,0:T(8,128)(2,1)S(1)}, bf16[96,512]{1,0:T(8,128)(2,1)S(1)}, u32[]{:S(2)}, u32[]{:S(2)}) collective-permute-start(bf16[96,512]{1,0:T(8,128)(2,1)S(1)} %fusion.91), channel_id=1, source_target_pairs={{0,4},{1,5},{2,6},{3,7},{4,0},{5,1},{6,2},{7,3},{8,12},{9,13},{10,... | collective-permute-start | bytes 294920 | tf_op jit(solution)/shard_map/ppermute | solution.py:124
  418.4 6.2 %collective-permute-start.20 = (bf16[96,512]{1,0:T(8,128)(2,1)S(1)}, bf16[96,512]{1,0:T(8,128)(2,1)S(1)}, u32[]{:S(2)}, u32[]{:S(2)}) collective-permute-start(bf16[96,512]{1,0:T(8,128)(2,1)S(1)} %fusion.96), channel_id=1, source_target_pairs={{0,4},{1,5},{2,6},{3,7},{4,0},{5,1},{6,2},{7,3},{8,12},{9,13},{10,... | collective-permute-start | bytes 294920 | tf_op jit(solution)/shard_map/ppermute | solution.py:124
  419.2 5.5 %collective-permute-start.14 = (bf16[2,24,1024]{2,1,0:T(8,128)(2,1)S(1)}, bf16[2,24,1024]{2,1,0:T(8,128)(2,1)S(1)}, u32[]{:S(2)}, u32[]{:S(2)}) collective-permute-start(bf16[2,24,1024]{2,1,0:T(8,128)(2,1)S(1)} %fusion.97), channel_id=1, source_target_pairs={{0,8},{8,0},{16,24},{24,16},{1,9},{9,1},{17,25},{25,17},{2,10},{10... | collective-permute-start | bytes 294920 | tf_op jit(solution)/shard_map/ppermute | solution.py:124
  421.7 5.5 %collective-permute-start.5 = (bf16[2,24,1024]{2,1,0:T(8,128)(2,1)S(1)}, bf16[2,24,1024]{2,1,0:T(8,128)(2,1)S(1)}, u32[]{:S(2)}, u32[]{:S(2)}) collective-permute-start(bf16[2,24,1024]{2,1,0:T(8,128)(2,1)S(1)} %fusion.93), channel_id=1, source_target_pairs={{0,8},{8,0},{16,24},{24,16},{1,9},{9,1},{17,25},{25,17},{2,10},{10... | collective-permute-start | bytes 294920 | tf_op jit(solution)/shard_map/ppermute | solution.py:124
  423.6 11.0 %collective-permute-start.22 = (bf16[96,640]{1,0:T(8,128)(2,1)S(1)}, bf16[96,640]{1,0:T(8,128)(2,1)S(1)}, u32[]{:S(2)}, u32[]{:S(2)}) collective-permute-start(bf16[96,640]{1,0:T(8,128)(2,1)S(1)} %fusion.88), channel_id=1, source_target_pairs={{0,2},{1,3},{2,0},{3,1},{4,6},{5,7},{6,4},{7,5},{8,10},{9,11},{10,... | collective-permute-start | bytes 368648 | tf_op jit(solution)/shard_map/ppermute | solution.py:124
  424.7 6.4 %collective-permute-start.15 = (bf16[24,1024]{1,0:T(8,128)(2,1)S(1)}, bf16[24,1024]{1,0:T(8,128)(2,1)S(1)}, u32[]{:S(2)}, u32[]{:S(2)}) collective-permute-start(bf16[24,1024]{1,0:T(8,128)(2,1)S(1)} %fusion.102), channel_id=1, source_target_pairs={{0,16},{8,24},{16,0},{24,8},{1,17},{9,25},{17,1},{25,9},{2,18},{10... | collective-permute-start | bytes 147464 | tf_op jit(solution)/shard_map/ppermute | solution.py:124
  427.2 6.7 %collective-permute-start.6 = (bf16[24,1024]{1,0:T(8,128)(2,1)S(1)}, bf16[24,1024]{1,0:T(8,128)(2,1)S(1)}, u32[]{:S(2)}, u32[]{:S(2)}) collective-permute-start(bf16[24,1024]{1,0:T(8,128)(2,1)S(1)} %fusion.101), channel_id=1, source_target_pairs={{0,16},{8,24},{16,0},{24,8},{1,17},{9,25},{17,1},{25,9},{2,18},{10... | collective-permute-start | bytes 147464 | tf_op jit(solution)/shard_map/ppermute | solution.py:124
  431.1 6.2 %collective-permute-start.16 = (bf16[24,1024]{1,0:T(8,128)(2,1)S(1)}, bf16[24,1024]{1,0:T(8,128)(2,1)S(1)}, u32[]{:S(2)}, u32[]{:S(2)}) collective-permute-start(bf16[24,1024]{1,0:T(8,128)(2,1)S(1)} %fusion.98), channel_id=1, source_target_pairs={{0,16},{8,24},{16,0},{24,8},{1,17},{9,25},{17,1},{25,9},{2,18},{10... | collective-permute-start | bytes 147464 | tf_op jit(solution)/shard_map/ppermute | solution.py:148
  433.9 6.4 %collective-permute-start.7 = (bf16[24,1024]{1,0:T(8,128)(2,1)S(1)}, bf16[24,1024]{1,0:T(8,128)(2,1)S(1)}, u32[]{:S(2)}, u32[]{:S(2)}) collective-permute-start(bf16[24,1024]{1,0:T(8,128)(2,1)S(1)} %fusion.99), channel_id=1, source_target_pairs={{0,16},{8,24},{16,0},{24,8},{1,17},{9,25},{17,1},{25,9},{2,18},{10... | collective-permute-start | bytes 147464 | tf_op jit(solution)/shard_map/ppermute | solution.py:148
  434.7 5.7 %collective-permute-start.23 = (bf16[2,24,1152]{2,1,0:T(8,128)(2,1)S(1)}, bf16[2,24,1152]{2,1,0:T(8,128)(2,1)S(1)}, u32[]{:S(2)}, u32[]{:S(2)}) collective-permute-start(bf16[2,24,1152]{2,1,0:T(8,128)(2,1)S(1)} %fusion.89), channel_id=1, source_target_pairs={{0,8},{8,0},{16,24},{24,16},{1,9},{9,1},{17,25},{25,17},{2,10},{10... | collective-permute-start | bytes 331784 | tf_op jit(solution)/shard_map/ppermute | solution.py:124
  437.4 5.7 %collective-permute-start.17 = (bf16[2,24,1024]{2,1,0:T(8,128)(2,1)S(1)}, bf16[2,24,1024]{2,1,0:T(8,128)(2,1)S(1)}, u32[]{:S(2)}, u32[]{:S(2)}) collective-permute-start(bf16[2,24,1024]{2,1,0:T(8,128)(2,1)S(1)} %pad_maximum_fusion.14), channel_id=1, source_target_pairs={{0,8},{8,0},{16,24},{24,16},{1,9},{9,1},{17,25},{25,17},{2,10},{10... | collective-permute-start | bytes 294920 | tf_op jit(solution)/shard_map/ppermute | solution.py:148
  440.3 4.7 collective-permute-start.8
  440.5 5.1 %collective-permute-start.24 = (bf16[24,1152]{1,0:T(8,128)(2,1)S(1)}, bf16[24,1152]{1,0:T(8,128)(2,1)S(1)}, u32[]{:S(2)}, u32[]{:S(2)}) collective-permute-start(bf16[24,1152]{1,0:T(8,128)(2,1)S(1)} %fusion.100), channel_id=1, source_target_pairs={{0,16},{8,24},{16,0},{24,8},{1,17},{9,25},{17,1},{25,9},{2,18},{10... | collective-permute-start | bytes 165896 | tf_op jit(solution)/shard_map/ppermute | solution.py:124
  445.6 5.1 %collective-permute-start.25 = (bf16[24,1152]{1,0:T(8,128)(2,1)S(1)}, bf16[24,1152]{1,0:T(8,128)(2,1)S(1)}, u32[]{:S(2)}, u32[]{:S(2)}) collective-permute-start(bf16[24,1152]{1,0:T(8,128)(2,1)S(1)} %fusion.90), channel_id=1, source_target_pairs={{0,16},{8,24},{16,0},{24,8},{1,17},{9,25},{17,1},{25,9},{2,18},{10... | collective-permute-start | bytes 165896 | tf_op jit(solution)/shard_map/ppermute | solution.py:148
  450.8 4.8 %collective-permute-start.26 = (bf16[2,24,1152]{2,1,0:T(8,128)(2,1)S(1)}, bf16[2,24,1152]{2,1,0:T(8,128)(2,1)S(1)}, u32[]{:S(2)}, u32[]{:S(2)}) collective-permute-start(bf16[2,24,1152]{2,1,0:T(8,128)(2,1)S(1)} %pad_maximum_fusion.12), channel_id=1, source_target_pairs={{0,8},{8,0},{16,24},{24,16},{1,9},{9,1},{17,25},{25,17},{2,10},{10... | collective-permute-start | bytes 331784 | tf_op jit(solution)/shard_map/ppermute | solution.py:148
  (44 other events, 99.5 us)
Sparse Core Ops, SparseCore 0:
  11.7 42.3 all-gather.2
  56.5 58.6 all-gather.4
  317.6 77.1 reduce-scatter.1

commit v19 on v9

--- a/solution.py
+++ b/solution.py
@@ -139,6 +139,17 @@
     return jnp.concatenate([first, second], axis=-1)
 
 
+def expert_all_reduce_doubling(values, axis_name):
+    size = lax.axis_size(axis_name)
+    n_bits = size.bit_length() - 1
+    total = values.astype(jnp.bfloat16)
+    for bit in range(n_bits):
+        pairs = [(i, i ^ (1 << bit)) for i in range(size)]
+        got = lax.ppermute(total, axis_name, pairs)
+        total = (total.astype(jnp.float32) + got.astype(jnp.float32)).astype(jnp.bfloat16)
+    return total.astype(jnp.float32)
+
+
 def layer_norm(values, norm_gain):
     row_mean = jnp.mean(values, axis=-1, keepdims=True)
     centered = values - row_mean
@@ -221,9 +232,8 @@
     slot_index = jnp.sum(before * flat_picks, axis=1).reshape(rows, 2)
     position = jnp.where(live_int[:, None] > 0, routes * capacity + slot_index, overflow)
 
-    n_chunks = 2
-    part_cap = 8 * ((capacity + 8 * n_chunks - 1) // (8 * n_chunks))
-    chunk_sizes = [min(part_cap, capacity - k * part_cap) for k in range(n_chunks)]
+    first_cap = min(capacity, 8 * round(capacity * 0.47 / 8))
+    chunk_sizes = [first_cap, capacity - first_cap]
     chunk_sizes = [size for size in chunk_sizes if size > 0]
     chunk_starts = [sum(chunk_sizes[:k]) for k in range(len(chunk_sizes))]
     slot_ids = jnp.concatenate(
@@ -367,8 +377,18 @@
     )
     small = jnp.pad(small, ((0, 0), (0, 128 - small.shape[1])))
     dense_grads = jnp.concatenate([grad_qkv, grad_wout, small], axis=1)
-    dense_share = shard_reduce_scatter(dense_grads, "shard", 128 * (dense_grads.shape[1] // 256))
-    dense_total = lax.psum(dense_share.astype(jnp.bfloat16), "expert").astype(jnp.float32)
+    n_parts = 3
+    bounds = [128 * (dense_grads.shape[1] * k // (128 * n_parts)) for k in range(n_parts)]
+    bounds = bounds + [dense_grads.shape[1]]
+    dense_total = jnp.concatenate(
+        [
+            expert_all_reduce_doubling(
+                shard_reduce_scatter(part, "shard", 128 * (part.shape[1] // 256)), "expert"
+            )
+            for part in (dense_grads[:, low:high] for low, high in zip(bounds[:-1], bounds[1:]))
+        ],
+        axis=1,
+    )
     return (
         output,
         grad_tokens,

time: 575 us -> 479 us (0.83)
  waiting for transfers between devices: 209 us -> 108 us
  starting transfers between devices: 24.1 us -> 39.8 us
  local copies, waits for them, and re-layouts: 54.1 us -> 47.9 us
    reduce_scatter x1, waiting for transfers between devices: 72.9 us -> 0.01 us  [shards(): lax.psum_scatter(expert_grads, 'shard', scatter_dimension=1, tiled=True)]
    all_to_all x2, waiting for transfers between devices: 41.9 us -> 0.01 us  [shards(): lax.all_to_all(returning, 'expert', split_axis=0, concat_axis=0, tiled=True)]
    ppermute x0 -> x6, waiting for transfers between devices: none -> 22.9 us  [expert_all_reduce_doubling(): got = lax.ppermute(total, axis_name, pairs)]
    all_to_all x2, waiting for transfers between devices: 23 us -> 41.8 us  [shards(): lax.all_to_all(dispatch_rows(experts * start, experts * (start + size)).r...]
    all_gather x1, waiting for transfers between devices: 13.7 us -> 0.02 us  [shards(): expert_full = lax.all_gather(expert_local, 'shard', axis=1, tiled=True)]
    ppermute x5 -> x15, starting transfers between devices: 5.14 us -> 13.5 us  [_exchange(): got = lax.ppermute(send.astype(jnp.bfloat16), axis_name, pairs)]
    ppermute x5 -> x15, waiting for transfers between devices: 21.6 us -> 14 us  [_exchange(): got = lax.ppermute(send.astype(jnp.bfloat16), axis_name, pairs)]
    ppermute x0 -> x6, starting transfers between devices: none -> 7.45 us  [expert_all_reduce_doubling(): got = lax.ppermute(total, axis_name, pairs)]
  transfers between devices with their start and end apart: 13 -> 28, of which waited for: 11 -> 11; matrix products, arithmetic and copies ran while one was open for 41% -> 54% of each run, Pallas kernels for 2% -> 7%
where the time goes in v19:
time: 479 us; the launch traced here: 471 us
  matrix products  185 us (39%)
  waiting for transfers between devices  108 us (23%)
  local copies, waits for them, and re-layouts  47.9 us (10%)
  starting transfers between devices  39.8 us (8%)
  other arithmetic  39.1 us (8%)
  Pallas kernels  35 us (7%)
  between operations  16.5 us (3%)
    dot_general x2, matrix products, shards(): jnp.dot(flat_arrived, expert_first, preferred_element_type=jnp.float32)  52.8 us
    all_to_all x2, waiting for transfers between devices, shards(): lax.all_to_all(dispatch_rows(experts * start, experts * (start + size)).r...  41.8 us
    all_gather x1, waiting for transfers between devices, shards(): dense_full = lax.all_gather(dense_local, 'shard', axis=0, tiled=True)  29 us
    ppermute x6, waiting for transfers between devices, expert_all_reduce_doubling(): got = lax.ppermute(total, axis_name, pairs)  22.9 us
    pallas_call x1, Pallas kernels, attention_bwd(): pl.pallas_call(functools.partial(attn_bwd_kernel, images=images), grid=(p...  21.6 us
    dot_general x2, matrix products, shards(): lax.dot_general(flat_grad, expert_second, COL_CONTRACT, preferred_element...  18.8 us
    dot_general x2, matrix products, shards(): lax.dot_general(activated, flat_grad, ROW_CONTRACT, preferred_element_typ...  17.7 us
    dot_general x2, matrix products, shards(): lax.dot_general(flat_arrived, pre_grad, ROW_CONTRACT, preferred_element_t...  15.6 us
  transfers between devices with their start and end apart: 28, of which 11 were waited for; matrix products, arithmetic and copies ran while one was open for 54% of the time, Pallas kernels for 7%

profile of v19, /device:TPU:0, one launch (start us, length us, event | category | flops | bytes accessed | tf_op | source)
XLA Modules:
  0.0 470.7 jit_solution(3226330978113600831)
XLA Ops:
  9.6 1.9 concatenate.58
  11.6 1.5 stack_reshape_squeeze.3
  13.2 2.3 pad_maximum_fusion.6
  21.7 3.4 fusion.123
  25.0 29.0 %all-gather.3.cloned.1.call-done = bf16[768,3078]{1,0:T(8,128)(2,1)} async-done(((bf16[96,3078]{1,0:T(8,128)(2,1)}), bf16[768,3078]{1,0:T(8,128)(2,1)}) %all-gather.3.cloned.1.call-update) | async-done | bytes 4727824 | tf_op jit(solution)/shard_map/all_gather | solution.py:201
  55.8 4.6 convolution_convert_fusion
  60.6 13.4 %shard_map.178 = bf16[640,768]{1,0:T(8,128)(2,1)S(1)} custom-call(bf16[640,2304]{1,0:T(8,128)(2,1)S(1)} %pad.18.q_ref.k_ref.v_ref, bf16[640,2304]{1,0:T(8,128)(2,1)S(1)} %pad.18.q_ref.k_ref.v_ref, bf16[640,2304]{1,0:T(8,128)(2,1)S(1)} %pad.18.q_ref.k_ref.v_ref), custom_call_target="tpu_custom_call" | custom-call | tf_op jit(solution)/shard_map/pallas_call | solution.py:90
  74.1 2.6 fusion.132
  78.3 1.5 fusion.133
  80.7 2.6 fusion.60
  83.4 2.2 convolution_convert_fusion.4
  85.6 2.3 add_convert_fusion.3
  87.9 1.5 pad_maximum_fusion.4
  89.4 4.6 all-to-all-start
  94.6 3.0 fusion.52
  100.7 1.6 pad_maximum_fusion.2
  102.3 41.8 %all-to-all-done = bf16[4,176,1536]{2,1,0:T(8,128)(2,1)S(1)} async-done(((bf16[4,176,1536]{2,1,0:T(8,128)(2,1)}), bf16[4,176,1536]{2,1,0:T(8,128)(2,1)S(1)}, u32[]{:S(2)}, u32[]{:S(2)}) %all-to-all-start) | async-done | bytes 2162720 | tf_op jit(solution)/shard_map/all_to_all | solution.py:269
  145.4 3.8 all-to-all-start.2
  149.2 25.1 %multiply_convert_fusion.1 = (bf16[704,3072]{1,0:T(8,128)(2,1)}, f32[704,3072]{1,0:T(8,128)}, f32[704,3072]{1,0:T(8,128)}) fusion(bf16[2,768,3072]{2,1,0:T(8,128)(2,1)} %all-gather.5.cloned.1.call-done, bf16[704,1536]{1,0:T(8,128)(2,1)} %bitcast.189), kind=kOutput, calls=%fused_computation.36 | convolution fusion | flops 3462463488 | bytes 27426816 | tf_op jit(solution)/shard_map/dot_general | solution.py:283
  174.4 2.5 slice.223
  176.9 8.5 %reshape_squeeze.3 = bf16[3072,768]{1,0:T(8,128)(2,1)} reshape(bf16[1,768,3072]{2,1,0:T(8,128)(2,1)} %slice.223) | data formatting | bytes 9437184 | tf_op jit(solution)/shard_map/reshape;squeeze | solution.py:214
  185.3 7.3 %convolution_convert_fusion.3 = bf16[704,768]{1,0:T(8,128)(2,1)S(1)} fusion(bf16[704,3072]{1,0:T(8,128)(2,1)} %get-tuple-element.96, bf16[3072,768]{1,0:T(8,128)(2,1)} %reshape_squeeze.3), kind=kOutput, calls=%fused_computation.120 | convolution fusion | flops 3322429440 | bytes 10125312 | tf_op jit(solution)/shard_map/dot_general | solution.py:287
  192.6 8.2 %fusion.19 = bf16[704,3072]{1,0:T(8,128)(2,1)S(1)} fusion(f32[704,3072]{1,0:T(8,128)} %get-tuple-element.117, f32[704,3072]{1,0:T(8,128)} %get-tuple-element.97, bf16[3072,768]{1,0:T(8,128)(2,1)S(1)} %copy-done.25, bf16[704,1536]{1,0:T(8,128)(2,1)S(1)} %bitcast.191), kind=kOutput, calls=%fused_computation.35 | convolution fusion | flops 3339190272 | bytes 27426816 | tf_op jit(solution)/shard_map/dot_general | solution.py:280
  200.9 7.4 %fusion.54 = bf16[704,768]{1,0:T(8,128)(2,1)S(1)} fusion(bf16[704,3072]{1,0:T(8,128)(2,1)S(1)} %fusion.19, bf16[2,768,3072]{2,1,0:T(8,128)(2,1)} %all-gather.5.cloned.1.call-done), kind=kOutput, calls=%fused_computation.119 | convolution fusion | flops 3322429440 | bytes 10125312 | tf_op jit(solution)/shard_map/dot_general | solution.py:290
  209.9 5.3 %all-to-all-start.1 = ((bf16[4,176,1536]{2,1,0:T(8,128)(2,1)}), bf16[4,176,1536]{2,1,0:T(8,128)(2,1)}, u32[]{:S(2)}, u32[]{:S(2)}) async-start(bf16[4,176,1536]{2,1,0:T(8,128)(2,1)} %bitcast.10), calls=%async_computation.1 | async-start | bytes 4325376 | tf_op jit(solution)/shard_map/all_to_all | solution.py:305
  215.2 27.6 %multiply_convert_fusion = (bf16[800,3072]{1,0:T(8,128)(2,1)}, f32[800,3072]{1,0:T(8,128)}, f32[800,3072]{1,0:T(8,128)}) fusion(bf16[2,768,3072]{2,1,0:T(8,128)(2,1)} %all-gather.5.cloned.1.call-done, bf16[800,1536]{1,0:T(8,128)(2,1)S(1)} %bitcast.185), kind=kOutput, calls=%fused_computation.11 | convolution fusion | flops 3934617600 | bytes 30523392 | tf_op jit(solution)/shard_map/dot_general | solution.py:283
  242.8 10.6 %fusion.6 = bf16[800,3072]{1,0:T(8,128)(2,1)S(1)} fusion(f32[800,3072]{1,0:T(8,128)} %get-tuple-element.118, f32[800,3072]{1,0:T(8,128)} %get-tuple-element.95, bf16[3072,768]{1,0:T(8,128)(2,1)} %reshape_squeeze.3, bf16[800,1536]{1,0:T(8,128)(2,1)S(1)} %bitcast.186), kind=kOutput, calls=%fused_computation.10 | convolution fusion | flops 3794534400 | bytes 30523392 | tf_op jit(solution)/shard_map/dot_general | solution.py:280
  253.4 8.2 %convolution_convert_fusion.1 = bf16[800,768]{1,0:T(8,128)(2,1)S(1)} fusion(bf16[800,3072]{1,0:T(8,128)(2,1)} %get-tuple-element.94, bf16[3072,768]{1,0:T(8,128)(2,1)S(1)} %copy-done.26), kind=kOutput, calls=%fused_computation.112 | convolution fusion | flops 3775488000 | bytes 10862592 | tf_op jit(solution)/shard_map/dot_general | solution.py:287
  261.6 4.0 fusion.48
  265.6 1.6 pad_maximum_fusion.3
  268.1 6.7 %fusion.72 = f32[3072,768]{1,0:T(8,128)} fusion(bf16[704,3072]{1,0:T(8,128)(2,1)S(1)} %bitcast.204, bf16[704,1536]{1,0:T(8,128)(2,1)S(1)} %bitcast.192), kind=kOutput, calls=%fused_computation.142 | convolution fusion | flops 3321888768 | bytes 14843904 | tf_op jit(solution)/shard_map/dot_general | solution.py:293
  274.8 5.1 %all-to-all-start.3 = ((bf16[4,200,1536]{2,1,0:T(8,128)(2,1)}), bf16[4,200,1536]{2,1,0:T(8,128)(2,1)}, u32[]{:S(2)}, u32[]{:S(2)}) async-start(bf16[4,200,1536]{2,1,0:T(8,128)(2,1)} %bitcast.15), calls=%async_computation.3 | async-start | bytes 4915200 | tf_op jit(solution)/shard_map/all_to_all | solution.py:305
  279.9 11.0 %add_convert_fusion = bf16[3072,768]{1,0:T(8,128)(2,1)} fusion(f32[3072,768]{1,0:T(8,128)} %fusion.72, bf16[800,3072]{1,0:T(8,128)(2,1)} %get-tuple-element.94, bf16[800,1536]{1,0:T(8,128)(2,1)S(1)} %bitcast.187), kind=kOutput, calls=%fused_computation.27 | convolution fusion | flops 3779592192 | bytes 20299776 | tf_op jit(solution)/shard_map/dot_general | solution.py:293
  290.9 8.5 %stack_reshape.4 = bf16[1,768,3072]{2,1,0:T(8,128)(2,1)} reshape(bf16[3072,768]{1,0:T(8,128)(2,1)} %add_convert_fusion) | data formatting | bytes 9437184 | tf_op jit(solution)/shard_map/stack;reshape | solution.py:308
  299.4 6.0 %fusion.75 = f32[768,3072]{1,0:T(8,128)S(1)} fusion(bf16[704,3072]{1,0:T(8,128)(2,1)} %copy-done.27, bf16[704,1536]{1,0:T(8,128)(2,1)} %bitcast.190), kind=kOutput, calls=%fused_computation.145 | convolution fusion | flops 3321888768 | bytes 14843904 | tf_op jit(solution)/shard_map/dot_general | solution.py:296
  305.4 9.6 %fusion.26 = bf16[1,768,3072]{2,1,0:T(8,128)(2,1)} fusion(f32[768,3072]{1,0:T(8,128)S(1)} %fusion.75, bf16[800,3072]{1,0:T(8,128)(2,1)} %copy-done.21, bf16[800,1536]{1,0:T(8,128)(2,1)S(1)} %bitcast.188), kind=kOutput, calls=%fused_computation.53 | convolution fusion | flops 3779592192 | bytes 20299776 | tf_op jit(solution)/shard_map/dot_general | solution.py:296
  315.0 8.3 %pad_maximum_fusion = bf16[2,768,3072]{2,1,0:T(8,128)(2,1)} fusion(bf16[1,768,3072]{2,1,0:T(8,128)(2,1)} %stack_reshape.4, bf16[1,768,3072]{2,1,0:T(8,128)(2,1)} %fusion.26), kind=kLoop, calls=%fused_computation.26 | loop fusion | flops 4718592 | bytes 18874368 | tf_op jit(solution)/shard_map/stack | solution.py:308
  324.4 5.5 %fusion.55 = f32[591,1536]{1,0:T(8,128)} fusion(bf16[704,1536]{1,0:T(8,128)(2,1)} %bitcast.11, pred[1504,591]{1,0:T(32,128)(4,1)S(1)} %copy-done.39), kind=kOutput, calls=%fused_computation.123 | convolution fusion | flops 1278148608 | bytes 6244352 | tf_op jit(solution)/shard_map/dot_general | solution.py:324
  329.9 5.4 %fusion.58 = f32[591,1536]{1,0:T(8,128)} fusion(bf16[704,1536]{1,0:T(8,128)(2,1)} %bitcast.11, pred[1504,591]{1,0:T(32,128)(4,1)S(1)} %copy-done.37), kind=kOutput, calls=%fused_computation.126 | convolution fusion | flops 1278148608 | bytes 6244352 | tf_op jit(solution)/shard_map/dot_general | solution.py:321
  335.3 6.6 %convolution_add_fusion = f32[591,1536]{1,0:T(8,128)S(1)} fusion(f32[591,1536]{1,0:T(8,128)} %fusion.55, bf16[800,1536]{1,0:T(8,128)(2,1)} %bitcast.16, pred[1504,591]{1,0:T(32,128)(4,1)S(1)} %copy-done.39), kind=kOutput, calls=%fused_computation.59 | convolution fusion | flops 1453349376 | bytes 10231808 | tf_op jit(solution)/shard_map/dot_general | solution.py:324
  341.9 4.3 convolution_add_fusion.1
  346.3 1.8 multiply_reduce_fusion.3
  351.7 21.6 %shard_map.179 = (bf16[640,768]{1,0:T(8,128)(2,1)S(1)}, bf16[640,768]{1,0:T(8,128)(2,1)S(1)}, bf16[640,768]{1,0:T(8,128)(2,1)S(1)}) custom-call(bf16[640,2304]{1,0:T(8,128)(2,1)} %copy-done, bf16[640,2304]{1,0:T(8,128)(2,1)} %copy-done, bf16[640,2304]{1,0:T(8,128)(2,1)} %copy-done, bf16[640,768]{1,0:T(8,128)(2,1)S(1)} %pad.20.g_ref), custom_call_target="tpu_custom_call" | custom-call | tf_op jit(solution)/shard_map/pallas_call | solution.py:106
  374.5 3.0 fusion.70
  378.5 2.1 copy-done.3
  381.8 1.5 fusion.84
  383.4 2.4 fusion.45
  387.7 2.3 fusion.80
  390.0 1.5 fusion.27
  392.4 2.0 add_convert_fusion.4
  394.4 1.6 bitcast_add_fusion.2
  396.3 1.7 collective-permute-start.1
  402.7 1.7 collective-permute-start.15
  406.9 1.7 collective-permute-done.8
  411.2 6.2 %collective-permute-done.2 = bf16[96,512]{1,0:T(8,128)(2,1)S(1)} collective-permute-done((bf16[96,512]{1,0:T(8,128)(2,1)S(1)}, bf16[96,512]{1,0:T(8,128)(2,1)S(1)}, u32[]{:S(2)}, u32[]{:S(2)}) %collective-permute-start.2) | collective-permute-done | bytes 98336 | tf_op jit(solution)/shard_map/ppermute | solution.py:122
  418.1 1.8 collective-permute-start.5
  419.9 2.1 collective-permute-done.11
  422.1 1.9 collective-permute-start.12
  426.0 2.8 collective-permute-done.16
  430.5 2.5 collective-permute-start.6
  433.7 14.0 %collective-permute-done.6 = bf16[96,1024]{1,0:T(8,128)(2,1)S(1)} collective-permute-done((bf16[96,1024]{1,0:T(8,128)(2,1)S(1)}, bf16[96,1024]{1,0:T(8,128)(2,1)S(1)}, u32[]{:S(2)}, u32[]{:S(2)}) %collective-permute-start.6) | collective-permute-done | bytes 196640 | tf_op jit(solution)/shard_map/ppermute | solution.py:148
  447.9 3.5 collective-permute-done.13
  451.5 5.3 %collective-permute-done.20 = bf16[96,1152]{1,0:T(8,128)(2,1)S(1)} collective-permute-done((bf16[96,1152]{1,0:T(8,128)(2,1)S(1)}, bf16[96,1152]{1,0:T(8,128)(2,1)S(1)}, u32[]{:S(2)}, u32[]{:S(2)}) %collective-permute-start.20) | collective-permute-done | bytes 221216 | tf_op jit(solution)/shard_map/ppermute | solution.py:148
  459.9 2.5 fusion.131
  (312 shorter events, 49.9 us)
Async XLA Ops:
  7.2 46.9 %all-gather.3.cloned.1.call-start = ((), (), s32[]{:S(2)}) async-start(), calls=%async_computation.5 | async-start | bytes 5529600 | tf_op jit(solution)/shard_map/all_gather | solution.py:201
  8.8 7.7 %copy-start.51 = (s32[591,2]{0,1:T(2,128)S(1)}, s32[591,2]{0,1:T(2,128)}, u32[]{:S(2)}) copy-start(s32[591,2]{0,1:T(2,128)} %param.13) | copy-start | bytes 14188
  11.6 7.9 %copy-start.6 = (bf16[591,768]{1,0:T(8,128)(2,1)S(1)}, bf16[591,768]{1,0:T(8,128)(2,1)}, u32[]{:S(2)}) copy-start(bf16[591,768]{1,0:T(8,128)(2,1)} %param.11) | copy-start | bytes 2723332
  11.6 137.6 %all-gather.5.cloned.1.call-start = ((), (), s32[]{:S(2)}) async-start(), calls=%async_computation.6 | async-start | bytes 10616832 | tf_op jit(solution)/shard_map/all_gather | solution.py:212
  13.2 7.0 %copy-start.10 = (bf16[591,768]{1,0:T(8,128)(2,1)S(1)}, bf16[591,768]{1,0:T(8,128)(2,1)}, u32[]{:S(2)}) copy-start(bf16[591,768]{1,0:T(8,128)(2,1)} %param.21) | copy-start | bytes 2723332
  19.4 60.5 %copy-start.41 = (f32[591]{0:T(1024)}, f32[591]{0:T(1024)S(1)}, u32[]{:S(2)}) copy-start(f32[591]{0:T(1024)S(1)} %fusion.120) | copy-start | bytes 7096
  19.7 35.7 %copy-start.49 = (f32[591]{0:T(1024)}, f32[591]{0:T(1024)S(1)}, u32[]{:S(2)}) copy-start(f32[591]{0:T(1024)S(1)} %broadcast_multiply_fusion.2) | copy-start | bytes 7096
  20.2 35.3 %copy-start.61 = (f32[591]{0:T(1024)}, f32[591]{0:T(1024)S(1)}, u32[]{:S(2)}) copy-start(f32[591]{0:T(1024)S(1)} %fusion.118) | copy-start | bytes 7096
  25.0 58.3 %copy-start.32 = (bf16[1504,591]{1,0:T(8,128)(2,1)}, bf16[1504,591]{1,0:T(8,128)(2,1)S(1)}, u32[]{:S(2)}) copy-start(bf16[1504,591]{1,0:T(8,128)(2,1)S(1)} %get-tuple-element.107) | copy-start | bytes 5333188
  55.4 5.0 %copy-start.59 = (f32[768]{0:T(1024)}, f32[768]{0:T(1024)S(1)}, u32[]{:S(2)}) copy-start(f32[768]{0:T(1024)S(1)} %get-tuple-element.79) | copy-start | bytes 9220
  55.4 22.3 %copy-start.53 = (f32[768]{0:T(1024)}, f32[768]{0:T(1024)S(1)}, u32[]{:S(2)}) copy-start(f32[768]{0:T(1024)S(1)} %get-tuple-element.78) | copy-start | bytes 9220
  55.8 4.6 copy-start.28
  60.6 13.4 %copy-start = (bf16[640,2304]{1,0:T(8,128)(2,1)}, bf16[640,2304]{1,0:T(8,128)(2,1)S(1)}, u32[]{:S(2)}) copy-start(bf16[640,2304]{1,0:T(8,128)(2,1)S(1)} %pad.18.q_ref.k_ref.v_ref) | copy-start | bytes 8847364
  78.2 19.4 %copy-start.16 = (bf16[591,768]{1,0:T(8,128)(2,1)}, bf16[591,768]{1,0:T(8,128)(2,1)S(1)}, u32[]{:S(2)}) copy-start(bf16[591,768]{1,0:T(8,128)(2,1)S(1)} %multiply_convert_fusion.4) | copy-start | bytes 2723332
  80.7 4.9 %copy-start.35 = (bf16[591,2,768]{2,0,1:T(8,128)(2,1)}, bf16[591,2,768]{2,0,1:T(8,128)(2,1)S(1)}, u32[]{:S(2)}) copy-start(bf16[591,2,768]{2,0,1:T(8,128)(2,1)S(1)} %multiply_convert_fusion.2) | copy-start | bytes 5446660
  89.4 54.6 %all-to-all-start = ((bf16[4,176,1536]{2,1,0:T(8,128)(2,1)}), bf16[4,176,1536]{2,1,0:T(8,128)(2,1)S(1)}, u32[]{:S(2)}, u32[]{:S(2)}) async-start(bf16[4,176,1536]{2,1,0:T(8,128)(2,1)} %pad_maximum_fusion.4), calls=%async_computation | async-start | bytes 4325376 | tf_op jit(solution)/shard_map/all_to_all | solution.py:269
  145.4 64.5 %all-to-all-start.2 = ((bf16[4,200,1536]{2,1,0:T(8,128)(2,1)}), bf16[4,200,1536]{2,1,0:T(8,128)(2,1)S(1)}, u32[]{:S(2)}, u32[]{:S(2)}) async-start(bf16[4,200,1536]{2,1,0:T(8,128)(2,1)} %pad_maximum_fusion.2), calls=%async_computation.2 | async-start | bytes 4915200 | tf_op jit(solution)/shard_map/all_to_all | solution.py:269
  149.2 25.2 %copy-start.30 = (bf16[2,768,3072]{2,1,0:T(8,128)(2,1)S(1)}, bf16[2,768,3072]{2,1,0:T(8,128)(2,1)}, u32[]{:S(2)}) copy-start(bf16[2,768,3072]{2,1,0:T(8,128)(2,1)} %all-gather.5.cloned.1.call-done) | copy-start | bytes 28311556
  185.3 7.3 %copy-start.23 = (bf16[4,176,1536]{2,1,0:T(8,128)(2,1)S(1)}, bf16[4,176,1536]{2,1,0:T(8,128)(2,1)}, u32[]{:S(2)}) copy-start(bf16[4,176,1536]{2,1,0:T(8,128)(2,1)} %copy-done.22) | copy-start | bytes 6488068
  185.3 7.3 %copy-start.25 = (bf16[3072,768]{1,0:T(8,128)(2,1)S(1)}, bf16[3072,768]{1,0:T(8,128)(2,1)}, u32[]{:S(2)}) copy-start(bf16[3072,768]{1,0:T(8,128)(2,1)} %reshape_squeeze.3) | copy-start | bytes 14155780
  200.9 7.5 %copy-start.27 = (bf16[704,3072]{1,0:T(8,128)(2,1)}, bf16[704,3072]{1,0:T(8,128)(2,1)S(1)}, u32[]{:S(2)}) copy-start(bf16[704,3072]{1,0:T(8,128)(2,1)S(1)} %fusion.19) | copy-start | bytes 12976132
  209.9 65.0 %all-to-all-start.1 = ((bf16[4,176,1536]{2,1,0:T(8,128)(2,1)}), bf16[4,176,1536]{2,1,0:T(8,128)(2,1)}, u32[]{:S(2)}, u32[]{:S(2)}) async-start(bf16[4,176,1536]{2,1,0:T(8,128)(2,1)} %bitcast.10), calls=%async_computation.1 | async-start | bytes 4325376 | tf_op jit(solution)/shard_map/all_to_all | solution.py:305
  242.8 10.6 %copy-start.26 = (bf16[3072,768]{1,0:T(8,128)(2,1)S(1)}, bf16[3072,768]{1,0:T(8,128)(2,1)}, u32[]{:S(2)}) copy-start(bf16[3072,768]{1,0:T(8,128)(2,1)} %reshape_squeeze.3) | copy-start | bytes 14155780
  253.4 8.2 %copy-start.21 = (bf16[800,3072]{1,0:T(8,128)(2,1)}, bf16[800,3072]{1,0:T(8,128)(2,1)S(1)}, u32[]{:S(2)}) copy-start(bf16[800,3072]{1,0:T(8,128)(2,1)S(1)} %fusion.6) | copy-start | bytes 14745604
  253.4 8.2 %copy-start.31 = (bf16[2,768,3072]{2,1,0:T(8,128)(2,1)S(1)}, bf16[2,768,3072]{2,1,0:T(8,128)(2,1)}, u32[]{:S(2)}) copy-start(bf16[2,768,3072]{2,1,0:T(8,128)(2,1)} %all-gather.5.cloned.1.call-done) | copy-start | bytes 28311556
  253.4 13.9 %slice-start.2 = ((s8[4325376]{0:T(1024)(128)(4,1)}), s8[4194304]{0:T(1024)(128)(4,1)S(1)}, s32[]{:S(2)}) async-start(s8[4325376]{0:T(1024)(128)(4,1)} %bitcast.203), calls=%async_computation.10 | async-start | bytes 8388608
  261.6 5.7 %slice-start.3 = ((s8[4325376]{0:T(1024)(128)(4,1)}), s8[131072]{0:T(1024)(128)(4,1)S(1)}, s32[]{:S(2)}) async-start(s8[4325376]{0:T(1024)(128)(4,1)} %bitcast.203), calls=%async_computation.11 | async-start | bytes 262144
  274.8 60.4 %all-to-all-start.3 = ((bf16[4,200,1536]{2,1,0:T(8,128)(2,1)}), bf16[4,200,1536]{2,1,0:T(8,128)(2,1)}, u32[]{:S(2)}, u32[]{:S(2)}) async-start(bf16[4,200,1536]{2,1,0:T(8,128)(2,1)} %bitcast.15), calls=%async_computation.3 | async-start | bytes 4915200 | tf_op jit(solution)/shard_map/all_to_all | solution.py:305
  279.9 179.9 %reduce-scatter.2.cloned.1.call-start = ((), (), s32[]{:S(2)}) async-start(), calls=%async_computation.7 | async-start | bytes 10616832 | tf_op jit(solution)/shard_map/reduce_scatter | solution.py:311
  324.4 5.5 %copy-start.37 = (pred[1504,591]{1,0:T(32,128)(4,1)S(1)}, pred[1504,591]{1,0:T(32,128)(4,1)}, u32[]{:S(2)}) copy-start(pred[1504,591]{1,0:T(32,128)(4,1)} %get-tuple-element.108) | copy-start | bytes 2666596
  335.3 6.6 %copy-start.69 = (f32[591,1536]{1,0:T(8,128)S(1)}, f32[591,1536]{1,0:T(8,128)}, u32[]{:S(2)}) copy-start(f32[591,1536]{1,0:T(8,128)} %fusion.58) | copy-start | bytes 10893316
  335.3 13.0 %slice-start = ((s8[4915200]{0:T(1024)(128)(4,1)}), s8[4194304]{0:T(1024)(128)(4,1)S(1)}, s32[]{:S(2)}) async-start(s8[4915200]{0:T(1024)(128)(4,1)} %bitcast.197), calls=%async_computation.8 | async-start | bytes 8388608
  341.8 4.3 copy-start.5
  341.9 4.3 copy-start.11
  341.9 4.3 copy-start.42
  341.9 4.3 copy-start.67
  341.9 6.3 %slice-start.1 = ((s8[4915200]{0:T(1024)(128)(4,1)}), s8[720896]{0:T(1024)(128)(4,1)S(1)}, s32[]{:S(2)}) async-start(s8[4915200]{0:T(1024)(128)(4,1)} %bitcast.197), calls=%async_computation.9 | async-start | bytes 1441792
  377.5 5.8 %copy-start.7 = (bf16[591,768]{1,0:T(8,128)(2,1)S(1)}, bf16[591,768]{1,0:T(8,128)(2,1)}, u32[]{:S(2)}) copy-start(bf16[591,768]{1,0:T(8,128)(2,1)} %param.11) | copy-start | bytes 2723332
  377.5 5.8 %copy-start.50 = (f32[591]{0:T(1024)S(1)}, f32[591]{0:T(1024)}, u32[]{:S(2)}) copy-start(f32[591]{0:T(1024)} %copy-done.49) | copy-start | bytes 7096
  377.5 5.8 %copy-start.60 = (f32[768]{0:T(1024)S(1)}, f32[768]{0:T(1024)}, u32[]{:S(2)}) copy-start(f32[768]{0:T(1024)} %copy-done.59) | copy-start | bytes 9220
  380.6 5.2 %copy-start.12 = (f32[768,1024]{1,0:T(8,128)}, f32[768,1024]{1,0:T(8,128)S(1)}, u32[]{:S(2)}) copy-start(f32[768,1024]{1,0:T(8,128)S(1)} %get-tuple-element.100) | copy-start | bytes 9437188
  380.6 5.2 %copy-start.14 = (f32[768,1024]{1,0:T(8,128)}, f32[768,1024]{1,0:T(8,128)S(1)}, u32[]{:S(2)}) copy-start(f32[768,1024]{1,0:T(8,128)S(1)} %get-tuple-element.99) | copy-start | bytes 9437188
  381.8 12.6 %collective-permute-start = (bf16[2,2,96,1024]{3,2,1,0:T(8,128)(2,1)}, bf16[2,2,96,1024]{3,2,1,0:T(8,128)(2,1)}, u32[]{:S(2)}, u32[]{:S(2)}) collective-permute-start(bf16[2,2,96,1024]{3,2,1,0:T(8,128)(2,1)} %fusion.83), channel_id=1, source_target_pairs={{0,1},{1,0},{2,3},{3,2},{4,5},{5,4},{6,7},{7,6},{8,9},{9,8},{10,11... | collective-permute-start | bytes 2359304 | tf_op jit(solution)/shard_map/ppermute | solution.py:122
  383.3 15.7 %collective-permute-start.7 = (bf16[2,2,96,1024]{3,2,1,0:T(8,128)(2,1)}, bf16[2,2,96,1024]{3,2,1,0:T(8,128)(2,1)}, u32[]{:S(2)}, u32[]{:S(2)}) collective-permute-start(bf16[2,2,96,1024]{3,2,1,0:T(8,128)(2,1)} %fusion.84), channel_id=1, source_target_pairs={{0,1},{1,0},{2,3},{3,2},{4,5},{5,4},{6,7},{7,6},{8,9},{9,8},{10,11... | collective-permute-start | bytes 2359304 | tf_op jit(solution)/shard_map/ppermute | solution.py:122
  391.6 10.7 %collective-permute-start.14 = (bf16[2,2,96,1152]{3,2,1,0:T(8,128)(2,1)S(1)}, bf16[2,2,96,1152]{3,2,1,0:T(8,128)(2,1)S(1)}, u32[]{:S(2)}, u32[]{:S(2)}) collective-permute-start(bf16[2,2,96,1152]{3,2,1,0:T(8,128)(2,1)S(1)} %fusion.79), channel_id=1, source_target_pairs={{0,1},{1,0},{2,3},{3,2},{4,5},{5,4},{6,7},{7,6},{8,9},{9,8},{10,11... | collective-permute-start | bytes 2654216 | tf_op jit(solution)/shard_map/ppermute | solution.py:122
  394.4 4.6 copy-start.13
  396.3 8.2 %collective-permute-start.1 = (bf16[2,96,512]{2,1,0:T(8,128)(2,1)S(1)}, bf16[2,96,512]{2,1,0:T(8,128)(2,1)S(1)}, u32[]{:S(2)}, u32[]{:S(2)}) collective-permute-start(bf16[2,96,512]{2,1,0:T(8,128)(2,1)S(1)} %fusion.92), channel_id=1, source_target_pairs={{0,2},{1,3},{2,0},{3,1},{4,6},{5,7},{6,4},{7,5},{8,10},{9,11},{10,... | collective-permute-start | bytes 589832 | tf_op jit(solution)/shard_map/ppermute | solution.py:122
  398.0 7.8 %collective-permute-start.3 = (bf16[2,96,512]{2,1,0:T(8,128)(2,1)S(1)}, bf16[2,96,512]{2,1,0:T(8,128)(2,1)S(1)}, u32[]{:S(2)}, u32[]{:S(2)}) collective-permute-start(bf16[2,96,512]{2,1,0:T(8,128)(2,1)S(1)} %fusion.88), channel_id=1, source_target_pairs={{0,4},{1,5},{2,6},{3,7},{4,0},{5,1},{6,2},{7,3},{8,12},{9,13},{10,... | collective-permute-start | bytes 589832 | tf_op jit(solution)/shard_map/ppermute | solution.py:122
  400.7 7.8 %collective-permute-start.8 = (bf16[2,96,512]{2,1,0:T(8,128)(2,1)S(1)}, bf16[2,96,512]{2,1,0:T(8,128)(2,1)S(1)}, u32[]{:S(2)}, u32[]{:S(2)}) collective-permute-start(bf16[2,96,512]{2,1,0:T(8,128)(2,1)S(1)} %fusion.93), channel_id=1, source_target_pairs={{0,2},{1,3},{2,0},{3,1},{4,6},{5,7},{6,4},{7,5},{8,10},{9,11},{10,... | collective-permute-start | bytes 589832 | tf_op jit(solution)/shard_map/ppermute | solution.py:122
  401.6 8.4 %collective-permute-start.10 = (bf16[2,96,512]{2,1,0:T(8,128)(2,1)S(1)}, bf16[2,96,512]{2,1,0:T(8,128)(2,1)S(1)}, u32[]{:S(2)}, u32[]{:S(2)}) collective-permute-start(bf16[2,96,512]{2,1,0:T(8,128)(2,1)S(1)} %fusion.90), channel_id=1, source_target_pairs={{0,4},{1,5},{2,6},{3,7},{4,0},{5,1},{6,2},{7,3},{8,12},{9,13},{10,... | collective-permute-start | bytes 589832 | tf_op jit(solution)/shard_map/ppermute | solution.py:122
  402.7 21.3 %collective-permute-start.15 = (bf16[2,96,512]{2,1,0:T(8,128)(2,1)S(1)}, bf16[2,96,512]{2,1,0:T(8,128)(2,1)S(1)}, u32[]{:S(2)}, u32[]{:S(2)}) collective-permute-start(bf16[2,96,512]{2,1,0:T(8,128)(2,1)S(1)} %fusion.94), channel_id=1, source_target_pairs={{0,2},{1,3},{2,0},{3,1},{4,6},{5,7},{6,4},{7,5},{8,10},{9,11},{10,... | collective-permute-start | bytes 589832 | tf_op jit(solution)/shard_map/ppermute | solution.py:122
  404.5 20.3 %collective-permute-start.17 = (bf16[2,96,640]{2,1,0:T(8,128)(2,1)S(1)}, bf16[2,96,640]{2,1,0:T(8,128)(2,1)S(1)}, u32[]{:S(2)}, u32[]{:S(2)}) collective-permute-start(bf16[2,96,640]{2,1,0:T(8,128)(2,1)S(1)} %fusion.85), channel_id=1, source_target_pairs={{0,4},{1,5},{2,6},{3,7},{4,0},{5,1},{6,2},{7,3},{8,12},{9,13},{10,... | collective-permute-start | bytes 737288 | tf_op jit(solution)/shard_map/ppermute | solution.py:122
  405.8 11.6 %collective-permute-start.2 = (bf16[96,512]{1,0:T(8,128)(2,1)S(1)}, bf16[96,512]{1,0:T(8,128)(2,1)S(1)}, u32[]{:S(2)}, u32[]{:S(2)}) collective-permute-start(bf16[96,512]{1,0:T(8,128)(2,1)S(1)} %fusion.104), channel_id=1, source_target_pairs={{0,4},{1,5},{2,6},{3,7},{4,0},{5,1},{6,2},{7,3},{8,12},{9,13},{10,... | collective-permute-start | bytes 294920 | tf_op jit(solution)/shard_map/ppermute | solution.py:122
  408.6 9.4 %collective-permute-start.4 = (bf16[96,512]{1,0:T(8,128)(2,1)S(1)}, bf16[96,512]{1,0:T(8,128)(2,1)S(1)}, u32[]{:S(2)}, u32[]{:S(2)}) collective-permute-start(bf16[96,512]{1,0:T(8,128)(2,1)S(1)} %fusion.105), channel_id=1, source_target_pairs={{0,2},{1,3},{2,0},{3,1},{4,6},{5,7},{6,4},{7,5},{8,10},{9,11},{10,... | collective-permute-start | bytes 294920 | tf_op jit(solution)/shard_map/ppermute | solution.py:122
  410.0 9.9 %collective-permute-start.9 = (bf16[96,512]{1,0:T(8,128)(2,1)S(1)}, bf16[96,512]{1,0:T(8,128)(2,1)S(1)}, u32[]{:S(2)}, u32[]{:S(2)}) collective-permute-start(bf16[96,512]{1,0:T(8,128)(2,1)S(1)} %fusion.106), channel_id=1, source_target_pairs={{0,4},{1,5},{2,6},{3,7},{4,0},{5,1},{6,2},{7,3},{8,12},{9,13},{10,... | collective-permute-start | bytes 294920 | tf_op jit(solution)/shard_map/ppermute | solution.py:122
  417.4 4.6 collective-permute-start.11
  418.1 12.4 %collective-permute-start.5 = (bf16[96,1024]{1,0:T(8,128)(2,1)S(1)}, bf16[96,1024]{1,0:T(8,128)(2,1)S(1)}, u32[]{:S(2)}, u32[]{:S(2)}) collective-permute-start(bf16[96,1024]{1,0:T(8,128)(2,1)S(1)} %pad_maximum_fusion.10), channel_id=1, source_target_pairs={{0,8},{8,0},{16,24},{24,16},{1,9},{9,1},{17,25},{25,17},{2,10},{10... | collective-permute-start | bytes 589832 | tf_op jit(solution)/shard_map/ppermute | solution.py:148
  422.1 10.9 %collective-permute-start.12 = (bf16[96,1024]{1,0:T(8,128)(2,1)S(1)}, bf16[96,1024]{1,0:T(8,128)(2,1)S(1)}, u32[]{:S(2)}, u32[]{:S(2)}) collective-permute-start(bf16[96,1024]{1,0:T(8,128)(2,1)S(1)} %pad_maximum_fusion.11), channel_id=1, source_target_pairs={{0,8},{8,0},{16,24},{24,16},{1,9},{9,1},{17,25},{25,17},{2,10},{10... | collective-permute-start | bytes 589832 | tf_op jit(solution)/shard_map/ppermute | solution.py:148
  424.1 4.7 collective-permute-start.16
  424.9 4.9 %collective-permute-start.18 = (bf16[96,640]{1,0:T(8,128)(2,1)S(1)}, bf16[96,640]{1,0:T(8,128)(2,1)S(1)}, u32[]{:S(2)}, u32[]{:S(2)}) collective-permute-start(bf16[96,640]{1,0:T(8,128)(2,1)S(1)} %fusion.103), channel_id=1, source_target_pairs={{0,2},{1,3},{2,0},{3,1},{4,6},{5,7},{6,4},{7,5},{8,10},{9,11},{10,... | collective-permute-start | bytes 368648 | tf_op jit(solution)/shard_map/ppermute | solution.py:122
  429.9 17.9 %collective-permute-start.19 = (bf16[96,1152]{1,0:T(8,128)(2,1)S(1)}, bf16[96,1152]{1,0:T(8,128)(2,1)S(1)}, u32[]{:S(2)}, u32[]{:S(2)}) collective-permute-start(bf16[96,1152]{1,0:T(8,128)(2,1)S(1)} %pad_maximum_fusion.9), channel_id=1, source_target_pairs={{0,8},{8,0},{16,24},{24,16},{1,9},{9,1},{17,25},{25,17},{2,10},{10... | collective-permute-start | bytes 663560 | tf_op jit(solution)/shard_map/ppermute | solution.py:148
  430.5 17.2 %collective-permute-start.6 = (bf16[96,1024]{1,0:T(8,128)(2,1)S(1)}, bf16[96,1024]{1,0:T(8,128)(2,1)S(1)}, u32[]{:S(2)}, u32[]{:S(2)}) collective-permute-start(bf16[96,1024]{1,0:T(8,128)(2,1)S(1)} %add_convert_fusion.10), channel_id=1, source_target_pairs={{0,16},{8,24},{16,0},{24,8},{1,17},{9,25},{17,1},{25,9},{2,18},{10... | collective-permute-start | bytes 589832 | tf_op jit(solution)/shard_map/ppermute | solution.py:148
  433.1 18.3 %collective-permute-start.13 = (bf16[96,1024]{1,0:T(8,128)(2,1)S(1)}, bf16[96,1024]{1,0:T(8,128)(2,1)S(1)}, u32[]{:S(2)}, u32[]{:S(2)}) collective-permute-start(bf16[96,1024]{1,0:T(8,128)(2,1)S(1)} %add_convert_fusion.8), channel_id=1, source_target_pairs={{0,16},{8,24},{16,0},{24,8},{1,17},{9,25},{17,1},{25,9},{2,18},{10... | collective-permute-start | bytes 589832 | tf_op jit(solution)/shard_map/ppermute | solution.py:148
  447.8 8.9 %collective-permute-start.20 = (bf16[96,1152]{1,0:T(8,128)(2,1)S(1)}, bf16[96,1152]{1,0:T(8,128)(2,1)S(1)}, u32[]{:S(2)}, u32[]{:S(2)}) collective-permute-start(bf16[96,1152]{1,0:T(8,128)(2,1)S(1)} %add_convert_fusion.6), channel_id=1, source_target_pairs={{0,16},{8,24},{16,0},{24,8},{1,17},{9,25},{17,1},{25,9},{2,18},{10... | collective-permute-start | bytes 663560 | tf_op jit(solution)/shard_map/ppermute | solution.py:148
  (38 other events, 76.9 us)
Sparse Core Ops, SparseCore 0:
  11.7 42.3 all-gather.2
  56.5 58.7 all-gather.4
  323.4 77.1 reduce-scatter.1

commit v20 on v19

--- a/solution.py
+++ b/solution.py
@@ -232,8 +232,9 @@
     slot_index = jnp.sum(before * flat_picks, axis=1).reshape(rows, 2)
     position = jnp.where(live_int[:, None] > 0, routes * capacity + slot_index, overflow)
 
-    first_cap = min(capacity, 8 * round(capacity * 0.47 / 8))
-    chunk_sizes = [first_cap, capacity - first_cap]
+    n_chunks = 2
+    part_cap = 8 * ((capacity + 8 * n_chunks - 1) // (8 * n_chunks))
+    chunk_sizes = [min(part_cap, capacity - k * part_cap) for k in range(n_chunks)]
     chunk_sizes = [size for size in chunk_sizes if size > 0]
     chunk_starts = [sum(chunk_sizes[:k]) for k in range(len(chunk_sizes))]
     slot_ids = jnp.concatenate(
@@ -377,7 +378,7 @@
     )
     small = jnp.pad(small, ((0, 0), (0, 128 - small.shape[1])))
     dense_grads = jnp.concatenate([grad_qkv, grad_wout, small], axis=1)
-    n_parts = 3
+    n_parts = 4
     bounds = [128 * (dense_grads.shape[1] * k // (128 * n_parts)) for k in range(n_parts)]
     bounds = bounds + [dense_grads.shape[1]]
     dense_total = jnp.concatenate(

time: 479 us -> 475 us (level)
  waiting for transfers between devices: 108 us -> 85.9 us
  starting transfers between devices: 39.8 us -> 49.7 us
  local copies, waits for them, and re-layouts: 47.9 us -> 54.1 us
    all_to_all x2, waiting for transfers between devices: 41.8 us -> 23 us  [shards(): lax.all_to_all(dispatch_rows(experts * start, experts * (start + size)).r...]
    all_gather x1, waiting for transfers between devices: 0.02 us -> 12.9 us  [shards(): expert_full = lax.all_gather(expert_local, 'shard', axis=1, tiled=True)]
    ppermute x6 -> x8, waiting for transfers between devices: 22.9 us -> 14.8 us  [expert_all_reduce_doubling(): got = lax.ppermute(total, axis_name, pairs)]
    ppermute x15 -> x20, waiting for transfers between devices: 14 us -> 6.12 us  [_exchange(): got = lax.ppermute(send.astype(jnp.bfloat16), axis_name, pairs)]
    ppermute x15 -> x20, starting transfers between devices: 13.5 us -> 19.2 us  [_exchange(): got = lax.ppermute(send.astype(jnp.bfloat16), axis_name, pairs)]
    concatenate x1 -> x2, local copies, waits for them, and re-layouts: 0.18 us -> 5.83 us  [the longest x1 3.36 us: shards(): dense_grads = jnp.concatenate([grad_qkv, grad_wout, small], axis=1)]
    ppermute x6 -> x8, starting transfers between devices: 7.45 us -> 12 us  [expert_all_reduce_doubling(): got = lax.ppermute(total, axis_name, pairs)]
    unnamed x154 -> x152, local copies, waits for them, and re-layouts: 11.1 us -> 8.16 us
  transfers between devices with their start and end apart: 28 -> 35, of which waited for: 11 -> 14; matrix products, arithmetic and copies ran while one was open for 54% -> 57% of each run, Pallas kernels for 7% -> 8%
where the time goes in v20:
time: 475 us; the launch traced here: 465 us
  matrix products  184 us (39%)
  waiting for transfers between devices  85.9 us (18%)
  local copies, waits for them, and re-layouts  54.1 us (11%)
  starting transfers between devices  49.7 us (10%)
  other arithmetic  40 us (8%)
  Pallas kernels  35.2 us (7%)
  between operations  16.6 us (3%)
    dot_general x2, matrix products, shards(): jnp.dot(flat_arrived, expert_first, preferred_element_type=jnp.float32)  52.1 us
    all_gather x1, waiting for transfers between devices, shards(): dense_full = lax.all_gather(dense_local, 'shard', axis=0, tiled=True)  29.1 us
    all_to_all x2, waiting for transfers between devices, shards(): lax.all_to_all(dispatch_rows(experts * start, experts * (start + size)).r...  23 us
    dot_general x2, matrix products, shards(): lax.dot_general(flat_grad, expert_second, COL_CONTRACT, preferred_element...  22.5 us
    pallas_call x1, Pallas kernels, attention_bwd(): pl.pallas_call(functools.partial(attn_bwd_kernel, images=images), grid=(p...  21.8 us
    dot_general x2, matrix products, shards(): lax.dot_general(activated, flat_grad, ROW_CONTRACT, preferred_element_typ...  20.4 us
    ppermute x20, starting transfers between devices, _exchange(): got = lax.ppermute(send.astype(jnp.bfloat16), axis_name, pairs)  19.2 us
    ppermute x8, waiting for transfers between devices, expert_all_reduce_doubling(): got = lax.ppermute(total, axis_name, pairs)  14.8 us
  transfers between devices with their start and end apart: 35, of which 14 were waited for; matrix products, arithmetic and copies ran while one was open for 57% of the time, Pallas kernels for 8%

profile of v20, /device:TPU:0, one launch (start us, length us, event | category | flops | bytes accessed | tf_op | source)
XLA Modules:
  0.0 465.4 jit_solution(13985448296520513796)
XLA Ops:
  9.6 1.9 concatenate.65
  11.6 1.5 stack_reshape_squeeze.3
  13.2 2.3 pad_maximum_fusion.6
  21.6 3.4 fusion.127
  25.0 29.1 %all-gather.3.cloned.1.call-done = bf16[768,3078]{1,0:T(8,128)(2,1)} async-done(((bf16[96,3078]{1,0:T(8,128)(2,1)}), bf16[768,3078]{1,0:T(8,128)(2,1)}) %all-gather.3.cloned.1.call-update) | async-done | bytes 4727824 | tf_op jit(solution)/shard_map/all_gather | solution.py:201
  55.8 4.6 convolution_convert_fusion
  60.6 13.4 %shard_map.178 = bf16[640,768]{1,0:T(8,128)(2,1)S(1)} custom-call(bf16[640,2304]{1,0:T(8,128)(2,1)S(1)} %pad.18.q_ref.k_ref.v_ref, bf16[640,2304]{1,0:T(8,128)(2,1)S(1)} %pad.18.q_ref.k_ref.v_ref, bf16[640,2304]{1,0:T(8,128)(2,1)S(1)} %pad.18.q_ref.k_ref.v_ref), custom_call_target="tpu_custom_call" | custom-call | tf_op jit(solution)/shard_map/pallas_call | solution.py:90
  74.1 2.6 fusion.137
  80.7 2.7 fusion.59
  83.4 2.3 convolution_convert_fusion.4
  85.7 2.4 add_convert_fusion.3
  88.0 1.6 pad_maximum_fusion.4
  89.6 4.6 all-to-all-start.2
  94.8 3.0 fusion.52
  100.8 1.6 pad_maximum_fusion.2
  102.4 12.9 %all-gather.5.cloned.1.call-done = bf16[2,768,3072]{2,1,0:T(8,128)(2,1)} async-done(((bf16[2,96,3072]{2,1,0:T(8,128)(2,1)}), bf16[2,768,3072]{2,1,0:T(8,128)(2,1)}) %all-gather.5.cloned.1.call-update) | async-done | bytes 9437200 | tf_op jit(solution)/shard_map/all_gather | solution.py:212
  115.3 4.9 %slice.227 = bf16[1,768,3072]{2,1,0:T(8,128)(2,1)} slice(bf16[2,768,3072]{2,1,0:T(8,128)(2,1)} %all-gather.5.cloned.1.call-done), slice={[1:2], [0:768], [0:3072]} | slice | bytes 9437184 | tf_op jit(solution)/shard_map/slice | solution.py:214
  120.1 8.5 %reshape_squeeze.3 = bf16[3072,768]{1,0:T(8,128)(2,1)} reshape(bf16[1,768,3072]{2,1,0:T(8,128)(2,1)} %slice.227) | data formatting | bytes 9437184 | tf_op jit(solution)/shard_map/reshape;squeeze | solution.py:214
  128.6 17.7 %all-to-all-done.2 = bf16[4,184,1536]{2,1,0:T(8,128)(2,1)S(1)} async-done(((bf16[4,184,1536]{2,1,0:T(8,128)(2,1)}), bf16[4,184,1536]{2,1,0:T(8,128)(2,1)S(1)}, u32[]{:S(2)}, u32[]{:S(2)}) %all-to-all-start.2) | async-done | bytes 2261024 | tf_op jit(solution)/shard_map/all_to_all | solution.py:270
  147.6 3.8 all-to-all-start
  151.5 25.8 %multiply_convert_fusion.1 = (bf16[736,3072]{1,0:T(8,128)(2,1)S(1)}, f32[736,3072]{1,0:T(8,128)}, f32[736,3072]{1,0:T(8,128)}) fusion(bf16[2,768,3072]{2,1,0:T(8,128)(2,1)} %all-gather.5.cloned.1.call-done, bf16[736,1536]{1,0:T(8,128)(2,1)} %bitcast.206), kind=kOutput, calls=%fused_computation.36 | convolution fusion | flops 3619848192 | bytes 28459008 | tf_op jit(solution)/shard_map/dot_general | solution.py:284
  177.3 3.7 convolution_convert_fusion.3
  181.0 10.8 %fusion.19 = bf16[736,3072]{1,0:T(8,128)(2,1)} fusion(f32[736,3072]{1,0:T(8,128)} %get-tuple-element.102, f32[736,3072]{1,0:T(8,128)} %get-tuple-element.79, bf16[3072,768]{1,0:T(8,128)(2,1)S(1)} %copy-done.22, bf16[736,1536]{1,0:T(8,128)(2,1)} %bitcast.207), kind=kOutput, calls=%fused_computation.35 | convolution fusion | flops 3490971648 | bytes 28459008 | tf_op jit(solution)/shard_map/dot_general | solution.py:281
  191.8 6.1 %fusion.48 = bf16[736,768]{1,0:T(8,128)(2,1)S(1)} fusion(bf16[736,3072]{1,0:T(8,128)(2,1)} %fusion.19, bf16[2,768,3072]{2,1,0:T(8,128)(2,1)S(1)} %bitcast.205), kind=kOutput, calls=%fused_computation.105 | convolution fusion | flops 3473448960 | bytes 10371072 | tf_op jit(solution)/shard_map/dot_general | solution.py:291
  197.9 1.6 pad_maximum_fusion.5
  199.5 5.3 %all-to-all-done = bf16[4,192,1536]{2,1,0:T(8,128)(2,1)S(1)} async-done(((bf16[4,192,1536]{2,1,0:T(8,128)(2,1)}), bf16[4,192,1536]{2,1,0:T(8,128)(2,1)S(1)}, u32[]{:S(2)}, u32[]{:S(2)}) %all-to-all-start) | async-done | bytes 2359328 | tf_op jit(solution)/shard_map/all_to_all | solution.py:270
  204.8 4.9 %all-to-all-start.3 = ((bf16[4,184,1536]{2,1,0:T(8,128)(2,1)}), bf16[4,184,1536]{2,1,0:T(8,128)(2,1)}, u32[]{:S(2)}, u32[]{:S(2)}) async-start(bf16[4,184,1536]{2,1,0:T(8,128)(2,1)} %bitcast.15), calls=%async_computation.3 | async-start | bytes 4521984 | tf_op jit(solution)/shard_map/all_to_all | solution.py:306
  209.7 26.2 %multiply_convert_fusion = (bf16[768,3072]{1,0:T(8,128)(2,1)S(1)}, f32[768,3072]{1,0:T(8,128)}, f32[768,3072]{1,0:T(8,128)}) fusion(bf16[2,768,3072]{2,1,0:T(8,128)(2,1)} %all-gather.5.cloned.1.call-done, bf16[768,1536]{1,0:T(8,128)(2,1)S(1)} %bitcast.200), kind=kOutput, calls=%fused_computation.14 | convolution fusion | flops 3777232896 | bytes 29491200 | tf_op jit(solution)/shard_map/dot_general | solution.py:284
  235.9 11.8 %fusion.6 = bf16[768,3072]{1,0:T(8,128)(2,1)S(1)} fusion(f32[768,3072]{1,0:T(8,128)} %get-tuple-element.103, f32[768,3072]{1,0:T(8,128)} %get-tuple-element.77, bf16[3072,768]{1,0:T(8,128)(2,1)} %reshape_squeeze.3, bf16[768,1536]{1,0:T(8,128)(2,1)S(1)} %bitcast.201), kind=kOutput, calls=%fused_computation.10 | convolution fusion | flops 3642753024 | bytes 29491200 | tf_op jit(solution)/shard_map/dot_general | solution.py:281
  247.7 8.1 %convolution_convert_fusion.1 = bf16[768,768]{0,1:T(8,128)(2,1)S(1)} fusion(bf16[768,3072]{1,0:T(8,128)(2,1)S(1)} %get-tuple-element.76, bf16[3072,768]{1,0:T(8,128)(2,1)} %reshape_squeeze.3), kind=kOutput, calls=%fused_computation.103 | convolution fusion | flops 3624468480 | bytes 10616832 | tf_op jit(solution)/shard_map/dot_general | solution.py:288
  255.9 6.3 %fusion.47 = bf16[768,768]{0,1:T(8,128)(2,1)S(1)} fusion(bf16[768,3072]{1,0:T(8,128)(2,1)S(1)} %fusion.6, bf16[2,768,3072]{2,1,0:T(8,128)(2,1)} %all-gather.5.cloned.1.call-done), kind=kOutput, calls=%fused_computation.102 | convolution fusion | flops 3624468480 | bytes 10616832 | tf_op jit(solution)/shard_map/dot_general | solution.py:291
  262.3 2.5 copy.81
  264.8 10.3 %fusion.62 = f32[3072,768]{1,0:T(8,128)} fusion(bf16[768,3072]{1,0:T(8,128)(2,1)} %copy-done.66, bf16[768,1536]{1,0:T(8,128)(2,1)} %bitcast.202), kind=kOutput, calls=%fused_computation.131 | convolution fusion | flops 3623878656 | bytes 15335424 | tf_op jit(solution)/shard_map/dot_general | solution.py:294
  275.1 5.2 %all-to-all-start.1 = ((bf16[4,192,1536]{2,1,0:T(8,128)(2,1)}), bf16[4,192,1536]{2,1,0:T(8,128)(2,1)}, u32[]{:S(2)}, u32[]{:S(2)}) async-start(bf16[4,192,1536]{2,1,0:T(8,128)(2,1)} %bitcast.10), calls=%async_computation.1 | async-start | bytes 4718592 | tf_op jit(solution)/shard_map/all_to_all | solution.py:306
  280.3 10.1 %add_convert_fusion = bf16[3072,768]{1,0:T(8,128)(2,1)} fusion(f32[3072,768]{1,0:T(8,128)} %fusion.62, bf16[736,3072]{1,0:T(8,128)(2,1)} %copy-done.67, bf16[736,1536]{1,0:T(8,128)(2,1)S(1)} %bitcast.208), kind=kOutput, calls=%fused_computation.12 | convolution fusion | flops 3477602304 | bytes 19808256 | tf_op jit(solution)/shard_map/dot_general | solution.py:294
  290.4 8.6 %stack_reshape.4 = bf16[1,768,3072]{2,1,0:T(8,128)(2,1)} reshape(bf16[3072,768]{1,0:T(8,128)(2,1)} %add_convert_fusion) | data formatting | bytes 9437184 | tf_op jit(solution)/shard_map/stack;reshape | solution.py:309
  299.0 5.9 %fusion.65 = f32[768,3072]{1,0:T(8,128)S(1)} fusion(bf16[768,3072]{1,0:T(8,128)(2,1)} %copy-done.23, bf16[768,1536]{1,0:T(8,128)(2,1)S(1)} %bitcast.203), kind=kOutput, calls=%fused_computation.134 | convolution fusion | flops 3623878656 | bytes 15335424 | tf_op jit(solution)/shard_map/dot_general | solution.py:297
  304.9 7.9 %fusion.26 = bf16[1,768,3072]{2,1,0:T(8,128)(2,1)} fusion(f32[768,3072]{1,0:T(8,128)S(1)} %fusion.65, bf16[736,3072]{1,0:T(8,128)(2,1)} %fusion.19, bf16[736,1536]{1,0:T(8,128)(2,1)S(1)} %bitcast.209), kind=kOutput, calls=%fused_computation.53 | convolution fusion | flops 3477602304 | bytes 19808256 | tf_op jit(solution)/shard_map/dot_general | solution.py:297
  312.8 8.3 %pad_maximum_fusion = bf16[2,768,3072]{2,1,0:T(8,128)(2,1)} fusion(bf16[1,768,3072]{2,1,0:T(8,128)(2,1)} %stack_reshape.4, bf16[1,768,3072]{2,1,0:T(8,128)(2,1)} %fusion.26), kind=kLoop, calls=%fused_computation.11 | loop fusion | flops 4718592 | bytes 18874368 | tf_op jit(solution)/shard_map/stack | solution.py:309
  322.3 5.5 %fusion.57 = f32[591,1536]{1,0:T(8,128)} fusion(bf16[736,1536]{1,0:T(8,128)(2,1)} %bitcast.16, pred[1504,591]{1,0:T(32,128)(4,1)S(1)} %copy-done.36), kind=kOutput, calls=%fused_computation.117 | convolution fusion | flops 1336246272 | bytes 6363136 | tf_op jit(solution)/shard_map/dot_general | solution.py:322
  327.8 5.4 %fusion.54 = f32[591,1536]{1,0:T(8,128)} fusion(bf16[736,1536]{1,0:T(8,128)(2,1)} %bitcast.16, pred[1504,591]{1,0:T(32,128)(4,1)S(1)} %copy-done.35), kind=kOutput, calls=%fused_computation.114 | convolution fusion | flops 1336246272 | bytes 6363136 | tf_op jit(solution)/shard_map/dot_general | solution.py:325
  333.2 6.1 %convolution_add_fusion.1 = f32[591,1536]{1,0:T(8,128)S(1)} fusion(f32[591,1536]{1,0:T(8,128)} %fusion.57, bf16[768,1536]{1,0:T(8,128)(2,1)} %bitcast.11, pred[1504,591]{1,0:T(32,128)(4,1)S(1)} %copy-done.36), kind=kOutput, calls=%fused_computation.56 | convolution fusion | flops 1395251712 | bytes 10113024 | tf_op jit(solution)/shard_map/dot_general | solution.py:322
  339.4 3.7 convolution_add_fusion
  343.2 1.9 multiply_reduce_fusion.3
  348.6 21.8 %shard_map.179 = (bf16[640,768]{1,0:T(8,128)(2,1)S(1)}, bf16[640,768]{1,0:T(8,128)(2,1)S(1)}, bf16[640,768]{1,0:T(8,128)(2,1)S(1)}) custom-call(bf16[640,2304]{1,0:T(8,128)(2,1)} %copy-done, bf16[640,2304]{1,0:T(8,128)(2,1)} %copy-done, bf16[640,2304]{1,0:T(8,128)(2,1)} %copy-done, bf16[640,768]{1,0:T(8,128)(2,1)S(1)} %pad.20.g_ref), custom_call_target="tpu_custom_call" | custom-call | tf_op jit(solution)/shard_map/pallas_call | solution.py:106
  371.7 3.0 fusion.75
  378.5 2.4 fusion.44
  384.1 1.7 pad_maximum_fusion.1
  385.8 3.4 copy.85
  389.2 1.6 fusion.81
  391.3 3.4 add_convert_fusion.4
  412.9 2.3 collective-permute-done.18
  417.3 1.6 collective-permute-start.2
  419.6 1.9 collective-permute-start.19
  422.4 2.2 collective-permute-start.5
  426.8 2.3 collective-permute-done.23
  429.2 2.4 collective-permute-start.20
  432.3 2.4 collective-permute-start.6
  434.8 1.6 collective-permute-start.26
  436.4 6.4 %collective-permute-done.20 = bf16[96,768]{1,0:T(8,128)(2,1)S(1)} collective-permute-done((bf16[96,768]{1,0:T(8,128)(2,1)S(1)}, bf16[96,768]{1,0:T(8,128)(2,1)S(1)}, u32[]{:S(2)}, u32[]{:S(2)}) %collective-permute-start.20) | collective-permute-done | bytes 147488 | tf_op jit(solution)/shard_map/ppermute | solution.py:148
  442.8 1.5 collective-permute-done.13
  444.4 1.5 collective-permute-done.6
  447.1 5.3 %collective-permute-done.27 = bf16[96,896]{1,0:T(8,128)(2,1)S(1)} collective-permute-done((bf16[96,896]{1,0:T(8,128)(2,1)S(1)}, bf16[96,896]{1,0:T(8,128)(2,1)S(1)}, u32[]{:S(2)}, u32[]{:S(2)}) %collective-permute-start.27) | collective-permute-done | bytes 172064 | tf_op jit(solution)/shard_map/ppermute | solution.py:148
  454.5 2.5 fusion.133
  (339 shorter events, 61.0 us)
Async XLA Ops:
  7.2 46.9 %all-gather.3.cloned.1.call-start = ((), (), s32[]{:S(2)}) async-start(), calls=%async_computation.5 | async-start | bytes 5529600 | tf_op jit(solution)/shard_map/all_gather | solution.py:201
  8.8 7.7 %copy-start.47 = (s32[591,2]{0,1:T(2,128)S(1)}, s32[591,2]{0,1:T(2,128)}, u32[]{:S(2)}) copy-start(s32[591,2]{0,1:T(2,128)} %param.13) | copy-start | bytes 14188
  11.6 7.9 %copy-start.5 = (bf16[591,768]{1,0:T(8,128)(2,1)S(1)}, bf16[591,768]{1,0:T(8,128)(2,1)}, u32[]{:S(2)}) copy-start(bf16[591,768]{1,0:T(8,128)(2,1)} %param.11) | copy-start | bytes 2723332
  11.6 103.7 %all-gather.5.cloned.1.call-start = ((), (), s32[]{:S(2)}) async-start(), calls=%async_computation.6 | async-start | bytes 10616832 | tf_op jit(solution)/shard_map/all_gather | solution.py:212
  13.2 6.9 %copy-start.7 = (bf16[591,768]{1,0:T(8,128)(2,1)S(1)}, bf16[591,768]{1,0:T(8,128)(2,1)}, u32[]{:S(2)}) copy-start(bf16[591,768]{1,0:T(8,128)(2,1)} %param.21) | copy-start | bytes 2723332
  19.4 60.5 %copy-start.37 = (f32[591]{0:T(1024)}, f32[591]{0:T(1024)S(1)}, u32[]{:S(2)}) copy-start(f32[591]{0:T(1024)S(1)} %fusion.124) | copy-start | bytes 7096
  19.6 35.8 %copy-start.45 = (f32[591]{0:T(1024)}, f32[591]{0:T(1024)S(1)}, u32[]{:S(2)}) copy-start(f32[591]{0:T(1024)S(1)} %broadcast_multiply_fusion.2) | copy-start | bytes 7096
  20.1 35.3 %copy-start.57 = (f32[591]{0:T(1024)}, f32[591]{0:T(1024)S(1)}, u32[]{:S(2)}) copy-start(f32[591]{0:T(1024)S(1)} %fusion.122) | copy-start | bytes 7096
  25.0 58.4 %copy-start.29 = (bf16[1504,591]{1,0:T(8,128)(2,1)}, bf16[1504,591]{1,0:T(8,128)(2,1)S(1)}, u32[]{:S(2)}) copy-start(bf16[1504,591]{1,0:T(8,128)(2,1)S(1)} %get-tuple-element.92) | copy-start | bytes 5333188
  55.4 22.3 %copy-start.49 = (f32[768]{0:T(1024)}, f32[768]{0:T(1024)S(1)}, u32[]{:S(2)}) copy-start(f32[768]{0:T(1024)S(1)} %get-tuple-element.60) | copy-start | bytes 9220
  60.6 13.4 %copy-start = (bf16[640,2304]{1,0:T(8,128)(2,1)}, bf16[640,2304]{1,0:T(8,128)(2,1)S(1)}, u32[]{:S(2)}) copy-start(bf16[640,2304]{1,0:T(8,128)(2,1)S(1)} %pad.18.q_ref.k_ref.v_ref) | copy-start | bytes 8847364
  78.2 19.6 %copy-start.10 = (bf16[591,768]{1,0:T(8,128)(2,1)}, bf16[591,768]{1,0:T(8,128)(2,1)S(1)}, u32[]{:S(2)}) copy-start(bf16[591,768]{1,0:T(8,128)(2,1)S(1)} %multiply_convert_fusion.4) | copy-start | bytes 2723332
  89.6 56.7 %all-to-all-start.2 = ((bf16[4,184,1536]{2,1,0:T(8,128)(2,1)}), bf16[4,184,1536]{2,1,0:T(8,128)(2,1)S(1)}, u32[]{:S(2)}, u32[]{:S(2)}) async-start(bf16[4,184,1536]{2,1,0:T(8,128)(2,1)} %pad_maximum_fusion.4), calls=%async_computation.2 | async-start | bytes 4521984 | tf_op jit(solution)/shard_map/all_to_all | solution.py:270
  147.6 57.2 %all-to-all-start = ((bf16[4,192,1536]{2,1,0:T(8,128)(2,1)}), bf16[4,192,1536]{2,1,0:T(8,128)(2,1)S(1)}, u32[]{:S(2)}, u32[]{:S(2)}) async-start(bf16[4,192,1536]{2,1,0:T(8,128)(2,1)} %pad_maximum_fusion.2), calls=%async_computation | async-start | bytes 4718592 | tf_op jit(solution)/shard_map/all_to_all | solution.py:270
  151.5 25.8 %copy-start.22 = (bf16[3072,768]{1,0:T(8,128)(2,1)S(1)}, bf16[3072,768]{1,0:T(8,128)(2,1)}, u32[]{:S(2)}) copy-start(bf16[3072,768]{1,0:T(8,128)(2,1)} %reshape_squeeze.3) | copy-start | bytes 14155780
  177.3 14.5 %slice-start = ((s8[9437184]{0:T(1024)(128)(4,1)}), s8[4194304]{0:T(1024)(128)(4,1)S(1)}, s32[]{:S(2)}) async-start(s8[9437184]{0:T(1024)(128)(4,1)} %bitcast.204), calls=%async_computation.8 | async-start | bytes 8388608
  177.3 14.5 %slice-start.1 = ((s8[9437184]{0:T(1024)(128)(4,1)}), s8[4194304]{0:T(1024)(128)(4,1)S(1)}, s32[]{:S(2)}) async-start(s8[9437184]{0:T(1024)(128)(4,1)} %bitcast.204), calls=%async_computation.9 | async-start | bytes 8388608
  181.0 10.8 %slice-start.2 = ((s8[9437184]{0:T(1024)(128)(4,1)}), s8[1048576]{0:T(1024)(128)(4,1)S(1)}, s32[]{:S(2)}) async-start(s8[9437184]{0:T(1024)(128)(4,1)} %bitcast.204), calls=%async_computation.10 | async-start | bytes 2097152
  204.8 31.1 %copy-start.20 = (bf16[4,192,1536]{2,1,0:T(8,128)(2,1)}, bf16[4,192,1536]{2,1,0:T(8,128)(2,1)S(1)}, u32[]{:S(2)}) copy-start(bf16[4,192,1536]{2,1,0:T(8,128)(2,1)S(1)} %all-to-all-done) | copy-start | bytes 7077892
  204.8 70.3 %all-to-all-start.3 = ((bf16[4,184,1536]{2,1,0:T(8,128)(2,1)}), bf16[4,184,1536]{2,1,0:T(8,128)(2,1)}, u32[]{:S(2)}, u32[]{:S(2)}) async-start(bf16[4,184,1536]{2,1,0:T(8,128)(2,1)} %bitcast.15), calls=%async_computation.3 | async-start | bytes 4521984 | tf_op jit(solution)/shard_map/all_to_all | solution.py:306
  235.9 11.8 %copy-start.66 = (bf16[768,3072]{1,0:T(8,128)(2,1)}, bf16[768,3072]{1,0:T(8,128)(2,1)S(1)}, u32[]{:S(2)}) copy-start(bf16[768,3072]{1,0:T(8,128)(2,1)S(1)} %get-tuple-element.76) | copy-start | bytes 14155780
  247.7 8.2 %copy-start.23 = (bf16[768,3072]{1,0:T(8,128)(2,1)}, bf16[768,3072]{1,0:T(8,128)(2,1)S(1)}, u32[]{:S(2)}) copy-start(bf16[768,3072]{1,0:T(8,128)(2,1)S(1)} %fusion.6) | copy-start | bytes 14155780
  275.1 5.2 %copy-start.27 = (bf16[4,184,1536]{2,1,0:T(8,128)(2,1)S(1)}, bf16[4,184,1536]{2,1,0:T(8,128)(2,1)}, u32[]{:S(2)}) copy-start(bf16[4,184,1536]{2,1,0:T(8,128)(2,1)} %copy-done.26) | copy-start | bytes 6782980
  275.1 58.1 %all-to-all-start.1 = ((bf16[4,192,1536]{2,1,0:T(8,128)(2,1)}), bf16[4,192,1536]{2,1,0:T(8,128)(2,1)}, u32[]{:S(2)}, u32[]{:S(2)}) async-start(bf16[4,192,1536]{2,1,0:T(8,128)(2,1)} %bitcast.10), calls=%async_computation.1 | async-start | bytes 4718592 | tf_op jit(solution)/shard_map/all_to_all | solution.py:306
  280.3 174.3 %reduce-scatter.2.cloned.1.call-start = ((), (), s32[]{:S(2)}) async-start(), calls=%async_computation.7 | async-start | bytes 10616832 | tf_op jit(solution)/shard_map/reduce_scatter | solution.py:312
  290.4 8.6 %copy-start.21 = (bf16[4,192,1536]{2,1,0:T(8,128)(2,1)S(1)}, bf16[4,192,1536]{2,1,0:T(8,128)(2,1)}, u32[]{:S(2)}) copy-start(bf16[4,192,1536]{2,1,0:T(8,128)(2,1)} %copy-done.20) | copy-start | bytes 7077892
  299.0 5.9 %copy-start.28 = (bf16[4,184,1536]{2,1,0:T(8,128)(2,1)S(1)}, bf16[4,184,1536]{2,1,0:T(8,128)(2,1)}, u32[]{:S(2)}) copy-start(bf16[4,184,1536]{2,1,0:T(8,128)(2,1)} %copy-done.26) | copy-start | bytes 6782980
  322.3 5.5 %copy-start.35 = (pred[1504,591]{1,0:T(32,128)(4,1)S(1)}, pred[1504,591]{1,0:T(32,128)(4,1)}, u32[]{:S(2)}) copy-start(pred[1504,591]{1,0:T(32,128)(4,1)} %get-tuple-element.96) | copy-start | bytes 2666596
  333.2 6.1 %copy-start.65 = (f32[591,1536]{1,0:T(8,128)S(1)}, f32[591,1536]{1,0:T(8,128)}, u32[]{:S(2)}) copy-start(f32[591,1536]{1,0:T(8,128)} %fusion.54) | copy-start | bytes 10893316
  333.2 12.1 %slice-start.3 = ((s8[4915200]{0:T(1024)(128)(4,1)}), s8[4194304]{0:T(1024)(128)(4,1)S(1)}, s32[]{:S(2)}) async-start(s8[4915200]{0:T(1024)(128)(4,1)} %bitcast.214), calls=%async_computation.11 | async-start | bytes 8388608
  339.4 5.9 %slice-start.4 = ((s8[4915200]{0:T(1024)(128)(4,1)}), s8[720896]{0:T(1024)(128)(4,1)S(1)}, s32[]{:S(2)}) async-start(s8[4915200]{0:T(1024)(128)(4,1)} %bitcast.214), calls=%async_computation.12 | async-start | bytes 1441792
  375.4 5.6 %copy-start.14 = (f32[768,768]{1,0:T(8,128)}, f32[768,768]{1,0:T(8,128)S(1)}, u32[]{:S(2)}) copy-start(f32[768,768]{1,0:T(8,128)S(1)} %get-tuple-element.81) | copy-start | bytes 7077892
  375.4 5.6 %copy-start.16 = (f32[768,768]{1,0:T(8,128)}, f32[768,768]{1,0:T(8,128)S(1)}, u32[]{:S(2)}) copy-start(f32[768,768]{1,0:T(8,128)S(1)} %get-tuple-element.83) | copy-start | bytes 7077892
  375.4 5.6 %copy-start.18 = (f32[768,768]{1,0:T(8,128)}, f32[768,768]{1,0:T(8,128)S(1)}, u32[]{:S(2)}) copy-start(f32[768,768]{1,0:T(8,128)S(1)} %get-tuple-element.82) | copy-start | bytes 7077892
  376.4 18.3 %collective-permute-start.14 = (bf16[2,2,96,768]{3,2,1,0:T(8,128)(2,1)}, bf16[2,2,96,768]{3,2,1,0:T(8,128)(2,1)}, u32[]{:S(2)}, u32[]{:S(2)}) collective-permute-start(bf16[2,2,96,768]{3,2,1,0:T(8,128)(2,1)} %fusion.84), channel_id=1, source_target_pairs={{0,1},{1,0},{2,3},{3,2},{4,5},{5,4},{6,7},{7,6},{8,9},{9,8},{10,11... | collective-permute-start | bytes 1769480 | tf_op jit(solution)/shard_map/ppermute | solution.py:122
  377.8 20.9 %collective-permute-start.7 = (bf16[2,2,96,768]{3,2,1,0:T(8,128)(2,1)}, bf16[2,2,96,768]{3,2,1,0:T(8,128)(2,1)}, u32[]{:S(2)}, u32[]{:S(2)}) collective-permute-start(bf16[2,2,96,768]{3,2,1,0:T(8,128)(2,1)} %fusion.83), channel_id=1, source_target_pairs={{0,1},{1,0},{2,3},{3,2},{4,5},{5,4},{6,7},{7,6},{8,9},{9,8},{10,11... | collective-permute-start | bytes 1769480 | tf_op jit(solution)/shard_map/ppermute | solution.py:122
  378.4 22.9 %collective-permute-start = (bf16[2,2,96,768]{3,2,1,0:T(8,128)(2,1)S(1)}, bf16[2,2,96,768]{3,2,1,0:T(8,128)(2,1)}, u32[]{:S(2)}, u32[]{:S(2)}) collective-permute-start(bf16[2,2,96,768]{3,2,1,0:T(8,128)(2,1)S(1)} %fusion.82), channel_id=1, source_target_pairs={{0,1},{1,0},{2,3},{3,2},{4,5},{5,4},{6,7},{7,6},{8,9},{9,8},{10,11... | collective-permute-start | bytes 1769480 | tf_op jit(solution)/shard_map/ppermute | solution.py:122
  389.2 5.5 %copy-start.19 = (f32[768,768]{1,0:T(8,128)S(1)}, f32[768,768]{1,0:T(8,128)}, u32[]{:S(2)}) copy-start(f32[768,768]{1,0:T(8,128)} %copy-done.18) | copy-start | bytes 7077892
  390.7 12.5 %collective-permute-start.21 = (bf16[2,2,96,896]{3,2,1,0:T(8,128)(2,1)S(1)}, bf16[2,2,96,896]{3,2,1,0:T(8,128)(2,1)S(1)}, u32[]{:S(2)}, u32[]{:S(2)}) collective-permute-start(bf16[2,2,96,896]{3,2,1,0:T(8,128)(2,1)S(1)} %fusion.81), channel_id=1, source_target_pairs={{0,1},{1,0},{2,3},{3,2},{4,5},{5,4},{6,7},{7,6},{8,9},{9,8},{10,11... | collective-permute-start | bytes 2064392 | tf_op jit(solution)/shard_map/ppermute | solution.py:122
  396.2 5.7 %copy-start.15 = (f32[768,768]{1,0:T(8,128)S(1)}, f32[768,768]{1,0:T(8,128)}, u32[]{:S(2)}) copy-start(f32[768,768]{1,0:T(8,128)} %copy-done.14) | copy-start | bytes 7077892
  396.2 8.9 %collective-permute-start.17 = (bf16[2,96,384]{2,1,0:T(8,128)(2,1)S(1)}, bf16[2,96,384]{2,1,0:T(8,128)(2,1)S(1)}, u32[]{:S(2)}, u32[]{:S(2)}) collective-permute-start(bf16[2,96,384]{2,1,0:T(8,128)(2,1)S(1)} %fusion.96), channel_id=1, source_target_pairs={{0,4},{1,5},{2,6},{3,7},{4,0},{5,1},{6,2},{7,3},{8,12},{9,13},{10,... | collective-permute-start | bytes 442376 | tf_op jit(solution)/shard_map/ppermute | solution.py:122
  397.7 9.7 %collective-permute-start.15 = (bf16[2,96,384]{2,1,0:T(8,128)(2,1)S(1)}, bf16[2,96,384]{2,1,0:T(8,128)(2,1)S(1)}, u32[]{:S(2)}, u32[]{:S(2)}) collective-permute-start(bf16[2,96,384]{2,1,0:T(8,128)(2,1)S(1)} %fusion.95), channel_id=1, source_target_pairs={{0,2},{1,3},{2,0},{3,1},{4,6},{5,7},{6,4},{7,5},{8,10},{9,11},{10,... | collective-permute-start | bytes 442376 | tf_op jit(solution)/shard_map/ppermute | solution.py:122
  400.1 6.2 %collective-permute-start.10 = (bf16[2,96,384]{2,1,0:T(8,128)(2,1)S(1)}, bf16[2,96,384]{2,1,0:T(8,128)(2,1)S(1)}, u32[]{:S(2)}, u32[]{:S(2)}) collective-permute-start(bf16[2,96,384]{2,1,0:T(8,128)(2,1)S(1)} %fusion.94), channel_id=1, source_target_pairs={{0,4},{1,5},{2,6},{3,7},{4,0},{5,1},{6,2},{7,3},{8,12},{9,13},{10,... | collective-permute-start | bytes 442376 | tf_op jit(solution)/shard_map/ppermute | solution.py:122
  401.3 7.1 %collective-permute-start.8 = (bf16[2,96,384]{2,1,0:T(8,128)(2,1)S(1)}, bf16[2,96,384]{2,1,0:T(8,128)(2,1)S(1)}, u32[]{:S(2)}, u32[]{:S(2)}) collective-permute-start(bf16[2,96,384]{2,1,0:T(8,128)(2,1)S(1)} %fusion.93), channel_id=1, source_target_pairs={{0,2},{1,3},{2,0},{3,1},{4,6},{5,7},{6,4},{7,5},{8,10},{9,11},{10,... | collective-permute-start | bytes 442376 | tf_op jit(solution)/shard_map/ppermute | solution.py:122
  403.3 6.7 %collective-permute-start.3 = (bf16[2,96,384]{2,1,0:T(8,128)(2,1)S(1)}, bf16[2,96,384]{2,1,0:T(8,128)(2,1)S(1)}, u32[]{:S(2)}, u32[]{:S(2)}) collective-permute-start(bf16[2,96,384]{2,1,0:T(8,128)(2,1)S(1)} %fusion.92), channel_id=1, source_target_pairs={{0,4},{1,5},{2,6},{3,7},{4,0},{5,1},{6,2},{7,3},{8,12},{9,13},{10,... | collective-permute-start | bytes 442376 | tf_op jit(solution)/shard_map/ppermute | solution.py:122
  405.1 6.8 %collective-permute-start.1 = (bf16[2,96,384]{2,1,0:T(8,128)(2,1)S(1)}, bf16[2,96,384]{2,1,0:T(8,128)(2,1)S(1)}, u32[]{:S(2)}, u32[]{:S(2)}) collective-permute-start(bf16[2,96,384]{2,1,0:T(8,128)(2,1)S(1)} %fusion.91), channel_id=1, source_target_pairs={{0,2},{1,3},{2,0},{3,1},{4,6},{5,7},{6,4},{7,5},{8,10},{9,11},{10,... | collective-permute-start | bytes 442376 | tf_op jit(solution)/shard_map/ppermute | solution.py:122
  406.3 19.1 %collective-permute-start.24 = (bf16[2,96,512]{2,1,0:T(8,128)(2,1)S(1)}, bf16[2,96,512]{2,1,0:T(8,128)(2,1)S(1)}, u32[]{:S(2)}, u32[]{:S(2)}) collective-permute-start(bf16[2,96,512]{2,1,0:T(8,128)(2,1)S(1)} %fusion.85), channel_id=1, source_target_pairs={{0,4},{1,5},{2,6},{3,7},{4,0},{5,1},{6,2},{7,3},{8,12},{9,13},{10,... | collective-permute-start | bytes 589832 | tf_op jit(solution)/shard_map/ppermute | solution.py:122
  407.4 17.2 %collective-permute-start.22 = (bf16[2,96,384]{2,1,0:T(8,128)(2,1)S(1)}, bf16[2,96,384]{2,1,0:T(8,128)(2,1)S(1)}, u32[]{:S(2)}, u32[]{:S(2)}) collective-permute-start(bf16[2,96,384]{2,1,0:T(8,128)(2,1)S(1)} %fusion.97), channel_id=1, source_target_pairs={{0,2},{1,3},{2,0},{3,1},{4,6},{5,7},{6,4},{7,5},{8,10},{9,11},{10,... | collective-permute-start | bytes 442376 | tf_op jit(solution)/shard_map/ppermute | solution.py:122
  408.3 6.9 %collective-permute-start.18 = (bf16[96,384]{1,0:T(8,128)(2,1)S(1)}, bf16[96,384]{1,0:T(8,128)(2,1)S(1)}, u32[]{:S(2)}, u32[]{:S(2)}) collective-permute-start(bf16[96,384]{1,0:T(8,128)(2,1)S(1)} %fusion.111), channel_id=1, source_target_pairs={{0,2},{1,3},{2,0},{3,1},{4,6},{5,7},{6,4},{7,5},{8,10},{9,11},{10,... | collective-permute-start | bytes 221192 | tf_op jit(solution)/shard_map/ppermute | solution.py:122
  410.0 6.4 %collective-permute-start.16 = (bf16[96,384]{1,0:T(8,128)(2,1)S(1)}, bf16[96,384]{1,0:T(8,128)(2,1)S(1)}, u32[]{:S(2)}, u32[]{:S(2)}) collective-permute-start(bf16[96,384]{1,0:T(8,128)(2,1)S(1)} %fusion.110), channel_id=1, source_target_pairs={{0,4},{1,5},{2,6},{3,7},{4,0},{5,1},{6,2},{7,3},{8,12},{9,13},{10,... | collective-permute-start | bytes 221192 | tf_op jit(solution)/shard_map/ppermute | solution.py:122
  411.9 5.4 %collective-permute-start.11 = (bf16[96,384]{1,0:T(8,128)(2,1)S(1)}, bf16[96,384]{1,0:T(8,128)(2,1)S(1)}, u32[]{:S(2)}, u32[]{:S(2)}) collective-permute-start(bf16[96,384]{1,0:T(8,128)(2,1)S(1)} %fusion.109), channel_id=1, source_target_pairs={{0,2},{1,3},{2,0},{3,1},{4,6},{5,7},{6,4},{7,5},{8,10},{9,11},{10,... | collective-permute-start | bytes 221192 | tf_op jit(solution)/shard_map/ppermute | solution.py:122
  415.3 4.4 collective-permute-start.9
  416.4 5.2 %collective-permute-start.4 = (bf16[96,384]{1,0:T(8,128)(2,1)S(1)}, bf16[96,384]{1,0:T(8,128)(2,1)S(1)}, u32[]{:S(2)}, u32[]{:S(2)}) collective-permute-start(bf16[96,384]{1,0:T(8,128)(2,1)S(1)} %fusion.107), channel_id=1, source_target_pairs={{0,2},{1,3},{2,0},{3,1},{4,6},{5,7},{6,4},{7,5},{8,10},{9,11},{10,... | collective-permute-start | bytes 221192 | tf_op jit(solution)/shard_map/ppermute | solution.py:122
  417.3 5.0 %collective-permute-start.2 = (bf16[96,384]{1,0:T(8,128)(2,1)S(1)}, bf16[96,384]{1,0:T(8,128)(2,1)S(1)}, u32[]{:S(2)}, u32[]{:S(2)}) collective-permute-start(bf16[96,384]{1,0:T(8,128)(2,1)S(1)} %fusion.106), channel_id=1, source_target_pairs={{0,4},{1,5},{2,6},{3,7},{4,0},{5,1},{6,2},{7,3},{8,12},{9,13},{10,... | collective-permute-start | bytes 221192 | tf_op jit(solution)/shard_map/ppermute | solution.py:122
  419.6 9.5 %collective-permute-start.19 = (bf16[96,768]{1,0:T(8,128)(2,1)S(1)}, bf16[96,768]{1,0:T(8,128)(2,1)S(1)}, u32[]{:S(2)}, u32[]{:S(2)}) collective-permute-start(bf16[96,768]{1,0:T(8,128)(2,1)S(1)} %pad_maximum_fusion.10), channel_id=1, source_target_pairs={{0,8},{8,0},{16,24},{24,16},{1,9},{9,1},{17,25},{25,17},{2,10},{10... | collective-permute-start | bytes 442376 | tf_op jit(solution)/shard_map/ppermute | solution.py:148
  421.6 10.0 %collective-permute-start.12 = (bf16[96,768]{1,0:T(8,128)(2,1)S(1)}, bf16[96,768]{1,0:T(8,128)(2,1)S(1)}, u32[]{:S(2)}, u32[]{:S(2)}) collective-permute-start(bf16[96,768]{1,0:T(8,128)(2,1)S(1)} %pad_maximum_fusion.9), channel_id=1, source_target_pairs={{0,8},{8,0},{16,24},{24,16},{1,9},{9,1},{17,25},{25,17},{2,10},{10... | collective-permute-start | bytes 442376 | tf_op jit(solution)/shard_map/ppermute | solution.py:148
  422.4 9.8 %collective-permute-start.5 = (bf16[96,768]{1,0:T(8,128)(2,1)S(1)}, bf16[96,768]{1,0:T(8,128)(2,1)S(1)}, u32[]{:S(2)}, u32[]{:S(2)}) collective-permute-start(bf16[96,768]{1,0:T(8,128)(2,1)S(1)} %pad_maximum_fusion.8), channel_id=1, source_target_pairs={{0,8},{8,0},{16,24},{24,16},{1,9},{9,1},{17,25},{25,17},{2,10},{10... | collective-permute-start | bytes 442376 | tf_op jit(solution)/shard_map/ppermute | solution.py:148
  424.7 4.4 collective-permute-start.23
  425.5 9.2 %collective-permute-start.25 = (bf16[96,512]{1,0:T(8,128)(2,1)S(1)}, bf16[96,512]{1,0:T(8,128)(2,1)S(1)}, u32[]{:S(2)}, u32[]{:S(2)}) collective-permute-start(bf16[96,512]{1,0:T(8,128)(2,1)S(1)} %fusion.105), channel_id=1, source_target_pairs={{0,2},{1,3},{2,0},{3,1},{4,6},{5,7},{6,4},{7,5},{8,10},{9,11},{10,... | collective-permute-start | bytes 294920 | tf_op jit(solution)/shard_map/ppermute | solution.py:122
  429.2 13.6 %collective-permute-start.20 = (bf16[96,768]{1,0:T(8,128)(2,1)S(1)}, bf16[96,768]{1,0:T(8,128)(2,1)S(1)}, u32[]{:S(2)}, u32[]{:S(2)}) collective-permute-start(bf16[96,768]{1,0:T(8,128)(2,1)S(1)} %add_convert_fusion.8), channel_id=1, source_target_pairs={{0,16},{8,24},{16,0},{24,8},{1,17},{9,25},{17,1},{25,9},{2,18},{10... | collective-permute-start | bytes 442376 | tf_op jit(solution)/shard_map/ppermute | solution.py:148
  431.6 12.7 %collective-permute-start.13 = (bf16[96,768]{1,0:T(8,128)(2,1)S(1)}, bf16[96,768]{1,0:T(8,128)(2,1)S(1)}, u32[]{:S(2)}, u32[]{:S(2)}) collective-permute-start(bf16[96,768]{1,0:T(8,128)(2,1)S(1)} %add_convert_fusion.10), channel_id=1, source_target_pairs={{0,16},{8,24},{16,0},{24,8},{1,17},{9,25},{17,1},{25,9},{2,18},{10... | collective-permute-start | bytes 442376 | tf_op jit(solution)/shard_map/ppermute | solution.py:148
  432.3 13.6 %collective-permute-start.6 = (bf16[96,768]{1,0:T(8,128)(2,1)S(1)}, bf16[96,768]{1,0:T(8,128)(2,1)S(1)}, u32[]{:S(2)}, u32[]{:S(2)}) collective-permute-start(bf16[96,768]{1,0:T(8,128)(2,1)S(1)} %add_convert_fusion.12), channel_id=1, source_target_pairs={{0,16},{8,24},{16,0},{24,8},{1,17},{9,25},{17,1},{25,9},{2,18},{10... | collective-permute-start | bytes 442376 | tf_op jit(solution)/shard_map/ppermute | solution.py:148
  434.8 11.2 %collective-permute-start.26 = (bf16[96,896]{1,0:T(8,128)(2,1)S(1)}, bf16[96,896]{1,0:T(8,128)(2,1)S(1)}, u32[]{:S(2)}, u32[]{:S(2)}) collective-permute-start(bf16[96,896]{1,0:T(8,128)(2,1)S(1)} %pad_maximum_fusion.7), channel_id=1, source_target_pairs={{0,8},{8,0},{16,24},{24,16},{1,9},{9,1},{17,25},{25,17},{2,10},{10... | collective-permute-start | bytes 516104 | tf_op jit(solution)/shard_map/ppermute | solution.py:148
  446.0 6.4 %collective-permute-start.27 = (bf16[96,896]{1,0:T(8,128)(2,1)S(1)}, bf16[96,896]{1,0:T(8,128)(2,1)S(1)}, u32[]{:S(2)}, u32[]{:S(2)}) collective-permute-start(bf16[96,896]{1,0:T(8,128)(2,1)S(1)} %add_convert_fusion.6), channel_id=1, source_target_pairs={{0,16},{8,24},{16,0},{24,8},{1,17},{9,25},{17,1},{25,9},{2,18},{10... | collective-permute-start | bytes 516104 | tf_op jit(solution)/shard_map/ppermute | solution.py:148
  (44 other events, 117.1 us)
Sparse Core Ops, SparseCore 0:
  11.7 42.3 all-gather.2
  56.5 58.6 all-gather.4
  321.2 77.1 reduce-scatter.1

commit v21 on v20

--- a/solution.py
+++ b/solution.py
@@ -195,15 +195,16 @@
     live_int = (row_ids // SEQ < image_counts[0, 0]).astype(jnp.int32)
     live_rows = live_int.astype(jnp.float32)
 
-    dense_local = jnp.concatenate(
-        [w_qkv, w_out, w_router, gain_attn[:, None], gain_moe[:, None]], axis=1
-    )
+    small_local = jnp.concatenate([w_router, gain_attn[:, None], gain_moe[:, None]], axis=1)
+    small_local = jnp.pad(small_local, ((0, 0), (0, -small_local.shape[1] % 128)))
+    dense_local = jnp.concatenate([w_qkv, w_out, small_local], axis=1)
     dense_full = lax.all_gather(dense_local, "shard", axis=0, tiled=True)
     full_qkv = dense_full[:, :qkv_cols]
     full_out = dense_full[:, qkv_cols : qkv_cols + width]
-    full_router = dense_full[:, qkv_cols + width : qkv_cols + width + n_route]
-    gain_one = dense_full[:, -2].astype(jnp.float32)
-    gain_two = dense_full[:, -1].astype(jnp.float32)
+    small_at = qkv_cols + width
+    full_router = dense_full[:, small_at : small_at + n_route]
+    gain_one = dense_full[:, small_at + n_route].astype(jnp.float32)
+    gain_two = dense_full[:, small_at + n_route + 1].astype(jnp.float32)
 
     back_rows = w_back.shape[1]
     expert_local = jnp.stack(
@@ -378,7 +379,7 @@
     )
     small = jnp.pad(small, ((0, 0), (0, 128 - small.shape[1])))
     dense_grads = jnp.concatenate([grad_qkv, grad_wout, small], axis=1)
-    n_parts = 4
+    n_parts = 3
     bounds = [128 * (dense_grads.shape[1] * k // (128 * n_parts)) for k in range(n_parts)]
     bounds = bounds + [dense_grads.shape[1]]
     dense_total = jnp.concatenate(

time: 475 us -> 471 us (level)
  waiting for transfers between devices: 85.9 us -> 104 us
  local copies, waits for them, and re-layouts: 54.1 us -> 44 us
  starting transfers between devices: 49.7 us -> 40.3 us
    ppermute x8 -> x6, waiting for transfers between devices: 14.8 us -> 24 us  [expert_all_reduce_doubling(): got = lax.ppermute(total, axis_name, pairs)]
    ppermute x20 -> x15, waiting for transfers between devices: 6.12 us -> 15 us  [_exchange(): got = lax.ppermute(send.astype(jnp.bfloat16), axis_name, pairs)]
    concatenate x2 -> x1, local copies, waits for them, and re-layouts: 5.31 us -> 0.18 us  [shards(): jnp.concatenate([grad_router, grad_gain_one[:, None], grad_gain_two[:, No...]
    ppermute x8 -> x6, starting transfers between devices: 12 us -> 7 us  [expert_all_reduce_doubling(): got = lax.ppermute(total, axis_name, pairs)]
    ppermute x20 -> x15, starting transfers between devices: 19.2 us -> 14.7 us  [_exchange(): got = lax.ppermute(send.astype(jnp.bfloat16), axis_name, pairs)]
  transfers between devices with their start and end apart: 35 -> 28, of which waited for: 14 -> 14; matrix products, arithmetic and copies ran while one was open for 57% -> 55% of each run, Pallas kernels for 8% -> 8%
where the time goes in v21:
time: 471 us; the launch traced here: 463 us
  matrix products  186 us (39%)
  waiting for transfers between devices  104 us (22%)
  local copies, waits for them, and re-layouts  44 us (9%)
  starting transfers between devices  40.3 us (9%)
  other arithmetic  36.7 us (8%)
  Pallas kernels  35.2 us (7%)
  between operations  16.5 us (4%)
    dot_general x2, matrix products, shards(): jnp.dot(flat_arrived, expert_first, preferred_element_type=jnp.float32)  51.9 us
    all_gather x1, waiting for transfers between devices, shards(): dense_full = lax.all_gather(dense_local, 'shard', axis=0, tiled=True)  29.4 us
    ppermute x6, waiting for transfers between devices, expert_all_reduce_doubling(): got = lax.ppermute(total, axis_name, pairs)  24 us
    all_to_all x2, waiting for transfers between devices, shards(): lax.all_to_all(dispatch_rows(experts * start, experts * (start + size)).r...  23.1 us
    dot_general x2, matrix products, shards(): lax.dot_general(flat_grad, expert_second, COL_CONTRACT, preferred_element...  22.6 us
    pallas_call x1, Pallas kernels, attention_bwd(): pl.pallas_call(functools.partial(attn_bwd_kernel, images=images), grid=(p...  21.8 us
    dot_general x2, matrix products, shards(): lax.dot_general(activated, flat_grad, ROW_CONTRACT, preferred_element_typ...  20.4 us
    ppermute x15, waiting for transfers between devices, _exchange(): got = lax.ppermute(send.astype(jnp.bfloat16), axis_name, pairs)  15 us
  transfers between devices with their start and end apart: 28, of which 14 were waited for; matrix products, arithmetic and copies ran while one was open for 55% of the time, Pallas kernels for 8%

profile of v21, /device:TPU:0, one launch (start us, length us, event | category | flops | bytes accessed | tf_op | source)
XLA Modules:
  0.0 463.0 jit_solution(12479506585235478140)
XLA Ops:
  8.1 2.0 fusion.86
  10.1 1.5 stack_reshape_squeeze.3
  11.7 2.3 pad_maximum_fusion.6
  20.1 3.3 fusion.125
  23.4 29.4 %all-gather.3.cloned.1.call-done = bf16[768,3200]{1,0:T(8,128)(2,1)} async-done(((bf16[96,3200]{1,0:T(8,128)(2,1)}), bf16[768,3200]{1,0:T(8,128)(2,1)}) %all-gather.3.cloned.1.call-update) | async-done | bytes 4915216 | tf_op jit(solution)/shard_map/all_gather | solution.py:201
  54.6 4.6 convolution_convert_fusion
  59.4 13.4 %shard_map.178 = bf16[640,768]{1,0:T(8,128)(2,1)S(1)} custom-call(bf16[640,2304]{1,0:T(8,128)(2,1)S(1)} %pad.23.q_ref.k_ref.v_ref, bf16[640,2304]{1,0:T(8,128)(2,1)S(1)} %pad.23.q_ref.k_ref.v_ref, bf16[640,2304]{1,0:T(8,128)(2,1)S(1)} %pad.23.q_ref.k_ref.v_ref), custom_call_target="tpu_custom_call" | custom-call | tf_op jit(solution)/shard_map/pallas_call | solution.py:90
  72.9 2.6 fusion.134
  77.0 1.5 fusion.135
  79.4 2.7 fusion.60
  82.1 2.3 convolution_convert_fusion.4
  84.4 2.4 add_convert_fusion.3
  86.8 1.6 pad_maximum_fusion.4
  88.4 4.6 all-to-all-start.2
  93.6 2.9 fusion.53
  99.6 1.6 pad_maximum_fusion.2
  101.2 12.9 %all-gather.5.cloned.1.call-done = bf16[2,768,3072]{2,1,0:T(8,128)(2,1)} async-done(((bf16[2,96,3072]{2,1,0:T(8,128)(2,1)}), bf16[2,768,3072]{2,1,0:T(8,128)(2,1)}) %all-gather.5.cloned.1.call-update) | async-done | bytes 9437200 | tf_op jit(solution)/shard_map/all_gather | solution.py:213
  114.0 4.9 %slice.223 = bf16[1,768,3072]{2,1,0:T(8,128)(2,1)} slice(bf16[2,768,3072]{2,1,0:T(8,128)(2,1)} %all-gather.5.cloned.1.call-done), slice={[1:2], [0:768], [0:3072]} | slice | bytes 9437184 | tf_op jit(solution)/shard_map/slice | solution.py:215
  118.9 8.5 %reshape_squeeze.3 = bf16[3072,768]{1,0:T(8,128)(2,1)} reshape(bf16[1,768,3072]{2,1,0:T(8,128)(2,1)} %slice.223) | data formatting | bytes 9437184 | tf_op jit(solution)/shard_map/reshape;squeeze | solution.py:215
  127.4 17.7 %all-to-all-done.2 = bf16[4,184,1536]{2,1,0:T(8,128)(2,1)S(1)} async-done(((bf16[4,184,1536]{2,1,0:T(8,128)(2,1)}), bf16[4,184,1536]{2,1,0:T(8,128)(2,1)S(1)}, u32[]{:S(2)}, u32[]{:S(2)}) %all-to-all-start.2) | async-done | bytes 2261024 | tf_op jit(solution)/shard_map/all_to_all | solution.py:271
  146.5 3.8 all-to-all-start
  150.3 25.8 %multiply_convert_fusion.1 = (bf16[736,3072]{1,0:T(8,128)(2,1)S(1)}, f32[736,3072]{1,0:T(8,128)}, f32[736,3072]{1,0:T(8,128)}) fusion(bf16[2,768,3072]{2,1,0:T(8,128)(2,1)} %all-gather.5.cloned.1.call-done, bf16[736,1536]{1,0:T(8,128)(2,1)} %bitcast.191), kind=kOutput, calls=%fused_computation.36 | convolution fusion | flops 3619848192 | bytes 28459008 | tf_op jit(solution)/shard_map/dot_general | solution.py:285
  176.1 3.7 convolution_convert_fusion.3
  179.8 10.8 %fusion.19 = bf16[736,3072]{1,0:T(8,128)(2,1)} fusion(f32[736,3072]{1,0:T(8,128)} %get-tuple-element.117, f32[736,3072]{1,0:T(8,128)} %get-tuple-element.97, bf16[3072,768]{1,0:T(8,128)(2,1)S(1)} %copy-done.18, bf16[736,1536]{1,0:T(8,128)(2,1)} %bitcast.192), kind=kOutput, calls=%fused_computation.35 | convolution fusion | flops 3490971648 | bytes 28459008 | tf_op jit(solution)/shard_map/dot_general | solution.py:282
  190.6 6.1 %fusion.49 = bf16[736,768]{1,0:T(8,128)(2,1)S(1)} fusion(bf16[736,3072]{1,0:T(8,128)(2,1)} %fusion.19, bf16[2,768,3072]{2,1,0:T(8,128)(2,1)S(1)} %bitcast.190), kind=kOutput, calls=%fused_computation.114 | convolution fusion | flops 3473448960 | bytes 10371072 | tf_op jit(solution)/shard_map/dot_general | solution.py:292
  196.7 1.6 pad_maximum_fusion.5
  198.3 5.3 %all-to-all-done = bf16[4,192,1536]{2,1,0:T(8,128)(2,1)S(1)} async-done(((bf16[4,192,1536]{2,1,0:T(8,128)(2,1)}), bf16[4,192,1536]{2,1,0:T(8,128)(2,1)S(1)}, u32[]{:S(2)}, u32[]{:S(2)}) %all-to-all-start) | async-done | bytes 2359328 | tf_op jit(solution)/shard_map/all_to_all | solution.py:271
  203.6 4.9 %all-to-all-start.3 = ((bf16[4,184,1536]{2,1,0:T(8,128)(2,1)}), bf16[4,184,1536]{2,1,0:T(8,128)(2,1)}, u32[]{:S(2)}, u32[]{:S(2)}) async-start(bf16[4,184,1536]{2,1,0:T(8,128)(2,1)} %bitcast.15), calls=%async_computation.3 | async-start | bytes 4521984 | tf_op jit(solution)/shard_map/all_to_all | solution.py:307
  208.5 26.2 %multiply_convert_fusion = (bf16[768,3072]{1,0:T(8,128)(2,1)S(1)}, f32[768,3072]{1,0:T(8,128)}, f32[768,3072]{1,0:T(8,128)}) fusion(bf16[2,768,3072]{2,1,0:T(8,128)(2,1)} %all-gather.5.cloned.1.call-done, bf16[768,1536]{1,0:T(8,128)(2,1)S(1)} %bitcast.185), kind=kOutput, calls=%fused_computation.14 | convolution fusion | flops 3777232896 | bytes 29491200 | tf_op jit(solution)/shard_map/dot_general | solution.py:285
  234.7 11.8 %fusion.6 = bf16[768,3072]{1,0:T(8,128)(2,1)S(1)} fusion(f32[768,3072]{1,0:T(8,128)} %get-tuple-element.118, f32[768,3072]{1,0:T(8,128)} %get-tuple-element.95, bf16[3072,768]{1,0:T(8,128)(2,1)} %reshape_squeeze.3, bf16[768,1536]{1,0:T(8,128)(2,1)S(1)} %bitcast.186), kind=kOutput, calls=%fused_computation.10 | convolution fusion | flops 3642753024 | bytes 29491200 | tf_op jit(solution)/shard_map/dot_general | solution.py:282
  246.5 8.1 %convolution_convert_fusion.1 = bf16[768,768]{0,1:T(8,128)(2,1)S(1)} fusion(bf16[768,3072]{1,0:T(8,128)(2,1)S(1)} %get-tuple-element.94, bf16[3072,768]{1,0:T(8,128)(2,1)} %reshape_squeeze.3), kind=kOutput, calls=%fused_computation.112 | convolution fusion | flops 3624468480 | bytes 10616832 | tf_op jit(solution)/shard_map/dot_general | solution.py:289
  254.7 6.3 %fusion.48 = bf16[768,768]{0,1:T(8,128)(2,1)S(1)} fusion(bf16[768,3072]{1,0:T(8,128)(2,1)S(1)} %fusion.6, bf16[2,768,3072]{2,1,0:T(8,128)(2,1)} %all-gather.5.cloned.1.call-done), kind=kOutput, calls=%fused_computation.111 | convolution fusion | flops 3624468480 | bytes 10616832 | tf_op jit(solution)/shard_map/dot_general | solution.py:292
  261.1 2.5 copy.124
  263.6 10.2 %fusion.64 = f32[3072,768]{1,0:T(8,128)} fusion(bf16[768,3072]{1,0:T(8,128)(2,1)} %copy-done.63, bf16[768,1536]{1,0:T(8,128)(2,1)} %bitcast.187), kind=kOutput, calls=%fused_computation.134 | convolution fusion | flops 3623878656 | bytes 15335424 | tf_op jit(solution)/shard_map/dot_general | solution.py:295
  273.8 5.2 %all-to-all-start.1 = ((bf16[4,192,1536]{2,1,0:T(8,128)(2,1)}), bf16[4,192,1536]{2,1,0:T(8,128)(2,1)}, u32[]{:S(2)}, u32[]{:S(2)}) async-start(bf16[4,192,1536]{2,1,0:T(8,128)(2,1)} %bitcast.10), calls=%async_computation.1 | async-start | bytes 4718592 | tf_op jit(solution)/shard_map/all_to_all | solution.py:307
  279.0 10.2 %add_convert_fusion = bf16[3072,768]{1,0:T(8,128)(2,1)} fusion(f32[3072,768]{1,0:T(8,128)} %fusion.64, bf16[736,3072]{1,0:T(8,128)(2,1)} %copy-done.64, bf16[736,1536]{1,0:T(8,128)(2,1)S(1)} %bitcast.193), kind=kOutput, calls=%fused_computation.12 | convolution fusion | flops 3477602304 | bytes 19808256 | tf_op jit(solution)/shard_map/dot_general | solution.py:295
  289.2 8.6 %stack_reshape.4 = bf16[1,768,3072]{2,1,0:T(8,128)(2,1)} reshape(bf16[3072,768]{1,0:T(8,128)(2,1)} %add_convert_fusion) | data formatting | bytes 9437184 | tf_op jit(solution)/shard_map/stack;reshape | solution.py:310
  297.8 5.9 %fusion.67 = f32[768,3072]{1,0:T(8,128)S(1)} fusion(bf16[768,3072]{1,0:T(8,128)(2,1)} %copy-done.19, bf16[768,1536]{1,0:T(8,128)(2,1)S(1)} %bitcast.188), kind=kOutput, calls=%fused_computation.137 | convolution fusion | flops 3623878656 | bytes 15335424 | tf_op jit(solution)/shard_map/dot_general | solution.py:298
  303.7 7.9 %fusion.26 = bf16[1,768,3072]{2,1,0:T(8,128)(2,1)} fusion(f32[768,3072]{1,0:T(8,128)S(1)} %fusion.67, bf16[736,3072]{1,0:T(8,128)(2,1)} %fusion.19, bf16[736,1536]{1,0:T(8,128)(2,1)S(1)} %bitcast.194), kind=kOutput, calls=%fused_computation.53 | convolution fusion | flops 3477602304 | bytes 19808256 | tf_op jit(solution)/shard_map/dot_general | solution.py:298
  311.6 8.3 %pad_maximum_fusion = bf16[2,768,3072]{2,1,0:T(8,128)(2,1)} fusion(bf16[1,768,3072]{2,1,0:T(8,128)(2,1)} %stack_reshape.4, bf16[1,768,3072]{2,1,0:T(8,128)(2,1)} %fusion.26), kind=kLoop, calls=%fused_computation.11 | loop fusion | flops 4718592 | bytes 18874368 | tf_op jit(solution)/shard_map/stack | solution.py:310
  321.0 5.5 %fusion.58 = f32[591,1536]{1,0:T(8,128)} fusion(bf16[736,1536]{1,0:T(8,128)(2,1)} %bitcast.16, pred[1504,591]{1,0:T(32,128)(4,1)S(1)} %copy-done.31), kind=kOutput, calls=%fused_computation.126 | convolution fusion | flops 1336246272 | bytes 6363136 | tf_op jit(solution)/shard_map/dot_general | solution.py:323
  326.5 5.4 %fusion.55 = f32[591,1536]{1,0:T(8,128)} fusion(bf16[736,1536]{1,0:T(8,128)(2,1)} %bitcast.16, pred[1504,591]{1,0:T(32,128)(4,1)S(1)} %copy-done.30), kind=kOutput, calls=%fused_computation.123 | convolution fusion | flops 1336246272 | bytes 6363136 | tf_op jit(solution)/shard_map/dot_general | solution.py:326
  331.9 6.1 %convolution_add_fusion.1 = f32[591,1536]{1,0:T(8,128)S(1)} fusion(f32[591,1536]{1,0:T(8,128)} %fusion.58, bf16[768,1536]{1,0:T(8,128)(2,1)} %bitcast.11, pred[1504,591]{1,0:T(32,128)(4,1)S(1)} %copy-done.31), kind=kOutput, calls=%fused_computation.60 | convolution fusion | flops 1395251712 | bytes 10113024 | tf_op jit(solution)/shard_map/dot_general | solution.py:323
  338.1 3.7 convolution_add_fusion
  342.0 1.9 multiply_reduce_fusion.3
  347.4 21.8 %shard_map.179 = (bf16[640,768]{1,0:T(8,128)(2,1)S(1)}, bf16[640,768]{1,0:T(8,128)(2,1)S(1)}, bf16[640,768]{1,0:T(8,128)(2,1)S(1)}) custom-call(bf16[640,2304]{1,0:T(8,128)(2,1)} %copy-done, bf16[640,2304]{1,0:T(8,128)(2,1)} %copy-done, bf16[640,2304]{1,0:T(8,128)(2,1)} %copy-done, bf16[640,768]{1,0:T(8,128)(2,1)S(1)} %pad.25.g_ref), custom_call_target="tpu_custom_call" | custom-call | tf_op jit(solution)/shard_map/pallas_call | solution.py:106
  370.4 2.4 fusion.45
  374.3 5.2 %fusion.77 = f32[768,2304]{1,0:T(8,128)S(1)} fusion(bf16[640,2304]{1,0:T(8,128)(2,1)} %copy-done.17, bf16[591,768]{1,0:T(8,128)(2,1)} %copy-done.20), kind=kOutput, calls=%fused_computation.148 | convolution fusion | flops 2264924160 | bytes 10934784 | tf_op jit(solution)/shard_map/dot_general | solution.py:367
  384.4 2.0 add_convert_fusion.4
  393.7 5.3 %collective-permute-done.10 = bf16[2,96,512]{2,1,0:T(8,128)(2,1)S(1)} collective-permute-done((bf16[2,96,512]{2,1,0:T(8,128)(2,1)S(1)}, bf16[2,96,512]{2,1,0:T(8,128)(2,1)S(1)}, u32[]{:S(2)}, u32[]{:S(2)}) %collective-permute-start.10) | collective-permute-done | bytes 196640 | tf_op jit(solution)/shard_map/ppermute | solution.py:122
  401.3 3.0 collective-permute-done.3
  404.6 1.7 collective-permute-start.4
  406.5 2.0 collective-permute-done.15
  408.5 1.5 collective-permute-start.2
  410.6 1.5 collective-permute-start.16
  412.2 1.6 collective-permute-start.12
  414.2 1.6 collective-permute-start.5
  417.0 3.8 collective-permute-done.18
  421.5 2.5 collective-permute-start.13
  424.0 5.0 %collective-permute-done.5 = bf16[96,1024]{1,0:T(8,128)(2,1)S(1)} collective-permute-done((bf16[96,1024]{1,0:T(8,128)(2,1)S(1)}, bf16[96,1024]{1,0:T(8,128)(2,1)S(1)}, u32[]{:S(2)}, u32[]{:S(2)}) %collective-permute-start.5) | collective-permute-done | bytes 196640 | tf_op jit(solution)/shard_map/ppermute | solution.py:148
  429.7 3.8 collective-permute-done.19
  433.7 12.6 %collective-permute-done.6 = bf16[96,1024]{1,0:T(8,128)(2,1)S(1)} collective-permute-done((bf16[96,1024]{1,0:T(8,128)(2,1)S(1)}, bf16[96,1024]{1,0:T(8,128)(2,1)S(1)}, u32[]{:S(2)}, u32[]{:S(2)}) %collective-permute-start.6) | collective-permute-done | bytes 196640 | tf_op jit(solution)/shard_map/ppermute | solution.py:148
  446.3 2.7 collective-permute-done.20
  452.1 2.5 fusion.133
  (304 shorter events, 45.7 us)
Async XLA Ops:
  7.2 7.8 %copy-start.44 = (s32[591,2]{0,1:T(2,128)S(1)}, s32[591,2]{0,1:T(2,128)}, u32[]{:S(2)}) copy-start(s32[591,2]{0,1:T(2,128)} %param.13) | copy-start | bytes 14188
  7.2 45.6 %all-gather.3.cloned.1.call-start = ((), (), s32[]{:S(2)}) async-start(), calls=%async_computation.5 | async-start | bytes 5529600 | tf_op jit(solution)/shard_map/all_gather | solution.py:201
  10.1 7.9 %copy-start.5 = (bf16[591,768]{1,0:T(8,128)(2,1)S(1)}, bf16[591,768]{1,0:T(8,128)(2,1)}, u32[]{:S(2)}) copy-start(bf16[591,768]{1,0:T(8,128)(2,1)} %param.11) | copy-start | bytes 2723332
  10.1 103.9 %all-gather.5.cloned.1.call-start = ((), (), s32[]{:S(2)}) async-start(), calls=%async_computation.6 | async-start | bytes 10616832 | tf_op jit(solution)/shard_map/all_gather | solution.py:213
  11.7 6.9 %copy-start.7 = (bf16[591,768]{1,0:T(8,128)(2,1)S(1)}, bf16[591,768]{1,0:T(8,128)(2,1)}, u32[]{:S(2)}) copy-start(bf16[591,768]{1,0:T(8,128)(2,1)} %param.21) | copy-start | bytes 2723332
  17.9 60.8 %copy-start.34 = (f32[591]{0:T(1024)}, f32[591]{0:T(1024)S(1)}, u32[]{:S(2)}) copy-start(f32[591]{0:T(1024)S(1)} %fusion.122) | copy-start | bytes 7096
  18.2 36.0 %copy-start.42 = (f32[591]{0:T(1024)}, f32[591]{0:T(1024)S(1)}, u32[]{:S(2)}) copy-start(f32[591]{0:T(1024)S(1)} %broadcast_multiply_fusion.2) | copy-start | bytes 7096
  18.6 35.6 %copy-start.54 = (f32[591]{0:T(1024)}, f32[591]{0:T(1024)S(1)}, u32[]{:S(2)}) copy-start(f32[591]{0:T(1024)S(1)} %fusion.120) | copy-start | bytes 7096
  23.4 58.7 %copy-start.24 = (bf16[1504,591]{1,0:T(8,128)(2,1)}, bf16[1504,591]{1,0:T(8,128)(2,1)S(1)}, u32[]{:S(2)}) copy-start(bf16[1504,591]{1,0:T(8,128)(2,1)S(1)} %get-tuple-element.107) | copy-start | bytes 5333188
  54.2 5.0 %copy-start.52 = (f32[768]{0:T(1024)}, f32[768]{0:T(1024)S(1)}, u32[]{:S(2)}) copy-start(f32[768]{0:T(1024)S(1)} %get-tuple-element.79) | copy-start | bytes 9220
  54.2 22.3 %copy-start.46 = (f32[768]{0:T(1024)}, f32[768]{0:T(1024)S(1)}, u32[]{:S(2)}) copy-start(f32[768]{0:T(1024)S(1)} %get-tuple-element.78) | copy-start | bytes 9220
  54.5 4.6 %copy-start.20 = (bf16[591,768]{1,0:T(8,128)(2,1)}, bf16[591,768]{1,0:T(8,128)(2,1)S(1)}, u32[]{:S(2)}) copy-start(bf16[591,768]{1,0:T(8,128)(2,1)S(1)} %fusion.42) | copy-start | bytes 2723332
  59.4 13.4 %copy-start = (bf16[640,2304]{1,0:T(8,128)(2,1)}, bf16[640,2304]{1,0:T(8,128)(2,1)S(1)}, u32[]{:S(2)}) copy-start(bf16[640,2304]{1,0:T(8,128)(2,1)S(1)} %pad.23.q_ref.k_ref.v_ref) | copy-start | bytes 8847364
  75.5 3.7 copy-start.14
  77.0 19.6 %copy-start.10 = (bf16[591,768]{1,0:T(8,128)(2,1)}, bf16[591,768]{1,0:T(8,128)(2,1)S(1)}, u32[]{:S(2)}) copy-start(bf16[591,768]{1,0:T(8,128)(2,1)S(1)} %multiply_convert_fusion.4) | copy-start | bytes 2723332
  79.4 5.0 %copy-start.27 = (bf16[591,2,768]{2,0,1:T(8,128)(2,1)}, bf16[591,2,768]{2,0,1:T(8,128)(2,1)S(1)}, u32[]{:S(2)}) copy-start(bf16[591,2,768]{2,0,1:T(8,128)(2,1)S(1)} %multiply_convert_fusion.2) | copy-start | bytes 5446660
  88.4 56.7 %all-to-all-start.2 = ((bf16[4,184,1536]{2,1,0:T(8,128)(2,1)}), bf16[4,184,1536]{2,1,0:T(8,128)(2,1)S(1)}, u32[]{:S(2)}, u32[]{:S(2)}) async-start(bf16[4,184,1536]{2,1,0:T(8,128)(2,1)} %pad_maximum_fusion.4), calls=%async_computation.2 | async-start | bytes 4521984 | tf_op jit(solution)/shard_map/all_to_all | solution.py:271
  93.0 3.6 copy-start.25
  93.0 3.6 copy-start.26
  146.5 57.2 %all-to-all-start = ((bf16[4,192,1536]{2,1,0:T(8,128)(2,1)}), bf16[4,192,1536]{2,1,0:T(8,128)(2,1)S(1)}, u32[]{:S(2)}, u32[]{:S(2)}) async-start(bf16[4,192,1536]{2,1,0:T(8,128)(2,1)} %pad_maximum_fusion.2), calls=%async_computation | async-start | bytes 4718592 | tf_op jit(solution)/shard_map/all_to_all | solution.py:271
  150.3 25.8 %copy-start.18 = (bf16[3072,768]{1,0:T(8,128)(2,1)S(1)}, bf16[3072,768]{1,0:T(8,128)(2,1)}, u32[]{:S(2)}) copy-start(bf16[3072,768]{1,0:T(8,128)(2,1)} %reshape_squeeze.3) | copy-start | bytes 14155780
  176.1 3.7 copy-start.64
  176.1 14.5 %slice-start = ((s8[9437184]{0:T(1024)(128)(4,1)}), s8[4194304]{0:T(1024)(128)(4,1)S(1)}, s32[]{:S(2)}) async-start(s8[9437184]{0:T(1024)(128)(4,1)} %bitcast.189), calls=%async_computation.8 | async-start | bytes 8388608
  176.1 14.5 %slice-start.1 = ((s8[9437184]{0:T(1024)(128)(4,1)}), s8[4194304]{0:T(1024)(128)(4,1)S(1)}, s32[]{:S(2)}) async-start(s8[9437184]{0:T(1024)(128)(4,1)} %bitcast.189), calls=%async_computation.9 | async-start | bytes 8388608
  179.8 10.8 %slice-start.2 = ((s8[9437184]{0:T(1024)(128)(4,1)}), s8[1048576]{0:T(1024)(128)(4,1)S(1)}, s32[]{:S(2)}) async-start(s8[9437184]{0:T(1024)(128)(4,1)} %bitcast.189), calls=%async_computation.10 | async-start | bytes 2097152
  203.6 31.1 %copy-start.15 = (bf16[4,192,1536]{2,1,0:T(8,128)(2,1)}, bf16[4,192,1536]{2,1,0:T(8,128)(2,1)S(1)}, u32[]{:S(2)}) copy-start(bf16[4,192,1536]{2,1,0:T(8,128)(2,1)S(1)} %all-to-all-done) | copy-start | bytes 7077892
  203.6 70.1 %all-to-all-start.3 = ((bf16[4,184,1536]{2,1,0:T(8,128)(2,1)}), bf16[4,184,1536]{2,1,0:T(8,128)(2,1)}, u32[]{:S(2)}, u32[]{:S(2)}) async-start(bf16[4,184,1536]{2,1,0:T(8,128)(2,1)} %bitcast.15), calls=%async_computation.3 | async-start | bytes 4521984 | tf_op jit(solution)/shard_map/all_to_all | solution.py:307
  234.7 11.8 %copy-start.63 = (bf16[768,3072]{1,0:T(8,128)(2,1)}, bf16[768,3072]{1,0:T(8,128)(2,1)S(1)}, u32[]{:S(2)}) copy-start(bf16[768,3072]{1,0:T(8,128)(2,1)S(1)} %get-tuple-element.94) | copy-start | bytes 14155780
  246.5 8.2 %copy-start.19 = (bf16[768,3072]{1,0:T(8,128)(2,1)}, bf16[768,3072]{1,0:T(8,128)(2,1)S(1)}, u32[]{:S(2)}) copy-start(bf16[768,3072]{1,0:T(8,128)(2,1)S(1)} %fusion.6) | copy-start | bytes 14155780
  273.8 5.2 %copy-start.22 = (bf16[4,184,1536]{2,1,0:T(8,128)(2,1)S(1)}, bf16[4,184,1536]{2,1,0:T(8,128)(2,1)}, u32[]{:S(2)}) copy-start(bf16[4,184,1536]{2,1,0:T(8,128)(2,1)} %copy-done.21) | copy-start | bytes 6782980
  273.8 58.1 %all-to-all-start.1 = ((bf16[4,192,1536]{2,1,0:T(8,128)(2,1)}), bf16[4,192,1536]{2,1,0:T(8,128)(2,1)}, u32[]{:S(2)}, u32[]{:S(2)}) async-start(bf16[4,192,1536]{2,1,0:T(8,128)(2,1)} %bitcast.10), calls=%async_computation.1 | async-start | bytes 4718592 | tf_op jit(solution)/shard_map/all_to_all | solution.py:307
  279.0 173.2 %reduce-scatter.2.cloned.1.call-start = ((), (), s32[]{:S(2)}) async-start(), calls=%async_computation.7 | async-start | bytes 10616832 | tf_op jit(solution)/shard_map/reduce_scatter | solution.py:313
  289.2 8.6 %copy-start.16 = (bf16[4,192,1536]{2,1,0:T(8,128)(2,1)S(1)}, bf16[4,192,1536]{2,1,0:T(8,128)(2,1)}, u32[]{:S(2)}) copy-start(bf16[4,192,1536]{2,1,0:T(8,128)(2,1)} %copy-done.15) | copy-start | bytes 7077892
  297.8 5.9 %copy-start.23 = (bf16[4,184,1536]{2,1,0:T(8,128)(2,1)S(1)}, bf16[4,184,1536]{2,1,0:T(8,128)(2,1)}, u32[]{:S(2)}) copy-start(bf16[4,184,1536]{2,1,0:T(8,128)(2,1)} %copy-done.21) | copy-start | bytes 6782980
  321.0 5.5 %copy-start.30 = (pred[1504,591]{1,0:T(32,128)(4,1)S(1)}, pred[1504,591]{1,0:T(32,128)(4,1)}, u32[]{:S(2)}) copy-start(pred[1504,591]{1,0:T(32,128)(4,1)} %get-tuple-element.111) | copy-start | bytes 2666596
  331.9 6.2 %copy-start.62 = (f32[591,1536]{1,0:T(8,128)S(1)}, f32[591,1536]{1,0:T(8,128)}, u32[]{:S(2)}) copy-start(f32[591,1536]{1,0:T(8,128)} %fusion.55) | copy-start | bytes 10893316
  331.9 12.1 %slice-start.3 = ((s8[4915200]{0:T(1024)(128)(4,1)}), s8[4194304]{0:T(1024)(128)(4,1)S(1)}, s32[]{:S(2)}) async-start(s8[4915200]{0:T(1024)(128)(4,1)} %bitcast.199), calls=%async_computation.11 | async-start | bytes 8388608
  338.1 3.8 copy-start.4
  338.1 3.8 copy-start.8
  338.1 3.8 copy-start.35
  338.1 3.8 copy-start.60
  338.1 3.8 copy-start.61
  338.1 5.9 %slice-start.4 = ((s8[4915200]{0:T(1024)(128)(4,1)}), s8[720896]{0:T(1024)(128)(4,1)S(1)}, s32[]{:S(2)}) async-start(s8[4915200]{0:T(1024)(128)(4,1)} %bitcast.199), calls=%async_computation.12 | async-start | bytes 1441792
  380.7 5.7 %collective-permute-start.7 = (bf16[2,2,96,1024]{3,2,1,0:T(8,128)(2,1)S(1)}, bf16[2,2,96,1024]{3,2,1,0:T(8,128)(2,1)S(1)}, u32[]{:S(2)}, u32[]{:S(2)}) collective-permute-start(bf16[2,2,96,1024]{3,2,1,0:T(8,128)(2,1)S(1)} %fusion.85), channel_id=1, source_target_pairs={{0,1},{1,0},{2,3},{3,2},{4,5},{5,4},{6,7},{7,6},{8,9},{9,8},{10,11... | collective-permute-start | bytes 2359304 | tf_op jit(solution)/shard_map/ppermute | solution.py:122
  382.7 9.1 %collective-permute-start.14 = (bf16[2,2,96,1152]{3,2,1,0:T(8,128)(2,1)S(1)}, bf16[2,2,96,1152]{3,2,1,0:T(8,128)(2,1)S(1)}, u32[]{:S(2)}, u32[]{:S(2)}) collective-permute-start(bf16[2,2,96,1152]{3,2,1,0:T(8,128)(2,1)S(1)} %fusion.80), channel_id=1, source_target_pairs={{0,1},{1,0},{2,3},{3,2},{4,5},{5,4},{6,7},{7,6},{8,9},{9,8},{10,11... | collective-permute-start | bytes 2654216 | tf_op jit(solution)/shard_map/ppermute | solution.py:122
  383.0 6.7 %collective-permute-start = (bf16[2,2,96,1024]{3,2,1,0:T(8,128)(2,1)S(1)}, bf16[2,2,96,1024]{3,2,1,0:T(8,128)(2,1)S(1)}, u32[]{:S(2)}, u32[]{:S(2)}) collective-permute-start(bf16[2,2,96,1024]{3,2,1,0:T(8,128)(2,1)S(1)} %fusion.84), channel_id=1, source_target_pairs={{0,1},{1,0},{2,3},{3,2},{4,5},{5,4},{6,7},{7,6},{8,9},{9,8},{10,11... | collective-permute-start | bytes 2359304 | tf_op jit(solution)/shard_map/ppermute | solution.py:122
  386.9 12.0 %collective-permute-start.10 = (bf16[2,96,512]{2,1,0:T(8,128)(2,1)S(1)}, bf16[2,96,512]{2,1,0:T(8,128)(2,1)S(1)}, u32[]{:S(2)}, u32[]{:S(2)}) collective-permute-start(bf16[2,96,512]{2,1,0:T(8,128)(2,1)S(1)} %fusion.92), channel_id=1, source_target_pairs={{0,4},{1,5},{2,6},{3,7},{4,0},{5,1},{6,2},{7,3},{8,12},{9,13},{10,... | collective-permute-start | bytes 589832 | tf_op jit(solution)/shard_map/ppermute | solution.py:122
  388.4 12.2 %collective-permute-start.8 = (bf16[2,96,512]{2,1,0:T(8,128)(2,1)S(1)}, bf16[2,96,512]{2,1,0:T(8,128)(2,1)S(1)}, u32[]{:S(2)}, u32[]{:S(2)}) collective-permute-start(bf16[2,96,512]{2,1,0:T(8,128)(2,1)S(1)} %fusion.95), channel_id=1, source_target_pairs={{0,2},{1,3},{2,0},{3,1},{4,6},{5,7},{6,4},{7,5},{8,10},{9,11},{10,... | collective-permute-start | bytes 589832 | tf_op jit(solution)/shard_map/ppermute | solution.py:122
  390.2 14.1 %collective-permute-start.3 = (bf16[2,96,512]{2,1,0:T(8,128)(2,1)S(1)}, bf16[2,96,512]{2,1,0:T(8,128)(2,1)S(1)}, u32[]{:S(2)}, u32[]{:S(2)}) collective-permute-start(bf16[2,96,512]{2,1,0:T(8,128)(2,1)S(1)} %fusion.90), channel_id=1, source_target_pairs={{0,4},{1,5},{2,6},{3,7},{4,0},{5,1},{6,2},{7,3},{8,12},{9,13},{10,... | collective-permute-start | bytes 589832 | tf_op jit(solution)/shard_map/ppermute | solution.py:122
  391.2 13.4 %collective-permute-start.1 = (bf16[2,96,512]{2,1,0:T(8,128)(2,1)S(1)}, bf16[2,96,512]{2,1,0:T(8,128)(2,1)S(1)}, u32[]{:S(2)}, u32[]{:S(2)}) collective-permute-start(bf16[2,96,512]{2,1,0:T(8,128)(2,1)S(1)} %fusion.94), channel_id=1, source_target_pairs={{0,2},{1,3},{2,0},{3,1},{4,6},{5,7},{6,4},{7,5},{8,10},{9,11},{10,... | collective-permute-start | bytes 589832 | tf_op jit(solution)/shard_map/ppermute | solution.py:122
  392.2 23.6 %collective-permute-start.17 = (bf16[2,96,640]{2,1,0:T(8,128)(2,1)S(1)}, bf16[2,96,640]{2,1,0:T(8,128)(2,1)S(1)}, u32[]{:S(2)}, u32[]{:S(2)}) collective-permute-start(bf16[2,96,640]{2,1,0:T(8,128)(2,1)S(1)} %fusion.87), channel_id=1, source_target_pairs={{0,4},{1,5},{2,6},{3,7},{4,0},{5,1},{6,2},{7,3},{8,12},{9,13},{10,... | collective-permute-start | bytes 737288 | tf_op jit(solution)/shard_map/ppermute | solution.py:122
  399.0 9.5 %collective-permute-start.15 = (bf16[2,96,512]{2,1,0:T(8,128)(2,1)S(1)}, bf16[2,96,512]{2,1,0:T(8,128)(2,1)S(1)}, u32[]{:S(2)}, u32[]{:S(2)}) collective-permute-start(bf16[2,96,512]{2,1,0:T(8,128)(2,1)S(1)} %fusion.96), channel_id=1, source_target_pairs={{0,2},{1,3},{2,0},{3,1},{4,6},{5,7},{6,4},{7,5},{8,10},{9,11},{10,... | collective-permute-start | bytes 589832 | tf_op jit(solution)/shard_map/ppermute | solution.py:122
  400.5 10.1 %collective-permute-start.11 = (bf16[96,512]{1,0:T(8,128)(2,1)S(1)}, bf16[96,512]{1,0:T(8,128)(2,1)S(1)}, u32[]{:S(2)}, u32[]{:S(2)}) collective-permute-start(bf16[96,512]{1,0:T(8,128)(2,1)S(1)} %fusion.109), channel_id=1, source_target_pairs={{0,2},{1,3},{2,0},{3,1},{4,6},{5,7},{6,4},{7,5},{8,10},{9,11},{10,... | collective-permute-start | bytes 294920 | tf_op jit(solution)/shard_map/ppermute | solution.py:122
  404.3 7.9 %collective-permute-start.9 = (bf16[96,512]{1,0:T(8,128)(2,1)S(1)}, bf16[96,512]{1,0:T(8,128)(2,1)S(1)}, u32[]{:S(2)}, u32[]{:S(2)}) collective-permute-start(bf16[96,512]{1,0:T(8,128)(2,1)S(1)} %fusion.108), channel_id=1, source_target_pairs={{0,4},{1,5},{2,6},{3,7},{4,0},{5,1},{6,2},{7,3},{8,12},{9,13},{10,... | collective-permute-start | bytes 294920 | tf_op jit(solution)/shard_map/ppermute | solution.py:122
  404.6 9.2 %collective-permute-start.4 = (bf16[96,512]{1,0:T(8,128)(2,1)S(1)}, bf16[96,512]{1,0:T(8,128)(2,1)S(1)}, u32[]{:S(2)}, u32[]{:S(2)}) collective-permute-start(bf16[96,512]{1,0:T(8,128)(2,1)S(1)} %fusion.107), channel_id=1, source_target_pairs={{0,2},{1,3},{2,0},{3,1},{4,6},{5,7},{6,4},{7,5},{8,10},{9,11},{10,... | collective-permute-start | bytes 294920 | tf_op jit(solution)/shard_map/ppermute | solution.py:122
  408.5 5.7 %collective-permute-start.2 = (bf16[96,512]{1,0:T(8,128)(2,1)S(1)}, bf16[96,512]{1,0:T(8,128)(2,1)S(1)}, u32[]{:S(2)}, u32[]{:S(2)}) collective-permute-start(bf16[96,512]{1,0:T(8,128)(2,1)S(1)} %fusion.106), channel_id=1, source_target_pairs={{0,4},{1,5},{2,6},{3,7},{4,0},{5,1},{6,2},{7,3},{8,12},{9,13},{10,... | collective-permute-start | bytes 294920 | tf_op jit(solution)/shard_map/ppermute | solution.py:122
  410.6 6.4 %collective-permute-start.16 = (bf16[96,512]{1,0:T(8,128)(2,1)S(1)}, bf16[96,512]{1,0:T(8,128)(2,1)S(1)}, u32[]{:S(2)}, u32[]{:S(2)}) collective-permute-start(bf16[96,512]{1,0:T(8,128)(2,1)S(1)} %fusion.110), channel_id=1, source_target_pairs={{0,4},{1,5},{2,6},{3,7},{4,0},{5,1},{6,2},{7,3},{8,12},{9,13},{10,... | collective-permute-start | bytes 294920 | tf_op jit(solution)/shard_map/ppermute | solution.py:122
  412.2 9.2 %collective-permute-start.12 = (bf16[96,1024]{1,0:T(8,128)(2,1)S(1)}, bf16[96,1024]{1,0:T(8,128)(2,1)S(1)}, u32[]{:S(2)}, u32[]{:S(2)}) collective-permute-start(bf16[96,1024]{1,0:T(8,128)(2,1)S(1)} %pad_maximum_fusion.11), channel_id=1, source_target_pairs={{0,8},{8,0},{16,24},{24,16},{1,9},{9,1},{17,25},{25,17},{2,10},{10... | collective-permute-start | bytes 589832 | tf_op jit(solution)/shard_map/ppermute | solution.py:148
  414.2 14.8 %collective-permute-start.5 = (bf16[96,1024]{1,0:T(8,128)(2,1)S(1)}, bf16[96,1024]{1,0:T(8,128)(2,1)S(1)}, u32[]{:S(2)}, u32[]{:S(2)}) collective-permute-start(bf16[96,1024]{1,0:T(8,128)(2,1)S(1)} %pad_maximum_fusion.10), channel_id=1, source_target_pairs={{0,8},{8,0},{16,24},{24,16},{1,9},{9,1},{17,25},{25,17},{2,10},{10... | collective-permute-start | bytes 589832 | tf_op jit(solution)/shard_map/ppermute | solution.py:148
  415.9 4.9 %collective-permute-start.18 = (bf16[96,640]{1,0:T(8,128)(2,1)S(1)}, bf16[96,640]{1,0:T(8,128)(2,1)S(1)}, u32[]{:S(2)}, u32[]{:S(2)}) collective-permute-start(bf16[96,640]{1,0:T(8,128)(2,1)S(1)} %fusion.105), channel_id=1, source_target_pairs={{0,2},{1,3},{2,0},{3,1},{4,6},{5,7},{6,4},{7,5},{8,10},{9,11},{10,... | collective-permute-start | bytes 368648 | tf_op jit(solution)/shard_map/ppermute | solution.py:122
  420.9 12.6 %collective-permute-start.19 = (bf16[96,1152]{1,0:T(8,128)(2,1)S(1)}, bf16[96,1152]{1,0:T(8,128)(2,1)S(1)}, u32[]{:S(2)}, u32[]{:S(2)}) collective-permute-start(bf16[96,1152]{1,0:T(8,128)(2,1)S(1)} %pad_maximum_fusion.9), channel_id=1, source_target_pairs={{0,8},{8,0},{16,24},{24,16},{1,9},{9,1},{17,25},{25,17},{2,10},{10... | collective-permute-start | bytes 663560 | tf_op jit(solution)/shard_map/ppermute | solution.py:148
  421.5 12.1 %collective-permute-start.13 = (bf16[96,1024]{1,0:T(8,128)(2,1)S(1)}, bf16[96,1024]{1,0:T(8,128)(2,1)S(1)}, u32[]{:S(2)}, u32[]{:S(2)}) collective-permute-start(bf16[96,1024]{1,0:T(8,128)(2,1)S(1)} %add_convert_fusion.8), channel_id=1, source_target_pairs={{0,16},{8,24},{16,0},{24,8},{1,17},{9,25},{17,1},{25,9},{2,18},{10... | collective-permute-start | bytes 589832 | tf_op jit(solution)/shard_map/ppermute | solution.py:148
  429.0 17.3 %collective-permute-start.6 = (bf16[96,1024]{1,0:T(8,128)(2,1)S(1)}, bf16[96,1024]{1,0:T(8,128)(2,1)S(1)}, u32[]{:S(2)}, u32[]{:S(2)}) collective-permute-start(bf16[96,1024]{1,0:T(8,128)(2,1)S(1)} %add_convert_fusion.10), channel_id=1, source_target_pairs={{0,16},{8,24},{16,0},{24,8},{1,17},{9,25},{17,1},{25,9},{2,18},{10... | collective-permute-start | bytes 589832 | tf_op jit(solution)/shard_map/ppermute | solution.py:148
  433.6 15.4 %collective-permute-start.20 = (bf16[96,1152]{1,0:T(8,128)(2,1)S(1)}, bf16[96,1152]{1,0:T(8,128)(2,1)S(1)}, u32[]{:S(2)}, u32[]{:S(2)}) collective-permute-start(bf16[96,1152]{1,0:T(8,128)(2,1)S(1)} %add_convert_fusion.6), channel_id=1, source_target_pairs={{0,16},{8,24},{16,0},{24,8},{1,17},{9,25},{17,1},{25,9},{2,18},{10... | collective-permute-start | bytes 663560 | tf_op jit(solution)/shard_map/ppermute | solution.py:148
  (34 other events, 58.1 us)
Sparse Core Ops, SparseCore 0:
  10.5 42.3 all-gather.2
  55.3 58.6 all-gather.4
  320.0 83.0 reduce-scatter.1
